TPU v7x, 32 devices: a whole 2x2x4 slice. The times are simulated.
32 devices in a mesh: group: 2 (over y), ctx: 8 (over z, x), dp: 2 (over core).
Axes of the slice: x: 2, y: 2, z: 4, core: 2. Of those that a mesh axis runs over, the one named last changes fastest.
Arguments:
- queries: bfloat16 [4, 1024, 512], P(('group', 'dp'), 'ctx'), parts along dimension 0, may hold values from -30 to 30
- key_rows: bfloat16 [4, 1024, 512], P(('group', 'dp'), 'ctx'), parts along dimension 0, may hold values from -30 to 30
- values: bfloat16 [4, 1024, 512], P(('group', 'dp'), 'ctx'), parts along dimension 0, may hold values from -6 to 6
- cotangent: bfloat16 [4, 1024, 1024], P(('group', 'dp'), 'ctx'), parts along dimension 0, may hold values from -6 to 6
- out_proj: bfloat16 [512, 1024], replicated, may hold values from -6 to 6
- conv_kernel: float32 [31, 1024], replicated, may hold values from -1.8 to 1.8
- lengths: int32 [4], P(('group', 'dp')), parts along dimension 0, may hold values from 640 to 1024, as said below
Outputs:
- grad_query: bfloat16 [4, 1024, 512], P(('group', 'dp'), 'ctx'), parts along dimension 0
- grad_key: bfloat16 [4, 1024, 512], P(('group', 'dp'), 'ctx'), parts along dimension 0
- grad_value: bfloat16 [4, 1024, 512], P(('group', 'dp'), 'ctx'), parts along dimension 0
- grad_out_proj: bfloat16 [1024, 1024], P('group'), parts along dimension 0
- grad_kernel: float32 [62, 1024], P('group'), parts along dimension 0
There are 2 independent parts, one for each index of `group`. A program takes and returns all parts, laid end to end along the dimension named above; an argument that names none is the same for every part. Nothing has to cross between parts.
Inputs may be any that keep to these rules, and one draw needn't show every extreme that they name: `lengths`: in every draw at least one recording is valid over all its 1024 frames.
All inputs are finite; a program needn't handle non-finite values.
Results may differ from a plain program's by a relative error of at most 0.014.
The roundings to bfloat16 on the way count: a program that leaves them out, or rounds other values in their place, can miss the bound.
Values may be sent and summed in bfloat16 or wider, within the bound.
No kernel may reach another device: no remote copies, remote signals or barrier semaphores. Data moves between devices by JAX's collectives and lax.ppermute only.
A program may use at most 64 MiB of HBM per device.

v0:
```python
import math

import jax
import jax.numpy as jnp
from jax import lax
from jax.sharding import PartitionSpec as P

HEADS = 8
HDIM = 64
KW = 31
REACH = 3


def passed_along(block, axis, distance):
    devices = range(lax.axis_size(axis))
    route = [(i - distance, i) for i in devices if i - distance in devices]
    return lax.ppermute(block, axis, route)


def padded(cells, sides, width):
    for axis, dim in sides:
        count = lax.axis_size(axis)
        ends = count - 1
        head = lax.slice_in_dim(cells, 0, width, axis=dim)
        tail = lax.slice_in_dim(cells, cells.shape[dim] - width, cells.shape[dim], axis=dim)
        cells = jnp.concatenate(
            [
                lax.ppermute(tail, axis, [(i, (i + 1) % count) for i in range(ends)]),
                cells,
                lax.ppermute(head, axis, [((i + 1) % count, i) for i in range(ends)]),
            ],
            axis=dim,
        )
    return cells


def collect(piece_own, shifter):
    from_below = []
    from_above = []
    moving = piece_own
    for repeat in range(REACH):
        moving = shifter(moving, 1)
        from_below.append(moving)
    moving = piece_own
    for repeat in range(REACH):
        moving = shifter(moving, -1)
        from_above.append(moving)
    return jnp.stack(from_below[::-1] + [piece_own] + from_above, axis=0)


def give_back(partials, shifter):
    moving = partials[0]
    for offset in range(1, REACH):
        moving = shifter(moving, -1) + partials[offset]
    from_below = shifter(moving, -1)
    moving = partials[2 * REACH]
    for offset in range(2 * REACH - 1, REACH, -1):
        moving = shifter(moving, 1) + partials[offset]
    from_above = shifter(moving, 1)
    return partials[REACH] + from_below + from_above


def on_device(queries, key_rows, values, cotangent, out_proj, conv_kernel, lengths):
    tokens = queries.shape[1]
    width_heads = queries.shape[2]
    channels = out_proj.shape[1]
    span_blocks = 2 * REACH + 1
    scale_factor = 1.0 / math.sqrt(HDIM)
    halo_width = (KW - 1) // 2
    block_index = lax.axis_index("ctx")
    length_here = lengths[0]
    query_here = queries[0]
    key_here = key_rows[0]
    value_here = values[0]
    cot_here = cotangent[0]
    frames = block_index * tokens + jnp.arange(tokens, dtype=jnp.int32)
    valid_rows = frames < length_here
    key_frames = (block_index - REACH) * tokens + jnp.arange(span_blocks * tokens, dtype=jnp.int32)
    valid_keys = (key_frames >= 0) & (key_frames < length_here)

    def kv_shift(piece_rows, offset_by):
        return passed_along(piece_rows, "ctx", offset_by)

    gathered = collect(jnp.stack([key_here, value_here], axis=0), kv_shift)
    key_all = gathered[:, 0].reshape(span_blocks * tokens, HEADS, HDIM)
    value_all = gathered[:, 1].reshape(span_blocks * tokens, HEADS, HDIM)
    query_heads = query_here.reshape(tokens, HEADS, HDIM)
    scores = (
        jnp.einsum("qhd,khd->hqk", query_heads, key_all, preferred_element_type=jnp.float32)
        * scale_factor
    )
    scores = jnp.where(valid_keys[None, None, :], scores, -jnp.inf)
    row_max = jnp.max(scores, axis=2, keepdims=True)
    row_total = jnp.sum(jnp.exp(scores - row_max), axis=2, keepdims=True)
    log_total = row_max + jnp.log(row_total)
    weights = jnp.exp(scores - log_total).astype(jnp.bfloat16)
    attended = jnp.einsum("hqk,khd->qhd", weights, value_all, preferred_element_type=jnp.float32)
    attended = attended.reshape(tokens, width_heads).astype(jnp.bfloat16)
    hidden = jnp.dot(attended, out_proj, preferred_element_type=jnp.float32)
    masked = jnp.where(valid_rows[:, None], hidden, 0.0).astype(jnp.bfloat16)

    def pad_time(field_rows):
        return padded(field_rows, (("ctx", 0),), halo_width)

    padded_m = pad_time(masked)
    conv_out = jnp.zeros((tokens, channels), jnp.float32)
    for tap_index in range(KW):
        conv_out = conv_out + conv_kernel[tap_index] * padded_m[tap_index : tap_index + tokens]
    sigmoid_c = jax.nn.sigmoid(conv_out)
    grad_conv = (
        cot_here.astype(jnp.float32) * (sigmoid_c + conv_out * sigmoid_c * (1.0 - sigmoid_c))
    ).astype(jnp.bfloat16)
    padded_g = pad_time(grad_conv)
    grad_wide = grad_conv.astype(jnp.float32)
    grad_masked = jnp.zeros((tokens, channels), jnp.float32)
    kernel_terms = []
    for tap_index in range(KW):
        start_row = 2 * halo_width - tap_index
        grad_masked = (
            grad_masked + conv_kernel[tap_index] * padded_g[start_row : start_row + tokens]
        )
        kernel_terms.append(
            jnp.sum(
                padded_m[tap_index : tap_index + tokens].astype(jnp.float32) * grad_wide, axis=0
            )
        )
    kernel_local = jnp.stack(kernel_terms, axis=0)
    grad_hidden = (
        cot_here.astype(jnp.float32) + jnp.where(valid_rows[:, None], grad_masked, 0.0)
    ).astype(jnp.bfloat16)
    proj_local = lax.dot_general(
        attended, grad_hidden, (((0,), (0,)), ((), ())), preferred_element_type=jnp.float32
    )
    proj_sum, kernel_sum = lax.psum((proj_local, kernel_local), ("ctx", "dp"))
    grad_attended = lax.dot_general(
        grad_hidden, out_proj, (((1,), (1,)), ((), ())), preferred_element_type=jnp.float32
    ).astype(jnp.bfloat16)
    grad_heads = grad_attended.reshape(tokens, HEADS, HDIM)
    attended_heads = attended.reshape(tokens, HEADS, HDIM)
    delta_rows = jnp.sum(
        grad_heads.astype(jnp.float32) * attended_heads.astype(jnp.float32), axis=2
    )
    grad_weights = jnp.einsum(
        "qhd,khd->hqk", grad_heads, value_all, preferred_element_type=jnp.float32
    )
    grad_logits = (weights.astype(jnp.float32) * (grad_weights - delta_rows.T[:, :, None])).astype(
        jnp.bfloat16
    )
    grad_query = (
        jnp.einsum("hqk,khd->qhd", grad_logits, key_all, preferred_element_type=jnp.float32)
        * scale_factor
    )
    grad_query = grad_query.reshape(tokens, width_heads).astype(jnp.bfloat16)
    grad_key_all = (
        jnp.einsum("hqk,qhd->khd", grad_logits, query_heads, preferred_element_type=jnp.float32)
        * scale_factor
    )
    grad_value_all = jnp.einsum(
        "hqk,qhd->khd", weights, grad_heads, preferred_element_type=jnp.float32
    )
    placed = jnp.stack(
        [
            grad_key_all.reshape(span_blocks, tokens, width_heads),
            grad_value_all.reshape(span_blocks, tokens, width_heads),
        ],
        axis=1,
    )

    def grad_shift(piece_rows, offset_by):
        return passed_along(piece_rows, "ctx", offset_by)

    own_grads = give_back(placed, grad_shift)
    grad_key = own_grads[0].astype(jnp.bfloat16)
    grad_value = own_grads[1].astype(jnp.bfloat16)
    return (
        grad_query[None],
        grad_key[None],
        grad_value[None],
        proj_sum.astype(jnp.bfloat16),
        kernel_sum,
    )


def solution(mesh):
    return jax.shard_map(
        on_device,
        mesh=mesh,
        in_specs=(
            P(("group", "dp"), "ctx", None),
            P(("group", "dp"), "ctx", None),
            P(("group", "dp"), "ctx", None),
            P(("group", "dp"), "ctx", None),
            P(),
            P(),
            P(("group", "dp")),
        ),
        out_specs=(
            P(("group", "dp"), "ctx", None),
            P(("group", "dp"), "ctx", None),
            P(("group", "dp"), "ctx", None),
            P("group", None),
            P("group", None),
        ),
        check_vma=False,
    )
```

profile of v0, /device:TPU:0, one launch (start us, length us, event | category | flops | bytes accessed | tf_op | source)
XLA Modules:
  0.0 282.0 jit_solution(4670167653859747844)
XLA Ops:
  9.1 4.9 %collective-permute-start = (bf16[2,128,512]{2,1,0:T(8,128)(2,1)S(1)}, bf16[2,128,512]{2,1,0:T(8,128)(2,1)S(1)}, u32[]{:S(2)}, u32[]{:S(2)}) collective-permute-start(bf16[2,128,512]{2,1,0:T(8,128)(2,1)S(1)} %constant_dynamic-update-slice_fusion), channel_id=1, source_target_pairs={{0,2},{2,4},{4,6},{6,8},{8,10},{10,12},{12,14},{1,3},{3,5},{5,7},{... | collective-permute-start | bytes 786440 | tf_op jit(solution)/shard_map/ppermute | solution.py:17
  14.0 1.3 collective-permute-start.3
  15.3 9.8 %collective-permute-done = bf16[2,128,512]{2,1,0:T(8,128)(2,1)S(1)} collective-permute-done((bf16[2,128,512]{2,1,0:T(8,128)(2,1)S(1)}, bf16[2,128,512]{2,1,0:T(8,128)(2,1)S(1)}, u32[]{:S(2)}, u32[]{:S(2)}) %collective-permute-start) | collective-permute-done | bytes 262176 | tf_op jit(solution)/shard_map/ppermute | solution.py:17
  25.2 4.4 %collective-permute-start.1 = (bf16[2,128,512]{2,1,0:T(8,128)(2,1)S(1)}, bf16[2,128,512]{2,1,0:T(8,128)(2,1)S(1)}, u32[]{:S(2)}, u32[]{:S(2)}) collective-permute-start(bf16[2,128,512]{2,1,0:T(8,128)(2,1)S(1)} %collective-permute-done), channel_id=1, source_target_pairs={{0,2},{2,4},{4,6},{6,8},{8,10},{10,12},{12,14},{1,3},{3,5},{5,7},{... | collective-permute-start | bytes 786440 | tf_op jit(solution)/shard_map/ppermute | solution.py:17
  30.3 1.3 collective-permute-start.4
  31.6 10.2 %collective-permute-done.1 = bf16[2,128,512]{2,1,0:T(8,128)(2,1)S(1)} collective-permute-done((bf16[2,128,512]{2,1,0:T(8,128)(2,1)S(1)}, bf16[2,128,512]{2,1,0:T(8,128)(2,1)S(1)}, u32[]{:S(2)}, u32[]{:S(2)}) %collective-permute-start.1) | collective-permute-done | bytes 262176 | tf_op jit(solution)/shard_map/ppermute | solution.py:17
  41.8 4.4 %collective-permute-start.2 = (bf16[2,128,512]{2,1,0:T(8,128)(2,1)S(1)}, bf16[2,128,512]{2,1,0:T(8,128)(2,1)S(1)}, u32[]{:S(2)}, u32[]{:S(2)}) collective-permute-start(bf16[2,128,512]{2,1,0:T(8,128)(2,1)S(1)} %collective-permute-done.1), channel_id=1, source_target_pairs={{0,2},{2,4},{4,6},{6,8},{8,10},{10,12},{12,14},{1,3},{3,5},{5,7},{... | collective-permute-start | bytes 786440 | tf_op jit(solution)/shard_map/ppermute | solution.py:17
  47.2 2.0 fusion.150
  49.3 1.3 collective-permute-start.5
  51.7 5.8 %collective-permute-done.5 = bf16[2,128,512]{2,1,0:T(8,128)(2,1)S(1)} collective-permute-done((bf16[2,128,512]{2,1,0:T(8,128)(2,1)S(1)}, bf16[2,128,512]{2,1,0:T(8,128)(2,1)S(1)}, u32[]{:S(2)}, u32[]{:S(2)}) %collective-permute-start.5) | collective-permute-done | bytes 262176 | tf_op jit(solution)/shard_map/ppermute | solution.py:17
  57.5 1.0 fusion.146
  59.3 1.0 reshape_squeeze.9
  63.1 2.4 copy.27
  65.5 2.9 %reshape_squeeze.11 = bf16[896,8,64]{0,2,1:T(8,128)(2,1)} reshape(bf16[7,1,128,512]{2,0,3,1:T(8,128)(2,1)} %copy.27) | data formatting | bytes 1835008 | tf_op jit(solution)/shard_map/reshape;squeeze | solution.py:86
  68.6 1.7 convolution_convert_fusion
  70.7 1.3 collective-permute-start.7
  72.0 4.5 %collective-permute-start.6 = (bf16[15,1024]{1,0:T(8,128)(2,1)S(1)}, bf16[15,1024]{1,0:T(8,128)(2,1)S(1)}, u32[]{:S(2)}, u32[]{:S(2)}) collective-permute-start(bf16[15,1024]{1,0:T(8,128)(2,1)S(1)} %get-tuple-element.60), channel_id=1, source_target_pairs={{0,2},{2,4},{4,6},{6,8},{8,10},{10,12},{12,14},{1,3},{3,5},{5,7},{... | collective-permute-start | bytes 92168 | tf_op jit(solution)/shard_map/ppermute | solution.py:28
  76.5 1.1 fusion.151
  78.3 4.1 %fusion.84 = (f32[1024]{0:T(1024)}, f32[1024]{0:T(1024)}, f32[1024]{0:T(1024)}, f32[1024]{0:T(1024)}, f32[1024]{0:T(1024)}, /*index=5*/f32[1024]{0:T(1024)}, f32...) fusion(bf16[15,1024]{1,0:T(8,128)(2,1)S(1)} %collective-permute-done.7, ...), kind=kLoop, calls=%fused_computation.216 | loop fusion | flops 31841280 | bytes 1011712 | tf_op jit(solution)/shard_map/reduce_sum | solution.py:123
  82.4 4.2 %collective-permute-start.9 = (bf16[15,1024]{1,0:T(8,128)(2,1)S(1)}, bf16[15,1024]{1,0:T(8,128)(2,1)S(1)}, u32[]{:S(2)}, u32[]{:S(2)}) collective-permute-start(bf16[15,1024]{1,0:T(8,128)(2,1)S(1)} %get-tuple-element.59), channel_id=1, source_target_pairs={{0,2},{2,4},{4,6},{6,8},{8,10},{10,12},{12,14},{1,3},{3,5},{5,7},{... | collective-permute-start | bytes 92168 | tf_op jit(solution)/shard_map/ppermute | solution.py:28
  86.6 1.5 collective-permute-start.8
  88.2 5.4 %collective-permute-done.8 = bf16[15,1024]{1,0:T(8,128)(2,1)S(1)} collective-permute-done((bf16[15,1024]{1,0:T(8,128)(2,1)S(1)}, bf16[15,1024]{1,0:T(8,128)(2,1)S(1)}, u32[]{:S(2)}, u32[]{:S(2)}) %collective-permute-start.8) | collective-permute-done | bytes 30752 | tf_op jit(solution)/shard_map/ppermute | solution.py:30
  93.6 3.1 %fusion.37 = bf16[128,1024]{1,0:T(8,128)(2,1)S(1)} fusion(bf16[128,1024]{1,0:T(8,128)(2,1)S(1)} %get-tuple-element.46, bf16[15,1024]{1,0:T(8,128)(2,1)S(1)} %collective-permute-done.9, bf16[15,1024]{1,0:T(8,128)(2,1)S(1)} %collective-permute-done.8, bf16[1,128,1024]{2,1,0:T(8,128)(2,1)S(1)} %copy-done.13, f32[1024]{0:T(1024)S(1)} %bitcast.229, ...), kind=kLoop, calls=%fused_computation.169 | loop fusion | flops 24379392 | bytes 974976 | tf_op jit(solution)/shard_map/convert_element_type | solution.py:130
  97.5 1.2 convolution_convert_fusion.1
  98.6 1.7 copy.29
  101.3 3.1 %convolution_bitcast_fusion = f32[896,8,64]{0,2,1:T(8,128)} fusion(bf16[128,8,64]{0,2,1:T(8,128)(2,1)} %bitcast.163, bf16[8,128,896]{1,2,0:T(8,128)(2,1)S(1)} %fusion.3), kind=kOutput, calls=%fused_computation.42 | convolution fusion | flops 117440512 | bytes 3801088 | tf_op jit(solution)/shard_map/hqk,qhd->khd/dot_general | solution.py:158
  105.3 1.3 copy-done.1
  106.5 2.1 multiply_bitcast_fusion
  108.6 1.6 stack_reshape.6
  110.2 1.5 constant_dynamic-update-slice_fusion.3
  111.7 1.6 stack_reshape.7
  113.3 1.4 constant_dynamic-update-slice_fusion.2
  114.7 15.0 %fusion.145 = (f32[1,2,128,512]{2,0,3,1:T(1,128)S(1)}, f32[1,2,128,512]{2,0,3,1:T(1,128)S(1)}, f32[1,2,128,512]{2,0,3,1:T(1,128)S(1)}, f32[1,2,128,512]{2,0,3,1:...) fusion(f32[7,2,128,512]{2,0,3,1:T(8,128)} %constant_dynamic-update-slic, ...), kind=kLoop, calls=%fused_computation.316 | loop fusion | bytes 7340032 | tf_op jit(solution)/shard_map/slice | solution.py:54
  129.7 4.8 %collective-permute-start.13 = (f32[2,128,512]{1,2,0:T(8,128)S(1)}, f32[2,128,512]{1,2,0:T(8,128)S(1)}, u32[]{:S(2)}, u32[]{:S(2)}) collective-permute-start(f32[2,128,512]{1,2,0:T(8,128)S(1)} %bitcast.168), channel_id=1, source_target_pairs={{0,2},{2,4},{4,6},{6,8},{8,10},{10,12},{12,14},{1,3},{3,5},{5,7},{... | collective-permute-start | bytes 1572872 | tf_op jit(solution)/shard_map/ppermute | solution.py:17
  134.6 1.3 collective-permute-start.10
  137.2 15.2 %collective-permute-done.13 = f32[2,128,512]{1,2,0:T(8,128)S(1)} collective-permute-done((f32[2,128,512]{1,2,0:T(8,128)S(1)}, f32[2,128,512]{1,2,0:T(8,128)S(1)}, u32[]{:S(2)}, u32[]{:S(2)}) %collective-permute-start.13) | collective-permute-done | bytes 524320 | tf_op jit(solution)/shard_map/ppermute | solution.py:17
  153.2 5.2 %collective-permute-start.14 = (f32[2,128,512]{1,2,0:T(8,128)}, f32[2,128,512]{1,2,0:T(8,128)}, u32[]{:S(2)}, u32[]{:S(2)}) collective-permute-start(f32[2,128,512]{1,2,0:T(8,128)} %add.311), channel_id=1, source_target_pairs={{0,2},{2,4},{4,6},{6,8},{8,10},{10,12},{12,14},{1,3},{3,5},{5,7},{... | collective-permute-start | bytes 1572872 | tf_op jit(solution)/shard_map/ppermute | solution.py:17
  159.3 1.3 collective-permute-start.11
  161.2 2.7 stack.167
  163.9 1.8 fusion.152
  165.7 10.9 %collective-permute-done.14 = f32[2,128,512]{1,2,0:T(8,128)} collective-permute-done((f32[2,128,512]{1,2,0:T(8,128)}, f32[2,128,512]{1,2,0:T(8,128)}, u32[]{:S(2)}, u32[]{:S(2)}) %collective-permute-start.14) | collective-permute-done | bytes 524320 | tf_op jit(solution)/shard_map/ppermute | solution.py:17
  176.5 1.9 add.312
  178.4 5.2 %collective-permute-start.15 = (f32[2,128,512]{1,2,0:T(8,128)}, f32[2,128,512]{1,2,0:T(8,128)}, u32[]{:S(2)}, u32[]{:S(2)}) collective-permute-start(f32[2,128,512]{1,2,0:T(8,128)} %add.312), channel_id=1, source_target_pairs={{0,2},{2,4},{4,6},{6,8},{8,10},{10,12},{12,14},{1,3},{3,5},{5,7},{... | collective-permute-start | bytes 1572872 | tf_op jit(solution)/shard_map/ppermute | solution.py:17
  184.5 1.4 collective-permute-start.12
  185.9 82.4 %all-reduce.4 = bf16[512,1024]{1,0:T(8,128)(2,1)} all-reduce(f32[512,1024]{1,0:T(8,128)} %fusion.152), channel_id=1, replica_groups=mesh['group'=2,'ctx'=8,'dp'=2] {'ctx','dp'}, use_global_device_ids=true, to_apply=%region_3.4 | all-reduce | flops 524288 | bytes 3145728 | tf_op jit(solution)/shard_map/psum | solution.py:134
  268.3 1.7 fusion.5
  270.8 1.3 add_convert_fusion
  273.6 1.6 copy.66
  (130 shorter events, 17.8 us)
Async XLA Ops:
  7.2 63.1 %copy-start = (bf16[512,1024]{1,0:T(8,128)(2,1)S(1)}, bf16[512,1024]{1,0:T(8,128)(2,1)}, u32[]{:S(2)}) copy-start(bf16[512,1024]{1,0:T(8,128)(2,1)} %param.11) | copy-start | bytes 3145732
  7.2 266.5 %all-reduce.3.cloned.1.call-start = ((), (), s32[]{:S(2)}) async-start(), calls=%async_computation | async-start | bytes 262144 | tf_op jit(solution)/shard_map/psum | solution.py:134
  9.1 16.0 %collective-permute-start = (bf16[2,128,512]{2,1,0:T(8,128)(2,1)S(1)}, bf16[2,128,512]{2,1,0:T(8,128)(2,1)S(1)}, u32[]{:S(2)}, u32[]{:S(2)}) collective-permute-start(bf16[2,128,512]{2,1,0:T(8,128)(2,1)S(1)} %constant_dynamic-update-slice_fusion), channel_id=1, source_target_pairs={{0,2},{2,4},{4,6},{6,8},{8,10},{10,12},{12,14},{1,3},{3,5},{5,7},{... | collective-permute-start | bytes 786440 | tf_op jit(solution)/shard_map/ppermute | solution.py:17
  14.0 16.2 %collective-permute-start.3 = (bf16[2,128,512]{2,1,0:T(8,128)(2,1)S(1)}, bf16[2,128,512]{2,1,0:T(8,128)(2,1)S(1)}, u32[]{:S(2)}, u32[]{:S(2)}) collective-permute-start(bf16[2,128,512]{2,1,0:T(8,128)(2,1)S(1)} %constant_dynamic-update-slice_fusion), channel_id=1, source_target_pairs={{2,0},{4,2},{6,4},{8,6},{10,8},{12,10},{14,12},{3,1},{5,3},{7,5},{... | collective-permute-start | bytes 786440 | tf_op jit(solution)/shard_map/ppermute | solution.py:17
  25.2 16.6 %collective-permute-start.1 = (bf16[2,128,512]{2,1,0:T(8,128)(2,1)S(1)}, bf16[2,128,512]{2,1,0:T(8,128)(2,1)S(1)}, u32[]{:S(2)}, u32[]{:S(2)}) collective-permute-start(bf16[2,128,512]{2,1,0:T(8,128)(2,1)S(1)} %collective-permute-done), channel_id=1, source_target_pairs={{0,2},{2,4},{4,6},{6,8},{8,10},{10,12},{12,14},{1,3},{3,5},{5,7},{... | collective-permute-start | bytes 786440 | tf_op jit(solution)/shard_map/ppermute | solution.py:17
  30.3 19.0 %collective-permute-start.4 = (bf16[2,128,512]{2,1,0:T(8,128)(2,1)S(1)}, bf16[2,128,512]{2,1,0:T(8,128)(2,1)S(1)}, u32[]{:S(2)}, u32[]{:S(2)}) collective-permute-start(bf16[2,128,512]{2,1,0:T(8,128)(2,1)S(1)} %collective-permute-done.3), channel_id=1, source_target_pairs={{2,0},{4,2},{6,4},{8,6},{10,8},{12,10},{14,12},{3,1},{5,3},{7,5},{... | collective-permute-start | bytes 786440 | tf_op jit(solution)/shard_map/ppermute | solution.py:17
  41.8 9.8 %collective-permute-start.2 = (bf16[2,128,512]{2,1,0:T(8,128)(2,1)S(1)}, bf16[2,128,512]{2,1,0:T(8,128)(2,1)S(1)}, u32[]{:S(2)}, u32[]{:S(2)}) collective-permute-start(bf16[2,128,512]{2,1,0:T(8,128)(2,1)S(1)} %collective-permute-done.1), channel_id=1, source_target_pairs={{0,2},{2,4},{4,6},{6,8},{8,10},{10,12},{12,14},{1,3},{3,5},{5,7},{... | collective-permute-start | bytes 786440 | tf_op jit(solution)/shard_map/ppermute | solution.py:17
  46.2 24.1 %copy-start.42 = (pred[128]{0:T(512)(128)(4,1)}, pred[128]{0:T(512)(128)(4,1)S(1)}, u32[]{:S(2)}) copy-start(pred[128]{0:T(512)(128)(4,1)S(1)} %add_compare_fusion) | copy-start | bytes 388
  47.2 13.2 %copy-start.11 = (bf16[1,128,512]{1,2,0:T(8,128)(2,1)}, bf16[1,128,512]{1,2,0:T(8,128)(2,1)S(1)}, u32[]{:S(2)}) copy-start(bf16[1,128,512]{1,2,0:T(8,128)(2,1)S(1)} %copy.26) | copy-start | bytes 393220
  49.3 8.3 %collective-permute-start.5 = (bf16[2,128,512]{2,1,0:T(8,128)(2,1)S(1)}, bf16[2,128,512]{2,1,0:T(8,128)(2,1)S(1)}, u32[]{:S(2)}, u32[]{:S(2)}) collective-permute-start(bf16[2,128,512]{2,1,0:T(8,128)(2,1)S(1)} %collective-permute-done.4), channel_id=1, source_target_pairs={{2,0},{4,2},{6,4},{8,6},{10,8},{12,10},{14,12},{3,1},{5,3},{7,5},{... | collective-permute-start | bytes 786440 | tf_op jit(solution)/shard_map/ppermute | solution.py:17
  68.5 9.7 %copy-start.13 = (bf16[1,128,1024]{2,1,0:T(8,128)(2,1)S(1)}, bf16[1,128,1024]{2,1,0:T(8,128)(2,1)}, u32[]{:S(2)}) copy-start(bf16[1,128,1024]{2,1,0:T(8,128)(2,1)} %param.10) | copy-start | bytes 786436
  68.5 9.7 %copy-start.18 = (f32[1,1024]{1,0:T(1,128)S(1)}, f32[1,1024]{1,0:T(1,128)}, u32[]{:S(2)}) copy-start(f32[1,1024]{1,0:T(1,128)} %get-tuple-element.66) | copy-start | bytes 12292
  68.5 9.7 %copy-start.19 = (f32[1,1024]{1,0:T(1,128)S(1)}, f32[1,1024]{1,0:T(1,128)}, u32[]{:S(2)}) copy-start(f32[1,1024]{1,0:T(1,128)} %get-tuple-element.67) | copy-start | bytes 12292
  68.5 9.7 %copy-start.20 = (f32[1,1024]{1,0:T(1,128)S(1)}, f32[1,1024]{1,0:T(1,128)}, u32[]{:S(2)}) copy-start(f32[1,1024]{1,0:T(1,128)} %get-tuple-element.68) | copy-start | bytes 12292
  68.5 9.7 %copy-start.21 = (f32[1,1024]{1,0:T(1,128)S(1)}, f32[1,1024]{1,0:T(1,128)}, u32[]{:S(2)}) copy-start(f32[1,1024]{1,0:T(1,128)} %get-tuple-element.69) | copy-start | bytes 12292
  68.5 9.7 %copy-start.22 = (f32[1,1024]{1,0:T(1,128)S(1)}, f32[1,1024]{1,0:T(1,128)}, u32[]{:S(2)}) copy-start(f32[1,1024]{1,0:T(1,128)} %get-tuple-element.70) | copy-start | bytes 12292
  68.5 9.7 %copy-start.23 = (f32[1,1024]{1,0:T(1,128)S(1)}, f32[1,1024]{1,0:T(1,128)}, u32[]{:S(2)}) copy-start(f32[1,1024]{1,0:T(1,128)} %get-tuple-element.71) | copy-start | bytes 12292
  68.5 9.7 %copy-start.24 = (f32[1,1024]{1,0:T(1,128)S(1)}, f32[1,1024]{1,0:T(1,128)}, u32[]{:S(2)}) copy-start(f32[1,1024]{1,0:T(1,128)} %get-tuple-element.72) | copy-start | bytes 12292
  68.5 9.7 %copy-start.25 = (f32[1,1024]{1,0:T(1,128)S(1)}, f32[1,1024]{1,0:T(1,128)}, u32[]{:S(2)}) copy-start(f32[1,1024]{1,0:T(1,128)} %get-tuple-element.73) | copy-start | bytes 12292
  68.5 9.7 %copy-start.26 = (f32[1,1024]{1,0:T(1,128)S(1)}, f32[1,1024]{1,0:T(1,128)}, u32[]{:S(2)}) copy-start(f32[1,1024]{1,0:T(1,128)} %get-tuple-element.74) | copy-start | bytes 12292
  68.5 9.7 %copy-start.27 = (f32[1,1024]{1,0:T(1,128)S(1)}, f32[1,1024]{1,0:T(1,128)}, u32[]{:S(2)}) copy-start(f32[1,1024]{1,0:T(1,128)} %get-tuple-element.75) | copy-start | bytes 12292
  68.5 9.7 %copy-start.28 = (f32[1,1024]{1,0:T(1,128)S(1)}, f32[1,1024]{1,0:T(1,128)}, u32[]{:S(2)}) copy-start(f32[1,1024]{1,0:T(1,128)} %get-tuple-element.76) | copy-start | bytes 12292
  68.6 9.7 %copy-start.29 = (f32[1,1024]{1,0:T(1,128)S(1)}, f32[1,1024]{1,0:T(1,128)}, u32[]{:S(2)}) copy-start(f32[1,1024]{1,0:T(1,128)} %get-tuple-element.77) | copy-start | bytes 12292
  68.6 9.7 %copy-start.30 = (f32[1,1024]{1,0:T(1,128)S(1)}, f32[1,1024]{1,0:T(1,128)}, u32[]{:S(2)}) copy-start(f32[1,1024]{1,0:T(1,128)} %get-tuple-element.78) | copy-start | bytes 12292
  68.6 9.7 %copy-start.31 = (f32[1,1024]{1,0:T(1,128)S(1)}, f32[1,1024]{1,0:T(1,128)}, u32[]{:S(2)}) copy-start(f32[1,1024]{1,0:T(1,128)} %get-tuple-element.79) | copy-start | bytes 12292
  68.6 9.7 %copy-start.32 = (f32[1,1024]{1,0:T(1,128)S(1)}, f32[1,1024]{1,0:T(1,128)}, u32[]{:S(2)}) copy-start(f32[1,1024]{1,0:T(1,128)} %get-tuple-element.80) | copy-start | bytes 12292
  70.7 28.0 %copy-start.5 = (bf16[128,1024]{1,0:T(8,128)(2,1)}, bf16[128,1024]{1,0:T(8,128)(2,1)S(1)}, u32[]{:S(2)}) copy-start(bf16[128,1024]{1,0:T(8,128)(2,1)S(1)} %fusion.4) | copy-start | bytes 786436
  70.7 7.0 %collective-permute-start.7 = (bf16[15,1024]{1,0:T(8,128)(2,1)S(1)}, bf16[15,1024]{1,0:T(8,128)(2,1)S(1)}, u32[]{:S(2)}, u32[]{:S(2)}) collective-permute-start(bf16[15,1024]{1,0:T(8,128)(2,1)S(1)} %get-tuple-element.61), channel_id=1, source_target_pairs={{2,0},{4,2},{6,4},{8,6},{10,8},{12,10},{14,12},{3,1},{5,3},{7,5},{... | collective-permute-start | bytes 92168 | tf_op jit(solution)/shard_map/ppermute | solution.py:30
  72.0 6.1 %collective-permute-start.6 = (bf16[15,1024]{1,0:T(8,128)(2,1)S(1)}, bf16[15,1024]{1,0:T(8,128)(2,1)S(1)}, u32[]{:S(2)}, u32[]{:S(2)}) collective-permute-start(bf16[15,1024]{1,0:T(8,128)(2,1)S(1)} %get-tuple-element.60), channel_id=1, source_target_pairs={{0,2},{2,4},{4,6},{6,8},{8,10},{10,12},{12,14},{1,3},{3,5},{5,7},{... | collective-permute-start | bytes 92168 | tf_op jit(solution)/shard_map/ppermute | solution.py:28
  77.7 19.1 %copy-start.16 = (bf16[15,1024]{1,0:T(8,128)(2,1)}, bf16[15,1024]{1,0:T(8,128)(2,1)S(1)}, u32[]{:S(2)}) copy-start(bf16[15,1024]{1,0:T(8,128)(2,1)S(1)} %collective-permute-done.7) | copy-start | bytes 92164
  78.1 18.6 %copy-start.14 = (bf16[15,1024]{1,0:T(8,128)(2,1)}, bf16[15,1024]{1,0:T(8,128)(2,1)S(1)}, u32[]{:S(2)}) copy-start(bf16[15,1024]{1,0:T(8,128)(2,1)S(1)} %collective-permute-done.6) | copy-start | bytes 92164
  82.4 5.8 %collective-permute-start.9 = (bf16[15,1024]{1,0:T(8,128)(2,1)S(1)}, bf16[15,1024]{1,0:T(8,128)(2,1)S(1)}, u32[]{:S(2)}, u32[]{:S(2)}) collective-permute-start(bf16[15,1024]{1,0:T(8,128)(2,1)S(1)} %get-tuple-element.59), channel_id=1, source_target_pairs={{0,2},{2,4},{4,6},{6,8},{8,10},{10,12},{12,14},{1,3},{3,5},{5,7},{... | collective-permute-start | bytes 92168 | tf_op jit(solution)/shard_map/ppermute | solution.py:28
  86.6 7.0 %collective-permute-start.8 = (bf16[15,1024]{1,0:T(8,128)(2,1)S(1)}, bf16[15,1024]{1,0:T(8,128)(2,1)S(1)}, u32[]{:S(2)}, u32[]{:S(2)}) collective-permute-start(bf16[15,1024]{1,0:T(8,128)(2,1)S(1)} %get-tuple-element.58), channel_id=1, source_target_pairs={{2,0},{4,2},{6,4},{8,6},{10,8},{12,10},{14,12},{3,1},{5,3},{7,5},{... | collective-permute-start | bytes 92168 | tf_op jit(solution)/shard_map/ppermute | solution.py:30
  114.7 21.2 %copy-start.6 = (bf16[128,1024]{1,0:T(8,128)(2,1)S(1)}, bf16[128,1024]{1,0:T(8,128)(2,1)}, u32[]{:S(2)}) copy-start(bf16[128,1024]{1,0:T(8,128)(2,1)} %copy-done.5) | copy-start | bytes 786436
  114.7 21.2 %copy-start.17 = (bf16[15,1024]{1,0:T(8,128)(2,1)S(1)}, bf16[15,1024]{1,0:T(8,128)(2,1)}, u32[]{:S(2)}) copy-start(bf16[15,1024]{1,0:T(8,128)(2,1)} %copy-done.16) | copy-start | bytes 92164
  114.7 21.7 %copy-start.15 = (bf16[15,1024]{1,0:T(8,128)(2,1)S(1)}, bf16[15,1024]{1,0:T(8,128)(2,1)}, u32[]{:S(2)}) copy-start(bf16[15,1024]{1,0:T(8,128)(2,1)} %copy-done.14) | copy-start | bytes 92164
  129.7 22.6 %collective-permute-start.13 = (f32[2,128,512]{1,2,0:T(8,128)S(1)}, f32[2,128,512]{1,2,0:T(8,128)S(1)}, u32[]{:S(2)}, u32[]{:S(2)}) collective-permute-start(f32[2,128,512]{1,2,0:T(8,128)S(1)} %bitcast.168), channel_id=1, source_target_pairs={{0,2},{2,4},{4,6},{6,8},{8,10},{10,12},{12,14},{1,3},{3,5},{5,7},{... | collective-permute-start | bytes 1572872 | tf_op jit(solution)/shard_map/ppermute | solution.py:17
  134.6 23.8 %collective-permute-start.10 = (f32[2,128,512]{1,2,0:T(8,128)S(1)}, f32[2,128,512]{1,2,0:T(8,128)S(1)}, u32[]{:S(2)}, u32[]{:S(2)}) collective-permute-start(f32[2,128,512]{1,2,0:T(8,128)S(1)} %bitcast.167), channel_id=1, source_target_pairs={{2,0},{4,2},{6,4},{8,6},{10,8},{12,10},{14,12},{3,1},{5,3},{7,5},{... | collective-permute-start | bytes 1572872 | tf_op jit(solution)/shard_map/ppermute | solution.py:17
  152.3 8.8 %copy-start.38 = (f32[1024]{0:T(1024)S(1)}, f32[1024]{0:T(1024)}, u32[]{:S(2)}) copy-start(f32[1024]{0:T(1024)} %get-tuple-element.20) | copy-start | bytes 12292
  152.3 8.8 %copy-start.39 = (f32[1024]{0:T(1024)S(1)}, f32[1024]{0:T(1024)}, u32[]{:S(2)}) copy-start(f32[1024]{0:T(1024)} %get-tuple-element.21) | copy-start | bytes 12292
  152.4 8.8 %copy-start.40 = (f32[1024]{0:T(1024)S(1)}, f32[1024]{0:T(1024)}, u32[]{:S(2)}) copy-start(f32[1024]{0:T(1024)} %get-tuple-element.22) | copy-start | bytes 12292
  152.4 8.8 %copy-start.41 = (f32[1024]{0:T(1024)S(1)}, f32[1024]{0:T(1024)}, u32[]{:S(2)}) copy-start(f32[1024]{0:T(1024)} %get-tuple-element.23) | copy-start | bytes 12292
  152.4 11.5 %copy-start.8 = (bf16[128,1024]{1,0:T(8,128)(2,1)S(1)}, bf16[128,1024]{1,0:T(8,128)(2,1)}, u32[]{:S(2)}) copy-start(bf16[128,1024]{1,0:T(8,128)(2,1)} %copy-done.7) | copy-start | bytes 786436
  153.2 23.3 %collective-permute-start.14 = (f32[2,128,512]{1,2,0:T(8,128)}, f32[2,128,512]{1,2,0:T(8,128)}, u32[]{:S(2)}, u32[]{:S(2)}) collective-permute-start(f32[2,128,512]{1,2,0:T(8,128)} %add.311), channel_id=1, source_target_pairs={{0,2},{2,4},{4,6},{6,8},{8,10},{10,12},{12,14},{1,3},{3,5},{5,7},{... | collective-permute-start | bytes 1572872 | tf_op jit(solution)/shard_map/ppermute | solution.py:17
  159.3 24.3 %collective-permute-start.11 = (f32[2,128,512]{1,2,0:T(8,128)}, f32[2,128,512]{1,2,0:T(8,128)S(1)}, u32[]{:S(2)}, u32[]{:S(2)}) collective-permute-start(f32[2,128,512]{1,2,0:T(8,128)} %add.308), channel_id=1, source_target_pairs={{2,0},{4,2},{6,4},{8,6},{10,8},{12,10},{14,12},{3,1},{5,3},{7,5},{... | collective-permute-start | bytes 1572872 | tf_op jit(solution)/shard_map/ppermute | solution.py:17
  178.4 92.4 %collective-permute-start.15 = (f32[2,128,512]{1,2,0:T(8,128)}, f32[2,128,512]{1,2,0:T(8,128)}, u32[]{:S(2)}, u32[]{:S(2)}) collective-permute-start(f32[2,128,512]{1,2,0:T(8,128)} %add.312), channel_id=1, source_target_pairs={{0,2},{2,4},{4,6},{6,8},{8,10},{10,12},{12,14},{1,3},{3,5},{5,7},{... | collective-permute-start | bytes 1572872 | tf_op jit(solution)/shard_map/ppermute | solution.py:17
  184.5 83.8 %copy-start.2 = (bf16[8,128,896]{1,2,0:T(8,128)(2,1)S(1)}, bf16[8,128,896]{1,2,0:T(8,128)(2,1)}, u32[]{:S(2)}) copy-start(bf16[8,128,896]{1,2,0:T(8,128)(2,1)} %copy-done.1) | copy-start | bytes 5505028
  184.5 86.3 %collective-permute-start.12 = (f32[2,128,512]{1,2,0:T(8,128)}, f32[2,128,512]{1,2,0:T(8,128)}, u32[]{:S(2)}, u32[]{:S(2)}) collective-permute-start(f32[2,128,512]{1,2,0:T(8,128)} %add.309), channel_id=1, source_target_pairs={{2,0},{4,2},{6,4},{8,6},{10,8},{12,10},{14,12},{3,1},{5,3},{7,5},{... | collective-permute-start | bytes 1572872 | tf_op jit(solution)/shard_map/ppermute | solution.py:17
  (12 other events, 57.8 us)
Sparse Core Ops, SparseCore 0:
  164.0 89.8 all-reduce.2
where the time goes:
time: 283 us; the launch traced here: 282 us
  blocking collectives  82.4 us (29%)
  waiting for transfers between devices  58.9 us (21%)
  starting transfers between devices  48.3 us (17%)
  local copies, waits for them, and re-layouts  45.9 us (16%)
  other arithmetic  17.3 us (6%)
  between operations  15.5 us (5%)
  matrix products  13.8 us (5%)
    psum x1, blocking collectives, on_device(): proj_sum, kernel_sum = lax.psum((proj_local, kernel_local), ('ctx', 'dp'))  82.4 us
    ppermute x12, waiting for transfers between devices, passed_along(): return lax.ppermute(block, axis, route)  52.9 us
    ppermute x12, starting transfers between devices, passed_along(): return lax.ppermute(block, axis, route)  36.7 us
    slice x1, local copies, waits for them, and re-layouts, give_back(): moving = shifter(moving, -1) + partials[offset]  15 us
    unnamed x99, local copies, waits for them, and re-layouts  9.63 us
    ppermute x2, starting transfers between devices, padded(): lax.ppermute(tail, axis, [(i, (i + 1) % count) for i in range(ends)])  8.79 us
    reduce_sum x4, other arithmetic, on_device(): jnp.sum(padded_m[tap_index:tap_index + tokens].astype(jnp.float32) * grad...  5.83 us
  transfers between devices with their start and end apart: 17, of which 9 were waited for; matrix products, arithmetic and copies ran while one was open for 7% of the time, Pallas kernels for 0%

commit v1 on v0

--- a/solution.py
+++ b/solution.py
@@ -35,29 +35,17 @@
 
 
 def collect(piece_own, shifter):
-    from_below = []
-    from_above = []
-    moving = piece_own
-    for repeat in range(REACH):
-        moving = shifter(moving, 1)
-        from_below.append(moving)
-    moving = piece_own
-    for repeat in range(REACH):
-        moving = shifter(moving, -1)
-        from_above.append(moving)
-    return jnp.stack(from_below[::-1] + [piece_own] + from_above, axis=0)
+    from_below = [shifter(piece_own, distance) for distance in range(REACH, 0, -1)]
+    from_above = [shifter(piece_own, -distance) for distance in range(1, REACH + 1)]
+    return jnp.stack(from_below + [piece_own] + from_above, axis=0)
 
 
 def give_back(partials, shifter):
-    moving = partials[0]
-    for offset in range(1, REACH):
-        moving = shifter(moving, -1) + partials[offset]
-    from_below = shifter(moving, -1)
-    moving = partials[2 * REACH]
-    for offset in range(2 * REACH - 1, REACH, -1):
-        moving = shifter(moving, 1) + partials[offset]
-    from_above = shifter(moving, 1)
-    return partials[REACH] + from_below + from_above
+    total = partials[REACH]
+    for offset in range(2 * REACH + 1):
+        if offset != REACH:
+            total = total + shifter(partials[offset], offset - REACH)
+    return total
 
 
 def on_device(queries, key_rows, values, cotangent, out_proj, conv_kernel, lengths):
@@ -131,7 +119,9 @@
     proj_local = lax.dot_general(
         attended, grad_hidden, (((0,), (0,)), ((), ())), preferred_element_type=jnp.float32
     )
-    proj_sum, kernel_sum = lax.psum((proj_local, kernel_local), ("ctx", "dp"))
+    proj_part = lax.psum_scatter(proj_local, ("ctx", "dp"), scatter_dimension=0, tiled=True)
+    proj_sum = lax.all_gather(proj_part.astype(jnp.bfloat16), ("ctx", "dp"), axis=0, tiled=True)
+    kernel_sum = lax.psum(kernel_local, ("ctx", "dp"))
     grad_attended = lax.dot_general(
         grad_hidden, out_proj, (((1,), (1,)), ((), ())), preferred_element_type=jnp.float32
     ).astype(jnp.bfloat16)
@@ -176,7 +166,7 @@
         grad_query[None],
         grad_key[None],
         grad_value[None],
-        proj_sum.astype(jnp.bfloat16),
+        proj_sum,
         kernel_sum,
     )
 

time: 283 us -> 317 us (1.12)
  the two profiles are of different devices: /device:TPU:0 before, /device:TPU:2 now
where the time goes in v1:
time: 317 us; the launch traced here: 313 us
  waiting for transfers between devices  171 us (54%)
  local copies, waits for them, and re-layouts  50.2 us (16%)
  starting transfers between devices  47.7 us (15%)
  between operations  15.3 us (5%)
  other arithmetic  14.2 us (4%)
  matrix products  14 us (4%)
    psum x1, waiting for transfers between devices, on_device(): kernel_sum = lax.psum(kernel_local, ('ctx', 'dp'))  61.3 us
    ppermute x12, waiting for transfers between devices, passed_along(): return lax.ppermute(block, axis, route)  58.5 us
    reduce_scatter x1, waiting for transfers between devices, on_device(): lax.psum_scatter(proj_local, ('ctx', 'dp'), scatter_dimension=0, tiled=True)  46.1 us
    ppermute x12, starting transfers between devices, passed_along(): return lax.ppermute(block, axis, route)  33.7 us
    slice x1, local copies, waits for them, and re-layouts, give_back(): total = total + shifter(partials[offset], offset - REACH)  15.1 us
    unnamed x100, local copies, waits for them, and re-layouts  13.3 us
    ppermute x2, starting transfers between devices, padded(): lax.ppermute(tail, axis, [(i, (i + 1) % count) for i in range(ends)])  9.95 us
  transfers between devices with their start and end apart: 19, of which 11 were waited for; matrix products, arithmetic and copies ran while one was open for 15% of the time, Pallas kernels for 0%

profile of v1, /device:TPU:2, one launch (start us, length us, event | category | flops | bytes accessed | tf_op | source)
XLA Modules:
  0.0 312.6 jit_solution(5518717356108394734)
XLA Ops:
  9.1 4.5 %collective-permute-start = (bf16[2,128,512]{2,1,0:T(8,128)(2,1)S(1)}, bf16[2,128,512]{2,1,0:T(8,128)(2,1)S(1)}, u32[]{:S(2)}, u32[]{:S(2)}) collective-permute-start(bf16[2,128,512]{2,1,0:T(8,128)(2,1)S(1)} %constant_dynamic-update-slice_fusion), channel_id=1, source_target_pairs={{0,6},{2,8},{4,10},{6,12},{8,14},{1,7},{3,9},{5,11},{7,13},{9,15},... | collective-permute-start | bytes 786440 | tf_op jit(solution)/shard_map/ppermute | solution.py:17
  13.6 3.5 %collective-permute-start.1 = (bf16[2,128,512]{2,1,0:T(8,128)(2,1)S(1)}, bf16[2,128,512]{2,1,0:T(8,128)(2,1)S(1)}, u32[]{:S(2)}, u32[]{:S(2)}) collective-permute-start(bf16[2,128,512]{2,1,0:T(8,128)(2,1)S(1)} %constant_dynamic-update-slice_fusion), channel_id=1, source_target_pairs={{0,4},{2,6},{4,8},{6,10},{8,12},{10,14},{1,5},{3,7},{5,9},{7,11},{... | collective-permute-start | bytes 786440 | tf_op jit(solution)/shard_map/ppermute | solution.py:17
  17.1 3.4 %collective-permute-start.2 = (bf16[2,128,512]{2,1,0:T(8,128)(2,1)S(1)}, bf16[2,128,512]{2,1,0:T(8,128)(2,1)S(1)}, u32[]{:S(2)}, u32[]{:S(2)}) collective-permute-start(bf16[2,128,512]{2,1,0:T(8,128)(2,1)S(1)} %constant_dynamic-update-slice_fusion), channel_id=1, source_target_pairs={{0,2},{2,4},{4,6},{6,8},{8,10},{10,12},{12,14},{1,3},{3,5},{5,7},{... | collective-permute-start | bytes 786440 | tf_op jit(solution)/shard_map/ppermute | solution.py:17
  20.5 2.5 collective-permute-start.3
  23.0 1.3 collective-permute-start.4
  24.3 2.0 fusion.150
  28.1 1.3 collective-permute-start.5
  29.4 2.3 collective-permute-done.2
  32.5 14.6 %collective-permute-done.5 = bf16[2,128,512]{2,1,0:T(8,128)(2,1)S(1)} collective-permute-done((bf16[2,128,512]{2,1,0:T(8,128)(2,1)S(1)}, bf16[2,128,512]{2,1,0:T(8,128)(2,1)S(1)}, u32[]{:S(2)}, u32[]{:S(2)}) %collective-permute-start.5) | collective-permute-done | bytes 262176 | tf_op jit(solution)/shard_map/ppermute | solution.py:17
  52.7 2.4 copy.27
  55.2 2.9 reshape_squeeze.11
  58.2 1.7 convolution_convert_fusion
  60.3 1.9 collective-permute-start.7
  62.2 4.8 %collective-permute-start.6 = (bf16[15,1024]{1,0:T(8,128)(2,1)S(1)}, bf16[15,1024]{1,0:T(8,128)(2,1)S(1)}, u32[]{:S(2)}, u32[]{:S(2)}) collective-permute-start(bf16[15,1024]{1,0:T(8,128)(2,1)S(1)} %get-tuple-element.60), channel_id=1, source_target_pairs={{0,2},{2,4},{4,6},{6,8},{8,10},{10,12},{12,14},{1,3},{3,5},{5,7},{... | collective-permute-start | bytes 92168 | tf_op jit(solution)/shard_map/ppermute | solution.py:28
  67.0 1.1 fusion.151
  68.8 4.1 %fusion.84 = (f32[1024]{0:T(1024)}, f32[1024]{0:T(1024)}, f32[1024]{0:T(1024)}, f32[1024]{0:T(1024)}, f32[1024]{0:T(1024)}, /*index=5*/f32[1024]{0:T(1024)}, f32...) fusion(bf16[15,1024]{1,0:T(8,128)(2,1)S(1)} %collective-permute-done.7, ...), kind=kLoop, calls=%fused_computation.216 | loop fusion | flops 31841280 | bytes 1011712 | tf_op jit(solution)/shard_map/reduce_sum | solution.py:111
  72.9 5.1 %collective-permute-start.9 = (bf16[15,1024]{1,0:T(8,128)(2,1)S(1)}, bf16[15,1024]{1,0:T(8,128)(2,1)S(1)}, u32[]{:S(2)}, u32[]{:S(2)}) collective-permute-start(bf16[15,1024]{1,0:T(8,128)(2,1)S(1)} %get-tuple-element.59), channel_id=1, source_target_pairs={{0,2},{2,4},{4,6},{6,8},{8,10},{10,12},{12,14},{1,3},{3,5},{5,7},{... | collective-permute-start | bytes 92168 | tf_op jit(solution)/shard_map/ppermute | solution.py:28
  78.0 1.9 collective-permute-start.8
  80.0 4.8 %collective-permute-done.8 = bf16[15,1024]{1,0:T(8,128)(2,1)S(1)} collective-permute-done((bf16[15,1024]{1,0:T(8,128)(2,1)S(1)}, bf16[15,1024]{1,0:T(8,128)(2,1)S(1)}, u32[]{:S(2)}, u32[]{:S(2)}) %collective-permute-start.8) | collective-permute-done | bytes 30752 | tf_op jit(solution)/shard_map/ppermute | solution.py:30
  84.7 3.1 fusion.37
  88.6 1.8 fusion.152
  91.3 1.1 convolution_convert_fusion.1
  93.5 2.2 multiply_convert_fusion
  95.7 1.2 copy-done.1
  97.0 2.1 multiply_bitcast_fusion
  99.0 2.8 stack_reshape.6
  101.8 2.1 convolution_bitcast_fusion
  103.9 46.1 %reduce-scatter.2.cloned.1.call-done = f32[32,1024]{1,0:T(8,128)} async-done(((f32[512,1024]{1,0:T(8,128)}), f32[32,1024]{1,0:T(8,128)}) %reduce-scatter.2.cloned.1.call-update) | async-done | bytes 131088 | tf_op jit(solution)/shard_map/reduce_scatter | solution.py:122
  150.1 1.5 convert_element_type.366
  151.7 3.1 constant_dynamic-update-slice_fusion.3
  154.8 1.6 stack_reshape.7
  156.4 1.4 constant_dynamic-update-slice_fusion.2
  157.8 15.1 %fusion.145 = (f32[1,2,128,512]{2,0,3,1:T(1,128)}, f32[1,2,128,512]{2,0,3,1:T(1,128)}, f32[1,2,128,512]{2,0,3,1:T(1,128)}, f32[1,2,128,512]{2,0,3,1:T(1,128)}, f...) fusion(f32[7,2,128,512]{2,0,3,1:T(8,128)} %constant_dynamic-update-slice_fusion.2), kind=kLoop, calls=%fused_computation.316 | loop fusion | bytes 7340032 | tf_op jit(solution)/shard_map/slice | solution.py:47
  173.0 3.9 %collective-permute-start.15 = (f32[2,128,512]{1,2,0:T(8,128)S(1)}, f32[2,128,512]{1,2,0:T(8,128)S(1)}, u32[]{:S(2)}, u32[]{:S(2)}) collective-permute-start(f32[2,128,512]{1,2,0:T(8,128)S(1)} %bitcast.163), channel_id=1, source_target_pairs={{0,6},{2,8},{4,10},{6,12},{8,14},{1,7},{3,9},{5,11},{7,13},{9,15},... | collective-permute-start | bytes 1572872 | tf_op jit(solution)/shard_map/ppermute | solution.py:17
  178.2 4.2 %collective-permute-start.14 = (f32[2,128,512]{1,2,0:T(8,128)}, f32[2,128,512]{1,2,0:T(8,128)}, u32[]{:S(2)}, u32[]{:S(2)}) collective-permute-start(f32[2,128,512]{1,2,0:T(8,128)} %bitcast.56), channel_id=1, source_target_pairs={{0,4},{2,6},{4,8},{6,10},{8,12},{10,14},{1,5},{3,7},{5,9},{7,11},{... | collective-permute-start | bytes 1572872 | tf_op jit(solution)/shard_map/ppermute | solution.py:17
  182.4 1.9 collective-permute-start.13
  184.3 4.7 %collective-permute-start.12 = (f32[2,128,512]{1,2,0:T(8,128)}, f32[2,128,512]{1,2,0:T(8,128)}, u32[]{:S(2)}, u32[]{:S(2)}) collective-permute-start(f32[2,128,512]{1,2,0:T(8,128)} %bitcast.54), channel_id=1, source_target_pairs={{2,0},{4,2},{6,4},{8,6},{10,8},{12,10},{14,12},{3,1},{5,3},{7,5},{... | collective-permute-start | bytes 1572872 | tf_op jit(solution)/shard_map/ppermute | solution.py:17
  189.0 1.3 collective-permute-start.11
  190.3 1.7 collective-permute-done.15
  192.0 1.3 collective-permute-start.10
  193.9 2.7 stack.167
  196.6 1.7 fusion.5
  199.0 4.3 %collective-permute-done.14 = f32[2,128,512]{1,2,0:T(8,128)} collective-permute-done((f32[2,128,512]{1,2,0:T(8,128)}, f32[2,128,512]{1,2,0:T(8,128)}, u32[]{:S(2)}, u32[]{:S(2)}) %collective-permute-start.14) | collective-permute-done | bytes 524320 | tf_op jit(solution)/shard_map/ppermute | solution.py:17
  203.3 17.2 %collective-permute-done.13 = f32[2,128,512]{1,2,0:T(8,128)} collective-permute-done((f32[2,128,512]{1,2,0:T(8,128)}, f32[2,128,512]{1,2,0:T(8,128)}, u32[]{:S(2)}, u32[]{:S(2)}) %collective-permute-start.13) | collective-permute-done | bytes 524320 | tf_op jit(solution)/shard_map/ppermute | solution.py:17
  220.5 17.7 %collective-permute-done.10 = f32[2,128,512]{1,2,0:T(8,128)} collective-permute-done((f32[2,128,512]{1,2,0:T(8,128)}, f32[2,128,512]{1,2,0:T(8,128)}, u32[]{:S(2)}, u32[]{:S(2)}) %collective-permute-start.10) | collective-permute-done | bytes 524320 | tf_op jit(solution)/shard_map/ppermute | solution.py:17
  238.3 2.0 add_convert_fusion
  241.8 61.3 %all-reduce.2.cloned.1.call-done = f32[31,1024]{1,0:T(8,128)} async-done(((f32[31,1024]{1,0:T(8,128)}), f32[31,1024]{1,0:T(8,128)}) %all-reduce.2.cloned.1.call-update) | async-done | bytes 126992 | tf_op jit(solution)/shard_map/psum | solution.py:124
  303.1 2.3 copy.65
  (133 shorter events, 17.8 us)
Async XLA Ops:
  7.2 52.7 %copy-start = (bf16[512,1024]{1,0:T(8,128)(2,1)S(1)}, bf16[512,1024]{1,0:T(8,128)(2,1)}, u32[]{:S(2)}) copy-start(bf16[512,1024]{1,0:T(8,128)(2,1)} %param.11) | copy-start | bytes 3145732
  7.2 142.9 %reduce-scatter.2.cloned.1.call-start = ((), (), s32[]{:S(2)}) async-start(), calls=%async_computation.1 | async-start | bytes 2228224 | tf_op jit(solution)/shard_map/reduce_scatter | solution.py:122
  9.1 18.9 %collective-permute-start = (bf16[2,128,512]{2,1,0:T(8,128)(2,1)S(1)}, bf16[2,128,512]{2,1,0:T(8,128)(2,1)S(1)}, u32[]{:S(2)}, u32[]{:S(2)}) collective-permute-start(bf16[2,128,512]{2,1,0:T(8,128)(2,1)S(1)} %constant_dynamic-update-slice_fusion), channel_id=1, source_target_pairs={{0,6},{2,8},{4,10},{6,12},{8,14},{1,7},{3,9},{5,11},{7,13},{9,15},... | collective-permute-start | bytes 786440 | tf_op jit(solution)/shard_map/ppermute | solution.py:17
  13.6 15.8 %collective-permute-start.1 = (bf16[2,128,512]{2,1,0:T(8,128)(2,1)S(1)}, bf16[2,128,512]{2,1,0:T(8,128)(2,1)S(1)}, u32[]{:S(2)}, u32[]{:S(2)}) collective-permute-start(bf16[2,128,512]{2,1,0:T(8,128)(2,1)S(1)} %constant_dynamic-update-slice_fusion), channel_id=1, source_target_pairs={{0,4},{2,6},{4,8},{6,10},{8,12},{10,14},{1,5},{3,7},{5,9},{7,11},{... | collective-permute-start | bytes 786440 | tf_op jit(solution)/shard_map/ppermute | solution.py:17
  17.1 14.6 %collective-permute-start.2 = (bf16[2,128,512]{2,1,0:T(8,128)(2,1)S(1)}, bf16[2,128,512]{2,1,0:T(8,128)(2,1)S(1)}, u32[]{:S(2)}, u32[]{:S(2)}) collective-permute-start(bf16[2,128,512]{2,1,0:T(8,128)(2,1)S(1)} %constant_dynamic-update-slice_fusion), channel_id=1, source_target_pairs={{0,2},{2,4},{4,6},{6,8},{8,10},{10,12},{12,14},{1,3},{3,5},{5,7},{... | collective-permute-start | bytes 786440 | tf_op jit(solution)/shard_map/ppermute | solution.py:17
  20.5 12.0 %collective-permute-start.3 = (bf16[2,128,512]{2,1,0:T(8,128)(2,1)S(1)}, bf16[2,128,512]{2,1,0:T(8,128)(2,1)S(1)}, u32[]{:S(2)}, u32[]{:S(2)}) collective-permute-start(bf16[2,128,512]{2,1,0:T(8,128)(2,1)S(1)} %constant_dynamic-update-slice_fusion), channel_id=1, source_target_pairs={{2,0},{4,2},{6,4},{8,6},{10,8},{12,10},{14,12},{3,1},{5,3},{7,5},{... | collective-permute-start | bytes 786440 | tf_op jit(solution)/shard_map/ppermute | solution.py:17
  23.0 9.5 %collective-permute-start.4 = (bf16[2,128,512]{2,1,0:T(8,128)(2,1)S(1)}, bf16[2,128,512]{2,1,0:T(8,128)(2,1)S(1)}, u32[]{:S(2)}, u32[]{:S(2)}) collective-permute-start(bf16[2,128,512]{2,1,0:T(8,128)(2,1)S(1)} %constant_dynamic-update-slice_fusion), channel_id=1, source_target_pairs={{4,0},{6,2},{8,4},{10,6},{12,8},{14,10},{5,1},{7,3},{9,5},{11,7},{... | collective-permute-start | bytes 786440 | tf_op jit(solution)/shard_map/ppermute | solution.py:17
  27.0 32.9 %copy-start.42 = (pred[128]{0:T(512)(128)(4,1)}, pred[128]{0:T(512)(128)(4,1)S(1)}, u32[]{:S(2)}) copy-start(pred[128]{0:T(512)(128)(4,1)S(1)} %add_compare_fusion) | copy-start | bytes 388
  28.0 22.0 %copy-start.9 = (bf16[1,128,512]{1,2,0:T(8,128)(2,1)}, bf16[1,128,512]{1,2,0:T(8,128)(2,1)S(1)}, u32[]{:S(2)}) copy-start(bf16[1,128,512]{1,2,0:T(8,128)(2,1)S(1)} %copy.26) | copy-start | bytes 393220
  28.1 19.1 %collective-permute-start.5 = (bf16[2,128,512]{2,1,0:T(8,128)(2,1)S(1)}, bf16[2,128,512]{2,1,0:T(8,128)(2,1)S(1)}, u32[]{:S(2)}, u32[]{:S(2)}) collective-permute-start(bf16[2,128,512]{2,1,0:T(8,128)(2,1)S(1)} %constant_dynamic-update-slice_fusion), channel_id=1, source_target_pairs={{6,0},{8,2},{10,4},{12,6},{14,8},{7,1},{9,3},{11,5},{13,7},{15,9},... | collective-permute-start | bytes 786440 | tf_op jit(solution)/shard_map/ppermute | solution.py:17
  58.1 10.6 %copy-start.21 = (f32[1,1024]{1,0:T(1,128)S(1)}, f32[1,1024]{1,0:T(1,128)}, u32[]{:S(2)}) copy-start(f32[1,1024]{1,0:T(1,128)} %get-tuple-element.69) | copy-start | bytes 12292
  58.1 10.6 %copy-start.22 = (f32[1,1024]{1,0:T(1,128)S(1)}, f32[1,1024]{1,0:T(1,128)}, u32[]{:S(2)}) copy-start(f32[1,1024]{1,0:T(1,128)} %get-tuple-element.70) | copy-start | bytes 12292
  58.1 10.6 %copy-start.23 = (f32[1,1024]{1,0:T(1,128)S(1)}, f32[1,1024]{1,0:T(1,128)}, u32[]{:S(2)}) copy-start(f32[1,1024]{1,0:T(1,128)} %get-tuple-element.71) | copy-start | bytes 12292
  58.1 10.6 %copy-start.24 = (f32[1,1024]{1,0:T(1,128)S(1)}, f32[1,1024]{1,0:T(1,128)}, u32[]{:S(2)}) copy-start(f32[1,1024]{1,0:T(1,128)} %get-tuple-element.72) | copy-start | bytes 12292
  58.1 10.6 %copy-start.25 = (f32[1,1024]{1,0:T(1,128)S(1)}, f32[1,1024]{1,0:T(1,128)}, u32[]{:S(2)}) copy-start(f32[1,1024]{1,0:T(1,128)} %get-tuple-element.73) | copy-start | bytes 12292
  58.1 10.6 %copy-start.26 = (f32[1,1024]{1,0:T(1,128)S(1)}, f32[1,1024]{1,0:T(1,128)}, u32[]{:S(2)}) copy-start(f32[1,1024]{1,0:T(1,128)} %get-tuple-element.74) | copy-start | bytes 12292
  58.1 10.6 %copy-start.27 = (f32[1,1024]{1,0:T(1,128)S(1)}, f32[1,1024]{1,0:T(1,128)}, u32[]{:S(2)}) copy-start(f32[1,1024]{1,0:T(1,128)} %get-tuple-element.75) | copy-start | bytes 12292
  58.2 10.6 %copy-start.28 = (f32[1,1024]{1,0:T(1,128)S(1)}, f32[1,1024]{1,0:T(1,128)}, u32[]{:S(2)}) copy-start(f32[1,1024]{1,0:T(1,128)} %get-tuple-element.76) | copy-start | bytes 12292
  58.2 10.6 %copy-start.29 = (f32[1,1024]{1,0:T(1,128)S(1)}, f32[1,1024]{1,0:T(1,128)}, u32[]{:S(2)}) copy-start(f32[1,1024]{1,0:T(1,128)} %get-tuple-element.77) | copy-start | bytes 12292
  60.3 30.1 %copy-start.4 = (bf16[128,1024]{1,0:T(8,128)(2,1)}, bf16[128,1024]{1,0:T(8,128)(2,1)S(1)}, u32[]{:S(2)}) copy-start(bf16[128,1024]{1,0:T(8,128)(2,1)S(1)} %fusion.4) | copy-start | bytes 786436
  60.3 7.9 %collective-permute-start.7 = (bf16[15,1024]{1,0:T(8,128)(2,1)S(1)}, bf16[15,1024]{1,0:T(8,128)(2,1)S(1)}, u32[]{:S(2)}, u32[]{:S(2)}) collective-permute-start(bf16[15,1024]{1,0:T(8,128)(2,1)S(1)} %get-tuple-element.61), channel_id=1, source_target_pairs={{2,0},{4,2},{6,4},{8,6},{10,8},{12,10},{14,12},{3,1},{5,3},{7,5},{... | collective-permute-start | bytes 92168 | tf_op jit(solution)/shard_map/ppermute | solution.py:30
  62.2 6.4 %collective-permute-start.6 = (bf16[15,1024]{1,0:T(8,128)(2,1)S(1)}, bf16[15,1024]{1,0:T(8,128)(2,1)S(1)}, u32[]{:S(2)}, u32[]{:S(2)}) collective-permute-start(bf16[15,1024]{1,0:T(8,128)(2,1)S(1)} %get-tuple-element.60), channel_id=1, source_target_pairs={{0,2},{2,4},{4,6},{6,8},{8,10},{10,12},{12,14},{1,3},{3,5},{5,7},{... | collective-permute-start | bytes 92168 | tf_op jit(solution)/shard_map/ppermute | solution.py:28
  68.2 19.7 %copy-start.15 = (bf16[15,1024]{1,0:T(8,128)(2,1)}, bf16[15,1024]{1,0:T(8,128)(2,1)S(1)}, u32[]{:S(2)}) copy-start(bf16[15,1024]{1,0:T(8,128)(2,1)S(1)} %collective-permute-done.7) | copy-start | bytes 92164
  68.6 19.3 %copy-start.13 = (bf16[15,1024]{1,0:T(8,128)(2,1)}, bf16[15,1024]{1,0:T(8,128)(2,1)S(1)}, u32[]{:S(2)}) copy-start(bf16[15,1024]{1,0:T(8,128)(2,1)S(1)} %collective-permute-done.6) | copy-start | bytes 92164
  72.9 7.1 %collective-permute-start.9 = (bf16[15,1024]{1,0:T(8,128)(2,1)S(1)}, bf16[15,1024]{1,0:T(8,128)(2,1)S(1)}, u32[]{:S(2)}, u32[]{:S(2)}) collective-permute-start(bf16[15,1024]{1,0:T(8,128)(2,1)S(1)} %get-tuple-element.59), channel_id=1, source_target_pairs={{0,2},{2,4},{4,6},{6,8},{8,10},{10,12},{12,14},{1,3},{3,5},{5,7},{... | collective-permute-start | bytes 92168 | tf_op jit(solution)/shard_map/ppermute | solution.py:28
  78.0 6.7 %collective-permute-start.8 = (bf16[15,1024]{1,0:T(8,128)(2,1)S(1)}, bf16[15,1024]{1,0:T(8,128)(2,1)S(1)}, u32[]{:S(2)}, u32[]{:S(2)}) collective-permute-start(bf16[15,1024]{1,0:T(8,128)(2,1)S(1)} %get-tuple-element.58), channel_id=1, source_target_pairs={{2,0},{4,2},{6,4},{8,6},{10,8},{12,10},{14,12},{3,1},{5,3},{7,5},{... | collective-permute-start | bytes 92168 | tf_op jit(solution)/shard_map/ppermute | solution.py:30
  90.4 151.5 %all-gather.2.cloned.1.call-start = ((), (), s32[]{:S(2)}) async-start(), calls=%async_computation.2 | async-start | bytes 1114112 | tf_op jit(solution)/shard_map/all_gather | solution.py:123
  151.6 151.5 %all-reduce.2.cloned.1.call-start = ((), (), s32[]{:S(2)}) async-start(), calls=%async_computation.3 | async-start | bytes 262144 | tf_op jit(solution)/shard_map/psum | solution.py:124
  157.8 19.1 %copy-start.5 = (bf16[128,1024]{1,0:T(8,128)(2,1)S(1)}, bf16[128,1024]{1,0:T(8,128)(2,1)}, u32[]{:S(2)}) copy-start(bf16[128,1024]{1,0:T(8,128)(2,1)} %copy-done.4) | copy-start | bytes 786436
  157.8 19.1 %copy-start.16 = (bf16[15,1024]{1,0:T(8,128)(2,1)S(1)}, bf16[15,1024]{1,0:T(8,128)(2,1)}, u32[]{:S(2)}) copy-start(bf16[15,1024]{1,0:T(8,128)(2,1)} %copy-done.15) | copy-start | bytes 92164
  157.8 19.7 %copy-start.14 = (bf16[15,1024]{1,0:T(8,128)(2,1)S(1)}, bf16[15,1024]{1,0:T(8,128)(2,1)}, u32[]{:S(2)}) copy-start(bf16[15,1024]{1,0:T(8,128)(2,1)} %copy-done.13) | copy-start | bytes 92164
  172.9 20.9 %copy-start.33 = (f32[1024]{0:T(1024)S(1)}, f32[1024]{0:T(1024)}, u32[]{:S(2)}) copy-start(f32[1024]{0:T(1024)} %get-tuple-element.15) | copy-start | bytes 12292
  172.9 20.9 %copy-start.34 = (f32[1024]{0:T(1024)S(1)}, f32[1024]{0:T(1024)}, u32[]{:S(2)}) copy-start(f32[1024]{0:T(1024)} %get-tuple-element.16) | copy-start | bytes 12292
  173.0 20.9 %copy-start.35 = (f32[1024]{0:T(1024)S(1)}, f32[1024]{0:T(1024)}, u32[]{:S(2)}) copy-start(f32[1024]{0:T(1024)} %get-tuple-element.17) | copy-start | bytes 12292
  173.0 20.9 %copy-start.36 = (f32[1024]{0:T(1024)S(1)}, f32[1024]{0:T(1024)}, u32[]{:S(2)}) copy-start(f32[1024]{0:T(1024)} %get-tuple-element.18) | copy-start | bytes 12292
  173.0 20.9 %copy-start.37 = (f32[1024]{0:T(1024)S(1)}, f32[1024]{0:T(1024)}, u32[]{:S(2)}) copy-start(f32[1024]{0:T(1024)} %get-tuple-element.19) | copy-start | bytes 12292
  173.0 20.9 %copy-start.38 = (f32[1024]{0:T(1024)S(1)}, f32[1024]{0:T(1024)}, u32[]{:S(2)}) copy-start(f32[1024]{0:T(1024)} %get-tuple-element.20) | copy-start | bytes 12292
  173.0 20.9 %copy-start.39 = (f32[1024]{0:T(1024)S(1)}, f32[1024]{0:T(1024)}, u32[]{:S(2)}) copy-start(f32[1024]{0:T(1024)} %get-tuple-element.21) | copy-start | bytes 12292
  173.0 20.9 %copy-start.40 = (f32[1024]{0:T(1024)S(1)}, f32[1024]{0:T(1024)}, u32[]{:S(2)}) copy-start(f32[1024]{0:T(1024)} %get-tuple-element.22) | copy-start | bytes 12292
  173.0 20.9 %copy-start.41 = (f32[1024]{0:T(1024)S(1)}, f32[1024]{0:T(1024)}, u32[]{:S(2)}) copy-start(f32[1024]{0:T(1024)} %get-tuple-element.23) | copy-start | bytes 12292
  173.0 23.6 %copy-start.2 = (bf16[8,128,896]{1,2,0:T(8,128)(2,1)S(1)}, bf16[8,128,896]{1,2,0:T(8,128)(2,1)}, u32[]{:S(2)}) copy-start(bf16[8,128,896]{1,2,0:T(8,128)(2,1)} %copy-done.1) | copy-start | bytes 5505028
  173.0 19.0 %collective-permute-start.15 = (f32[2,128,512]{1,2,0:T(8,128)S(1)}, f32[2,128,512]{1,2,0:T(8,128)S(1)}, u32[]{:S(2)}, u32[]{:S(2)}) collective-permute-start(f32[2,128,512]{1,2,0:T(8,128)S(1)} %bitcast.163), channel_id=1, source_target_pairs={{0,6},{2,8},{4,10},{6,12},{8,14},{1,7},{3,9},{5,11},{7,13},{9,15},... | collective-permute-start | bytes 1572872 | tf_op jit(solution)/shard_map/ppermute | solution.py:17
  178.2 25.1 %collective-permute-start.14 = (f32[2,128,512]{1,2,0:T(8,128)}, f32[2,128,512]{1,2,0:T(8,128)}, u32[]{:S(2)}, u32[]{:S(2)}) collective-permute-start(f32[2,128,512]{1,2,0:T(8,128)} %bitcast.56), channel_id=1, source_target_pairs={{0,4},{2,6},{4,8},{6,10},{8,12},{10,14},{1,5},{3,7},{5,9},{7,11},{... | collective-permute-start | bytes 1572872 | tf_op jit(solution)/shard_map/ppermute | solution.py:17
  182.4 38.1 %collective-permute-start.13 = (f32[2,128,512]{1,2,0:T(8,128)}, f32[2,128,512]{1,2,0:T(8,128)}, u32[]{:S(2)}, u32[]{:S(2)}) collective-permute-start(f32[2,128,512]{1,2,0:T(8,128)} %bitcast.55), channel_id=1, source_target_pairs={{0,2},{2,4},{4,6},{6,8},{8,10},{10,12},{12,14},{1,3},{3,5},{5,7},{... | collective-permute-start | bytes 1572872 | tf_op jit(solution)/shard_map/ppermute | solution.py:17
  184.3 36.2 %collective-permute-start.12 = (f32[2,128,512]{1,2,0:T(8,128)}, f32[2,128,512]{1,2,0:T(8,128)}, u32[]{:S(2)}, u32[]{:S(2)}) collective-permute-start(f32[2,128,512]{1,2,0:T(8,128)} %bitcast.54), channel_id=1, source_target_pairs={{2,0},{4,2},{6,4},{8,6},{10,8},{12,10},{14,12},{3,1},{5,3},{7,5},{... | collective-permute-start | bytes 1572872 | tf_op jit(solution)/shard_map/ppermute | solution.py:17
  189.0 31.5 %collective-permute-start.11 = (f32[2,128,512]{1,2,0:T(8,128)}, f32[2,128,512]{1,2,0:T(8,128)}, u32[]{:S(2)}, u32[]{:S(2)}) collective-permute-start(f32[2,128,512]{1,2,0:T(8,128)} %bitcast.53), channel_id=1, source_target_pairs={{4,0},{6,2},{8,4},{10,6},{12,8},{14,10},{5,1},{7,3},{9,5},{11,7},{... | collective-permute-start | bytes 1572872 | tf_op jit(solution)/shard_map/ppermute | solution.py:17
  192.0 46.3 %collective-permute-start.10 = (f32[2,128,512]{1,2,0:T(8,128)}, f32[2,128,512]{1,2,0:T(8,128)}, u32[]{:S(2)}, u32[]{:S(2)}) collective-permute-start(f32[2,128,512]{1,2,0:T(8,128)} %bitcast.52), channel_id=1, source_target_pairs={{6,0},{8,2},{10,4},{12,6},{14,8},{7,1},{9,3},{11,5},{13,7},{15,9},... | collective-permute-start | bytes 1572872 | tf_op jit(solution)/shard_map/ppermute | solution.py:17
  193.8 44.5 %copy-start.8 = (f32[1,2,128,512]{2,0,3,1:T(1,128)S(1)}, f32[1,2,128,512]{2,0,3,1:T(1,128)}, u32[]{:S(2)}) copy-start(f32[1,2,128,512]{2,0,3,1:T(1,128)} %get-tuple-element.51) | copy-start | bytes 1572868
  (14 other events, 85.3 us)
Sparse Core Ops, SparseCore 0:
  90.5 59.5 reduce-scatter.1
  152.3 56.0 all-gather.1
  212.4 90.6 all-reduce.1

commit v2 on v1

--- a/solution.py
+++ b/solution.py
@@ -119,9 +119,18 @@
     proj_local = lax.dot_general(
         attended, grad_hidden, (((0,), (0,)), ((), ())), preferred_element_type=jnp.float32
     )
-    proj_part = lax.psum_scatter(proj_local, ("ctx", "dp"), scatter_dimension=0, tiled=True)
-    proj_sum = lax.all_gather(proj_part.astype(jnp.bfloat16), ("ctx", "dp"), axis=0, tiled=True)
-    kernel_sum = lax.psum(kernel_local, ("ctx", "dp"))
+    members = lax.axis_size("ctx") * lax.axis_size("dp")
+    proj_rows = proj_local.shape[0] // members
+    kernel_rows = -(-KW // members)
+    kernel_padded = jnp.pad(kernel_local, ((0, kernel_rows * members - KW), (0, 0)))
+    stacked = jnp.concatenate(
+        [
+            proj_local.reshape(members, proj_rows, channels),
+            kernel_padded.reshape(members, kernel_rows, channels),
+        ],
+        axis=1,
+    )
+    summed = lax.psum_scatter(stacked, ("ctx", "dp"), scatter_dimension=0, tiled=False)
     grad_attended = lax.dot_general(
         grad_hidden, out_proj, (((1,), (1,)), ((), ())), preferred_element_type=jnp.float32
     ).astype(jnp.bfloat16)
@@ -159,6 +168,23 @@
     def grad_shift(piece_rows, offset_by):
         return passed_along(piece_rows, "ctx", offset_by)
 
+    summed, placed, grad_query = lax.optimization_barrier((summed, placed, grad_query))
+    kernel_part = summed[proj_rows:]
+    kernel_high = lax.reduce_precision(kernel_part, exponent_bits=8, mantissa_bits=7)
+    payload = jnp.concatenate(
+        [
+            summed[:proj_rows].astype(jnp.bfloat16),
+            kernel_high.astype(jnp.bfloat16),
+            (kernel_part - kernel_high).astype(jnp.bfloat16),
+        ],
+        axis=0,
+    )
+    gathered = lax.all_gather(payload, ("ctx", "dp"), axis=0, tiled=False)
+    proj_sum = gathered[:, :proj_rows].reshape(members * proj_rows, channels)
+    kernel_sum = (
+        gathered[:, proj_rows : proj_rows + kernel_rows].astype(jnp.float32)
+        + gathered[:, proj_rows + kernel_rows :].astype(jnp.float32)
+    ).reshape(members * kernel_rows, channels)[:KW]
     own_grads = give_back(placed, grad_shift)
     grad_key = own_grads[0].astype(jnp.bfloat16)
     grad_value = own_grads[1].astype(jnp.bfloat16)

time: 317 us -> 240 us (0.76)
  the two profiles are of different devices: /device:TPU:2 before, /device:TPU:8 now
where the time goes in v2:
time: 240 us; the launch traced here: 238 us
  waiting for transfers between devices  100 us (42%)
  starting transfers between devices  53.2 us (22%)
  local copies, waits for them, and re-layouts  36.7 us (15%)
  other arithmetic  22.9 us (10%)
  between operations  15.7 us (7%)
  matrix products  9.53 us (4%)
    reduce_scatter x1, waiting for transfers between devices, on_device(): lax.psum_scatter(stacked, ('ctx', 'dp'), scatter_dimension=0, tiled=False)  49.3 us
    ppermute x12, waiting for transfers between devices, passed_along(): return lax.ppermute(block, axis, route)  47.6 us
    ppermute x12, starting transfers between devices, passed_along(): return lax.ppermute(block, axis, route)  40.3 us
    ppermute x2, starting transfers between devices, padded(): lax.ppermute(tail, axis, [(i, (i + 1) % count) for i in range(ends)])  7.25 us
    unnamed x108, local copies, waits for them, and re-layouts  6.4 us
    reduce_sum x4, other arithmetic, on_device(): jnp.sum(padded_m[tap_index:tap_index + tokens].astype(jnp.float32) * grad...  5.83 us
    another operation x2, local copies, waits for them, and re-layouts, on_device(): jnp.stack([grad_key_all.reshape(span_blocks, tokens, width_heads), grad_v...  5.7 us
    ppermute x2, starting transfers between devices, padded(): lax.ppermute(head, axis, [((i + 1) % count, i) for i in range(ends)])  5.59 us
  transfers between devices with their start and end apart: 18, of which 8 were waited for; matrix products, arithmetic and copies ran while one was open for 15% of the time, Pallas kernels for 0%

profile of v2, /device:TPU:8, one launch (start us, length us, event | category | flops | bytes accessed | tf_op | source)
XLA Modules:
  0.0 238.3 jit_solution(17232835184790234244)
XLA Ops:
  9.1 1.3 collective-permute-start.5
  10.4 1.9 collective-permute-start.4
  12.4 2.7 %collective-permute-start.3 = (bf16[2,128,512]{2,1,0:T(8,128)(2,1)S(1)}, bf16[2,128,512]{2,1,0:T(8,128)(2,1)S(1)}, u32[]{:S(2)}, u32[]{:S(2)}) collective-permute-start(bf16[2,128,512]{2,1,0:T(8,128)(2,1)S(1)} %constant_dynamic-update-slice_fusion), channel_id=1, source_target_pairs={{2,0},{4,2},{6,4},{8,6},{10,8},{12,10},{14,12},{3,1},{5,3},{7,5},{... | collective-permute-start | bytes 786440 | tf_op jit(solution)/shard_map/ppermute | solution.py:17
  15.0 4.7 %collective-permute-start.1 = (bf16[2,128,512]{2,1,0:T(8,128)(2,1)S(1)}, bf16[2,128,512]{2,1,0:T(8,128)(2,1)S(1)}, u32[]{:S(2)}, u32[]{:S(2)}) collective-permute-start(bf16[2,128,512]{2,1,0:T(8,128)(2,1)S(1)} %constant_dynamic-update-slice_fusion), channel_id=1, source_target_pairs={{0,4},{2,6},{4,8},{6,10},{8,12},{10,14},{1,5},{3,7},{5,9},{7,11},{... | collective-permute-start | bytes 786440 | tf_op jit(solution)/shard_map/ppermute | solution.py:17
  19.8 5.3 %collective-permute-start = (bf16[2,128,512]{2,1,0:T(8,128)(2,1)S(1)}, bf16[2,128,512]{2,1,0:T(8,128)(2,1)S(1)}, u32[]{:S(2)}, u32[]{:S(2)}) collective-permute-start(bf16[2,128,512]{2,1,0:T(8,128)(2,1)S(1)} %constant_dynamic-update-slice_fusion), channel_id=1, source_target_pairs={{0,6},{2,8},{4,10},{6,12},{8,14},{1,7},{3,9},{5,11},{7,13},{9,15},... | collective-permute-start | bytes 786440 | tf_op jit(solution)/shard_map/ppermute | solution.py:17
  25.1 2.0 fusion.159
  28.3 1.0 copy.45
  29.3 5.0 %collective-permute-done = bf16[2,128,512]{2,1,0:T(8,128)(2,1)S(1)} collective-permute-done((bf16[2,128,512]{2,1,0:T(8,128)(2,1)S(1)}, bf16[2,128,512]{2,1,0:T(8,128)(2,1)S(1)}, u32[]{:S(2)}, u32[]{:S(2)}) %collective-permute-start) | collective-permute-done | bytes 262176 | tf_op jit(solution)/shard_map/ppermute | solution.py:17
  34.3 5.5 %collective-permute-start.2 = (bf16[2,128,512]{2,1,0:T(8,128)(2,1)S(1)}, bf16[2,128,512]{2,1,0:T(8,128)(2,1)S(1)}, u32[]{:S(2)}, u32[]{:S(2)}) collective-permute-start(bf16[2,128,512]{2,1,0:T(8,128)(2,1)S(1)} %constant_dynamic-update-slice_fusion), channel_id=1, source_target_pairs={{0,2},{2,4},{4,6},{6,8},{8,10},{10,12},{12,14},{1,3},{3,5},{5,7},{... | collective-permute-start | bytes 786440 | tf_op jit(solution)/shard_map/ppermute | solution.py:17
  39.9 4.1 %collective-permute-done.2 = bf16[2,128,512]{2,1,0:T(8,128)(2,1)S(1)} collective-permute-done((bf16[2,128,512]{2,1,0:T(8,128)(2,1)S(1)}, bf16[2,128,512]{2,1,0:T(8,128)(2,1)S(1)}, u32[]{:S(2)}, u32[]{:S(2)}) %collective-permute-start.2) | collective-permute-done | bytes 262176 | tf_op jit(solution)/shard_map/ppermute | solution.py:17
  44.1 1.0 fusion.155
  45.9 1.0 reshape_squeeze.10
  47.0 2.0 copy.43
  49.0 2.0 reshape_squeeze.9
  51.0 1.0 bitcast_reduce_fusion
  55.0 4.4 %collective-permute-start.6 = (bf16[15,1024]{1,0:T(8,128)(2,1)S(1)}, bf16[15,1024]{1,0:T(8,128)(2,1)S(1)}, u32[]{:S(2)}, u32[]{:S(2)}) collective-permute-start(bf16[15,1024]{1,0:T(8,128)(2,1)S(1)} %get-tuple-element.64), channel_id=1, source_target_pairs={{0,2},{2,4},{4,6},{6,8},{8,10},{10,12},{12,14},{1,3},{3,5},{5,7},{... | collective-permute-start | bytes 92168 | tf_op jit(solution)/shard_map/ppermute | solution.py:28
  59.4 2.3 collective-permute-start.7
  61.8 1.1 fusion.160
  63.1 2.2 collective-permute-done.7
  65.4 4.1 %fusion.84 = (f32[1024]{0:T(1024)}, f32[1024]{0:T(1024)}, f32[1024]{0:T(1024)}, f32[1024]{0:T(1024)}, f32[1024]{0:T(1024)}, /*index=5*/f32[1024]{0:T(1024)}, f32...) fusion(bf16[15,1024]{1,0:T(8,128)(2,1)S(1)} %collective-permute-done.7, ...), kind=kLoop, calls=%fused_computation.218 | loop fusion | flops 31841280 | bytes 1011712 | tf_op jit(solution)/shard_map/reduce_sum | solution.py:111
  70.2 3.2 %collective-permute-start.8 = (bf16[15,1024]{1,0:T(8,128)(2,1)}, bf16[15,1024]{1,0:T(8,128)(2,1)}, u32[]{:S(2)}, u32[]{:S(2)}) collective-permute-start(bf16[15,1024]{1,0:T(8,128)(2,1)} %get-tuple-element.62), channel_id=1, source_target_pairs={{2,0},{4,2},{6,4},{8,6},{10,8},{12,10},{14,12},{3,1},{5,3},{7,5},{... | collective-permute-start | bytes 92168 | tf_op jit(solution)/shard_map/ppermute | solution.py:30
  73.4 2.9 %collective-permute-start.9 = (bf16[15,1024]{1,0:T(8,128)(2,1)}, bf16[15,1024]{1,0:T(8,128)(2,1)}, u32[]{:S(2)}, u32[]{:S(2)}) collective-permute-start(bf16[15,1024]{1,0:T(8,128)(2,1)} %get-tuple-element.63), channel_id=1, source_target_pairs={{0,2},{2,4},{4,6},{6,8},{8,10},{10,12},{12,14},{1,3},{3,5},{5,7},{... | collective-permute-start | bytes 92168 | tf_op jit(solution)/shard_map/ppermute | solution.py:28
  79.2 1.2 collective-permute-done.9
  80.5 4.7 %fusion.37 = bf16[128,1024]{1,0:T(8,128)(2,1)S(1)} fusion(bf16[128,1024]{1,0:T(8,128)(2,1)S(1)} %get-tuple-element.52, bf16[15,1024]{1,0:T(8,128)(2,1)} %collective-permute-done.9, bf16[15,1024]{1,0:T(8,128)(2,1)} %collective-permute-done.8, bf16[1,128,1024]{2,1,0:T(8,128)(2,1)} %param.10, f32[1024]{0:T(1024)} %bitcast.246, f32[1024]{0:T(1024)} %bitcast.248, ...), kind=kLoop, calls=%fused_computation.171 | loop fusion | flops 24379392 | bytes 974976 | tf_op jit(solution)/shard_map/convert_element_type | solution.py:118
  85.6 1.8 pad_maximum_fusion.1
  88.0 2.1 convolution_bitcast_fusion
  90.1 2.7 %stack_reshape.7 = f32[7,1,128,512]{2,0,3,1:T(8,128)} reshape(f32[896,8,64]{0,2,1:T(8,128)} %convolution_bitcast_fusion) | data formatting | bytes 3670016 | tf_op jit(solution)/shard_map/stack;reshape | solution.py:160
  92.9 2.1 multiply_convert_fusion
  95.0 1.3 copy-done.1
  96.3 2.1 multiply_bitcast_fusion
  98.4 3.0 %stack_reshape.6 = f32[7,1,128,512]{2,0,3,1:T(8,128)} reshape(f32[896,8,64]{0,2,1:T(8,128)} %multiply_bitcast_fusion) | data formatting | bytes 3670016 | tf_op jit(solution)/shard_map/stack;reshape | solution.py:160
  101.4 4.1 %pad_maximum_fusion = f32[7,2,128,512]{2,0,3,1:T(8,128)} fusion(f32[7,1,128,512]{2,0,3,1:T(8,128)S(1)} %copy-done.4, f32[7,1,128,512]{2,0,3,1:T(8,128)} %stack_reshape.6), kind=kLoop, calls=%fused_computation.32 | loop fusion | flops 917504 | bytes 7340032 | tf_op jit(solution)/shard_map/stack | solution.py:160
  106.0 49.3 %reduce-scatter.2.cloned.1.call-done = f32[1,34,1024]{2,1,0:T(8,128)} async-done(((f32[16,34,1024]{2,1,0:T(8,128)}), f32[1,34,1024]{2,1,0:T(8,128)}) %reduce-scatter.2.cloned.1.call-update) | async-done | bytes 139280 | tf_op jit(solution)/shard_map/reduce_scatter | solution.py:133
  157.6 2.7 %slice.563 = f32[1,2,128,512]{2,0,3,1:T(1,128)S(1)} slice(f32[7,2,128,512]{2,0,3,1:T(8,128)} %pad_maximum_fusion), slice={[6:7], [0:2], [0:128], [0:512]} | slice | bytes 1048576 | tf_op jit(solution)/shard_map/slice | solution.py:47
  160.4 3.6 %collective-permute-start.15 = (f32[2,128,512]{1,2,0:T(8,128)S(1)}, f32[2,128,512]{1,2,0:T(8,128)S(1)}, u32[]{:S(2)}, u32[]{:S(2)}) collective-permute-start(f32[2,128,512]{1,2,0:T(8,128)S(1)} %bitcast.184), channel_id=1, source_target_pairs={{0,6},{2,8},{4,10},{6,12},{8,14},{1,7},{3,9},{5,11},{7,13},{9,15},... | collective-permute-start | bytes 1572872 | tf_op jit(solution)/shard_map/ppermute | solution.py:17
  164.0 3.0 %copy.53 = f32[7,2,128,512]{2,3,1,0:T(8,128)S(1)} copy(f32[7,2,128,512]{2,0,3,1:T(8,128)} %pad_maximum_fusion) | data formatting | bytes 7340032 | tf_op jit(solution)/shard_map/optimization_barrier | solution.py:171
  167.0 1.5 slice_bitcast_fusion.4
  169.4 1.3 collective-permute-start.10
  170.7 5.3 %collective-permute-start.14 = (f32[2,128,512]{1,2,0:T(8,128)}, f32[2,128,512]{1,2,0:T(8,128)S(1)}, u32[]{:S(2)}, u32[]{:S(2)}) collective-permute-start(f32[2,128,512]{1,2,0:T(8,128)} %get-tuple-element.54), channel_id=1, source_target_pairs={{0,4},{2,6},{4,8},{6,10},{8,12},{10,14},{1,5},{3,7},{5,9},{7,11},{... | collective-permute-start | bytes 1572872 | tf_op jit(solution)/shard_map/ppermute | solution.py:17
  176.0 2.6 %collective-permute-start.13 = (f32[2,128,512]{1,2,0:T(8,128)}, f32[2,128,512]{1,2,0:T(8,128)}, u32[]{:S(2)}, u32[]{:S(2)}) collective-permute-start(f32[2,128,512]{1,2,0:T(8,128)} %get-tuple-element.55), channel_id=1, source_target_pairs={{0,2},{2,4},{4,6},{6,8},{8,10},{10,12},{12,14},{1,3},{3,5},{5,7},{... | collective-permute-start | bytes 1572872 | tf_op jit(solution)/shard_map/ppermute | solution.py:17
  178.7 4.1 %collective-permute-start.12 = (f32[2,128,512]{1,2,0:T(8,128)}, f32[2,128,512]{1,2,0:T(8,128)}, u32[]{:S(2)}, u32[]{:S(2)}) collective-permute-start(f32[2,128,512]{1,2,0:T(8,128)} %get-tuple-element.56), channel_id=1, source_target_pairs={{2,0},{4,2},{6,4},{8,6},{10,8},{12,10},{14,12},{3,1},{5,3},{7,5},{... | collective-permute-start | bytes 1572872 | tf_op jit(solution)/shard_map/ppermute | solution.py:17
  182.8 1.9 collective-permute-start.11
  185.5 5.1 %collective-permute-done.14 = f32[2,128,512]{1,2,0:T(8,128)S(1)} collective-permute-done((f32[2,128,512]{1,2,0:T(8,128)}, f32[2,128,512]{1,2,0:T(8,128)S(1)}, u32[]{:S(2)}, u32[]{:S(2)}) %collective-permute-start.14) | collective-permute-done | bytes 524320 | tf_op jit(solution)/shard_map/ppermute | solution.py:17
  190.6 22.3 %collective-permute-done.13 = f32[2,128,512]{1,2,0:T(8,128)} collective-permute-done((f32[2,128,512]{1,2,0:T(8,128)}, f32[2,128,512]{1,2,0:T(8,128)}, u32[]{:S(2)}, u32[]{:S(2)}) %collective-permute-start.13) | collective-permute-done | bytes 524320 | tf_op jit(solution)/shard_map/ppermute | solution.py:17
  212.8 11.2 %collective-permute-done.11 = f32[2,128,512]{1,2,0:T(8,128)} collective-permute-done((f32[2,128,512]{1,2,0:T(8,128)S(1)}, f32[2,128,512]{1,2,0:T(8,128)}, u32[]{:S(2)}, u32[]{:S(2)}) %collective-permute-start.11) | collective-permute-done | bytes 524320 | tf_op jit(solution)/shard_map/ppermute | solution.py:17
  224.0 1.7 fusion.91
  227.3 1.2 convert_add_fusion.1
  229.2 2.3 slice.699
  (149 shorter events, 17.7 us)
Async XLA Ops:
  7.2 47.5 %copy-start = (bf16[512,1024]{1,0:T(8,128)(2,1)S(1)}, bf16[512,1024]{1,0:T(8,128)(2,1)}, u32[]{:S(2)}) copy-start(bf16[512,1024]{1,0:T(8,128)(2,1)} %param.11) | copy-start | bytes 3145732
  7.2 148.1 %reduce-scatter.2.cloned.1.call-start = ((), (), s32[]{:S(2)}) async-start(), calls=%async_computation.1 | async-start | bytes 2785280 | tf_op jit(solution)/shard_map/reduce_scatter | solution.py:133
  9.1 34.9 %collective-permute-start.5 = (bf16[2,128,512]{2,1,0:T(8,128)(2,1)S(1)}, bf16[2,128,512]{2,1,0:T(8,128)(2,1)S(1)}, u32[]{:S(2)}, u32[]{:S(2)}) collective-permute-start(bf16[2,128,512]{2,1,0:T(8,128)(2,1)S(1)} %constant_dynamic-update-slice_fusion), channel_id=1, source_target_pairs={{6,0},{8,2},{10,4},{12,6},{14,8},{7,1},{9,3},{11,5},{13,7},{15,9},... | collective-permute-start | bytes 786440 | tf_op jit(solution)/shard_map/ppermute | solution.py:17
  10.4 33.6 %collective-permute-start.4 = (bf16[2,128,512]{2,1,0:T(8,128)(2,1)S(1)}, bf16[2,128,512]{2,1,0:T(8,128)(2,1)S(1)}, u32[]{:S(2)}, u32[]{:S(2)}) collective-permute-start(bf16[2,128,512]{2,1,0:T(8,128)(2,1)S(1)} %constant_dynamic-update-slice_fusion), channel_id=1, source_target_pairs={{4,0},{6,2},{8,4},{10,6},{12,8},{14,10},{5,1},{7,3},{9,5},{11,7},{... | collective-permute-start | bytes 786440 | tf_op jit(solution)/shard_map/ppermute | solution.py:17
  12.4 31.6 %collective-permute-start.3 = (bf16[2,128,512]{2,1,0:T(8,128)(2,1)S(1)}, bf16[2,128,512]{2,1,0:T(8,128)(2,1)S(1)}, u32[]{:S(2)}, u32[]{:S(2)}) collective-permute-start(bf16[2,128,512]{2,1,0:T(8,128)(2,1)S(1)} %constant_dynamic-update-slice_fusion), channel_id=1, source_target_pairs={{2,0},{4,2},{6,4},{8,6},{10,8},{12,10},{14,12},{3,1},{5,3},{7,5},{... | collective-permute-start | bytes 786440 | tf_op jit(solution)/shard_map/ppermute | solution.py:17
  15.0 24.8 %collective-permute-start.1 = (bf16[2,128,512]{2,1,0:T(8,128)(2,1)S(1)}, bf16[2,128,512]{2,1,0:T(8,128)(2,1)S(1)}, u32[]{:S(2)}, u32[]{:S(2)}) collective-permute-start(bf16[2,128,512]{2,1,0:T(8,128)(2,1)S(1)} %constant_dynamic-update-slice_fusion), channel_id=1, source_target_pairs={{0,4},{2,6},{4,8},{6,10},{8,12},{10,14},{1,5},{3,7},{5,9},{7,11},{... | collective-permute-start | bytes 786440 | tf_op jit(solution)/shard_map/ppermute | solution.py:17
  19.8 14.6 %collective-permute-start = (bf16[2,128,512]{2,1,0:T(8,128)(2,1)S(1)}, bf16[2,128,512]{2,1,0:T(8,128)(2,1)S(1)}, u32[]{:S(2)}, u32[]{:S(2)}) collective-permute-start(bf16[2,128,512]{2,1,0:T(8,128)(2,1)S(1)} %constant_dynamic-update-slice_fusion), channel_id=1, source_target_pairs={{0,6},{2,8},{4,10},{6,12},{8,14},{1,7},{3,9},{5,11},{7,13},{9,15},... | collective-permute-start | bytes 786440 | tf_op jit(solution)/shard_map/ppermute | solution.py:17
  29.3 21.7 %copy-start.8 = (bf16[1,128,512]{1,2,0:T(8,128)(2,1)}, bf16[1,128,512]{1,2,0:T(8,128)(2,1)S(1)}, u32[]{:S(2)}) copy-start(bf16[1,128,512]{1,2,0:T(8,128)(2,1)S(1)} %copy.45) | copy-start | bytes 393220
  34.3 9.6 %collective-permute-start.2 = (bf16[2,128,512]{2,1,0:T(8,128)(2,1)S(1)}, bf16[2,128,512]{2,1,0:T(8,128)(2,1)S(1)}, u32[]{:S(2)}, u32[]{:S(2)}) collective-permute-start(bf16[2,128,512]{2,1,0:T(8,128)(2,1)S(1)} %constant_dynamic-update-slice_fusion), channel_id=1, source_target_pairs={{0,2},{2,4},{4,6},{6,8},{8,10},{10,12},{12,14},{1,3},{3,5},{5,7},{... | collective-permute-start | bytes 786440 | tf_op jit(solution)/shard_map/ppermute | solution.py:17
  54.0 11.2 %copy-start.10 = (bf16[1,128,1024]{2,1,0:T(8,128)(2,1)S(1)}, bf16[1,128,1024]{2,1,0:T(8,128)(2,1)}, u32[]{:S(2)}) copy-start(bf16[1,128,1024]{2,1,0:T(8,128)(2,1)} %param.10) | copy-start | bytes 786436
  54.0 11.2 %copy-start.12 = (f32[1,1024]{1,0:T(1,128)S(1)}, f32[1,1024]{1,0:T(1,128)}, u32[]{:S(2)}) copy-start(f32[1,1024]{1,0:T(1,128)} %get-tuple-element.72) | copy-start | bytes 12292
  54.0 11.2 %copy-start.13 = (f32[1,1024]{1,0:T(1,128)S(1)}, f32[1,1024]{1,0:T(1,128)}, u32[]{:S(2)}) copy-start(f32[1,1024]{1,0:T(1,128)} %get-tuple-element.73) | copy-start | bytes 12292
  54.0 11.2 %copy-start.14 = (f32[1,1024]{1,0:T(1,128)S(1)}, f32[1,1024]{1,0:T(1,128)}, u32[]{:S(2)}) copy-start(f32[1,1024]{1,0:T(1,128)} %get-tuple-element.74) | copy-start | bytes 12292
  54.0 11.2 %copy-start.15 = (f32[1,1024]{1,0:T(1,128)S(1)}, f32[1,1024]{1,0:T(1,128)}, u32[]{:S(2)}) copy-start(f32[1,1024]{1,0:T(1,128)} %get-tuple-element.75) | copy-start | bytes 12292
  54.0 11.2 %copy-start.16 = (f32[1,1024]{1,0:T(1,128)S(1)}, f32[1,1024]{1,0:T(1,128)}, u32[]{:S(2)}) copy-start(f32[1,1024]{1,0:T(1,128)} %get-tuple-element.76) | copy-start | bytes 12292
  54.1 11.2 %copy-start.17 = (f32[1,1024]{1,0:T(1,128)S(1)}, f32[1,1024]{1,0:T(1,128)}, u32[]{:S(2)}) copy-start(f32[1,1024]{1,0:T(1,128)} %get-tuple-element.77) | copy-start | bytes 12292
  54.1 11.2 %copy-start.18 = (f32[1,1024]{1,0:T(1,128)S(1)}, f32[1,1024]{1,0:T(1,128)}, u32[]{:S(2)}) copy-start(f32[1,1024]{1,0:T(1,128)} %get-tuple-element.78) | copy-start | bytes 12292
  54.1 11.2 %copy-start.19 = (f32[1,1024]{1,0:T(1,128)S(1)}, f32[1,1024]{1,0:T(1,128)}, u32[]{:S(2)}) copy-start(f32[1,1024]{1,0:T(1,128)} %get-tuple-element.79) | copy-start | bytes 12292
  54.1 11.2 %copy-start.20 = (f32[1,1024]{1,0:T(1,128)S(1)}, f32[1,1024]{1,0:T(1,128)}, u32[]{:S(2)}) copy-start(f32[1,1024]{1,0:T(1,128)} %get-tuple-element.80) | copy-start | bytes 12292
  54.1 11.2 %copy-start.21 = (f32[1,1024]{1,0:T(1,128)S(1)}, f32[1,1024]{1,0:T(1,128)}, u32[]{:S(2)}) copy-start(f32[1,1024]{1,0:T(1,128)} %get-tuple-element.81) | copy-start | bytes 12292
  54.1 11.2 %copy-start.22 = (f32[1,1024]{1,0:T(1,128)S(1)}, f32[1,1024]{1,0:T(1,128)}, u32[]{:S(2)}) copy-start(f32[1,1024]{1,0:T(1,128)} %get-tuple-element.82) | copy-start | bytes 12292
  54.1 11.2 %copy-start.23 = (f32[1,1024]{1,0:T(1,128)S(1)}, f32[1,1024]{1,0:T(1,128)}, u32[]{:S(2)}) copy-start(f32[1,1024]{1,0:T(1,128)} %get-tuple-element.83) | copy-start | bytes 12292
  54.1 11.2 %copy-start.24 = (f32[1,1024]{1,0:T(1,128)S(1)}, f32[1,1024]{1,0:T(1,128)}, u32[]{:S(2)}) copy-start(f32[1,1024]{1,0:T(1,128)} %get-tuple-element.84) | copy-start | bytes 12292
  54.1 11.2 %copy-start.25 = (f32[1,1024]{1,0:T(1,128)S(1)}, f32[1,1024]{1,0:T(1,128)}, u32[]{:S(2)}) copy-start(f32[1,1024]{1,0:T(1,128)} %get-tuple-element.85) | copy-start | bytes 12292
  54.1 11.2 %copy-start.26 = (f32[1,1024]{1,0:T(1,128)S(1)}, f32[1,1024]{1,0:T(1,128)}, u32[]{:S(2)}) copy-start(f32[1,1024]{1,0:T(1,128)} %get-tuple-element.86) | copy-start | bytes 12292
  55.0 8.0 %collective-permute-start.6 = (bf16[15,1024]{1,0:T(8,128)(2,1)S(1)}, bf16[15,1024]{1,0:T(8,128)(2,1)S(1)}, u32[]{:S(2)}, u32[]{:S(2)}) collective-permute-start(bf16[15,1024]{1,0:T(8,128)(2,1)S(1)} %get-tuple-element.64), channel_id=1, source_target_pairs={{0,2},{2,4},{4,6},{6,8},{8,10},{10,12},{12,14},{1,3},{3,5},{5,7},{... | collective-permute-start | bytes 92168 | tf_op jit(solution)/shard_map/ppermute | solution.py:28
  59.4 5.8 %collective-permute-start.7 = (bf16[15,1024]{1,0:T(8,128)(2,1)S(1)}, bf16[15,1024]{1,0:T(8,128)(2,1)S(1)}, u32[]{:S(2)}, u32[]{:S(2)}) collective-permute-start(bf16[15,1024]{1,0:T(8,128)(2,1)S(1)} %get-tuple-element.65), channel_id=1, source_target_pairs={{2,0},{4,2},{6,4},{8,6},{10,8},{12,10},{14,12},{3,1},{5,3},{7,5},{... | collective-permute-start | bytes 92168 | tf_op jit(solution)/shard_map/ppermute | solution.py:30
  62.9 15.1 %copy-start.27 = (f32[1,1024]{1,0:T(1,128)}, f32[1,1024]{1,0:T(1,128)S(1)}, u32[]{:S(2)}) copy-start(f32[1,1024]{1,0:T(1,128)S(1)} %get-tuple-element.87) | copy-start | bytes 12292
  62.9 15.1 %copy-start.28 = (f32[1,1024]{1,0:T(1,128)}, f32[1,1024]{1,0:T(1,128)S(1)}, u32[]{:S(2)}) copy-start(f32[1,1024]{1,0:T(1,128)S(1)} %get-tuple-element.88) | copy-start | bytes 12292
  62.9 15.1 %copy-start.29 = (f32[1,1024]{1,0:T(1,128)}, f32[1,1024]{1,0:T(1,128)S(1)}, u32[]{:S(2)}) copy-start(f32[1,1024]{1,0:T(1,128)S(1)} %get-tuple-element.89) | copy-start | bytes 12292
  63.0 15.1 %copy-start.30 = (f32[1,1024]{1,0:T(1,128)}, f32[1,1024]{1,0:T(1,128)S(1)}, u32[]{:S(2)}) copy-start(f32[1,1024]{1,0:T(1,128)S(1)} %get-tuple-element.90) | copy-start | bytes 12292
  63.0 15.1 %copy-start.31 = (f32[1,1024]{1,0:T(1,128)}, f32[1,1024]{1,0:T(1,128)S(1)}, u32[]{:S(2)}) copy-start(f32[1,1024]{1,0:T(1,128)S(1)} %get-tuple-element.91) | copy-start | bytes 12292
  63.0 15.1 %copy-start.32 = (f32[1,1024]{1,0:T(1,128)}, f32[1,1024]{1,0:T(1,128)S(1)}, u32[]{:S(2)}) copy-start(f32[1,1024]{1,0:T(1,128)S(1)} %get-tuple-element.92) | copy-start | bytes 12292
  63.0 15.1 %copy-start.33 = (f32[1,1024]{1,0:T(1,128)}, f32[1,1024]{1,0:T(1,128)S(1)}, u32[]{:S(2)}) copy-start(f32[1,1024]{1,0:T(1,128)S(1)} %get-tuple-element.93) | copy-start | bytes 12292
  63.0 15.1 %copy-start.34 = (f32[1,1024]{1,0:T(1,128)}, f32[1,1024]{1,0:T(1,128)S(1)}, u32[]{:S(2)}) copy-start(f32[1,1024]{1,0:T(1,128)S(1)} %get-tuple-element.94) | copy-start | bytes 12292
  63.0 15.1 %copy-start.35 = (f32[1,1024]{1,0:T(1,128)}, f32[1,1024]{1,0:T(1,128)S(1)}, u32[]{:S(2)}) copy-start(f32[1,1024]{1,0:T(1,128)S(1)} %get-tuple-element.95) | copy-start | bytes 12292
  63.0 15.1 %copy-start.36 = (f32[1,1024]{1,0:T(1,128)}, f32[1,1024]{1,0:T(1,128)S(1)}, u32[]{:S(2)}) copy-start(f32[1,1024]{1,0:T(1,128)S(1)} %get-tuple-element.96) | copy-start | bytes 12292
  63.0 15.1 %copy-start.37 = (f32[1,1024]{1,0:T(1,128)}, f32[1,1024]{1,0:T(1,128)S(1)}, u32[]{:S(2)}) copy-start(f32[1,1024]{1,0:T(1,128)S(1)} %get-tuple-element.97) | copy-start | bytes 12292
  63.0 15.1 %copy-start.38 = (f32[1,1024]{1,0:T(1,128)}, f32[1,1024]{1,0:T(1,128)S(1)}, u32[]{:S(2)}) copy-start(f32[1,1024]{1,0:T(1,128)S(1)} %get-tuple-element.98) | copy-start | bytes 12292
  70.2 9.1 %collective-permute-start.8 = (bf16[15,1024]{1,0:T(8,128)(2,1)}, bf16[15,1024]{1,0:T(8,128)(2,1)}, u32[]{:S(2)}, u32[]{:S(2)}) collective-permute-start(bf16[15,1024]{1,0:T(8,128)(2,1)} %get-tuple-element.62), channel_id=1, source_target_pairs={{2,0},{4,2},{6,4},{8,6},{10,8},{12,10},{14,12},{3,1},{5,3},{7,5},{... | collective-permute-start | bytes 92168 | tf_op jit(solution)/shard_map/ppermute | solution.py:30
  73.4 7.0 %collective-permute-start.9 = (bf16[15,1024]{1,0:T(8,128)(2,1)}, bf16[15,1024]{1,0:T(8,128)(2,1)}, u32[]{:S(2)}, u32[]{:S(2)}) collective-permute-start(bf16[15,1024]{1,0:T(8,128)(2,1)} %get-tuple-element.63), channel_id=1, source_target_pairs={{0,2},{2,4},{4,6},{6,8},{8,10},{10,12},{12,14},{1,3},{3,5},{5,7},{... | collective-permute-start | bytes 92168 | tf_op jit(solution)/shard_map/ppermute | solution.py:28
  87.4 139.9 %all-gather.4.cloned.1.call-start = ((), (), s32[]{:S(2)}) async-start(), calls=%async_computation.2 | async-start | bytes 1392640 | tf_op jit(solution)/shard_map/all_gather | solution.py:182
  160.4 22.4 %collective-permute-start.15 = (f32[2,128,512]{1,2,0:T(8,128)S(1)}, f32[2,128,512]{1,2,0:T(8,128)S(1)}, u32[]{:S(2)}, u32[]{:S(2)}) collective-permute-start(f32[2,128,512]{1,2,0:T(8,128)S(1)} %bitcast.184), channel_id=1, source_target_pairs={{0,6},{2,8},{4,10},{6,12},{8,14},{1,7},{3,9},{5,11},{7,13},{9,15},... | collective-permute-start | bytes 1572872 | tf_op jit(solution)/shard_map/ppermute | solution.py:17
  169.4 16.1 %collective-permute-start.10 = (f32[2,128,512]{1,2,0:T(8,128)}, f32[2,128,512]{1,2,0:T(8,128)S(1)}, u32[]{:S(2)}, u32[]{:S(2)}) collective-permute-start(f32[2,128,512]{1,2,0:T(8,128)} %get-tuple-element.53), channel_id=1, source_target_pairs={{6,0},{8,2},{10,4},{12,6},{14,8},{7,1},{9,3},{11,5},{13,7},{15,9},... | collective-permute-start | bytes 1572872 | tf_op jit(solution)/shard_map/ppermute | solution.py:17
  170.7 19.9 %collective-permute-start.14 = (f32[2,128,512]{1,2,0:T(8,128)}, f32[2,128,512]{1,2,0:T(8,128)S(1)}, u32[]{:S(2)}, u32[]{:S(2)}) collective-permute-start(f32[2,128,512]{1,2,0:T(8,128)} %get-tuple-element.54), channel_id=1, source_target_pairs={{0,4},{2,6},{4,8},{6,10},{8,12},{10,14},{1,5},{3,7},{5,9},{7,11},{... | collective-permute-start | bytes 1572872 | tf_op jit(solution)/shard_map/ppermute | solution.py:17
  176.0 36.8 %collective-permute-start.13 = (f32[2,128,512]{1,2,0:T(8,128)}, f32[2,128,512]{1,2,0:T(8,128)}, u32[]{:S(2)}, u32[]{:S(2)}) collective-permute-start(f32[2,128,512]{1,2,0:T(8,128)} %get-tuple-element.55), channel_id=1, source_target_pairs={{0,2},{2,4},{4,6},{6,8},{8,10},{10,12},{12,14},{1,3},{3,5},{5,7},{... | collective-permute-start | bytes 1572872 | tf_op jit(solution)/shard_map/ppermute | solution.py:17
  178.7 34.2 %collective-permute-start.12 = (f32[2,128,512]{1,2,0:T(8,128)}, f32[2,128,512]{1,2,0:T(8,128)}, u32[]{:S(2)}, u32[]{:S(2)}) collective-permute-start(f32[2,128,512]{1,2,0:T(8,128)} %get-tuple-element.56), channel_id=1, source_target_pairs={{2,0},{4,2},{6,4},{8,6},{10,8},{12,10},{14,12},{3,1},{5,3},{7,5},{... | collective-permute-start | bytes 1572872 | tf_op jit(solution)/shard_map/ppermute | solution.py:17
  182.8 41.2 %collective-permute-start.11 = (f32[2,128,512]{1,2,0:T(8,128)S(1)}, f32[2,128,512]{1,2,0:T(8,128)}, u32[]{:S(2)}, u32[]{:S(2)}) collective-permute-start(f32[2,128,512]{1,2,0:T(8,128)S(1)} %get-tuple-element.57), channel_id=1, source_target_pairs={{4,0},{6,2},{8,4},{10,6},{12,8},{14,10},{5,1},{7,3},{9,5},{11,7},{... | collective-permute-start | bytes 1572872 | tf_op jit(solution)/shard_map/ppermute | solution.py:17
  (19 other events, 108.8 us)
Sparse Core Ops, SparseCore 0:
  87.5 67.7 reduce-scatter.1
  158.1 53.6 all-gather.3

commit v3 on v2

--- a/solution.py
+++ b/solution.py
@@ -44,7 +44,8 @@
     total = partials[REACH]
     for offset in range(2 * REACH + 1):
         if offset != REACH:
-            total = total + shifter(partials[offset], offset - REACH)
+            moved = shifter(partials[offset].astype(jnp.bfloat16), offset - REACH)
+            total = total + moved.astype(jnp.float32)
     return total
 
 
@@ -130,7 +131,9 @@
         ],
         axis=1,
     )
-    summed = lax.psum_scatter(stacked, ("ctx", "dp"), scatter_dimension=0, tiled=False)
+    summed = lax.psum_scatter(
+        stacked.astype(jnp.bfloat16), ("ctx", "dp"), scatter_dimension=0, tiled=False
+    )
     grad_attended = lax.dot_general(
         grad_hidden, out_proj, (((1,), (1,)), ((), ())), preferred_element_type=jnp.float32
     ).astype(jnp.bfloat16)
@@ -169,22 +172,11 @@
         return passed_along(piece_rows, "ctx", offset_by)
 
     summed, placed, grad_query = lax.optimization_barrier((summed, placed, grad_query))
-    kernel_part = summed[proj_rows:]
-    kernel_high = lax.reduce_precision(kernel_part, exponent_bits=8, mantissa_bits=7)
-    payload = jnp.concatenate(
-        [
-            summed[:proj_rows].astype(jnp.bfloat16),
-            kernel_high.astype(jnp.bfloat16),
-            (kernel_part - kernel_high).astype(jnp.bfloat16),
-        ],
-        axis=0,
-    )
-    gathered = lax.all_gather(payload, ("ctx", "dp"), axis=0, tiled=False)
+    gathered = lax.all_gather(summed, ("ctx", "dp"), axis=0, tiled=False)
     proj_sum = gathered[:, :proj_rows].reshape(members * proj_rows, channels)
     kernel_sum = (
-        gathered[:, proj_rows : proj_rows + kernel_rows].astype(jnp.float32)
-        + gathered[:, proj_rows + kernel_rows :].astype(jnp.float32)
-    ).reshape(members * kernel_rows, channels)[:KW]
+        gathered[:, proj_rows:].astype(jnp.float32).reshape(members * kernel_rows, channels)[:KW]
+    )
     own_grads = give_back(placed, grad_shift)
     grad_key = own_grads[0].astype(jnp.bfloat16)
     grad_value = own_grads[1].astype(jnp.bfloat16)

time: 240 us -> 215 us (0.90)
  the two profiles are of different devices: /device:TPU:8 before, /device:TPU:2 now
where the time goes in v3:
time: 215 us; the launch traced here: 211 us
  waiting for transfers between devices  69.2 us (32%)
  starting transfers between devices  55.1 us (26%)
  local copies, waits for them, and re-layouts  40.9 us (19%)
  other arithmetic  21.6 us (10%)
  between operations  15.8 us (7%)
  matrix products  8.3 us (4%)
    reduce_scatter x1, waiting for transfers between devices, on_device(): lax.psum_scatter(stacked.astype(jnp.bfloat16), ('ctx', 'dp'), scatter_dim...  45.7 us
    ppermute x12, starting transfers between devices, passed_along(): return lax.ppermute(block, axis, route)  40.4 us
    ppermute x12, waiting for transfers between devices, passed_along(): return lax.ppermute(block, axis, route)  17.7 us
    ppermute x2, starting transfers between devices, padded(): lax.ppermute(tail, axis, [(i, (i + 1) % count) for i in range(ends)])  10.7 us
    unnamed x90, local copies, waits for them, and re-layouts  6.11 us
    another operation x32, local copies, waits for them, and re-layouts, on_device(): kernel_local = jnp.stack(kernel_terms, axis=0)  5.95 us
    reduce_sum x4, other arithmetic, on_device(): jnp.sum(padded_m[tap_index:tap_index + tokens].astype(jnp.float32) * grad...  5.24 us
    another operation x1, other arithmetic, on_device(): jnp.stack([grad_key_all.reshape(span_blocks, tokens, width_heads), grad_v...  4.79 us
  transfers between devices with their start and end apart: 18, of which 8 were waited for; matrix products, arithmetic and copies ran while one was open for 20% of the time, Pallas kernels for 0%

profile of v3, /device:TPU:2, one launch (start us, length us, event | category | flops | bytes accessed | tf_op | source)
XLA Modules:
  0.0 210.9 jit_solution(4816137259332399054)
XLA Ops:
  7.2 1.0 constant_dynamic-update-slice_fusion.1
  9.1 1.3 collective-permute-start.5
  10.4 1.3 collective-permute-start.4
  11.7 1.9 collective-permute-start.3
  13.7 4.8 %collective-permute-start.1 = (bf16[2,128,512]{2,1,0:T(8,128)(2,1)S(1)}, bf16[2,128,512]{2,1,0:T(8,128)(2,1)S(1)}, u32[]{:S(2)}, u32[]{:S(2)}) collective-permute-start(bf16[2,128,512]{2,1,0:T(8,128)(2,1)S(1)} %constant_dynamic-update-slice_fusion), channel_id=1, source_target_pairs={{0,4},{2,6},{4,8},{6,10},{8,12},{10,14},{1,5},{3,7},{5,9},{7,11},{... | collective-permute-start | bytes 786440 | tf_op jit(solution)/shard_map/ppermute | solution.py:17
  18.4 6.3 %collective-permute-start = (bf16[2,128,512]{2,1,0:T(8,128)(2,1)S(1)}, bf16[2,128,512]{2,1,0:T(8,128)(2,1)S(1)}, u32[]{:S(2)}, u32[]{:S(2)}) collective-permute-start(bf16[2,128,512]{2,1,0:T(8,128)(2,1)S(1)} %constant_dynamic-update-slice_fusion), channel_id=1, source_target_pairs={{0,6},{2,8},{4,10},{6,12},{8,14},{1,7},{3,9},{5,11},{7,13},{9,15},... | collective-permute-start | bytes 786440 | tf_op jit(solution)/shard_map/ppermute | solution.py:17
  24.7 2.0 fusion.151
  27.4 1.0 copy.174
  28.4 1.2 collective-permute-done
  29.6 8.2 %collective-permute-start.2 = (bf16[2,128,512]{2,1,0:T(8,128)(2,1)S(1)}, bf16[2,128,512]{2,1,0:T(8,128)(2,1)S(1)}, u32[]{:S(2)}, u32[]{:S(2)}) collective-permute-start(bf16[2,128,512]{2,1,0:T(8,128)(2,1)S(1)} %constant_dynamic-update-slice_fusion), channel_id=1, source_target_pairs={{0,2},{2,4},{4,6},{6,8},{8,10},{10,12},{12,14},{1,3},{3,5},{5,7},{... | collective-permute-start | bytes 786440 | tf_op jit(solution)/shard_map/ppermute | solution.py:17
  37.9 3.8 %collective-permute-done.2 = bf16[2,128,512]{2,1,0:T(8,128)(2,1)S(1)} collective-permute-done((bf16[2,128,512]{2,1,0:T(8,128)(2,1)S(1)}, bf16[2,128,512]{2,1,0:T(8,128)(2,1)S(1)}, u32[]{:S(2)}, u32[]{:S(2)}) %collective-permute-start.2) | collective-permute-done | bytes 262176 | tf_op jit(solution)/shard_map/ppermute | solution.py:17
  42.0 1.5 copy.173
  43.4 2.2 %reshape_squeeze.10 = bf16[896,8,64]{0,2,1:T(8,128)(2,1)S(1)} reshape(bf16[7,1,128,512]{2,0,3,1:T(8,128)(2,1)} %copy.173) | data formatting | bytes 1835008 | tf_op jit(solution)/shard_map/reshape;squeeze | solution.py:74
  45.6 1.5 copy.172
  47.1 2.9 %reshape_squeeze.9 = bf16[896,8,64]{0,2,1:T(8,128)(2,1)} reshape(bf16[7,1,128,512]{2,0,3,1:T(8,128)(2,1)} %copy.172) | data formatting | bytes 1835008 | tf_op jit(solution)/shard_map/reshape;squeeze | solution.py:75
  50.0 1.0 bitcast_reduce_fusion
  54.1 5.7 %collective-permute-start.6 = (bf16[15,1024]{1,0:T(8,128)(2,1)S(1)}, bf16[15,1024]{1,0:T(8,128)(2,1)S(1)}, u32[]{:S(2)}, u32[]{:S(2)}) collective-permute-start(bf16[15,1024]{1,0:T(8,128)(2,1)S(1)} %get-tuple-element.95), channel_id=1, source_target_pairs={{0,2},{2,4},{4,6},{6,8},{8,10},{10,12},{12,14},{1,3},{3,5},{5,7},{... | collective-permute-start | bytes 92168 | tf_op jit(solution)/shard_map/ppermute | solution.py:28
  59.8 1.9 collective-permute-start.7
  61.8 1.1 fusion.152
  63.0 3.5 %collective-permute-done.7 = bf16[15,1024]{1,0:T(8,128)(2,1)S(1)} collective-permute-done((bf16[15,1024]{1,0:T(8,128)(2,1)S(1)}, bf16[15,1024]{1,0:T(8,128)(2,1)S(1)}, u32[]{:S(2)}, u32[]{:S(2)}) %collective-permute-start.7) | collective-permute-done | bytes 30752 | tf_op jit(solution)/shard_map/ppermute | solution.py:30
  66.7 3.5 %fusion.84 = (bf16[1024]{0:T(1024)(128)(2,1)S(1)}, bf16[1024]{0:T(1024)(128)(2,1)S(1)}, bf16[1024]{0:T(1024)(128)(2,1)S(1)}, bf16[1024]{0:T(1024)(128)(2,1)S(1)}...) fusion(bf16[15,1024]{1,0:T(8,128)(2,1)S(1)} %collective-permute, ...), kind=kLoop, calls=%fused_computation.219 | loop fusion | flops 31841280 | bytes 993280 | tf_op jit(solution)/shard_map/reduce_sum | solution.py:112
  70.2 1.9 collective-permute-start.8
  72.1 5.0 %collective-permute-start.9 = (bf16[15,1024]{1,0:T(8,128)(2,1)S(1)}, bf16[15,1024]{1,0:T(8,128)(2,1)}, u32[]{:S(2)}, u32[]{:S(2)}) collective-permute-start(bf16[15,1024]{1,0:T(8,128)(2,1)S(1)} %get-tuple-element.94), channel_id=1, source_target_pairs={{0,2},{2,4},{4,6},{6,8},{8,10},{10,12},{12,14},{1,3},{3,5},{5,7},{... | collective-permute-start | bytes 92168 | tf_op jit(solution)/shard_map/ppermute | solution.py:28
  83.5 1.7 stack.198
  86.4 4.2 %fusion.37 = bf16[128,1024]{1,0:T(8,128)(2,1)S(1)} fusion(bf16[128,1024]{1,0:T(8,128)(2,1)S(1)} %get-tuple-element.82, bf16[15,1024]{1,0:T(8,128)(2,1)} %collective-permute-done.9, bf16[15,1024]{1,0:T(8,128)(2,1)} %copy-done.38, bf16[1,128,1024]{2,1,0:T(8,128)(2,1)} %param.10, f32[1024]{0:T(1024)} %bitcast.213, f32[1024]{0:T(1024)} %bitcast.215, ...), kind=kLoop, calls=%fused_computation.172 | loop fusion | flops 24379392 | bytes 974976 | tf_op jit(solution)/shard_map/convert_element_type | solution.py:119
  91.1 1.2 pad_maximum_fusion.1
  93.0 2.1 convolution_bitcast_fusion
  95.1 2.7 %stack_reshape.7 = f32[7,1,128,512]{2,0,3,1:T(8,128)} reshape(f32[896,8,64]{0,2,1:T(8,128)} %convolution_bitcast_fusion) | data formatting | bytes 3670016 | tf_op jit(solution)/shard_map/stack;reshape | solution.py:163
  97.8 2.1 %multiply_convert_fusion = bf16[8,128,896]{1,2,0:T(8,128)(2,1)S(1)} fusion(bf16[8,128,896]{1,2,0:T(8,128)(2,1)S(1)} %fusion.3, bf16[128,8,64]{0,2,1:T(8,128)(2,1)S(1)} %bitcast.145, bf16[896,8,64]{0,2,1:T(8,128)(2,1)} %reshape_squeeze.9, f32[8,128]{1,0:T(8,128)S(1)} %bitcast.216), kind=kOutput, calls=%fused_computation.40 | convolution fusion | flops 121110528 | bytes 4722688 | tf_op jit(solution)/shard_map/qhd,khd->hqk/dot_general | solution.py:145
  100.0 1.3 copy-done.1
  102.1 1.6 stack_reshape.6
  103.7 4.8 %pad_maximum_fusion = f32[7,2,128,512]{2,0,3,1:T(8,128)} fusion(f32[7,1,128,512]{2,0,3,1:T(8,128)} %stack_reshape.7, f32[7,1,128,512]{2,0,3,1:T(8,128)} %stack_reshape.6), kind=kLoop, calls=%fused_computation.32 | loop fusion | flops 917504 | bytes 7340032 | tf_op jit(solution)/shard_map/stack | solution.py:163
  109.0 45.7 %reduce-scatter.2.cloned.1.call-done = bf16[1,34,1024]{2,1,0:T(8,128)(2,1)} async-done(((bf16[16,34,1024]{2,1,0:T(8,128)(2,1)}), bf16[1,34,1024]{2,1,0:T(8,128)(2,1)}) %reduce-scatter.2.cloned.1.call-update) | async-done | bytes 69648 | tf_op jit(solution)/shard_map/reduce_scatter | solution.py:134
  154.8 2.5 %convert.179 = bf16[7,2,128,512]{2,0,3,1:T(8,128)(2,1)S(1)} convert(f32[7,2,128,512]{2,0,3,1:T(8,128)} %pad_maximum_fusion) | non-fusion elementwise | flops 917504 | bytes 5505024 | tf_op jit(solution)/shard_map/convert.11
  157.3 2.3 %fusion.146 = (bf16[1,2,128,512]{2,0,3,1:T(2,128)(2,1)S(1)}, bf16[1,2,128,512]{2,0,3,1:T(2,128)(2,1)S(1)}, bf16[1,2,128,512]{2,0,3,1:T(2,128)(2,1)S(1)}, bf16[1,...) fusion(bf16[7,2,128,512]{2,0,3,1:T(8,128)(2,1)S(1)} %convert.179), kind=kLoop, calls=%fused_computation.325 | loop fusion | bytes 3145728 | tf_op jit(solution)/shard_map/slice | solution.py:47
  159.7 1.3 collective-permute-start.11
  163.3 2.6 %collective-permute-start.12 = (bf16[2,128,512]{1,2,0:T(8,128)(2,1)}, bf16[2,128,512]{1,2,0:T(8,128)(2,1)S(1)}, u32[]{:S(2)}, u32[]{:S(2)}) collective-permute-start(bf16[2,128,512]{1,2,0:T(8,128)(2,1)} %bitcast.136), channel_id=1, source_target_pairs={{2,0},{4,2},{6,4},{8,6},{10,8},{12,10},{14,12},{3,1},{5,3},{7,5},{... | collective-permute-start | bytes 786440 | tf_op jit(solution)/shard_map/ppermute | solution.py:17
  166.0 4.1 %collective-permute-start.13 = (bf16[2,128,512]{1,2,0:T(8,128)(2,1)}, bf16[2,128,512]{1,2,0:T(8,128)(2,1)S(1)}, u32[]{:S(2)}, u32[]{:S(2)}) collective-permute-start(bf16[2,128,512]{1,2,0:T(8,128)(2,1)} %bitcast.135), channel_id=1, source_target_pairs={{0,2},{2,4},{4,6},{6,8},{8,10},{10,12},{12,14},{1,3},{3,5},{5,7},{... | collective-permute-start | bytes 786440 | tf_op jit(solution)/shard_map/ppermute | solution.py:17
  170.1 4.6 %collective-permute-start.14 = (bf16[2,128,512]{1,2,0:T(8,128)(2,1)}, bf16[2,128,512]{1,2,0:T(8,128)(2,1)S(1)}, u32[]{:S(2)}, u32[]{:S(2)}) collective-permute-start(bf16[2,128,512]{1,2,0:T(8,128)(2,1)} %bitcast.134), channel_id=1, source_target_pairs={{0,4},{2,6},{4,8},{6,10},{8,12},{10,14},{1,5},{3,7},{5,9},{7,11},{... | collective-permute-start | bytes 786440 | tf_op jit(solution)/shard_map/ppermute | solution.py:17
  174.7 2.9 %collective-permute-start.15 = (bf16[2,128,512]{1,2,0:T(8,128)(2,1)S(1)}, bf16[2,128,512]{1,2,0:T(8,128)(2,1)S(1)}, u32[]{:S(2)}, u32[]{:S(2)}) collective-permute-start(bf16[2,128,512]{1,2,0:T(8,128)(2,1)S(1)} %bitcast.151), channel_id=1, source_target_pairs={{0,6},{2,8},{4,10},{6,12},{8,14},{1,7},{3,9},{5,11},{7,13},{9,15},... | collective-permute-start | bytes 786440 | tf_op jit(solution)/shard_map/ppermute | solution.py:17
  177.6 1.3 collective-permute-start.10
  178.9 2.7 %slice.556 = f32[1,2,128,512]{2,0,3,1:T(1,128)S(1)} slice(f32[7,2,128,512]{2,0,3,1:T(8,128)} %pad_maximum_fusion), slice={[3:4], [0:2], [0:128], [0:512]} | slice | bytes 1048576 | tf_op jit(solution)/shard_map/slice | solution.py:44
  182.4 3.2 %collective-permute-done.14 = bf16[2,128,512]{1,2,0:T(8,128)(2,1)S(1)} collective-permute-done((bf16[2,128,512]{1,2,0:T(8,128)(2,1)}, bf16[2,128,512]{1,2,0:T(8,128)(2,1)S(1)}, u32[]{:S(2)}, u32[]{:S(2)}) %collective-permute-start.14) | collective-permute-done | bytes 262176 | tf_op jit(solution)/shard_map/ppermute | solution.py:17
  185.6 5.0 %collective-permute-done.15 = bf16[2,128,512]{1,2,0:T(8,128)(2,1)S(1)} collective-permute-done((bf16[2,128,512]{1,2,0:T(8,128)(2,1)S(1)}, bf16[2,128,512]{1,2,0:T(8,128)(2,1)S(1)}, u32[]{:S(2)}, u32[]{:S(2)}) %collective-permute-start.15) | collective-permute-done | bytes 262176 | tf_op jit(solution)/shard_map/ppermute | solution.py:17
  190.6 4.5 %collective-permute-done.10 = bf16[2,128,512]{1,2,0:T(8,128)(2,1)} collective-permute-done((bf16[2,128,512]{1,2,0:T(8,128)(2,1)S(1)}, bf16[2,128,512]{1,2,0:T(8,128)(2,1)}, u32[]{:S(2)}, u32[]{:S(2)}) %collective-permute-start.10) | collective-permute-done | bytes 262176 | tf_op jit(solution)/shard_map/ppermute | solution.py:17
  195.1 1.3 add_convert_fusion
  197.9 2.1 %all-gather.4.cloned.1.call-done = bf16[16,34,1024]{2,1,0:T(8,128)(2,1)} async-done(((bf16[1,34,1024]{2,1,0:T(8,128)(2,1)}), bf16[16,34,1024]{2,1,0:T(8,128)(2,1)}) %all-gather.4.cloned.1.call-update) | async-done | bytes 1114128 | tf_op jit(solution)/shard_map/all_gather | solution.py:175
  201.8 2.3 %slice.695 = bf16[16,32,1024]{2,1,0:T(8,128)(2,1)} slice(bf16[16,34,1024]{2,1,0:T(8,128)(2,1)} %all-gather.4.cloned.1.call-done), slice={[0:16], [0:32], [0:1024]} | slice | bytes 2097152 | tf_op jit(solution)/shard_map/slice | solution.py:176
  (166 shorter events, 20.4 us)
Async XLA Ops:
  7.2 46.6 %copy-start = (bf16[512,1024]{1,0:T(8,128)(2,1)S(1)}, bf16[512,1024]{1,0:T(8,128)(2,1)}, u32[]{:S(2)}) copy-start(bf16[512,1024]{1,0:T(8,128)(2,1)} %param.11) | copy-start | bytes 3145732
  7.2 147.6 %reduce-scatter.2.cloned.1.call-start = ((), (), s32[]{:S(2)}) async-start(), calls=%async_computation.1 | async-start | bytes 1392640 | tf_op jit(solution)/shard_map/reduce_scatter | solution.py:134
  9.1 32.6 %collective-permute-start.5 = (bf16[2,128,512]{2,1,0:T(8,128)(2,1)S(1)}, bf16[2,128,512]{2,1,0:T(8,128)(2,1)S(1)}, u32[]{:S(2)}, u32[]{:S(2)}) collective-permute-start(bf16[2,128,512]{2,1,0:T(8,128)(2,1)S(1)} %constant_dynamic-update-slice_fusion), channel_id=1, source_target_pairs={{6,0},{8,2},{10,4},{12,6},{14,8},{7,1},{9,3},{11,5},{13,7},{15,9},... | collective-permute-start | bytes 786440 | tf_op jit(solution)/shard_map/ppermute | solution.py:17
  10.4 31.3 %collective-permute-start.4 = (bf16[2,128,512]{2,1,0:T(8,128)(2,1)S(1)}, bf16[2,128,512]{2,1,0:T(8,128)(2,1)S(1)}, u32[]{:S(2)}, u32[]{:S(2)}) collective-permute-start(bf16[2,128,512]{2,1,0:T(8,128)(2,1)S(1)} %constant_dynamic-update-slice_fusion), channel_id=1, source_target_pairs={{4,0},{6,2},{8,4},{10,6},{12,8},{14,10},{5,1},{7,3},{9,5},{11,7},{... | collective-permute-start | bytes 786440 | tf_op jit(solution)/shard_map/ppermute | solution.py:17
  11.7 30.0 %collective-permute-start.3 = (bf16[2,128,512]{2,1,0:T(8,128)(2,1)S(1)}, bf16[2,128,512]{2,1,0:T(8,128)(2,1)S(1)}, u32[]{:S(2)}, u32[]{:S(2)}) collective-permute-start(bf16[2,128,512]{2,1,0:T(8,128)(2,1)S(1)} %constant_dynamic-update-slice_fusion), channel_id=1, source_target_pairs={{2,0},{4,2},{6,4},{8,6},{10,8},{12,10},{14,12},{3,1},{5,3},{7,5},{... | collective-permute-start | bytes 786440 | tf_op jit(solution)/shard_map/ppermute | solution.py:17
  13.7 24.2 %collective-permute-start.1 = (bf16[2,128,512]{2,1,0:T(8,128)(2,1)S(1)}, bf16[2,128,512]{2,1,0:T(8,128)(2,1)S(1)}, u32[]{:S(2)}, u32[]{:S(2)}) collective-permute-start(bf16[2,128,512]{2,1,0:T(8,128)(2,1)S(1)} %constant_dynamic-update-slice_fusion), channel_id=1, source_target_pairs={{0,4},{2,6},{4,8},{6,10},{8,12},{10,14},{1,5},{3,7},{5,9},{7,11},{... | collective-permute-start | bytes 786440 | tf_op jit(solution)/shard_map/ppermute | solution.py:17
  18.4 11.2 %collective-permute-start = (bf16[2,128,512]{2,1,0:T(8,128)(2,1)S(1)}, bf16[2,128,512]{2,1,0:T(8,128)(2,1)S(1)}, u32[]{:S(2)}, u32[]{:S(2)}) collective-permute-start(bf16[2,128,512]{2,1,0:T(8,128)(2,1)S(1)} %constant_dynamic-update-slice_fusion), channel_id=1, source_target_pairs={{0,6},{2,8},{4,10},{6,12},{8,14},{1,7},{3,9},{5,11},{7,13},{9,15},... | collective-permute-start | bytes 786440 | tf_op jit(solution)/shard_map/ppermute | solution.py:17
  27.4 26.3 %copy-start.39 = (pred[128]{0:T(512)(128)(4,1)}, pred[128]{0:T(512)(128)(4,1)S(1)}, u32[]{:S(2)}) copy-start(pred[128]{0:T(512)(128)(4,1)S(1)} %add_compare_fusion) | copy-start | bytes 388
  28.4 21.6 %copy-start.6 = (bf16[1,128,512]{1,2,0:T(8,128)(2,1)}, bf16[1,128,512]{1,2,0:T(8,128)(2,1)S(1)}, u32[]{:S(2)}) copy-start(bf16[1,128,512]{1,2,0:T(8,128)(2,1)S(1)} %copy.174) | copy-start | bytes 393220
  29.6 12.0 %collective-permute-start.2 = (bf16[2,128,512]{2,1,0:T(8,128)(2,1)S(1)}, bf16[2,128,512]{2,1,0:T(8,128)(2,1)S(1)}, u32[]{:S(2)}, u32[]{:S(2)}) collective-permute-start(bf16[2,128,512]{2,1,0:T(8,128)(2,1)S(1)} %constant_dynamic-update-slice_fusion), channel_id=1, source_target_pairs={{0,2},{2,4},{4,6},{6,8},{8,10},{10,12},{12,14},{1,3},{3,5},{5,7},{... | collective-permute-start | bytes 786440 | tf_op jit(solution)/shard_map/ppermute | solution.py:17
  53.1 13.5 %copy-start.11 = (f32[1,1024]{1,0:T(1,128)S(1)}, f32[1,1024]{1,0:T(1,128)}, u32[]{:S(2)}) copy-start(f32[1,1024]{1,0:T(1,128)} %get-tuple-element.101) | copy-start | bytes 12292
  53.1 13.5 %copy-start.12 = (f32[1,1024]{1,0:T(1,128)S(1)}, f32[1,1024]{1,0:T(1,128)}, u32[]{:S(2)}) copy-start(f32[1,1024]{1,0:T(1,128)} %get-tuple-element.102) | copy-start | bytes 12292
  53.1 13.5 %copy-start.13 = (f32[1,1024]{1,0:T(1,128)S(1)}, f32[1,1024]{1,0:T(1,128)}, u32[]{:S(2)}) copy-start(f32[1,1024]{1,0:T(1,128)} %get-tuple-element.103) | copy-start | bytes 12292
  53.1 13.5 %copy-start.14 = (f32[1,1024]{1,0:T(1,128)S(1)}, f32[1,1024]{1,0:T(1,128)}, u32[]{:S(2)}) copy-start(f32[1,1024]{1,0:T(1,128)} %get-tuple-element.104) | copy-start | bytes 12292
  53.1 13.5 %copy-start.15 = (f32[1,1024]{1,0:T(1,128)S(1)}, f32[1,1024]{1,0:T(1,128)}, u32[]{:S(2)}) copy-start(f32[1,1024]{1,0:T(1,128)} %get-tuple-element.105) | copy-start | bytes 12292
  53.1 13.5 %copy-start.16 = (f32[1,1024]{1,0:T(1,128)S(1)}, f32[1,1024]{1,0:T(1,128)}, u32[]{:S(2)}) copy-start(f32[1,1024]{1,0:T(1,128)} %get-tuple-element.106) | copy-start | bytes 12292
  53.1 13.5 %copy-start.17 = (f32[1,1024]{1,0:T(1,128)S(1)}, f32[1,1024]{1,0:T(1,128)}, u32[]{:S(2)}) copy-start(f32[1,1024]{1,0:T(1,128)} %get-tuple-element.107) | copy-start | bytes 12292
  53.1 13.5 %copy-start.18 = (f32[1,1024]{1,0:T(1,128)S(1)}, f32[1,1024]{1,0:T(1,128)}, u32[]{:S(2)}) copy-start(f32[1,1024]{1,0:T(1,128)} %get-tuple-element.108) | copy-start | bytes 12292
  53.1 13.5 %copy-start.19 = (f32[1,1024]{1,0:T(1,128)S(1)}, f32[1,1024]{1,0:T(1,128)}, u32[]{:S(2)}) copy-start(f32[1,1024]{1,0:T(1,128)} %get-tuple-element.109) | copy-start | bytes 12292
  53.1 13.5 %copy-start.20 = (f32[1,1024]{1,0:T(1,128)S(1)}, f32[1,1024]{1,0:T(1,128)}, u32[]{:S(2)}) copy-start(f32[1,1024]{1,0:T(1,128)} %get-tuple-element.110) | copy-start | bytes 12292
  53.1 13.5 %copy-start.21 = (f32[1,1024]{1,0:T(1,128)S(1)}, f32[1,1024]{1,0:T(1,128)}, u32[]{:S(2)}) copy-start(f32[1,1024]{1,0:T(1,128)} %get-tuple-element.111) | copy-start | bytes 12292
  53.2 13.5 %copy-start.22 = (f32[1,1024]{1,0:T(1,128)S(1)}, f32[1,1024]{1,0:T(1,128)}, u32[]{:S(2)}) copy-start(f32[1,1024]{1,0:T(1,128)} %get-tuple-element.112) | copy-start | bytes 12292
  53.2 13.5 %copy-start.23 = (f32[1,1024]{1,0:T(1,128)S(1)}, f32[1,1024]{1,0:T(1,128)}, u32[]{:S(2)}) copy-start(f32[1,1024]{1,0:T(1,128)} %get-tuple-element.113) | copy-start | bytes 12292
  53.2 13.5 %copy-start.24 = (f32[1,1024]{1,0:T(1,128)S(1)}, f32[1,1024]{1,0:T(1,128)}, u32[]{:S(2)}) copy-start(f32[1,1024]{1,0:T(1,128)} %get-tuple-element.114) | copy-start | bytes 12292
  53.2 13.5 %copy-start.25 = (f32[1,1024]{1,0:T(1,128)S(1)}, f32[1,1024]{1,0:T(1,128)}, u32[]{:S(2)}) copy-start(f32[1,1024]{1,0:T(1,128)} %get-tuple-element.115) | copy-start | bytes 12292
  54.1 8.9 %collective-permute-start.6 = (bf16[15,1024]{1,0:T(8,128)(2,1)S(1)}, bf16[15,1024]{1,0:T(8,128)(2,1)S(1)}, u32[]{:S(2)}, u32[]{:S(2)}) collective-permute-start(bf16[15,1024]{1,0:T(8,128)(2,1)S(1)} %get-tuple-element.95), channel_id=1, source_target_pairs={{0,2},{2,4},{4,6},{6,8},{8,10},{10,12},{12,14},{1,3},{3,5},{5,7},{... | collective-permute-start | bytes 92168 | tf_op jit(solution)/shard_map/ppermute | solution.py:28
  59.8 6.7 %collective-permute-start.7 = (bf16[15,1024]{1,0:T(8,128)(2,1)S(1)}, bf16[15,1024]{1,0:T(8,128)(2,1)S(1)}, u32[]{:S(2)}, u32[]{:S(2)}) collective-permute-start(bf16[15,1024]{1,0:T(8,128)(2,1)S(1)} %get-tuple-element.96), channel_id=1, source_target_pairs={{2,0},{4,2},{6,4},{8,6},{10,8},{12,10},{14,12},{3,1},{5,3},{7,5},{... | collective-permute-start | bytes 92168 | tf_op jit(solution)/shard_map/ppermute | solution.py:30
  62.9 19.9 %copy-start.26 = (f32[1,1024]{1,0:T(1,128)}, f32[1,1024]{1,0:T(1,128)S(1)}, u32[]{:S(2)}) copy-start(f32[1,1024]{1,0:T(1,128)S(1)} %get-tuple-element.116) | copy-start | bytes 12292
  62.9 19.9 %copy-start.27 = (f32[1,1024]{1,0:T(1,128)}, f32[1,1024]{1,0:T(1,128)S(1)}, u32[]{:S(2)}) copy-start(f32[1,1024]{1,0:T(1,128)S(1)} %get-tuple-element.117) | copy-start | bytes 12292
  62.9 19.9 %copy-start.28 = (f32[1,1024]{1,0:T(1,128)}, f32[1,1024]{1,0:T(1,128)S(1)}, u32[]{:S(2)}) copy-start(f32[1,1024]{1,0:T(1,128)S(1)} %get-tuple-element.118) | copy-start | bytes 12292
  62.9 19.9 %copy-start.29 = (f32[1,1024]{1,0:T(1,128)}, f32[1,1024]{1,0:T(1,128)S(1)}, u32[]{:S(2)}) copy-start(f32[1,1024]{1,0:T(1,128)S(1)} %get-tuple-element.119) | copy-start | bytes 12292
  62.9 19.9 %copy-start.30 = (f32[1,1024]{1,0:T(1,128)}, f32[1,1024]{1,0:T(1,128)S(1)}, u32[]{:S(2)}) copy-start(f32[1,1024]{1,0:T(1,128)S(1)} %get-tuple-element.120) | copy-start | bytes 12292
  62.9 19.9 %copy-start.31 = (f32[1,1024]{1,0:T(1,128)}, f32[1,1024]{1,0:T(1,128)S(1)}, u32[]{:S(2)}) copy-start(f32[1,1024]{1,0:T(1,128)S(1)} %get-tuple-element.121) | copy-start | bytes 12292
  62.9 19.9 %copy-start.32 = (f32[1,1024]{1,0:T(1,128)}, f32[1,1024]{1,0:T(1,128)S(1)}, u32[]{:S(2)}) copy-start(f32[1,1024]{1,0:T(1,128)S(1)} %get-tuple-element.122) | copy-start | bytes 12292
  62.9 19.9 %copy-start.33 = (f32[1,1024]{1,0:T(1,128)}, f32[1,1024]{1,0:T(1,128)S(1)}, u32[]{:S(2)}) copy-start(f32[1,1024]{1,0:T(1,128)S(1)} %get-tuple-element.123) | copy-start | bytes 12292
  63.0 19.9 %copy-start.34 = (f32[1,1024]{1,0:T(1,128)}, f32[1,1024]{1,0:T(1,128)S(1)}, u32[]{:S(2)}) copy-start(f32[1,1024]{1,0:T(1,128)S(1)} %get-tuple-element.124) | copy-start | bytes 12292
  63.0 19.9 %copy-start.35 = (f32[1,1024]{1,0:T(1,128)}, f32[1,1024]{1,0:T(1,128)S(1)}, u32[]{:S(2)}) copy-start(f32[1,1024]{1,0:T(1,128)S(1)} %get-tuple-element.125) | copy-start | bytes 12292
  63.0 19.9 %copy-start.36 = (f32[1,1024]{1,0:T(1,128)}, f32[1,1024]{1,0:T(1,128)S(1)}, u32[]{:S(2)}) copy-start(f32[1,1024]{1,0:T(1,128)S(1)} %get-tuple-element.126) | copy-start | bytes 12292
  63.0 19.9 %copy-start.37 = (f32[1,1024]{1,0:T(1,128)}, f32[1,1024]{1,0:T(1,128)S(1)}, u32[]{:S(2)}) copy-start(f32[1,1024]{1,0:T(1,128)S(1)} %get-tuple-element.127) | copy-start | bytes 12292
  70.2 15.6 %collective-permute-start.8 = (bf16[15,1024]{1,0:T(8,128)(2,1)S(1)}, bf16[15,1024]{1,0:T(8,128)(2,1)S(1)}, u32[]{:S(2)}, u32[]{:S(2)}) collective-permute-start(bf16[15,1024]{1,0:T(8,128)(2,1)S(1)} %get-tuple-element.93), channel_id=1, source_target_pairs={{2,0},{4,2},{6,4},{8,6},{10,8},{12,10},{14,12},{3,1},{5,3},{7,5},{... | collective-permute-start | bytes 92168 | tf_op jit(solution)/shard_map/ppermute | solution.py:30
  72.1 14.3 %collective-permute-start.9 = (bf16[15,1024]{1,0:T(8,128)(2,1)S(1)}, bf16[15,1024]{1,0:T(8,128)(2,1)}, u32[]{:S(2)}, u32[]{:S(2)}) collective-permute-start(bf16[15,1024]{1,0:T(8,128)(2,1)S(1)} %get-tuple-element.94), channel_id=1, source_target_pairs={{0,2},{2,4},{4,6},{6,8},{8,10},{10,12},{12,14},{1,3},{3,5},{5,7},{... | collective-permute-start | bytes 92168 | tf_op jit(solution)/shard_map/ppermute | solution.py:28
  92.3 107.8 %all-gather.4.cloned.1.call-start = ((), (), s32[]{:S(2)}) async-start(), calls=%async_computation.2 | async-start | bytes 1392640 | tf_op jit(solution)/shard_map/all_gather | solution.py:175
  159.7 17.8 %collective-permute-start.11 = (bf16[2,128,512]{1,2,0:T(8,128)(2,1)S(1)}, bf16[2,128,512]{1,2,0:T(8,128)(2,1)S(1)}, u32[]{:S(2)}, u32[]{:S(2)}) collective-permute-start(bf16[2,128,512]{1,2,0:T(8,128)(2,1)S(1)} %bitcast.152), channel_id=1, source_target_pairs={{4,0},{6,2},{8,4},{10,6},{12,8},{14,10},{5,1},{7,3},{9,5},{11,7},{... | collective-permute-start | bytes 786440 | tf_op jit(solution)/shard_map/ppermute | solution.py:17
  163.3 19.0 %collective-permute-start.12 = (bf16[2,128,512]{1,2,0:T(8,128)(2,1)}, bf16[2,128,512]{1,2,0:T(8,128)(2,1)S(1)}, u32[]{:S(2)}, u32[]{:S(2)}) collective-permute-start(bf16[2,128,512]{1,2,0:T(8,128)(2,1)} %bitcast.136), channel_id=1, source_target_pairs={{2,0},{4,2},{6,4},{8,6},{10,8},{12,10},{14,12},{3,1},{5,3},{7,5},{... | collective-permute-start | bytes 786440 | tf_op jit(solution)/shard_map/ppermute | solution.py:17
  166.0 16.4 %collective-permute-start.13 = (bf16[2,128,512]{1,2,0:T(8,128)(2,1)}, bf16[2,128,512]{1,2,0:T(8,128)(2,1)S(1)}, u32[]{:S(2)}, u32[]{:S(2)}) collective-permute-start(bf16[2,128,512]{1,2,0:T(8,128)(2,1)} %bitcast.135), channel_id=1, source_target_pairs={{0,2},{2,4},{4,6},{6,8},{8,10},{10,12},{12,14},{1,3},{3,5},{5,7},{... | collective-permute-start | bytes 786440 | tf_op jit(solution)/shard_map/ppermute | solution.py:17
  170.1 15.5 %collective-permute-start.14 = (bf16[2,128,512]{1,2,0:T(8,128)(2,1)}, bf16[2,128,512]{1,2,0:T(8,128)(2,1)S(1)}, u32[]{:S(2)}, u32[]{:S(2)}) collective-permute-start(bf16[2,128,512]{1,2,0:T(8,128)(2,1)} %bitcast.134), channel_id=1, source_target_pairs={{0,4},{2,6},{4,8},{6,10},{8,12},{10,14},{1,5},{3,7},{5,9},{7,11},{... | collective-permute-start | bytes 786440 | tf_op jit(solution)/shard_map/ppermute | solution.py:17
  174.7 15.9 %collective-permute-start.15 = (bf16[2,128,512]{1,2,0:T(8,128)(2,1)S(1)}, bf16[2,128,512]{1,2,0:T(8,128)(2,1)S(1)}, u32[]{:S(2)}, u32[]{:S(2)}) collective-permute-start(bf16[2,128,512]{1,2,0:T(8,128)(2,1)S(1)} %bitcast.151), channel_id=1, source_target_pairs={{0,6},{2,8},{4,10},{6,12},{8,14},{1,7},{3,9},{5,11},{7,13},{9,15},... | collective-permute-start | bytes 786440 | tf_op jit(solution)/shard_map/ppermute | solution.py:17
  177.6 17.6 %collective-permute-start.10 = (bf16[2,128,512]{1,2,0:T(8,128)(2,1)S(1)}, bf16[2,128,512]{1,2,0:T(8,128)(2,1)}, u32[]{:S(2)}, u32[]{:S(2)}) collective-permute-start(bf16[2,128,512]{1,2,0:T(8,128)(2,1)S(1)} %bitcast.150), channel_id=1, source_target_pairs={{6,0},{8,2},{10,4},{12,6},{14,8},{7,1},{9,3},{11,5},{13,7},{15,9},... | collective-permute-start | bytes 786440 | tf_op jit(solution)/shard_map/ppermute | solution.py:17
  (10 other events, 43.8 us)
Sparse Core Ops, SparseCore 0:
  92.4 62.2 reduce-scatter.1
  157.0 43.0 all-gather.3

commit v4 on v3

--- a/solution.py
+++ b/solution.py
@@ -47,6 +47,38 @@
             moved = shifter(partials[offset].astype(jnp.bfloat16), offset - REACH)
             total = total + moved.astype(jnp.float32)
     return total
+
+
+def exchange(block, axis, bit):
+    count = lax.axis_size(axis)
+    return lax.ppermute(block, axis, [(i, i ^ bit) for i in range(count)])
+
+
+def halving(acc, axis):
+    here = lax.axis_index(axis)
+    bit = 1
+    while acc.shape[0] > 1:
+        pairs = acc.reshape(acc.shape[0] // 2, 2, *acc.shape[1:])
+        mine = (here // bit) % 2
+        keep = lax.dynamic_index_in_dim(pairs, mine, 1, keepdims=False)
+        send = lax.dynamic_index_in_dim(pairs, 1 - mine, 1, keepdims=False)
+        acc = keep + exchange(send.astype(jnp.bfloat16), axis, bit).astype(jnp.float32)
+        bit *= 2
+    return acc[0]
+
+
+def doubling(acc, axis):
+    here = lax.axis_index(axis)
+    bit = lax.axis_size(axis) // 2
+    acc = acc[None]
+    while bit >= 1:
+        theirs = exchange(acc, axis, bit)
+        first = (here // bit) % 2 == 0
+        low = jnp.where(first, acc, theirs)
+        high = jnp.where(first, theirs, acc)
+        acc = jnp.stack([low, high], axis=1).reshape(-1, *acc.shape[1:])
+        bit //= 2
+    return acc
 
 
 def on_device(queries, key_rows, values, cotangent, out_proj, conv_kernel, lengths):
@@ -120,20 +152,20 @@
     proj_local = lax.dot_general(
         attended, grad_hidden, (((0,), (0,)), ((), ())), preferred_element_type=jnp.float32
     )
-    members = lax.axis_size("ctx") * lax.axis_size("dp")
+    ctx_count = lax.axis_size("ctx")
+    dp_count = lax.axis_size("dp")
+    members = ctx_count * dp_count
     proj_rows = proj_local.shape[0] // members
     kernel_rows = -(-KW // members)
     kernel_padded = jnp.pad(kernel_local, ((0, kernel_rows * members - KW), (0, 0)))
     stacked = jnp.concatenate(
         [
-            proj_local.reshape(members, proj_rows, channels),
-            kernel_padded.reshape(members, kernel_rows, channels),
+            proj_local.reshape(dp_count, ctx_count, proj_rows, channels),
+            kernel_padded.reshape(dp_count, ctx_count, kernel_rows, channels),
         ],
-        axis=1,
-    )
-    summed = lax.psum_scatter(
-        stacked.astype(jnp.bfloat16), ("ctx", "dp"), scatter_dimension=0, tiled=False
-    )
+        axis=2,
+    )
+    summed = halving(halving(stacked, "dp"), "ctx").astype(jnp.bfloat16)
     grad_attended = lax.dot_general(
         grad_hidden, out_proj, (((1,), (1,)), ((), ())), preferred_element_type=jnp.float32
     ).astype(jnp.bfloat16)
@@ -171,11 +203,10 @@
     def grad_shift(piece_rows, offset_by):
         return passed_along(piece_rows, "ctx", offset_by)
 
-    summed, placed, grad_query = lax.optimization_barrier((summed, placed, grad_query))
-    gathered = lax.all_gather(summed, ("ctx", "dp"), axis=0, tiled=False)
-    proj_sum = gathered[:, :proj_rows].reshape(members * proj_rows, channels)
+    gathered = doubling(doubling(summed, "ctx"), "dp")
+    proj_sum = gathered[:, :, :proj_rows].reshape(members * proj_rows, channels)
     kernel_sum = (
-        gathered[:, proj_rows:].astype(jnp.float32).reshape(members * kernel_rows, channels)[:KW]
+        gathered[:, :, proj_rows:].astype(jnp.float32).reshape(members * kernel_rows, channels)[:KW]
     )
     own_grads = give_back(placed, grad_shift)
     grad_key = own_grads[0].astype(jnp.bfloat16)

time: 215 us -> 202 us (0.940)
  waiting for transfers between devices: 69.2 us -> 44.3 us
  local copies, waits for them, and re-layouts: 40.9 us -> 56.4 us
  between operations: 15.8 us -> 2.06 us
  other arithmetic: 21.6 us -> 33.8 us
  matrix products: 8.3 us -> 14.2 us
  starting transfers between devices: 55.1 us -> 49.2 us
    reduce_scatter x1 -> x0, waiting for transfers between devices: 45.7 us -> none  [on_device(): lax.psum_scatter(stacked.astype(jnp.bfloat16), ('ctx', 'dp'), scatter_dim...]
    ppermute x0 -> x8, waiting for transfers between devices: none -> 19.2 us  [exchange(): return lax.ppermute(block, axis, [(i, i ^ bit) for i in range(count)])]
    ppermute x12, starting transfers between devices: 40.4 us -> 32.6 us  [passed_along(): return lax.ppermute(block, axis, route)]
    ppermute x12, waiting for transfers between devices: 17.7 us -> 25.1 us  [passed_along(): return lax.ppermute(block, axis, route)]
    reduce_sum x4, other arithmetic: 5.24 us -> 12.5 us  [on_device(): jnp.sum(padded_m[tap_index:tap_index + tokens].astype(jnp.float32) * grad...]
    another operation x0 -> x4, local copies, waits for them, and re-layouts: none -> 7.16 us  [the longest x1 2.86 us: halving(): pairs = acc.reshape(acc.shape[0] // 2, 2, *acc.shape[1:])]
    add x0 -> x3, other arithmetic: none -> 3.79 us  [halving(): keep + exchange(send.astype(jnp.bfloat16), axis, bit).astype(jnp.float32)]
    ppermute x2, waiting for transfers between devices: 3.53 us -> 0.01 us  [padded(): lax.ppermute(head, axis, [((i + 1) % count, i) for i in range(ends)])]
  transfers between devices with their start and end apart: 18 -> 24, of which waited for: 8 -> 10; matrix products, arithmetic and copies ran while one was open for 20% -> 27% of each run, Pallas kernels for 0% -> 0%
where the time goes in v4:
time: 202 us; the launch traced here: 200 us
  local copies, waits for them, and re-layouts  56.4 us (28%)
  starting transfers between devices  49.2 us (24%)
  waiting for transfers between devices  44.3 us (22%)
  other arithmetic  33.8 us (17%)
  matrix products  14.2 us (7%)
  between operations  2.06 us (1%)
    ppermute x12, starting transfers between devices, passed_along(): return lax.ppermute(block, axis, route)  32.6 us
    ppermute x12, waiting for transfers between devices, passed_along(): return lax.ppermute(block, axis, route)  25.1 us
    ppermute x8, waiting for transfers between devices, exchange(): return lax.ppermute(block, axis, [(i, i ^ bit) for i in range(count)])  19.2 us
    reduce_sum x4, other arithmetic, on_device(): jnp.sum(padded_m[tap_index:tap_index + tokens].astype(jnp.float32) * grad...  12.5 us
    ppermute x2, starting transfers between devices, padded(): lax.ppermute(tail, axis, [(i, (i + 1) % count) for i in range(ends)])  9.65 us
    unnamed x47, local copies, waits for them, and re-layouts  9.16 us
    convert_element_type x1, other arithmetic, on_device(): grad_hidden = (cot_here.astype(jnp.float32) + jnp.where(valid_rows[:, Non...  4.72 us
    another operation x3, local copies, waits for them, and re-layouts, on_device(): jnp.stack([grad_key_all.reshape(span_blocks, tokens, width_heads), grad_v...  4.71 us
  transfers between devices with their start and end apart: 24, of which 10 were waited for; matrix products, arithmetic and copies ran while one was open for 27% of the time, Pallas kernels for 0%

profile of v4, /device:TPU:2, one launch (start us, length us, event | category | flops | bytes accessed | tf_op | source)
XLA Modules:
  0.0 200.0 jit_solution(12703799173774571436)
XLA Ops:
  2.6 4.5 %collective-permute-start = (bf16[2,128,512]{2,1,0:T(8,128)(2,1)S(1)}, bf16[2,128,512]{2,1,0:T(8,128)(2,1)S(1)}, u32[]{:S(2)}, u32[]{:S(2)}) collective-permute-start(bf16[2,128,512]{2,1,0:T(8,128)(2,1)S(1)} %constant_dynamic-update-slice_fusion), channel_id=1, source_target_pairs={{0,6},{2,8},{4,10},{6,12},{8,14},{1,7},{3,9},{5,11},{7,13},{9,15},... | collective-permute-start | bytes 786440 | tf_op jit(solution)/shard_map/ppermute | solution.py:17
  7.1 3.5 %collective-permute-start.1 = (bf16[2,128,512]{2,1,0:T(8,128)(2,1)S(1)}, bf16[2,128,512]{2,1,0:T(8,128)(2,1)S(1)}, u32[]{:S(2)}, u32[]{:S(2)}) collective-permute-start(bf16[2,128,512]{2,1,0:T(8,128)(2,1)S(1)} %constant_dynamic-update-slice_fusion), channel_id=1, source_target_pairs={{0,4},{2,6},{4,8},{6,10},{8,12},{10,14},{1,5},{3,7},{5,9},{7,11},{... | collective-permute-start | bytes 786440 | tf_op jit(solution)/shard_map/ppermute | solution.py:17
  10.6 3.4 %collective-permute-start.2 = (bf16[2,128,512]{2,1,0:T(8,128)(2,1)S(1)}, bf16[2,128,512]{2,1,0:T(8,128)(2,1)S(1)}, u32[]{:S(2)}, u32[]{:S(2)}) collective-permute-start(bf16[2,128,512]{2,1,0:T(8,128)(2,1)S(1)} %constant_dynamic-update-slice_fusion), channel_id=1, source_target_pairs={{0,2},{2,4},{4,6},{6,8},{8,10},{10,12},{12,14},{1,3},{3,5},{5,7},{... | collective-permute-start | bytes 786440 | tf_op jit(solution)/shard_map/ppermute | solution.py:17
  13.9 2.5 %collective-permute-start.3 = (bf16[2,128,512]{2,1,0:T(8,128)(2,1)S(1)}, bf16[2,128,512]{2,1,0:T(8,128)(2,1)S(1)}, u32[]{:S(2)}, u32[]{:S(2)}) collective-permute-start(bf16[2,128,512]{2,1,0:T(8,128)(2,1)S(1)} %constant_dynamic-update-slice_fusion), channel_id=1, source_target_pairs={{2,0},{4,2},{6,4},{8,6},{10,8},{12,10},{14,12},{3,1},{5,3},{7,5},{... | collective-permute-start | bytes 786440 | tf_op jit(solution)/shard_map/ppermute | solution.py:17
  17.7 1.8 fusion.158
  23.1 2.0 %collective-permute-done.2 = bf16[2,128,512]{2,1,0:T(8,128)(2,1)S(1)} collective-permute-done((bf16[2,128,512]{2,1,0:T(8,128)(2,1)S(1)}, bf16[2,128,512]{2,1,0:T(8,128)(2,1)S(1)}, u32[]{:S(2)}, u32[]{:S(2)}) %collective-permute-start.2) | collective-permute-done | bytes 262176 | tf_op jit(solution)/shard_map/ppermute | solution.py:17
  26.0 14.6 %collective-permute-done.5 = bf16[2,128,512]{2,1,0:T(8,128)(2,1)S(1)} collective-permute-done((bf16[2,128,512]{2,1,0:T(8,128)(2,1)S(1)}, bf16[2,128,512]{2,1,0:T(8,128)(2,1)S(1)}, u32[]{:S(2)}, u32[]{:S(2)}) %collective-permute-start.5) | collective-permute-done | bytes 262176 | tf_op jit(solution)/shard_map/ppermute | solution.py:17
  46.2 2.4 %copy.289 = bf16[7,1,128,512]{2,0,3,1:T(8,128)(2,1)} copy(bf16[7,1,128,512]{3,2,1,0:T(8,128)(2,1)} %get-tuple-element.98) | data formatting | bytes 1835008 | tf_op jit(solution)/shard_map/slice | solution.py:107
  48.6 2.9 %reshape_squeeze.14 = bf16[896,8,64]{0,2,1:T(8,128)(2,1)} reshape(bf16[7,1,128,512]{2,0,3,1:T(8,128)(2,1)} %copy.289) | data formatting | bytes 1835008 | tf_op jit(solution)/shard_map/reshape;squeeze | solution.py:107
  51.6 1.7 convolution_convert_fusion
  53.6 1.9 collective-permute-start.7
  55.5 4.8 %collective-permute-start.6 = (bf16[15,1024]{1,0:T(8,128)(2,1)S(1)}, bf16[15,1024]{1,0:T(8,128)(2,1)S(1)}, u32[]{:S(2)}, u32[]{:S(2)}) collective-permute-start(bf16[15,1024]{1,0:T(8,128)(2,1)S(1)} %get-tuple-element.112), channel_id=1, source_target_pairs={{0,2},{2,4},{4,6},{6,8},{8,10},{10,12},{12,14},{1,3},{3,5},{5,7},{... | collective-permute-start | bytes 92168 | tf_op jit(solution)/shard_map/ppermute | solution.py:28
  60.4 1.7 fusion.159
  62.8 6.8 %fusion.88 = (f32[1024]{0:T(1024)}, f32[1024]{0:T(1024)}, f32[1024]{0:T(1024)}, f32[1024]{0:T(1024)}, f32[1024]{0:T(1024)}, /*index=5*/f32[1024]{0:T(1024)}, f32...) fusion(bf16[15,1024]{1,0:T(8,128)(2,1)} %copy-done.14, bf16[128,1024]{1,0:T(8,128)(2,1)S(1)} %fusion.4, ...), kind=kLoop, calls=%fused_computation.230 | loop fusion | flops 31841280 | bytes 1011712 | tf_op jit(solution)/shard_map/reduce_sum | solution.py:144
  70.3 4.8 %collective-permute-start.9 = (bf16[15,1024]{1,0:T(8,128)(2,1)}, bf16[15,1024]{1,0:T(8,128)(2,1)}, u32[]{:S(2)}, u32[]{:S(2)}) collective-permute-start(bf16[15,1024]{1,0:T(8,128)(2,1)} %get-tuple-element.111), channel_id=1, source_target_pairs={{0,2},{2,4},{4,6},{6,8},{8,10},{10,12},{12,14},{1,3},{3,5},{5,7},{... | collective-permute-start | bytes 92168 | tf_op jit(solution)/shard_map/ppermute | solution.py:28
  75.1 1.9 collective-permute-start.8
  77.0 2.4 %fusion.72 = (f32[1024]{0:T(1024)}, f32[1024]{0:T(1024)}, f32[1024]{0:T(1024)}, f32[1024]{0:T(1024)}, f32[1024]{0:T(1024)}, /*index=5*/f32[1024]{0:T(1024)}, f32[1024]{0:T(1024)}, f32[1024]{0:T(1024)}, f32[1024]{0:T(1024)}) fusion(bf16[128,1024]{1,0:T(8,128)(2,1)S(1)} %get-tuple-element.91, bf16[128,1024]{1,0:T(8,128)(2,1)S(1)} %fusion.4, ...), kind=kLoop, calls=%fused_computation.214 | loop fusion | flops 7199744 | bytes 591872 | tf_op jit(solution)/shard_map/reduce_sum | solution.py:144
  79.4 2.3 %fusion.87 = (f32[1024]{0:T(1024)}, f32[1024]{0:T(1024)}, f32[1024]{0:T(1024)}, f32[1024]{0:T(1024)}, f32[1024]{0:T(1024)}, /*index=5*/f32[1024]{0:T(1024)}, f32[1024]{0:T(1024)}) fusion(bf16[128,1024]{1,0:T(8,128)(2,1)S(1)} %get-tuple-element.91, bf16[15,1024]{1,0:T(8,128)(2,1)} %copy-done.14, bf16[128,1024]{1,0:T(8,128)(2,1)S(1)} %fusion.4), kind=kLoop, calls=%fused_computation.229 | loop fusion | flops 5235712 | bytes 583680 | tf_op jit(solution)/shard_map/reduce_sum | solution.py:144
  82.7 3.1 %stack.203 = f32[31,1024]{1,0:T(8,128)S(1)} concatenate(f32[1,1024]{1,0:T(1,128)} %bitcast.315, f32[1,1024]{1,0:T(1,128)} %bitcast.317, f32[1,1024]{1,0:T(1,128)} %bitcast.316, f32[1,1024]{1,0:T(1,128)} %bitcast.318, f32[1,1024]{1,0:T(1,128)} %bitcast.298, f32[1,1024]{1,0:T(1,128)} %bitcast.299, f32[1,1024]{1,0:T(1,128)} %bitcast.300, f32[1,1024]{1,0:T(1,128)} %bitcast.301, ...), dimensions={0} | concatenate | bytes 253952 | tf_op jit(solution)/shard_map/stack | solution.py:148
  86.0 4.7 %fusion.41 = bf16[128,1024]{1,0:T(8,128)(2,1)S(1)} fusion(bf16[128,1024]{1,0:T(8,128)(2,1)S(1)} %get-tuple-element.91, bf16[15,1024]{1,0:T(8,128)(2,1)} %collective-permute-done.9, bf16[15,1024]{1,0:T(8,128)(2,1)} %collective-permute-done.8, bf16[1,128,1024]{2,1,0:T(8,128)(2,1)} %param.10, f32[1024]{0:T(1024)} %bitcast.285, f32[1024]{0:T(1024)} %bitcast.287, ...), kind=kLoop, calls=%fused_computation.183 | loop fusion | flops 24379392 | bytes 974976 | tf_op jit(solution)/shard_map/convert_element_type | solution.py:151
  95.7 2.6 %fusion.9 = f32[1,8,34,1024]{3,1,2,0:T(8,128)} fusion(s32[]{:T(128)S(6)} %select_n.144, f32[2,8,32,1024]{3,1,2,0:T(8,128)} %copy-done.1, f32[2,8,2,1024]{3,1,2,0:T(8,128)S(1)} %copy-done.9, bf16[1,8,34,1024]{3,1,2,0:T(8,128)(2,1)} %collective-permute-done.16), kind=kLoop, calls=%fused_computation.112 | loop fusion | flops 835584 | bytes 3899396 | tf_op jit(solution)/shard_map/add | solution.py:65
  98.3 2.9 %reshape_squeeze.15 = f32[4,2,34,1024]{3,1,0,2:T(2,128)} reshape(f32[1,8,34,1024]{3,1,2,0:T(8,128)} %fusion.9) | data formatting | bytes 2228224 | tf_op jit(solution)/shard_map/reshape;squeeze | solution.py:61
  101.1 1.9 constant_dynamic-slice_fusion.1
  103.3 2.2 %multiply_convert_fusion = bf16[8,128,896]{1,2,0:T(8,128)(2,1)} fusion(bf16[8,128,896]{1,2,0:T(8,128)(2,1)S(1)} %fusion.3, bf16[128,8,64]{0,2,1:T(8,128)(2,1)S(1)} %bitcast.217, bf16[896,8,64]{0,2,1:T(8,128)(2,1)S(1)} %copy-done.5, f32[8,128]{1,0:T(8,128)S(1)} %bitcast.319), kind=kOutput, calls=%fused_computation.39 | convolution fusion | flops 121110528 | bytes 4722688 | tf_op jit(solution)/shard_map/qhd,khd->hqk/dot_general | solution.py:177
  106.1 6.2 %collective-permute-done.17 = bf16[4,34,1024]{2,0,1:T(4,128)(2,1)S(1)} collective-permute-done((bf16[4,34,1024]{2,0,1:T(4,128)(2,1)S(1)}, bf16[4,34,1024]{2,0,1:T(4,128)(2,1)S(1)}, u32[]{:S(2)}, u32[]{:S(2)}) %collective-permute-start.17) | collective-permute-done | bytes 278560 | tf_op jit(solution)/shard_map/ppermute | solution.py:54
  115.3 1.8 collective-permute-start.18
  117.1 3.0 %convolution_bitcast_fusion = f32[896,8,64]{0,2,1:T(8,128)} fusion(bf16[128,8,64]{0,2,1:T(8,128)(2,1)} %bitcast.218, bf16[8,128,896]{1,2,0:T(8,128)(2,1)S(1)} %fusion.3), kind=kOutput, calls=%fused_computation.46 | convolution fusion | flops 117440512 | bytes 3801088 | tf_op jit(solution)/shard_map/hqk,qhd->khd/dot_general | solution.py:192
  121.8 2.1 %multiply_bitcast_fusion = f32[896,8,64]{0,2,1:T(8,128)} fusion(bf16[8,128,896]{1,2,0:T(8,128)(2,1)S(1)} %copy-done.2, bf16[128,8,64]{0,2,1:T(8,128)(2,1)S(1)} %bitcast.220), kind=kOutput, calls=%fused_computation.45 | convolution fusion | flops 117899264 | bytes 3801088 | tf_op jit(solution)/shard_map/hqk,qhd->khd/dot_general | solution.py:189
  123.9 1.6 stack_reshape.6
  125.5 5.3 %collective-permute-done.19 = bf16[1,34,1024]{2,0,1:T(2,128)(2,1)} collective-permute-done((bf16[1,34,1024]{2,0,1:T(2,128)(2,1)}, bf16[1,34,1024]{2,0,1:T(2,128)(2,1)}, u32[]{:S(2)}, u32[]{:S(2)}) %collective-permute-start.19) | collective-permute-done | bytes 69664 | tf_op jit(solution)/shard_map/ppermute | solution.py:54
  130.8 1.8 add_convert_fusion.1
  134.0 1.6 stack_reshape.7
  135.6 5.2 %collective-permute-done.20 = bf16[1,34,1024]{2,0,1:T(2,128)(2,1)S(1)} collective-permute-done((bf16[1,34,1024]{2,0,1:T(2,128)(2,1)}, bf16[1,34,1024]{2,0,1:T(2,128)(2,1)S(1)}, u32[]{:S(2)}, u32[]{:S(2)}) %collective-permute-start.20) | collective-permute-done | bytes 69664 | tf_op jit(solution)/shard_map/ppermute | solution.py:54
  142.2 1.5 constant_dynamic-update-slice_fusion.2
  143.7 2.5 %convert.16 = bf16[7,2,128,512]{2,0,3,1:T(8,128)(2,1)S(1)} convert(f32[7,2,128,512]{2,0,3,1:T(8,128)} %constant_dynamic-update-slice_fusion.2) | non-fusion elementwise | flops 917504 | bytes 5505024 | tf_op jit(solution)/shard_map/convert.11
  146.2 2.0 %collective-permute-done.21 = bf16[2,34,1024]{2,1,0:T(8,128)(2,1)S(1)} collective-permute-done((bf16[2,34,1024]{2,1,0:T(8,128)(2,1)S(1)}, bf16[2,34,1024]{2,1,0:T(8,128)(2,1)S(1)}, u32[]{:S(2)}, u32[]{:S(2)}) %collective-permute-start.21) | collective-permute-done | bytes 139296 | tf_op jit(solution)/shard_map/ppermute | solution.py:54
  151.6 2.3 %fusion.153 = (bf16[1,2,128,512]{2,0,3,1:T(2,128)(2,1)S(1)}, bf16[1,2,128,512]{2,0,3,1:T(2,128)(2,1)S(1)}, bf16[1,2,128,512]{2,0,3,1:T(2,128)(2,1)S(1)}, bf16[1,...) fusion(bf16[7,2,128,512]{2,0,3,1:T(8,128)(2,1)S(1)} %convert.16), kind=kLoop, calls=%fused_computation.359 | loop fusion | bytes 3145728 | tf_op jit(solution)/shard_map/slice | solution.py:47
  154.7 3.4 %collective-permute-start.15 = (bf16[2,128,512]{1,2,0:T(8,128)(2,1)}, bf16[2,128,512]{1,2,0:T(8,128)(2,1)}, u32[]{:S(2)}, u32[]{:S(2)}) collective-permute-start(bf16[2,128,512]{1,2,0:T(8,128)(2,1)} %bitcast.205), channel_id=1, source_target_pairs={{0,6},{2,8},{4,10},{6,12},{8,14},{1,7},{3,9},{5,11},{7,13},{9,15},... | collective-permute-start | bytes 786440 | tf_op jit(solution)/shard_map/ppermute | solution.py:17
  158.9 3.7 %collective-permute-start.14 = (bf16[2,128,512]{1,2,0:T(8,128)(2,1)}, bf16[2,128,512]{1,2,0:T(8,128)(2,1)}, u32[]{:S(2)}, u32[]{:S(2)}) collective-permute-start(bf16[2,128,512]{1,2,0:T(8,128)(2,1)} %bitcast.206), channel_id=1, source_target_pairs={{0,4},{2,6},{4,8},{6,10},{8,12},{10,14},{1,5},{3,7},{5,9},{7,11},{... | collective-permute-start | bytes 786440 | tf_op jit(solution)/shard_map/ppermute | solution.py:17
  163.3 3.0 %collective-permute-start.13 = (bf16[2,128,512]{1,2,0:T(8,128)(2,1)}, bf16[2,128,512]{1,2,0:T(8,128)(2,1)}, u32[]{:S(2)}, u32[]{:S(2)}) collective-permute-start(bf16[2,128,512]{1,2,0:T(8,128)(2,1)} %bitcast.207), channel_id=1, source_target_pairs={{0,2},{2,4},{4,6},{6,8},{8,10},{10,12},{12,14},{1,3},{3,5},{5,7},{... | collective-permute-start | bytes 786440 | tf_op jit(solution)/shard_map/ppermute | solution.py:17
  167.0 3.5 %collective-permute-start.12 = (bf16[2,128,512]{1,2,0:T(8,128)(2,1)}, bf16[2,128,512]{1,2,0:T(8,128)(2,1)}, u32[]{:S(2)}, u32[]{:S(2)}) collective-permute-start(bf16[2,128,512]{1,2,0:T(8,128)(2,1)} %bitcast.208), channel_id=1, source_target_pairs={{2,0},{4,2},{6,4},{8,6},{10,8},{12,10},{14,12},{3,1},{5,3},{7,5},{... | collective-permute-start | bytes 786440 | tf_op jit(solution)/shard_map/ppermute | solution.py:17
  175.3 1.9 broadcast_in_dim_reshape.3
  178.7 2.3 %fusion.5 = bf16[8,64,128]{2,1,0:T(8,128)(2,1)} fusion(bf16[896,8,64]{0,2,1:T(8,128)(2,1)} %copy-done.4, bf16[8,128,896]{1,2,0:T(8,128)(2,1)S(1)} %copy-done.3), kind=kOutput, calls=%fused_computation.106 | convolution fusion | flops 117571584 | bytes 2883584 | tf_op jit(solution)/shard_map/hqk,khd->qhd/dot_general | solution.py:184
  181.0 2.7 %slice.687 = f32[1,2,128,512]{2,0,3,1:T(1,128)S(1)} slice(f32[7,2,128,512]{2,0,3,1:T(8,128)} %constant_dynamic-update-slice_fusion.2), slice={[3:4], [0:2], [0:128], [0:512]} | slice | bytes 1048576 | tf_op jit(solution)/shard_map/slice | solution.py:44
  183.7 1.7 copy.317
  185.4 7.8 %collective-permute-done.10 = bf16[2,128,512]{1,2,0:T(8,128)(2,1)} collective-permute-done((bf16[2,128,512]{1,2,0:T(8,128)(2,1)}, bf16[2,128,512]{1,2,0:T(8,128)(2,1)}, u32[]{:S(2)}, u32[]{:S(2)}) %collective-permute-start.10) | collective-permute-done | bytes 262176 | tf_op jit(solution)/shard_map/ppermute | solution.py:17
  193.2 1.6 add_convert_fusion
  197.7 1.5 copy.315
  (127 shorter events, 44.5 us)
Async XLA Ops:
  0.6 52.6 %copy-start = (bf16[512,1024]{1,0:T(8,128)(2,1)S(1)}, bf16[512,1024]{1,0:T(8,128)(2,1)}, u32[]{:S(2)}) copy-start(bf16[512,1024]{1,0:T(8,128)(2,1)} %param.11) | copy-start | bytes 3145732
  2.6 19.2 %collective-permute-start = (bf16[2,128,512]{2,1,0:T(8,128)(2,1)S(1)}, bf16[2,128,512]{2,1,0:T(8,128)(2,1)S(1)}, u32[]{:S(2)}, u32[]{:S(2)}) collective-permute-start(bf16[2,128,512]{2,1,0:T(8,128)(2,1)S(1)} %constant_dynamic-update-slice_fusion), channel_id=1, source_target_pairs={{0,6},{2,8},{4,10},{6,12},{8,14},{1,7},{3,9},{5,11},{7,13},{9,15},... | collective-permute-start | bytes 786440 | tf_op jit(solution)/shard_map/ppermute | solution.py:17
  7.1 16.0 %collective-permute-start.1 = (bf16[2,128,512]{2,1,0:T(8,128)(2,1)S(1)}, bf16[2,128,512]{2,1,0:T(8,128)(2,1)S(1)}, u32[]{:S(2)}, u32[]{:S(2)}) collective-permute-start(bf16[2,128,512]{2,1,0:T(8,128)(2,1)S(1)} %constant_dynamic-update-slice_fusion), channel_id=1, source_target_pairs={{0,4},{2,6},{4,8},{6,10},{8,12},{10,14},{1,5},{3,7},{5,9},{7,11},{... | collective-permute-start | bytes 786440 | tf_op jit(solution)/shard_map/ppermute | solution.py:17
  10.6 14.6 %collective-permute-start.2 = (bf16[2,128,512]{2,1,0:T(8,128)(2,1)S(1)}, bf16[2,128,512]{2,1,0:T(8,128)(2,1)S(1)}, u32[]{:S(2)}, u32[]{:S(2)}) collective-permute-start(bf16[2,128,512]{2,1,0:T(8,128)(2,1)S(1)} %constant_dynamic-update-slice_fusion), channel_id=1, source_target_pairs={{0,2},{2,4},{4,6},{6,8},{8,10},{10,12},{12,14},{1,3},{3,5},{5,7},{... | collective-permute-start | bytes 786440 | tf_op jit(solution)/shard_map/ppermute | solution.py:17
  13.9 12.0 %collective-permute-start.3 = (bf16[2,128,512]{2,1,0:T(8,128)(2,1)S(1)}, bf16[2,128,512]{2,1,0:T(8,128)(2,1)S(1)}, u32[]{:S(2)}, u32[]{:S(2)}) collective-permute-start(bf16[2,128,512]{2,1,0:T(8,128)(2,1)S(1)} %constant_dynamic-update-slice_fusion), channel_id=1, source_target_pairs={{2,0},{4,2},{6,4},{8,6},{10,8},{12,10},{14,12},{3,1},{5,3},{7,5},{... | collective-permute-start | bytes 786440 | tf_op jit(solution)/shard_map/ppermute | solution.py:17
  16.4 9.5 %collective-permute-start.4 = (bf16[2,128,512]{2,1,0:T(8,128)(2,1)S(1)}, bf16[2,128,512]{2,1,0:T(8,128)(2,1)S(1)}, u32[]{:S(2)}, u32[]{:S(2)}) collective-permute-start(bf16[2,128,512]{2,1,0:T(8,128)(2,1)S(1)} %constant_dynamic-update-slice_fusion), channel_id=1, source_target_pairs={{4,0},{6,2},{8,4},{10,6},{12,8},{14,10},{5,1},{7,3},{9,5},{11,7},{... | collective-permute-start | bytes 786440 | tf_op jit(solution)/shard_map/ppermute | solution.py:17
  21.7 21.8 %copy-start.10 = (bf16[1,128,512]{1,2,0:T(8,128)(2,1)}, bf16[1,128,512]{1,2,0:T(8,128)(2,1)S(1)}, u32[]{:S(2)}) copy-start(bf16[1,128,512]{1,2,0:T(8,128)(2,1)S(1)} %copy.288) | copy-start | bytes 393220
  21.8 18.8 %collective-permute-start.5 = (bf16[2,128,512]{2,1,0:T(8,128)(2,1)S(1)}, bf16[2,128,512]{2,1,0:T(8,128)(2,1)S(1)}, u32[]{:S(2)}, u32[]{:S(2)}) collective-permute-start(bf16[2,128,512]{2,1,0:T(8,128)(2,1)S(1)} %constant_dynamic-update-slice_fusion), channel_id=1, source_target_pairs={{6,0},{8,2},{10,4},{12,6},{14,8},{7,1},{9,3},{11,5},{13,7},{15,9},... | collective-permute-start | bytes 786440 | tf_op jit(solution)/shard_map/ppermute | solution.py:17
  43.5 1.1 copy-start.4
  51.6 1.7 copy-start.15
  53.6 8.5 %collective-permute-start.7 = (bf16[15,1024]{1,0:T(8,128)(2,1)S(1)}, bf16[15,1024]{1,0:T(8,128)(2,1)S(1)}, u32[]{:S(2)}, u32[]{:S(2)}) collective-permute-start(bf16[15,1024]{1,0:T(8,128)(2,1)S(1)} %get-tuple-element.113), channel_id=1, source_target_pairs={{2,0},{4,2},{6,4},{8,6},{10,8},{12,10},{14,12},{3,1},{5,3},{7,5},{... | collective-permute-start | bytes 92168 | tf_op jit(solution)/shard_map/ppermute | solution.py:30
  55.5 6.6 %collective-permute-start.6 = (bf16[15,1024]{1,0:T(8,128)(2,1)S(1)}, bf16[15,1024]{1,0:T(8,128)(2,1)S(1)}, u32[]{:S(2)}, u32[]{:S(2)}) collective-permute-start(bf16[15,1024]{1,0:T(8,128)(2,1)S(1)} %get-tuple-element.112), channel_id=1, source_target_pairs={{0,2},{2,4},{4,6},{6,8},{8,10},{10,12},{12,14},{1,3},{3,5},{5,7},{... | collective-permute-start | bytes 92168 | tf_op jit(solution)/shard_map/ppermute | solution.py:28
  62.1 0.6 copy-start.14
  62.2 0.6 copy-start.12
  62.8 18.9 %copy-start.13 = (bf16[15,1024]{1,0:T(8,128)(2,1)S(1)}, bf16[15,1024]{1,0:T(8,128)(2,1)}, u32[]{:S(2)}) copy-start(bf16[15,1024]{1,0:T(8,128)(2,1)} %copy-done.12) | copy-start | bytes 92164
  70.3 15.8 %collective-permute-start.9 = (bf16[15,1024]{1,0:T(8,128)(2,1)}, bf16[15,1024]{1,0:T(8,128)(2,1)}, u32[]{:S(2)}, u32[]{:S(2)}) collective-permute-start(bf16[15,1024]{1,0:T(8,128)(2,1)} %get-tuple-element.111), channel_id=1, source_target_pairs={{0,2},{2,4},{4,6},{6,8},{8,10},{10,12},{12,14},{1,3},{3,5},{5,7},{... | collective-permute-start | bytes 92168 | tf_op jit(solution)/shard_map/ppermute | solution.py:28
  75.1 10.9 %collective-permute-start.8 = (bf16[15,1024]{1,0:T(8,128)(2,1)}, bf16[15,1024]{1,0:T(8,128)(2,1)}, u32[]{:S(2)}, u32[]{:S(2)}) collective-permute-start(bf16[15,1024]{1,0:T(8,128)(2,1)} %get-tuple-element.110), channel_id=1, source_target_pairs={{2,0},{4,2},{6,4},{8,6},{10,8},{12,10},{14,12},{3,1},{5,3},{7,5},{... | collective-permute-start | bytes 92168 | tf_op jit(solution)/shard_map/ppermute | solution.py:30
  86.0 7.4 %copy-start.8 = (f32[2,8,2,1024]{3,1,2,0:T(8,128)}, f32[2,8,2,1024]{3,1,2,0:T(8,128)S(1)}, u32[]{:S(2)}) copy-start(f32[2,8,2,1024]{3,1,2,0:T(8,128)S(1)} %copy.309) | copy-start | bytes 393220
  91.2 1.3 copy-start.1
  93.4 2.3 %collective-permute-start.16 = (bf16[1,8,34,1024]{3,1,2,0:T(8,128)(2,1)}, bf16[1,8,34,1024]{3,1,2,0:T(8,128)(2,1)}, u32[]{:S(2)}, u32[]{:S(2)}) collective-permute-start(bf16[1,8,34,1024]{3,1,2,0:T(8,128)(2,1)} %fusion.7), channel_id=1, source_target_pairs={{0,1},{1,0},{2,3},{3,2},{4,5},{5,4},{6,7},{7,6},{8,9},{9,8},{10,11... | collective-permute-start | bytes 1671176 | tf_op jit(solution)/shard_map/ppermute | solution.py:54
  93.4 2.3 %copy-start.9 = (f32[2,8,2,1024]{3,1,2,0:T(8,128)S(1)}, f32[2,8,2,1024]{3,1,2,0:T(8,128)}, u32[]{:S(2)}) copy-start(f32[2,8,2,1024]{3,1,2,0:T(8,128)} %copy-done.8) | copy-start | bytes 393220
  95.6 7.7 %copy-start.7 = (bf16[128,512]{0,1:T(8,128)(2,1)}, bf16[128,512]{0,1:T(8,128)(2,1)S(1)}, u32[]{:S(2)}) copy-start(bf16[128,512]{0,1:T(8,128)(2,1)S(1)} %copy.291) | copy-start | bytes 393220
  101.1 2.2 %copy-start.5 = (bf16[896,8,64]{0,2,1:T(8,128)(2,1)S(1)}, bf16[896,8,64]{0,2,1:T(8,128)(2,1)}, u32[]{:S(2)}) copy-start(bf16[896,8,64]{0,2,1:T(8,128)(2,1)} %reshape_squeeze.14) | copy-start | bytes 2752516
  103.2 9.1 %collective-permute-start.17 = (bf16[4,34,1024]{2,0,1:T(4,128)(2,1)S(1)}, bf16[4,34,1024]{2,0,1:T(4,128)(2,1)S(1)}, u32[]{:S(2)}, u32[]{:S(2)}) collective-permute-start(bf16[4,34,1024]{2,0,1:T(4,128)(2,1)S(1)} %bitcast.223), channel_id=1, source_target_pairs={{0,2},{2,0},{4,6},{6,4},{8,10},{10,8},{12,14},{14,12},{1,3},{3,1},... | collective-permute-start | bytes 835592 | tf_op jit(solution)/shard_map/ppermute | solution.py:54
  103.3 2.2 %copy-start.6 = (f32[4,2,34,1024]{3,1,0,2:T(2,128)S(1)}, f32[4,2,34,1024]{3,1,0,2:T(2,128)}, u32[]{:S(2)}) copy-start(f32[4,2,34,1024]{3,1,0,2:T(2,128)} %reshape_squeeze.15) | copy-start | bytes 3342340
  115.3 6.6 %copy-start.2 = (bf16[8,128,896]{1,2,0:T(8,128)(2,1)S(1)}, bf16[8,128,896]{1,2,0:T(8,128)(2,1)}, u32[]{:S(2)}) copy-start(bf16[8,128,896]{1,2,0:T(8,128)(2,1)} %multiply_convert_fusion) | copy-start | bytes 5505028
  115.3 6.6 %copy-start.11 = (bf16[1,128,512]{1,2,0:T(8,128)(2,1)S(1)}, bf16[1,128,512]{1,2,0:T(8,128)(2,1)}, u32[]{:S(2)}) copy-start(bf16[1,128,512]{1,2,0:T(8,128)(2,1)} %copy-done.10) | copy-start | bytes 393220
  115.3 5.5 %collective-permute-start.18 = (bf16[2,34,1024]{2,0,1:T(2,128)(2,1)S(1)}, bf16[2,34,1024]{2,0,1:T(2,128)(2,1)S(1)}, u32[]{:S(2)}, u32[]{:S(2)}) collective-permute-start(bf16[2,34,1024]{2,0,1:T(2,128)(2,1)S(1)} %bitcast.225), channel_id=1, source_target_pairs={{0,4},{2,6},{4,0},{6,2},{8,12},{10,14},{12,8},{14,10},{1,5},{3,7},... | collective-permute-start | bytes 417800 | tf_op jit(solution)/shard_map/ppermute | solution.py:54
  121.8 9.0 %collective-permute-start.19 = (bf16[1,34,1024]{2,0,1:T(2,128)(2,1)}, bf16[1,34,1024]{2,0,1:T(2,128)(2,1)}, u32[]{:S(2)}, u32[]{:S(2)}) collective-permute-start(bf16[1,34,1024]{2,0,1:T(2,128)(2,1)} %dynamic-slice_convert_fusion.1), channel_id=1, source_target_pairs={{0,8},{2,10},{4,12},{6,14},{8,0},{10,2},{12,4},{14,6},{1,9},{3,11}... | collective-permute-start | bytes 208904 | tf_op jit(solution)/shard_map/ppermute | solution.py:54
  132.6 8.2 %collective-permute-start.20 = (bf16[1,34,1024]{2,0,1:T(2,128)(2,1)}, bf16[1,34,1024]{2,0,1:T(2,128)(2,1)S(1)}, u32[]{:S(2)}, u32[]{:S(2)}) collective-permute-start(bf16[1,34,1024]{2,0,1:T(2,128)(2,1)} %add_convert_fusion.1), channel_id=1, source_target_pairs={{0,8},{2,10},{4,12},{6,14},{8,0},{10,2},{12,4},{14,6},{1,9},{3,11}... | collective-permute-start | bytes 208904 | tf_op jit(solution)/shard_map/ppermute | solution.py:54
  142.1 6.2 %collective-permute-start.21 = (bf16[2,34,1024]{2,1,0:T(8,128)(2,1)S(1)}, bf16[2,34,1024]{2,1,0:T(8,128)(2,1)S(1)}, u32[]{:S(2)}, u32[]{:S(2)}) collective-permute-start(bf16[2,34,1024]{2,1,0:T(8,128)(2,1)S(1)} %maximum_bitcast_fusion.1), channel_id=1, source_target_pairs={{0,4},{2,6},{4,0},{6,2},{8,12},{10,14},{12,8},{14,10},{1,5},{3,7},... | collective-permute-start | bytes 417800 | tf_op jit(solution)/shard_map/ppermute | solution.py:54
  150.4 21.6 %collective-permute-start.22 = (bf16[4,34,1024]{2,0,1:T(4,128)(2,1)S(1)}, bf16[4,34,1024]{2,0,1:T(4,128)(2,1)S(1)}, u32[]{:S(2)}, u32[]{:S(2)}) collective-permute-start(bf16[4,34,1024]{2,0,1:T(4,128)(2,1)S(1)} %reshape.102), channel_id=1, source_target_pairs={{0,2},{2,0},{4,6},{6,4},{8,10},{10,8},{12,14},{14,12},{1,3},{3,1},... | collective-permute-start | bytes 835592 | tf_op jit(solution)/shard_map/ppermute | solution.py:54
  154.7 22.6 %collective-permute-start.15 = (bf16[2,128,512]{1,2,0:T(8,128)(2,1)}, bf16[2,128,512]{1,2,0:T(8,128)(2,1)}, u32[]{:S(2)}, u32[]{:S(2)}) collective-permute-start(bf16[2,128,512]{1,2,0:T(8,128)(2,1)} %bitcast.205), channel_id=1, source_target_pairs={{0,6},{2,8},{4,10},{6,12},{8,14},{1,7},{3,9},{5,11},{7,13},{9,15},... | collective-permute-start | bytes 786440 | tf_op jit(solution)/shard_map/ppermute | solution.py:17
  158.9 19.7 %collective-permute-start.14 = (bf16[2,128,512]{1,2,0:T(8,128)(2,1)}, bf16[2,128,512]{1,2,0:T(8,128)(2,1)}, u32[]{:S(2)}, u32[]{:S(2)}) collective-permute-start(bf16[2,128,512]{1,2,0:T(8,128)(2,1)} %bitcast.206), channel_id=1, source_target_pairs={{0,4},{2,6},{4,8},{6,10},{8,12},{10,14},{1,5},{3,7},{5,9},{7,11},{... | collective-permute-start | bytes 786440 | tf_op jit(solution)/shard_map/ppermute | solution.py:17
  163.3 22.1 %collective-permute-start.13 = (bf16[2,128,512]{1,2,0:T(8,128)(2,1)}, bf16[2,128,512]{1,2,0:T(8,128)(2,1)}, u32[]{:S(2)}, u32[]{:S(2)}) collective-permute-start(bf16[2,128,512]{1,2,0:T(8,128)(2,1)} %bitcast.207), channel_id=1, source_target_pairs={{0,2},{2,4},{4,6},{6,8},{8,10},{10,12},{12,14},{1,3},{3,5},{5,7},{... | collective-permute-start | bytes 786440 | tf_op jit(solution)/shard_map/ppermute | solution.py:17
  167.0 18.4 %collective-permute-start.12 = (bf16[2,128,512]{1,2,0:T(8,128)(2,1)}, bf16[2,128,512]{1,2,0:T(8,128)(2,1)}, u32[]{:S(2)}, u32[]{:S(2)}) collective-permute-start(bf16[2,128,512]{1,2,0:T(8,128)(2,1)} %bitcast.208), channel_id=1, source_target_pairs={{2,0},{4,2},{6,4},{8,6},{10,8},{12,10},{14,12},{3,1},{5,3},{7,5},{... | collective-permute-start | bytes 786440 | tf_op jit(solution)/shard_map/ppermute | solution.py:17
  172.0 13.4 %collective-permute-start.11 = (bf16[2,128,512]{1,2,0:T(8,128)(2,1)}, bf16[2,128,512]{1,2,0:T(8,128)(2,1)}, u32[]{:S(2)}, u32[]{:S(2)}) collective-permute-start(bf16[2,128,512]{1,2,0:T(8,128)(2,1)} %bitcast.209), channel_id=1, source_target_pairs={{4,0},{6,2},{8,4},{10,6},{12,8},{14,10},{5,1},{7,3},{9,5},{11,7},{... | collective-permute-start | bytes 786440 | tf_op jit(solution)/shard_map/ppermute | solution.py:17
  173.5 5.1 %copy-start.3 = (bf16[8,128,896]{1,2,0:T(8,128)(2,1)S(1)}, bf16[8,128,896]{1,2,0:T(8,128)(2,1)}, u32[]{:S(2)}) copy-start(bf16[8,128,896]{1,2,0:T(8,128)(2,1)} %multiply_convert_fusion) | copy-start | bytes 5505028
  177.3 15.9 %collective-permute-start.10 = (bf16[2,128,512]{1,2,0:T(8,128)(2,1)}, bf16[2,128,512]{1,2,0:T(8,128)(2,1)}, u32[]{:S(2)}, u32[]{:S(2)}) collective-permute-start(bf16[2,128,512]{1,2,0:T(8,128)(2,1)} %bitcast.224), channel_id=1, source_target_pairs={{6,0},{8,2},{10,4},{12,6},{14,8},{7,1},{9,3},{11,5},{13,7},{15,9},... | collective-permute-start | bytes 786440 | tf_op jit(solution)/shard_map/ppermute | solution.py:17
  178.6 17.8 %collective-permute-start.23 = (bf16[1,8,34,1024]{3,1,2,0:T(8,128)(2,1)S(1)}, bf16[1,8,34,1024]{3,1,2,0:T(8,128)(2,1)}, u32[]{:S(2)}, u32[]{:S(2)}) collective-permute-start(bf16[1,8,34,1024]{3,1,2,0:T(8,128)(2,1)S(1)} %broadcast_in_dim_reshape.3), channel_id=1, source_target_pairs={{0,1},{1,0},{2,3},{3,2},{4,5},{5,4},{6,7},{7,6},{8,9},{9,8},{10,11... | collective-permute-start | bytes 1671176 | tf_op jit(solution)/shard_map/ppermute | solution.py:54

commit v5 on v4

--- a/solution.py
+++ b/solution.py
@@ -102,7 +102,15 @@
     def kv_shift(piece_rows, offset_by):
         return passed_along(piece_rows, "ctx", offset_by)
 
-    gathered = collect(jnp.stack([key_here, value_here], axis=0), kv_shift)
+    own_kv = jnp.stack([key_here, value_here], axis=0)
+    if lax.axis_size("ctx") <= span_blocks + 1:
+        ctx_count = lax.axis_size("ctx")
+        spread = jnp.broadcast_to(own_kv[None], (ctx_count,) + own_kv.shape)
+        everyone = lax.all_to_all(spread, "ctx", 0, 0, tiled=True)
+        everyone = jnp.pad(everyone, ((REACH, REACH), (0, 0), (0, 0), (0, 0)))
+        gathered = lax.dynamic_slice_in_dim(everyone, block_index, span_blocks, 0)
+    else:
+        gathered = collect(own_kv, kv_shift)
     key_all = gathered[:, 0].reshape(span_blocks * tokens, HEADS, HDIM)
     value_all = gathered[:, 1].reshape(span_blocks * tokens, HEADS, HDIM)
     query_heads = query_here.reshape(tokens, HEADS, HDIM)

time: 202 us -> 219 us (1.084)
  waiting for transfers between devices: 44.3 us -> 72.6 us
  starting transfers between devices: 49.2 us -> 39.6 us
  local copies, waits for them, and re-layouts: 56.4 us -> 53.7 us
    all_to_all x0 -> x1, waiting for transfers between devices: none -> 45.7 us  [on_device(): everyone = lax.all_to_all(spread, 'ctx', 0, 0, tiled=True)]
    ppermute x12 -> x6, waiting for transfers between devices: 25.1 us -> 7.75 us  [passed_along(): return lax.ppermute(block, axis, route)]
    ppermute x12 -> x6, starting transfers between devices: 32.6 us -> 16.3 us  [passed_along(): return lax.ppermute(block, axis, route)]
    all_to_all x0 -> x1, starting transfers between devices: none -> 6.47 us  [on_device(): everyone = lax.all_to_all(spread, 'ctx', 0, 0, tiled=True)]
    unnamed x47 -> x46, local copies, waits for them, and re-layouts: 9.16 us -> 7.51 us
    another operation x2 -> x3, other arithmetic: 4.12 us -> 5.2 us
  transfers between devices with their start and end apart: 24 -> 19, of which waited for: 10 -> 8; matrix products, arithmetic and copies ran while one was open for 27% -> 24% of each run, Pallas kernels for 0% -> 0%
where the time goes in v5:
time: 219 us; the launch traced here: 217 us
  waiting for transfers between devices  72.6 us (33%)
  local copies, waits for them, and re-layouts  53.7 us (25%)
  starting transfers between devices  39.6 us (18%)
  other arithmetic  34.7 us (16%)
  matrix products  14.2 us (6%)
    all_to_all x1, waiting for transfers between devices, on_device(): everyone = lax.all_to_all(spread, 'ctx', 0, 0, tiled=True)  45.7 us
    ppermute x8, waiting for transfers between devices, exchange(): return lax.ppermute(block, axis, [(i, i ^ bit) for i in range(count)])  19.2 us
    ppermute x6, starting transfers between devices, passed_along(): return lax.ppermute(block, axis, route)  16.3 us
    reduce_sum x4, other arithmetic, on_device(): jnp.sum(padded_m[tap_index:tap_index + tokens].astype(jnp.float32) * grad...  12.5 us
    ppermute x2, starting transfers between devices, padded(): lax.ppermute(tail, axis, [(i, (i + 1) % count) for i in range(ends)])  9.09 us
    ppermute x6, waiting for transfers between devices, passed_along(): return lax.ppermute(block, axis, route)  7.75 us
    unnamed x46, local copies, waits for them, and re-layouts  7.51 us
    all_to_all x1, starting transfers between devices, on_device(): everyone = lax.all_to_all(spread, 'ctx', 0, 0, tiled=True)  6.47 us
  transfers between devices with their start and end apart: 19, of which 8 were waited for; matrix products, arithmetic and copies ran while one was open for 24% of the time, Pallas kernels for 0%

profile of v5, /device:TPU:2, one launch (start us, length us, event | category | flops | bytes accessed | tf_op | source)
XLA Modules:
  0.0 216.8 jit_solution(14117932864716104804)
XLA Ops:
  1.9 1.7 broadcast_in_dim.44
  3.6 6.5 %all-to-all-start = ((bf16[8,2,128,512]{2,3,1,0:T(8,128)(2,1)}), bf16[8,2,128,512]{2,3,1,0:T(8,128)(2,1)S(1)}, u32[]{:S(2)}, u32[]{:S(2)}) async-start(bf16[8,2,128,512]{2,3,1,0:T(8,128)(2,1)} %broadcast_in_dim.44), calls=%async_computation | async-start | bytes 4194304 | tf_op jit(solution)/shard_map/all_to_all | solution.py:109
  12.1 45.7 %all-to-all-done = bf16[8,2,128,512]{2,3,1,0:T(8,128)(2,1)S(1)} async-done(((bf16[8,2,128,512]{2,3,1,0:T(8,128)(2,1)}), bf16[8,2,128,512]{2,3,1,0:T(8,128)(2,1)S(1)}, u32[]{:S(2)}, u32[]{:S(2)}) %all-to-all-start) | async-done | bytes 2097184 | tf_op jit(solution)/shard_map/all_to_all | solution.py:109
  63.8 1.6 copy.284
  65.4 2.9 %reshape_squeeze.14 = bf16[896,8,64]{0,2,1:T(8,128)(2,1)} reshape(bf16[7,1,128,512]{2,0,3,1:T(8,128)(2,1)} %copy.284) | data formatting | bytes 1835008 | tf_op jit(solution)/shard_map/reshape;squeeze | solution.py:115
  68.3 1.7 convolution_convert_fusion
  70.3 2.5 %collective-permute-start.1 = (bf16[15,1024]{1,0:T(8,128)(2,1)S(1)}, bf16[15,1024]{1,0:T(8,128)(2,1)S(1)}, u32[]{:S(2)}, u32[]{:S(2)}) collective-permute-start(bf16[15,1024]{1,0:T(8,128)(2,1)S(1)} %get-tuple-element.113), channel_id=1, source_target_pairs={{2,0},{4,2},{6,4},{8,6},{10,8},{12,10},{14,12},{3,1},{5,3},{7,5},{... | collective-permute-start | bytes 92168 | tf_op jit(solution)/shard_map/ppermute | solution.py:30
  72.8 4.3 %collective-permute-start = (bf16[15,1024]{1,0:T(8,128)(2,1)S(1)}, bf16[15,1024]{1,0:T(8,128)(2,1)S(1)}, u32[]{:S(2)}, u32[]{:S(2)}) collective-permute-start(bf16[15,1024]{1,0:T(8,128)(2,1)S(1)} %get-tuple-element.112), channel_id=1, source_target_pairs={{0,2},{2,4},{4,6},{6,8},{8,10},{10,12},{12,14},{1,3},{3,5},{5,7},{... | collective-permute-start | bytes 92168 | tf_op jit(solution)/shard_map/ppermute | solution.py:28
  77.1 1.7 fusion.158
  79.5 6.8 %fusion.88 = (f32[1024]{0:T(1024)}, f32[1024]{0:T(1024)}, f32[1024]{0:T(1024)}, f32[1024]{0:T(1024)}, f32[1024]{0:T(1024)}, /*index=5*/f32[1024]{0:T(1024)}, f32...) fusion(bf16[15,1024]{1,0:T(8,128)(2,1)} %copy-done.15, bf16[128,1024]{1,0:T(8,128)(2,1)S(1)} %fusion.4, ...), kind=kLoop, calls=%fused_computation.232 | loop fusion | flops 31841280 | bytes 1011712 | tf_op jit(solution)/shard_map/reduce_sum | solution.py:152
  87.0 4.8 %collective-permute-start.3 = (bf16[15,1024]{1,0:T(8,128)(2,1)}, bf16[15,1024]{1,0:T(8,128)(2,1)}, u32[]{:S(2)}, u32[]{:S(2)}) collective-permute-start(bf16[15,1024]{1,0:T(8,128)(2,1)} %get-tuple-element.111), channel_id=1, source_target_pairs={{0,2},{2,4},{4,6},{6,8},{8,10},{10,12},{12,14},{1,3},{3,5},{5,7},{... | collective-permute-start | bytes 92168 | tf_op jit(solution)/shard_map/ppermute | solution.py:28
  91.8 2.1 collective-permute-start.2
  93.9 2.4 %fusion.72 = (f32[1024]{0:T(1024)}, f32[1024]{0:T(1024)}, f32[1024]{0:T(1024)}, f32[1024]{0:T(1024)}, f32[1024]{0:T(1024)}, /*index=5*/f32[1024]{0:T(1024)}, f32[1024]{0:T(1024)}, f32[1024]{0:T(1024)}, f32[1024]{0:T(1024)}) fusion(bf16[128,1024]{1,0:T(8,128)(2,1)S(1)} %get-tuple-element.91, bf16[128,1024]{1,0:T(8,128)(2,1)S(1)} %fusion.4, ...), kind=kLoop, calls=%fused_computation.216 | loop fusion | flops 7199744 | bytes 591872 | tf_op jit(solution)/shard_map/reduce_sum | solution.py:152
  96.3 2.3 %fusion.87 = (f32[1024]{0:T(1024)}, f32[1024]{0:T(1024)}, f32[1024]{0:T(1024)}, f32[1024]{0:T(1024)}, f32[1024]{0:T(1024)}, /*index=5*/f32[1024]{0:T(1024)}, f32[1024]{0:T(1024)}) fusion(bf16[128,1024]{1,0:T(8,128)(2,1)S(1)} %get-tuple-element.91, bf16[15,1024]{1,0:T(8,128)(2,1)} %copy-done.15, bf16[128,1024]{1,0:T(8,128)(2,1)S(1)} %fusion.4), kind=kLoop, calls=%fused_computation.231 | loop fusion | flops 5235712 | bytes 583680 | tf_op jit(solution)/shard_map/reduce_sum | solution.py:152
  99.6 3.1 %stack.171 = f32[31,1024]{1,0:T(8,128)S(1)} concatenate(f32[1,1024]{1,0:T(1,128)} %bitcast.301, f32[1,1024]{1,0:T(1,128)} %bitcast.303, f32[1,1024]{1,0:T(1,128)} %bitcast.302, f32[1,1024]{1,0:T(1,128)} %bitcast.304, f32[1,1024]{1,0:T(1,128)} %bitcast.284, f32[1,1024]{1,0:T(1,128)} %bitcast.285, f32[1,1024]{1,0:T(1,128)} %bitcast.286, f32[1,1024]{1,0:T(1,128)} %bitcast.287, ...), dimensions={0} | concatenate | bytes 253952 | tf_op jit(solution)/shard_map/stack | solution.py:156
  102.9 4.5 %fusion.41 = bf16[128,1024]{1,0:T(8,128)(2,1)S(1)} fusion(bf16[128,1024]{1,0:T(8,128)(2,1)S(1)} %get-tuple-element.91, bf16[15,1024]{1,0:T(8,128)(2,1)} %collective-permute-done.3, bf16[15,1024]{1,0:T(8,128)(2,1)} %collective-permute-done.2, bf16[1,128,1024]{2,1,0:T(8,128)(2,1)} %param.10, f32[1024]{0:T(1024)} %bitcast.271, f32[1024]{0:T(1024)} %bitcast.273, ...), kind=kLoop, calls=%fused_computation.185 | loop fusion | flops 24379392 | bytes 974976 | tf_op jit(solution)/shard_map/convert_element_type | solution.py:159
  112.4 2.6 %fusion.9 = f32[1,8,34,1024]{3,1,2,0:T(8,128)} fusion(s32[]{:T(128)S(6)} %select_n.148, f32[2,8,32,1024]{3,1,2,0:T(8,128)} %copy-done.1, f32[2,8,2,1024]{3,1,2,0:T(8,128)S(1)} %copy-done.10, bf16[1,8,34,1024]{3,1,2,0:T(8,128)(2,1)} %collective-permute-done.10), kind=kLoop, calls=%fused_computation.114 | loop fusion | flops 835584 | bytes 3899396 | tf_op jit(solution)/shard_map/add | solution.py:65
  115.0 2.9 %reshape_squeeze.15 = f32[4,2,34,1024]{3,1,0,2:T(2,128)} reshape(f32[1,8,34,1024]{3,1,2,0:T(8,128)} %fusion.9) | data formatting | bytes 2228224 | tf_op jit(solution)/shard_map/reshape;squeeze | solution.py:61
  117.9 1.9 constant_dynamic-slice_fusion.1
  120.1 2.2 %multiply_convert_fusion = bf16[8,128,896]{1,2,0:T(8,128)(2,1)} fusion(bf16[8,128,896]{1,2,0:T(8,128)(2,1)S(1)} %fusion.3, bf16[128,8,64]{0,2,1:T(8,128)(2,1)S(1)} %bitcast.203, bf16[896,8,64]{0,2,1:T(8,128)(2,1)S(1)} %copy-done.5, f32[8,128]{1,0:T(8,128)S(1)} %bitcast.305), kind=kOutput, calls=%fused_computation.41 | convolution fusion | flops 121110528 | bytes 4722688 | tf_op jit(solution)/shard_map/qhd,khd->hqk/dot_general | solution.py:185
  122.9 6.2 %collective-permute-done.11 = bf16[4,34,1024]{2,0,1:T(4,128)(2,1)S(1)} collective-permute-done((bf16[4,34,1024]{2,0,1:T(4,128)(2,1)S(1)}, bf16[4,34,1024]{2,0,1:T(4,128)(2,1)S(1)}, u32[]{:S(2)}, u32[]{:S(2)}) %collective-permute-start.11) | collective-permute-done | bytes 278560 | tf_op jit(solution)/shard_map/ppermute | solution.py:54
  130.1 1.5 reshape.101
  132.0 1.8 collective-permute-start.12
  133.8 3.0 %convolution_bitcast_fusion = f32[896,8,64]{0,2,1:T(8,128)} fusion(bf16[128,8,64]{0,2,1:T(8,128)(2,1)} %bitcast.204, bf16[8,128,896]{1,2,0:T(8,128)(2,1)S(1)} %fusion.3), kind=kOutput, calls=%fused_computation.48 | convolution fusion | flops 117440512 | bytes 3801088 | tf_op jit(solution)/shard_map/hqk,qhd->khd/dot_general | solution.py:200
  138.6 2.1 multiply_bitcast_fusion
  140.6 1.6 stack_reshape.6
  142.2 5.3 %collective-permute-done.13 = bf16[1,34,1024]{2,0,1:T(2,128)(2,1)} collective-permute-done((bf16[1,34,1024]{2,0,1:T(2,128)(2,1)}, bf16[1,34,1024]{2,0,1:T(2,128)(2,1)}, u32[]{:S(2)}, u32[]{:S(2)}) %collective-permute-start.13) | collective-permute-done | bytes 69664 | tf_op jit(solution)/shard_map/ppermute | solution.py:54
  147.5 1.8 add_convert_fusion.1
  149.3 1.5 constant_dynamic-update-slice_fusion.1
  150.8 1.6 stack_reshape.7
  152.4 5.2 %collective-permute-done.14 = bf16[1,34,1024]{2,0,1:T(2,128)(2,1)S(1)} collective-permute-done((bf16[1,34,1024]{2,0,1:T(2,128)(2,1)}, bf16[1,34,1024]{2,0,1:T(2,128)(2,1)S(1)}, u32[]{:S(2)}, u32[]{:S(2)}) %collective-permute-start.14) | collective-permute-done | bytes 69664 | tf_op jit(solution)/shard_map/ppermute | solution.py:54
  158.9 1.5 constant_dynamic-update-slice_fusion
  160.4 2.5 %convert.16 = bf16[7,2,128,512]{2,0,3,1:T(8,128)(2,1)S(1)} convert(f32[7,2,128,512]{2,0,3,1:T(8,128)} %constant_dynamic-update-slice_fusion) | non-fusion elementwise | flops 917504 | bytes 5505024 | tf_op jit(solution)/shard_map/convert.11
  163.0 2.0 collective-permute-done.15
  168.3 2.3 %fusion.153 = (bf16[1,2,128,512]{2,0,3,1:T(2,128)(2,1)S(1)}, bf16[1,2,128,512]{2,0,3,1:T(2,128)(2,1)S(1)}, bf16[1,2,128,512]{2,0,3,1:T(2,128)(2,1)S(1)}, bf16[1,...) fusion(bf16[7,2,128,512]{2,0,3,1:T(8,128)(2,1)S(1)} %convert.16), kind=kLoop, calls=%fused_computation.353 | loop fusion | bytes 3145728 | tf_op jit(solution)/shard_map/slice | solution.py:47
  171.4 3.4 %collective-permute-start.9 = (bf16[2,128,512]{1,2,0:T(8,128)(2,1)}, bf16[2,128,512]{1,2,0:T(8,128)(2,1)}, u32[]{:S(2)}, u32[]{:S(2)}) collective-permute-start(bf16[2,128,512]{1,2,0:T(8,128)(2,1)} %bitcast.191), channel_id=1, source_target_pairs={{0,6},{2,8},{4,10},{6,12},{8,14},{1,7},{3,9},{5,11},{7,13},{9,15},... | collective-permute-start | bytes 786440 | tf_op jit(solution)/shard_map/ppermute | solution.py:17
  175.6 3.7 %collective-permute-start.8 = (bf16[2,128,512]{1,2,0:T(8,128)(2,1)}, bf16[2,128,512]{1,2,0:T(8,128)(2,1)}, u32[]{:S(2)}, u32[]{:S(2)}) collective-permute-start(bf16[2,128,512]{1,2,0:T(8,128)(2,1)} %bitcast.192), channel_id=1, source_target_pairs={{0,4},{2,6},{4,8},{6,10},{8,12},{10,14},{1,5},{3,7},{5,9},{7,11},{... | collective-permute-start | bytes 786440 | tf_op jit(solution)/shard_map/ppermute | solution.py:17
  180.0 3.0 %collective-permute-start.7 = (bf16[2,128,512]{1,2,0:T(8,128)(2,1)}, bf16[2,128,512]{1,2,0:T(8,128)(2,1)}, u32[]{:S(2)}, u32[]{:S(2)}) collective-permute-start(bf16[2,128,512]{1,2,0:T(8,128)(2,1)} %bitcast.193), channel_id=1, source_target_pairs={{0,2},{2,4},{4,6},{6,8},{8,10},{10,12},{12,14},{1,3},{3,5},{5,7},{... | collective-permute-start | bytes 786440 | tf_op jit(solution)/shard_map/ppermute | solution.py:17
  183.7 3.5 %collective-permute-start.6 = (bf16[2,128,512]{1,2,0:T(8,128)(2,1)}, bf16[2,128,512]{1,2,0:T(8,128)(2,1)}, u32[]{:S(2)}, u32[]{:S(2)}) collective-permute-start(bf16[2,128,512]{1,2,0:T(8,128)(2,1)} %bitcast.194), channel_id=1, source_target_pairs={{2,0},{4,2},{6,4},{8,6},{10,8},{12,10},{14,12},{3,1},{5,3},{7,5},{... | collective-permute-start | bytes 786440 | tf_op jit(solution)/shard_map/ppermute | solution.py:17
  188.8 1.4 collective-permute-start.5
  190.8 1.4 copy.309
  192.2 1.9 broadcast_in_dim_reshape.3
  195.5 2.3 %fusion.5 = bf16[8,64,128]{2,1,0:T(8,128)(2,1)} fusion(bf16[896,8,64]{0,2,1:T(8,128)(2,1)} %copy-done.4, bf16[8,128,896]{1,2,0:T(8,128)(2,1)S(1)} %copy-done.3), kind=kOutput, calls=%fused_computation.108 | convolution fusion | flops 117571584 | bytes 2883584 | tf_op jit(solution)/shard_map/hqk,khd->qhd/dot_general | solution.py:192
  197.9 2.7 %slice.685 = f32[1,2,128,512]{2,0,3,1:T(1,128)S(1)} slice(f32[7,2,128,512]{2,0,3,1:T(8,128)} %constant_dynamic-update-slice_fusion), slice={[3:4], [0:2], [0:128], [0:512]} | slice | bytes 1048576 | tf_op jit(solution)/shard_map/slice | solution.py:44
  200.6 1.7 copy.312
  202.3 7.7 %collective-permute-done.4 = bf16[2,128,512]{1,2,0:T(8,128)(2,1)} collective-permute-done((bf16[2,128,512]{1,2,0:T(8,128)(2,1)}, bf16[2,128,512]{1,2,0:T(8,128)(2,1)}, u32[]{:S(2)}, u32[]{:S(2)}) %collective-permute-start.4) | collective-permute-done | bytes 262176 | tf_op jit(solution)/shard_map/ppermute | solution.py:17
  210.0 1.6 add_convert_fusion
  214.5 1.5 copy.310
  (117 shorter events, 35.0 us)
Async XLA Ops:
  0.6 69.3 %copy-start = (bf16[512,1024]{1,0:T(8,128)(2,1)S(1)}, bf16[512,1024]{1,0:T(8,128)(2,1)}, u32[]{:S(2)}) copy-start(bf16[512,1024]{1,0:T(8,128)(2,1)} %param.11) | copy-start | bytes 3145732
  3.6 7.1 %copy-start.16 = (bf16[1,128,512]{2,1,0:T(8,128)(2,1)S(1)}, bf16[1,128,512]{2,1,0:T(8,128)(2,1)}, u32[]{:S(2)}) copy-start(bf16[1,128,512]{2,1,0:T(8,128)(2,1)} %param.7) | copy-start | bytes 393220
  3.6 7.8 %copy-start.17 = (f32[31,1024]{1,0:T(8,128)S(1)}, f32[31,1024]{1,0:T(8,128)}, u32[]{:S(2)}) copy-start(f32[31,1024]{1,0:T(8,128)} %param.12) | copy-start | bytes 380932
  3.6 54.1 %all-to-all-start = ((bf16[8,2,128,512]{2,3,1,0:T(8,128)(2,1)}), bf16[8,2,128,512]{2,3,1,0:T(8,128)(2,1)S(1)}, u32[]{:S(2)}, u32[]{:S(2)}) async-start(bf16[8,2,128,512]{2,3,1,0:T(8,128)(2,1)} %broadcast_in_dim.44), calls=%async_computation | async-start | bytes 4194304 | tf_op jit(solution)/shard_map/all_to_all | solution.py:109
  10.9 49.8 %copy-start.11 = (bf16[1,128,512]{1,2,0:T(8,128)(2,1)}, bf16[1,128,512]{1,2,0:T(8,128)(2,1)S(1)}, u32[]{:S(2)}) copy-start(bf16[1,128,512]{1,2,0:T(8,128)(2,1)S(1)} %copy.283) | copy-start | bytes 393220
  60.7 1.1 copy-start.4
  62.6 1.2 copy-start.7
  65.4 4.6 %copy-start.18 = (pred[128]{0:T(512)(128)(4,1)S(1)}, pred[128]{0:T(512)(128)(4,1)}, u32[]{:S(2)}) copy-start(pred[128]{0:T(512)(128)(4,1)} %add_compare_fusion) | copy-start | bytes 388
  70.3 8.5 %collective-permute-start.1 = (bf16[15,1024]{1,0:T(8,128)(2,1)S(1)}, bf16[15,1024]{1,0:T(8,128)(2,1)S(1)}, u32[]{:S(2)}, u32[]{:S(2)}) collective-permute-start(bf16[15,1024]{1,0:T(8,128)(2,1)S(1)} %get-tuple-element.113), channel_id=1, source_target_pairs={{2,0},{4,2},{6,4},{8,6},{10,8},{12,10},{14,12},{3,1},{5,3},{7,5},{... | collective-permute-start | bytes 92168 | tf_op jit(solution)/shard_map/ppermute | solution.py:30
  72.8 6.1 %collective-permute-start = (bf16[15,1024]{1,0:T(8,128)(2,1)S(1)}, bf16[15,1024]{1,0:T(8,128)(2,1)S(1)}, u32[]{:S(2)}, u32[]{:S(2)}) collective-permute-start(bf16[15,1024]{1,0:T(8,128)(2,1)S(1)} %get-tuple-element.112), channel_id=1, source_target_pairs={{0,2},{2,4},{4,6},{6,8},{8,10},{10,12},{12,14},{1,3},{3,5},{5,7},{... | collective-permute-start | bytes 92168 | tf_op jit(solution)/shard_map/ppermute | solution.py:28
  78.9 0.6 copy-start.15
  78.9 0.6 copy-start.13
  79.5 19.0 %copy-start.14 = (bf16[15,1024]{1,0:T(8,128)(2,1)S(1)}, bf16[15,1024]{1,0:T(8,128)(2,1)}, u32[]{:S(2)}) copy-start(bf16[15,1024]{1,0:T(8,128)(2,1)} %copy-done.13) | copy-start | bytes 92164
  87.0 15.9 %collective-permute-start.3 = (bf16[15,1024]{1,0:T(8,128)(2,1)}, bf16[15,1024]{1,0:T(8,128)(2,1)}, u32[]{:S(2)}, u32[]{:S(2)}) collective-permute-start(bf16[15,1024]{1,0:T(8,128)(2,1)} %get-tuple-element.111), channel_id=1, source_target_pairs={{0,2},{2,4},{4,6},{6,8},{8,10},{10,12},{12,14},{1,3},{3,5},{5,7},{... | collective-permute-start | bytes 92168 | tf_op jit(solution)/shard_map/ppermute | solution.py:28
  91.8 11.1 %collective-permute-start.2 = (bf16[15,1024]{1,0:T(8,128)(2,1)}, bf16[15,1024]{1,0:T(8,128)(2,1)}, u32[]{:S(2)}, u32[]{:S(2)}) collective-permute-start(bf16[15,1024]{1,0:T(8,128)(2,1)} %get-tuple-element.110), channel_id=1, source_target_pairs={{2,0},{4,2},{6,4},{8,6},{10,8},{12,10},{14,12},{3,1},{5,3},{7,5},{... | collective-permute-start | bytes 92168 | tf_op jit(solution)/shard_map/ppermute | solution.py:30
  102.9 7.2 %copy-start.9 = (f32[2,8,2,1024]{3,1,2,0:T(8,128)}, f32[2,8,2,1024]{3,1,2,0:T(8,128)S(1)}, u32[]{:S(2)}) copy-start(f32[2,8,2,1024]{3,1,2,0:T(8,128)S(1)} %copy.304) | copy-start | bytes 393220
  107.9 1.3 copy-start.1
  110.1 2.3 %collective-permute-start.10 = (bf16[1,8,34,1024]{3,1,2,0:T(8,128)(2,1)}, bf16[1,8,34,1024]{3,1,2,0:T(8,128)(2,1)}, u32[]{:S(2)}, u32[]{:S(2)}) collective-permute-start(bf16[1,8,34,1024]{3,1,2,0:T(8,128)(2,1)} %fusion.7), channel_id=1, source_target_pairs={{0,1},{1,0},{2,3},{3,2},{4,5},{5,4},{6,7},{7,6},{8,9},{9,8},{10,11... | collective-permute-start | bytes 1671176 | tf_op jit(solution)/shard_map/ppermute | solution.py:54
  110.1 2.3 %copy-start.10 = (f32[2,8,2,1024]{3,1,2,0:T(8,128)S(1)}, f32[2,8,2,1024]{3,1,2,0:T(8,128)}, u32[]{:S(2)}) copy-start(f32[2,8,2,1024]{3,1,2,0:T(8,128)} %copy-done.9) | copy-start | bytes 393220
  112.3 7.7 %copy-start.8 = (bf16[128,512]{0,1:T(8,128)(2,1)}, bf16[128,512]{0,1:T(8,128)(2,1)S(1)}, u32[]{:S(2)}) copy-start(bf16[128,512]{0,1:T(8,128)(2,1)S(1)} %copy.286) | copy-start | bytes 393220
  117.9 2.2 %copy-start.5 = (bf16[896,8,64]{0,2,1:T(8,128)(2,1)S(1)}, bf16[896,8,64]{0,2,1:T(8,128)(2,1)}, u32[]{:S(2)}) copy-start(bf16[896,8,64]{0,2,1:T(8,128)(2,1)} %reshape_squeeze.14) | copy-start | bytes 2752516
  119.9 9.1 %collective-permute-start.11 = (bf16[4,34,1024]{2,0,1:T(4,128)(2,1)S(1)}, bf16[4,34,1024]{2,0,1:T(4,128)(2,1)S(1)}, u32[]{:S(2)}, u32[]{:S(2)}) collective-permute-start(bf16[4,34,1024]{2,0,1:T(4,128)(2,1)S(1)} %bitcast.209), channel_id=1, source_target_pairs={{0,2},{2,0},{4,6},{6,4},{8,10},{10,8},{12,14},{14,12},{1,3},{3,1},... | collective-permute-start | bytes 835592 | tf_op jit(solution)/shard_map/ppermute | solution.py:54
  120.0 2.2 %copy-start.6 = (f32[4,2,34,1024]{3,1,0,2:T(2,128)S(1)}, f32[4,2,34,1024]{3,1,0,2:T(2,128)}, u32[]{:S(2)}) copy-start(f32[4,2,34,1024]{3,1,0,2:T(2,128)} %reshape_squeeze.15) | copy-start | bytes 3342340
  132.0 6.6 %copy-start.2 = (bf16[8,128,896]{1,2,0:T(8,128)(2,1)S(1)}, bf16[8,128,896]{1,2,0:T(8,128)(2,1)}, u32[]{:S(2)}) copy-start(bf16[8,128,896]{1,2,0:T(8,128)(2,1)} %multiply_convert_fusion) | copy-start | bytes 5505028
  132.0 6.6 %copy-start.12 = (bf16[1,128,512]{1,2,0:T(8,128)(2,1)S(1)}, bf16[1,128,512]{1,2,0:T(8,128)(2,1)}, u32[]{:S(2)}) copy-start(bf16[1,128,512]{1,2,0:T(8,128)(2,1)} %copy-done.11) | copy-start | bytes 393220
  132.0 5.5 %collective-permute-start.12 = (bf16[2,34,1024]{2,0,1:T(2,128)(2,1)S(1)}, bf16[2,34,1024]{2,0,1:T(2,128)(2,1)S(1)}, u32[]{:S(2)}, u32[]{:S(2)}) collective-permute-start(bf16[2,34,1024]{2,0,1:T(2,128)(2,1)S(1)} %bitcast.211), channel_id=1, source_target_pairs={{0,4},{2,6},{4,0},{6,2},{8,12},{10,14},{12,8},{14,10},{1,5},{3,7},... | collective-permute-start | bytes 417800 | tf_op jit(solution)/shard_map/ppermute | solution.py:54
  138.6 9.0 %collective-permute-start.13 = (bf16[1,34,1024]{2,0,1:T(2,128)(2,1)}, bf16[1,34,1024]{2,0,1:T(2,128)(2,1)}, u32[]{:S(2)}, u32[]{:S(2)}) collective-permute-start(bf16[1,34,1024]{2,0,1:T(2,128)(2,1)} %dynamic-slice_convert_fusion.1), channel_id=1, source_target_pairs={{0,8},{2,10},{4,12},{6,14},{8,0},{10,2},{12,4},{14,6},{1,9},{3,11}... | collective-permute-start | bytes 208904 | tf_op jit(solution)/shard_map/ppermute | solution.py:54
  149.3 8.2 %collective-permute-start.14 = (bf16[1,34,1024]{2,0,1:T(2,128)(2,1)}, bf16[1,34,1024]{2,0,1:T(2,128)(2,1)S(1)}, u32[]{:S(2)}, u32[]{:S(2)}) collective-permute-start(bf16[1,34,1024]{2,0,1:T(2,128)(2,1)} %add_convert_fusion.1), channel_id=1, source_target_pairs={{0,8},{2,10},{4,12},{6,14},{8,0},{10,2},{12,4},{14,6},{1,9},{3,11}... | collective-permute-start | bytes 208904 | tf_op jit(solution)/shard_map/ppermute | solution.py:54
  158.8 6.2 %collective-permute-start.15 = (bf16[2,34,1024]{2,1,0:T(8,128)(2,1)S(1)}, bf16[2,34,1024]{2,1,0:T(8,128)(2,1)S(1)}, u32[]{:S(2)}, u32[]{:S(2)}) collective-permute-start(bf16[2,34,1024]{2,1,0:T(8,128)(2,1)S(1)} %maximum_bitcast_fusion.1), channel_id=1, source_target_pairs={{0,4},{2,6},{4,0},{6,2},{8,12},{10,14},{12,8},{14,10},{1,5},{3,7},... | collective-permute-start | bytes 417800 | tf_op jit(solution)/shard_map/ppermute | solution.py:54
  167.1 21.6 %collective-permute-start.16 = (bf16[4,34,1024]{2,0,1:T(4,128)(2,1)S(1)}, bf16[4,34,1024]{2,0,1:T(4,128)(2,1)S(1)}, u32[]{:S(2)}, u32[]{:S(2)}) collective-permute-start(bf16[4,34,1024]{2,0,1:T(4,128)(2,1)S(1)} %reshape.103), channel_id=1, source_target_pairs={{0,2},{2,0},{4,6},{6,4},{8,10},{10,8},{12,14},{14,12},{1,3},{3,1},... | collective-permute-start | bytes 835592 | tf_op jit(solution)/shard_map/ppermute | solution.py:54
  171.4 22.7 %collective-permute-start.9 = (bf16[2,128,512]{1,2,0:T(8,128)(2,1)}, bf16[2,128,512]{1,2,0:T(8,128)(2,1)}, u32[]{:S(2)}, u32[]{:S(2)}) collective-permute-start(bf16[2,128,512]{1,2,0:T(8,128)(2,1)} %bitcast.191), channel_id=1, source_target_pairs={{0,6},{2,8},{4,10},{6,12},{8,14},{1,7},{3,9},{5,11},{7,13},{9,15},... | collective-permute-start | bytes 786440 | tf_op jit(solution)/shard_map/ppermute | solution.py:17
  175.6 19.8 %collective-permute-start.8 = (bf16[2,128,512]{1,2,0:T(8,128)(2,1)}, bf16[2,128,512]{1,2,0:T(8,128)(2,1)}, u32[]{:S(2)}, u32[]{:S(2)}) collective-permute-start(bf16[2,128,512]{1,2,0:T(8,128)(2,1)} %bitcast.192), channel_id=1, source_target_pairs={{0,4},{2,6},{4,8},{6,10},{8,12},{10,14},{1,5},{3,7},{5,9},{7,11},{... | collective-permute-start | bytes 786440 | tf_op jit(solution)/shard_map/ppermute | solution.py:17
  180.0 22.2 %collective-permute-start.7 = (bf16[2,128,512]{1,2,0:T(8,128)(2,1)}, bf16[2,128,512]{1,2,0:T(8,128)(2,1)}, u32[]{:S(2)}, u32[]{:S(2)}) collective-permute-start(bf16[2,128,512]{1,2,0:T(8,128)(2,1)} %bitcast.193), channel_id=1, source_target_pairs={{0,2},{2,4},{4,6},{6,8},{8,10},{10,12},{12,14},{1,3},{3,5},{5,7},{... | collective-permute-start | bytes 786440 | tf_op jit(solution)/shard_map/ppermute | solution.py:17
  183.7 18.5 %collective-permute-start.6 = (bf16[2,128,512]{1,2,0:T(8,128)(2,1)}, bf16[2,128,512]{1,2,0:T(8,128)(2,1)}, u32[]{:S(2)}, u32[]{:S(2)}) collective-permute-start(bf16[2,128,512]{1,2,0:T(8,128)(2,1)} %bitcast.194), channel_id=1, source_target_pairs={{2,0},{4,2},{6,4},{8,6},{10,8},{12,10},{14,12},{3,1},{5,3},{7,5},{... | collective-permute-start | bytes 786440 | tf_op jit(solution)/shard_map/ppermute | solution.py:17
  188.8 6.8 %copy-start.3 = (bf16[8,128,896]{1,2,0:T(8,128)(2,1)S(1)}, bf16[8,128,896]{1,2,0:T(8,128)(2,1)}, u32[]{:S(2)}) copy-start(bf16[8,128,896]{1,2,0:T(8,128)(2,1)} %multiply_convert_fusion) | copy-start | bytes 5505028
  188.8 13.5 %collective-permute-start.5 = (bf16[2,128,512]{1,2,0:T(8,128)(2,1)}, bf16[2,128,512]{1,2,0:T(8,128)(2,1)}, u32[]{:S(2)}, u32[]{:S(2)}) collective-permute-start(bf16[2,128,512]{1,2,0:T(8,128)(2,1)} %bitcast.195), channel_id=1, source_target_pairs={{4,0},{6,2},{8,4},{10,6},{12,8},{14,10},{5,1},{7,3},{9,5},{11,7},{... | collective-permute-start | bytes 786440 | tf_op jit(solution)/shard_map/ppermute | solution.py:17
  194.1 15.9 %collective-permute-start.4 = (bf16[2,128,512]{1,2,0:T(8,128)(2,1)}, bf16[2,128,512]{1,2,0:T(8,128)(2,1)}, u32[]{:S(2)}, u32[]{:S(2)}) collective-permute-start(bf16[2,128,512]{1,2,0:T(8,128)(2,1)} %bitcast.210), channel_id=1, source_target_pairs={{6,0},{8,2},{10,4},{12,6},{14,8},{7,1},{9,3},{11,5},{13,7},{15,9},... | collective-permute-start | bytes 786440 | tf_op jit(solution)/shard_map/ppermute | solution.py:17
  195.4 17.7 %collective-permute-start.17 = (bf16[1,8,34,1024]{3,1,2,0:T(8,128)(2,1)S(1)}, bf16[1,8,34,1024]{3,1,2,0:T(8,128)(2,1)}, u32[]{:S(2)}, u32[]{:S(2)}) collective-permute-start(bf16[1,8,34,1024]{3,1,2,0:T(8,128)(2,1)S(1)} %broadcast_in_dim_reshape.3), channel_id=1, source_target_pairs={{0,1},{1,0},{2,3},{3,2},{4,5},{5,4},{6,7},{7,6},{8,9},{9,8},{10,11... | collective-permute-start | bytes 1671176 | tf_op jit(solution)/shard_map/ppermute | solution.py:54

commit v6 on v4

--- a/solution.py
+++ b/solution.py
@@ -35,18 +35,28 @@
 
 
 def collect(piece_own, shifter):
-    from_below = [shifter(piece_own, distance) for distance in range(REACH, 0, -1)]
-    from_above = [shifter(piece_own, -distance) for distance in range(1, REACH + 1)]
-    return jnp.stack(from_below + [piece_own] + from_above, axis=0)
+    below_one = shifter(piece_own, 1)
+    above_one = shifter(piece_own, -1)
+    below = shifter(jnp.stack([below_one, piece_own], axis=0), 2)
+    above = shifter(jnp.stack([piece_own, above_one], axis=0), -2)
+    return jnp.stack(
+        [below[0], below[1], below_one, piece_own, above_one, above[0], above[1]], axis=0
+    )
 
 
 def give_back(partials, shifter):
-    total = partials[REACH]
-    for offset in range(2 * REACH + 1):
-        if offset != REACH:
-            moved = shifter(partials[offset].astype(jnp.bfloat16), offset - REACH)
-            total = total + moved.astype(jnp.float32)
-    return total
+    narrow = partials.astype(jnp.bfloat16)
+    from_below = shifter(narrow[REACH + 2 :], 2).astype(jnp.float32)
+    from_above = shifter(narrow[REACH - 2 :: -1], -2).astype(jnp.float32)
+    upward = (partials[REACH + 1] + from_below[1]).astype(jnp.bfloat16)
+    downward = (partials[REACH - 1] + from_above[1]).astype(jnp.bfloat16)
+    return (
+        partials[REACH]
+        + from_below[0]
+        + from_above[0]
+        + shifter(upward, 1).astype(jnp.float32)
+        + shifter(downward, -1).astype(jnp.float32)
+    )
 
 
 def exchange(block, axis, bit):

time: 202 us -> 201 us (level)
  local copies, waits for them, and re-layouts: 56.4 us -> 49.5 us
  waiting for transfers between devices: 44.3 us -> 49.5 us
  starting transfers between devices: 49.2 us -> 45.2 us
  other arithmetic: 33.8 us -> 36.2 us
    ppermute x8, waiting for transfers between devices: 19.2 us -> 26.8 us  [exchange(): return lax.ppermute(block, axis, [(i, i ^ bit) for i in range(count)])]
    ppermute x12 -> x8, starting transfers between devices: 32.6 us -> 25.5 us  [passed_along(): return lax.ppermute(block, axis, route)]
    convert_element_type x0 -> x4, other arithmetic: none -> 5.63 us  [the longest x1 1.7 us: give_back(): narrow = partials.astype(jnp.bfloat16)]
    another operation x3 -> x4, local copies, waits for them, and re-layouts: 4.71 us -> 10.1 us  [on_device(): jnp.stack([grad_key_all.reshape(span_blocks, tokens, width_heads), grad_v...]
    convert_element_type x6 -> x0, local copies, waits for them, and re-layouts: 4.51 us -> none  [give_back(): moved = shifter(partials[offset].astype(jnp.bfloat16), offset - REACH)]
    slice x2 -> x1, local copies, waits for them, and re-layouts: 5.05 us -> 0.86 us  [give_back(): from_below = shifter(narrow[REACH + 2:], 2).astype(jnp.float32)]
    ppermute x8, starting transfers between devices: 3.18 us -> 6.3 us  [exchange(): return lax.ppermute(block, axis, [(i, i ^ bit) for i in range(count)])]
    ppermute x12 -> x8, waiting for transfers between devices: 25.1 us -> 22.7 us  [passed_along(): return lax.ppermute(block, axis, route)]
  transfers between devices with their start and end apart: 24 -> 20, of which waited for: 10 -> 8; matrix products, arithmetic and copies ran while one was open for 27% -> 28% of each run, Pallas kernels for 0% -> 0%
where the time goes in v6:
time: 201 us; the launch traced here: 198 us
  local copies, waits for them, and re-layouts  49.5 us (25%)
  waiting for transfers between devices  49.5 us (25%)
  starting transfers between devices  45.2 us (22%)
  other arithmetic  36.2 us (18%)
  matrix products  15.4 us (8%)
  between operations  2.07 us (1%)
    ppermute x8, waiting for transfers between devices, exchange(): return lax.ppermute(block, axis, [(i, i ^ bit) for i in range(count)])  26.8 us
    ppermute x8, starting transfers between devices, passed_along(): return lax.ppermute(block, axis, route)  25.5 us
    ppermute x8, waiting for transfers between devices, passed_along(): return lax.ppermute(block, axis, route)  22.7 us
    reduce_sum x4, other arithmetic, on_device(): jnp.sum(padded_m[tap_index:tap_index + tokens].astype(jnp.float32) * grad...  12.4 us
    another operation x4, local copies, waits for them, and re-layouts, on_device(): jnp.stack([grad_key_all.reshape(span_blocks, tokens, width_heads), grad_v...  10.1 us
    ppermute x2, starting transfers between devices, padded(): lax.ppermute(tail, axis, [(i, (i + 1) % count) for i in range(ends)])  9.6 us
    unnamed x42, local copies, waits for them, and re-layouts  6.98 us
    ppermute x8, starting transfers between devices, exchange(): return lax.ppermute(block, axis, [(i, i ^ bit) for i in range(count)])  6.3 us
  transfers between devices with their start and end apart: 20, of which 8 were waited for; matrix products, arithmetic and copies ran while one was open for 28% of the time, Pallas kernels for 0%

profile of v6, /device:TPU:2, one launch (start us, length us, event | category | flops | bytes accessed | tf_op | source)
XLA Modules:
  0.0 198.0 jit_solution(8832250977433173518)
XLA Ops:
  2.6 1.9 collective-permute-start.2
  4.5 4.8 %collective-permute-start = (bf16[2,128,512]{2,1,0:T(8,128)(2,1)S(1)}, bf16[2,128,512]{2,1,0:T(8,128)(2,1)S(1)}, u32[]{:S(2)}, u32[]{:S(2)}) collective-permute-start(bf16[2,128,512]{2,1,0:T(8,128)(2,1)S(1)} %constant_dynamic-update-slice_fusion), channel_id=1, source_target_pairs={{0,2},{2,4},{4,6},{6,8},{8,10},{10,12},{12,14},{1,3},{3,5},{5,7},{... | collective-permute-start | bytes 786440 | tf_op jit(solution)/shard_map/ppermute | solution.py:17
  9.4 4.2 %collective-permute-done.2 = bf16[2,128,512]{2,1,0:T(8,128)(2,1)S(1)} collective-permute-done((bf16[2,128,512]{2,1,0:T(8,128)(2,1)S(1)}, bf16[2,128,512]{2,1,0:T(8,128)(2,1)S(1)}, u32[]{:S(2)}, u32[]{:S(2)}) %collective-permute-start.2) | collective-permute-done | bytes 262176 | tf_op jit(solution)/shard_map/ppermute | solution.py:17
  13.5 5.5 %collective-permute-done = bf16[2,128,512]{2,1,0:T(8,128)(2,1)S(1)} collective-permute-done((bf16[2,128,512]{2,1,0:T(8,128)(2,1)S(1)}, bf16[2,128,512]{2,1,0:T(8,128)(2,1)S(1)}, u32[]{:S(2)}, u32[]{:S(2)}) %collective-permute-start) | collective-permute-done | bytes 262176 | tf_op jit(solution)/shard_map/ppermute | solution.py:17
  19.2 4.3 %collective-permute-start.1 = (bf16[2,2,128,512]{3,2,1,0:T(8,128)(2,1)S(1)}, bf16[2,2,128,512]{3,2,1,0:T(8,128)(2,1)}, u32[]{:S(2)}, u32[]{:S(2)}) collective-permute-start(bf16[2,2,128,512]{3,2,1,0:T(8,128)(2,1)S(1)} %get-tuple-element.93), channel_id=1, source_target_pairs={{0,4},{2,6},{4,8},{6,10},{8,12},{10,14},{1,5},{3,7},{5,9},{7,11},{... | collective-permute-start | bytes 1572872 | tf_op jit(solution)/shard_map/ppermute | solution.py:17
  26.8 7.2 %collective-permute-done.1 = bf16[2,2,128,512]{3,2,1,0:T(8,128)(2,1)} collective-permute-done((bf16[2,2,128,512]{3,2,1,0:T(8,128)(2,1)S(1)}, bf16[2,2,128,512]{3,2,1,0:T(8,128)(2,1)}, u32[]{:S(2)}, u32[]{:S(2)}) %collective-permute-start.1) | collective-permute-done | bytes 524320 | tf_op jit(solution)/shard_map/ppermute | solution.py:17
  35.1 5.8 %collective-permute-done.3 = bf16[2,2,128,512]{3,2,1,0:T(8,128)(2,1)S(1)} collective-permute-done((bf16[2,2,128,512]{3,2,1,0:T(8,128)(2,1)S(1)}, bf16[2,2,128,512]{3,2,1,0:T(8,128)(2,1)S(1)}, u32[]{:S(2)}, u32[]{:S(2)}) %collective-permute-start.3) | collective-permute-done | bytes 524320 | tf_op jit(solution)/shard_map/ppermute | solution.py:17
  46.6 2.4 %copy.147 = bf16[7,1,128,512]{2,0,3,1:T(8,128)(2,1)} copy(bf16[7,1,128,512]{3,2,1,0:T(8,128)(2,1)} %get-tuple-element.76) | data formatting | bytes 1835008 | tf_op jit(solution)/shard_map/slice | solution.py:117
  49.0 2.9 %reshape_squeeze.14 = bf16[896,8,64]{0,2,1:T(8,128)(2,1)} reshape(bf16[7,1,128,512]{2,0,3,1:T(8,128)(2,1)} %copy.147) | data formatting | bytes 1835008 | tf_op jit(solution)/shard_map/reshape;squeeze | solution.py:117
  51.9 1.7 convolution_convert_fusion
  54.0 1.9 collective-permute-start.5
  55.9 4.8 %collective-permute-start.4 = (bf16[15,1024]{1,0:T(8,128)(2,1)S(1)}, bf16[15,1024]{1,0:T(8,128)(2,1)S(1)}, u32[]{:S(2)}, u32[]{:S(2)}) collective-permute-start(bf16[15,1024]{1,0:T(8,128)(2,1)S(1)} %get-tuple-element.90), channel_id=1, source_target_pairs={{0,2},{2,4},{4,6},{6,8},{8,10},{10,12},{12,14},{1,3},{3,5},{5,7},{... | collective-permute-start | bytes 92168 | tf_op jit(solution)/shard_map/ppermute | solution.py:28
  60.7 1.7 fusion.175
  63.2 6.8 %fusion.89 = (f32[1024]{0:T(1024)}, f32[1024]{0:T(1024)}, f32[1024]{0:T(1024)}, f32[1024]{0:T(1024)}, f32[1024]{0:T(1024)}, /*index=5*/f32[1024]{0:T(1024)}, f32...) fusion(bf16[15,1024]{1,0:T(8,128)(2,1)} %copy-done.12, bf16[128,1024]{1,0:T(8,128)(2,1)S(1)} %fusion.5, ...), kind=kLoop, calls=%fused_computation.238 | loop fusion | flops 31841280 | bytes 1011712 | tf_op jit(solution)/shard_map/reduce_sum | solution.py:154
  70.7 4.8 %collective-permute-start.7 = (bf16[15,1024]{1,0:T(8,128)(2,1)}, bf16[15,1024]{1,0:T(8,128)(2,1)}, u32[]{:S(2)}, u32[]{:S(2)}) collective-permute-start(bf16[15,1024]{1,0:T(8,128)(2,1)} %get-tuple-element.89), channel_id=1, source_target_pairs={{0,2},{2,4},{4,6},{6,8},{8,10},{10,12},{12,14},{1,3},{3,5},{5,7},{... | collective-permute-start | bytes 92168 | tf_op jit(solution)/shard_map/ppermute | solution.py:28
  75.5 1.9 collective-permute-start.6
  77.4 2.4 %fusion.73 = (f32[1024]{0:T(1024)}, f32[1024]{0:T(1024)}, f32[1024]{0:T(1024)}, f32[1024]{0:T(1024)}, f32[1024]{0:T(1024)}, /*index=5*/f32[1024]{0:T(1024)}, f32[1024]{0:T(1024)}, f32[1024]{0:T(1024)}, f32[1024]{0:T(1024)}) fusion(bf16[128,1024]{1,0:T(8,128)(2,1)S(1)} %get-tuple-element.71, bf16[128,1024]{1,0:T(8,128)(2,1)S(1)} %fusion.5, ...), kind=kLoop, calls=%fused_computation.222 | loop fusion | flops 7199744 | bytes 591872 | tf_op jit(solution)/shard_map/reduce_sum | solution.py:154
  79.8 2.2 %fusion.88 = (f32[1024]{0:T(1024)}, f32[1024]{0:T(1024)}, f32[1024]{0:T(1024)}, f32[1024]{0:T(1024)}, f32[1024]{0:T(1024)}, /*index=5*/f32[1024]{0:T(1024)}, f32[1024]{0:T(1024)}) fusion(bf16[128,1024]{1,0:T(8,128)(2,1)S(1)} %get-tuple-element.71, bf16[15,1024]{1,0:T(8,128)(2,1)} %copy-done.12, bf16[128,1024]{1,0:T(8,128)(2,1)S(1)} %fusion.5), kind=kLoop, calls=%fused_computation.237 | loop fusion | flops 5235712 | bytes 583680 | tf_op jit(solution)/shard_map/reduce_sum | solution.py:154
  83.0 3.1 %stack.200 = f32[31,1024]{1,0:T(8,128)S(1)} concatenate(f32[1,1024]{1,0:T(1,128)} %bitcast.294, f32[1,1024]{1,0:T(1,128)} %bitcast.296, f32[1,1024]{1,0:T(1,128)} %bitcast.295, f32[1,1024]{1,0:T(1,128)} %bitcast.297, f32[1,1024]{1,0:T(1,128)} %bitcast.277, f32[1,1024]{1,0:T(1,128)} %bitcast.278, f32[1,1024]{1,0:T(1,128)} %bitcast.279, f32[1,1024]{1,0:T(1,128)} %bitcast.280, ...), dimensions={0} | concatenate | bytes 253952 | tf_op jit(solution)/shard_map/stack | solution.py:158
  87.8 5.0 %fusion.42 = bf16[128,1024]{1,0:T(8,128)(2,1)S(1)} fusion(bf16[128,1024]{1,0:T(8,128)(2,1)S(1)} %get-tuple-element.71, bf16[15,1024]{1,0:T(8,128)(2,1)} %collective-permute-done.7, bf16[15,1024]{1,0:T(8,128)(2,1)} %collective-permute-done.6, bf16[1,128,1024]{2,1,0:T(8,128)(2,1)} %param.10, f32[1024]{0:T(1024)} %bitcast.264, f32[1024]{0:T(1024)} %bitcast.266, ...), kind=kLoop, calls=%fused_computation.191 | loop fusion | flops 24379392 | bytes 974976 | tf_op jit(solution)/shard_map/convert_element_type | solution.py:161
  96.1 3.5 %multiply_convert_fusion = bf16[8,128,896]{1,2,0:T(8,128)(2,1)} fusion(bf16[8,128,896]{1,2,0:T(8,128)(2,1)S(1)} %fusion.4, bf16[128,8,64]{0,2,1:T(8,128)(2,1)S(1)} %bitcast.195, bf16[896,8,64]{0,2,1:T(8,128)(2,1)} %reshape_squeeze.14, f32[8,128]{1,0:T(8,128)S(1)} %bitcast.298), kind=kOutput, calls=%fused_computation.47 | convolution fusion | flops 121110528 | bytes 4722688 | tf_op jit(solution)/shard_map/qhd,khd->hqk/dot_general | solution.py:187
  99.6 2.2 %fusion.10 = f32[1,8,34,1024]{3,1,2,0:T(8,128)} fusion(s32[]{:T(128)S(6)} %select_n.144, f32[2,8,32,1024]{3,1,2,0:T(8,128)S(1)} %copy-done.3, f32[2,8,2,1024]{3,1,2,0:T(8,128)S(1)} %copy.157, bf16[1,8,34,1024]{3,1,2,0:T(8,128)(2,1)} %collective-permute-done.12), kind=kLoop, calls=%fused_computation.120 | loop fusion | flops 835584 | bytes 3899396 | tf_op jit(solution)/shard_map/add | solution.py:75
  101.8 2.9 %reshape_squeeze.15 = f32[4,2,34,1024]{3,1,0,2:T(2,128)} reshape(f32[1,8,34,1024]{3,1,2,0:T(8,128)} %fusion.10) | data formatting | bytes 2228224 | tf_op jit(solution)/shard_map/reshape;squeeze | solution.py:71
  104.7 1.8 constant_dynamic-slice_fusion.1
  106.8 2.1 %convolution_bitcast_fusion = f32[896,8,64]{0,2,1:T(8,128)} fusion(bf16[128,8,64]{0,2,1:T(8,128)(2,1)S(1)} %bitcast.196, bf16[8,128,896]{1,2,0:T(8,128)(2,1)S(1)} %fusion.4), kind=kOutput, calls=%fused_computation.54 | convolution fusion | flops 117440512 | bytes 3801088 | tf_op jit(solution)/shard_map/hqk,qhd->khd/dot_general | solution.py:202
  109.5 6.4 %collective-permute-done.13 = bf16[4,34,1024]{2,0,1:T(4,128)(2,1)S(1)} collective-permute-done((bf16[4,34,1024]{2,0,1:T(4,128)(2,1)S(1)}, bf16[4,34,1024]{2,0,1:T(4,128)(2,1)S(1)}, u32[]{:S(2)}, u32[]{:S(2)}) %collective-permute-start.13) | collective-permute-done | bytes 278560 | tf_op jit(solution)/shard_map/ppermute | solution.py:64
  116.8 1.5 reshape.100
  119.4 1.7 collective-permute-start.14
  121.1 3.0 %multiply_bitcast_fusion = f32[896,8,64]{0,2,1:T(8,128)} fusion(bf16[8,128,896]{1,2,0:T(8,128)(2,1)S(1)} %copy-done.4, bf16[128,8,64]{0,2,1:T(8,128)(2,1)} %bitcast.199), kind=kOutput, calls=%fused_computation.53 | convolution fusion | flops 117899264 | bytes 3801088 | tf_op jit(solution)/shard_map/hqk,qhd->khd/dot_general | solution.py:199
  124.1 2.7 %stack_reshape.7 = f32[7,1,128,512]{2,0,3,1:T(8,128)} reshape(f32[896,8,64]{0,2,1:T(8,128)} %convolution_bitcast_fusion) | data formatting | bytes 3670016 | tf_op jit(solution)/shard_map/stack;reshape | solution.py:205
  126.8 1.9 copy.155
  128.7 2.7 %stack_reshape.6 = f32[7,1,128,512]{2,0,3,1:T(8,128)} reshape(f32[896,8,64]{0,2,1:T(8,128)} %multiply_bitcast_fusion) | data formatting | bytes 3670016 | tf_op jit(solution)/shard_map/stack;reshape | solution.py:205
  131.4 2.8 %copy.154 = f32[7,1,128,512]{3,2,1,0:T(8,128)} copy(f32[7,1,128,512]{2,0,3,1:T(8,128)} %stack_reshape.6) | data formatting | bytes 3670016 | tf_op jit(solution)/shard_map/stack;reshape | solution.py:205
  136.4 1.7 fusion
  138.1 6.6 %collective-permute-done.15 = bf16[1,34,1024]{2,0,1:T(2,128)(2,1)S(1)} collective-permute-done((bf16[1,34,1024]{2,0,1:T(2,128)(2,1)S(1)}, bf16[1,34,1024]{2,0,1:T(2,128)(2,1)S(1)}, u32[]{:S(2)}, u32[]{:S(2)}) %collective-permute-start.15) | collective-permute-done | bytes 69664 | tf_op jit(solution)/shard_map/ppermute | solution.py:64
  145.9 4.9 %collective-permute-start.8 = (bf16[2,2,128,512]{3,2,1,0:T(8,128)(2,1)}, bf16[2,2,128,512]{3,2,1,0:T(8,128)(2,1)}, u32[]{:S(2)}, u32[]{:S(2)}) collective-permute-start(bf16[2,2,128,512]{3,2,1,0:T(8,128)(2,1)} %get-tuple-element.74), channel_id=1, source_target_pairs={{0,4},{2,6},{4,8},{6,10},{8,12},{10,14},{1,5},{3,7},{5,9},{7,11},{... | collective-permute-start | bytes 1572872 | tf_op jit(solution)/shard_map/ppermute | solution.py:17
  151.7 1.5 collective-permute-start.9
  154.9 2.3 %collective-permute-start.17 = (bf16[2,34,1024]{2,1,0:T(8,128)(2,1)S(1)}, bf16[2,34,1024]{2,1,0:T(8,128)(2,1)S(1)}, u32[]{:S(2)}, u32[]{:S(2)}) collective-permute-start(bf16[2,34,1024]{2,1,0:T(8,128)(2,1)S(1)} %maximum_bitcast_fusion.1), channel_id=1, source_target_pairs={{0,4},{2,6},{4,0},{6,2},{8,12},{10,14},{12,8},{14,10},{1,5},{3,7},... | collective-permute-start | bytes 417800 | tf_op jit(solution)/shard_map/ppermute | solution.py:64
  157.2 13.4 %collective-permute-done.17 = bf16[2,34,1024]{2,1,0:T(8,128)(2,1)S(1)} collective-permute-done((bf16[2,34,1024]{2,1,0:T(8,128)(2,1)S(1)}, bf16[2,34,1024]{2,1,0:T(8,128)(2,1)S(1)}, u32[]{:S(2)}, u32[]{:S(2)}) %collective-permute-start.17) | collective-permute-done | bytes 139296 | tf_op jit(solution)/shard_map/ppermute | solution.py:64
  171.0 1.5 collective-permute-start.18
  173.9 1.5 convert_element_type.433
  176.6 2.5 %collective-permute-start.11 = (bf16[2,128,512]{2,1,0:T(8,128)(2,1)}, bf16[2,128,512]{2,1,0:T(8,128)(2,1)}, u32[]{:S(2)}, u32[]{:S(2)}) collective-permute-start(bf16[2,128,512]{2,1,0:T(8,128)(2,1)} %get-tuple-element.73), channel_id=1, source_target_pairs={{2,0},{4,2},{6,4},{8,6},{10,8},{12,10},{14,12},{3,1},{5,3},{7,5},{... | collective-permute-start | bytes 786440 | tf_op jit(solution)/shard_map/ppermute | solution.py:17
  179.1 4.2 %collective-permute-start.10 = (bf16[2,128,512]{2,1,0:T(8,128)(2,1)}, bf16[2,128,512]{2,1,0:T(8,128)(2,1)}, u32[]{:S(2)}, u32[]{:S(2)}) collective-permute-start(bf16[2,128,512]{2,1,0:T(8,128)(2,1)} %get-tuple-element.72), channel_id=1, source_target_pairs={{0,2},{2,4},{4,6},{6,8},{8,10},{10,12},{12,14},{1,3},{3,5},{5,7},{... | collective-permute-start | bytes 786440 | tf_op jit(solution)/shard_map/ppermute | solution.py:17
  185.3 1.9 broadcast_in_dim_reshape.3
  187.4 2.9 %fusion.6 = bf16[8,64,128]{2,1,0:T(8,128)(2,1)} fusion(bf16[896,8,64]{0,2,1:T(8,128)(2,1)} %copy-done.5, bf16[8,128,896]{1,2,0:T(8,128)(2,1)} %multiply_convert_fusion), kind=kOutput, calls=%fused_computation.114 | convolution fusion | flops 117571584 | bytes 2883584 | tf_op jit(solution)/shard_map/hqk,khd->qhd/dot_general | solution.py:194
  190.3 1.7 copy.165
  192.0 1.6 fusion.102
  195.7 1.5 copy.163
  (113 shorter events, 35.6 us)
Async XLA Ops:
  0.6 53.0 %copy-start = (bf16[512,1024]{1,0:T(8,128)(2,1)S(1)}, bf16[512,1024]{1,0:T(8,128)(2,1)}, u32[]{:S(2)}) copy-start(bf16[512,1024]{1,0:T(8,128)(2,1)} %param.11) | copy-start | bytes 3145732
  0.6 23.4 %copy-start.13 = (bf16[1,128,512]{2,1,0:T(8,128)(2,1)S(1)}, bf16[1,128,512]{2,1,0:T(8,128)(2,1)}, u32[]{:S(2)}) copy-start(bf16[1,128,512]{2,1,0:T(8,128)(2,1)} %param.7) | copy-start | bytes 393220
  0.7 24.2 %copy-start.14 = (f32[31,1024]{1,0:T(8,128)S(1)}, f32[31,1024]{1,0:T(8,128)}, u32[]{:S(2)}) copy-start(f32[31,1024]{1,0:T(8,128)} %param.12) | copy-start | bytes 380932
  2.6 10.9 %collective-permute-start.2 = (bf16[2,128,512]{2,1,0:T(8,128)(2,1)S(1)}, bf16[2,128,512]{2,1,0:T(8,128)(2,1)S(1)}, u32[]{:S(2)}, u32[]{:S(2)}) collective-permute-start(bf16[2,128,512]{2,1,0:T(8,128)(2,1)S(1)} %constant_dynamic-update-slice_fusion), channel_id=1, source_target_pairs={{2,0},{4,2},{6,4},{8,6},{10,8},{12,10},{14,12},{3,1},{5,3},{7,5},{... | collective-permute-start | bytes 786440 | tf_op jit(solution)/shard_map/ppermute | solution.py:17
  4.5 14.5 %collective-permute-start = (bf16[2,128,512]{2,1,0:T(8,128)(2,1)S(1)}, bf16[2,128,512]{2,1,0:T(8,128)(2,1)S(1)}, u32[]{:S(2)}, u32[]{:S(2)}) collective-permute-start(bf16[2,128,512]{2,1,0:T(8,128)(2,1)S(1)} %constant_dynamic-update-slice_fusion), channel_id=1, source_target_pairs={{0,2},{2,4},{4,6},{6,8},{8,10},{10,12},{12,14},{1,3},{3,5},{5,7},{... | collective-permute-start | bytes 786440 | tf_op jit(solution)/shard_map/ppermute | solution.py:17
  19.2 14.8 %collective-permute-start.1 = (bf16[2,2,128,512]{3,2,1,0:T(8,128)(2,1)S(1)}, bf16[2,2,128,512]{3,2,1,0:T(8,128)(2,1)}, u32[]{:S(2)}, u32[]{:S(2)}) collective-permute-start(bf16[2,2,128,512]{3,2,1,0:T(8,128)(2,1)S(1)} %get-tuple-element.93), channel_id=1, source_target_pairs={{0,4},{2,6},{4,8},{6,10},{8,12},{10,14},{1,5},{3,7},{5,9},{7,11},{... | collective-permute-start | bytes 1572872 | tf_op jit(solution)/shard_map/ppermute | solution.py:17
  24.2 19.7 %copy-start.9 = (bf16[1,128,512]{1,2,0:T(8,128)(2,1)}, bf16[1,128,512]{1,2,0:T(8,128)(2,1)S(1)}, u32[]{:S(2)}) copy-start(bf16[1,128,512]{1,2,0:T(8,128)(2,1)S(1)} %copy.146) | copy-start | bytes 393220
  25.5 15.4 %collective-permute-start.3 = (bf16[2,2,128,512]{3,2,1,0:T(8,128)(2,1)S(1)}, bf16[2,2,128,512]{3,2,1,0:T(8,128)(2,1)S(1)}, u32[]{:S(2)}, u32[]{:S(2)}) collective-permute-start(bf16[2,2,128,512]{3,2,1,0:T(8,128)(2,1)S(1)} %get-tuple-element.92), channel_id=1, source_target_pairs={{4,0},{6,2},{8,4},{10,6},{12,8},{14,10},{5,1},{7,3},{9,5},{11,7},{... | collective-permute-start | bytes 1572872 | tf_op jit(solution)/shard_map/ppermute | solution.py:17
  43.9 1.1 copy-start.5
  51.9 1.7 copy-start.15
  54.0 8.6 %collective-permute-start.5 = (bf16[15,1024]{1,0:T(8,128)(2,1)S(1)}, bf16[15,1024]{1,0:T(8,128)(2,1)S(1)}, u32[]{:S(2)}, u32[]{:S(2)}) collective-permute-start(bf16[15,1024]{1,0:T(8,128)(2,1)S(1)} %get-tuple-element.91), channel_id=1, source_target_pairs={{2,0},{4,2},{6,4},{8,6},{10,8},{12,10},{14,12},{3,1},{5,3},{7,5},{... | collective-permute-start | bytes 92168 | tf_op jit(solution)/shard_map/ppermute | solution.py:30
  55.9 6.7 %collective-permute-start.4 = (bf16[15,1024]{1,0:T(8,128)(2,1)S(1)}, bf16[15,1024]{1,0:T(8,128)(2,1)S(1)}, u32[]{:S(2)}, u32[]{:S(2)}) collective-permute-start(bf16[15,1024]{1,0:T(8,128)(2,1)S(1)} %get-tuple-element.90), channel_id=1, source_target_pairs={{0,2},{2,4},{4,6},{6,8},{8,10},{10,12},{12,14},{1,3},{3,5},{5,7},{... | collective-permute-start | bytes 92168 | tf_op jit(solution)/shard_map/ppermute | solution.py:28
  62.6 0.6 copy-start.12
  62.6 0.6 copy-start.10
  63.2 18.7 %copy-start.11 = (bf16[15,1024]{1,0:T(8,128)(2,1)S(1)}, bf16[15,1024]{1,0:T(8,128)(2,1)}, u32[]{:S(2)}) copy-start(bf16[15,1024]{1,0:T(8,128)(2,1)} %copy-done.10) | copy-start | bytes 92164
  70.7 17.1 %collective-permute-start.7 = (bf16[15,1024]{1,0:T(8,128)(2,1)}, bf16[15,1024]{1,0:T(8,128)(2,1)}, u32[]{:S(2)}, u32[]{:S(2)}) collective-permute-start(bf16[15,1024]{1,0:T(8,128)(2,1)} %get-tuple-element.89), channel_id=1, source_target_pairs={{0,2},{2,4},{4,6},{6,8},{8,10},{10,12},{12,14},{1,3},{3,5},{5,7},{... | collective-permute-start | bytes 92168 | tf_op jit(solution)/shard_map/ppermute | solution.py:28
  75.5 12.3 %collective-permute-start.6 = (bf16[15,1024]{1,0:T(8,128)(2,1)}, bf16[15,1024]{1,0:T(8,128)(2,1)}, u32[]{:S(2)}, u32[]{:S(2)}) collective-permute-start(bf16[15,1024]{1,0:T(8,128)(2,1)} %get-tuple-element.88), channel_id=1, source_target_pairs={{2,0},{4,2},{6,4},{8,6},{10,8},{12,10},{14,12},{3,1},{5,3},{7,5},{... | collective-permute-start | bytes 92168 | tf_op jit(solution)/shard_map/ppermute | solution.py:30
  93.2 1.4 copy-start.2
  95.4 4.2 %collective-permute-start.12 = (bf16[1,8,34,1024]{3,1,2,0:T(8,128)(2,1)}, bf16[1,8,34,1024]{3,1,2,0:T(8,128)(2,1)}, u32[]{:S(2)}, u32[]{:S(2)}) collective-permute-start(bf16[1,8,34,1024]{3,1,2,0:T(8,128)(2,1)} %fusion.8), channel_id=1, source_target_pairs={{0,1},{1,0},{2,3},{3,2},{4,5},{5,4},{6,7},{7,6},{8,9},{9,8},{10,11... | collective-permute-start | bytes 1671176 | tf_op jit(solution)/shard_map/ppermute | solution.py:64
  96.1 3.5 %copy-start.3 = (f32[2,8,32,1024]{3,1,2,0:T(8,128)S(1)}, f32[2,8,32,1024]{3,1,2,0:T(8,128)}, u32[]{:S(2)}) copy-start(f32[2,8,32,1024]{3,1,2,0:T(8,128)} %copy-done.2) | copy-start | bytes 6291460
  106.7 2.2 %copy-start.6 = (f32[4,2,34,1024]{3,1,0,2:T(2,128)S(1)}, f32[4,2,34,1024]{3,1,0,2:T(2,128)}, u32[]{:S(2)}) copy-start(f32[4,2,34,1024]{3,1,0,2:T(2,128)} %reshape_squeeze.15) | copy-start | bytes 3342340
  106.7 9.1 %collective-permute-start.13 = (bf16[4,34,1024]{2,0,1:T(4,128)(2,1)S(1)}, bf16[4,34,1024]{2,0,1:T(4,128)(2,1)S(1)}, u32[]{:S(2)}, u32[]{:S(2)}) collective-permute-start(bf16[4,34,1024]{2,0,1:T(4,128)(2,1)S(1)} %bitcast.204), channel_id=1, source_target_pairs={{0,2},{2,0},{4,6},{6,4},{8,10},{10,8},{12,14},{14,12},{1,3},{3,1},... | collective-permute-start | bytes 835592 | tf_op jit(solution)/shard_map/ppermute | solution.py:64
  109.4 11.7 %copy-start.4 = (bf16[8,128,896]{1,2,0:T(8,128)(2,1)S(1)}, bf16[8,128,896]{1,2,0:T(8,128)(2,1)}, u32[]{:S(2)}) copy-start(bf16[8,128,896]{1,2,0:T(8,128)(2,1)} %multiply_convert_fusion) | copy-start | bytes 5505028
  119.4 15.2 %collective-permute-start.14 = (bf16[2,34,1024]{2,0,1:T(2,128)(2,1)}, bf16[2,34,1024]{2,0,1:T(2,128)(2,1)}, u32[]{:S(2)}, u32[]{:S(2)}) collective-permute-start(bf16[2,34,1024]{2,0,1:T(2,128)(2,1)} %bitcast.190), channel_id=1, source_target_pairs={{0,4},{2,6},{4,0},{6,2},{8,12},{10,14},{12,8},{14,10},{1,5},{3,7},... | collective-permute-start | bytes 417800 | tf_op jit(solution)/shard_map/ppermute | solution.py:64
  135.8 8.9 %collective-permute-start.15 = (bf16[1,34,1024]{2,0,1:T(2,128)(2,1)S(1)}, bf16[1,34,1024]{2,0,1:T(2,128)(2,1)S(1)}, u32[]{:S(2)}, u32[]{:S(2)}) collective-permute-start(bf16[1,34,1024]{2,0,1:T(2,128)(2,1)S(1)} %dynamic-slice_convert_fusion.1), channel_id=1, source_target_pairs={{0,8},{2,10},{4,12},{6,14},{8,0},{10,2},{12,4},{14,6},{1,9},{3,11}... | collective-permute-start | bytes 208904 | tf_op jit(solution)/shard_map/ppermute | solution.py:64
  144.9 8.7 %collective-permute-start.16 = (bf16[1,34,1024]{2,0,1:T(2,128)(2,1)S(1)}, bf16[1,34,1024]{2,0,1:T(2,128)(2,1)}, u32[]{:S(2)}, u32[]{:S(2)}) collective-permute-start(bf16[1,34,1024]{2,0,1:T(2,128)(2,1)S(1)} %add_convert_fusion), channel_id=1, source_target_pairs={{0,8},{2,10},{4,12},{6,14},{8,0},{10,2},{12,4},{14,6},{1,9},{3,11}... | collective-permute-start | bytes 208904 | tf_op jit(solution)/shard_map/ppermute | solution.py:64
  145.9 26.7 %collective-permute-start.8 = (bf16[2,2,128,512]{3,2,1,0:T(8,128)(2,1)}, bf16[2,2,128,512]{3,2,1,0:T(8,128)(2,1)}, u32[]{:S(2)}, u32[]{:S(2)}) collective-permute-start(bf16[2,2,128,512]{3,2,1,0:T(8,128)(2,1)} %get-tuple-element.74), channel_id=1, source_target_pairs={{0,4},{2,6},{4,8},{6,10},{8,12},{10,14},{1,5},{3,7},{5,9},{7,11},{... | collective-permute-start | bytes 1572872 | tf_op jit(solution)/shard_map/ppermute | solution.py:17
  151.7 22.2 %collective-permute-start.9 = (bf16[2,2,128,512]{3,2,1,0:T(8,128)(2,1)}, bf16[2,2,128,512]{3,2,1,0:T(8,128)(2,1)}, u32[]{:S(2)}, u32[]{:S(2)}) collective-permute-start(bf16[2,2,128,512]{3,2,1,0:T(8,128)(2,1)} %rev.3), channel_id=1, source_target_pairs={{4,0},{6,2},{8,4},{10,6},{12,8},{14,10},{5,1},{7,3},{9,5},{11,7},{... | collective-permute-start | bytes 1572872 | tf_op jit(solution)/shard_map/ppermute | solution.py:17
  154.9 15.6 %collective-permute-start.17 = (bf16[2,34,1024]{2,1,0:T(8,128)(2,1)S(1)}, bf16[2,34,1024]{2,1,0:T(8,128)(2,1)S(1)}, u32[]{:S(2)}, u32[]{:S(2)}) collective-permute-start(bf16[2,34,1024]{2,1,0:T(8,128)(2,1)S(1)} %maximum_bitcast_fusion.1), channel_id=1, source_target_pairs={{0,4},{2,6},{4,0},{6,2},{8,12},{10,14},{12,8},{14,10},{1,5},{3,7},... | collective-permute-start | bytes 417800 | tf_op jit(solution)/shard_map/ppermute | solution.py:64
  171.0 12.3 %collective-permute-start.18 = (bf16[4,34,1024]{2,0,1:T(4,128)(2,1)S(1)}, bf16[4,34,1024]{2,0,1:T(4,128)(2,1)S(1)}, u32[]{:S(2)}, u32[]{:S(2)}) collective-permute-start(bf16[4,34,1024]{2,0,1:T(4,128)(2,1)S(1)} %reshape.102), channel_id=1, source_target_pairs={{0,2},{2,0},{4,6},{6,4},{8,10},{10,8},{12,14},{14,12},{1,3},{3,1},... | collective-permute-start | bytes 835592 | tf_op jit(solution)/shard_map/ppermute | solution.py:64
  172.5 2.9 %copy-start.1 = (f32[7,1,128,512]{3,2,1,0:T(8,128)S(1)}, f32[7,1,128,512]{3,2,1,0:T(8,128)}, u32[]{:S(2)}) copy-start(f32[7,1,128,512]{3,2,1,0:T(8,128)} %copy.154) | copy-start | bytes 5505028
  173.8 2.7 %copy-start.7 = (f32[2,2,128,512]{3,2,1,0:T(8,128)}, f32[2,2,128,512]{3,2,1,0:T(8,128)S(1)}, u32[]{:S(2)}) copy-start(f32[2,2,128,512]{3,2,1,0:T(8,128)S(1)} %convert_element_type.432) | copy-start | bytes 3145732
  175.4 1.1 copy-start.8
  176.6 15.4 %collective-permute-start.11 = (bf16[2,128,512]{2,1,0:T(8,128)(2,1)}, bf16[2,128,512]{2,1,0:T(8,128)(2,1)}, u32[]{:S(2)}, u32[]{:S(2)}) collective-permute-start(bf16[2,128,512]{2,1,0:T(8,128)(2,1)} %get-tuple-element.73), channel_id=1, source_target_pairs={{2,0},{4,2},{6,4},{8,6},{10,8},{12,10},{14,12},{3,1},{5,3},{7,5},{... | collective-permute-start | bytes 786440 | tf_op jit(solution)/shard_map/ppermute | solution.py:17
  179.1 12.9 %collective-permute-start.10 = (bf16[2,128,512]{2,1,0:T(8,128)(2,1)}, bf16[2,128,512]{2,1,0:T(8,128)(2,1)}, u32[]{:S(2)}, u32[]{:S(2)}) collective-permute-start(bf16[2,128,512]{2,1,0:T(8,128)(2,1)} %get-tuple-element.72), channel_id=1, source_target_pairs={{0,2},{2,4},{4,6},{6,8},{8,10},{10,12},{12,14},{1,3},{3,5},{5,7},{... | collective-permute-start | bytes 786440 | tf_op jit(solution)/shard_map/ppermute | solution.py:17
  187.3 7.1 %collective-permute-start.19 = (bf16[1,8,34,1024]{3,1,2,0:T(8,128)(2,1)S(1)}, bf16[1,8,34,1024]{3,1,2,0:T(8,128)(2,1)}, u32[]{:S(2)}, u32[]{:S(2)}) collective-permute-start(bf16[1,8,34,1024]{3,1,2,0:T(8,128)(2,1)S(1)} %broadcast_in_dim_reshape.3), channel_id=1, source_target_pairs={{0,1},{1,0},{2,3},{3,2},{4,5},{5,4},{6,7},{7,6},{8,9},{9,8},{10,11... | collective-permute-start | bytes 1671176 | tf_op jit(solution)/shard_map/ppermute | solution.py:64

commit v7 on v6

--- a/solution.py
+++ b/solution.py
@@ -44,14 +44,13 @@
     )
 
 
-def give_back(partials, shifter):
-    narrow = partials.astype(jnp.bfloat16)
+def give_back(near, narrow, shifter):
     from_below = shifter(narrow[REACH + 2 :], 2).astype(jnp.float32)
     from_above = shifter(narrow[REACH - 2 :: -1], -2).astype(jnp.float32)
-    upward = (partials[REACH + 1] + from_below[1]).astype(jnp.bfloat16)
-    downward = (partials[REACH - 1] + from_above[1]).astype(jnp.bfloat16)
+    upward = (near[2] + from_below[1]).astype(jnp.bfloat16)
+    downward = (near[0] + from_above[1]).astype(jnp.bfloat16)
     return (
-        partials[REACH]
+        near[1]
         + from_below[0]
         + from_above[0]
         + shifter(upward, 1).astype(jnp.float32)
@@ -66,28 +65,29 @@
 
 def halving(acc, axis):
     here = lax.axis_index(axis)
-    bit = 1
-    while acc.shape[0] > 1:
-        pairs = acc.reshape(acc.shape[0] // 2, 2, *acc.shape[1:])
+    bit = lax.axis_size(axis) // 2
+    while bit >= 1:
+        half = acc.shape[0] // 2
         mine = (here // bit) % 2
-        keep = lax.dynamic_index_in_dim(pairs, mine, 1, keepdims=False)
-        send = lax.dynamic_index_in_dim(pairs, 1 - mine, 1, keepdims=False)
+        keep = lax.dynamic_slice_in_dim(acc, mine * half, half, 0)
+        send = lax.dynamic_slice_in_dim(acc, (1 - mine) * half, half, 0)
         acc = keep + exchange(send.astype(jnp.bfloat16), axis, bit).astype(jnp.float32)
-        bit *= 2
+        bit //= 2
     return acc[0]
 
 
 def doubling(acc, axis):
     here = lax.axis_index(axis)
-    bit = lax.axis_size(axis) // 2
+    count = lax.axis_size(axis)
     acc = acc[None]
-    while bit >= 1:
+    bit = 1
+    while bit < count:
         theirs = exchange(acc, axis, bit)
         first = (here // bit) % 2 == 0
-        low = jnp.where(first, acc, theirs)
-        high = jnp.where(first, theirs, acc)
-        acc = jnp.stack([low, high], axis=1).reshape(-1, *acc.shape[1:])
-        bit //= 2
+        acc = jnp.concatenate(
+            [jnp.where(first, acc, theirs), jnp.where(first, theirs, acc)], axis=0
+        )
+        bit *= 2
     return acc
 
 
@@ -202,12 +202,11 @@
     grad_value_all = jnp.einsum(
         "hqk,qhd->khd", weights, grad_heads, preferred_element_type=jnp.float32
     )
-    placed = jnp.stack(
-        [
-            grad_key_all.reshape(span_blocks, tokens, width_heads),
-            grad_value_all.reshape(span_blocks, tokens, width_heads),
-        ],
-        axis=1,
+    key_blocks = grad_key_all.reshape(span_blocks, tokens, width_heads)
+    value_blocks = grad_value_all.reshape(span_blocks, tokens, width_heads)
+    narrow = jnp.stack([key_blocks, value_blocks], axis=1).astype(jnp.bfloat16)
+    near = jnp.stack(
+        [key_blocks[REACH - 1 : REACH + 2], value_blocks[REACH - 1 : REACH + 2]], axis=1
     )
 
     def grad_shift(piece_rows, offset_by):
@@ -218,7 +217,7 @@
     kernel_sum = (
         gathered[:, :, proj_rows:].astype(jnp.float32).reshape(members * kernel_rows, channels)[:KW]
     )
-    own_grads = give_back(placed, grad_shift)
+    own_grads = give_back(near, narrow, grad_shift)
     grad_key = own_grads[0].astype(jnp.bfloat16)
     grad_value = own_grads[1].astype(jnp.bfloat16)
     return (

time: 201 us -> 189 us (0.940)
  local copies, waits for them, and re-layouts: 49.5 us -> 40.7 us
  waiting for transfers between devices: 49.5 us -> 57.6 us
  matrix products: 15.4 us -> 8.9 us
  starting transfers between devices: 45.2 us -> 40.9 us
    another operation x8, local copies, waits for them, and re-layouts: 16.6 us -> 10.4 us  [the longest x4 7.15 us: on_device(): narrow = jnp.stack([key_blocks, value_blocks], axis=1).astype(jnp.bfloat16)]
    ppermute x8, waiting for transfers between devices: 26.8 us -> 30.7 us  [exchange(): return lax.ppermute(block, axis, [(i, i ^ bit) for i in range(count)])]
    ppermute x2, starting transfers between devices: 9.6 us -> 5.82 us  [padded(): lax.ppermute(tail, axis, [(i, (i + 1) % count) for i in range(ends)])]
    ppermute x8, starting transfers between devices: 6.3 us -> 3.15 us  [exchange(): return lax.ppermute(block, axis, [(i, i ^ bit) for i in range(count)])]
    ppermute x8, waiting for transfers between devices: 22.7 us -> 25.8 us  [passed_along(): return lax.ppermute(block, axis, route)]
    ppermute x2, starting transfers between devices: 3.84 us -> 6.93 us  [padded(): lax.ppermute(head, axis, [((i + 1) % count, i) for i in range(ends)])]
    dynamic_slice x3 -> x0, local copies, waits for them, and re-layouts: 2.71 us -> none  [the longest x1 1.84 us: halving(): send = lax.dynamic_index_in_dim(pairs, 1 - mine, 1, keepdims=False)]
    dot_general x1, matrix products: 3.47 us -> 0.92 us  [on_device(): jnp.einsum('qhd,khd->hqk', grad_heads, value_all, preferred_element_type=...]
  transfers between devices with their start and end apart: 20 -> 20, of which waited for: 8 -> 10; matrix products, arithmetic and copies ran while one was open for 28% -> 26% of each run, Pallas kernels for 0% -> 0%
where the time goes in v7:
time: 189 us; the launch traced here: 187 us
  waiting for transfers between devices  57.6 us (30%)
  starting transfers between devices  40.9 us (22%)
  local copies, waits for them, and re-layouts  40.7 us (22%)
  other arithmetic  36.7 us (19%)
  matrix products  8.9 us (5%)
  between operations  2.04 us (1%)
    ppermute x8, waiting for transfers between devices, exchange(): return lax.ppermute(block, axis, [(i, i ^ bit) for i in range(count)])  30.7 us
    ppermute x8, waiting for transfers between devices, passed_along(): return lax.ppermute(block, axis, route)  25.8 us
    ppermute x8, starting transfers between devices, passed_along(): return lax.ppermute(block, axis, route)  25 us
    reduce_sum x4, other arithmetic, on_device(): jnp.sum(padded_m[tap_index:tap_index + tokens].astype(jnp.float32) * grad...  12.4 us
    another operation x4, local copies, waits for them, and re-layouts, on_device(): narrow = jnp.stack([key_blocks, value_blocks], axis=1).astype(jnp.bfloat16)  7.15 us
    ppermute x2, starting transfers between devices, padded(): lax.ppermute(head, axis, [((i + 1) % count, i) for i in range(ends)])  6.93 us
    unnamed x61, local copies, waits for them, and re-layouts  6.51 us
    ppermute x2, starting transfers between devices, padded(): lax.ppermute(tail, axis, [(i, (i + 1) % count) for i in range(ends)])  5.82 us
  transfers between devices with their start and end apart: 20, of which 10 were waited for; matrix products, arithmetic and copies ran while one was open for 26% of the time, Pallas kernels for 0%

profile of v7, /device:TPU:2, one launch (start us, length us, event | category | flops | bytes accessed | tf_op | source)
XLA Modules:
  0.0 186.8 jit_solution(11927215956367488833)
XLA Ops:
  2.6 1.9 %collective-permute-start.2 = (bf16[2,128,512]{2,1,0:T(8,128)(2,1)S(1)}, bf16[2,128,512]{2,1,0:T(8,128)(2,1)S(1)}, u32[]{:S(2)}, u32[]{:S(2)}) collective-permute-start(bf16[2,128,512]{2,1,0:T(8,128)(2,1)S(1)} %constant_dynamic-update-slice_fusion), channel_id=1, source_target_pairs={{2,0},{4,2},{6,4},{8,6},{10,8},{12,10},{14,12},{3,1},{5,3},{7,5},{... | collective-permute-start | bytes 786440 | tf_op jit(solution)/shard_map/ppermute | solution.py:17
  4.5 4.8 %collective-permute-start = (bf16[2,128,512]{2,1,0:T(8,128)(2,1)S(1)}, bf16[2,128,512]{2,1,0:T(8,128)(2,1)S(1)}, u32[]{:S(2)}, u32[]{:S(2)}) collective-permute-start(bf16[2,128,512]{2,1,0:T(8,128)(2,1)S(1)} %constant_dynamic-update-slice_fusion), channel_id=1, source_target_pairs={{0,2},{2,4},{4,6},{6,8},{8,10},{10,12},{12,14},{1,3},{3,5},{5,7},{... | collective-permute-start | bytes 786440 | tf_op jit(solution)/shard_map/ppermute | solution.py:17
  9.4 4.2 %collective-permute-done.2 = bf16[2,128,512]{2,1,0:T(8,128)(2,1)S(1)} collective-permute-done((bf16[2,128,512]{2,1,0:T(8,128)(2,1)S(1)}, bf16[2,128,512]{2,1,0:T(8,128)(2,1)S(1)}, u32[]{:S(2)}, u32[]{:S(2)}) %collective-permute-start.2) | collective-permute-done | bytes 262176 | tf_op jit(solution)/shard_map/ppermute | solution.py:17
  13.5 5.5 %collective-permute-done = bf16[2,128,512]{2,1,0:T(8,128)(2,1)S(1)} collective-permute-done((bf16[2,128,512]{2,1,0:T(8,128)(2,1)S(1)}, bf16[2,128,512]{2,1,0:T(8,128)(2,1)S(1)}, u32[]{:S(2)}, u32[]{:S(2)}) %collective-permute-start) | collective-permute-done | bytes 262176 | tf_op jit(solution)/shard_map/ppermute | solution.py:17
  20.0 4.3 %collective-permute-start.1 = (bf16[2,2,128,512]{3,2,1,0:T(8,128)(2,1)S(1)}, bf16[2,2,128,512]{3,2,1,0:T(8,128)(2,1)}, u32[]{:S(2)}, u32[]{:S(2)}) collective-permute-start(bf16[2,2,128,512]{3,2,1,0:T(8,128)(2,1)S(1)} %get-tuple-element.88), channel_id=1, source_target_pairs={{0,4},{2,6},{4,8},{6,10},{8,12},{10,14},{1,5},{3,7},{5,9},{7,11},{... | collective-permute-start | bytes 1572872 | tf_op jit(solution)/shard_map/ppermute | solution.py:17
  26.8 1.3 collective-permute-start.3
  28.1 6.6 %collective-permute-done.1 = bf16[2,2,128,512]{3,2,1,0:T(8,128)(2,1)} collective-permute-done((bf16[2,2,128,512]{3,2,1,0:T(8,128)(2,1)S(1)}, bf16[2,2,128,512]{3,2,1,0:T(8,128)(2,1)}, u32[]{:S(2)}, u32[]{:S(2)}) %collective-permute-start.1) | collective-permute-done | bytes 524320 | tf_op jit(solution)/shard_map/ppermute | solution.py:17
  36.9 5.6 %collective-permute-done.3 = bf16[2,2,128,512]{3,2,1,0:T(8,128)(2,1)S(1)} collective-permute-done((bf16[2,2,128,512]{3,2,1,0:T(8,128)(2,1)}, bf16[2,2,128,512]{3,2,1,0:T(8,128)(2,1)S(1)}, u32[]{:S(2)}, u32[]{:S(2)}) %collective-permute-start.3) | collective-permute-done | bytes 524320 | tf_op jit(solution)/shard_map/ppermute | solution.py:17
  42.5 1.4 fusion.167
  43.9 1.7 copy.106
  45.6 2.0 %reshape_squeeze.11 = bf16[896,8,64]{0,2,1:T(8,128)(2,1)} reshape(bf16[7,1,128,512]{2,0,3,1:T(8,128)(2,1)S(1)} %copy.106) | data formatting | bytes 1835008 | tf_op jit(solution)/shard_map/reshape;squeeze | solution.py:117
  47.6 2.4 %copy.104 = bf16[7,1,128,512]{2,0,3,1:T(8,128)(2,1)} copy(bf16[7,1,128,512]{3,2,1,0:T(8,128)(2,1)} %get-tuple-element.70) | data formatting | bytes 1835008 | tf_op jit(solution)/shard_map/slice | solution.py:116
  50.0 2.2 %reshape_squeeze.9 = bf16[896,8,64]{0,2,1:T(8,128)(2,1)S(1)} reshape(bf16[7,1,128,512]{2,0,3,1:T(8,128)(2,1)} %copy.104) | data formatting | bytes 1835008 | tf_op jit(solution)/shard_map/reshape;squeeze | solution.py:116
  56.2 1.9 %collective-permute-start.4 = (bf16[15,1024]{1,0:T(8,128)(2,1)S(1)}, bf16[15,1024]{1,0:T(8,128)(2,1)S(1)}, u32[]{:S(2)}, u32[]{:S(2)}) collective-permute-start(bf16[15,1024]{1,0:T(8,128)(2,1)S(1)} %get-tuple-element.85), channel_id=1, source_target_pairs={{0,2},{2,4},{4,6},{6,8},{8,10},{10,12},{12,14},{1,3},{3,5},{5,7},{... | collective-permute-start | bytes 92168 | tf_op jit(solution)/shard_map/ppermute | solution.py:28
  58.2 3.9 %collective-permute-start.5 = (bf16[15,1024]{1,0:T(8,128)(2,1)S(1)}, bf16[15,1024]{1,0:T(8,128)(2,1)S(1)}, u32[]{:S(2)}, u32[]{:S(2)}) collective-permute-start(bf16[15,1024]{1,0:T(8,128)(2,1)S(1)} %get-tuple-element.86), channel_id=1, source_target_pairs={{2,0},{4,2},{6,4},{8,6},{10,8},{12,10},{14,12},{3,1},{5,3},{7,5},{... | collective-permute-start | bytes 92168 | tf_op jit(solution)/shard_map/ppermute | solution.py:30
  62.1 1.7 fusion.172
  65.5 6.8 %fusion.99 = (f32[1024]{0:T(1024)}, f32[1024]{0:T(1024)}, f32[1024]{0:T(1024)}, f32[1024]{0:T(1024)}, f32[1024]{0:T(1024)}, /*index=5*/f32[1024]{0:T(1024)}, f32...) fusion(bf16[15,1024]{1,0:T(8,128)(2,1)} %copy-done.22, bf16[128,1024]{1,0:T(8,128)(2,1)S(1)} %fusion.4, ...), kind=kLoop, calls=%fused_computation.246 | loop fusion | flops 31841280 | bytes 1011712 | tf_op jit(solution)/shard_map/reduce_sum | solution.py:154
  72.9 3.0 %collective-permute-start.6 = (bf16[15,1024]{1,0:T(8,128)(2,1)}, bf16[15,1024]{1,0:T(8,128)(2,1)}, u32[]{:S(2)}, u32[]{:S(2)}) collective-permute-start(bf16[15,1024]{1,0:T(8,128)(2,1)} %get-tuple-element.83), channel_id=1, source_target_pairs={{2,0},{4,2},{6,4},{8,6},{10,8},{12,10},{14,12},{3,1},{5,3},{7,5},{... | collective-permute-start | bytes 92168 | tf_op jit(solution)/shard_map/ppermute | solution.py:30
  76.0 3.9 %collective-permute-start.7 = (bf16[15,1024]{1,0:T(8,128)(2,1)}, bf16[15,1024]{1,0:T(8,128)(2,1)}, u32[]{:S(2)}, u32[]{:S(2)}) collective-permute-start(bf16[15,1024]{1,0:T(8,128)(2,1)} %get-tuple-element.84), channel_id=1, source_target_pairs={{0,2},{2,4},{4,6},{6,8},{8,10},{10,12},{12,14},{1,3},{3,5},{5,7},{... | collective-permute-start | bytes 92168 | tf_op jit(solution)/shard_map/ppermute | solution.py:28
  79.9 2.2 %fusion.98 = (f32[1024]{0:T(1024)}, f32[1024]{0:T(1024)}, f32[1024]{0:T(1024)}, f32[1024]{0:T(1024)}, f32[1024]{0:T(1024)}, /*index=5*/f32[1024]{0:T(1024)}, f32[1024]{0:T(1024)}) fusion(bf16[128,1024]{1,0:T(8,128)(2,1)S(1)} %get-tuple-element.66, bf16[15,1024]{1,0:T(8,128)(2,1)} %copy-done.22, bf16[128,1024]{1,0:T(8,128)(2,1)S(1)} %fusion.4), kind=kLoop, calls=%fused_computation.245 | loop fusion | flops 5235712 | bytes 583680 | tf_op jit(solution)/shard_map/reduce_sum | solution.py:154
  82.0 2.4 %fusion.83 = (f32[1024]{0:T(1024)}, f32[1024]{0:T(1024)}, f32[1024]{0:T(1024)}, f32[1024]{0:T(1024)}, f32[1024]{0:T(1024)}, /*index=5*/f32[1024]{0:T(1024)}, f32[1024]{0:T(1024)}, f32[1024]{0:T(1024)}, f32[1024]{0:T(1024)}) fusion(bf16[128,1024]{1,0:T(8,128)(2,1)S(1)} %get-tuple-element.66, bf16[128,1024]{1,0:T(8,128)(2,1)S(1)} %fusion.4, ...), kind=kLoop, calls=%fused_computation.230 | loop fusion | flops 7199744 | bytes 591872 | tf_op jit(solution)/shard_map/reduce_sum | solution.py:154
  85.5 3.1 %stack.177 = f32[31,1024]{1,0:T(8,128)S(1)} concatenate(f32[1,1024]{1,0:T(1,128)} %bitcast.263, f32[1,1024]{1,0:T(1,128)} %bitcast.265, f32[1,1024]{1,0:T(1,128)} %bitcast.264, f32[1,1024]{1,0:T(1,128)} %bitcast.266, f32[1,1024]{1,0:T(1,128)} %bitcast.253, f32[1,1024]{1,0:T(1,128)} %bitcast.254, f32[1,1024]{1,0:T(1,128)} %bitcast.255, f32[1,1024]{1,0:T(1,128)} %bitcast.256, ...), dimensions={0} | concatenate | bytes 253952 | tf_op jit(solution)/shard_map/stack | solution.py:158
  88.8 4.8 %fusion.42 = bf16[128,1024]{1,0:T(8,128)(2,1)S(1)} fusion(bf16[128,1024]{1,0:T(8,128)(2,1)S(1)} %get-tuple-element.66, bf16[15,1024]{1,0:T(8,128)(2,1)} %collective-permute-done.7, bf16[15,1024]{1,0:T(8,128)(2,1)} %collective-permute-done.6, bf16[1,128,1024]{2,1,0:T(8,128)(2,1)} %param.10, f32[1024]{0:T(1024)} %bitcast.233, f32[1024]{0:T(1024)} %bitcast.235, ...), kind=kLoop, calls=%fused_computation.189 | loop fusion | flops 24379392 | bytes 974976 | tf_op jit(solution)/shard_map/convert_element_type | solution.py:161
  94.0 1.3 copy-done.1
  96.9 1.6 collective-permute-done.12
  98.5 1.5 fusion.9
  101.7 14.1 %collective-permute-done.13 = bf16[4,34,1024]{2,0,1:T(4,128)(2,1)S(1)} collective-permute-done((bf16[4,34,1024]{2,0,1:T(4,128)(2,1)S(1)}, bf16[4,34,1024]{2,0,1:T(4,128)(2,1)S(1)}, u32[]{:S(2)}, u32[]{:S(2)}) %collective-permute-start.13) | collective-permute-done | bytes 278560 | tf_op jit(solution)/shard_map/ppermute | solution.py:63
  116.2 2.4 %fusion.173 = (bf16[896,8,64]{0,2,1:T(8,128)(2,1)}, f32[896,8,64]{0,2,1:T(8,128)}) fusion(bf16[128,8,64]{0,2,1:T(8,128)(2,1)S(1)} %bitcast.164, bf16[8,128,896]{1,2,0:T(8,128)(2,1)S(1)} %fusion.3), kind=kOutput, calls=%fused_computation.374 | convolution fusion | flops 117899264 | bytes 4718592 | tf_op jit(solution)/shard_map/hqk,qhd->khd/dot_general | solution.py:202
  118.6 3.0 %collective-permute-done.14 = bf16[2,34,1024]{2,0,1:T(2,128)(2,1)S(1)} collective-permute-done((bf16[2,34,1024]{2,0,1:T(2,128)(2,1)S(1)}, bf16[2,34,1024]{2,0,1:T(2,128)(2,1)S(1)}, u32[]{:S(2)}, u32[]{:S(2)}) %collective-permute-start.14) | collective-permute-done | bytes 139296 | tf_op jit(solution)/shard_map/ppermute | solution.py:63
  122.7 2.4 %fusion.174 = (bf16[896,8,64]{0,2,1:T(8,128)(2,1)}, f32[896,8,64]{0,2,1:T(8,128)}) fusion(bf16[8,128,896]{1,2,0:T(8,128)(2,1)S(1)} %multiply_convert_fusion, bf16[128,8,64]{0,2,1:T(8,128)(2,1)S(1)} %bitcast.169), kind=kOutput, calls=%fused_computation.375 | convolution fusion | flops 118358016 | bytes 4718592 | tf_op jit(solution)/shard_map/hqk,qhd->khd/dot_general | solution.py:199
  125.0 2.1 %stack_reshape.8 = bf16[7,1,128,512]{2,0,3,1:T(8,128)(2,1)S(1)} reshape(bf16[896,8,64]{0,2,1:T(8,128)(2,1)} %get-tuple-element.124) | data formatting | bytes 1835008 | tf_op jit(solution)/shard_map/stack;reshape | solution.py:207
  127.2 1.5 copy.115
  128.6 2.1 %stack_reshape.9 = bf16[7,1,128,512]{2,0,3,1:T(8,128)(2,1)S(1)} reshape(bf16[896,8,64]{0,2,1:T(8,128)(2,1)} %get-tuple-element.122) | data formatting | bytes 1835008 | tf_op jit(solution)/shard_map/stack;reshape | solution.py:207
  130.8 1.4 copy.116
  132.4 1.4 collective-permute-start.16
  133.8 2.1 %pad_maximum_fusion.2 = (bf16[2,2,128,512]{3,2,1,0:T(8,128)(2,1)}, bf16[2,2,128,512]{3,2,1,0:T(8,128)(2,1)S(1)}) fusion(bf16[7,1,128,512]{3,2,1,0:T(8,128)(2,1)} %copy.116, bf16[7,1,128,512]{3,2,1,0:T(8,128)(2,1)} %copy.115), kind=kLoop, calls=%fused_computation.251 | loop fusion | flops 524288 | bytes 2883584 | tf_op jit(solution)/shard_map/slice | solution.py:48
  136.7 1.3 collective-permute-start.9
  138.0 4.8 %collective-permute-start.8 = (bf16[2,2,128,512]{3,2,1,0:T(8,128)(2,1)}, bf16[2,2,128,512]{3,2,1,0:T(8,128)(2,1)S(1)}, u32[]{:S(2)}, u32[]{:S(2)}) collective-permute-start(bf16[2,2,128,512]{3,2,1,0:T(8,128)(2,1)} %get-tuple-element.67), channel_id=1, source_target_pairs={{0,4},{2,6},{4,8},{6,10},{8,12},{10,14},{1,5},{3,7},{5,9},{7,11},{... | collective-permute-start | bytes 1572872 | tf_op jit(solution)/shard_map/ppermute | solution.py:17
  143.8 12.0 %collective-permute-done.17 = bf16[2,34,1024]{2,0,1:T(2,128)(2,1)S(1)} collective-permute-done((bf16[2,34,1024]{2,0,1:T(2,128)(2,1)S(1)}, bf16[2,34,1024]{2,0,1:T(2,128)(2,1)S(1)}, u32[]{:S(2)}, u32[]{:S(2)}) %collective-permute-start.17) | collective-permute-done | bytes 139296 | tf_op jit(solution)/shard_map/ppermute | solution.py:63
  159.1 2.1 %slice.706 = f32[384,8,64]{0,2,1:T(8,128)} slice(f32[896,8,64]{0,2,1:T(8,128)} %get-tuple-element.123), slice={[256:640], [0:8], [0:64]} | slice | bytes 1572864 | tf_op jit(solution)/shard_map/slice | solution.py:209
  161.2 1.4 stack.143
  166.2 4.6 %collective-permute-start.10 = (bf16[2,128,512]{2,1,0:T(8,128)(2,1)}, bf16[2,128,512]{2,1,0:T(8,128)(2,1)}, u32[]{:S(2)}, u32[]{:S(2)}) collective-permute-start(bf16[2,128,512]{2,1,0:T(8,128)(2,1)} %get-tuple-element.71), channel_id=1, source_target_pairs={{0,2},{2,4},{4,6},{6,8},{8,10},{10,12},{12,14},{1,3},{3,5},{5,7},{... | collective-permute-start | bytes 786440 | tf_op jit(solution)/shard_map/ppermute | solution.py:17
  170.9 2.0 %collective-permute-start.11 = (bf16[2,128,512]{2,1,0:T(8,128)(2,1)}, bf16[2,128,512]{2,1,0:T(8,128)(2,1)}, u32[]{:S(2)}, u32[]{:S(2)}) collective-permute-start(bf16[2,128,512]{2,1,0:T(8,128)(2,1)} %get-tuple-element.72), channel_id=1, source_target_pairs={{2,0},{4,2},{6,4},{8,6},{10,8},{12,10},{14,12},{3,1},{5,3},{7,5},{... | collective-permute-start | bytes 786440 | tf_op jit(solution)/shard_map/ppermute | solution.py:17
  172.9 1.4 broadcast_select_fusion.7
  176.7 3.8 %collective-permute-done.10 = bf16[2,128,512]{2,1,0:T(8,128)(2,1)} collective-permute-done((bf16[2,128,512]{2,1,0:T(8,128)(2,1)}, bf16[2,128,512]{2,1,0:T(8,128)(2,1)}, u32[]{:S(2)}, u32[]{:S(2)}) %collective-permute-start.10) | collective-permute-done | bytes 262176 | tf_op jit(solution)/shard_map/ppermute | solution.py:17
  180.5 1.6 fusion.52
  182.9 1.5 broadcast_select_fusion
  184.5 1.5 copy.119
  (128 shorter events, 32.2 us)
Async XLA Ops:
  0.6 55.1 %copy-start = (bf16[512,1024]{1,0:T(8,128)(2,1)S(1)}, bf16[512,1024]{1,0:T(8,128)(2,1)}, u32[]{:S(2)}) copy-start(bf16[512,1024]{1,0:T(8,128)(2,1)} %param.11) | copy-start | bytes 3145732
  0.6 24.2 %copy-start.23 = (bf16[1,128,512]{2,1,0:T(8,128)(2,1)S(1)}, bf16[1,128,512]{2,1,0:T(8,128)(2,1)}, u32[]{:S(2)}) copy-start(bf16[1,128,512]{2,1,0:T(8,128)(2,1)} %param.7) | copy-start | bytes 393220
  0.7 25.5 %copy-start.24 = (f32[31,1024]{1,0:T(8,128)S(1)}, f32[31,1024]{1,0:T(8,128)}, u32[]{:S(2)}) copy-start(f32[31,1024]{1,0:T(8,128)} %param.12) | copy-start | bytes 380932
  2.6 10.9 %collective-permute-start.2 = (bf16[2,128,512]{2,1,0:T(8,128)(2,1)S(1)}, bf16[2,128,512]{2,1,0:T(8,128)(2,1)S(1)}, u32[]{:S(2)}, u32[]{:S(2)}) collective-permute-start(bf16[2,128,512]{2,1,0:T(8,128)(2,1)S(1)} %constant_dynamic-update-slice_fusion), channel_id=1, source_target_pairs={{2,0},{4,2},{6,4},{8,6},{10,8},{12,10},{14,12},{3,1},{5,3},{7,5},{... | collective-permute-start | bytes 786440 | tf_op jit(solution)/shard_map/ppermute | solution.py:17
  4.5 14.5 %collective-permute-start = (bf16[2,128,512]{2,1,0:T(8,128)(2,1)S(1)}, bf16[2,128,512]{2,1,0:T(8,128)(2,1)S(1)}, u32[]{:S(2)}, u32[]{:S(2)}) collective-permute-start(bf16[2,128,512]{2,1,0:T(8,128)(2,1)S(1)} %constant_dynamic-update-slice_fusion), channel_id=1, source_target_pairs={{0,2},{2,4},{4,6},{6,8},{8,10},{10,12},{12,14},{1,3},{3,5},{5,7},{... | collective-permute-start | bytes 786440 | tf_op jit(solution)/shard_map/ppermute | solution.py:17
  19.1 9.1 %copy-start.19 = (bf16[2,128,512]{2,1,0:T(8,128)(2,1)}, bf16[2,128,512]{2,1,0:T(8,128)(2,1)S(1)}, u32[]{:S(2)}) copy-start(bf16[2,128,512]{2,1,0:T(8,128)(2,1)S(1)} %collective-permute-done) | copy-start | bytes 786436
  20.0 14.8 %collective-permute-start.1 = (bf16[2,2,128,512]{3,2,1,0:T(8,128)(2,1)S(1)}, bf16[2,2,128,512]{3,2,1,0:T(8,128)(2,1)}, u32[]{:S(2)}, u32[]{:S(2)}) collective-permute-start(bf16[2,2,128,512]{3,2,1,0:T(8,128)(2,1)S(1)} %get-tuple-element.88), channel_id=1, source_target_pairs={{0,4},{2,6},{4,8},{6,10},{8,12},{10,14},{1,5},{3,7},{5,9},{7,11},{... | collective-permute-start | bytes 1572872 | tf_op jit(solution)/shard_map/ppermute | solution.py:17
  25.0 27.2 %copy-start.15 = (bf16[1,128,512]{1,2,0:T(8,128)(2,1)}, bf16[1,128,512]{1,2,0:T(8,128)(2,1)S(1)}, u32[]{:S(2)}) copy-start(bf16[1,128,512]{1,2,0:T(8,128)(2,1)S(1)} %copy.105) | copy-start | bytes 393220
  26.8 15.7 %collective-permute-start.3 = (bf16[2,2,128,512]{3,2,1,0:T(8,128)(2,1)}, bf16[2,2,128,512]{3,2,1,0:T(8,128)(2,1)S(1)}, u32[]{:S(2)}, u32[]{:S(2)}) collective-permute-start(bf16[2,2,128,512]{3,2,1,0:T(8,128)(2,1)} %get-tuple-element.87), channel_id=1, source_target_pairs={{4,0},{6,2},{8,4},{10,6},{12,8},{14,10},{5,1},{7,3},{9,5},{11,7},{... | collective-permute-start | bytes 1572872 | tf_op jit(solution)/shard_map/ppermute | solution.py:17
  47.6 4.6 %copy-start.25 = (pred[896]{0:T(1024)(128)(4,1)S(1)}, pred[896]{0:T(1024)(128)(4,1)}, u32[]{:S(2)}) copy-start(pred[896]{0:T(1024)(128)(4,1)} %fusion.165) | copy-start | bytes 2692
  52.2 1.1 copy-start.4
  54.1 1.2 copy-start.6
  55.3 0.6 copy-start.26
  56.2 7.6 %collective-permute-start.4 = (bf16[15,1024]{1,0:T(8,128)(2,1)S(1)}, bf16[15,1024]{1,0:T(8,128)(2,1)S(1)}, u32[]{:S(2)}, u32[]{:S(2)}) collective-permute-start(bf16[15,1024]{1,0:T(8,128)(2,1)S(1)} %get-tuple-element.85), channel_id=1, source_target_pairs={{0,2},{2,4},{4,6},{6,8},{8,10},{10,12},{12,14},{1,3},{3,5},{5,7},{... | collective-permute-start | bytes 92168 | tf_op jit(solution)/shard_map/ppermute | solution.py:28
  58.2 6.7 %collective-permute-start.5 = (bf16[15,1024]{1,0:T(8,128)(2,1)S(1)}, bf16[15,1024]{1,0:T(8,128)(2,1)S(1)}, u32[]{:S(2)}, u32[]{:S(2)}) collective-permute-start(bf16[15,1024]{1,0:T(8,128)(2,1)S(1)} %get-tuple-element.86), channel_id=1, source_target_pairs={{2,0},{4,2},{6,4},{8,6},{10,8},{12,10},{14,12},{3,1},{5,3},{7,5},{... | collective-permute-start | bytes 92168 | tf_op jit(solution)/shard_map/ppermute | solution.py:30
  63.8 1.1 copy-start.20
  64.9 0.6 copy-start.22
  65.5 18.9 %copy-start.21 = (bf16[15,1024]{1,0:T(8,128)(2,1)S(1)}, bf16[15,1024]{1,0:T(8,128)(2,1)}, u32[]{:S(2)}) copy-start(bf16[15,1024]{1,0:T(8,128)(2,1)} %copy-done.20) | copy-start | bytes 92164
  72.9 15.8 %collective-permute-start.6 = (bf16[15,1024]{1,0:T(8,128)(2,1)}, bf16[15,1024]{1,0:T(8,128)(2,1)}, u32[]{:S(2)}, u32[]{:S(2)}) collective-permute-start(bf16[15,1024]{1,0:T(8,128)(2,1)} %get-tuple-element.83), channel_id=1, source_target_pairs={{2,0},{4,2},{6,4},{8,6},{10,8},{12,10},{14,12},{3,1},{5,3},{7,5},{... | collective-permute-start | bytes 92168 | tf_op jit(solution)/shard_map/ppermute | solution.py:30
  76.0 12.8 %collective-permute-start.7 = (bf16[15,1024]{1,0:T(8,128)(2,1)}, bf16[15,1024]{1,0:T(8,128)(2,1)}, u32[]{:S(2)}, u32[]{:S(2)}) collective-permute-start(bf16[15,1024]{1,0:T(8,128)(2,1)} %get-tuple-element.84), channel_id=1, source_target_pairs={{0,2},{2,4},{4,6},{6,8},{8,10},{10,12},{12,14},{1,3},{3,5},{5,7},{... | collective-permute-start | bytes 92168 | tf_op jit(solution)/shard_map/ppermute | solution.py:28
  88.8 7.5 %copy-start.17 = (f32[2,8,2,1024]{3,1,2,0:T(8,128)}, f32[2,8,2,1024]{3,1,2,0:T(8,128)S(1)}, u32[]{:S(2)}) copy-start(f32[2,8,2,1024]{3,1,2,0:T(8,128)S(1)} %copy.118) | copy-start | bytes 393220
  94.0 1.4 copy-start.1
  96.2 2.3 %collective-permute-start.12 = (bf16[1,8,34,1024]{3,1,2,0:T(8,128)(2,1)}, bf16[1,8,34,1024]{3,1,2,0:T(8,128)(2,1)}, u32[]{:S(2)}, u32[]{:S(2)}) collective-permute-start(bf16[1,8,34,1024]{3,1,2,0:T(8,128)(2,1)} %fusion.7), channel_id=1, source_target_pairs={{0,1},{1,0},{2,3},{3,2},{4,5},{5,4},{6,7},{7,6},{8,9},{9,8},{10,11... | collective-permute-start | bytes 1671176 | tf_op jit(solution)/shard_map/ppermute | solution.py:63
  96.2 2.3 %copy-start.18 = (f32[2,8,2,1024]{3,1,2,0:T(8,128)S(1)}, f32[2,8,2,1024]{3,1,2,0:T(8,128)}, u32[]{:S(2)}) copy-start(f32[2,8,2,1024]{3,1,2,0:T(8,128)} %copy-done.17) | copy-start | bytes 393220
  96.9 3.9 %copy-start.7 = (bf16[896,8,64]{0,2,1:T(8,128)(2,1)S(1)}, bf16[896,8,64]{0,2,1:T(8,128)(2,1)}, u32[]{:S(2)}) copy-start(bf16[896,8,64]{0,2,1:T(8,128)(2,1)} %reshape_squeeze.11) | copy-start | bytes 2752516
  100.2 15.6 %collective-permute-start.13 = (bf16[4,34,1024]{2,0,1:T(4,128)(2,1)S(1)}, bf16[4,34,1024]{2,0,1:T(4,128)(2,1)S(1)}, u32[]{:S(2)}, u32[]{:S(2)}) collective-permute-start(bf16[4,34,1024]{2,0,1:T(4,128)(2,1)S(1)} %fusion.101), channel_id=1, source_target_pairs={{0,8},{2,10},{4,12},{6,14},{8,0},{10,2},{12,4},{14,6},{1,9},{3,11}... | collective-permute-start | bytes 835592 | tf_op jit(solution)/shard_map/ppermute | solution.py:63
  101.7 21.0 %copy-start.2 = (bf16[8,128,896]{1,2,0:T(8,128)(2,1)}, bf16[8,128,896]{1,2,0:T(8,128)(2,1)S(1)}, u32[]{:S(2)}) copy-start(bf16[8,128,896]{1,2,0:T(8,128)(2,1)S(1)} %multiply_convert_fusion) | copy-start | bytes 5505028
  116.1 6.5 %copy-start.16 = (bf16[1,128,512]{1,2,0:T(8,128)(2,1)S(1)}, bf16[1,128,512]{1,2,0:T(8,128)(2,1)}, u32[]{:S(2)}) copy-start(bf16[1,128,512]{1,2,0:T(8,128)(2,1)} %copy-done.15) | copy-start | bytes 393220
  116.1 5.4 %collective-permute-start.14 = (bf16[2,34,1024]{2,0,1:T(2,128)(2,1)S(1)}, bf16[2,34,1024]{2,0,1:T(2,128)(2,1)S(1)}, u32[]{:S(2)}, u32[]{:S(2)}) collective-permute-start(bf16[2,34,1024]{2,0,1:T(2,128)(2,1)S(1)} %dynamic-slice_convert_fusion.1), channel_id=1, source_target_pairs={{0,4},{2,6},{4,0},{6,2},{8,12},{10,14},{12,8},{14,10},{1,5},{3,7},... | collective-permute-start | bytes 417800 | tf_op jit(solution)/shard_map/ppermute | solution.py:63
  121.9 10.3 %collective-permute-start.15 = (bf16[1,34,1024]{2,0,1:T(2,128)(2,1)S(1)}, bf16[1,34,1024]{2,0,1:T(2,128)(2,1)S(1)}, u32[]{:S(2)}, u32[]{:S(2)}) collective-permute-start(bf16[1,34,1024]{2,0,1:T(2,128)(2,1)S(1)} %dynamic-slice_convert_fusion.2), channel_id=1, source_target_pairs={{0,2},{2,0},{4,6},{6,4},{8,10},{10,8},{12,14},{14,12},{1,3},{3,1},... | collective-permute-start | bytes 208904 | tf_op jit(solution)/shard_map/ppermute | solution.py:63
  132.4 10.4 %collective-permute-start.16 = (bf16[1,34,1024]{2,0,1:T(2,128)(2,1)S(1)}, bf16[1,34,1024]{2,0,1:T(2,128)(2,1)S(1)}, u32[]{:S(2)}, u32[]{:S(2)}) collective-permute-start(bf16[1,34,1024]{2,0,1:T(2,128)(2,1)S(1)} %add_convert_fusion), channel_id=1, source_target_pairs={{0,2},{2,0},{4,6},{6,4},{8,10},{10,8},{12,14},{14,12},{1,3},{3,1},... | collective-permute-start | bytes 208904 | tf_op jit(solution)/shard_map/ppermute | solution.py:63
  136.7 27.1 %collective-permute-start.9 = (bf16[2,2,128,512]{3,2,1,0:T(8,128)(2,1)}, bf16[2,2,128,512]{3,2,1,0:T(8,128)(2,1)}, u32[]{:S(2)}, u32[]{:S(2)}) collective-permute-start(bf16[2,2,128,512]{3,2,1,0:T(8,128)(2,1)} %rev.3), channel_id=1, source_target_pairs={{4,0},{6,2},{8,4},{10,6},{12,8},{14,10},{5,1},{7,3},{9,5},{11,7},{... | collective-permute-start | bytes 1572872 | tf_op jit(solution)/shard_map/ppermute | solution.py:17
  138.0 27.1 %collective-permute-start.8 = (bf16[2,2,128,512]{3,2,1,0:T(8,128)(2,1)}, bf16[2,2,128,512]{3,2,1,0:T(8,128)(2,1)S(1)}, u32[]{:S(2)}, u32[]{:S(2)}) collective-permute-start(bf16[2,2,128,512]{3,2,1,0:T(8,128)(2,1)} %get-tuple-element.67), channel_id=1, source_target_pairs={{0,4},{2,6},{4,8},{6,10},{8,12},{10,14},{1,5},{3,7},{5,9},{7,11},{... | collective-permute-start | bytes 1572872 | tf_op jit(solution)/shard_map/ppermute | solution.py:17
  143.4 12.3 %collective-permute-start.17 = (bf16[2,34,1024]{2,0,1:T(2,128)(2,1)S(1)}, bf16[2,34,1024]{2,0,1:T(2,128)(2,1)S(1)}, u32[]{:S(2)}, u32[]{:S(2)}) collective-permute-start(bf16[2,34,1024]{2,0,1:T(2,128)(2,1)S(1)} %pad_maximum_fusion.10), channel_id=1, source_target_pairs={{0,4},{2,6},{4,0},{6,2},{8,12},{10,14},{12,8},{14,10},{1,5},{3,7},... | collective-permute-start | bytes 417800 | tf_op jit(solution)/shard_map/ppermute | solution.py:63
  156.2 1.1 copy-start.11
  156.2 1.1 copy-start.13
  157.3 15.6 %collective-permute-start.18 = (bf16[4,34,1024]{2,0,1:T(4,128)(2,1)}, bf16[4,34,1024]{2,0,1:T(4,128)(2,1)}, u32[]{:S(2)}, u32[]{:S(2)}) collective-permute-start(bf16[4,34,1024]{2,0,1:T(4,128)(2,1)} %pad_maximum_fusion.5), channel_id=1, source_target_pairs={{0,8},{2,10},{4,12},{6,14},{8,0},{10,2},{12,4},{14,6},{1,9},{3,11}... | collective-permute-start | bytes 835592 | tf_op jit(solution)/shard_map/ppermute | solution.py:63
  163.8 1.4 copy-start.8
  165.1 1.2 copy-start.9
  165.2 9.1 %copy-start.10 = (f32[2,2,128,512]{3,2,1,0:T(8,128)}, f32[2,2,128,512]{3,2,1,0:T(8,128)S(1)}, u32[]{:S(2)}) copy-start(f32[2,2,128,512]{3,2,1,0:T(8,128)S(1)} %convert_element_type.422) | copy-start | bytes 3145732
  165.2 7.7 %copy-start.12 = (bf16[2,34,1024]{2,0,1:T(2,128)(2,1)S(1)}, bf16[2,34,1024]{2,0,1:T(2,128)(2,1)}, u32[]{:S(2)}) copy-start(bf16[2,34,1024]{2,0,1:T(2,128)(2,1)} %copy-done.11) | copy-start | bytes 417796
  165.2 7.7 %copy-start.14 = (bf16[2,34,1024]{2,0,1:T(2,128)(2,1)S(1)}, bf16[2,34,1024]{2,0,1:T(2,128)(2,1)}, u32[]{:S(2)}) copy-start(bf16[2,34,1024]{2,0,1:T(2,128)(2,1)} %copy-done.13) | copy-start | bytes 417796
  165.3 10.2 %copy-start.5 = (bf16[896,8,64]{0,2,1:T(8,128)(2,1)S(1)}, bf16[896,8,64]{0,2,1:T(8,128)(2,1)}, u32[]{:S(2)}) copy-start(bf16[896,8,64]{0,2,1:T(8,128)(2,1)} %copy-done.4) | copy-start | bytes 2752516
  166.2 9.2 %copy-start.3 = (bf16[8,128,896]{1,2,0:T(8,128)(2,1)S(1)}, bf16[8,128,896]{1,2,0:T(8,128)(2,1)}, u32[]{:S(2)}) copy-start(bf16[8,128,896]{1,2,0:T(8,128)(2,1)} %copy-done.2) | copy-start | bytes 5505028
  166.2 14.3 %collective-permute-start.10 = (bf16[2,128,512]{2,1,0:T(8,128)(2,1)}, bf16[2,128,512]{2,1,0:T(8,128)(2,1)}, u32[]{:S(2)}, u32[]{:S(2)}) collective-permute-start(bf16[2,128,512]{2,1,0:T(8,128)(2,1)} %get-tuple-element.71), channel_id=1, source_target_pairs={{0,2},{2,4},{4,6},{6,8},{8,10},{10,12},{12,14},{1,3},{3,5},{5,7},{... | collective-permute-start | bytes 786440 | tf_op jit(solution)/shard_map/ppermute | solution.py:17
  170.9 9.7 %collective-permute-start.11 = (bf16[2,128,512]{2,1,0:T(8,128)(2,1)}, bf16[2,128,512]{2,1,0:T(8,128)(2,1)}, u32[]{:S(2)}, u32[]{:S(2)}) collective-permute-start(bf16[2,128,512]{2,1,0:T(8,128)(2,1)} %get-tuple-element.72), channel_id=1, source_target_pairs={{2,0},{4,2},{6,4},{8,6},{10,8},{12,10},{14,12},{3,1},{5,3},{7,5},{... | collective-permute-start | bytes 786440 | tf_op jit(solution)/shard_map/ppermute | solution.py:17
  175.4 7.5 %collective-permute-start.19 = (bf16[1,8,34,1024]{3,1,2,0:T(8,128)(2,1)}, bf16[1,8,34,1024]{3,1,2,0:T(8,128)(2,1)}, u32[]{:S(2)}, u32[]{:S(2)}) collective-permute-start(bf16[1,8,34,1024]{3,1,2,0:T(8,128)(2,1)} %maximum_bitcast_fusion), channel_id=1, source_target_pairs={{0,1},{1,0},{2,3},{3,2},{4,5},{5,4},{6,7},{7,6},{8,9},{9,8},{10,11... | collective-permute-start | bytes 1671176 | tf_op jit(solution)/shard_map/ppermute | solution.py:63

commit v8 on v7

--- a/solution.py
+++ b/solution.py
@@ -144,18 +144,20 @@
     padded_g = pad_time(grad_conv)
     grad_wide = grad_conv.astype(jnp.float32)
     grad_masked = jnp.zeros((tokens, channels), jnp.float32)
-    kernel_terms = []
     for tap_index in range(KW):
         start_row = 2 * halo_width - tap_index
         grad_masked = (
             grad_masked + conv_kernel[tap_index] * padded_g[start_row : start_row + tokens]
         )
-        kernel_terms.append(
-            jnp.sum(
-                padded_m[tap_index : tap_index + tokens].astype(jnp.float32) * grad_wide, axis=0
-            )
-        )
-    kernel_local = jnp.stack(kernel_terms, axis=0)
+    kernel_local = lax.conv_general_dilated(
+        padded_m[None],
+        grad_conv[:, None, :],
+        window_strides=(1,),
+        padding="VALID",
+        dimension_numbers=("NWC", "WIO", "NWC"),
+        feature_group_count=channels,
+        preferred_element_type=jnp.float32,
+    )[0]
     grad_hidden = (
         cot_here.astype(jnp.float32) + jnp.where(valid_rows[:, None], grad_masked, 0.0)
     ).astype(jnp.bfloat16)

time: 189 us -> 180 us (0.952)
  other arithmetic: 36.7 us -> 29.2 us
  local copies, waits for them, and re-layouts: 40.7 us -> 37.6 us
  matrix products: 8.9 us -> 11.3 us
    reduce_sum x4 -> x0, other arithmetic: 12.4 us -> none  [on_device(): jnp.sum(padded_m[tap_index:tap_index + tokens].astype(jnp.float32) * grad...]
    convert_element_type x0 -> x1, other arithmetic: none -> 4.4 us  [on_device(): grad_conv = (cot_here.astype(jnp.float32) * (sigmoid_c + conv_out * sigmo...]
    another operation x1 -> x0, local copies, waits for them, and re-layouts: 3.13 us -> none  [on_device(): kernel_local = jnp.stack(kernel_terms, axis=0)]
    conv_general_dilated x0 -> x1, matrix products: none -> 2.36 us  [on_device(): lax.conv_general_dilated(padded_m[None], grad_conv[:, None, :], window_st...]
    unnamed x61 -> x60, local copies, waits for them, and re-layouts: 6.51 us -> 6.47 us
  transfers between devices with their start and end apart: 20 -> 20, of which waited for: 10 -> 10; matrix products, arithmetic and copies ran while one was open for 26% -> 24% of each run, Pallas kernels for 0% -> 0%
where the time goes in v8:
time: 180 us; the launch traced here: 179 us
  waiting for transfers between devices  57.5 us (32%)
  starting transfers between devices  41.1 us (23%)
  local copies, waits for them, and re-layouts  37.6 us (21%)
  other arithmetic  29.2 us (16%)
  matrix products  11.3 us (6%)
  between operations  2.07 us (1%)
    ppermute x8, waiting for transfers between devices, exchange(): return lax.ppermute(block, axis, [(i, i ^ bit) for i in range(count)])  30.7 us
    ppermute x8, waiting for transfers between devices, passed_along(): return lax.ppermute(block, axis, route)  25.8 us
    ppermute x8, starting transfers between devices, passed_along(): return lax.ppermute(block, axis, route)  25.2 us
    another operation x4, local copies, waits for them, and re-layouts, on_device(): narrow = jnp.stack([key_blocks, value_blocks], axis=1).astype(jnp.bfloat16)  7.15 us
    ppermute x2, starting transfers between devices, padded(): lax.ppermute(head, axis, [((i + 1) % count, i) for i in range(ends)])  6.93 us
    unnamed x60, local copies, waits for them, and re-layouts  6.47 us
    ppermute x2, starting transfers between devices, padded(): lax.ppermute(tail, axis, [(i, (i + 1) % count) for i in range(ends)])  5.82 us
    convert_element_type x1, other arithmetic, on_device(): grad_hidden = (cot_here.astype(jnp.float32) + jnp.where(valid_rows[:, Non...  4.54 us
  transfers between devices with their start and end apart: 20, of which 10 were waited for; matrix products, arithmetic and copies ran while one was open for 24% of the time, Pallas kernels for 0%

profile of v8, /device:TPU:2, one launch (start us, length us, event | category | flops | bytes accessed | tf_op | source)
XLA Modules:
  0.0 178.7 jit_solution(14333464405838319080)
XLA Ops:
  2.6 1.9 %collective-permute-start.2 = (bf16[2,128,512]{2,1,0:T(8,128)(2,1)S(1)}, bf16[2,128,512]{2,1,0:T(8,128)(2,1)S(1)}, u32[]{:S(2)}, u32[]{:S(2)}) collective-permute-start(bf16[2,128,512]{2,1,0:T(8,128)(2,1)S(1)} %constant_dynamic-update-slice_fusion), channel_id=1, source_target_pairs={{2,0},{4,2},{6,4},{8,6},{10,8},{12,10},{14,12},{3,1},{5,3},{7,5},{... | collective-permute-start | bytes 786440 | tf_op jit(solution)/shard_map/ppermute | solution.py:17
  4.5 4.8 %collective-permute-start = (bf16[2,128,512]{2,1,0:T(8,128)(2,1)S(1)}, bf16[2,128,512]{2,1,0:T(8,128)(2,1)S(1)}, u32[]{:S(2)}, u32[]{:S(2)}) collective-permute-start(bf16[2,128,512]{2,1,0:T(8,128)(2,1)S(1)} %constant_dynamic-update-slice_fusion), channel_id=1, source_target_pairs={{0,2},{2,4},{4,6},{6,8},{8,10},{10,12},{12,14},{1,3},{3,5},{5,7},{... | collective-permute-start | bytes 786440 | tf_op jit(solution)/shard_map/ppermute | solution.py:17
  9.4 4.2 %collective-permute-done.2 = bf16[2,128,512]{2,1,0:T(8,128)(2,1)S(1)} collective-permute-done((bf16[2,128,512]{2,1,0:T(8,128)(2,1)S(1)}, bf16[2,128,512]{2,1,0:T(8,128)(2,1)S(1)}, u32[]{:S(2)}, u32[]{:S(2)}) %collective-permute-start.2) | collective-permute-done | bytes 262176 | tf_op jit(solution)/shard_map/ppermute | solution.py:17
  13.5 5.5 %collective-permute-done = bf16[2,128,512]{2,1,0:T(8,128)(2,1)S(1)} collective-permute-done((bf16[2,128,512]{2,1,0:T(8,128)(2,1)S(1)}, bf16[2,128,512]{2,1,0:T(8,128)(2,1)S(1)}, u32[]{:S(2)}, u32[]{:S(2)}) %collective-permute-start) | collective-permute-done | bytes 262176 | tf_op jit(solution)/shard_map/ppermute | solution.py:17
  20.0 4.3 %collective-permute-start.1 = (bf16[2,2,128,512]{3,2,1,0:T(8,128)(2,1)S(1)}, bf16[2,2,128,512]{3,2,1,0:T(8,128)(2,1)}, u32[]{:S(2)}, u32[]{:S(2)}) collective-permute-start(bf16[2,2,128,512]{3,2,1,0:T(8,128)(2,1)S(1)} %get-tuple-element.56), channel_id=1, source_target_pairs={{0,4},{2,6},{4,8},{6,10},{8,12},{10,14},{1,5},{3,7},{5,9},{7,11},{... | collective-permute-start | bytes 1572872 | tf_op jit(solution)/shard_map/ppermute | solution.py:17
  26.8 1.3 collective-permute-start.3
  28.1 6.7 %collective-permute-done.1 = bf16[2,2,128,512]{3,2,1,0:T(8,128)(2,1)} collective-permute-done((bf16[2,2,128,512]{3,2,1,0:T(8,128)(2,1)S(1)}, bf16[2,2,128,512]{3,2,1,0:T(8,128)(2,1)}, u32[]{:S(2)}, u32[]{:S(2)}) %collective-permute-start.1) | collective-permute-done | bytes 524320 | tf_op jit(solution)/shard_map/ppermute | solution.py:17
  36.9 5.5 %collective-permute-done.3 = bf16[2,2,128,512]{3,2,1,0:T(8,128)(2,1)S(1)} collective-permute-done((bf16[2,2,128,512]{3,2,1,0:T(8,128)(2,1)}, bf16[2,2,128,512]{3,2,1,0:T(8,128)(2,1)S(1)}, u32[]{:S(2)}, u32[]{:S(2)}) %collective-permute-start.3) | collective-permute-done | bytes 524320 | tf_op jit(solution)/shard_map/ppermute | solution.py:17
  42.5 1.4 fusion.92
  43.9 1.7 copy.116
  45.6 2.0 %reshape_squeeze.11 = bf16[896,8,64]{0,2,1:T(8,128)(2,1)} reshape(bf16[7,1,128,512]{2,0,3,1:T(8,128)(2,1)S(1)} %copy.116) | data formatting | bytes 1835008 | tf_op jit(solution)/shard_map/reshape;squeeze | solution.py:117
  47.6 2.4 %copy.114 = bf16[7,1,128,512]{2,0,3,1:T(8,128)(2,1)} copy(bf16[7,1,128,512]{3,2,1,0:T(8,128)(2,1)} %get-tuple-element.38) | data formatting | bytes 1835008 | tf_op jit(solution)/shard_map/slice | solution.py:116
  50.0 2.2 %reshape_squeeze.9 = bf16[896,8,64]{0,2,1:T(8,128)(2,1)S(1)} reshape(bf16[7,1,128,512]{2,0,3,1:T(8,128)(2,1)} %copy.114) | data formatting | bytes 1835008 | tf_op jit(solution)/shard_map/reshape;squeeze | solution.py:116
  56.2 1.9 %collective-permute-start.4 = (bf16[15,1024]{1,0:T(8,128)(2,1)S(1)}, bf16[15,1024]{1,0:T(8,128)(2,1)S(1)}, u32[]{:S(2)}, u32[]{:S(2)}) collective-permute-start(bf16[15,1024]{1,0:T(8,128)(2,1)S(1)} %get-tuple-element.53), channel_id=1, source_target_pairs={{0,2},{2,4},{4,6},{6,8},{8,10},{10,12},{12,14},{1,3},{3,5},{5,7},{... | collective-permute-start | bytes 92168 | tf_op jit(solution)/shard_map/ppermute | solution.py:28
  58.1 3.9 %collective-permute-start.5 = (bf16[15,1024]{1,0:T(8,128)(2,1)S(1)}, bf16[15,1024]{1,0:T(8,128)(2,1)S(1)}, u32[]{:S(2)}, u32[]{:S(2)}) collective-permute-start(bf16[15,1024]{1,0:T(8,128)(2,1)S(1)} %get-tuple-element.54), channel_id=1, source_target_pairs={{2,0},{4,2},{6,4},{8,6},{10,8},{12,10},{14,12},{3,1},{5,3},{7,5},{... | collective-permute-start | bytes 92168 | tf_op jit(solution)/shard_map/ppermute | solution.py:30
  62.0 1.7 fusion.97
  65.4 4.4 %fusion.13 = bf16[128,1024]{1,0:T(8,128)(2,1)S(1)} fusion(bf16[128,1024]{1,0:T(8,128)(2,1)S(1)} %fusion.4, bf16[15,1024]{1,0:T(8,128)(2,1)} %copy-done.21, bf16[15,1024]{1,0:T(8,128)(2,1)} %copy-done.20, bf16[1,128,1024]{2,1,0:T(8,128)(2,1)} %param.10, f32[1024]{0:T(1024)} %bitcast.208, f32[1024]{0:T(1024)} %bitcast.210, f32[1024]{0:T(1024)S(1)} %bitcast.152, ...), kind=kLoop, calls=%fused_computation.97 | loop fusion | flops 25165824 | bytes 974848 | tf_op jit(solution)/shard_map/convert_element_type | solution.py:143
  70.5 3.0 %collective-permute-start.6 = (bf16[15,1024]{1,0:T(8,128)(2,1)}, bf16[15,1024]{1,0:T(8,128)(2,1)}, u32[]{:S(2)}, u32[]{:S(2)}) collective-permute-start(bf16[15,1024]{1,0:T(8,128)(2,1)} %get-tuple-element.51), channel_id=1, source_target_pairs={{2,0},{4,2},{6,4},{8,6},{10,8},{12,10},{14,12},{3,1},{5,3},{7,5},{... | collective-permute-start | bytes 92168 | tf_op jit(solution)/shard_map/ppermute | solution.py:30
  73.5 3.9 %collective-permute-start.7 = (bf16[15,1024]{1,0:T(8,128)(2,1)}, bf16[15,1024]{1,0:T(8,128)(2,1)}, u32[]{:S(2)}, u32[]{:S(2)}) collective-permute-start(bf16[15,1024]{1,0:T(8,128)(2,1)} %get-tuple-element.52), channel_id=1, source_target_pairs={{0,2},{2,4},{4,6},{6,8},{8,10},{10,12},{12,14},{1,3},{3,5},{5,7},{... | collective-permute-start | bytes 92168 | tf_op jit(solution)/shard_map/ppermute | solution.py:28
  78.3 2.4 %fusion.11 = f32[1,31,1024]{2,0,1:T(1,128)S(1)} fusion(bf16[1,158,1024]{2,1,0:T(8,128)(2,1)S(1)} %maximum_bitcast_fusion.1, bf16[128,1,1024]{2,0,1:T(8,128)(2,1)S(1)} %bitcast.142), kind=kOutput, calls=%fused_computation.90 | convolution fusion | flops 8126464 | bytes 712704 | tf_op jit(solution)/shard_map/conv_general_dilated | solution.py:152
  80.9 4.5 %fusion.14 = bf16[128,1024]{1,0:T(8,128)(2,1)S(1)} fusion(bf16[128,1024]{1,0:T(8,128)(2,1)S(1)} %fusion.13, bf16[15,1024]{1,0:T(8,128)(2,1)} %collective-permute-done.7, bf16[15,1024]{1,0:T(8,128)(2,1)} %collective-permute-done.6, bf16[1,128,1024]{2,1,0:T(8,128)(2,1)} %param.10, f32[1024]{0:T(1024)} %bitcast.209, f32[1024]{0:T(1024)} %bitcast.211, ...), kind=kLoop, calls=%fused_computation.98 | loop fusion | flops 24379392 | bytes 974976 | tf_op jit(solution)/shard_map/convert_element_type | solution.py:163
  85.8 1.3 copy-done.1
  88.7 1.6 collective-permute-done.12
  90.3 1.5 fusion.9
  93.5 14.1 %collective-permute-done.13 = bf16[4,34,1024]{2,0,1:T(4,128)(2,1)S(1)} collective-permute-done((bf16[4,34,1024]{2,0,1:T(4,128)(2,1)S(1)}, bf16[4,34,1024]{2,0,1:T(4,128)(2,1)S(1)}, u32[]{:S(2)}, u32[]{:S(2)}) %collective-permute-start.13) | collective-permute-done | bytes 278560 | tf_op jit(solution)/shard_map/ppermute | solution.py:63
  108.0 2.4 %fusion.98 = (bf16[896,8,64]{0,2,1:T(8,128)(2,1)}, f32[896,8,64]{0,2,1:T(8,128)}) fusion(bf16[128,8,64]{0,2,1:T(8,128)(2,1)S(1)} %bitcast.138, bf16[8,128,896]{1,2,0:T(8,128)(2,1)S(1)} %fusion.3), kind=kOutput, calls=%fused_computation.259 | convolution fusion | flops 117899264 | bytes 4718592 | tf_op jit(solution)/shard_map/hqk,qhd->khd/dot_general | solution.py:204
  110.4 3.0 %collective-permute-done.14 = bf16[2,34,1024]{2,0,1:T(2,128)(2,1)S(1)} collective-permute-done((bf16[2,34,1024]{2,0,1:T(2,128)(2,1)S(1)}, bf16[2,34,1024]{2,0,1:T(2,128)(2,1)S(1)}, u32[]{:S(2)}, u32[]{:S(2)}) %collective-permute-start.14) | collective-permute-done | bytes 139296 | tf_op jit(solution)/shard_map/ppermute | solution.py:63
  114.1 2.3 %fusion.99 = (bf16[896,8,64]{0,2,1:T(8,128)(2,1)}, f32[896,8,64]{0,2,1:T(8,128)}) fusion(bf16[8,128,896]{1,2,0:T(8,128)(2,1)S(1)} %multiply_convert_fusion, bf16[128,8,64]{0,2,1:T(8,128)(2,1)S(1)} %bitcast.144), kind=kOutput, calls=%fused_computation.260 | convolution fusion | flops 118358016 | bytes 4718592 | tf_op jit(solution)/shard_map/hqk,qhd->khd/dot_general | solution.py:201
  116.5 2.1 %stack_reshape.8 = bf16[7,1,128,512]{2,0,3,1:T(8,128)(2,1)S(1)} reshape(bf16[896,8,64]{0,2,1:T(8,128)(2,1)} %get-tuple-element.92) | data formatting | bytes 1835008 | tf_op jit(solution)/shard_map/stack;reshape | solution.py:209
  118.6 1.5 copy.125
  120.1 2.1 %stack_reshape.9 = bf16[7,1,128,512]{2,0,3,1:T(8,128)(2,1)S(1)} reshape(bf16[896,8,64]{0,2,1:T(8,128)(2,1)} %get-tuple-element.90) | data formatting | bytes 1835008 | tf_op jit(solution)/shard_map/stack;reshape | solution.py:209
  122.2 1.4 copy.126
  123.8 1.8 collective-permute-start.16
  125.6 2.1 %pad_maximum_fusion.2 = (bf16[2,2,128,512]{3,2,1,0:T(8,128)(2,1)}, bf16[2,2,128,512]{3,2,1,0:T(8,128)(2,1)S(1)}) fusion(bf16[7,1,128,512]{3,2,1,0:T(8,128)(2,1)} %copy.126, bf16[7,1,128,512]{3,2,1,0:T(8,128)(2,1)} %copy.125), kind=kLoop, calls=%fused_computation.113 | loop fusion | flops 524288 | bytes 2883584 | tf_op jit(solution)/shard_map/slice | solution.py:48
  128.5 1.3 collective-permute-start.9
  129.8 4.8 %collective-permute-start.8 = (bf16[2,2,128,512]{3,2,1,0:T(8,128)(2,1)}, bf16[2,2,128,512]{3,2,1,0:T(8,128)(2,1)S(1)}, u32[]{:S(2)}, u32[]{:S(2)}) collective-permute-start(bf16[2,2,128,512]{3,2,1,0:T(8,128)(2,1)} %get-tuple-element.35), channel_id=1, source_target_pairs={{0,4},{2,6},{4,8},{6,10},{8,12},{10,14},{1,5},{3,7},{5,9},{7,11},{... | collective-permute-start | bytes 1572872 | tf_op jit(solution)/shard_map/ppermute | solution.py:17
  135.6 11.9 %collective-permute-done.17 = bf16[2,34,1024]{2,0,1:T(2,128)(2,1)S(1)} collective-permute-done((bf16[2,34,1024]{2,0,1:T(2,128)(2,1)S(1)}, bf16[2,34,1024]{2,0,1:T(2,128)(2,1)S(1)}, u32[]{:S(2)}, u32[]{:S(2)}) %collective-permute-start.17) | collective-permute-done | bytes 139296 | tf_op jit(solution)/shard_map/ppermute | solution.py:63
  149.1 1.2 slice.675
  150.9 2.1 %slice.676 = f32[384,8,64]{0,2,1:T(8,128)} slice(f32[896,8,64]{0,2,1:T(8,128)} %get-tuple-element.91), slice={[256:640], [0:8], [0:64]} | slice | bytes 1572864 | tf_op jit(solution)/shard_map/slice | solution.py:211
  152.9 1.4 stack.47
  155.6 1.2 convert_element_type.391
  157.9 4.4 %collective-permute-start.10 = (bf16[2,128,512]{2,1,0:T(8,128)(2,1)}, bf16[2,128,512]{2,1,0:T(8,128)(2,1)}, u32[]{:S(2)}, u32[]{:S(2)}) collective-permute-start(bf16[2,128,512]{2,1,0:T(8,128)(2,1)} %get-tuple-element.39), channel_id=1, source_target_pairs={{0,2},{2,4},{4,6},{6,8},{8,10},{10,12},{12,14},{1,3},{3,5},{5,7},{... | collective-permute-start | bytes 786440 | tf_op jit(solution)/shard_map/ppermute | solution.py:17
  162.4 2.4 %collective-permute-start.11 = (bf16[2,128,512]{2,1,0:T(8,128)(2,1)}, bf16[2,128,512]{2,1,0:T(8,128)(2,1)}, u32[]{:S(2)}, u32[]{:S(2)}) collective-permute-start(bf16[2,128,512]{2,1,0:T(8,128)(2,1)} %get-tuple-element.40), channel_id=1, source_target_pairs={{2,0},{4,2},{6,4},{8,6},{10,8},{12,10},{14,12},{3,1},{5,3},{7,5},{... | collective-permute-start | bytes 786440 | tf_op jit(solution)/shard_map/ppermute | solution.py:17
  164.8 1.4 broadcast_select_fusion.7
  168.5 3.8 %collective-permute-done.10 = bf16[2,128,512]{2,1,0:T(8,128)(2,1)} collective-permute-done((bf16[2,128,512]{2,1,0:T(8,128)(2,1)}, bf16[2,128,512]{2,1,0:T(8,128)(2,1)}, u32[]{:S(2)}, u32[]{:S(2)}) %collective-permute-start.10) | collective-permute-done | bytes 262176 | tf_op jit(solution)/shard_map/ppermute | solution.py:17
  172.4 1.6 fusion.24
  174.8 1.5 broadcast_select_fusion
  176.3 1.5 copy.131
  (125 shorter events, 29.1 us)
Async XLA Ops:
  0.6 55.1 %copy-start = (bf16[512,1024]{1,0:T(8,128)(2,1)S(1)}, bf16[512,1024]{1,0:T(8,128)(2,1)}, u32[]{:S(2)}) copy-start(bf16[512,1024]{1,0:T(8,128)(2,1)} %param.11) | copy-start | bytes 3145732
  0.6 24.2 %copy-start.22 = (bf16[1,128,512]{2,1,0:T(8,128)(2,1)S(1)}, bf16[1,128,512]{2,1,0:T(8,128)(2,1)}, u32[]{:S(2)}) copy-start(bf16[1,128,512]{2,1,0:T(8,128)(2,1)} %param.7) | copy-start | bytes 393220
  0.7 25.5 %copy-start.23 = (f32[31,1024]{1,0:T(8,128)S(1)}, f32[31,1024]{1,0:T(8,128)}, u32[]{:S(2)}) copy-start(f32[31,1024]{1,0:T(8,128)} %param.12) | copy-start | bytes 380932
  2.6 10.9 %collective-permute-start.2 = (bf16[2,128,512]{2,1,0:T(8,128)(2,1)S(1)}, bf16[2,128,512]{2,1,0:T(8,128)(2,1)S(1)}, u32[]{:S(2)}, u32[]{:S(2)}) collective-permute-start(bf16[2,128,512]{2,1,0:T(8,128)(2,1)S(1)} %constant_dynamic-update-slice_fusion), channel_id=1, source_target_pairs={{2,0},{4,2},{6,4},{8,6},{10,8},{12,10},{14,12},{3,1},{5,3},{7,5},{... | collective-permute-start | bytes 786440 | tf_op jit(solution)/shard_map/ppermute | solution.py:17
  4.5 14.5 %collective-permute-start = (bf16[2,128,512]{2,1,0:T(8,128)(2,1)S(1)}, bf16[2,128,512]{2,1,0:T(8,128)(2,1)S(1)}, u32[]{:S(2)}, u32[]{:S(2)}) collective-permute-start(bf16[2,128,512]{2,1,0:T(8,128)(2,1)S(1)} %constant_dynamic-update-slice_fusion), channel_id=1, source_target_pairs={{0,2},{2,4},{4,6},{6,8},{8,10},{10,12},{12,14},{1,3},{3,5},{5,7},{... | collective-permute-start | bytes 786440 | tf_op jit(solution)/shard_map/ppermute | solution.py:17
  19.1 9.0 %copy-start.19 = (bf16[2,128,512]{2,1,0:T(8,128)(2,1)}, bf16[2,128,512]{2,1,0:T(8,128)(2,1)S(1)}, u32[]{:S(2)}) copy-start(bf16[2,128,512]{2,1,0:T(8,128)(2,1)S(1)} %collective-permute-done) | copy-start | bytes 786436
  20.0 14.8 %collective-permute-start.1 = (bf16[2,2,128,512]{3,2,1,0:T(8,128)(2,1)S(1)}, bf16[2,2,128,512]{3,2,1,0:T(8,128)(2,1)}, u32[]{:S(2)}, u32[]{:S(2)}) collective-permute-start(bf16[2,2,128,512]{3,2,1,0:T(8,128)(2,1)S(1)} %get-tuple-element.56), channel_id=1, source_target_pairs={{0,4},{2,6},{4,8},{6,10},{8,12},{10,14},{1,5},{3,7},{5,9},{7,11},{... | collective-permute-start | bytes 1572872 | tf_op jit(solution)/shard_map/ppermute | solution.py:17
  25.0 27.2 %copy-start.15 = (bf16[1,128,512]{1,2,0:T(8,128)(2,1)}, bf16[1,128,512]{1,2,0:T(8,128)(2,1)S(1)}, u32[]{:S(2)}) copy-start(bf16[1,128,512]{1,2,0:T(8,128)(2,1)S(1)} %copy.115) | copy-start | bytes 393220
  26.8 15.7 %collective-permute-start.3 = (bf16[2,2,128,512]{3,2,1,0:T(8,128)(2,1)}, bf16[2,2,128,512]{3,2,1,0:T(8,128)(2,1)S(1)}, u32[]{:S(2)}, u32[]{:S(2)}) collective-permute-start(bf16[2,2,128,512]{3,2,1,0:T(8,128)(2,1)} %get-tuple-element.55), channel_id=1, source_target_pairs={{4,0},{6,2},{8,4},{10,6},{12,8},{14,10},{5,1},{7,3},{9,5},{11,7},{... | collective-permute-start | bytes 1572872 | tf_op jit(solution)/shard_map/ppermute | solution.py:17
  47.6 4.6 %copy-start.24 = (pred[896]{0:T(1024)(128)(4,1)S(1)}, pred[896]{0:T(1024)(128)(4,1)}, u32[]{:S(2)}) copy-start(pred[896]{0:T(1024)(128)(4,1)} %fusion.91) | copy-start | bytes 2692
  52.2 1.1 copy-start.4
  54.1 1.2 copy-start.6
  55.3 0.6 copy-start.25
  56.2 7.6 %collective-permute-start.4 = (bf16[15,1024]{1,0:T(8,128)(2,1)S(1)}, bf16[15,1024]{1,0:T(8,128)(2,1)S(1)}, u32[]{:S(2)}, u32[]{:S(2)}) collective-permute-start(bf16[15,1024]{1,0:T(8,128)(2,1)S(1)} %get-tuple-element.53), channel_id=1, source_target_pairs={{0,2},{2,4},{4,6},{6,8},{8,10},{10,12},{12,14},{1,3},{3,5},{5,7},{... | collective-permute-start | bytes 92168 | tf_op jit(solution)/shard_map/ppermute | solution.py:28
  58.1 6.7 %collective-permute-start.5 = (bf16[15,1024]{1,0:T(8,128)(2,1)S(1)}, bf16[15,1024]{1,0:T(8,128)(2,1)S(1)}, u32[]{:S(2)}, u32[]{:S(2)}) collective-permute-start(bf16[15,1024]{1,0:T(8,128)(2,1)S(1)} %get-tuple-element.54), channel_id=1, source_target_pairs={{2,0},{4,2},{6,4},{8,6},{10,8},{12,10},{14,12},{3,1},{5,3},{7,5},{... | collective-permute-start | bytes 92168 | tf_op jit(solution)/shard_map/ppermute | solution.py:30
  63.8 1.1 copy-start.20
  64.8 0.6 copy-start.21
  70.5 10.4 %collective-permute-start.6 = (bf16[15,1024]{1,0:T(8,128)(2,1)}, bf16[15,1024]{1,0:T(8,128)(2,1)}, u32[]{:S(2)}, u32[]{:S(2)}) collective-permute-start(bf16[15,1024]{1,0:T(8,128)(2,1)} %get-tuple-element.51), channel_id=1, source_target_pairs={{2,0},{4,2},{6,4},{8,6},{10,8},{12,10},{14,12},{3,1},{5,3},{7,5},{... | collective-permute-start | bytes 92168 | tf_op jit(solution)/shard_map/ppermute | solution.py:30
  73.5 7.4 %collective-permute-start.7 = (bf16[15,1024]{1,0:T(8,128)(2,1)}, bf16[15,1024]{1,0:T(8,128)(2,1)}, u32[]{:S(2)}, u32[]{:S(2)}) collective-permute-start(bf16[15,1024]{1,0:T(8,128)(2,1)} %get-tuple-element.52), channel_id=1, source_target_pairs={{0,2},{2,4},{4,6},{6,8},{8,10},{10,12},{12,14},{1,3},{3,5},{5,7},{... | collective-permute-start | bytes 92168 | tf_op jit(solution)/shard_map/ppermute | solution.py:28
  80.8 7.2 %copy-start.17 = (f32[2,8,2,1024]{3,1,2,0:T(8,128)}, f32[2,8,2,1024]{3,1,2,0:T(8,128)S(1)}, u32[]{:S(2)}) copy-start(f32[2,8,2,1024]{3,1,2,0:T(8,128)S(1)} %copy.130) | copy-start | bytes 393220
  85.8 1.3 copy-start.1
  88.0 2.3 %collective-permute-start.12 = (bf16[1,8,34,1024]{3,1,2,0:T(8,128)(2,1)}, bf16[1,8,34,1024]{3,1,2,0:T(8,128)(2,1)}, u32[]{:S(2)}, u32[]{:S(2)}) collective-permute-start(bf16[1,8,34,1024]{3,1,2,0:T(8,128)(2,1)} %fusion.7), channel_id=1, source_target_pairs={{0,1},{1,0},{2,3},{3,2},{4,5},{5,4},{6,7},{7,6},{8,9},{9,8},{10,11... | collective-permute-start | bytes 1671176 | tf_op jit(solution)/shard_map/ppermute | solution.py:63
  88.0 2.3 %copy-start.18 = (f32[2,8,2,1024]{3,1,2,0:T(8,128)S(1)}, f32[2,8,2,1024]{3,1,2,0:T(8,128)}, u32[]{:S(2)}) copy-start(f32[2,8,2,1024]{3,1,2,0:T(8,128)} %copy-done.17) | copy-start | bytes 393220
  88.7 3.9 %copy-start.7 = (bf16[896,8,64]{0,2,1:T(8,128)(2,1)S(1)}, bf16[896,8,64]{0,2,1:T(8,128)(2,1)}, u32[]{:S(2)}) copy-start(bf16[896,8,64]{0,2,1:T(8,128)(2,1)} %reshape_squeeze.11) | copy-start | bytes 2752516
  92.0 15.6 %collective-permute-start.13 = (bf16[4,34,1024]{2,0,1:T(4,128)(2,1)S(1)}, bf16[4,34,1024]{2,0,1:T(4,128)(2,1)S(1)}, u32[]{:S(2)}, u32[]{:S(2)}) collective-permute-start(bf16[4,34,1024]{2,0,1:T(4,128)(2,1)S(1)} %fusion.27), channel_id=1, source_target_pairs={{0,8},{2,10},{4,12},{6,14},{8,0},{10,2},{12,4},{14,6},{1,9},{3,11}... | collective-permute-start | bytes 835592 | tf_op jit(solution)/shard_map/ppermute | solution.py:63
  93.5 20.6 %copy-start.2 = (bf16[8,128,896]{1,2,0:T(8,128)(2,1)}, bf16[8,128,896]{1,2,0:T(8,128)(2,1)S(1)}, u32[]{:S(2)}) copy-start(bf16[8,128,896]{1,2,0:T(8,128)(2,1)S(1)} %multiply_convert_fusion) | copy-start | bytes 5505028
  108.0 6.2 %copy-start.16 = (bf16[1,128,512]{1,2,0:T(8,128)(2,1)S(1)}, bf16[1,128,512]{1,2,0:T(8,128)(2,1)}, u32[]{:S(2)}) copy-start(bf16[1,128,512]{1,2,0:T(8,128)(2,1)} %copy-done.15) | copy-start | bytes 393220
  108.0 5.4 %collective-permute-start.14 = (bf16[2,34,1024]{2,0,1:T(2,128)(2,1)S(1)}, bf16[2,34,1024]{2,0,1:T(2,128)(2,1)S(1)}, u32[]{:S(2)}, u32[]{:S(2)}) collective-permute-start(bf16[2,34,1024]{2,0,1:T(2,128)(2,1)S(1)} %dynamic-slice_convert_fusion.1), channel_id=1, source_target_pairs={{0,4},{2,6},{4,0},{6,2},{8,12},{10,14},{12,8},{14,10},{1,5},{3,7},... | collective-permute-start | bytes 417800 | tf_op jit(solution)/shard_map/ppermute | solution.py:63
  113.7 9.9 %collective-permute-start.15 = (bf16[1,34,1024]{2,0,1:T(2,128)(2,1)S(1)}, bf16[1,34,1024]{2,0,1:T(2,128)(2,1)S(1)}, u32[]{:S(2)}, u32[]{:S(2)}) collective-permute-start(bf16[1,34,1024]{2,0,1:T(2,128)(2,1)S(1)} %dynamic-slice_convert_fusion.2), channel_id=1, source_target_pairs={{0,2},{2,0},{4,6},{6,4},{8,10},{10,8},{12,14},{14,12},{1,3},{3,1},... | collective-permute-start | bytes 208904 | tf_op jit(solution)/shard_map/ppermute | solution.py:63
  123.8 10.8 %collective-permute-start.16 = (bf16[1,34,1024]{2,0,1:T(2,128)(2,1)S(1)}, bf16[1,34,1024]{2,0,1:T(2,128)(2,1)S(1)}, u32[]{:S(2)}, u32[]{:S(2)}) collective-permute-start(bf16[1,34,1024]{2,0,1:T(2,128)(2,1)S(1)} %add_convert_fusion), channel_id=1, source_target_pairs={{0,2},{2,0},{4,6},{6,4},{8,10},{10,8},{12,14},{14,12},{1,3},{3,1},... | collective-permute-start | bytes 208904 | tf_op jit(solution)/shard_map/ppermute | solution.py:63
  128.5 27.0 %collective-permute-start.9 = (bf16[2,2,128,512]{3,2,1,0:T(8,128)(2,1)}, bf16[2,2,128,512]{3,2,1,0:T(8,128)(2,1)}, u32[]{:S(2)}, u32[]{:S(2)}) collective-permute-start(bf16[2,2,128,512]{3,2,1,0:T(8,128)(2,1)} %rev.3), channel_id=1, source_target_pairs={{4,0},{6,2},{8,4},{10,6},{12,8},{14,10},{5,1},{7,3},{9,5},{11,7},{... | collective-permute-start | bytes 1572872 | tf_op jit(solution)/shard_map/ppermute | solution.py:17
  129.8 27.0 %collective-permute-start.8 = (bf16[2,2,128,512]{3,2,1,0:T(8,128)(2,1)}, bf16[2,2,128,512]{3,2,1,0:T(8,128)(2,1)S(1)}, u32[]{:S(2)}, u32[]{:S(2)}) collective-permute-start(bf16[2,2,128,512]{3,2,1,0:T(8,128)(2,1)} %get-tuple-element.35), channel_id=1, source_target_pairs={{0,4},{2,6},{4,8},{6,10},{8,12},{10,14},{1,5},{3,7},{5,9},{7,11},{... | collective-permute-start | bytes 1572872 | tf_op jit(solution)/shard_map/ppermute | solution.py:17
  135.3 12.3 %collective-permute-start.17 = (bf16[2,34,1024]{2,0,1:T(2,128)(2,1)S(1)}, bf16[2,34,1024]{2,0,1:T(2,128)(2,1)S(1)}, u32[]{:S(2)}, u32[]{:S(2)}) collective-permute-start(bf16[2,34,1024]{2,0,1:T(2,128)(2,1)S(1)} %pad_maximum_fusion.10), channel_id=1, source_target_pairs={{0,4},{2,6},{4,0},{6,2},{8,12},{10,14},{12,8},{14,10},{1,5},{3,7},... | collective-permute-start | bytes 417800 | tf_op jit(solution)/shard_map/ppermute | solution.py:63
  148.0 1.1 copy-start.11
  148.0 1.0 copy-start.13
  149.0 15.7 %collective-permute-start.18 = (bf16[4,34,1024]{2,0,1:T(4,128)(2,1)}, bf16[4,34,1024]{2,0,1:T(4,128)(2,1)}, u32[]{:S(2)}, u32[]{:S(2)}) collective-permute-start(bf16[4,34,1024]{2,0,1:T(4,128)(2,1)} %pad_maximum_fusion.5), channel_id=1, source_target_pairs={{0,8},{2,10},{4,12},{6,14},{8,0},{10,2},{12,4},{14,6},{1,9},{3,11}... | collective-permute-start | bytes 835592 | tf_op jit(solution)/shard_map/ppermute | solution.py:63
  155.5 1.4 copy-start.8
  156.8 1.1 copy-start.9
  157.0 9.2 %copy-start.10 = (f32[2,2,128,512]{3,2,1,0:T(8,128)}, f32[2,2,128,512]{3,2,1,0:T(8,128)S(1)}, u32[]{:S(2)}) copy-start(f32[2,2,128,512]{3,2,1,0:T(8,128)S(1)} %convert_element_type.390) | copy-start | bytes 3145732
  157.0 7.8 %copy-start.12 = (bf16[2,34,1024]{2,0,1:T(2,128)(2,1)S(1)}, bf16[2,34,1024]{2,0,1:T(2,128)(2,1)}, u32[]{:S(2)}) copy-start(bf16[2,34,1024]{2,0,1:T(2,128)(2,1)} %copy-done.11) | copy-start | bytes 417796
  157.0 7.8 %copy-start.14 = (bf16[2,34,1024]{2,0,1:T(2,128)(2,1)S(1)}, bf16[2,34,1024]{2,0,1:T(2,128)(2,1)}, u32[]{:S(2)}) copy-start(bf16[2,34,1024]{2,0,1:T(2,128)(2,1)} %copy-done.13) | copy-start | bytes 417796
  157.0 10.3 %copy-start.5 = (bf16[896,8,64]{0,2,1:T(8,128)(2,1)S(1)}, bf16[896,8,64]{0,2,1:T(8,128)(2,1)}, u32[]{:S(2)}) copy-start(bf16[896,8,64]{0,2,1:T(8,128)(2,1)} %copy-done.4) | copy-start | bytes 2752516
  157.9 9.3 %copy-start.3 = (bf16[8,128,896]{1,2,0:T(8,128)(2,1)S(1)}, bf16[8,128,896]{1,2,0:T(8,128)(2,1)}, u32[]{:S(2)}) copy-start(bf16[8,128,896]{1,2,0:T(8,128)(2,1)} %copy-done.2) | copy-start | bytes 5505028
  157.9 14.5 %collective-permute-start.10 = (bf16[2,128,512]{2,1,0:T(8,128)(2,1)}, bf16[2,128,512]{2,1,0:T(8,128)(2,1)}, u32[]{:S(2)}, u32[]{:S(2)}) collective-permute-start(bf16[2,128,512]{2,1,0:T(8,128)(2,1)} %get-tuple-element.39), channel_id=1, source_target_pairs={{0,2},{2,4},{4,6},{6,8},{8,10},{10,12},{12,14},{1,3},{3,5},{5,7},{... | collective-permute-start | bytes 786440 | tf_op jit(solution)/shard_map/ppermute | solution.py:17
  162.4 10.0 %collective-permute-start.11 = (bf16[2,128,512]{2,1,0:T(8,128)(2,1)}, bf16[2,128,512]{2,1,0:T(8,128)(2,1)}, u32[]{:S(2)}, u32[]{:S(2)}) collective-permute-start(bf16[2,128,512]{2,1,0:T(8,128)(2,1)} %get-tuple-element.40), channel_id=1, source_target_pairs={{2,0},{4,2},{6,4},{8,6},{10,8},{12,10},{14,12},{3,1},{5,3},{7,5},{... | collective-permute-start | bytes 786440 | tf_op jit(solution)/shard_map/ppermute | solution.py:17
  167.3 7.5 %collective-permute-start.19 = (bf16[1,8,34,1024]{3,1,2,0:T(8,128)(2,1)}, bf16[1,8,34,1024]{3,1,2,0:T(8,128)(2,1)}, u32[]{:S(2)}, u32[]{:S(2)}) collective-permute-start(bf16[1,8,34,1024]{3,1,2,0:T(8,128)(2,1)} %maximum_bitcast_fusion), channel_id=1, source_target_pairs={{0,1},{1,0},{2,3},{3,2},{4,5},{5,4},{6,7},{7,6},{8,9},{9,8},{10,11... | collective-permute-start | bytes 1671176 | tf_op jit(solution)/shard_map/ppermute | solution.py:63

commit v9 on v8

--- a/solution.py
+++ b/solution.py
@@ -35,13 +35,9 @@
 
 
 def collect(piece_own, shifter):
-    below_one = shifter(piece_own, 1)
-    above_one = shifter(piece_own, -1)
-    below = shifter(jnp.stack([below_one, piece_own], axis=0), 2)
-    above = shifter(jnp.stack([piece_own, above_one], axis=0), -2)
-    return jnp.stack(
-        [below[0], below[1], below_one, piece_own, above_one, above[0], above[1]], axis=0
-    )
+    from_below = [shifter(piece_own, distance) for distance in range(REACH, 0, -1)]
+    from_above = [shifter(piece_own, -distance) for distance in range(1, REACH + 1)]
+    return jnp.stack(from_below + [piece_own] + from_above, axis=0)
 
 
 def give_back(near, narrow, shifter):

time: 180 us -> 186 us (1.033)
  starting transfers between devices: 41.1 us -> 63.3 us
  waiting for transfers between devices: 57.5 us -> 35.7 us
  local copies, waits for them, and re-layouts: 37.6 us -> 42.4 us
    ppermute x8 -> x10, waiting for transfers between devices: 25.8 us -> 5.67 us  [passed_along(): return lax.ppermute(block, axis, route)]
    ppermute x8 -> x10, starting transfers between devices: 25.2 us -> 38.4 us  [passed_along(): return lax.ppermute(block, axis, route)]
    ppermute x8, starting transfers between devices: 3.15 us -> 10.7 us  [exchange(): return lax.ppermute(block, axis, [(i, i ^ bit) for i in range(count)])]
    ppermute x2, starting transfers between devices: 5.82 us -> 10.3 us  [padded(): lax.ppermute(tail, axis, [(i, (i + 1) % count) for i in range(ends)])]
    ppermute x8, waiting for transfers between devices: 30.7 us -> 27 us  [exchange(): return lax.ppermute(block, axis, [(i, i ^ bit) for i in range(count)])]
    unnamed x60 -> x58, local copies, waits for them, and re-layouts: 6.47 us -> 9.99 us
    ppermute x2, starting transfers between devices: 6.93 us -> 3.83 us  [padded(): lax.ppermute(head, axis, [((i + 1) % count, i) for i in range(ends)])]
    ppermute x2, waiting for transfers between devices: 1.05 us -> 3.04 us  [padded(): lax.ppermute(head, axis, [((i + 1) % count, i) for i in range(ends)])]
  transfers between devices with their start and end apart: 20 -> 22, of which waited for: 10 -> 8; matrix products, arithmetic and copies ran while one was open for 24% -> 25% of each run, Pallas kernels for 0% -> 0%
where the time goes in v9:
time: 186 us; the launch traced here: 183 us
  starting transfers between devices  63.3 us (34%)
  local copies, waits for them, and re-layouts  42.4 us (23%)
  waiting for transfers between devices  35.7 us (19%)
  other arithmetic  28.3 us (15%)
  matrix products  11.3 us (6%)
  between operations  2.11 us (1%)
    ppermute x10, starting transfers between devices, passed_along(): return lax.ppermute(block, axis, route)  38.4 us
    ppermute x8, waiting for transfers between devices, exchange(): return lax.ppermute(block, axis, [(i, i ^ bit) for i in range(count)])  27 us
    ppermute x8, starting transfers between devices, exchange(): return lax.ppermute(block, axis, [(i, i ^ bit) for i in range(count)])  10.7 us
    ppermute x2, starting transfers between devices, padded(): lax.ppermute(tail, axis, [(i, (i + 1) % count) for i in range(ends)])  10.3 us
    unnamed x58, local copies, waits for them, and re-layouts  9.99 us
    another operation x4, local copies, waits for them, and re-layouts, on_device(): narrow = jnp.stack([key_blocks, value_blocks], axis=1).astype(jnp.bfloat16)  7.15 us
    ppermute x10, waiting for transfers between devices, passed_along(): return lax.ppermute(block, axis, route)  5.67 us
    convert_element_type x1, other arithmetic, on_device(): grad_hidden = (cot_here.astype(jnp.float32) + jnp.where(valid_rows[:, Non...  4.49 us
  transfers between devices with their start and end apart: 22, of which 8 were waited for; matrix products, arithmetic and copies ran while one was open for 25% of the time, Pallas kernels for 0%

profile of v9, /device:TPU:2, one launch (start us, length us, event | category | flops | bytes accessed | tf_op | source)
XLA Modules:
  0.0 183.1 jit_solution(3617581665298591966)
XLA Ops:
  2.6 1.3 collective-permute-start.5
  3.9 1.3 collective-permute-start.4
  5.2 1.9 %collective-permute-start.3 = (bf16[2,128,512]{2,1,0:T(8,128)(2,1)S(1)}, bf16[2,128,512]{2,1,0:T(8,128)(2,1)}, u32[]{:S(2)}, u32[]{:S(2)}) collective-permute-start(bf16[2,128,512]{2,1,0:T(8,128)(2,1)S(1)} %constant_dynamic-update-slice_fusion), channel_id=1, source_target_pairs={{2,0},{4,2},{6,4},{8,6},{10,8},{12,10},{14,12},{3,1},{5,3},{7,5},{... | collective-permute-start | bytes 786440 | tf_op jit(solution)/shard_map/ppermute | solution.py:17
  7.1 5.5 %collective-permute-start.1 = (bf16[2,128,512]{2,1,0:T(8,128)(2,1)S(1)}, bf16[2,128,512]{2,1,0:T(8,128)(2,1)}, u32[]{:S(2)}, u32[]{:S(2)}) collective-permute-start(bf16[2,128,512]{2,1,0:T(8,128)(2,1)S(1)} %constant_dynamic-update-slice_fusion), channel_id=1, source_target_pairs={{0,4},{2,6},{4,8},{6,10},{8,12},{10,14},{1,5},{3,7},{5,9},{7,11},{... | collective-permute-start | bytes 786440 | tf_op jit(solution)/shard_map/ppermute | solution.py:17
  12.6 6.1 %collective-permute-start = (bf16[2,128,512]{2,1,0:T(8,128)(2,1)S(1)}, bf16[2,128,512]{2,1,0:T(8,128)(2,1)S(1)}, u32[]{:S(2)}, u32[]{:S(2)}) collective-permute-start(bf16[2,128,512]{2,1,0:T(8,128)(2,1)S(1)} %constant_dynamic-update-slice_fusion), channel_id=1, source_target_pairs={{0,6},{2,8},{4,10},{6,12},{8,14},{1,7},{3,9},{5,11},{7,13},{9,15},... | collective-permute-start | bytes 786440 | tf_op jit(solution)/shard_map/ppermute | solution.py:17
  18.7 1.9 %fusion.96 = (f32[1,1024]{1,0:T(1,128)S(1)}, f32[1,1024]{1,0:T(1,128)S(1)}, f32[1,1024]{1,0:T(1,128)S(1)}, f32[1,1024]{1,0:T(1,128)S(1)}, f32[1,1024]{1,0:T(1,12...) fusion(f32[31,1024]{1,0:T(8,128)} %param.12), kind=kLoop, calls=%fused_computation.257 | loop fusion | bytes 155648 | tf_op jit(solution)/shard_map/slice | solution.py:146
  24.2 8.5 %collective-permute-start.2 = (bf16[2,128,512]{2,1,0:T(8,128)(2,1)S(1)}, bf16[2,128,512]{2,1,0:T(8,128)(2,1)S(1)}, u32[]{:S(2)}, u32[]{:S(2)}) collective-permute-start(bf16[2,128,512]{2,1,0:T(8,128)(2,1)S(1)} %constant_dynamic-update-slice_fusion), channel_id=1, source_target_pairs={{0,2},{2,4},{4,6},{6,8},{8,10},{10,12},{12,14},{1,3},{3,5},{5,7},{... | collective-permute-start | bytes 786440 | tf_op jit(solution)/shard_map/ppermute | solution.py:17
  34.7 1.9 %collective-permute-done.2 = bf16[2,128,512]{2,1,0:T(8,128)(2,1)S(1)} collective-permute-done((bf16[2,128,512]{2,1,0:T(8,128)(2,1)S(1)}, bf16[2,128,512]{2,1,0:T(8,128)(2,1)S(1)}, u32[]{:S(2)}, u32[]{:S(2)}) %collective-permute-start.2) | collective-permute-done | bytes 262176 | tf_op jit(solution)/shard_map/ppermute | solution.py:17
  38.7 1.4 fusion.92
  40.1 1.7 copy.116
  41.8 2.0 %reshape_squeeze.11 = bf16[896,8,64]{0,2,1:T(8,128)(2,1)} reshape(bf16[7,1,128,512]{2,0,3,1:T(8,128)(2,1)S(1)} %copy.116) | data formatting | bytes 1835008 | tf_op jit(solution)/shard_map/reshape;squeeze | solution.py:113
  43.8 2.4 %copy.114 = bf16[7,1,128,512]{2,0,3,1:T(8,128)(2,1)} copy(bf16[7,1,128,512]{3,2,1,0:T(8,128)(2,1)} %get-tuple-element.38) | data formatting | bytes 1835008 | tf_op jit(solution)/shard_map/slice | solution.py:112
  46.2 2.2 %reshape_squeeze.9 = bf16[896,8,64]{0,2,1:T(8,128)(2,1)S(1)} reshape(bf16[7,1,128,512]{2,0,3,1:T(8,128)(2,1)} %copy.114) | data formatting | bytes 1835008 | tf_op jit(solution)/shard_map/reshape;squeeze | solution.py:112
  52.5 5.3 %collective-permute-start.6 = (bf16[15,1024]{1,0:T(8,128)(2,1)S(1)}, bf16[15,1024]{1,0:T(8,128)(2,1)S(1)}, u32[]{:S(2)}, u32[]{:S(2)}) collective-permute-start(bf16[15,1024]{1,0:T(8,128)(2,1)S(1)} %get-tuple-element.53), channel_id=1, source_target_pairs={{0,2},{2,4},{4,6},{6,8},{8,10},{10,12},{12,14},{1,3},{3,5},{5,7},{... | collective-permute-start | bytes 92168 | tf_op jit(solution)/shard_map/ppermute | solution.py:28
  57.8 1.9 %collective-permute-start.7 = (bf16[15,1024]{1,0:T(8,128)(2,1)S(1)}, bf16[15,1024]{1,0:T(8,128)(2,1)S(1)}, u32[]{:S(2)}, u32[]{:S(2)}) collective-permute-start(bf16[15,1024]{1,0:T(8,128)(2,1)S(1)} %get-tuple-element.54), channel_id=1, source_target_pairs={{2,0},{4,2},{6,4},{8,6},{10,8},{12,10},{14,12},{3,1},{5,3},{7,5},{... | collective-permute-start | bytes 92168 | tf_op jit(solution)/shard_map/ppermute | solution.py:30
  59.7 1.7 fusion.97
  61.4 3.0 %collective-permute-done.7 = bf16[15,1024]{1,0:T(8,128)(2,1)S(1)} collective-permute-done((bf16[15,1024]{1,0:T(8,128)(2,1)S(1)}, bf16[15,1024]{1,0:T(8,128)(2,1)S(1)}, u32[]{:S(2)}, u32[]{:S(2)}) %collective-permute-start.7) | collective-permute-done | bytes 30752 | tf_op jit(solution)/shard_map/ppermute | solution.py:30
  65.1 4.4 %fusion.13 = bf16[128,1024]{1,0:T(8,128)(2,1)S(1)} fusion(bf16[128,1024]{1,0:T(8,128)(2,1)S(1)} %fusion.4, bf16[15,1024]{1,0:T(8,128)(2,1)} %copy-done.21, bf16[15,1024]{1,0:T(8,128)(2,1)} %copy-done.20, bf16[1,128,1024]{2,1,0:T(8,128)(2,1)} %param.10, f32[1024]{0:T(1024)} %bitcast.213, f32[1024]{0:T(1024)} %bitcast.215, f32[1024]{0:T(1024)S(1)} %bitcast.157, ...), kind=kLoop, calls=%fused_computation.97 | loop fusion | flops 25165824 | bytes 974848 | tf_op jit(solution)/shard_map/convert_element_type | solution.py:139
  70.1 1.9 %collective-permute-start.8 = (bf16[15,1024]{1,0:T(8,128)(2,1)}, bf16[15,1024]{1,0:T(8,128)(2,1)}, u32[]{:S(2)}, u32[]{:S(2)}) collective-permute-start(bf16[15,1024]{1,0:T(8,128)(2,1)} %get-tuple-element.51), channel_id=1, source_target_pairs={{2,0},{4,2},{6,4},{8,6},{10,8},{12,10},{14,12},{3,1},{5,3},{7,5},{... | collective-permute-start | bytes 92168 | tf_op jit(solution)/shard_map/ppermute | solution.py:30
  72.1 5.0 %collective-permute-start.9 = (bf16[15,1024]{1,0:T(8,128)(2,1)}, bf16[15,1024]{1,0:T(8,128)(2,1)}, u32[]{:S(2)}, u32[]{:S(2)}) collective-permute-start(bf16[15,1024]{1,0:T(8,128)(2,1)} %get-tuple-element.52), channel_id=1, source_target_pairs={{0,2},{2,4},{4,6},{6,8},{8,10},{10,12},{12,14},{1,3},{3,5},{5,7},{... | collective-permute-start | bytes 92168 | tf_op jit(solution)/shard_map/ppermute | solution.py:28
  77.9 2.4 %fusion.11 = f32[1,31,1024]{2,0,1:T(1,128)S(1)} fusion(bf16[1,158,1024]{2,1,0:T(8,128)(2,1)S(1)} %maximum_bitcast_fusion.1, bf16[128,1,1024]{2,0,1:T(8,128)(2,1)S(1)} %bitcast.149), kind=kOutput, calls=%fused_computation.90 | convolution fusion | flops 8126464 | bytes 712704 | tf_op jit(solution)/shard_map/conv_general_dilated | solution.py:148
  80.5 4.5 %fusion.14 = bf16[128,1024]{1,0:T(8,128)(2,1)S(1)} fusion(bf16[128,1024]{1,0:T(8,128)(2,1)S(1)} %fusion.13, bf16[15,1024]{1,0:T(8,128)(2,1)} %collective-permute-done.9, bf16[15,1024]{1,0:T(8,128)(2,1)} %collective-permute-done.8, bf16[1,128,1024]{2,1,0:T(8,128)(2,1)} %param.10, f32[1024]{0:T(1024)} %bitcast.214, f32[1024]{0:T(1024)} %bitcast.216, ...), kind=kLoop, calls=%fused_computation.98 | loop fusion | flops 24379392 | bytes 974976 | tf_op jit(solution)/shard_map/convert_element_type | solution.py:159
  85.5 1.3 copy-done.1
  88.3 1.6 collective-permute-done.14
  90.0 1.5 fusion.9
  91.6 5.8 %collective-permute-start.15 = (bf16[4,34,1024]{2,0,1:T(4,128)(2,1)S(1)}, bf16[4,34,1024]{2,0,1:T(4,128)(2,1)S(1)}, u32[]{:S(2)}, u32[]{:S(2)}) collective-permute-start(bf16[4,34,1024]{2,0,1:T(4,128)(2,1)S(1)} %fusion.27), channel_id=1, source_target_pairs={{0,8},{2,10},{4,12},{6,14},{8,0},{10,2},{12,4},{14,6},{1,9},{3,11}... | collective-permute-start | bytes 835592 | tf_op jit(solution)/shard_map/ppermute | solution.py:59
  98.4 10.5 %collective-permute-done.15 = bf16[4,34,1024]{2,0,1:T(4,128)(2,1)S(1)} collective-permute-done((bf16[4,34,1024]{2,0,1:T(4,128)(2,1)S(1)}, bf16[4,34,1024]{2,0,1:T(4,128)(2,1)S(1)}, u32[]{:S(2)}, u32[]{:S(2)}) %collective-permute-start.15) | collective-permute-done | bytes 278560 | tf_op jit(solution)/shard_map/ppermute | solution.py:59
  109.3 2.4 %fusion.98 = (bf16[896,8,64]{0,2,1:T(8,128)(2,1)}, f32[896,8,64]{0,2,1:T(8,128)}) fusion(bf16[128,8,64]{0,2,1:T(8,128)(2,1)S(1)} %bitcast.146, bf16[8,128,896]{1,2,0:T(8,128)(2,1)S(1)} %fusion.3), kind=kOutput, calls=%fused_computation.259 | convolution fusion | flops 117899264 | bytes 4718592 | tf_op jit(solution)/shard_map/hqk,qhd->khd/dot_general | solution.py:200
  111.7 3.3 %collective-permute-done.16 = bf16[2,34,1024]{2,0,1:T(2,128)(2,1)S(1)} collective-permute-done((bf16[2,34,1024]{2,0,1:T(2,128)(2,1)S(1)}, bf16[2,34,1024]{2,0,1:T(2,128)(2,1)S(1)}, u32[]{:S(2)}, u32[]{:S(2)}) %collective-permute-start.16) | collective-permute-done | bytes 139296 | tf_op jit(solution)/shard_map/ppermute | solution.py:59
  115.5 2.4 %fusion.99 = (bf16[896,8,64]{0,2,1:T(8,128)(2,1)}, f32[896,8,64]{0,2,1:T(8,128)}) fusion(bf16[8,128,896]{1,2,0:T(8,128)(2,1)S(1)} %multiply_convert_fusion, bf16[128,8,64]{0,2,1:T(8,128)(2,1)S(1)} %bitcast.151), kind=kOutput, calls=%fused_computation.260 | convolution fusion | flops 118358016 | bytes 4718592 | tf_op jit(solution)/shard_map/hqk,qhd->khd/dot_general | solution.py:197
  117.8 2.1 %stack_reshape.8 = bf16[7,1,128,512]{2,0,3,1:T(8,128)(2,1)S(1)} reshape(bf16[896,8,64]{0,2,1:T(8,128)(2,1)} %get-tuple-element.90) | data formatting | bytes 1835008 | tf_op jit(solution)/shard_map/stack;reshape | solution.py:205
  119.9 1.5 copy.125
  121.4 2.1 %stack_reshape.9 = bf16[7,1,128,512]{2,0,3,1:T(8,128)(2,1)S(1)} reshape(bf16[896,8,64]{0,2,1:T(8,128)(2,1)} %get-tuple-element.88) | data formatting | bytes 1835008 | tf_op jit(solution)/shard_map/stack;reshape | solution.py:205
  123.5 1.4 copy.126
  125.2 2.0 %collective-permute-start.18 = (bf16[1,34,1024]{2,0,1:T(2,128)(2,1)S(1)}, bf16[1,34,1024]{2,0,1:T(2,128)(2,1)S(1)}, u32[]{:S(2)}, u32[]{:S(2)}) collective-permute-start(bf16[1,34,1024]{2,0,1:T(2,128)(2,1)S(1)} %add_convert_fusion), channel_id=1, source_target_pairs={{0,2},{2,0},{4,6},{6,4},{8,10},{10,8},{12,14},{14,12},{1,3},{3,1},... | collective-permute-start | bytes 208904 | tf_op jit(solution)/shard_map/ppermute | solution.py:59
  127.1 2.1 %pad_maximum_fusion.2 = (bf16[2,2,128,512]{3,2,1,0:T(8,128)(2,1)}, bf16[2,2,128,512]{3,2,1,0:T(8,128)(2,1)S(1)}) fusion(bf16[7,1,128,512]{3,2,1,0:T(8,128)(2,1)} %copy.126, bf16[7,1,128,512]{3,2,1,0:T(8,128)(2,1)} %copy.125), kind=kLoop, calls=%fused_computation.113 | loop fusion | flops 524288 | bytes 2883584 | tf_op jit(solution)/shard_map/slice | solution.py:44
  131.4 4.8 %collective-permute-start.10 = (bf16[2,2,128,512]{3,2,1,0:T(8,128)(2,1)}, bf16[2,2,128,512]{3,2,1,0:T(8,128)(2,1)S(1)}, u32[]{:S(2)}, u32[]{:S(2)}) collective-permute-start(bf16[2,2,128,512]{3,2,1,0:T(8,128)(2,1)} %get-tuple-element.35), channel_id=1, source_target_pairs={{0,4},{2,6},{4,8},{6,10},{8,12},{10,14},{1,5},{3,7},{5,9},{7,11},{... | collective-permute-start | bytes 1572872 | tf_op jit(solution)/shard_map/ppermute | solution.py:17
  137.1 11.7 %collective-permute-done.19 = bf16[2,34,1024]{2,0,1:T(2,128)(2,1)S(1)} collective-permute-done((bf16[2,34,1024]{2,0,1:T(2,128)(2,1)S(1)}, bf16[2,34,1024]{2,0,1:T(2,128)(2,1)S(1)}, u32[]{:S(2)}, u32[]{:S(2)}) %collective-permute-start.19) | collective-permute-done | bytes 139296 | tf_op jit(solution)/shard_map/ppermute | solution.py:59
  150.3 2.3 %collective-permute-start.20 = (bf16[4,34,1024]{2,0,1:T(4,128)(2,1)}, bf16[4,34,1024]{2,0,1:T(4,128)(2,1)}, u32[]{:S(2)}, u32[]{:S(2)}) collective-permute-start(bf16[4,34,1024]{2,0,1:T(4,128)(2,1)} %pad_maximum_fusion.3), channel_id=1, source_target_pairs={{0,8},{2,10},{4,12},{6,14},{8,0},{10,2},{12,4},{14,6},{1,9},{3,11}... | collective-permute-start | bytes 835592 | tf_op jit(solution)/shard_map/ppermute | solution.py:59
  154.5 2.1 %slice.670 = f32[384,8,64]{0,2,1:T(8,128)} slice(f32[896,8,64]{0,2,1:T(8,128)} %get-tuple-element.89), slice={[256:640], [0:8], [0:64]} | slice | bytes 1572864 | tf_op jit(solution)/shard_map/slice | solution.py:207
  156.5 1.4 stack.50
  161.5 5.8 %collective-permute-start.12 = (bf16[2,128,512]{2,1,0:T(8,128)(2,1)}, bf16[2,128,512]{2,1,0:T(8,128)(2,1)}, u32[]{:S(2)}, u32[]{:S(2)}) collective-permute-start(bf16[2,128,512]{2,1,0:T(8,128)(2,1)} %get-tuple-element.39), channel_id=1, source_target_pairs={{0,2},{2,4},{4,6},{6,8},{8,10},{10,12},{12,14},{1,3},{3,5},{5,7},{... | collective-permute-start | bytes 786440 | tf_op jit(solution)/shard_map/ppermute | solution.py:17
  167.3 1.9 %collective-permute-start.13 = (bf16[2,128,512]{2,1,0:T(8,128)(2,1)}, bf16[2,128,512]{2,1,0:T(8,128)(2,1)}, u32[]{:S(2)}, u32[]{:S(2)}) collective-permute-start(bf16[2,128,512]{2,1,0:T(8,128)(2,1)} %get-tuple-element.40), channel_id=1, source_target_pairs={{2,0},{4,2},{6,4},{8,6},{10,8},{12,10},{14,12},{3,1},{5,3},{7,5},{... | collective-permute-start | bytes 786440 | tf_op jit(solution)/shard_map/ppermute | solution.py:17
  169.3 1.4 broadcast_select_fusion.7
  173.2 3.6 %collective-permute-done.13 = bf16[2,128,512]{2,1,0:T(8,128)(2,1)} collective-permute-done((bf16[2,128,512]{2,1,0:T(8,128)(2,1)}, bf16[2,128,512]{2,1,0:T(8,128)(2,1)}, u32[]{:S(2)}, u32[]{:S(2)}) %collective-permute-start.13) | collective-permute-done | bytes 262176 | tf_op jit(solution)/shard_map/ppermute | solution.py:17
  176.8 1.6 fusion.24
  179.2 1.5 broadcast_select_fusion
  180.8 1.5 copy.131
  (126 shorter events, 33.1 us)
Async XLA Ops:
  0.6 51.3 %copy-start = (bf16[512,1024]{1,0:T(8,128)(2,1)S(1)}, bf16[512,1024]{1,0:T(8,128)(2,1)}, u32[]{:S(2)}) copy-start(bf16[512,1024]{1,0:T(8,128)(2,1)} %param.11) | copy-start | bytes 3145732
  2.6 36.1 %collective-permute-start.5 = (bf16[2,128,512]{2,1,0:T(8,128)(2,1)S(1)}, bf16[2,128,512]{2,1,0:T(8,128)(2,1)S(1)}, u32[]{:S(2)}, u32[]{:S(2)}) collective-permute-start(bf16[2,128,512]{2,1,0:T(8,128)(2,1)S(1)} %constant_dynamic-update-slice_fusion), channel_id=1, source_target_pairs={{6,0},{8,2},{10,4},{12,6},{14,8},{7,1},{9,3},{11,5},{13,7},{15,9},... | collective-permute-start | bytes 786440 | tf_op jit(solution)/shard_map/ppermute | solution.py:17
  3.9 33.8 %collective-permute-start.4 = (bf16[2,128,512]{2,1,0:T(8,128)(2,1)S(1)}, bf16[2,128,512]{2,1,0:T(8,128)(2,1)}, u32[]{:S(2)}, u32[]{:S(2)}) collective-permute-start(bf16[2,128,512]{2,1,0:T(8,128)(2,1)S(1)} %constant_dynamic-update-slice_fusion), channel_id=1, source_target_pairs={{4,0},{6,2},{8,4},{10,6},{12,8},{14,10},{5,1},{7,3},{9,5},{11,7},{... | collective-permute-start | bytes 786440 | tf_op jit(solution)/shard_map/ppermute | solution.py:17
  5.2 31.5 %collective-permute-start.3 = (bf16[2,128,512]{2,1,0:T(8,128)(2,1)S(1)}, bf16[2,128,512]{2,1,0:T(8,128)(2,1)}, u32[]{:S(2)}, u32[]{:S(2)}) collective-permute-start(bf16[2,128,512]{2,1,0:T(8,128)(2,1)S(1)} %constant_dynamic-update-slice_fusion), channel_id=1, source_target_pairs={{2,0},{4,2},{6,4},{8,6},{10,8},{12,10},{14,12},{3,1},{5,3},{7,5},{... | collective-permute-start | bytes 786440 | tf_op jit(solution)/shard_map/ppermute | solution.py:17
  7.1 26.7 %collective-permute-start.1 = (bf16[2,128,512]{2,1,0:T(8,128)(2,1)S(1)}, bf16[2,128,512]{2,1,0:T(8,128)(2,1)}, u32[]{:S(2)}, u32[]{:S(2)}) collective-permute-start(bf16[2,128,512]{2,1,0:T(8,128)(2,1)S(1)} %constant_dynamic-update-slice_fusion), channel_id=1, source_target_pairs={{0,4},{2,6},{4,8},{6,10},{8,12},{10,14},{1,5},{3,7},{5,9},{7,11},{... | collective-permute-start | bytes 786440 | tf_op jit(solution)/shard_map/ppermute | solution.py:17
  12.6 10.9 %collective-permute-start = (bf16[2,128,512]{2,1,0:T(8,128)(2,1)S(1)}, bf16[2,128,512]{2,1,0:T(8,128)(2,1)S(1)}, u32[]{:S(2)}, u32[]{:S(2)}) collective-permute-start(bf16[2,128,512]{2,1,0:T(8,128)(2,1)S(1)} %constant_dynamic-update-slice_fusion), channel_id=1, source_target_pairs={{0,6},{2,8},{4,10},{6,12},{8,14},{1,7},{3,9},{5,11},{7,13},{9,15},... | collective-permute-start | bytes 786440 | tf_op jit(solution)/shard_map/ppermute | solution.py:17
  23.5 24.9 %copy-start.15 = (bf16[1,128,512]{1,2,0:T(8,128)(2,1)}, bf16[1,128,512]{1,2,0:T(8,128)(2,1)S(1)}, u32[]{:S(2)}) copy-start(bf16[1,128,512]{1,2,0:T(8,128)(2,1)S(1)} %copy.115) | copy-start | bytes 393220
  23.5 0.7 copy-start.19
  24.2 12.4 %collective-permute-start.2 = (bf16[2,128,512]{2,1,0:T(8,128)(2,1)S(1)}, bf16[2,128,512]{2,1,0:T(8,128)(2,1)S(1)}, u32[]{:S(2)}, u32[]{:S(2)}) collective-permute-start(bf16[2,128,512]{2,1,0:T(8,128)(2,1)S(1)} %constant_dynamic-update-slice_fusion), channel_id=1, source_target_pairs={{0,2},{2,4},{4,6},{6,8},{8,10},{10,12},{12,14},{1,3},{3,5},{5,7},{... | collective-permute-start | bytes 786440 | tf_op jit(solution)/shard_map/ppermute | solution.py:17
  43.8 4.6 %copy-start.22 = (pred[896]{0:T(1024)(128)(4,1)S(1)}, pred[896]{0:T(1024)(128)(4,1)}, u32[]{:S(2)}) copy-start(pred[896]{0:T(1024)(128)(4,1)} %fusion.91) | copy-start | bytes 2692
  48.4 1.1 copy-start.4
  50.3 1.2 copy-start.6
  51.5 0.7 copy-start.23
  52.5 8.9 %collective-permute-start.6 = (bf16[15,1024]{1,0:T(8,128)(2,1)S(1)}, bf16[15,1024]{1,0:T(8,128)(2,1)S(1)}, u32[]{:S(2)}, u32[]{:S(2)}) collective-permute-start(bf16[15,1024]{1,0:T(8,128)(2,1)S(1)} %get-tuple-element.53), channel_id=1, source_target_pairs={{0,2},{2,4},{4,6},{6,8},{8,10},{10,12},{12,14},{1,3},{3,5},{5,7},{... | collective-permute-start | bytes 92168 | tf_op jit(solution)/shard_map/ppermute | solution.py:28
  57.8 6.7 %collective-permute-start.7 = (bf16[15,1024]{1,0:T(8,128)(2,1)S(1)}, bf16[15,1024]{1,0:T(8,128)(2,1)S(1)}, u32[]{:S(2)}, u32[]{:S(2)}) collective-permute-start(bf16[15,1024]{1,0:T(8,128)(2,1)S(1)} %get-tuple-element.54), channel_id=1, source_target_pairs={{2,0},{4,2},{6,4},{8,6},{10,8},{12,10},{14,12},{3,1},{5,3},{7,5},{... | collective-permute-start | bytes 92168 | tf_op jit(solution)/shard_map/ppermute | solution.py:30
  61.4 3.1 %copy-start.20 = (bf16[15,1024]{1,0:T(8,128)(2,1)}, bf16[15,1024]{1,0:T(8,128)(2,1)S(1)}, u32[]{:S(2)}) copy-start(bf16[15,1024]{1,0:T(8,128)(2,1)S(1)} %collective-permute-done.6) | copy-start | bytes 92164
  64.5 0.6 copy-start.21
  70.1 10.4 %collective-permute-start.8 = (bf16[15,1024]{1,0:T(8,128)(2,1)}, bf16[15,1024]{1,0:T(8,128)(2,1)}, u32[]{:S(2)}, u32[]{:S(2)}) collective-permute-start(bf16[15,1024]{1,0:T(8,128)(2,1)} %get-tuple-element.51), channel_id=1, source_target_pairs={{2,0},{4,2},{6,4},{8,6},{10,8},{12,10},{14,12},{3,1},{5,3},{7,5},{... | collective-permute-start | bytes 92168 | tf_op jit(solution)/shard_map/ppermute | solution.py:30
  72.1 8.5 %collective-permute-start.9 = (bf16[15,1024]{1,0:T(8,128)(2,1)}, bf16[15,1024]{1,0:T(8,128)(2,1)}, u32[]{:S(2)}, u32[]{:S(2)}) collective-permute-start(bf16[15,1024]{1,0:T(8,128)(2,1)} %get-tuple-element.52), channel_id=1, source_target_pairs={{0,2},{2,4},{4,6},{6,8},{8,10},{10,12},{12,14},{1,3},{3,5},{5,7},{... | collective-permute-start | bytes 92168 | tf_op jit(solution)/shard_map/ppermute | solution.py:28
  80.5 7.2 %copy-start.17 = (f32[2,8,2,1024]{3,1,2,0:T(8,128)}, f32[2,8,2,1024]{3,1,2,0:T(8,128)S(1)}, u32[]{:S(2)}) copy-start(f32[2,8,2,1024]{3,1,2,0:T(8,128)S(1)} %copy.130) | copy-start | bytes 393220
  85.5 1.3 copy-start.1
  87.7 2.3 %collective-permute-start.14 = (bf16[1,8,34,1024]{3,1,2,0:T(8,128)(2,1)}, bf16[1,8,34,1024]{3,1,2,0:T(8,128)(2,1)}, u32[]{:S(2)}, u32[]{:S(2)}) collective-permute-start(bf16[1,8,34,1024]{3,1,2,0:T(8,128)(2,1)} %fusion.7), channel_id=1, source_target_pairs={{0,1},{1,0},{2,3},{3,2},{4,5},{5,4},{6,7},{7,6},{8,9},{9,8},{10,11... | collective-permute-start | bytes 1671176 | tf_op jit(solution)/shard_map/ppermute | solution.py:59
  87.7 2.3 %copy-start.18 = (f32[2,8,2,1024]{3,1,2,0:T(8,128)S(1)}, f32[2,8,2,1024]{3,1,2,0:T(8,128)}, u32[]{:S(2)}) copy-start(f32[2,8,2,1024]{3,1,2,0:T(8,128)} %copy-done.17) | copy-start | bytes 393220
  88.3 9.1 %copy-start.7 = (bf16[896,8,64]{0,2,1:T(8,128)(2,1)S(1)}, bf16[896,8,64]{0,2,1:T(8,128)(2,1)}, u32[]{:S(2)}) copy-start(bf16[896,8,64]{0,2,1:T(8,128)(2,1)} %reshape_squeeze.11) | copy-start | bytes 2752516
  91.6 17.3 %collective-permute-start.15 = (bf16[4,34,1024]{2,0,1:T(4,128)(2,1)S(1)}, bf16[4,34,1024]{2,0,1:T(4,128)(2,1)S(1)}, u32[]{:S(2)}, u32[]{:S(2)}) collective-permute-start(bf16[4,34,1024]{2,0,1:T(4,128)(2,1)S(1)} %fusion.27), channel_id=1, source_target_pairs={{0,8},{2,10},{4,12},{6,14},{8,0},{10,2},{12,4},{14,6},{1,9},{3,11}... | collective-permute-start | bytes 835592 | tf_op jit(solution)/shard_map/ppermute | solution.py:59
  98.4 17.1 %copy-start.2 = (bf16[8,128,896]{1,2,0:T(8,128)(2,1)}, bf16[8,128,896]{1,2,0:T(8,128)(2,1)S(1)}, u32[]{:S(2)}) copy-start(bf16[8,128,896]{1,2,0:T(8,128)(2,1)S(1)} %multiply_convert_fusion) | copy-start | bytes 5505028
  109.2 6.2 %copy-start.16 = (bf16[1,128,512]{1,2,0:T(8,128)(2,1)S(1)}, bf16[1,128,512]{1,2,0:T(8,128)(2,1)}, u32[]{:S(2)}) copy-start(bf16[1,128,512]{1,2,0:T(8,128)(2,1)} %copy-done.15) | copy-start | bytes 393220
  109.2 5.7 %collective-permute-start.16 = (bf16[2,34,1024]{2,0,1:T(2,128)(2,1)S(1)}, bf16[2,34,1024]{2,0,1:T(2,128)(2,1)S(1)}, u32[]{:S(2)}, u32[]{:S(2)}) collective-permute-start(bf16[2,34,1024]{2,0,1:T(2,128)(2,1)S(1)} %dynamic-slice_convert_fusion.1), channel_id=1, source_target_pairs={{0,4},{2,6},{4,0},{6,2},{8,12},{10,14},{12,8},{14,10},{1,5},{3,7},... | collective-permute-start | bytes 417800 | tf_op jit(solution)/shard_map/ppermute | solution.py:59
  115.3 9.7 %collective-permute-start.17 = (bf16[1,34,1024]{2,0,1:T(2,128)(2,1)S(1)}, bf16[1,34,1024]{2,0,1:T(2,128)(2,1)S(1)}, u32[]{:S(2)}, u32[]{:S(2)}) collective-permute-start(bf16[1,34,1024]{2,0,1:T(2,128)(2,1)S(1)} %dynamic-slice_convert_fusion.2), channel_id=1, source_target_pairs={{0,2},{2,0},{4,6},{6,4},{8,10},{10,8},{12,14},{14,12},{1,3},{3,1},... | collective-permute-start | bytes 208904 | tf_op jit(solution)/shard_map/ppermute | solution.py:59
  125.2 11.0 %collective-permute-start.18 = (bf16[1,34,1024]{2,0,1:T(2,128)(2,1)S(1)}, bf16[1,34,1024]{2,0,1:T(2,128)(2,1)S(1)}, u32[]{:S(2)}, u32[]{:S(2)}) collective-permute-start(bf16[1,34,1024]{2,0,1:T(2,128)(2,1)S(1)} %add_convert_fusion), channel_id=1, source_target_pairs={{0,2},{2,0},{4,6},{6,4},{8,10},{10,8},{12,14},{14,12},{1,3},{3,1},... | collective-permute-start | bytes 208904 | tf_op jit(solution)/shard_map/ppermute | solution.py:59
  130.1 29.1 %collective-permute-start.11 = (bf16[2,2,128,512]{3,2,1,0:T(8,128)(2,1)}, bf16[2,2,128,512]{3,2,1,0:T(8,128)(2,1)}, u32[]{:S(2)}, u32[]{:S(2)}) collective-permute-start(bf16[2,2,128,512]{3,2,1,0:T(8,128)(2,1)} %rev.3), channel_id=1, source_target_pairs={{4,0},{6,2},{8,4},{10,6},{12,8},{14,10},{5,1},{7,3},{9,5},{11,7},{... | collective-permute-start | bytes 1572872 | tf_op jit(solution)/shard_map/ppermute | solution.py:17
  131.4 29.0 %collective-permute-start.10 = (bf16[2,2,128,512]{3,2,1,0:T(8,128)(2,1)}, bf16[2,2,128,512]{3,2,1,0:T(8,128)(2,1)S(1)}, u32[]{:S(2)}, u32[]{:S(2)}) collective-permute-start(bf16[2,2,128,512]{3,2,1,0:T(8,128)(2,1)} %get-tuple-element.35), channel_id=1, source_target_pairs={{0,4},{2,6},{4,8},{6,10},{8,12},{10,14},{1,5},{3,7},{5,9},{7,11},{... | collective-permute-start | bytes 1572872 | tf_op jit(solution)/shard_map/ppermute | solution.py:17
  136.8 12.0 %collective-permute-start.19 = (bf16[2,34,1024]{2,0,1:T(2,128)(2,1)S(1)}, bf16[2,34,1024]{2,0,1:T(2,128)(2,1)S(1)}, u32[]{:S(2)}, u32[]{:S(2)}) collective-permute-start(bf16[2,34,1024]{2,0,1:T(2,128)(2,1)S(1)} %pad_maximum_fusion.8), channel_id=1, source_target_pairs={{0,4},{2,6},{4,0},{6,2},{8,12},{10,14},{12,8},{14,10},{1,5},{3,7},... | collective-permute-start | bytes 417800 | tf_op jit(solution)/shard_map/ppermute | solution.py:59
  149.3 3.4 %copy-start.11 = (bf16[2,34,1024]{2,0,1:T(2,128)(2,1)}, bf16[2,34,1024]{2,0,1:T(2,128)(2,1)S(1)}, u32[]{:S(2)}) copy-start(bf16[2,34,1024]{2,0,1:T(2,128)(2,1)S(1)} %get-tuple-element.45) | copy-start | bytes 417796
  149.3 3.4 %copy-start.13 = (bf16[2,34,1024]{2,0,1:T(2,128)(2,1)}, bf16[2,34,1024]{2,0,1:T(2,128)(2,1)S(1)}, u32[]{:S(2)}) copy-start(bf16[2,34,1024]{2,0,1:T(2,128)(2,1)S(1)} %get-tuple-element.46) | copy-start | bytes 417796
  150.3 19.0 %collective-permute-start.20 = (bf16[4,34,1024]{2,0,1:T(4,128)(2,1)}, bf16[4,34,1024]{2,0,1:T(4,128)(2,1)}, u32[]{:S(2)}, u32[]{:S(2)}) collective-permute-start(bf16[4,34,1024]{2,0,1:T(4,128)(2,1)} %pad_maximum_fusion.3), channel_id=1, source_target_pairs={{0,8},{2,10},{4,12},{6,14},{8,0},{10,2},{12,4},{14,6},{1,9},{3,11}... | collective-permute-start | bytes 835592 | tf_op jit(solution)/shard_map/ppermute | solution.py:59
  159.2 1.4 copy-start.8
  160.4 1.1 copy-start.9
  160.6 10.1 %copy-start.10 = (f32[2,2,128,512]{3,2,1,0:T(8,128)}, f32[2,2,128,512]{3,2,1,0:T(8,128)S(1)}, u32[]{:S(2)}) copy-start(f32[2,2,128,512]{3,2,1,0:T(8,128)S(1)} %convert_element_type.390) | copy-start | bytes 3145732
  160.6 8.7 %copy-start.12 = (bf16[2,34,1024]{2,0,1:T(2,128)(2,1)S(1)}, bf16[2,34,1024]{2,0,1:T(2,128)(2,1)}, u32[]{:S(2)}) copy-start(bf16[2,34,1024]{2,0,1:T(2,128)(2,1)} %copy-done.11) | copy-start | bytes 417796
  160.6 8.7 %copy-start.14 = (bf16[2,34,1024]{2,0,1:T(2,128)(2,1)S(1)}, bf16[2,34,1024]{2,0,1:T(2,128)(2,1)}, u32[]{:S(2)}) copy-start(bf16[2,34,1024]{2,0,1:T(2,128)(2,1)} %copy-done.13) | copy-start | bytes 417796
  160.6 11.2 %copy-start.5 = (bf16[896,8,64]{0,2,1:T(8,128)(2,1)S(1)}, bf16[896,8,64]{0,2,1:T(8,128)(2,1)}, u32[]{:S(2)}) copy-start(bf16[896,8,64]{0,2,1:T(8,128)(2,1)} %copy-done.4) | copy-start | bytes 2752516
  161.5 10.3 %copy-start.3 = (bf16[8,128,896]{1,2,0:T(8,128)(2,1)S(1)}, bf16[8,128,896]{1,2,0:T(8,128)(2,1)}, u32[]{:S(2)}) copy-start(bf16[8,128,896]{1,2,0:T(8,128)(2,1)} %copy-done.2) | copy-start | bytes 5505028
  161.5 11.6 %collective-permute-start.12 = (bf16[2,128,512]{2,1,0:T(8,128)(2,1)}, bf16[2,128,512]{2,1,0:T(8,128)(2,1)}, u32[]{:S(2)}, u32[]{:S(2)}) collective-permute-start(bf16[2,128,512]{2,1,0:T(8,128)(2,1)} %get-tuple-element.39), channel_id=1, source_target_pairs={{0,2},{2,4},{4,6},{6,8},{8,10},{10,12},{12,14},{1,3},{3,5},{5,7},{... | collective-permute-start | bytes 786440 | tf_op jit(solution)/shard_map/ppermute | solution.py:17
  167.3 9.5 %collective-permute-start.13 = (bf16[2,128,512]{2,1,0:T(8,128)(2,1)}, bf16[2,128,512]{2,1,0:T(8,128)(2,1)}, u32[]{:S(2)}, u32[]{:S(2)}) collective-permute-start(bf16[2,128,512]{2,1,0:T(8,128)(2,1)} %get-tuple-element.40), channel_id=1, source_target_pairs={{2,0},{4,2},{6,4},{8,6},{10,8},{12,10},{14,12},{3,1},{5,3},{7,5},{... | collective-permute-start | bytes 786440 | tf_op jit(solution)/shard_map/ppermute | solution.py:17
  171.8 7.4 %collective-permute-start.21 = (bf16[1,8,34,1024]{3,1,2,0:T(8,128)(2,1)}, bf16[1,8,34,1024]{3,1,2,0:T(8,128)(2,1)}, u32[]{:S(2)}, u32[]{:S(2)}) collective-permute-start(bf16[1,8,34,1024]{3,1,2,0:T(8,128)(2,1)} %maximum_bitcast_fusion), channel_id=1, source_target_pairs={{0,1},{1,0},{2,3},{3,2},{4,5},{5,4},{6,7},{7,6},{8,9},{9,8},{10,11... | collective-permute-start | bytes 1671176 | tf_op jit(solution)/shard_map/ppermute | solution.py:59

commit v10 on v8

--- a/solution.py
+++ b/solution.py
@@ -34,14 +34,19 @@
     return cells
 
 
-def collect(piece_own, shifter):
-    below_one = shifter(piece_own, 1)
-    above_one = shifter(piece_own, -1)
+def collect(piece_own, shifter, up_extra, down_extra):
+    rows = piece_own.shape[0] * piece_own.shape[1]
+    flat = piece_own.reshape(rows, piece_own.shape[2])
+    got_below = shifter(jnp.concatenate([flat, up_extra], axis=0), 1)
+    got_above = shifter(jnp.concatenate([flat, down_extra], axis=0), -1)
+    below_one = got_below[:rows].reshape(piece_own.shape)
+    above_one = got_above[:rows].reshape(piece_own.shape)
     below = shifter(jnp.stack([below_one, piece_own], axis=0), 2)
     above = shifter(jnp.stack([piece_own, above_one], axis=0), -2)
-    return jnp.stack(
+    window = jnp.stack(
         [below[0], below[1], below_one, piece_own, above_one, above[0], above[1]], axis=0
     )
+    return window, got_below[rows:], got_above[rows:]
 
 
 def give_back(near, narrow, shifter):
@@ -112,7 +117,22 @@
     def kv_shift(piece_rows, offset_by):
         return passed_along(piece_rows, "ctx", offset_by)
 
-    gathered = collect(jnp.stack([key_here, value_here], axis=0), kv_shift)
+    halo_rows = -(-halo_width // 8) * 8
+
+    def edge_rows(rows_here):
+        padded_rows = jnp.pad(rows_here, ((0, halo_rows - halo_width), (0, 0)))
+        return padded_rows.reshape(-1, width_heads)
+
+    def edge_back(packed):
+        return packed.reshape(halo_rows, channels)[:halo_width]
+
+    gathered, cot_low, cot_high = collect(
+        jnp.stack([key_here, value_here], axis=0),
+        kv_shift,
+        edge_rows(cot_here[tokens - halo_width :]),
+        edge_rows(cot_here[:halo_width]),
+    )
+    cot_wide = jnp.concatenate([edge_back(cot_low), cot_here, edge_back(cot_high)], axis=0)
     key_all = gathered[:, 0].reshape(span_blocks * tokens, HEADS, HDIM)
     value_all = gathered[:, 1].reshape(span_blocks * tokens, HEADS, HDIM)
     query_heads = query_here.reshape(tokens, HEADS, HDIM)
@@ -130,28 +150,24 @@
     hidden = jnp.dot(attended, out_proj, preferred_element_type=jnp.float32)
     masked = jnp.where(valid_rows[:, None], hidden, 0.0).astype(jnp.bfloat16)
 
-    def pad_time(field_rows):
-        return padded(field_rows, (("ctx", 0),), halo_width)
-
-    padded_m = pad_time(masked)
-    conv_out = jnp.zeros((tokens, channels), jnp.float32)
+    wide_rows = tokens + 2 * halo_width
+    padded_m = padded(masked, (("ctx", 0),), 2 * halo_width)
+    conv_out = jnp.zeros((wide_rows, channels), jnp.float32)
     for tap_index in range(KW):
-        conv_out = conv_out + conv_kernel[tap_index] * padded_m[tap_index : tap_index + tokens]
+        conv_out = conv_out + conv_kernel[tap_index] * padded_m[tap_index : tap_index + wide_rows]
     sigmoid_c = jax.nn.sigmoid(conv_out)
     grad_conv = (
-        cot_here.astype(jnp.float32) * (sigmoid_c + conv_out * sigmoid_c * (1.0 - sigmoid_c))
+        cot_wide.astype(jnp.float32) * (sigmoid_c + conv_out * sigmoid_c * (1.0 - sigmoid_c))
     ).astype(jnp.bfloat16)
-    padded_g = pad_time(grad_conv)
-    grad_wide = grad_conv.astype(jnp.float32)
     grad_masked = jnp.zeros((tokens, channels), jnp.float32)
     for tap_index in range(KW):
         start_row = 2 * halo_width - tap_index
         grad_masked = (
-            grad_masked + conv_kernel[tap_index] * padded_g[start_row : start_row + tokens]
+            grad_masked + conv_kernel[tap_index] * grad_conv[start_row : start_row + tokens]
         )
     kernel_local = lax.conv_general_dilated(
-        padded_m[None],
-        grad_conv[:, None, :],
+        padded_m[None, halo_width : halo_width + wide_rows],
+        grad_conv[halo_width : halo_width + tokens, None, :],
         window_strides=(1,),
         padding="VALID",
         dimension_numbers=("NWC", "WIO", "NWC"),

time: 180 us -> 179 us (level)
  starting transfers between devices: 41.1 us -> 34.5 us
  local copies, waits for them, and re-layouts: 37.6 us -> 43 us
  other arithmetic: 29.2 us -> 26.1 us
    slice x3 -> x9, local copies, waits for them, and re-layouts: 2.99 us -> 8.79 us  [the longest x4 5.52 us: edge_back(): return packed.reshape(halo_rows, channels)[:halo_width]]
    ppermute x2 -> x1, starting transfers between devices: 5.82 us -> 1.91 us  [padded(): lax.ppermute(tail, axis, [(i, (i + 1) % count) for i in range(ends)])]
    convert_element_type x1, other arithmetic: 4.54 us -> 2.24 us  [on_device(): grad_hidden = (cot_here.astype(jnp.float32) + jnp.where(valid_rows[:, Non...]
    ppermute x2 -> x1, starting transfers between devices: 6.93 us -> 4.7 us  [padded(): lax.ppermute(head, axis, [((i + 1) % count, i) for i in range(ends)])]
    ppermute x8, waiting for transfers between devices: 25.8 us -> 27.9 us  [passed_along(): return lax.ppermute(block, axis, route)]
    unnamed x60 -> x112, local copies, waits for them, and re-layouts: 6.47 us -> 5.25 us
  transfers between devices with their start and end apart: 20 -> 18, of which waited for: 10 -> 9; matrix products, arithmetic and copies ran while one was open for 24% -> 24% of each run, Pallas kernels for 0% -> 0%
where the time goes in v10:
time: 179 us; the launch traced here: 176 us
  waiting for transfers between devices  58.9 us (33%)
  local copies, waits for them, and re-layouts  43 us (24%)
  starting transfers between devices  34.5 us (19%)
  other arithmetic  26.1 us (15%)
  matrix products  11.3 us (6%)
  between operations  2.6 us (1%)
    ppermute x8, waiting for transfers between devices, exchange(): return lax.ppermute(block, axis, [(i, i ^ bit) for i in range(count)])  31 us
    ppermute x8, waiting for transfers between devices, passed_along(): return lax.ppermute(block, axis, route)  27.9 us
    ppermute x8, starting transfers between devices, passed_along(): return lax.ppermute(block, axis, route)  25.2 us
    another operation x4, local copies, waits for them, and re-layouts, on_device(): narrow = jnp.stack([key_blocks, value_blocks], axis=1).astype(jnp.bfloat16)  7.13 us
    slice x4, local copies, waits for them, and re-layouts, edge_back(): return packed.reshape(halo_rows, channels)[:halo_width]  5.52 us
    unnamed x112, local copies, waits for them, and re-layouts  5.25 us
    ppermute x1, starting transfers between devices, padded(): lax.ppermute(head, axis, [((i + 1) % count, i) for i in range(ends)])  4.7 us
    convert_element_type x1, other arithmetic, on_device(): grad_conv = (cot_wide.astype(jnp.float32) * (sigmoid_c + conv_out * sigmo...  4.03 us
  transfers between devices with their start and end apart: 18, of which 9 were waited for; matrix products, arithmetic and copies ran while one was open for 24% of the time, Pallas kernels for 0%

profile of v10, /device:TPU:2, one launch (start us, length us, event | category | flops | bytes accessed | tf_op | source)
XLA Modules:
  0.0 176.4 jit_solution(2114385668864392882)
XLA Ops:
  3.5 2.1 %collective-permute-start.2 = (bf16[288,512]{1,0:T(8,128)(2,1)S(1)}, bf16[288,512]{1,0:T(8,128)(2,1)S(1)}, u32[]{:S(2)}, u32[]{:S(2)}) collective-permute-start(bf16[288,512]{1,0:T(8,128)(2,1)S(1)} %get-tuple-element.55), channel_id=1, source_target_pairs={{2,0},{4,2},{6,4},{8,6},{10,8},{12,10},{14,12},{3,1},{5,3},{7,5},{... | collective-permute-start | bytes 884744 | tf_op jit(solution)/shard_map/ppermute | solution.py:17
  5.6 4.8 %collective-permute-start = (bf16[288,512]{1,0:T(8,128)(2,1)S(1)}, bf16[288,512]{1,0:T(8,128)(2,1)S(1)}, u32[]{:S(2)}, u32[]{:S(2)}) collective-permute-start(bf16[288,512]{1,0:T(8,128)(2,1)S(1)} %get-tuple-element.56), channel_id=1, source_target_pairs={{0,2},{2,4},{4,6},{6,8},{8,10},{10,12},{12,14},{1,3},{3,5},{5,7},{... | collective-permute-start | bytes 884744 | tf_op jit(solution)/shard_map/ppermute | solution.py:17
  10.4 4.9 %collective-permute-done.2 = bf16[288,512]{1,0:T(8,128)(2,1)S(1)} collective-permute-done((bf16[288,512]{1,0:T(8,128)(2,1)S(1)}, bf16[288,512]{1,0:T(8,128)(2,1)S(1)}, u32[]{:S(2)}, u32[]{:S(2)}) %collective-permute-start.2) | collective-permute-done | bytes 294944 | tf_op jit(solution)/shard_map/ppermute | solution.py:17
  15.3 6.2 %collective-permute-done = bf16[288,512]{1,0:T(8,128)(2,1)S(1)} collective-permute-done((bf16[288,512]{1,0:T(8,128)(2,1)S(1)}, bf16[288,512]{1,0:T(8,128)(2,1)S(1)}, u32[]{:S(2)}, u32[]{:S(2)}) %collective-permute-start) | collective-permute-done | bytes 294944 | tf_op jit(solution)/shard_map/ppermute | solution.py:17
  22.3 4.3 %collective-permute-start.1 = (bf16[2,2,128,512]{3,2,1,0:T(8,128)(2,1)S(1)}, bf16[2,2,128,512]{3,2,1,0:T(8,128)(2,1)}, u32[]{:S(2)}, u32[]{:S(2)}) collective-permute-start(bf16[2,2,128,512]{3,2,1,0:T(8,128)(2,1)S(1)} %get-tuple-element.54), channel_id=1, source_target_pairs={{0,4},{2,6},{4,8},{6,10},{8,12},{10,14},{1,5},{3,7},{5,9},{7,11},{... | collective-permute-start | bytes 1572872 | tf_op jit(solution)/shard_map/ppermute | solution.py:17
  28.7 1.3 collective-permute-start.3
  30.0 7.2 %collective-permute-done.1 = bf16[2,2,128,512]{3,2,1,0:T(8,128)(2,1)} collective-permute-done((bf16[2,2,128,512]{3,2,1,0:T(8,128)(2,1)S(1)}, bf16[2,2,128,512]{3,2,1,0:T(8,128)(2,1)}, u32[]{:S(2)}, u32[]{:S(2)}) %collective-permute-start.1) | collective-permute-done | bytes 524320 | tf_op jit(solution)/shard_map/ppermute | solution.py:17
  38.3 5.8 %collective-permute-done.3 = bf16[2,2,128,512]{3,2,1,0:T(8,128)(2,1)S(1)} collective-permute-done((bf16[2,2,128,512]{3,2,1,0:T(8,128)(2,1)S(1)}, bf16[2,2,128,512]{3,2,1,0:T(8,128)(2,1)S(1)}, u32[]{:S(2)}, u32[]{:S(2)}) %collective-permute-start.3) | collective-permute-done | bytes 524320 | tf_op jit(solution)/shard_map/ppermute | solution.py:17
  44.2 1.4 fusion.34
  45.6 1.7 copy.116
  47.3 2.0 %reshape_squeeze.11 = bf16[896,8,64]{0,2,1:T(8,128)(2,1)} reshape(bf16[7,1,128,512]{2,0,3,1:T(8,128)(2,1)S(1)} %copy.116) | data formatting | bytes 1835008 | tf_op jit(solution)/shard_map/reshape;squeeze | solution.py:137
  49.3 2.4 %copy.114 = bf16[7,1,128,512]{2,0,3,1:T(8,128)(2,1)} copy(bf16[7,1,128,512]{3,2,1,0:T(8,128)(2,1)} %get-tuple-element.38) | data formatting | bytes 1835008 | tf_op jit(solution)/shard_map/slice | solution.py:136
  51.7 2.2 %reshape_squeeze.9 = bf16[896,8,64]{0,2,1:T(8,128)(2,1)S(1)} reshape(bf16[7,1,128,512]{2,0,3,1:T(8,128)(2,1)} %copy.114) | data formatting | bytes 1835008 | tf_op jit(solution)/shard_map/reshape;squeeze | solution.py:136
  55.8 1.6 fusion.3
  59.0 1.9 %collective-permute-start.4 = (bf16[30,1024]{1,0:T(8,128)(2,1)}, bf16[30,1024]{1,0:T(8,128)(2,1)}, u32[]{:S(2)}, u32[]{:S(2)}) collective-permute-start(bf16[30,1024]{1,0:T(8,128)(2,1)} %get-tuple-element.51), channel_id=1, source_target_pairs={{0,2},{2,4},{4,6},{6,8},{8,10},{10,12},{12,14},{1,3},{3,5},{5,7},{... | collective-permute-start | bytes 184328 | tf_op jit(solution)/shard_map/ppermute | solution.py:28
  60.9 4.7 %collective-permute-start.5 = (bf16[30,1024]{1,0:T(8,128)(2,1)}, bf16[30,1024]{1,0:T(8,128)(2,1)}, u32[]{:S(2)}, u32[]{:S(2)}) collective-permute-start(bf16[30,1024]{1,0:T(8,128)(2,1)} %get-tuple-element.52), channel_id=1, source_target_pairs={{2,0},{4,2},{6,4},{8,6},{10,8},{12,10},{14,12},{3,1},{5,3},{7,5},{... | collective-permute-start | bytes 184328 | tf_op jit(solution)/shard_map/ppermute | solution.py:30
  65.6 1.7 fusion.38
  67.3 1.4 slice.543
  68.7 1.4 slice.428
  70.1 1.4 slice.542
  71.4 1.4 slice.426
  74.2 4.0 %multiply_convert_fusion.1 = bf16[158,1024]{1,0:T(8,128)(2,1)S(1)} fusion(bf16[188,1024]{1,0:T(8,128)(2,1)S(1)} %pad_maximum_fusion.5, bf16[15,1024]{1,0:T(8,128)(2,1)} %slice.428, bf16[128,1024]{1,0:T(8,128)(2,1)S(1)} %bitcast.149, bf16[15,1024]{1,0:T(8,128)(2,1)} %slice.426, bf16[128,1024]{1,0:T(8,128)(2,1)S(1)} %fusion.4, ...), kind=kLoop, calls=%fused_computation.32 | loop fusion | flops 18282496 | bytes 10543104 | tf_op jit(solution)/shard_map/convert_element_type | solution.py:161
  78.5 2.2 %add_convert_fusion = bf16[128,1024]{1,0:T(8,128)(2,1)S(1)} fusion(bf16[158,1024]{1,0:T(8,128)(2,1)S(1)} %multiply_convert_fusion.1, f32[1024]{0:T(1024)S(1)} %bitcast.214, f32[1024]{0:T(1024)S(1)} %bitcast.216, f32[1024]{0:T(1024)S(1)} %bitcast.158, f32[1024]{0:T(1024)S(1)} %bitcast.160, f32[1024]{0:T(1024)S(1)} %bitcast.162, f32[1024]{0:T(1024)S(1)} %bitcast.164, ...), kind=kLoop, calls=%fused_computation.58 | loop fusion | flops 12582912 | bytes 8777856 | tf_op jit(solution)/shard_map/convert_element_type | solution.py:179
  80.8 2.4 %fusion.11 = f32[1,31,1024]{2,0,1:T(1,128)S(1)} fusion(bf16[1,158,1024]{2,1,0:T(8,128)(2,1)S(1)} %slice_bitcast_fusion, bf16[128,1,1024]{2,0,1:T(8,128)(2,1)S(1)} %slice_bitcast_fusion.1), kind=kOutput, calls=%fused_computation.33 | convolution fusion | flops 8126464 | bytes 712704 | tf_op jit(solution)/shard_map/conv_general_dilated | solution.py:168
  83.8 1.3 copy-done.1
  86.7 1.6 collective-permute-done.10
  88.3 1.5 fusion.9
  91.0 14.2 %collective-permute-done.11 = bf16[4,34,1024]{2,0,1:T(4,128)(2,1)S(1)} collective-permute-done((bf16[4,34,1024]{2,0,1:T(4,128)(2,1)S(1)}, bf16[4,34,1024]{2,0,1:T(4,128)(2,1)S(1)}, u32[]{:S(2)}, u32[]{:S(2)}) %collective-permute-start.11) | collective-permute-done | bytes 278560 | tf_op jit(solution)/shard_map/ppermute | solution.py:68
  105.6 2.4 %fusion.39 = (bf16[896,8,64]{0,2,1:T(8,128)(2,1)}, f32[896,8,64]{0,2,1:T(8,128)}) fusion(bf16[128,8,64]{0,2,1:T(8,128)(2,1)S(1)} %bitcast.146, bf16[8,128,896]{1,2,0:T(8,128)(2,1)S(1)} %fusion.3), kind=kOutput, calls=%fused_computation.106 | convolution fusion | flops 117899264 | bytes 4718592 | tf_op jit(solution)/shard_map/hqk,qhd->khd/dot_general | solution.py:220
  108.0 3.2 %collective-permute-done.12 = bf16[2,34,1024]{2,0,1:T(2,128)(2,1)S(1)} collective-permute-done((bf16[2,34,1024]{2,0,1:T(2,128)(2,1)S(1)}, bf16[2,34,1024]{2,0,1:T(2,128)(2,1)S(1)}, u32[]{:S(2)}, u32[]{:S(2)}) %collective-permute-start.12) | collective-permute-done | bytes 139296 | tf_op jit(solution)/shard_map/ppermute | solution.py:68
  111.6 2.4 %fusion.40 = (bf16[896,8,64]{0,2,1:T(8,128)(2,1)}, f32[896,8,64]{0,2,1:T(8,128)}) fusion(bf16[8,128,896]{1,2,0:T(8,128)(2,1)S(1)} %multiply_convert_fusion, bf16[128,8,64]{0,2,1:T(8,128)(2,1)S(1)} %bitcast.151), kind=kOutput, calls=%fused_computation.107 | convolution fusion | flops 118358016 | bytes 4718592 | tf_op jit(solution)/shard_map/hqk,qhd->khd/dot_general | solution.py:217
  114.0 2.1 %stack_reshape.18 = bf16[7,1,128,512]{2,0,3,1:T(8,128)(2,1)S(1)} reshape(bf16[896,8,64]{0,2,1:T(8,128)(2,1)} %get-tuple-element.94) | data formatting | bytes 1835008 | tf_op jit(solution)/shard_map/stack;reshape | solution.py:225
  116.1 1.5 copy.125
  117.5 2.1 %stack_reshape.19 = bf16[7,1,128,512]{2,0,3,1:T(8,128)(2,1)S(1)} reshape(bf16[896,8,64]{0,2,1:T(8,128)(2,1)} %get-tuple-element.92) | data formatting | bytes 1835008 | tf_op jit(solution)/shard_map/stack;reshape | solution.py:225
  119.7 1.4 copy.126
  121.3 2.1 %collective-permute-start.14 = (bf16[1,34,1024]{2,0,1:T(2,128)(2,1)S(1)}, bf16[1,34,1024]{2,0,1:T(2,128)(2,1)S(1)}, u32[]{:S(2)}, u32[]{:S(2)}) collective-permute-start(bf16[1,34,1024]{2,0,1:T(2,128)(2,1)S(1)} %add_convert_fusion.1), channel_id=1, source_target_pairs={{0,2},{2,0},{4,6},{6,4},{8,10},{10,8},{12,14},{14,12},{1,3},{3,1},... | collective-permute-start | bytes 208904 | tf_op jit(solution)/shard_map/ppermute | solution.py:68
  123.4 2.1 %pad_maximum_fusion.2 = (bf16[2,2,128,512]{3,2,1,0:T(8,128)(2,1)}, bf16[2,2,128,512]{3,2,1,0:T(8,128)(2,1)S(1)}) fusion(bf16[7,1,128,512]{3,2,1,0:T(8,128)(2,1)} %copy.126, bf16[7,1,128,512]{3,2,1,0:T(8,128)(2,1)} %copy.125), kind=kLoop, calls=%fused_computation.54 | loop fusion | flops 524288 | bytes 2883584 | tf_op jit(solution)/shard_map/slice | solution.py:53
  127.6 4.8 %collective-permute-start.6 = (bf16[2,2,128,512]{3,2,1,0:T(8,128)(2,1)}, bf16[2,2,128,512]{3,2,1,0:T(8,128)(2,1)S(1)}, u32[]{:S(2)}, u32[]{:S(2)}) collective-permute-start(bf16[2,2,128,512]{3,2,1,0:T(8,128)(2,1)} %get-tuple-element.35), channel_id=1, source_target_pairs={{0,4},{2,6},{4,8},{6,10},{8,12},{10,14},{1,5},{3,7},{5,9},{7,11},{... | collective-permute-start | bytes 1572872 | tf_op jit(solution)/shard_map/ppermute | solution.py:17
  133.4 12.0 %collective-permute-done.15 = bf16[2,34,1024]{2,0,1:T(2,128)(2,1)S(1)} collective-permute-done((bf16[2,34,1024]{2,0,1:T(2,128)(2,1)S(1)}, bf16[2,34,1024]{2,0,1:T(2,128)(2,1)S(1)}, u32[]{:S(2)}, u32[]{:S(2)}) %collective-permute-start.15) | collective-permute-done | bytes 139296 | tf_op jit(solution)/shard_map/ppermute | solution.py:68
  148.7 2.1 %slice.608 = f32[384,8,64]{0,2,1:T(8,128)} slice(f32[896,8,64]{0,2,1:T(8,128)} %get-tuple-element.93), slice={[256:640], [0:8], [0:64]} | slice | bytes 1572864 | tf_op jit(solution)/shard_map/slice | solution.py:227
  150.8 1.4 stack.37
  155.8 4.3 %collective-permute-start.8 = (bf16[2,128,512]{2,1,0:T(8,128)(2,1)}, bf16[2,128,512]{2,1,0:T(8,128)(2,1)}, u32[]{:S(2)}, u32[]{:S(2)}) collective-permute-start(bf16[2,128,512]{2,1,0:T(8,128)(2,1)} %get-tuple-element.39), channel_id=1, source_target_pairs={{0,2},{2,4},{4,6},{6,8},{8,10},{10,12},{12,14},{1,3},{3,5},{5,7},{... | collective-permute-start | bytes 786440 | tf_op jit(solution)/shard_map/ppermute | solution.py:17
  160.0 2.4 %collective-permute-start.9 = (bf16[2,128,512]{2,1,0:T(8,128)(2,1)}, bf16[2,128,512]{2,1,0:T(8,128)(2,1)}, u32[]{:S(2)}, u32[]{:S(2)}) collective-permute-start(bf16[2,128,512]{2,1,0:T(8,128)(2,1)} %get-tuple-element.40), channel_id=1, source_target_pairs={{2,0},{4,2},{6,4},{8,6},{10,8},{12,10},{14,12},{3,1},{5,3},{7,5},{... | collective-permute-start | bytes 786440 | tf_op jit(solution)/shard_map/ppermute | solution.py:17
  162.5 1.4 broadcast_select_fusion.7
  166.3 3.8 %collective-permute-done.8 = bf16[2,128,512]{2,1,0:T(8,128)(2,1)} collective-permute-done((bf16[2,128,512]{2,1,0:T(8,128)(2,1)}, bf16[2,128,512]{2,1,0:T(8,128)(2,1)}, u32[]{:S(2)}, u32[]{:S(2)}) %collective-permute-start.8) | collective-permute-done | bytes 262176 | tf_op jit(solution)/shard_map/ppermute | solution.py:17
  170.1 1.6 fusion.22
  172.5 1.5 broadcast_select_fusion
  174.0 1.5 copy.131
  (186 shorter events, 28.9 us)
Async XLA Ops:
  0.6 57.3 %copy-start = (bf16[512,1024]{1,0:T(8,128)(2,1)S(1)}, bf16[512,1024]{1,0:T(8,128)(2,1)}, u32[]{:S(2)}) copy-start(bf16[512,1024]{1,0:T(8,128)(2,1)} %param.11) | copy-start | bytes 3145732
  3.4 23.9 %copy-start.20 = (bf16[1,128,512]{2,1,0:T(8,128)(2,1)S(1)}, bf16[1,128,512]{2,1,0:T(8,128)(2,1)}, u32[]{:S(2)}) copy-start(bf16[1,128,512]{2,1,0:T(8,128)(2,1)} %param.7) | copy-start | bytes 393220
  3.5 24.5 %copy-start.21 = (f32[31,1024]{1,0:T(8,128)S(1)}, f32[31,1024]{1,0:T(8,128)}, u32[]{:S(2)}) copy-start(f32[31,1024]{1,0:T(8,128)} %param.12) | copy-start | bytes 380932
  3.5 11.8 %collective-permute-start.2 = (bf16[288,512]{1,0:T(8,128)(2,1)S(1)}, bf16[288,512]{1,0:T(8,128)(2,1)S(1)}, u32[]{:S(2)}, u32[]{:S(2)}) collective-permute-start(bf16[288,512]{1,0:T(8,128)(2,1)S(1)} %get-tuple-element.55), channel_id=1, source_target_pairs={{2,0},{4,2},{6,4},{8,6},{10,8},{12,10},{14,12},{3,1},{5,3},{7,5},{... | collective-permute-start | bytes 884744 | tf_op jit(solution)/shard_map/ppermute | solution.py:17
  5.6 15.9 %collective-permute-start = (bf16[288,512]{1,0:T(8,128)(2,1)S(1)}, bf16[288,512]{1,0:T(8,128)(2,1)S(1)}, u32[]{:S(2)}, u32[]{:S(2)}) collective-permute-start(bf16[288,512]{1,0:T(8,128)(2,1)S(1)} %get-tuple-element.56), channel_id=1, source_target_pairs={{0,2},{2,4},{4,6},{6,8},{8,10},{10,12},{12,14},{1,3},{3,5},{5,7},{... | collective-permute-start | bytes 884744 | tf_op jit(solution)/shard_map/ppermute | solution.py:17
  15.3 6.2 %copy-start.18 = (bf16[288,512]{1,0:T(8,128)(2,1)}, bf16[288,512]{1,0:T(8,128)(2,1)S(1)}, u32[]{:S(2)}) copy-start(bf16[288,512]{1,0:T(8,128)(2,1)S(1)} %collective-permute-done.2) | copy-start | bytes 884740
  22.3 14.8 %collective-permute-start.1 = (bf16[2,2,128,512]{3,2,1,0:T(8,128)(2,1)S(1)}, bf16[2,2,128,512]{3,2,1,0:T(8,128)(2,1)}, u32[]{:S(2)}, u32[]{:S(2)}) collective-permute-start(bf16[2,2,128,512]{3,2,1,0:T(8,128)(2,1)S(1)} %get-tuple-element.54), channel_id=1, source_target_pairs={{0,4},{2,6},{4,8},{6,10},{8,12},{10,14},{1,5},{3,7},{5,9},{7,11},{... | collective-permute-start | bytes 1572872 | tf_op jit(solution)/shard_map/ppermute | solution.py:17
  27.4 26.5 %copy-start.16 = (bf16[1,128,512]{1,2,0:T(8,128)(2,1)}, bf16[1,128,512]{1,2,0:T(8,128)(2,1)S(1)}, u32[]{:S(2)}) copy-start(bf16[1,128,512]{1,2,0:T(8,128)(2,1)S(1)} %copy.115) | copy-start | bytes 393220
  28.0 26.9 %copy-start.49 = (pred[896]{0:T(1024)(128)(4,1)}, pred[896]{0:T(1024)(128)(4,1)S(1)}, u32[]{:S(2)}) copy-start(pred[896]{0:T(1024)(128)(4,1)S(1)} %fusion.33) | copy-start | bytes 2692
  28.7 15.4 %collective-permute-start.3 = (bf16[2,2,128,512]{3,2,1,0:T(8,128)(2,1)S(1)}, bf16[2,2,128,512]{3,2,1,0:T(8,128)(2,1)S(1)}, u32[]{:S(2)}, u32[]{:S(2)}) collective-permute-start(bf16[2,2,128,512]{3,2,1,0:T(8,128)(2,1)S(1)} %get-tuple-element.53), channel_id=1, source_target_pairs={{4,0},{6,2},{8,4},{10,6},{12,8},{14,10},{5,1},{7,3},{9,5},{11,7},{... | collective-permute-start | bytes 1572872 | tf_op jit(solution)/shard_map/ppermute | solution.py:17
  57.9 16.0 %copy-start.11 = (bf16[1,128,1024]{2,1,0:T(8,128)(2,1)S(1)}, bf16[1,128,1024]{2,1,0:T(8,128)(2,1)}, u32[]{:S(2)}) copy-start(bf16[1,128,1024]{2,1,0:T(8,128)(2,1)} %param.10) | copy-start | bytes 786436
  59.0 13.9 %collective-permute-start.4 = (bf16[30,1024]{1,0:T(8,128)(2,1)}, bf16[30,1024]{1,0:T(8,128)(2,1)}, u32[]{:S(2)}, u32[]{:S(2)}) collective-permute-start(bf16[30,1024]{1,0:T(8,128)(2,1)} %get-tuple-element.51), channel_id=1, source_target_pairs={{0,2},{2,4},{4,6},{6,8},{8,10},{10,12},{12,14},{1,3},{3,5},{5,7},{... | collective-permute-start | bytes 184328 | tf_op jit(solution)/shard_map/ppermute | solution.py:28
  60.9 11.9 %collective-permute-start.5 = (bf16[30,1024]{1,0:T(8,128)(2,1)}, bf16[30,1024]{1,0:T(8,128)(2,1)}, u32[]{:S(2)}, u32[]{:S(2)}) collective-permute-start(bf16[30,1024]{1,0:T(8,128)(2,1)} %get-tuple-element.52), channel_id=1, source_target_pairs={{2,0},{4,2},{6,4},{8,6},{10,8},{12,10},{14,12},{3,1},{5,3},{7,5},{... | collective-permute-start | bytes 184328 | tf_op jit(solution)/shard_map/ppermute | solution.py:30
  73.9 4.3 %copy-start.22 = (f32[1,1024]{1,0:T(1,128)S(1)}, f32[1,1024]{1,0:T(1,128)}, u32[]{:S(2)}) copy-start(f32[1,1024]{1,0:T(1,128)} %get-tuple-element.63) | copy-start | bytes 12292
  73.9 4.3 %copy-start.23 = (f32[1,1024]{1,0:T(1,128)S(1)}, f32[1,1024]{1,0:T(1,128)}, u32[]{:S(2)}) copy-start(f32[1,1024]{1,0:T(1,128)} %get-tuple-element.64) | copy-start | bytes 12292
  73.9 4.3 %copy-start.24 = (f32[1,1024]{1,0:T(1,128)S(1)}, f32[1,1024]{1,0:T(1,128)}, u32[]{:S(2)}) copy-start(f32[1,1024]{1,0:T(1,128)} %get-tuple-element.65) | copy-start | bytes 12292
  73.9 4.3 %copy-start.25 = (f32[1,1024]{1,0:T(1,128)S(1)}, f32[1,1024]{1,0:T(1,128)}, u32[]{:S(2)}) copy-start(f32[1,1024]{1,0:T(1,128)} %get-tuple-element.66) | copy-start | bytes 12292
  73.9 4.3 %copy-start.26 = (f32[1,1024]{1,0:T(1,128)S(1)}, f32[1,1024]{1,0:T(1,128)}, u32[]{:S(2)}) copy-start(f32[1,1024]{1,0:T(1,128)} %get-tuple-element.67) | copy-start | bytes 12292
  73.9 4.3 %copy-start.27 = (f32[1,1024]{1,0:T(1,128)S(1)}, f32[1,1024]{1,0:T(1,128)}, u32[]{:S(2)}) copy-start(f32[1,1024]{1,0:T(1,128)} %get-tuple-element.68) | copy-start | bytes 12292
  74.0 4.3 %copy-start.28 = (f32[1,1024]{1,0:T(1,128)S(1)}, f32[1,1024]{1,0:T(1,128)}, u32[]{:S(2)}) copy-start(f32[1,1024]{1,0:T(1,128)} %get-tuple-element.69) | copy-start | bytes 12292
  74.0 4.3 %copy-start.29 = (f32[1,1024]{1,0:T(1,128)S(1)}, f32[1,1024]{1,0:T(1,128)}, u32[]{:S(2)}) copy-start(f32[1,1024]{1,0:T(1,128)} %get-tuple-element.70) | copy-start | bytes 12292
  74.0 4.3 %copy-start.30 = (f32[1,1024]{1,0:T(1,128)S(1)}, f32[1,1024]{1,0:T(1,128)}, u32[]{:S(2)}) copy-start(f32[1,1024]{1,0:T(1,128)} %get-tuple-element.71) | copy-start | bytes 12292
  74.0 4.3 %copy-start.31 = (f32[1,1024]{1,0:T(1,128)S(1)}, f32[1,1024]{1,0:T(1,128)}, u32[]{:S(2)}) copy-start(f32[1,1024]{1,0:T(1,128)} %get-tuple-element.72) | copy-start | bytes 12292
  74.0 4.3 %copy-start.32 = (f32[1,1024]{1,0:T(1,128)S(1)}, f32[1,1024]{1,0:T(1,128)}, u32[]{:S(2)}) copy-start(f32[1,1024]{1,0:T(1,128)} %get-tuple-element.73) | copy-start | bytes 12292
  74.0 4.3 %copy-start.33 = (f32[1,1024]{1,0:T(1,128)S(1)}, f32[1,1024]{1,0:T(1,128)}, u32[]{:S(2)}) copy-start(f32[1,1024]{1,0:T(1,128)} %get-tuple-element.74) | copy-start | bytes 12292
  74.0 4.3 %copy-start.34 = (f32[1,1024]{1,0:T(1,128)S(1)}, f32[1,1024]{1,0:T(1,128)}, u32[]{:S(2)}) copy-start(f32[1,1024]{1,0:T(1,128)} %get-tuple-element.75) | copy-start | bytes 12292
  74.0 4.3 %copy-start.35 = (f32[1,1024]{1,0:T(1,128)S(1)}, f32[1,1024]{1,0:T(1,128)}, u32[]{:S(2)}) copy-start(f32[1,1024]{1,0:T(1,128)} %get-tuple-element.76) | copy-start | bytes 12292
  74.0 4.3 %copy-start.36 = (f32[1,1024]{1,0:T(1,128)S(1)}, f32[1,1024]{1,0:T(1,128)}, u32[]{:S(2)}) copy-start(f32[1,1024]{1,0:T(1,128)} %get-tuple-element.77) | copy-start | bytes 12292
  74.0 4.3 %copy-start.37 = (f32[1,1024]{1,0:T(1,128)S(1)}, f32[1,1024]{1,0:T(1,128)}, u32[]{:S(2)}) copy-start(f32[1,1024]{1,0:T(1,128)} %get-tuple-element.78) | copy-start | bytes 12292
  86.0 2.3 %collective-permute-start.10 = (bf16[1,8,34,1024]{3,1,2,0:T(8,128)(2,1)}, bf16[1,8,34,1024]{3,1,2,0:T(8,128)(2,1)}, u32[]{:S(2)}, u32[]{:S(2)}) collective-permute-start(bf16[1,8,34,1024]{3,1,2,0:T(8,128)(2,1)} %fusion.7), channel_id=1, source_target_pairs={{0,1},{1,0},{2,3},{3,2},{4,5},{5,4},{6,7},{7,6},{8,9},{9,8},{10,11... | collective-permute-start | bytes 1671176 | tf_op jit(solution)/shard_map/ppermute | solution.py:68
  89.9 15.2 %collective-permute-start.11 = (bf16[4,34,1024]{2,0,1:T(4,128)(2,1)S(1)}, bf16[4,34,1024]{2,0,1:T(4,128)(2,1)S(1)}, u32[]{:S(2)}, u32[]{:S(2)}) collective-permute-start(bf16[4,34,1024]{2,0,1:T(4,128)(2,1)S(1)} %fusion.25), channel_id=1, source_target_pairs={{0,8},{2,10},{4,12},{6,14},{8,0},{10,2},{12,4},{14,6},{1,9},{3,11}... | collective-permute-start | bytes 835592 | tf_op jit(solution)/shard_map/ppermute | solution.py:68
  90.9 20.6 %copy-start.2 = (bf16[8,128,896]{1,2,0:T(8,128)(2,1)}, bf16[8,128,896]{1,2,0:T(8,128)(2,1)S(1)}, u32[]{:S(2)}) copy-start(bf16[8,128,896]{1,2,0:T(8,128)(2,1)S(1)} %multiply_convert_fusion) | copy-start | bytes 5505028
  105.5 6.1 %copy-start.17 = (bf16[1,128,512]{1,2,0:T(8,128)(2,1)S(1)}, bf16[1,128,512]{1,2,0:T(8,128)(2,1)}, u32[]{:S(2)}) copy-start(bf16[1,128,512]{1,2,0:T(8,128)(2,1)} %copy-done.16) | copy-start | bytes 393220
  105.5 5.7 %collective-permute-start.12 = (bf16[2,34,1024]{2,0,1:T(2,128)(2,1)S(1)}, bf16[2,34,1024]{2,0,1:T(2,128)(2,1)S(1)}, u32[]{:S(2)}, u32[]{:S(2)}) collective-permute-start(bf16[2,34,1024]{2,0,1:T(2,128)(2,1)S(1)} %dynamic-slice_convert_fusion.1), channel_id=1, source_target_pairs={{0,4},{2,6},{4,0},{6,2},{8,12},{10,14},{12,8},{14,10},{1,5},{3,7},... | collective-permute-start | bytes 417800 | tf_op jit(solution)/shard_map/ppermute | solution.py:68
  111.5 9.6 %collective-permute-start.13 = (bf16[1,34,1024]{2,0,1:T(2,128)(2,1)S(1)}, bf16[1,34,1024]{2,0,1:T(2,128)(2,1)S(1)}, u32[]{:S(2)}, u32[]{:S(2)}) collective-permute-start(bf16[1,34,1024]{2,0,1:T(2,128)(2,1)S(1)} %dynamic-slice_convert_fusion.2), channel_id=1, source_target_pairs={{0,2},{2,0},{4,6},{6,4},{8,10},{10,8},{12,14},{14,12},{1,3},{3,1},... | collective-permute-start | bytes 208904 | tf_op jit(solution)/shard_map/ppermute | solution.py:68
  121.3 11.1 %collective-permute-start.14 = (bf16[1,34,1024]{2,0,1:T(2,128)(2,1)S(1)}, bf16[1,34,1024]{2,0,1:T(2,128)(2,1)S(1)}, u32[]{:S(2)}, u32[]{:S(2)}) collective-permute-start(bf16[1,34,1024]{2,0,1:T(2,128)(2,1)S(1)} %add_convert_fusion.1), channel_id=1, source_target_pairs={{0,2},{2,0},{4,6},{6,4},{8,10},{10,8},{12,14},{14,12},{1,3},{3,1},... | collective-permute-start | bytes 208904 | tf_op jit(solution)/shard_map/ppermute | solution.py:68
  126.3 27.1 %collective-permute-start.7 = (bf16[2,2,128,512]{3,2,1,0:T(8,128)(2,1)}, bf16[2,2,128,512]{3,2,1,0:T(8,128)(2,1)}, u32[]{:S(2)}, u32[]{:S(2)}) collective-permute-start(bf16[2,2,128,512]{3,2,1,0:T(8,128)(2,1)} %rev.3), channel_id=1, source_target_pairs={{4,0},{6,2},{8,4},{10,6},{12,8},{14,10},{5,1},{7,3},{9,5},{11,7},{... | collective-permute-start | bytes 1572872 | tf_op jit(solution)/shard_map/ppermute | solution.py:17
  127.6 27.0 %collective-permute-start.6 = (bf16[2,2,128,512]{3,2,1,0:T(8,128)(2,1)}, bf16[2,2,128,512]{3,2,1,0:T(8,128)(2,1)S(1)}, u32[]{:S(2)}, u32[]{:S(2)}) collective-permute-start(bf16[2,2,128,512]{3,2,1,0:T(8,128)(2,1)} %get-tuple-element.35), channel_id=1, source_target_pairs={{0,4},{2,6},{4,8},{6,10},{8,12},{10,14},{1,5},{3,7},{5,9},{7,11},{... | collective-permute-start | bytes 1572872 | tf_op jit(solution)/shard_map/ppermute | solution.py:17
  133.1 12.3 %collective-permute-start.15 = (bf16[2,34,1024]{2,0,1:T(2,128)(2,1)S(1)}, bf16[2,34,1024]{2,0,1:T(2,128)(2,1)S(1)}, u32[]{:S(2)}, u32[]{:S(2)}) collective-permute-start(bf16[2,34,1024]{2,0,1:T(2,128)(2,1)S(1)} %pad_maximum_fusion.9), channel_id=1, source_target_pairs={{0,4},{2,6},{4,0},{6,2},{8,12},{10,14},{12,8},{14,10},{1,5},{3,7},... | collective-permute-start | bytes 417800 | tf_op jit(solution)/shard_map/ppermute | solution.py:68
  146.8 15.6 %collective-permute-start.16 = (bf16[4,34,1024]{2,0,1:T(4,128)(2,1)}, bf16[4,34,1024]{2,0,1:T(4,128)(2,1)}, u32[]{:S(2)}, u32[]{:S(2)}) collective-permute-start(bf16[4,34,1024]{2,0,1:T(4,128)(2,1)} %pad_maximum_fusion.8), channel_id=1, source_target_pairs={{0,8},{2,10},{4,12},{6,14},{8,0},{10,2},{12,4},{14,6},{1,9},{3,11}... | collective-permute-start | bytes 835592 | tf_op jit(solution)/shard_map/ppermute | solution.py:68
  154.8 9.1 %copy-start.10 = (f32[2,2,128,512]{3,2,1,0:T(8,128)}, f32[2,2,128,512]{3,2,1,0:T(8,128)S(1)}, u32[]{:S(2)}) copy-start(f32[2,2,128,512]{3,2,1,0:T(8,128)S(1)} %convert_element_type.392) | copy-start | bytes 3145732
  154.8 7.7 %copy-start.13 = (bf16[2,34,1024]{2,0,1:T(2,128)(2,1)S(1)}, bf16[2,34,1024]{2,0,1:T(2,128)(2,1)}, u32[]{:S(2)}) copy-start(bf16[2,34,1024]{2,0,1:T(2,128)(2,1)} %copy-done.12) | copy-start | bytes 417796
  154.8 7.7 %copy-start.15 = (bf16[2,34,1024]{2,0,1:T(2,128)(2,1)S(1)}, bf16[2,34,1024]{2,0,1:T(2,128)(2,1)}, u32[]{:S(2)}) copy-start(bf16[2,34,1024]{2,0,1:T(2,128)(2,1)} %copy-done.14) | copy-start | bytes 417796
  154.8 10.2 %copy-start.5 = (bf16[896,8,64]{0,2,1:T(8,128)(2,1)S(1)}, bf16[896,8,64]{0,2,1:T(8,128)(2,1)}, u32[]{:S(2)}) copy-start(bf16[896,8,64]{0,2,1:T(8,128)(2,1)} %copy-done.4) | copy-start | bytes 2752516
  155.8 9.2 %copy-start.3 = (bf16[8,128,896]{1,2,0:T(8,128)(2,1)S(1)}, bf16[8,128,896]{1,2,0:T(8,128)(2,1)}, u32[]{:S(2)}) copy-start(bf16[8,128,896]{1,2,0:T(8,128)(2,1)} %copy-done.2) | copy-start | bytes 5505028
  155.8 14.3 %collective-permute-start.8 = (bf16[2,128,512]{2,1,0:T(8,128)(2,1)}, bf16[2,128,512]{2,1,0:T(8,128)(2,1)}, u32[]{:S(2)}, u32[]{:S(2)}) collective-permute-start(bf16[2,128,512]{2,1,0:T(8,128)(2,1)} %get-tuple-element.39), channel_id=1, source_target_pairs={{0,2},{2,4},{4,6},{6,8},{8,10},{10,12},{12,14},{1,3},{3,5},{5,7},{... | collective-permute-start | bytes 786440 | tf_op jit(solution)/shard_map/ppermute | solution.py:17
  160.0 10.1 %collective-permute-start.9 = (bf16[2,128,512]{2,1,0:T(8,128)(2,1)}, bf16[2,128,512]{2,1,0:T(8,128)(2,1)}, u32[]{:S(2)}, u32[]{:S(2)}) collective-permute-start(bf16[2,128,512]{2,1,0:T(8,128)(2,1)} %get-tuple-element.40), channel_id=1, source_target_pairs={{2,0},{4,2},{6,4},{8,6},{10,8},{12,10},{14,12},{3,1},{5,3},{7,5},{... | collective-permute-start | bytes 786440 | tf_op jit(solution)/shard_map/ppermute | solution.py:17
  165.0 7.5 %collective-permute-start.17 = (bf16[1,8,34,1024]{3,1,2,0:T(8,128)(2,1)}, bf16[1,8,34,1024]{3,1,2,0:T(8,128)(2,1)}, u32[]{:S(2)}, u32[]{:S(2)}) collective-permute-start(bf16[1,8,34,1024]{3,1,2,0:T(8,128)(2,1)} %maximum_bitcast_fusion), channel_id=1, source_target_pairs={{0,1},{1,0},{2,3},{3,2},{4,5},{5,4},{6,7},{7,6},{8,9},{9,8},{10,11... | collective-permute-start | bytes 1671176 | tf_op jit(solution)/shard_map/ppermute | solution.py:68
  (22 other events, 65.1 us)

commit v11 on v10

--- a/solution.py
+++ b/solution.py
@@ -133,20 +133,36 @@
         edge_rows(cot_here[:halo_width]),
     )
     cot_wide = jnp.concatenate([edge_back(cot_low), cot_here, edge_back(cot_high)], axis=0)
-    key_all = gathered[:, 0].reshape(span_blocks * tokens, HEADS, HDIM)
-    value_all = gathered[:, 1].reshape(span_blocks * tokens, HEADS, HDIM)
-    query_heads = query_here.reshape(tokens, HEADS, HDIM)
-    scores = (
-        jnp.einsum("qhd,khd->hqk", query_heads, key_all, preferred_element_type=jnp.float32)
-        * scale_factor
-    )
-    scores = jnp.where(valid_keys[None, None, :], scores, -jnp.inf)
-    row_max = jnp.max(scores, axis=2, keepdims=True)
-    row_total = jnp.sum(jnp.exp(scores - row_max), axis=2, keepdims=True)
+    kv_rows = span_blocks * tokens
+    key_all = gathered[:, 0].reshape(kv_rows, width_heads)
+    value_all = gathered[:, 1].reshape(kv_rows, width_heads)
+    head_mask = (
+        jnp.arange(HEADS, dtype=jnp.int32)[:, None, None]
+        == (jnp.arange(width_heads, dtype=jnp.int32) // HDIM)[None, None, :]
+    )
+
+    def spread(rows):
+        return jnp.where(head_mask, rows[None], jnp.zeros((), rows.dtype)).reshape(
+            HEADS * tokens, width_heads
+        )
+
+    def own_heads(stacked_rows):
+        picked = jnp.where(head_mask, stacked_rows.reshape(HEADS, tokens, width_heads), 0.0)
+        return jnp.sum(picked, axis=0)
+
+    def contract(lhs, rhs, lhs_dim, rhs_dim):
+        return lax.dot_general(
+            lhs, rhs, (((lhs_dim,), (rhs_dim,)), ((), ())), preferred_element_type=jnp.float32
+        )
+
+    query_spread = spread(query_here)
+    scores = contract(query_spread, key_all, 1, 1) * scale_factor
+    scores = jnp.where(valid_keys[None, :], scores, -jnp.inf)
+    row_max = jnp.max(scores, axis=1, keepdims=True)
+    row_total = jnp.sum(jnp.exp(scores - row_max), axis=1, keepdims=True)
     log_total = row_max + jnp.log(row_total)
     weights = jnp.exp(scores - log_total).astype(jnp.bfloat16)
-    attended = jnp.einsum("hqk,khd->qhd", weights, value_all, preferred_element_type=jnp.float32)
-    attended = attended.reshape(tokens, width_heads).astype(jnp.bfloat16)
+    attended = own_heads(contract(weights, value_all, 1, 0)).astype(jnp.bfloat16)
     hidden = jnp.dot(attended, out_proj, preferred_element_type=jnp.float32)
     masked = jnp.where(valid_rows[:, None], hidden, 0.0).astype(jnp.bfloat16)
 
@@ -197,29 +213,22 @@
     grad_attended = lax.dot_general(
         grad_hidden, out_proj, (((1,), (1,)), ((), ())), preferred_element_type=jnp.float32
     ).astype(jnp.bfloat16)
-    grad_heads = grad_attended.reshape(tokens, HEADS, HDIM)
-    attended_heads = attended.reshape(tokens, HEADS, HDIM)
     delta_rows = jnp.sum(
-        grad_heads.astype(jnp.float32) * attended_heads.astype(jnp.float32), axis=2
-    )
-    grad_weights = jnp.einsum(
-        "qhd,khd->hqk", grad_heads, value_all, preferred_element_type=jnp.float32
-    )
-    grad_logits = (weights.astype(jnp.float32) * (grad_weights - delta_rows.T[:, :, None])).astype(
+        (grad_attended.astype(jnp.float32) * attended.astype(jnp.float32)).reshape(
+            tokens, HEADS, HDIM
+        ),
+        axis=2,
+    )
+    grad_spread = spread(grad_attended)
+    grad_weights = contract(grad_spread, value_all, 1, 1)
+    grad_logits = (
+        weights.astype(jnp.float32) * (grad_weights - delta_rows.T.reshape(HEADS * tokens, 1))
+    ).astype(jnp.bfloat16)
+    grad_query = (own_heads(contract(grad_logits, key_all, 1, 0)) * scale_factor).astype(
         jnp.bfloat16
     )
-    grad_query = (
-        jnp.einsum("hqk,khd->qhd", grad_logits, key_all, preferred_element_type=jnp.float32)
-        * scale_factor
-    )
-    grad_query = grad_query.reshape(tokens, width_heads).astype(jnp.bfloat16)
-    grad_key_all = (
-        jnp.einsum("hqk,qhd->khd", grad_logits, query_heads, preferred_element_type=jnp.float32)
-        * scale_factor
-    )
-    grad_value_all = jnp.einsum(
-        "hqk,qhd->khd", weights, grad_heads, preferred_element_type=jnp.float32
-    )
+    grad_key_all = contract(grad_logits, query_spread, 0, 0) * scale_factor
+    grad_value_all = contract(weights, grad_spread, 0, 0)
     key_blocks = grad_key_all.reshape(span_blocks, tokens, width_heads)
     value_blocks = grad_value_all.reshape(span_blocks, tokens, width_heads)
     narrow = jnp.stack([key_blocks, value_blocks], axis=1).astype(jnp.bfloat16)

time: 179 us -> 155 us (0.87)
  the two profiles are of different devices: /device:TPU:2 before, /device:TPU:24 now
where the time goes in v11:
time: 155 us; the launch traced here: 154 us
  waiting for transfers between devices  54.5 us (35%)
  starting transfers between devices  43.5 us (28%)
  matrix products  18.3 us (12%)
  other arithmetic  18.1 us (12%)
  local copies, waits for them, and re-layouts  17.5 us (11%)
  between operations  2.1 us (1%)
    ppermute x8, starting transfers between devices, passed_along(): return lax.ppermute(block, axis, route)  30.6 us
    ppermute x8, waiting for transfers between devices, passed_along(): return lax.ppermute(block, axis, route)  29 us
    ppermute x8, waiting for transfers between devices, exchange(): return lax.ppermute(block, axis, [(i, i ^ bit) for i in range(count)])  20.6 us
    dot_general x6, matrix products, contract(): lax.dot_general(lhs, rhs, (((lhs_dim,), (rhs_dim,)), ((), ())), preferred...  13.1 us
    ppermute x1, starting transfers between devices, padded(): lax.ppermute(head, axis, [((i + 1) % count, i) for i in range(ends)])  5.93 us
    ppermute x8, starting transfers between devices, exchange(): return lax.ppermute(block, axis, [(i, i ^ bit) for i in range(count)])  4.86 us
    ppermute x1, waiting for transfers between devices, padded(): lax.ppermute(tail, axis, [(i, (i + 1) % count) for i in range(ends)])  4.8 us
    unnamed x39, local copies, waits for them, and re-layouts  3.34 us
  transfers between devices with their start and end apart: 18, of which 12 were waited for; matrix products, arithmetic and copies ran while one was open for 15% of the time, Pallas kernels for 0%

profile of v11, /device:TPU:24, one launch (start us, length us, event | category | flops | bytes accessed | tf_op | source)
XLA Modules:
  0.0 153.9 jit_solution(17787398152026693024)
XLA Ops:
  1.6 0.9 constant_dynamic-update-slice_fusion.1
  3.5 3.4 %collective-permute-start.2 = (bf16[288,512]{1,0:T(8,128)(2,1)S(1)}, bf16[288,512]{1,0:T(8,128)(2,1)S(1)}, u32[]{:S(2)}, u32[]{:S(2)}) collective-permute-start(bf16[288,512]{1,0:T(8,128)(2,1)S(1)} %get-tuple-element.25), channel_id=1, source_target_pairs={{2,0},{4,2},{6,4},{8,6},{10,8},{12,10},{14,12},{3,1},{5,3},{7,5},{... | collective-permute-start | bytes 884744 | tf_op jit(solution)/shard_map/ppermute | solution.py:17
  6.9 2.6 %collective-permute-start = (bf16[288,512]{1,0:T(8,128)(2,1)S(1)}, bf16[288,512]{1,0:T(8,128)(2,1)S(1)}, u32[]{:S(2)}, u32[]{:S(2)}) collective-permute-start(bf16[288,512]{1,0:T(8,128)(2,1)S(1)} %get-tuple-element.26), channel_id=1, source_target_pairs={{0,2},{2,4},{4,6},{6,8},{8,10},{10,12},{12,14},{1,3},{3,5},{5,7},{... | collective-permute-start | bytes 884744 | tf_op jit(solution)/shard_map/ppermute | solution.py:17
  10.2 10.4 %collective-permute-done.2 = bf16[288,512]{1,0:T(8,128)(2,1)S(1)} collective-permute-done((bf16[288,512]{1,0:T(8,128)(2,1)S(1)}, bf16[288,512]{1,0:T(8,128)(2,1)S(1)}, u32[]{:S(2)}, u32[]{:S(2)}) %collective-permute-start.2) | collective-permute-done | bytes 294944 | tf_op jit(solution)/shard_map/ppermute | solution.py:17
  20.8 1.3 collective-permute-start.1
  22.3 4.6 %collective-permute-start.3 = (bf16[2,2,128,512]{3,2,1,0:T(8,128)(2,1)S(1)}, bf16[2,2,128,512]{3,2,1,0:T(8,128)(2,1)S(1)}, u32[]{:S(2)}, u32[]{:S(2)}) collective-permute-start(bf16[2,2,128,512]{3,2,1,0:T(8,128)(2,1)S(1)} %get-tuple-element.23), channel_id=1, source_target_pairs={{4,0},{6,2},{8,4},{10,6},{12,8},{14,10},{5,1},{7,3},{9,5},{11,7},{... | collective-permute-start | bytes 1572872 | tf_op jit(solution)/shard_map/ppermute | solution.py:17
  26.8 8.6 %collective-permute-done.1 = bf16[2,2,128,512]{3,2,1,0:T(8,128)(2,1)S(1)} collective-permute-done((bf16[2,2,128,512]{3,2,1,0:T(8,128)(2,1)S(1)}, bf16[2,2,128,512]{3,2,1,0:T(8,128)(2,1)S(1)}, u32[]{:S(2)}, u32[]{:S(2)}) %collective-permute-start.1) | collective-permute-done | bytes 524320 | tf_op jit(solution)/shard_map/ppermute | solution.py:17
  35.6 1.3 collective-permute-done.3
  37.1 1.4 fusion
  38.5 0.9 exponential_reduce_fusion
  40.1 1.2 select_reduce_fusion.1
  41.8 5.9 %collective-permute-start.5 = (bf16[30,1024]{1,0:T(8,128)(2,1)S(1)}, bf16[30,1024]{1,0:T(8,128)(2,1)S(1)}, u32[]{:S(2)}, u32[]{:S(2)}) collective-permute-start(bf16[30,1024]{1,0:T(8,128)(2,1)S(1)} %get-tuple-element.22), channel_id=1, source_target_pairs={{2,0},{4,2},{6,4},{8,6},{10,8},{12,10},{14,12},{3,1},{5,3},{7,5},{... | collective-permute-start | bytes 184328 | tf_op jit(solution)/shard_map/ppermute | solution.py:30
  47.7 2.1 %collective-permute-start.4 = (bf16[30,1024]{1,0:T(8,128)(2,1)S(1)}, bf16[30,1024]{1,0:T(8,128)(2,1)S(1)}, u32[]{:S(2)}, u32[]{:S(2)}) collective-permute-start(bf16[30,1024]{1,0:T(8,128)(2,1)S(1)} %get-tuple-element.21), channel_id=1, source_target_pairs={{0,2},{2,4},{4,6},{6,8},{8,10},{10,12},{12,14},{1,3},{3,5},{5,7},{... | collective-permute-start | bytes 184328 | tf_op jit(solution)/shard_map/ppermute | solution.py:28
  50.0 4.8 %collective-permute-done.4 = bf16[30,1024]{1,0:T(8,128)(2,1)S(1)} collective-permute-done((bf16[30,1024]{1,0:T(8,128)(2,1)S(1)}, bf16[30,1024]{1,0:T(8,128)(2,1)S(1)}, u32[]{:S(2)}, u32[]{:S(2)}) %collective-permute-start.4) | collective-permute-done | bytes 61472 | tf_op jit(solution)/shard_map/ppermute | solution.py:28
  55.0 3.0 %multiply_convert_fusion.1 = bf16[158,1024]{1,0:T(8,128)(2,1)S(1)} fusion(bf16[188,1024]{1,0:T(8,128)(2,1)S(1)} %pad_maximum_fusion.5, bf16[15,1024]{1,0:T(8,128)(2,1)S(1)} %slice.428, bf16[128,1024]{1,0:T(8,128)(2,1)S(1)} %bitcast.136, bf16[15,1024]{1,0:T(8,128)(2,1)S(1)} %slice.426, bf16[128,1024]{1,0:T(8,128)(2,1)S(1)} %fusion.1, ...), kind=kLoop, calls=%fused_computation.23 | loop fusion | flops 18282496 | bytes 10543104 | tf_op jit(solution)/shard_map/convert_element_type | solution.py:177
  58.0 2.2 %add_convert_fusion = bf16[128,1024]{1,0:T(8,128)(2,1)S(1)} fusion(bf16[158,1024]{1,0:T(8,128)(2,1)S(1)} %multiply_convert_fusion.1, f32[1024]{0:T(1024)S(1)} %bitcast.209, f32[1024]{0:T(1024)S(1)} %bitcast.211, f32[1024]{0:T(1024)S(1)} %bitcast.153, f32[1024]{0:T(1024)S(1)} %bitcast.155, f32[1024]{0:T(1024)S(1)} %bitcast.157, f32[1024]{0:T(1024)S(1)} %bitcast.159, ...), kind=kLoop, calls=%fused_computation.49 | loop fusion | flops 12582912 | bytes 8777856 | tf_op jit(solution)/shard_map/convert_element_type | solution.py:195
  60.8 1.2 copy_dynamic-update-slice_fusion
  62.0 2.4 %fusion.3 = f32[1,31,1024]{2,0,1:T(1,128)S(1)} fusion(bf16[1,158,1024]{2,1,0:T(8,128)(2,1)S(1)} %slice_bitcast_fusion, bf16[128,1,1024]{2,0,1:T(8,128)(2,1)S(1)} %slice_bitcast_fusion.1), kind=kOutput, calls=%fused_computation.24 | convolution fusion | flops 8126464 | bytes 712704 | tf_op jit(solution)/shard_map/conv_general_dilated | solution.py:184
  65.1 1.6 %reshape.167 = f32[2,8,2,1024]{3,2,1,0:T(2,128)} reshape(f32[32,1024]{1,0:T(8,128)} %pad.13) | data formatting | bytes 262144 | tf_op jit(solution)/shard_map/reshape | solution.py:208
  66.7 0.9 copy_dynamic-update-slice_fusion.1
  68.6 2.3 %collective-permute-done.10 = bf16[1,8,34,1024]{3,1,2,0:T(8,128)(2,1)} collective-permute-done((bf16[1,8,34,1024]{3,1,2,0:T(8,128)(2,1)}, bf16[1,8,34,1024]{3,1,2,0:T(8,128)(2,1)}, u32[]{:S(2)}, u32[]{:S(2)}) %collective-permute-start.10) | collective-permute-done | bytes 557088 | tf_op jit(solution)/shard_map/ppermute | solution.py:68
  70.9 1.2 convert_add_fusion
  72.1 1.0 copy-done.1
  73.3 1.7 %collective-permute-start.11 = (bf16[4,34,1024]{2,0,1:T(4,128)(2,1)S(1)}, bf16[4,34,1024]{2,0,1:T(4,128)(2,1)S(1)}, u32[]{:S(2)}, u32[]{:S(2)}) collective-permute-start(bf16[4,34,1024]{2,0,1:T(4,128)(2,1)S(1)} %fusion.17), channel_id=1, source_target_pairs={{0,8},{2,10},{4,12},{6,14},{8,0},{10,2},{12,4},{14,6},{1,9},{3,11}... | collective-permute-start | bytes 835592 | tf_op jit(solution)/shard_map/ppermute | solution.py:68
  75.0 2.1 %convert_multiply_fusion = (f32[128,512]{1,0:T(8,128)}, bf16[128,512]{1,0:T(8,128)(2,1)S(1)}) fusion(bf16[128,512]{1,0:T(8,128)(2,1)} %copy-done.6, bf16[128,1024]{1,0:T(8,128)(2,1)S(1)} %add_convert_fusion, bf16[512,1024]{1,0:T(8,128)(2,1)S(1)} %copy-done), kind=kOutput, calls=%fused_computation.67 | convolution fusion | flops 134479872 | bytes 1835008 | tf_op jit(solution)/shard_map/dot_general | solution.py:213
  77.1 11.8 %collective-permute-done.11 = bf16[4,34,1024]{2,0,1:T(4,128)(2,1)S(1)} collective-permute-done((bf16[4,34,1024]{2,0,1:T(4,128)(2,1)S(1)}, bf16[4,34,1024]{2,0,1:T(4,128)(2,1)S(1)}, u32[]{:S(2)}, u32[]{:S(2)}) %collective-permute-start.11) | collective-permute-done | bytes 278560 | tf_op jit(solution)/shard_map/ppermute | solution.py:68
  89.9 1.0 broadcast_select_fusion
  91.0 1.8 %copy.55 = f32[128,512]{0,1:T(8,128)} copy(f32[128,512]{1,0:T(8,128)} %get-tuple-element.62) | data formatting | bytes 524288 | tf_op jit(solution)/shard_map/mul | solution.py:217
  92.7 1.0 bitcast_reduce_fusion
  93.7 1.6 %collective-permute-done.12 = bf16[2,34,1024]{2,0,1:T(2,128)(2,1)} collective-permute-done((bf16[2,34,1024]{2,0,1:T(2,128)(2,1)}, bf16[2,34,1024]{2,0,1:T(2,128)(2,1)}, u32[]{:S(2)}, u32[]{:S(2)}) %collective-permute-start.12) | collective-permute-done | bytes 139296 | tf_op jit(solution)/shard_map/ppermute | solution.py:68
  95.3 1.1 convert_add_fusion.1
  96.6 2.9 %multiply_convert_fusion = bf16[1024,896]{1,0:T(8,128)(2,1)S(1)} fusion(bf16[1024,896]{1,0:T(8,128)(2,1)S(1)} %copy-done.4, bf16[1024,512]{1,0:T(8,128)(2,1)} %bitcast.139, bf16[896,512]{1,0:T(8,128)(2,1)} %bitcast.145, f32[1024]{0:T(1024)S(1)} %bitcast.212), kind=kOutput, calls=%fused_computation | convolution fusion | flops 943194112 | bytes 5640192 | tf_op jit(solution)/shard_map/dot_general | solution.py:154
  99.5 2.3 %collective-permute-done.13 = bf16[1,34,1024]{2,0,1:T(2,128)(2,1)S(1)} collective-permute-done((bf16[1,34,1024]{2,0,1:T(2,128)(2,1)S(1)}, bf16[1,34,1024]{2,0,1:T(2,128)(2,1)S(1)}, u32[]{:S(2)}, u32[]{:S(2)}) %collective-permute-start.13) | collective-permute-done | bytes 69664 | tf_op jit(solution)/shard_map/ppermute | solution.py:68
  102.1 2.4 %fusion.35 = (bf16[896,512]{1,0:T(8,128)(2,1)S(1)}, f32[896,512]{1,0:T(8,128)}) fusion(bf16[1024,896]{1,0:T(8,128)(2,1)S(1)} %copy-done.4, bf16[1024,512]{1,0:T(8,128)(2,1)S(1)} %bitcast.140), kind=kOutput, calls=%fused_computation.109 | convolution fusion | flops 939982848 | bytes 5636096 | tf_op jit(solution)/shard_map/dot_general | solution.py:154
  104.5 2.6 %collective-permute-done.14 = bf16[1,34,1024]{2,0,1:T(2,128)(2,1)S(1)} collective-permute-done((bf16[1,34,1024]{2,0,1:T(2,128)(2,1)S(1)}, bf16[1,34,1024]{2,0,1:T(2,128)(2,1)S(1)}, u32[]{:S(2)}, u32[]{:S(2)}) %collective-permute-start.14) | collective-permute-done | bytes 69664 | tf_op jit(solution)/shard_map/ppermute | solution.py:68
  107.4 1.0 pad_maximum_fusion.9
  108.7 2.4 %fusion.36 = (bf16[896,512]{1,0:T(8,128)(2,1)S(1)}, f32[896,512]{1,0:T(8,128)}) fusion(bf16[1024,896]{1,0:T(8,128)(2,1)S(1)} %multiply_convert_fusion, bf16[1024,512]{1,0:T(8,128)(2,1)S(1)} %bitcast.138), kind=kOutput, calls=%fused_computation.110 | convolution fusion | flops 940441600 | bytes 5636096 | tf_op jit(solution)/shard_map/dot_general | solution.py:154
  112.1 3.8 %collective-permute-start.7 = (bf16[2,2,128,512]{3,2,1,0:T(8,128)(2,1)S(1)}, bf16[2,2,128,512]{3,2,1,0:T(8,128)(2,1)S(1)}, u32[]{:S(2)}, u32[]{:S(2)}) collective-permute-start(bf16[2,2,128,512]{3,2,1,0:T(8,128)(2,1)S(1)} %rev.3), channel_id=1, source_target_pairs={{4,0},{6,2},{8,4},{10,6},{12,8},{14,10},{5,1},{7,3},{9,5},{11,7},{... | collective-permute-start | bytes 1572872 | tf_op jit(solution)/shard_map/ppermute | solution.py:17
  115.8 1.5 collective-permute-start.6
  118.1 2.6 %collective-permute-start.16 = (bf16[4,34,1024]{2,0,1:T(4,128)(2,1)S(1)}, bf16[4,34,1024]{2,0,1:T(4,128)(2,1)S(1)}, u32[]{:S(2)}, u32[]{:S(2)}) collective-permute-start(bf16[4,34,1024]{2,0,1:T(4,128)(2,1)S(1)} %pad_maximum_fusion.8), channel_id=1, source_target_pairs={{0,8},{2,10},{4,12},{6,14},{8,0},{10,2},{12,4},{14,6},{1,9},{3,11}... | collective-permute-start | bytes 835592 | tf_op jit(solution)/shard_map/ppermute | solution.py:68
  120.7 2.8 %select_reduce_fusion = f32[128,512]{1,0:T(8,128)S(1)} fusion(bf16[8,128,896]{2,1,0:T(8,128)(2,1)} %bitcast.213, bf16[896,512,1]{1,0,2:T(8,128)(2,1)S(1)} %bitcast.143, pred[8,512]{1,0:T(8,128)(4,1)S(1)} %iota_compare_fusion), kind=kOutput, calls=%fused_computation.6 | convolution fusion | flops 940507136 | bytes 3018752 | tf_op jit(solution)/shard_map/dot_general | solution.py:154
  123.5 1.2 slice.607
  124.7 1.2 slice.608
  126.0 3.0 %collective-permute-done.6 = bf16[2,2,128,512]{3,2,1,0:T(8,128)(2,1)S(1)} collective-permute-done((bf16[2,2,128,512]{3,2,1,0:T(8,128)(2,1)}, bf16[2,2,128,512]{3,2,1,0:T(8,128)(2,1)S(1)}, u32[]{:S(2)}, u32[]{:S(2)}) %collective-permute-start.6) | collective-permute-done | bytes 524320 | tf_op jit(solution)/shard_map/ppermute | solution.py:17
  129.4 11.5 %collective-permute-start.9 = (bf16[2,128,512]{2,1,0:T(8,128)(2,1)S(1)}, bf16[2,128,512]{2,1,0:T(8,128)(2,1)S(1)}, u32[]{:S(2)}, u32[]{:S(2)}) collective-permute-start(bf16[2,128,512]{2,1,0:T(8,128)(2,1)S(1)} %get-tuple-element.10), channel_id=1, source_target_pairs={{2,0},{4,2},{6,4},{8,6},{10,8},{12,10},{14,12},{3,1},{5,3},{7,5},{... | collective-permute-start | bytes 786440 | tf_op jit(solution)/shard_map/ppermute | solution.py:17
  140.9 1.9 %collective-permute-start.8 = (bf16[2,128,512]{2,1,0:T(8,128)(2,1)S(1)}, bf16[2,128,512]{2,1,0:T(8,128)(2,1)S(1)}, u32[]{:S(2)}, u32[]{:S(2)}) collective-permute-start(bf16[2,128,512]{2,1,0:T(8,128)(2,1)S(1)} %get-tuple-element.9), channel_id=1, source_target_pairs={{0,2},{2,4},{4,6},{6,8},{8,10},{10,12},{12,14},{1,3},{3,5},{5,7},{... | collective-permute-start | bytes 786440 | tf_op jit(solution)/shard_map/ppermute | solution.py:17
  144.8 5.3 %collective-permute-done.8 = bf16[2,128,512]{2,1,0:T(8,128)(2,1)S(1)} collective-permute-done((bf16[2,128,512]{2,1,0:T(8,128)(2,1)S(1)}, bf16[2,128,512]{2,1,0:T(8,128)(2,1)S(1)}, u32[]{:S(2)}, u32[]{:S(2)}) %collective-permute-start.8) | collective-permute-done | bytes 262176 | tf_op jit(solution)/shard_map/ppermute | solution.py:17
  151.6 1.5 %copy.64 = bf16[2,8,32,1024]{3,2,1,0:T(8,128)(2,1)} copy(bf16[2,8,32,1024]{3,1,2,0:T(8,128)(2,1)S(1)} %fusion.2) | data formatting | bytes 2097152 | tf_op jit(solution)/shard_map/slice | solution.py:243
  (106 shorter events, 14.4 us)
Async XLA Ops:
  0.6 40.8 %copy-start = (bf16[512,1024]{1,0:T(8,128)(2,1)S(1)}, bf16[512,1024]{1,0:T(8,128)(2,1)}, u32[]{:S(2)}) copy-start(bf16[512,1024]{1,0:T(8,128)(2,1)} %param.11) | copy-start | bytes 3145732
  3.4 18.6 %copy-start.14 = (f32[31,1024]{1,0:T(8,128)S(1)}, f32[31,1024]{1,0:T(8,128)}, u32[]{:S(2)}) copy-start(f32[31,1024]{1,0:T(8,128)} %param.12) | copy-start | bytes 380932
  3.5 18.7 %copy-start.13 = (bf16[1,128,512]{2,1,0:T(8,128)(2,1)S(1)}, bf16[1,128,512]{2,1,0:T(8,128)(2,1)}, u32[]{:S(2)}) copy-start(bf16[1,128,512]{2,1,0:T(8,128)(2,1)} %param.7) | copy-start | bytes 393220
  3.5 17.1 %collective-permute-start.2 = (bf16[288,512]{1,0:T(8,128)(2,1)S(1)}, bf16[288,512]{1,0:T(8,128)(2,1)S(1)}, u32[]{:S(2)}, u32[]{:S(2)}) collective-permute-start(bf16[288,512]{1,0:T(8,128)(2,1)S(1)} %get-tuple-element.25), channel_id=1, source_target_pairs={{2,0},{4,2},{6,4},{8,6},{10,8},{12,10},{14,12},{3,1},{5,3},{7,5},{... | collective-permute-start | bytes 884744 | tf_op jit(solution)/shard_map/ppermute | solution.py:17
  6.9 13.7 %collective-permute-start = (bf16[288,512]{1,0:T(8,128)(2,1)S(1)}, bf16[288,512]{1,0:T(8,128)(2,1)S(1)}, u32[]{:S(2)}, u32[]{:S(2)}) collective-permute-start(bf16[288,512]{1,0:T(8,128)(2,1)S(1)} %get-tuple-element.26), channel_id=1, source_target_pairs={{0,2},{2,4},{4,6},{6,8},{8,10},{10,12},{12,14},{1,3},{3,5},{5,7},{... | collective-permute-start | bytes 884744 | tf_op jit(solution)/shard_map/ppermute | solution.py:17
  20.8 14.7 %collective-permute-start.1 = (bf16[2,2,128,512]{3,2,1,0:T(8,128)(2,1)S(1)}, bf16[2,2,128,512]{3,2,1,0:T(8,128)(2,1)S(1)}, u32[]{:S(2)}, u32[]{:S(2)}) collective-permute-start(bf16[2,2,128,512]{3,2,1,0:T(8,128)(2,1)S(1)} %get-tuple-element.24), channel_id=1, source_target_pairs={{0,4},{2,6},{4,8},{6,10},{8,12},{10,14},{1,5},{3,7},{5,9},{7,11},{... | collective-permute-start | bytes 1572872 | tf_op jit(solution)/shard_map/ppermute | solution.py:17
  22.2 14.8 %copy-start.7 = (bf16[8,128,512]{2,1,0:T(8,128)(2,1)}, bf16[8,128,512]{2,1,0:T(8,128)(2,1)S(1)}, u32[]{:S(2)}) copy-start(bf16[8,128,512]{2,1,0:T(8,128)(2,1)S(1)} %broadcast_select_fusion.1) | copy-start | bytes 3145732
  22.3 14.6 %collective-permute-start.3 = (bf16[2,2,128,512]{3,2,1,0:T(8,128)(2,1)S(1)}, bf16[2,2,128,512]{3,2,1,0:T(8,128)(2,1)S(1)}, u32[]{:S(2)}, u32[]{:S(2)}) collective-permute-start(bf16[2,2,128,512]{3,2,1,0:T(8,128)(2,1)S(1)} %get-tuple-element.23), channel_id=1, source_target_pairs={{4,0},{6,2},{8,4},{10,6},{12,8},{14,10},{5,1},{7,3},{9,5},{11,7},{... | collective-permute-start | bytes 1572872 | tf_op jit(solution)/shard_map/ppermute | solution.py:17
  37.0 1.4 copy-start.10
  37.1 3.1 %copy-start.12 = (bf16[7,1,128,512]{3,2,1,0:T(8,128)(2,1)}, bf16[7,1,128,512]{3,2,1,0:T(8,128)(2,1)S(1)}, u32[]{:S(2)}) copy-start(bf16[7,1,128,512]{3,2,1,0:T(8,128)(2,1)S(1)} %get-tuple-element.7) | copy-start | bytes 2752516
  40.1 1.3 copy-start.3
  41.4 18.9 %copy-start.6 = (bf16[128,512]{1,0:T(8,128)(2,1)}, bf16[128,512]{1,0:T(8,128)(2,1)S(1)}, u32[]{:S(2)}) copy-start(bf16[128,512]{1,0:T(8,128)(2,1)S(1)} %select_reduce_fusion.1) | copy-start | bytes 393220
  41.4 13.5 %copy-start.5 = (bf16[1,128,1024]{2,1,0:T(8,128)(2,1)S(1)}, bf16[1,128,1024]{2,1,0:T(8,128)(2,1)}, u32[]{:S(2)}) copy-start(bf16[1,128,1024]{2,1,0:T(8,128)(2,1)} %param.10) | copy-start | bytes 786436
  41.8 8.2 %collective-permute-start.5 = (bf16[30,1024]{1,0:T(8,128)(2,1)S(1)}, bf16[30,1024]{1,0:T(8,128)(2,1)S(1)}, u32[]{:S(2)}, u32[]{:S(2)}) collective-permute-start(bf16[30,1024]{1,0:T(8,128)(2,1)S(1)} %get-tuple-element.22), channel_id=1, source_target_pairs={{2,0},{4,2},{6,4},{8,6},{10,8},{12,10},{14,12},{3,1},{5,3},{7,5},{... | collective-permute-start | bytes 184328 | tf_op jit(solution)/shard_map/ppermute | solution.py:30
  47.7 7.1 %collective-permute-start.4 = (bf16[30,1024]{1,0:T(8,128)(2,1)S(1)}, bf16[30,1024]{1,0:T(8,128)(2,1)S(1)}, u32[]{:S(2)}, u32[]{:S(2)}) collective-permute-start(bf16[30,1024]{1,0:T(8,128)(2,1)S(1)} %get-tuple-element.21), channel_id=1, source_target_pairs={{0,2},{2,4},{4,6},{6,8},{8,10},{10,12},{12,14},{1,3},{3,5},{5,7},{... | collective-permute-start | bytes 184328 | tf_op jit(solution)/shard_map/ppermute | solution.py:28
  68.6 2.3 %collective-permute-start.10 = (bf16[1,8,34,1024]{3,1,2,0:T(8,128)(2,1)}, bf16[1,8,34,1024]{3,1,2,0:T(8,128)(2,1)}, u32[]{:S(2)}, u32[]{:S(2)}) collective-permute-start(bf16[1,8,34,1024]{3,1,2,0:T(8,128)(2,1)} %dynamic-slice_convert_fusion), channel_id=1, source_target_pairs={{0,1},{1,0},{2,3},{3,2},{4,5},{5,4},{6,7},{7,6},{8,9},{9,8},{10,11... | collective-permute-start | bytes 1671176 | tf_op jit(solution)/shard_map/ppermute | solution.py:68
  72.1 1.0 copy-start.1
  73.3 15.6 %copy-start.2 = (f32[1,8,34,1024]{3,1,2,0:T(8,128)S(1)}, f32[1,8,34,1024]{3,1,2,0:T(8,128)}, u32[]{:S(2)}) copy-start(f32[1,8,34,1024]{3,1,2,0:T(8,128)} %copy-done.1) | copy-start | bytes 3342340
  73.3 15.6 %collective-permute-start.11 = (bf16[4,34,1024]{2,0,1:T(4,128)(2,1)S(1)}, bf16[4,34,1024]{2,0,1:T(4,128)(2,1)S(1)}, u32[]{:S(2)}, u32[]{:S(2)}) collective-permute-start(bf16[4,34,1024]{2,0,1:T(4,128)(2,1)S(1)} %fusion.17), channel_id=1, source_target_pairs={{0,8},{2,10},{4,12},{6,14},{8,0},{10,2},{12,4},{14,6},{1,9},{3,11}... | collective-permute-start | bytes 835592 | tf_op jit(solution)/shard_map/ppermute | solution.py:68
  89.1 7.5 %copy-start.4 = (bf16[1024,896]{1,0:T(8,128)(2,1)S(1)}, bf16[1024,896]{1,0:T(8,128)(2,1)}, u32[]{:S(2)}) copy-start(bf16[1024,896]{1,0:T(8,128)(2,1)} %copy-done.3) | copy-start | bytes 5505028
  89.9 5.4 %collective-permute-start.12 = (bf16[2,34,1024]{2,0,1:T(2,128)(2,1)}, bf16[2,34,1024]{2,0,1:T(2,128)(2,1)}, u32[]{:S(2)}, u32[]{:S(2)}) collective-permute-start(bf16[2,34,1024]{2,0,1:T(2,128)(2,1)} %dynamic-slice_convert_fusion.2), channel_id=1, source_target_pairs={{0,4},{2,6},{4,0},{6,2},{8,12},{10,14},{12,8},{14,10},{1,5},{3,7},... | collective-permute-start | bytes 417800 | tf_op jit(solution)/shard_map/ppermute | solution.py:68
  96.5 5.3 %collective-permute-start.13 = (bf16[1,34,1024]{2,0,1:T(2,128)(2,1)S(1)}, bf16[1,34,1024]{2,0,1:T(2,128)(2,1)S(1)}, u32[]{:S(2)}, u32[]{:S(2)}) collective-permute-start(bf16[1,34,1024]{2,0,1:T(2,128)(2,1)S(1)} %dynamic-slice_convert_fusion.3), channel_id=1, source_target_pairs={{0,2},{2,0},{4,6},{6,4},{8,10},{10,8},{12,14},{14,12},{1,3},{3,1},... | collective-permute-start | bytes 208904 | tf_op jit(solution)/shard_map/ppermute | solution.py:68
  96.6 5.5 %copy-start.9 = (bf16[8,128,512]{2,1,0:T(8,128)(2,1)S(1)}, bf16[8,128,512]{2,1,0:T(8,128)(2,1)}, u32[]{:S(2)}) copy-start(bf16[8,128,512]{2,1,0:T(8,128)(2,1)} %broadcast_select_fusion) | copy-start | bytes 3145732
  99.5 9.2 %copy-start.15 = (bf16[1024,896]{1,0:T(8,128)(2,1)}, bf16[1024,896]{1,0:T(8,128)(2,1)S(1)}, u32[]{:S(2)}) copy-start(bf16[1024,896]{1,0:T(8,128)(2,1)S(1)} %multiply_convert_fusion) | copy-start | bytes 5505028
  102.0 6.7 %copy-start.8 = (bf16[8,128,512]{2,1,0:T(8,128)(2,1)S(1)}, bf16[8,128,512]{2,1,0:T(8,128)(2,1)}, u32[]{:S(2)}) copy-start(bf16[8,128,512]{2,1,0:T(8,128)(2,1)} %copy-done.7) | copy-start | bytes 3145732
  102.0 5.1 %collective-permute-start.14 = (bf16[1,34,1024]{2,0,1:T(2,128)(2,1)S(1)}, bf16[1,34,1024]{2,0,1:T(2,128)(2,1)S(1)}, u32[]{:S(2)}, u32[]{:S(2)}) collective-permute-start(bf16[1,34,1024]{2,0,1:T(2,128)(2,1)S(1)} %add_convert_fusion.1), channel_id=1, source_target_pairs={{0,2},{2,0},{4,6},{6,4},{8,10},{10,8},{12,14},{14,12},{1,3},{3,1},... | collective-permute-start | bytes 208904 | tf_op jit(solution)/shard_map/ppermute | solution.py:68
  108.4 9.0 %collective-permute-start.15 = (bf16[2,34,1024]{2,0,1:T(2,128)(2,1)}, bf16[2,34,1024]{2,0,1:T(2,128)(2,1)S(1)}, u32[]{:S(2)}, u32[]{:S(2)}) collective-permute-start(bf16[2,34,1024]{2,0,1:T(2,128)(2,1)} %pad_maximum_fusion.9), channel_id=1, source_target_pairs={{0,4},{2,6},{4,0},{6,2},{8,12},{10,14},{12,8},{14,10},{1,5},{3,7},... | collective-permute-start | bytes 417800 | tf_op jit(solution)/shard_map/ppermute | solution.py:68
  112.0 8.7 %copy-start.11 = (bf16[7,1,128,512]{3,2,1,0:T(8,128)(2,1)S(1)}, bf16[7,1,128,512]{3,2,1,0:T(8,128)(2,1)}, u32[]{:S(2)}) copy-start(bf16[7,1,128,512]{3,2,1,0:T(8,128)(2,1)} %copy-done.10) | copy-start | bytes 2752516
  112.1 13.8 %collective-permute-start.7 = (bf16[2,2,128,512]{3,2,1,0:T(8,128)(2,1)S(1)}, bf16[2,2,128,512]{3,2,1,0:T(8,128)(2,1)S(1)}, u32[]{:S(2)}, u32[]{:S(2)}) collective-permute-start(bf16[2,2,128,512]{3,2,1,0:T(8,128)(2,1)S(1)} %rev.3), channel_id=1, source_target_pairs={{4,0},{6,2},{8,4},{10,6},{12,8},{14,10},{5,1},{7,3},{9,5},{11,7},{... | collective-permute-start | bytes 1572872 | tf_op jit(solution)/shard_map/ppermute | solution.py:17
  115.8 13.2 %collective-permute-start.6 = (bf16[2,2,128,512]{3,2,1,0:T(8,128)(2,1)}, bf16[2,2,128,512]{3,2,1,0:T(8,128)(2,1)S(1)}, u32[]{:S(2)}, u32[]{:S(2)}) collective-permute-start(bf16[2,2,128,512]{3,2,1,0:T(8,128)(2,1)} %get-tuple-element.5), channel_id=1, source_target_pairs={{0,4},{2,6},{4,8},{6,10},{8,12},{10,14},{1,5},{3,7},{5,9},{7,11},{... | collective-permute-start | bytes 1572872 | tf_op jit(solution)/shard_map/ppermute | solution.py:17
  118.1 24.7 %collective-permute-start.16 = (bf16[4,34,1024]{2,0,1:T(4,128)(2,1)S(1)}, bf16[4,34,1024]{2,0,1:T(4,128)(2,1)S(1)}, u32[]{:S(2)}, u32[]{:S(2)}) collective-permute-start(bf16[4,34,1024]{2,0,1:T(4,128)(2,1)S(1)} %pad_maximum_fusion.8), channel_id=1, source_target_pairs={{0,8},{2,10},{4,12},{6,14},{8,0},{10,2},{12,4},{14,6},{1,9},{3,11}... | collective-permute-start | bytes 835592 | tf_op jit(solution)/shard_map/ppermute | solution.py:68
  129.4 15.4 %collective-permute-start.9 = (bf16[2,128,512]{2,1,0:T(8,128)(2,1)S(1)}, bf16[2,128,512]{2,1,0:T(8,128)(2,1)S(1)}, u32[]{:S(2)}, u32[]{:S(2)}) collective-permute-start(bf16[2,128,512]{2,1,0:T(8,128)(2,1)S(1)} %get-tuple-element.10), channel_id=1, source_target_pairs={{2,0},{4,2},{6,4},{8,6},{10,8},{12,10},{14,12},{3,1},{5,3},{7,5},{... | collective-permute-start | bytes 786440 | tf_op jit(solution)/shard_map/ppermute | solution.py:17
  140.9 9.2 %collective-permute-start.8 = (bf16[2,128,512]{2,1,0:T(8,128)(2,1)S(1)}, bf16[2,128,512]{2,1,0:T(8,128)(2,1)S(1)}, u32[]{:S(2)}, u32[]{:S(2)}) collective-permute-start(bf16[2,128,512]{2,1,0:T(8,128)(2,1)S(1)} %get-tuple-element.9), channel_id=1, source_target_pairs={{0,2},{2,4},{4,6},{6,8},{8,10},{10,12},{12,14},{1,3},{3,5},{5,7},{... | collective-permute-start | bytes 786440 | tf_op jit(solution)/shard_map/ppermute | solution.py:17
  143.6 7.4 %collective-permute-start.17 = (bf16[1,8,34,1024]{3,1,2,0:T(8,128)(2,1)S(1)}, bf16[1,8,34,1024]{3,1,2,0:T(8,128)(2,1)S(1)}, u32[]{:S(2)}, u32[]{:S(2)}) collective-permute-start(bf16[1,8,34,1024]{3,1,2,0:T(8,128)(2,1)S(1)} %maximum_bitcast_fusion), channel_id=1, source_target_pairs={{0,1},{1,0},{2,3},{3,2},{4,5},{5,4},{6,7},{7,6},{8,9},{9,8},{10,11... | collective-permute-start | bytes 1671176 | tf_op jit(solution)/shard_map/ppermute | solution.py:68

commit v12 on v11

--- a/solution.py
+++ b/solution.py
@@ -70,29 +70,28 @@
 
 def halving(acc, axis):
     here = lax.axis_index(axis)
-    bit = lax.axis_size(axis) // 2
-    while bit >= 1:
+    count = lax.axis_size(axis)
+    levels = count.bit_length() - 1
+    for level in range(levels):
         half = acc.shape[0] // 2
-        mine = (here // bit) % 2
+        mine = (here >> level) % 2
         keep = lax.dynamic_slice_in_dim(acc, mine * half, half, 0)
         send = lax.dynamic_slice_in_dim(acc, (1 - mine) * half, half, 0)
-        acc = keep + exchange(send.astype(jnp.bfloat16), axis, bit).astype(jnp.float32)
-        bit //= 2
+        acc = keep + exchange(send.astype(jnp.bfloat16), axis, 1 << level).astype(jnp.float32)
     return acc[0]
 
 
 def doubling(acc, axis):
     here = lax.axis_index(axis)
     count = lax.axis_size(axis)
+    levels = count.bit_length() - 1
     acc = acc[None]
-    bit = 1
-    while bit < count:
-        theirs = exchange(acc, axis, bit)
-        first = (here // bit) % 2 == 0
+    for level in range(levels - 1, -1, -1):
+        theirs = exchange(acc, axis, 1 << level)
+        first = (here >> level) % 2 == 0
         acc = jnp.concatenate(
             [jnp.where(first, acc, theirs), jnp.where(first, theirs, acc)], axis=0
         )
-        bit *= 2
     return acc
 
 

time: 155 us -> 151 us (0.974)
  the two profiles are of different devices: /device:TPU:24 before, /device:TPU:2 now
where the time goes in v12:
time: 151 us; the launch traced here: 150 us
  waiting for transfers between devices  55.3 us (37%)
  starting transfers between devices  38.7 us (26%)
  matrix products  18.4 us (12%)
  other arithmetic  18.1 us (12%)
  local copies, waits for them, and re-layouts  17.5 us (12%)
  between operations  2.13 us (1%)
    ppermute x8, waiting for transfers between devices, passed_along(): return lax.ppermute(block, axis, route)  35.4 us
    ppermute x8, starting transfers between devices, passed_along(): return lax.ppermute(block, axis, route)  25.1 us
    ppermute x8, waiting for transfers between devices, exchange(): return lax.ppermute(block, axis, [(i, i ^ bit) for i in range(count)])  18.4 us
    dot_general x6, matrix products, contract(): lax.dot_general(lhs, rhs, (((lhs_dim,), (rhs_dim,)), ((), ())), preferred...  13.1 us
    ppermute x8, starting transfers between devices, exchange(): return lax.ppermute(block, axis, [(i, i ^ bit) for i in range(count)])  6.63 us
    ppermute x1, starting transfers between devices, padded(): lax.ppermute(tail, axis, [(i, (i + 1) % count) for i in range(ends)])  5 us
    unnamed x39, local copies, waits for them, and re-layouts  3.33 us
    convert_element_type x1, other arithmetic, on_device(): grad_conv = (cot_wide.astype(jnp.float32) * (sigmoid_c + conv_out * sigmo...  3.04 us
  transfers between devices with their start and end apart: 18, of which 13 were waited for; matrix products, arithmetic and copies ran while one was open for 16% of the time, Pallas kernels for 0%

profile of v12, /device:TPU:2, one launch (start us, length us, event | category | flops | bytes accessed | tf_op | source)
XLA Modules:
  0.0 150.1 jit_solution(3240033383265020960)
XLA Ops:
  3.5 2.1 %collective-permute-start.2 = (bf16[288,512]{1,0:T(8,128)(2,1)S(1)}, bf16[288,512]{1,0:T(8,128)(2,1)S(1)}, u32[]{:S(2)}, u32[]{:S(2)}) collective-permute-start(bf16[288,512]{1,0:T(8,128)(2,1)S(1)} %get-tuple-element.25), channel_id=1, source_target_pairs={{2,0},{4,2},{6,4},{8,6},{10,8},{12,10},{14,12},{3,1},{5,3},{7,5},{... | collective-permute-start | bytes 884744 | tf_op jit(solution)/shard_map/ppermute | solution.py:17
  5.6 4.8 %collective-permute-start = (bf16[288,512]{1,0:T(8,128)(2,1)S(1)}, bf16[288,512]{1,0:T(8,128)(2,1)S(1)}, u32[]{:S(2)}, u32[]{:S(2)}) collective-permute-start(bf16[288,512]{1,0:T(8,128)(2,1)S(1)} %get-tuple-element.26), channel_id=1, source_target_pairs={{0,2},{2,4},{4,6},{6,8},{8,10},{10,12},{12,14},{1,3},{3,5},{5,7},{... | collective-permute-start | bytes 884744 | tf_op jit(solution)/shard_map/ppermute | solution.py:17
  11.1 4.2 %collective-permute-done.2 = bf16[288,512]{1,0:T(8,128)(2,1)S(1)} collective-permute-done((bf16[288,512]{1,0:T(8,128)(2,1)S(1)}, bf16[288,512]{1,0:T(8,128)(2,1)S(1)}, u32[]{:S(2)}, u32[]{:S(2)}) %collective-permute-start.2) | collective-permute-done | bytes 294944 | tf_op jit(solution)/shard_map/ppermute | solution.py:17
  15.3 6.2 %collective-permute-done = bf16[288,512]{1,0:T(8,128)(2,1)S(1)} collective-permute-done((bf16[288,512]{1,0:T(8,128)(2,1)S(1)}, bf16[288,512]{1,0:T(8,128)(2,1)S(1)}, u32[]{:S(2)}, u32[]{:S(2)}) %collective-permute-start) | collective-permute-done | bytes 294944 | tf_op jit(solution)/shard_map/ppermute | solution.py:17
  21.6 3.5 %collective-permute-start.1 = (bf16[2,2,128,512]{3,2,1,0:T(8,128)(2,1)S(1)}, bf16[2,2,128,512]{3,2,1,0:T(8,128)(2,1)S(1)}, u32[]{:S(2)}, u32[]{:S(2)}) collective-permute-start(bf16[2,2,128,512]{3,2,1,0:T(8,128)(2,1)S(1)} %get-tuple-element.24), channel_id=1, source_target_pairs={{0,4},{2,6},{4,8},{6,10},{8,12},{10,14},{1,5},{3,7},{5,9},{7,11},{... | collective-permute-start | bytes 1572872 | tf_op jit(solution)/shard_map/ppermute | solution.py:17
  25.3 1.3 collective-permute-start.3
  26.6 9.8 %collective-permute-done.1 = bf16[2,2,128,512]{3,2,1,0:T(8,128)(2,1)S(1)} collective-permute-done((bf16[2,2,128,512]{3,2,1,0:T(8,128)(2,1)S(1)}, bf16[2,2,128,512]{3,2,1,0:T(8,128)(2,1)S(1)}, u32[]{:S(2)}, u32[]{:S(2)}) %collective-permute-start.1) | collective-permute-done | bytes 524320 | tf_op jit(solution)/shard_map/ppermute | solution.py:17
  36.6 4.2 %collective-permute-done.3 = bf16[2,2,128,512]{3,2,1,0:T(8,128)(2,1)S(1)} collective-permute-done((bf16[2,2,128,512]{3,2,1,0:T(8,128)(2,1)S(1)}, bf16[2,2,128,512]{3,2,1,0:T(8,128)(2,1)S(1)}, u32[]{:S(2)}, u32[]{:S(2)}) %collective-permute-start.3) | collective-permute-done | bytes 524320 | tf_op jit(solution)/shard_map/ppermute | solution.py:17
  41.0 1.4 fusion
  44.1 1.2 select_reduce_fusion.1
  45.7 1.9 %collective-permute-start.5 = (bf16[30,1024]{1,0:T(8,128)(2,1)S(1)}, bf16[30,1024]{1,0:T(8,128)(2,1)S(1)}, u32[]{:S(2)}, u32[]{:S(2)}) collective-permute-start(bf16[30,1024]{1,0:T(8,128)(2,1)S(1)} %get-tuple-element.22), channel_id=1, source_target_pairs={{2,0},{4,2},{6,4},{8,6},{10,8},{12,10},{14,12},{3,1},{5,3},{7,5},{... | collective-permute-start | bytes 184328 | tf_op jit(solution)/shard_map/ppermute | solution.py:30
  47.7 5.0 %collective-permute-start.4 = (bf16[30,1024]{1,0:T(8,128)(2,1)S(1)}, bf16[30,1024]{1,0:T(8,128)(2,1)S(1)}, u32[]{:S(2)}, u32[]{:S(2)}) collective-permute-start(bf16[30,1024]{1,0:T(8,128)(2,1)S(1)} %get-tuple-element.21), channel_id=1, source_target_pairs={{0,2},{2,4},{4,6},{6,8},{8,10},{10,12},{12,14},{1,3},{3,5},{5,7},{... | collective-permute-start | bytes 184328 | tf_op jit(solution)/shard_map/ppermute | solution.py:28
  52.8 1.6 %collective-permute-done.4 = bf16[30,1024]{1,0:T(8,128)(2,1)S(1)} collective-permute-done((bf16[30,1024]{1,0:T(8,128)(2,1)S(1)}, bf16[30,1024]{1,0:T(8,128)(2,1)S(1)}, u32[]{:S(2)}, u32[]{:S(2)}) %collective-permute-start.4) | collective-permute-done | bytes 61472 | tf_op jit(solution)/shard_map/ppermute | solution.py:28
  54.6 3.0 %multiply_convert_fusion.1 = bf16[158,1024]{1,0:T(8,128)(2,1)S(1)} fusion(bf16[188,1024]{1,0:T(8,128)(2,1)S(1)} %pad_maximum_fusion.5, bf16[15,1024]{1,0:T(8,128)(2,1)S(1)} %slice.428, bf16[128,1024]{1,0:T(8,128)(2,1)S(1)} %bitcast.136, bf16[15,1024]{1,0:T(8,128)(2,1)S(1)} %slice.426, bf16[128,1024]{1,0:T(8,128)(2,1)S(1)} %fusion.1, ...), kind=kLoop, calls=%fused_computation.23 | loop fusion | flops 18282496 | bytes 10543104 | tf_op jit(solution)/shard_map/convert_element_type | solution.py:176
  57.6 2.2 %add_convert_fusion = bf16[128,1024]{1,0:T(8,128)(2,1)S(1)} fusion(bf16[158,1024]{1,0:T(8,128)(2,1)S(1)} %multiply_convert_fusion.1, f32[1024]{0:T(1024)S(1)} %bitcast.209, f32[1024]{0:T(1024)S(1)} %bitcast.211, f32[1024]{0:T(1024)S(1)} %bitcast.153, f32[1024]{0:T(1024)S(1)} %bitcast.155, f32[1024]{0:T(1024)S(1)} %bitcast.157, f32[1024]{0:T(1024)S(1)} %bitcast.159, ...), kind=kLoop, calls=%fused_computation.49 | loop fusion | flops 12582912 | bytes 8777856 | tf_op jit(solution)/shard_map/convert_element_type | solution.py:194
  60.4 1.2 copy_dynamic-update-slice_fusion
  61.6 2.4 %fusion.3 = f32[1,31,1024]{2,0,1:T(1,128)S(1)} fusion(bf16[1,158,1024]{2,1,0:T(8,128)(2,1)S(1)} %slice_bitcast_fusion, bf16[128,1,1024]{2,0,1:T(8,128)(2,1)S(1)} %slice_bitcast_fusion.1), kind=kOutput, calls=%fused_computation.24 | convolution fusion | flops 8126464 | bytes 712704 | tf_op jit(solution)/shard_map/conv_general_dilated | solution.py:183
  64.7 1.6 %reshape.167 = f32[2,8,2,1024]{3,2,1,0:T(2,128)} reshape(f32[32,1024]{1,0:T(8,128)} %pad.13) | data formatting | bytes 262144 | tf_op jit(solution)/shard_map/reshape | solution.py:207
  68.2 2.3 %collective-permute-done.10 = bf16[1,8,34,1024]{3,1,2,0:T(8,128)(2,1)} collective-permute-done((bf16[1,8,34,1024]{3,1,2,0:T(8,128)(2,1)}, bf16[1,8,34,1024]{3,1,2,0:T(8,128)(2,1)}, u32[]{:S(2)}, u32[]{:S(2)}) %collective-permute-start.10) | collective-permute-done | bytes 557088 | tf_op jit(solution)/shard_map/ppermute | solution.py:68
  70.5 1.2 convert_add_fusion
  71.8 1.0 copy-done.1
  73.0 2.2 %convert_multiply_fusion = (f32[128,512]{1,0:T(8,128)}, bf16[128,512]{1,0:T(8,128)(2,1)S(1)}) fusion(bf16[128,512]{1,0:T(8,128)(2,1)} %copy-done.6, bf16[128,1024]{1,0:T(8,128)(2,1)S(1)} %add_convert_fusion, bf16[512,1024]{1,0:T(8,128)(2,1)S(1)} %copy-done), kind=kOutput, calls=%fused_computation.67 | convolution fusion | flops 134479872 | bytes 1835008 | tf_op jit(solution)/shard_map/dot_general | solution.py:212
  75.2 6.5 %collective-permute-done.11 = bf16[4,34,1024]{2,0,1:T(4,128)(2,1)S(1)} collective-permute-done((bf16[4,34,1024]{2,0,1:T(4,128)(2,1)S(1)}, bf16[4,34,1024]{2,0,1:T(4,128)(2,1)S(1)}, u32[]{:S(2)}, u32[]{:S(2)}) %collective-permute-start.11) | collective-permute-done | bytes 278560 | tf_op jit(solution)/shard_map/ppermute | solution.py:68
  82.6 2.1 %collective-permute-start.12 = (bf16[2,34,1024]{2,0,1:T(2,128)(2,1)}, bf16[2,34,1024]{2,0,1:T(2,128)(2,1)}, u32[]{:S(2)}, u32[]{:S(2)}) collective-permute-start(bf16[2,34,1024]{2,0,1:T(2,128)(2,1)} %dynamic-slice_convert_fusion.2), channel_id=1, source_target_pairs={{0,4},{2,6},{4,0},{6,2},{8,12},{10,14},{12,8},{14,10},{1,5},{3,7},... | collective-permute-start | bytes 417800 | tf_op jit(solution)/shard_map/ppermute | solution.py:68
  84.7 1.0 broadcast_select_fusion
  85.8 1.8 %copy.55 = f32[128,512]{0,1:T(8,128)} copy(f32[128,512]{1,0:T(8,128)} %get-tuple-element.62) | data formatting | bytes 524288 | tf_op jit(solution)/shard_map/mul | solution.py:216
  87.5 1.0 bitcast_reduce_fusion
  88.5 1.1 convert_add_fusion.1
  89.8 2.7 %collective-permute-start.13 = (bf16[1,34,1024]{2,0,1:T(2,128)(2,1)S(1)}, bf16[1,34,1024]{2,0,1:T(2,128)(2,1)S(1)}, u32[]{:S(2)}, u32[]{:S(2)}) collective-permute-start(bf16[1,34,1024]{2,0,1:T(2,128)(2,1)S(1)} %dynamic-slice_convert_fusion.3), channel_id=1, source_target_pairs={{0,8},{2,10},{4,12},{6,14},{8,0},{10,2},{12,4},{14,6},{1,9},{3,11}... | collective-permute-start | bytes 208904 | tf_op jit(solution)/shard_map/ppermute | solution.py:68
  92.5 2.9 %multiply_convert_fusion = bf16[1024,896]{1,0:T(8,128)(2,1)S(1)} fusion(bf16[1024,896]{1,0:T(8,128)(2,1)S(1)} %copy-done.4, bf16[1024,512]{1,0:T(8,128)(2,1)} %bitcast.139, bf16[896,512]{1,0:T(8,128)(2,1)} %bitcast.145, f32[1024]{0:T(1024)S(1)} %bitcast.212), kind=kOutput, calls=%fused_computation | convolution fusion | flops 943194112 | bytes 5640192 | tf_op jit(solution)/shard_map/dot_general | solution.py:153
  95.3 3.2 %collective-permute-done.13 = bf16[1,34,1024]{2,0,1:T(2,128)(2,1)S(1)} collective-permute-done((bf16[1,34,1024]{2,0,1:T(2,128)(2,1)S(1)}, bf16[1,34,1024]{2,0,1:T(2,128)(2,1)S(1)}, u32[]{:S(2)}, u32[]{:S(2)}) %collective-permute-start.13) | collective-permute-done | bytes 69664 | tf_op jit(solution)/shard_map/ppermute | solution.py:68
  98.9 2.4 %fusion.35 = (bf16[896,512]{1,0:T(8,128)(2,1)S(1)}, f32[896,512]{1,0:T(8,128)}) fusion(bf16[1024,896]{1,0:T(8,128)(2,1)S(1)} %copy-done.4, bf16[1024,512]{1,0:T(8,128)(2,1)S(1)} %bitcast.140), kind=kOutput, calls=%fused_computation.109 | convolution fusion | flops 939982848 | bytes 5636096 | tf_op jit(solution)/shard_map/dot_general | solution.py:153
  101.3 6.4 %collective-permute-done.14 = bf16[1,34,1024]{2,0,1:T(2,128)(2,1)S(1)} collective-permute-done((bf16[1,34,1024]{2,0,1:T(2,128)(2,1)S(1)}, bf16[1,34,1024]{2,0,1:T(2,128)(2,1)S(1)}, u32[]{:S(2)}, u32[]{:S(2)}) %collective-permute-start.14) | collective-permute-done | bytes 69664 | tf_op jit(solution)/shard_map/ppermute | solution.py:68
  107.9 1.0 pad_maximum_fusion.9
  108.9 2.4 %fusion.36 = (bf16[896,512]{1,0:T(8,128)(2,1)S(1)}, f32[896,512]{1,0:T(8,128)}) fusion(bf16[1024,896]{1,0:T(8,128)(2,1)S(1)} %multiply_convert_fusion, bf16[1024,512]{1,0:T(8,128)(2,1)S(1)} %bitcast.138), kind=kOutput, calls=%fused_computation.110 | convolution fusion | flops 940441600 | bytes 5636096 | tf_op jit(solution)/shard_map/dot_general | solution.py:153
  112.3 1.4 collective-permute-start.7
  113.7 4.8 %collective-permute-start.6 = (bf16[2,2,128,512]{3,2,1,0:T(8,128)(2,1)}, bf16[2,2,128,512]{3,2,1,0:T(8,128)(2,1)S(1)}, u32[]{:S(2)}, u32[]{:S(2)}) collective-permute-start(bf16[2,2,128,512]{3,2,1,0:T(8,128)(2,1)} %get-tuple-element.5), channel_id=1, source_target_pairs={{0,4},{2,6},{4,8},{6,10},{8,12},{10,14},{1,5},{3,7},{5,9},{7,11},{... | collective-permute-start | bytes 1572872 | tf_op jit(solution)/shard_map/ppermute | solution.py:17
  119.3 1.6 %collective-permute-start.16 = (bf16[4,34,1024]{2,0,1:T(4,128)(2,1)S(1)}, bf16[4,34,1024]{2,0,1:T(4,128)(2,1)S(1)}, u32[]{:S(2)}, u32[]{:S(2)}) collective-permute-start(bf16[4,34,1024]{2,0,1:T(4,128)(2,1)S(1)} %pad_maximum_fusion.8), channel_id=1, source_target_pairs={{0,2},{2,0},{4,6},{6,4},{8,10},{10,8},{12,14},{14,12},{1,3},{3,1},... | collective-permute-start | bytes 835592 | tf_op jit(solution)/shard_map/ppermute | solution.py:68
  120.9 2.8 %select_reduce_fusion = f32[128,512]{1,0:T(8,128)S(1)} fusion(bf16[8,128,896]{2,1,0:T(8,128)(2,1)} %bitcast.213, bf16[896,512,1]{1,0,2:T(8,128)(2,1)S(1)} %bitcast.143, pred[8,512]{1,0:T(8,128)(4,1)S(1)} %iota_compare_fusion), kind=kOutput, calls=%fused_computation.6 | convolution fusion | flops 940507136 | bytes 3018752 | tf_op jit(solution)/shard_map/dot_general | solution.py:153
  123.7 1.2 slice.607
  124.9 1.2 slice.608
  126.1 2.1 %collective-permute-done.7 = bf16[2,2,128,512]{3,2,1,0:T(8,128)(2,1)S(1)} collective-permute-done((bf16[2,2,128,512]{3,2,1,0:T(8,128)(2,1)S(1)}, bf16[2,2,128,512]{3,2,1,0:T(8,128)(2,1)S(1)}, u32[]{:S(2)}, u32[]{:S(2)}) %collective-permute-start.7) | collective-permute-done | bytes 524320 | tf_op jit(solution)/shard_map/ppermute | solution.py:17
  128.3 1.4 collective-permute-done.6
  130.0 3.5 %collective-permute-start.9 = (bf16[2,128,512]{2,1,0:T(8,128)(2,1)S(1)}, bf16[2,128,512]{2,1,0:T(8,128)(2,1)S(1)}, u32[]{:S(2)}, u32[]{:S(2)}) collective-permute-start(bf16[2,128,512]{2,1,0:T(8,128)(2,1)S(1)} %get-tuple-element.10), channel_id=1, source_target_pairs={{2,0},{4,2},{6,4},{8,6},{10,8},{12,10},{14,12},{3,1},{5,3},{7,5},{... | collective-permute-start | bytes 786440 | tf_op jit(solution)/shard_map/ppermute | solution.py:17
  133.5 3.7 %collective-permute-start.8 = (bf16[2,128,512]{2,1,0:T(8,128)(2,1)S(1)}, bf16[2,128,512]{2,1,0:T(8,128)(2,1)S(1)}, u32[]{:S(2)}, u32[]{:S(2)}) collective-permute-start(bf16[2,128,512]{2,1,0:T(8,128)(2,1)S(1)} %get-tuple-element.9), channel_id=1, source_target_pairs={{0,2},{2,4},{4,6},{6,8},{8,10},{10,12},{12,14},{1,3},{3,5},{5,7},{... | collective-permute-start | bytes 786440 | tf_op jit(solution)/shard_map/ppermute | solution.py:17
  138.8 2.0 %collective-permute-done.9 = bf16[2,128,512]{2,1,0:T(8,128)(2,1)S(1)} collective-permute-done((bf16[2,128,512]{2,1,0:T(8,128)(2,1)S(1)}, bf16[2,128,512]{2,1,0:T(8,128)(2,1)S(1)}, u32[]{:S(2)}, u32[]{:S(2)}) %collective-permute-start.9) | collective-permute-done | bytes 262176 | tf_op jit(solution)/shard_map/ppermute | solution.py:17
  140.8 5.5 %collective-permute-done.8 = bf16[2,128,512]{2,1,0:T(8,128)(2,1)S(1)} collective-permute-done((bf16[2,128,512]{2,1,0:T(8,128)(2,1)S(1)}, bf16[2,128,512]{2,1,0:T(8,128)(2,1)S(1)}, u32[]{:S(2)}, u32[]{:S(2)}) %collective-permute-start.8) | collective-permute-done | bytes 262176 | tf_op jit(solution)/shard_map/ppermute | solution.py:17
  147.8 1.5 %copy.64 = bf16[2,8,32,1024]{3,2,1,0:T(8,128)(2,1)} copy(bf16[2,8,32,1024]{3,1,2,0:T(8,128)(2,1)S(1)} %fusion.2) | data formatting | bytes 2097152 | tf_op jit(solution)/shard_map/slice | solution.py:242
  (106 shorter events, 16.4 us)
Async XLA Ops:
  0.6 44.7 %copy-start = (bf16[512,1024]{1,0:T(8,128)(2,1)S(1)}, bf16[512,1024]{1,0:T(8,128)(2,1)}, u32[]{:S(2)}) copy-start(bf16[512,1024]{1,0:T(8,128)(2,1)} %param.11) | copy-start | bytes 3145732
  3.4 21.7 %copy-start.14 = (f32[31,1024]{1,0:T(8,128)S(1)}, f32[31,1024]{1,0:T(8,128)}, u32[]{:S(2)}) copy-start(f32[31,1024]{1,0:T(8,128)} %param.12) | copy-start | bytes 380932
  3.5 21.8 %copy-start.13 = (bf16[1,128,512]{2,1,0:T(8,128)(2,1)S(1)}, bf16[1,128,512]{2,1,0:T(8,128)(2,1)}, u32[]{:S(2)}) copy-start(bf16[1,128,512]{2,1,0:T(8,128)(2,1)} %param.7) | copy-start | bytes 393220
  3.5 11.8 %collective-permute-start.2 = (bf16[288,512]{1,0:T(8,128)(2,1)S(1)}, bf16[288,512]{1,0:T(8,128)(2,1)S(1)}, u32[]{:S(2)}, u32[]{:S(2)}) collective-permute-start(bf16[288,512]{1,0:T(8,128)(2,1)S(1)} %get-tuple-element.25), channel_id=1, source_target_pairs={{2,0},{4,2},{6,4},{8,6},{10,8},{12,10},{14,12},{3,1},{5,3},{7,5},{... | collective-permute-start | bytes 884744 | tf_op jit(solution)/shard_map/ppermute | solution.py:17
  5.6 15.9 %collective-permute-start = (bf16[288,512]{1,0:T(8,128)(2,1)S(1)}, bf16[288,512]{1,0:T(8,128)(2,1)S(1)}, u32[]{:S(2)}, u32[]{:S(2)}) collective-permute-start(bf16[288,512]{1,0:T(8,128)(2,1)S(1)} %get-tuple-element.26), channel_id=1, source_target_pairs={{0,2},{2,4},{4,6},{6,8},{8,10},{10,12},{12,14},{1,3},{3,5},{5,7},{... | collective-permute-start | bytes 884744 | tf_op jit(solution)/shard_map/ppermute | solution.py:17
  21.6 14.8 %collective-permute-start.1 = (bf16[2,2,128,512]{3,2,1,0:T(8,128)(2,1)S(1)}, bf16[2,2,128,512]{3,2,1,0:T(8,128)(2,1)S(1)}, u32[]{:S(2)}, u32[]{:S(2)}) collective-permute-start(bf16[2,2,128,512]{3,2,1,0:T(8,128)(2,1)S(1)} %get-tuple-element.24), channel_id=1, source_target_pairs={{0,4},{2,6},{4,8},{6,10},{8,12},{10,14},{1,5},{3,7},{5,9},{7,11},{... | collective-permute-start | bytes 1572872 | tf_op jit(solution)/shard_map/ppermute | solution.py:17
  25.3 15.7 %copy-start.7 = (bf16[8,128,512]{2,1,0:T(8,128)(2,1)}, bf16[8,128,512]{2,1,0:T(8,128)(2,1)S(1)}, u32[]{:S(2)}) copy-start(bf16[8,128,512]{2,1,0:T(8,128)(2,1)S(1)} %broadcast_select_fusion.1) | copy-start | bytes 3145732
  25.3 15.5 %collective-permute-start.3 = (bf16[2,2,128,512]{3,2,1,0:T(8,128)(2,1)S(1)}, bf16[2,2,128,512]{3,2,1,0:T(8,128)(2,1)S(1)}, u32[]{:S(2)}, u32[]{:S(2)}) collective-permute-start(bf16[2,2,128,512]{3,2,1,0:T(8,128)(2,1)S(1)} %get-tuple-element.23), channel_id=1, source_target_pairs={{4,0},{6,2},{8,4},{10,6},{12,8},{14,10},{5,1},{7,3},{9,5},{11,7},{... | collective-permute-start | bytes 1572872 | tf_op jit(solution)/shard_map/ppermute | solution.py:17
  41.0 1.4 copy-start.10
  41.0 3.1 %copy-start.12 = (bf16[7,1,128,512]{3,2,1,0:T(8,128)(2,1)}, bf16[7,1,128,512]{3,2,1,0:T(8,128)(2,1)S(1)}, u32[]{:S(2)}) copy-start(bf16[7,1,128,512]{3,2,1,0:T(8,128)(2,1)S(1)} %get-tuple-element.7) | copy-start | bytes 2752516
  44.1 1.3 copy-start.3
  45.4 14.6 %copy-start.6 = (bf16[128,512]{1,0:T(8,128)(2,1)}, bf16[128,512]{1,0:T(8,128)(2,1)S(1)}, u32[]{:S(2)}) copy-start(bf16[128,512]{1,0:T(8,128)(2,1)S(1)} %select_reduce_fusion.1) | copy-start | bytes 393220
  45.4 9.2 %copy-start.5 = (bf16[1,128,1024]{2,1,0:T(8,128)(2,1)S(1)}, bf16[1,128,1024]{2,1,0:T(8,128)(2,1)}, u32[]{:S(2)}) copy-start(bf16[1,128,1024]{2,1,0:T(8,128)(2,1)} %param.10) | copy-start | bytes 786436
  45.7 7.1 %collective-permute-start.5 = (bf16[30,1024]{1,0:T(8,128)(2,1)S(1)}, bf16[30,1024]{1,0:T(8,128)(2,1)S(1)}, u32[]{:S(2)}, u32[]{:S(2)}) collective-permute-start(bf16[30,1024]{1,0:T(8,128)(2,1)S(1)} %get-tuple-element.22), channel_id=1, source_target_pairs={{2,0},{4,2},{6,4},{8,6},{10,8},{12,10},{14,12},{3,1},{5,3},{7,5},{... | collective-permute-start | bytes 184328 | tf_op jit(solution)/shard_map/ppermute | solution.py:30
  47.7 6.7 %collective-permute-start.4 = (bf16[30,1024]{1,0:T(8,128)(2,1)S(1)}, bf16[30,1024]{1,0:T(8,128)(2,1)S(1)}, u32[]{:S(2)}, u32[]{:S(2)}) collective-permute-start(bf16[30,1024]{1,0:T(8,128)(2,1)S(1)} %get-tuple-element.21), channel_id=1, source_target_pairs={{0,2},{2,4},{4,6},{6,8},{8,10},{10,12},{12,14},{1,3},{3,5},{5,7},{... | collective-permute-start | bytes 184328 | tf_op jit(solution)/shard_map/ppermute | solution.py:28
  68.2 2.3 %collective-permute-start.10 = (bf16[1,8,34,1024]{3,1,2,0:T(8,128)(2,1)}, bf16[1,8,34,1024]{3,1,2,0:T(8,128)(2,1)}, u32[]{:S(2)}, u32[]{:S(2)}) collective-permute-start(bf16[1,8,34,1024]{3,1,2,0:T(8,128)(2,1)} %dynamic-slice_convert_fusion), channel_id=1, source_target_pairs={{0,1},{1,0},{2,3},{3,2},{4,5},{5,4},{6,7},{7,6},{8,9},{9,8},{10,11... | collective-permute-start | bytes 1671176 | tf_op jit(solution)/shard_map/ppermute | solution.py:68
  71.7 1.0 copy-start.1
  72.9 8.8 %copy-start.2 = (f32[1,8,34,1024]{3,1,2,0:T(8,128)S(1)}, f32[1,8,34,1024]{3,1,2,0:T(8,128)}, u32[]{:S(2)}) copy-start(f32[1,8,34,1024]{3,1,2,0:T(8,128)} %copy-done.1) | copy-start | bytes 3342340
  72.9 8.8 %collective-permute-start.11 = (bf16[4,34,1024]{2,0,1:T(4,128)(2,1)S(1)}, bf16[4,34,1024]{2,0,1:T(4,128)(2,1)S(1)}, u32[]{:S(2)}, u32[]{:S(2)}) collective-permute-start(bf16[4,34,1024]{2,0,1:T(4,128)(2,1)S(1)} %fusion.17), channel_id=1, source_target_pairs={{0,2},{2,0},{4,6},{6,4},{8,10},{10,8},{12,14},{14,12},{1,3},{3,1},... | collective-permute-start | bytes 835592 | tf_op jit(solution)/shard_map/ppermute | solution.py:68
  81.8 10.6 %copy-start.4 = (bf16[1024,896]{1,0:T(8,128)(2,1)S(1)}, bf16[1024,896]{1,0:T(8,128)(2,1)}, u32[]{:S(2)}) copy-start(bf16[1024,896]{1,0:T(8,128)(2,1)} %copy-done.3) | copy-start | bytes 5505028
  82.6 5.9 %collective-permute-start.12 = (bf16[2,34,1024]{2,0,1:T(2,128)(2,1)}, bf16[2,34,1024]{2,0,1:T(2,128)(2,1)}, u32[]{:S(2)}, u32[]{:S(2)}) collective-permute-start(bf16[2,34,1024]{2,0,1:T(2,128)(2,1)} %dynamic-slice_convert_fusion.2), channel_id=1, source_target_pairs={{0,4},{2,6},{4,0},{6,2},{8,12},{10,14},{12,8},{14,10},{1,5},{3,7},... | collective-permute-start | bytes 417800 | tf_op jit(solution)/shard_map/ppermute | solution.py:68
  89.8 8.8 %collective-permute-start.13 = (bf16[1,34,1024]{2,0,1:T(2,128)(2,1)S(1)}, bf16[1,34,1024]{2,0,1:T(2,128)(2,1)S(1)}, u32[]{:S(2)}, u32[]{:S(2)}) collective-permute-start(bf16[1,34,1024]{2,0,1:T(2,128)(2,1)S(1)} %dynamic-slice_convert_fusion.3), channel_id=1, source_target_pairs={{0,8},{2,10},{4,12},{6,14},{8,0},{10,2},{12,4},{14,6},{1,9},{3,11}... | collective-permute-start | bytes 208904 | tf_op jit(solution)/shard_map/ppermute | solution.py:68
  92.5 6.4 %copy-start.9 = (bf16[8,128,512]{2,1,0:T(8,128)(2,1)S(1)}, bf16[8,128,512]{2,1,0:T(8,128)(2,1)}, u32[]{:S(2)}) copy-start(bf16[8,128,512]{2,1,0:T(8,128)(2,1)} %broadcast_select_fusion) | copy-start | bytes 3145732
  95.3 13.6 %copy-start.15 = (bf16[1024,896]{1,0:T(8,128)(2,1)}, bf16[1024,896]{1,0:T(8,128)(2,1)S(1)}, u32[]{:S(2)}) copy-start(bf16[1024,896]{1,0:T(8,128)(2,1)S(1)} %multiply_convert_fusion) | copy-start | bytes 5505028
  98.8 10.1 %copy-start.8 = (bf16[8,128,512]{2,1,0:T(8,128)(2,1)S(1)}, bf16[8,128,512]{2,1,0:T(8,128)(2,1)}, u32[]{:S(2)}) copy-start(bf16[8,128,512]{2,1,0:T(8,128)(2,1)} %copy-done.7) | copy-start | bytes 3145732
  98.8 8.9 %collective-permute-start.14 = (bf16[1,34,1024]{2,0,1:T(2,128)(2,1)S(1)}, bf16[1,34,1024]{2,0,1:T(2,128)(2,1)S(1)}, u32[]{:S(2)}, u32[]{:S(2)}) collective-permute-start(bf16[1,34,1024]{2,0,1:T(2,128)(2,1)S(1)} %add_convert_fusion.1), channel_id=1, source_target_pairs={{0,8},{2,10},{4,12},{6,14},{8,0},{10,2},{12,4},{14,6},{1,9},{3,11}... | collective-permute-start | bytes 208904 | tf_op jit(solution)/shard_map/ppermute | solution.py:68
  108.9 9.6 %collective-permute-start.15 = (bf16[2,34,1024]{2,0,1:T(2,128)(2,1)}, bf16[2,34,1024]{2,0,1:T(2,128)(2,1)S(1)}, u32[]{:S(2)}, u32[]{:S(2)}) collective-permute-start(bf16[2,34,1024]{2,0,1:T(2,128)(2,1)} %pad_maximum_fusion.9), channel_id=1, source_target_pairs={{0,4},{2,6},{4,0},{6,2},{8,12},{10,14},{12,8},{14,10},{1,5},{3,7},... | collective-permute-start | bytes 417800 | tf_op jit(solution)/shard_map/ppermute | solution.py:68
  112.2 8.7 %copy-start.11 = (bf16[7,1,128,512]{3,2,1,0:T(8,128)(2,1)S(1)}, bf16[7,1,128,512]{3,2,1,0:T(8,128)(2,1)}, u32[]{:S(2)}) copy-start(bf16[7,1,128,512]{3,2,1,0:T(8,128)(2,1)} %copy-done.10) | copy-start | bytes 2752516
  112.3 15.9 %collective-permute-start.7 = (bf16[2,2,128,512]{3,2,1,0:T(8,128)(2,1)S(1)}, bf16[2,2,128,512]{3,2,1,0:T(8,128)(2,1)S(1)}, u32[]{:S(2)}, u32[]{:S(2)}) collective-permute-start(bf16[2,2,128,512]{3,2,1,0:T(8,128)(2,1)S(1)} %rev.3), channel_id=1, source_target_pairs={{4,0},{6,2},{8,4},{10,6},{12,8},{14,10},{5,1},{7,3},{9,5},{11,7},{... | collective-permute-start | bytes 1572872 | tf_op jit(solution)/shard_map/ppermute | solution.py:17
  113.7 15.9 %collective-permute-start.6 = (bf16[2,2,128,512]{3,2,1,0:T(8,128)(2,1)}, bf16[2,2,128,512]{3,2,1,0:T(8,128)(2,1)S(1)}, u32[]{:S(2)}, u32[]{:S(2)}) collective-permute-start(bf16[2,2,128,512]{3,2,1,0:T(8,128)(2,1)} %get-tuple-element.5), channel_id=1, source_target_pairs={{0,4},{2,6},{4,8},{6,10},{8,12},{10,14},{1,5},{3,7},{5,9},{7,11},{... | collective-permute-start | bytes 1572872 | tf_op jit(solution)/shard_map/ppermute | solution.py:17
  119.3 18.0 %collective-permute-start.16 = (bf16[4,34,1024]{2,0,1:T(4,128)(2,1)S(1)}, bf16[4,34,1024]{2,0,1:T(4,128)(2,1)S(1)}, u32[]{:S(2)}, u32[]{:S(2)}) collective-permute-start(bf16[4,34,1024]{2,0,1:T(4,128)(2,1)S(1)} %pad_maximum_fusion.8), channel_id=1, source_target_pairs={{0,2},{2,0},{4,6},{6,4},{8,10},{10,8},{12,14},{14,12},{1,3},{3,1},... | collective-permute-start | bytes 835592 | tf_op jit(solution)/shard_map/ppermute | solution.py:68
  130.0 10.7 %collective-permute-start.9 = (bf16[2,128,512]{2,1,0:T(8,128)(2,1)S(1)}, bf16[2,128,512]{2,1,0:T(8,128)(2,1)S(1)}, u32[]{:S(2)}, u32[]{:S(2)}) collective-permute-start(bf16[2,128,512]{2,1,0:T(8,128)(2,1)S(1)} %get-tuple-element.10), channel_id=1, source_target_pairs={{2,0},{4,2},{6,4},{8,6},{10,8},{12,10},{14,12},{3,1},{5,3},{7,5},{... | collective-permute-start | bytes 786440 | tf_op jit(solution)/shard_map/ppermute | solution.py:17
  133.5 12.8 %collective-permute-start.8 = (bf16[2,128,512]{2,1,0:T(8,128)(2,1)S(1)}, bf16[2,128,512]{2,1,0:T(8,128)(2,1)S(1)}, u32[]{:S(2)}, u32[]{:S(2)}) collective-permute-start(bf16[2,128,512]{2,1,0:T(8,128)(2,1)S(1)} %get-tuple-element.9), channel_id=1, source_target_pairs={{0,2},{2,4},{4,6},{6,8},{8,10},{10,12},{12,14},{1,3},{3,5},{5,7},{... | collective-permute-start | bytes 786440 | tf_op jit(solution)/shard_map/ppermute | solution.py:17
  138.0 9.2 %collective-permute-start.17 = (bf16[1,8,34,1024]{3,1,2,0:T(8,128)(2,1)S(1)}, bf16[1,8,34,1024]{3,1,2,0:T(8,128)(2,1)S(1)}, u32[]{:S(2)}, u32[]{:S(2)}) collective-permute-start(bf16[1,8,34,1024]{3,1,2,0:T(8,128)(2,1)S(1)} %maximum_bitcast_fusion), channel_id=1, source_target_pairs={{0,1},{1,0},{2,3},{3,2},{4,5},{5,4},{6,7},{7,6},{8,9},{9,8},{10,11... | collective-permute-start | bytes 1671176 | tf_op jit(solution)/shard_map/ppermute | solution.py:68

commit v13 on v12

--- a/solution.py
+++ b/solution.py
@@ -68,17 +68,17 @@
     return lax.ppermute(block, axis, [(i, i ^ bit) for i in range(count)])
 
 
-def halving(acc, axis):
+def halving(acc, axis, first=0, last=None):
     here = lax.axis_index(axis)
     count = lax.axis_size(axis)
     levels = count.bit_length() - 1
-    for level in range(levels):
+    for level in range(first, levels if last is None else min(last, levels)):
         half = acc.shape[0] // 2
         mine = (here >> level) % 2
         keep = lax.dynamic_slice_in_dim(acc, mine * half, half, 0)
         send = lax.dynamic_slice_in_dim(acc, (1 - mine) * half, half, 0)
         acc = keep + exchange(send.astype(jnp.bfloat16), axis, 1 << level).astype(jnp.float32)
-    return acc[0]
+    return acc[0] if acc.shape[0] == 1 else acc
 
 
 def doubling(acc, axis):
@@ -208,7 +208,7 @@
         ],
         axis=2,
     )
-    summed = halving(halving(stacked, "dp"), "ctx").astype(jnp.bfloat16)
+    partly = halving(halving(stacked, "dp"), "ctx", 0, 1)
     grad_attended = lax.dot_general(
         grad_hidden, out_proj, (((1,), (1,)), ((), ())), preferred_element_type=jnp.float32
     ).astype(jnp.bfloat16)
@@ -234,6 +234,8 @@
     near = jnp.stack(
         [key_blocks[REACH - 1 : REACH + 2], value_blocks[REACH - 1 : REACH + 2]], axis=1
     )
+    partly, narrow = lax.optimization_barrier((partly, narrow))
+    summed = halving(partly, "ctx", 1).astype(jnp.bfloat16)
 
     def grad_shift(piece_rows, offset_by):
         return passed_along(piece_rows, "ctx", offset_by)

time: 151 us -> 161 us (1.066)
  waiting for transfers between devices: 55.3 us -> 60.4 us
  other arithmetic: 18.1 us -> 20.5 us
  local copies, waits for them, and re-layouts: 17.5 us -> 19.5 us
  starting transfers between devices: 38.7 us -> 37 us
    ppermute x8, waiting for transfers between devices: 18.4 us -> 24.3 us  [exchange(): return lax.ppermute(block, axis, [(i, i ^ bit) for i in range(count)])]
    dot_general x6, matrix products: 13.1 us -> 15.9 us  [contract(): lax.dot_general(lhs, rhs, (((lhs_dim,), (rhs_dim,)), ((), ())), preferred...]
    dot_general x1, matrix products: 2.16 us -> 0.49 us  [on_device(): lax.dot_general(grad_hidden, out_proj, (((1,), (1,)), ((), ())), preferre...]
    unnamed x39 -> x31, local copies, waits for them, and re-layouts: 3.33 us -> 3.61 us
  transfers between devices with their start and end apart: 18 -> 18, of which waited for: 13 -> 13; matrix products, arithmetic and copies ran while one was open for 16% -> 15% of each run, Pallas kernels for 0% -> 0%
where the time goes in v13:
time: 161 us; the launch traced here: 159 us
  waiting for transfers between devices  60.4 us (38%)
  starting transfers between devices  37 us (23%)
  other arithmetic  20.5 us (13%)
  matrix products  19.6 us (12%)
  local copies, waits for them, and re-layouts  19.5 us (12%)
  between operations  2.09 us (1%)
    ppermute x8, waiting for transfers between devices, passed_along(): return lax.ppermute(block, axis, route)  34.6 us
    ppermute x8, starting transfers between devices, passed_along(): return lax.ppermute(block, axis, route)  24.5 us
    ppermute x8, waiting for transfers between devices, exchange(): return lax.ppermute(block, axis, [(i, i ^ bit) for i in range(count)])  24.3 us
    dot_general x6, matrix products, contract(): lax.dot_general(lhs, rhs, (((lhs_dim,), (rhs_dim,)), ((), ())), preferred...  15.9 us
    ppermute x8, starting transfers between devices, exchange(): return lax.ppermute(block, axis, [(i, i ^ bit) for i in range(count)])  5.57 us
    ppermute x1, starting transfers between devices, padded(): lax.ppermute(tail, axis, [(i, (i + 1) % count) for i in range(ends)])  5 us
    add x3, other arithmetic, halving(): keep + exchange(send.astype(jnp.bfloat16), axis, 1 << level).astype(jnp.f...  3.68 us
    unnamed x31, local copies, waits for them, and re-layouts  3.61 us
  transfers between devices with their start and end apart: 18, of which 13 were waited for; matrix products, arithmetic and copies ran while one was open for 15% of the time, Pallas kernels for 0%

profile of v13, /device:TPU:2, one launch (start us, length us, event | category | flops | bytes accessed | tf_op | source)
XLA Modules:
  0.0 159.1 jit_solution(8887831127413925278)
XLA Ops:
  3.5 2.1 %collective-permute-start.2 = (bf16[288,512]{1,0:T(8,128)(2,1)S(1)}, bf16[288,512]{1,0:T(8,128)(2,1)S(1)}, u32[]{:S(2)}, u32[]{:S(2)}) collective-permute-start(bf16[288,512]{1,0:T(8,128)(2,1)S(1)} %get-tuple-element.29), channel_id=1, source_target_pairs={{2,0},{4,2},{6,4},{8,6},{10,8},{12,10},{14,12},{3,1},{5,3},{7,5},{... | collective-permute-start | bytes 884744 | tf_op jit(solution)/shard_map/ppermute | solution.py:17
  5.6 4.8 %collective-permute-start = (bf16[288,512]{1,0:T(8,128)(2,1)S(1)}, bf16[288,512]{1,0:T(8,128)(2,1)S(1)}, u32[]{:S(2)}, u32[]{:S(2)}) collective-permute-start(bf16[288,512]{1,0:T(8,128)(2,1)S(1)} %get-tuple-element.30), channel_id=1, source_target_pairs={{0,2},{2,4},{4,6},{6,8},{8,10},{10,12},{12,14},{1,3},{3,5},{5,7},{... | collective-permute-start | bytes 884744 | tf_op jit(solution)/shard_map/ppermute | solution.py:17
  11.1 4.2 %collective-permute-done.2 = bf16[288,512]{1,0:T(8,128)(2,1)S(1)} collective-permute-done((bf16[288,512]{1,0:T(8,128)(2,1)S(1)}, bf16[288,512]{1,0:T(8,128)(2,1)S(1)}, u32[]{:S(2)}, u32[]{:S(2)}) %collective-permute-start.2) | collective-permute-done | bytes 294944 | tf_op jit(solution)/shard_map/ppermute | solution.py:17
  15.3 6.2 %collective-permute-done = bf16[288,512]{1,0:T(8,128)(2,1)S(1)} collective-permute-done((bf16[288,512]{1,0:T(8,128)(2,1)S(1)}, bf16[288,512]{1,0:T(8,128)(2,1)S(1)}, u32[]{:S(2)}, u32[]{:S(2)}) %collective-permute-start) | collective-permute-done | bytes 294944 | tf_op jit(solution)/shard_map/ppermute | solution.py:17
  21.6 3.5 %collective-permute-start.1 = (bf16[2,2,128,512]{3,2,1,0:T(8,128)(2,1)S(1)}, bf16[2,2,128,512]{3,2,1,0:T(8,128)(2,1)S(1)}, u32[]{:S(2)}, u32[]{:S(2)}) collective-permute-start(bf16[2,2,128,512]{3,2,1,0:T(8,128)(2,1)S(1)} %get-tuple-element.28), channel_id=1, source_target_pairs={{0,4},{2,6},{4,8},{6,10},{8,12},{10,14},{1,5},{3,7},{5,9},{7,11},{... | collective-permute-start | bytes 1572872 | tf_op jit(solution)/shard_map/ppermute | solution.py:17
  25.3 1.3 collective-permute-start.3
  26.6 9.8 %collective-permute-done.1 = bf16[2,2,128,512]{3,2,1,0:T(8,128)(2,1)S(1)} collective-permute-done((bf16[2,2,128,512]{3,2,1,0:T(8,128)(2,1)S(1)}, bf16[2,2,128,512]{3,2,1,0:T(8,128)(2,1)S(1)}, u32[]{:S(2)}, u32[]{:S(2)}) %collective-permute-start.1) | collective-permute-done | bytes 524320 | tf_op jit(solution)/shard_map/ppermute | solution.py:17
  36.6 4.2 %collective-permute-done.3 = bf16[2,2,128,512]{3,2,1,0:T(8,128)(2,1)S(1)} collective-permute-done((bf16[2,2,128,512]{3,2,1,0:T(8,128)(2,1)S(1)}, bf16[2,2,128,512]{3,2,1,0:T(8,128)(2,1)S(1)}, u32[]{:S(2)}, u32[]{:S(2)}) %collective-permute-start.3) | collective-permute-done | bytes 524320 | tf_op jit(solution)/shard_map/ppermute | solution.py:17
  41.0 1.4 fusion
  44.1 1.2 copy-done.1
  45.3 1.2 select_reduce_fusion.1
  46.9 1.9 %collective-permute-start.5 = (bf16[30,1024]{1,0:T(8,128)(2,1)S(1)}, bf16[30,1024]{1,0:T(8,128)(2,1)S(1)}, u32[]{:S(2)}, u32[]{:S(2)}) collective-permute-start(bf16[30,1024]{1,0:T(8,128)(2,1)S(1)} %get-tuple-element.26), channel_id=1, source_target_pairs={{2,0},{4,2},{6,4},{8,6},{10,8},{12,10},{14,12},{3,1},{5,3},{7,5},{... | collective-permute-start | bytes 184328 | tf_op jit(solution)/shard_map/ppermute | solution.py:30
  48.8 5.0 %collective-permute-start.4 = (bf16[30,1024]{1,0:T(8,128)(2,1)S(1)}, bf16[30,1024]{1,0:T(8,128)(2,1)S(1)}, u32[]{:S(2)}, u32[]{:S(2)}) collective-permute-start(bf16[30,1024]{1,0:T(8,128)(2,1)S(1)} %get-tuple-element.25), channel_id=1, source_target_pairs={{0,2},{2,4},{4,6},{6,8},{8,10},{10,12},{12,14},{1,3},{3,5},{5,7},{... | collective-permute-start | bytes 184328 | tf_op jit(solution)/shard_map/ppermute | solution.py:28
  54.1 1.5 collective-permute-done.4
  55.7 3.0 %multiply_convert_fusion.1 = bf16[158,1024]{1,0:T(8,128)(2,1)S(1)} fusion(bf16[188,1024]{1,0:T(8,128)(2,1)S(1)} %pad_maximum_fusion.4, bf16[15,1024]{1,0:T(8,128)(2,1)S(1)} %slice.428, bf16[128,1024]{1,0:T(8,128)(2,1)S(1)} %bitcast.136, bf16[15,1024]{1,0:T(8,128)(2,1)S(1)} %slice.426, bf16[128,1024]{1,0:T(8,128)(2,1)S(1)} %fusion.1, ...), kind=kLoop, calls=%fused_computation.24 | loop fusion | flops 18282496 | bytes 10543104 | tf_op jit(solution)/shard_map/convert_element_type | solution.py:176
  58.7 2.2 %add_convert_fusion = bf16[128,1024]{1,0:T(8,128)(2,1)S(1)} fusion(bf16[158,1024]{1,0:T(8,128)(2,1)S(1)} %multiply_convert_fusion.1, f32[1024]{0:T(1024)S(1)} %bitcast.209, f32[1024]{0:T(1024)S(1)} %bitcast.211, f32[1024]{0:T(1024)S(1)} %bitcast.153, f32[1024]{0:T(1024)S(1)} %bitcast.155, f32[1024]{0:T(1024)S(1)} %bitcast.157, f32[1024]{0:T(1024)S(1)} %bitcast.159, ...), kind=kLoop, calls=%fused_computation.48 | loop fusion | flops 12582912 | bytes 8777856 | tf_op jit(solution)/shard_map/convert_element_type | solution.py:194
  62.1 1.0 broadcast_select_fusion
  63.1 1.2 copy_dynamic-update-slice_fusion
  64.4 2.4 %fusion.3 = f32[1,31,1024]{2,0,1:T(1,128)S(1)} fusion(bf16[1,158,1024]{2,1,0:T(8,128)(2,1)S(1)} %slice_bitcast_fusion, bf16[128,1,1024]{2,0,1:T(8,128)(2,1)S(1)} %slice_bitcast_fusion.1), kind=kOutput, calls=%fused_computation.25 | convolution fusion | flops 8126464 | bytes 712704 | tf_op jit(solution)/shard_map/conv_general_dilated | solution.py:183
  67.4 1.6 %reshape.167 = f32[2,8,2,1024]{3,2,1,0:T(2,128)} reshape(f32[32,1024]{1,0:T(8,128)} %pad.13) | data formatting | bytes 262144 | tf_op jit(solution)/shard_map/reshape | solution.py:207
  70.9 4.5 %fusion.36 = (bf16[896,512]{1,0:T(8,128)(2,1)}, f32[896,512]{1,0:T(8,128)}) fusion(bf16[1024,896]{1,0:T(8,128)(2,1)} %copy-done.1, bf16[1024,512]{1,0:T(8,128)(2,1)} %bitcast.139), kind=kOutput, calls=%fused_computation.109 | convolution fusion | flops 939982848 | bytes 5636096 | tf_op jit(solution)/shard_map/dot_general | solution.py:153
  76.3 1.0 bitcast_reduce_fusion
  77.3 3.4 %multiply_convert_fusion = bf16[1024,896]{1,0:T(8,128)(2,1)S(1)} fusion(bf16[1024,896]{1,0:T(8,128)(2,1)} %copy-done.1, bf16[1024,512]{1,0:T(8,128)(2,1)} %bitcast.140, bf16[896,512]{1,0:T(8,128)(2,1)} %bitcast.145, f32[1024]{0:T(1024)S(1)} %bitcast.212), kind=kOutput, calls=%fused_computation | convolution fusion | flops 943194112 | bytes 5640192 | tf_op jit(solution)/shard_map/dot_general | solution.py:153
  80.7 1.7 %convert_add_fusion = f32[1,8,34,1024]{3,1,2,0:T(8,128)S(1)} fusion(bf16[1,8,34,1024]{3,1,2,0:T(8,128)(2,1)} %collective-permute-done.6, f32[2,8,34,1024]{3,1,2,0:T(8,128)S(1)} %copy_dynamic-update-slice_fusion.1, s32[]{:T(128)S(6)} %select_n.172), kind=kLoop, calls=%fused_computation.19 | loop fusion | flops 557056 | bytes 2785284 | tf_op jit(solution)/shard_map/add | solution.py:80
  82.7 2.4 %fusion.37 = (bf16[896,512]{1,0:T(8,128)(2,1)S(1)}, f32[896,512]{1,0:T(8,128)}) fusion(bf16[1024,896]{1,0:T(8,128)(2,1)S(1)} %multiply_convert_fusion, bf16[1024,512]{1,0:T(8,128)(2,1)S(1)} %bitcast.138), kind=kOutput, calls=%fused_computation.110 | convolution fusion | flops 940441600 | bytes 5636096 | tf_op jit(solution)/shard_map/dot_general | solution.py:153
  85.3 6.3 %collective-permute-done.7 = bf16[4,34,1024]{2,0,1:T(4,128)(2,1)S(1)} collective-permute-done((bf16[4,34,1024]{2,0,1:T(4,128)(2,1)S(1)}, bf16[4,34,1024]{2,0,1:T(4,128)(2,1)S(1)}, u32[]{:S(2)}, u32[]{:S(2)}) %collective-permute-start.7) | collective-permute-done | bytes 278560 | tf_op jit(solution)/shard_map/ppermute | solution.py:68
  92.7 2.1 %collective-permute-start.12 = (bf16[2,34,1024]{2,0,1:T(2,128)(2,1)}, bf16[2,34,1024]{2,0,1:T(2,128)(2,1)}, u32[]{:S(2)}, u32[]{:S(2)}) collective-permute-start(bf16[2,34,1024]{2,0,1:T(2,128)(2,1)} %dynamic-slice_convert_fusion.2), channel_id=1, source_target_pairs={{0,4},{2,6},{4,0},{6,2},{8,12},{10,14},{12,8},{14,10},{1,5},{3,7},... | collective-permute-start | bytes 417800 | tf_op jit(solution)/shard_map/ppermute | solution.py:68
  94.7 4.1 %collective-permute-done.12 = bf16[2,34,1024]{2,0,1:T(2,128)(2,1)} collective-permute-done((bf16[2,34,1024]{2,0,1:T(2,128)(2,1)}, bf16[2,34,1024]{2,0,1:T(2,128)(2,1)}, u32[]{:S(2)}, u32[]{:S(2)}) %collective-permute-start.12) | collective-permute-done | bytes 139296 | tf_op jit(solution)/shard_map/ppermute | solution.py:68
  98.8 1.8 %convert_add_fusion.1 = f32[2,34,1024]{2,0,1:T(2,128)} fusion(bf16[2,34,1024]{2,0,1:T(2,128)(2,1)} %collective-permute-done.12, f32[4,34,1024]{2,0,1:T(4,128)S(1)} %bitcast_add_fusion, s32[]{:T(128)S(6)} %select_n.183), kind=kLoop, calls=%fused_computation.55 | loop fusion | flops 139264 | bytes 696324 | tf_op jit(solution)/shard_map/add | solution.py:80
  100.6 1.1 dynamic-slice_convert_fusion.3
  101.7 2.8 %collective-permute-start.13 = (bf16[1,34,1024]{2,0,1:T(2,128)(2,1)S(1)}, bf16[1,34,1024]{2,0,1:T(2,128)(2,1)S(1)}, u32[]{:S(2)}, u32[]{:S(2)}) collective-permute-start(bf16[1,34,1024]{2,0,1:T(2,128)(2,1)S(1)} %dynamic-slice_convert_fusion.3), channel_id=1, source_target_pairs={{0,8},{2,10},{4,12},{6,14},{8,0},{10,2},{12,4},{14,6},{1,9},{3,11}... | collective-permute-start | bytes 208904 | tf_op jit(solution)/shard_map/ppermute | solution.py:68
  104.5 6.1 %collective-permute-done.13 = bf16[1,34,1024]{2,0,1:T(2,128)(2,1)S(1)} collective-permute-done((bf16[1,34,1024]{2,0,1:T(2,128)(2,1)S(1)}, bf16[1,34,1024]{2,0,1:T(2,128)(2,1)S(1)}, u32[]{:S(2)}, u32[]{:S(2)}) %collective-permute-start.13) | collective-permute-done | bytes 69664 | tf_op jit(solution)/shard_map/ppermute | solution.py:68
  110.6 1.2 add_convert_fusion.1
  111.8 7.8 %collective-permute-done.14 = bf16[1,34,1024]{2,0,1:T(2,128)(2,1)S(1)} collective-permute-done((bf16[1,34,1024]{2,0,1:T(2,128)(2,1)S(1)}, bf16[1,34,1024]{2,0,1:T(2,128)(2,1)S(1)}, u32[]{:S(2)}, u32[]{:S(2)}) %collective-permute-start.14) | collective-permute-done | bytes 69664 | tf_op jit(solution)/shard_map/ppermute | solution.py:68
  119.9 1.0 pad_maximum_fusion.8
  122.7 1.3 collective-permute-start.9
  123.9 4.8 %collective-permute-start.8 = (bf16[2,2,128,512]{3,2,1,0:T(8,128)(2,1)}, bf16[2,2,128,512]{3,2,1,0:T(8,128)(2,1)S(1)}, u32[]{:S(2)}, u32[]{:S(2)}) collective-permute-start(bf16[2,2,128,512]{3,2,1,0:T(8,128)(2,1)} %get-tuple-element.9), channel_id=1, source_target_pairs={{0,4},{2,6},{4,8},{6,10},{8,12},{10,14},{1,5},{3,7},{5,9},{7,11},{... | collective-permute-start | bytes 1572872 | tf_op jit(solution)/shard_map/ppermute | solution.py:17
  128.8 1.4 broadcast_select_fusion.7
  131.0 3.0 %select_reduce_fusion = f32[128,512]{1,0:T(8,128)S(1)} fusion(bf16[8,128,896]{2,1,0:T(8,128)(2,1)} %bitcast.213, bf16[896,512,1]{1,0,2:T(8,128)(2,1)} %bitcast.143, pred[8,512]{1,0:T(8,128)(4,1)S(1)} %iota_compare_fusion), kind=kOutput, calls=%fused_computation.6 | convolution fusion | flops 940507136 | bytes 3018752 | tf_op jit(solution)/shard_map/dot_general | solution.py:153
  134.0 1.2 slice.607
  135.1 1.2 slice.608
  136.3 2.0 %collective-permute-done.9 = bf16[2,2,128,512]{3,2,1,0:T(8,128)(2,1)S(1)} collective-permute-done((bf16[2,2,128,512]{3,2,1,0:T(8,128)(2,1)}, bf16[2,2,128,512]{3,2,1,0:T(8,128)(2,1)S(1)}, u32[]{:S(2)}, u32[]{:S(2)}) %collective-permute-start.9) | collective-permute-done | bytes 524320 | tf_op jit(solution)/shard_map/ppermute | solution.py:17
  138.5 1.2 collective-permute-done.8
  140.0 1.9 %collective-permute-start.11 = (bf16[2,128,512]{2,1,0:T(8,128)(2,1)S(1)}, bf16[2,128,512]{2,1,0:T(8,128)(2,1)S(1)}, u32[]{:S(2)}, u32[]{:S(2)}) collective-permute-start(bf16[2,128,512]{2,1,0:T(8,128)(2,1)S(1)} %get-tuple-element.14), channel_id=1, source_target_pairs={{2,0},{4,2},{6,4},{8,6},{10,8},{12,10},{14,12},{3,1},{5,3},{7,5},{... | collective-permute-start | bytes 786440 | tf_op jit(solution)/shard_map/ppermute | solution.py:17
  141.9 4.8 %collective-permute-start.10 = (bf16[2,128,512]{2,1,0:T(8,128)(2,1)S(1)}, bf16[2,128,512]{2,1,0:T(8,128)(2,1)S(1)}, u32[]{:S(2)}, u32[]{:S(2)}) collective-permute-start(bf16[2,128,512]{2,1,0:T(8,128)(2,1)S(1)} %get-tuple-element.13), channel_id=1, source_target_pairs={{0,2},{2,4},{4,6},{6,8},{8,10},{10,12},{12,14},{1,3},{3,5},{5,7},{... | collective-permute-start | bytes 786440 | tf_op jit(solution)/shard_map/ppermute | solution.py:17
  148.3 1.5 collective-permute-done.11
  149.8 5.5 %collective-permute-done.10 = bf16[2,128,512]{2,1,0:T(8,128)(2,1)S(1)} collective-permute-done((bf16[2,128,512]{2,1,0:T(8,128)(2,1)S(1)}, bf16[2,128,512]{2,1,0:T(8,128)(2,1)S(1)}, u32[]{:S(2)}, u32[]{:S(2)}) %collective-permute-start.10) | collective-permute-done | bytes 262176 | tf_op jit(solution)/shard_map/ppermute | solution.py:17
  156.7 1.5 copy.64
  (99 shorter events, 18.6 us)
Async XLA Ops:
  0.6 45.9 %copy-start = (bf16[512,1024]{1,0:T(8,128)(2,1)S(1)}, bf16[512,1024]{1,0:T(8,128)(2,1)}, u32[]{:S(2)}) copy-start(bf16[512,1024]{1,0:T(8,128)(2,1)} %param.11) | copy-start | bytes 3145732
  3.4 21.7 %copy-start.10 = (f32[31,1024]{1,0:T(8,128)S(1)}, f32[31,1024]{1,0:T(8,128)}, u32[]{:S(2)}) copy-start(f32[31,1024]{1,0:T(8,128)} %param.12) | copy-start | bytes 380932
  3.5 21.8 %copy-start.9 = (bf16[1,128,512]{2,1,0:T(8,128)(2,1)S(1)}, bf16[1,128,512]{2,1,0:T(8,128)(2,1)}, u32[]{:S(2)}) copy-start(bf16[1,128,512]{2,1,0:T(8,128)(2,1)} %param.7) | copy-start | bytes 393220
  3.5 11.8 %collective-permute-start.2 = (bf16[288,512]{1,0:T(8,128)(2,1)S(1)}, bf16[288,512]{1,0:T(8,128)(2,1)S(1)}, u32[]{:S(2)}, u32[]{:S(2)}) collective-permute-start(bf16[288,512]{1,0:T(8,128)(2,1)S(1)} %get-tuple-element.29), channel_id=1, source_target_pairs={{2,0},{4,2},{6,4},{8,6},{10,8},{12,10},{14,12},{3,1},{5,3},{7,5},{... | collective-permute-start | bytes 884744 | tf_op jit(solution)/shard_map/ppermute | solution.py:17
  5.6 15.9 %collective-permute-start = (bf16[288,512]{1,0:T(8,128)(2,1)S(1)}, bf16[288,512]{1,0:T(8,128)(2,1)S(1)}, u32[]{:S(2)}, u32[]{:S(2)}) collective-permute-start(bf16[288,512]{1,0:T(8,128)(2,1)S(1)} %get-tuple-element.30), channel_id=1, source_target_pairs={{0,2},{2,4},{4,6},{6,8},{8,10},{10,12},{12,14},{1,3},{3,5},{5,7},{... | collective-permute-start | bytes 884744 | tf_op jit(solution)/shard_map/ppermute | solution.py:17
  21.6 14.8 %collective-permute-start.1 = (bf16[2,2,128,512]{3,2,1,0:T(8,128)(2,1)S(1)}, bf16[2,2,128,512]{3,2,1,0:T(8,128)(2,1)S(1)}, u32[]{:S(2)}, u32[]{:S(2)}) collective-permute-start(bf16[2,2,128,512]{3,2,1,0:T(8,128)(2,1)S(1)} %get-tuple-element.28), channel_id=1, source_target_pairs={{0,4},{2,6},{4,8},{6,10},{8,12},{10,14},{1,5},{3,7},{5,9},{7,11},{... | collective-permute-start | bytes 1572872 | tf_op jit(solution)/shard_map/ppermute | solution.py:17
  25.3 15.7 %copy-start.4 = (bf16[8,128,512]{2,1,0:T(8,128)(2,1)}, bf16[8,128,512]{2,1,0:T(8,128)(2,1)S(1)}, u32[]{:S(2)}) copy-start(bf16[8,128,512]{2,1,0:T(8,128)(2,1)S(1)} %broadcast_select_fusion.1) | copy-start | bytes 3145732
  25.3 15.5 %collective-permute-start.3 = (bf16[2,2,128,512]{3,2,1,0:T(8,128)(2,1)S(1)}, bf16[2,2,128,512]{3,2,1,0:T(8,128)(2,1)S(1)}, u32[]{:S(2)}, u32[]{:S(2)}) collective-permute-start(bf16[2,2,128,512]{3,2,1,0:T(8,128)(2,1)S(1)} %get-tuple-element.27), channel_id=1, source_target_pairs={{4,0},{6,2},{8,4},{10,6},{12,8},{14,10},{5,1},{7,3},{9,5},{11,7},{... | collective-permute-start | bytes 1572872 | tf_op jit(solution)/shard_map/ppermute | solution.py:17
  41.0 1.4 copy-start.6
  41.0 3.1 %copy-start.7 = (bf16[7,1,128,512]{3,2,1,0:T(8,128)(2,1)}, bf16[7,1,128,512]{3,2,1,0:T(8,128)(2,1)S(1)}, u32[]{:S(2)}) copy-start(bf16[7,1,128,512]{3,2,1,0:T(8,128)(2,1)S(1)} %get-tuple-element.11) | copy-start | bytes 2752516
  44.1 1.2 copy-start.1
  46.6 9.1 %copy-start.2 = (bf16[1,128,1024]{2,1,0:T(8,128)(2,1)S(1)}, bf16[1,128,1024]{2,1,0:T(8,128)(2,1)}, u32[]{:S(2)}) copy-start(bf16[1,128,1024]{2,1,0:T(8,128)(2,1)} %param.10) | copy-start | bytes 786436
  46.9 7.1 %collective-permute-start.5 = (bf16[30,1024]{1,0:T(8,128)(2,1)S(1)}, bf16[30,1024]{1,0:T(8,128)(2,1)S(1)}, u32[]{:S(2)}, u32[]{:S(2)}) collective-permute-start(bf16[30,1024]{1,0:T(8,128)(2,1)S(1)} %get-tuple-element.26), channel_id=1, source_target_pairs={{2,0},{4,2},{6,4},{8,6},{10,8},{12,10},{14,12},{3,1},{5,3},{7,5},{... | collective-permute-start | bytes 184328 | tf_op jit(solution)/shard_map/ppermute | solution.py:30
  48.8 6.7 %collective-permute-start.4 = (bf16[30,1024]{1,0:T(8,128)(2,1)S(1)}, bf16[30,1024]{1,0:T(8,128)(2,1)S(1)}, u32[]{:S(2)}, u32[]{:S(2)}) collective-permute-start(bf16[30,1024]{1,0:T(8,128)(2,1)S(1)} %get-tuple-element.25), channel_id=1, source_target_pairs={{0,2},{2,4},{4,6},{6,8},{8,10},{10,12},{12,14},{1,3},{3,5},{5,7},{... | collective-permute-start | bytes 184328 | tf_op jit(solution)/shard_map/ppermute | solution.py:28
  70.9 9.7 %collective-permute-start.6 = (bf16[1,8,34,1024]{3,1,2,0:T(8,128)(2,1)}, bf16[1,8,34,1024]{3,1,2,0:T(8,128)(2,1)}, u32[]{:S(2)}, u32[]{:S(2)}) collective-permute-start(bf16[1,8,34,1024]{3,1,2,0:T(8,128)(2,1)} %dynamic-slice_convert_fusion), channel_id=1, source_target_pairs={{0,1},{1,0},{2,3},{3,2},{4,5},{5,4},{6,7},{7,6},{8,9},{9,8},{10,11... | collective-permute-start | bytes 1671176 | tf_op jit(solution)/shard_map/ppermute | solution.py:68
  80.6 4.5 %copy-start.11 = (bf16[1024,896]{1,0:T(8,128)(2,1)}, bf16[1024,896]{1,0:T(8,128)(2,1)S(1)}, u32[]{:S(2)}) copy-start(bf16[1024,896]{1,0:T(8,128)(2,1)S(1)} %multiply_convert_fusion) | copy-start | bytes 5505028
  80.7 2.1 %copy-start.5 = (bf16[8,128,512]{2,1,0:T(8,128)(2,1)S(1)}, bf16[8,128,512]{2,1,0:T(8,128)(2,1)}, u32[]{:S(2)}) copy-start(bf16[8,128,512]{2,1,0:T(8,128)(2,1)} %copy-done.4) | copy-start | bytes 3145732
  82.5 2.6 %copy-start.8 = (bf16[896,512]{1,0:T(8,128)(2,1)S(1)}, bf16[896,512]{1,0:T(8,128)(2,1)}, u32[]{:S(2)}) copy-start(bf16[896,512]{1,0:T(8,128)(2,1)} %get-tuple-element.68) | copy-start | bytes 2752516
  82.5 9.1 %collective-permute-start.7 = (bf16[4,34,1024]{2,0,1:T(4,128)(2,1)S(1)}, bf16[4,34,1024]{2,0,1:T(4,128)(2,1)S(1)}, u32[]{:S(2)}, u32[]{:S(2)}) collective-permute-start(bf16[4,34,1024]{2,0,1:T(4,128)(2,1)S(1)} %fusion.17), channel_id=1, source_target_pairs={{0,2},{2,0},{4,6},{6,4},{8,10},{10,8},{12,14},{14,12},{1,3},{3,1},... | collective-permute-start | bytes 835592 | tf_op jit(solution)/shard_map/ppermute | solution.py:68
  92.7 6.2 %collective-permute-start.12 = (bf16[2,34,1024]{2,0,1:T(2,128)(2,1)}, bf16[2,34,1024]{2,0,1:T(2,128)(2,1)}, u32[]{:S(2)}, u32[]{:S(2)}) collective-permute-start(bf16[2,34,1024]{2,0,1:T(2,128)(2,1)} %dynamic-slice_convert_fusion.2), channel_id=1, source_target_pairs={{0,4},{2,6},{4,0},{6,2},{8,12},{10,14},{12,8},{14,10},{1,5},{3,7},... | collective-permute-start | bytes 417800 | tf_op jit(solution)/shard_map/ppermute | solution.py:68
  101.7 8.9 %collective-permute-start.13 = (bf16[1,34,1024]{2,0,1:T(2,128)(2,1)S(1)}, bf16[1,34,1024]{2,0,1:T(2,128)(2,1)S(1)}, u32[]{:S(2)}, u32[]{:S(2)}) collective-permute-start(bf16[1,34,1024]{2,0,1:T(2,128)(2,1)S(1)} %dynamic-slice_convert_fusion.3), channel_id=1, source_target_pairs={{0,8},{2,10},{4,12},{6,14},{8,0},{10,2},{12,4},{14,6},{1,9},{3,11}... | collective-permute-start | bytes 208904 | tf_op jit(solution)/shard_map/ppermute | solution.py:68
  111.7 7.9 %collective-permute-start.14 = (bf16[1,34,1024]{2,0,1:T(2,128)(2,1)S(1)}, bf16[1,34,1024]{2,0,1:T(2,128)(2,1)S(1)}, u32[]{:S(2)}, u32[]{:S(2)}) collective-permute-start(bf16[1,34,1024]{2,0,1:T(2,128)(2,1)S(1)} %add_convert_fusion.1), channel_id=1, source_target_pairs={{0,8},{2,10},{4,12},{6,14},{8,0},{10,2},{12,4},{14,6},{1,9},{3,11}... | collective-permute-start | bytes 208904 | tf_op jit(solution)/shard_map/ppermute | solution.py:68
  119.9 1.0 copy-start.3
  120.9 7.8 %collective-permute-start.15 = (bf16[2,34,1024]{2,0,1:T(2,128)(2,1)}, bf16[2,34,1024]{2,0,1:T(2,128)(2,1)}, u32[]{:S(2)}, u32[]{:S(2)}) collective-permute-start(bf16[2,34,1024]{2,0,1:T(2,128)(2,1)} %pad_maximum_fusion.8), channel_id=1, source_target_pairs={{0,4},{2,6},{4,0},{6,2},{8,12},{10,14},{12,8},{14,10},{1,5},{3,7},... | collective-permute-start | bytes 417800 | tf_op jit(solution)/shard_map/ppermute | solution.py:68
  122.7 15.7 %collective-permute-start.9 = (bf16[2,2,128,512]{3,2,1,0:T(8,128)(2,1)}, bf16[2,2,128,512]{3,2,1,0:T(8,128)(2,1)S(1)}, u32[]{:S(2)}, u32[]{:S(2)}) collective-permute-start(bf16[2,2,128,512]{3,2,1,0:T(8,128)(2,1)} %rev.3), channel_id=1, source_target_pairs={{4,0},{6,2},{8,4},{10,6},{12,8},{14,10},{5,1},{7,3},{9,5},{11,7},{... | collective-permute-start | bytes 1572872 | tf_op jit(solution)/shard_map/ppermute | solution.py:17
  123.9 15.7 %collective-permute-start.8 = (bf16[2,2,128,512]{3,2,1,0:T(8,128)(2,1)}, bf16[2,2,128,512]{3,2,1,0:T(8,128)(2,1)S(1)}, u32[]{:S(2)}, u32[]{:S(2)}) collective-permute-start(bf16[2,2,128,512]{3,2,1,0:T(8,128)(2,1)} %get-tuple-element.9), channel_id=1, source_target_pairs={{0,4},{2,6},{4,8},{6,10},{8,12},{10,14},{1,5},{3,7},{5,9},{7,11},{... | collective-permute-start | bytes 1572872 | tf_op jit(solution)/shard_map/ppermute | solution.py:17
  130.5 16.3 %collective-permute-start.16 = (bf16[4,34,1024]{2,0,1:T(4,128)(2,1)S(1)}, bf16[4,34,1024]{2,0,1:T(4,128)(2,1)S(1)}, u32[]{:S(2)}, u32[]{:S(2)}) collective-permute-start(bf16[4,34,1024]{2,0,1:T(4,128)(2,1)S(1)} %pad_maximum_fusion.7), channel_id=1, source_target_pairs={{0,2},{2,0},{4,6},{6,4},{8,10},{10,8},{12,14},{14,12},{1,3},{3,1},... | collective-permute-start | bytes 835592 | tf_op jit(solution)/shard_map/ppermute | solution.py:68
  140.0 9.7 %collective-permute-start.11 = (bf16[2,128,512]{2,1,0:T(8,128)(2,1)S(1)}, bf16[2,128,512]{2,1,0:T(8,128)(2,1)S(1)}, u32[]{:S(2)}, u32[]{:S(2)}) collective-permute-start(bf16[2,128,512]{2,1,0:T(8,128)(2,1)S(1)} %get-tuple-element.14), channel_id=1, source_target_pairs={{2,0},{4,2},{6,4},{8,6},{10,8},{12,10},{14,12},{3,1},{5,3},{7,5},{... | collective-permute-start | bytes 786440 | tf_op jit(solution)/shard_map/ppermute | solution.py:17
  141.9 13.3 %collective-permute-start.10 = (bf16[2,128,512]{2,1,0:T(8,128)(2,1)S(1)}, bf16[2,128,512]{2,1,0:T(8,128)(2,1)S(1)}, u32[]{:S(2)}, u32[]{:S(2)}) collective-permute-start(bf16[2,128,512]{2,1,0:T(8,128)(2,1)S(1)} %get-tuple-element.13), channel_id=1, source_target_pairs={{0,2},{2,4},{4,6},{6,8},{8,10},{10,12},{12,14},{1,3},{3,5},{5,7},{... | collective-permute-start | bytes 786440 | tf_op jit(solution)/shard_map/ppermute | solution.py:17
  147.5 8.7 %collective-permute-start.17 = (bf16[1,8,34,1024]{3,1,2,0:T(8,128)(2,1)S(1)}, bf16[1,8,34,1024]{3,1,2,0:T(8,128)(2,1)S(1)}, u32[]{:S(2)}, u32[]{:S(2)}) collective-permute-start(bf16[1,8,34,1024]{3,1,2,0:T(8,128)(2,1)S(1)} %maximum_bitcast_fusion), channel_id=1, source_target_pairs={{0,1},{1,0},{2,3},{3,2},{4,5},{5,4},{6,7},{7,6},{8,9},{9,8},{10,11... | collective-permute-start | bytes 1671176 | tf_op jit(solution)/shard_map/ppermute | solution.py:68

commit v14 on v12

--- a/solution.py
+++ b/solution.py
@@ -50,17 +50,11 @@
 
 
 def give_back(near, narrow, shifter):
-    from_below = shifter(narrow[REACH + 2 :], 2).astype(jnp.float32)
-    from_above = shifter(narrow[REACH - 2 :: -1], -2).astype(jnp.float32)
-    upward = (near[2] + from_below[1]).astype(jnp.bfloat16)
-    downward = (near[0] + from_above[1]).astype(jnp.bfloat16)
-    return (
-        near[1]
-        + from_below[0]
-        + from_above[0]
-        + shifter(upward, 1).astype(jnp.float32)
-        + shifter(downward, -1).astype(jnp.float32)
-    )
+    total = near[1]
+    for offset in range(2 * REACH + 1):
+        if offset != REACH:
+            total = total + shifter(narrow[offset], offset - REACH).astype(jnp.float32)
+    return total
 
 
 def exchange(block, axis, bit):

time: 151 us -> 162 us (1.073)
  waiting for transfers between devices: 55.3 us -> 81 us
  matrix products: 18.4 us -> 12.7 us
  local copies, waits for them, and re-layouts: 17.5 us -> 12.8 us
  other arithmetic: 18.1 us -> 13.5 us
    ppermute x8, waiting for transfers between devices: 18.4 us -> 35.5 us  [exchange(): return lax.ppermute(block, axis, [(i, i ^ bit) for i in range(count)])]
    ppermute x8 -> x10, waiting for transfers between devices: 35.4 us -> 43.9 us  [passed_along(): return lax.ppermute(block, axis, route)]
    dot_general x6, matrix products: 13.1 us -> 7.44 us  [contract(): lax.dot_general(lhs, rhs, (((lhs_dim,), (rhs_dim,)), ((), ())), preferred...]
    ppermute x8 -> x10, starting transfers between devices: 25.1 us -> 26.6 us  [passed_along(): return lax.ppermute(block, axis, route)]
    unnamed x39 -> x35, local copies, waits for them, and re-layouts: 3.33 us -> 2.33 us
  transfers between devices with their start and end apart: 18 -> 20, of which waited for: 13 -> 12; matrix products, arithmetic and copies ran while one was open for 16% -> 7% of each run, Pallas kernels for 0% -> 0%
where the time goes in v14:
time: 162 us; the launch traced here: 161 us
  waiting for transfers between devices  81 us (50%)
  starting transfers between devices  38.8 us (24%)
  other arithmetic  13.5 us (8%)
  local copies, waits for them, and re-layouts  12.8 us (8%)
  matrix products  12.7 us (8%)
  between operations  2.17 us (1%)
    ppermute x10, waiting for transfers between devices, passed_along(): return lax.ppermute(block, axis, route)  43.9 us
    ppermute x8, waiting for transfers between devices, exchange(): return lax.ppermute(block, axis, [(i, i ^ bit) for i in range(count)])  35.5 us
    ppermute x10, starting transfers between devices, passed_along(): return lax.ppermute(block, axis, route)  26.6 us
    dot_general x6, matrix products, contract(): lax.dot_general(lhs, rhs, (((lhs_dim,), (rhs_dim,)), ((), ())), preferred...  7.44 us
    ppermute x8, starting transfers between devices, exchange(): return lax.ppermute(block, axis, [(i, i ^ bit) for i in range(count)])  5.29 us
    ppermute x1, starting transfers between devices, padded(): lax.ppermute(tail, axis, [(i, (i + 1) % count) for i in range(ends)])  5 us
  transfers between devices with their start and end apart: 20, of which 12 were waited for; matrix products, arithmetic and copies ran while one was open for 7% of the time, Pallas kernels for 0%

profile of v14, /device:TPU:2, one launch (start us, length us, event | category | flops | bytes accessed | tf_op | source)
XLA Modules:
  0.0 161.0 jit_solution(6755406642775807989)
XLA Ops:
  0.6 0.9 slice_bitcast_fusion.2
  1.6 0.9 constant_dynamic-update-slice_fusion.1
  2.5 0.9 constant_dynamic-update-slice_fusion
  3.5 2.1 %collective-permute-start.2 = (bf16[288,512]{1,0:T(8,128)(2,1)S(1)}, bf16[288,512]{1,0:T(8,128)(2,1)S(1)}, u32[]{:S(2)}, u32[]{:S(2)}) collective-permute-start(bf16[288,512]{1,0:T(8,128)(2,1)S(1)} %get-tuple-element.27), channel_id=1, source_target_pairs={{2,0},{4,2},{6,4},{8,6},{10,8},{12,10},{14,12},{3,1},{5,3},{7,5},{... | collective-permute-start | bytes 884744 | tf_op jit(solution)/shard_map/ppermute | solution.py:17
  5.6 4.8 %collective-permute-start = (bf16[288,512]{1,0:T(8,128)(2,1)S(1)}, bf16[288,512]{1,0:T(8,128)(2,1)S(1)}, u32[]{:S(2)}, u32[]{:S(2)}) collective-permute-start(bf16[288,512]{1,0:T(8,128)(2,1)S(1)} %get-tuple-element.28), channel_id=1, source_target_pairs={{0,2},{2,4},{4,6},{6,8},{8,10},{10,12},{12,14},{1,3},{3,5},{5,7},{... | collective-permute-start | bytes 884744 | tf_op jit(solution)/shard_map/ppermute | solution.py:17
  11.1 4.2 %collective-permute-done.2 = bf16[288,512]{1,0:T(8,128)(2,1)S(1)} collective-permute-done((bf16[288,512]{1,0:T(8,128)(2,1)S(1)}, bf16[288,512]{1,0:T(8,128)(2,1)S(1)}, u32[]{:S(2)}, u32[]{:S(2)}) %collective-permute-start.2) | collective-permute-done | bytes 294944 | tf_op jit(solution)/shard_map/ppermute | solution.py:17
  15.3 6.2 %collective-permute-done = bf16[288,512]{1,0:T(8,128)(2,1)S(1)} collective-permute-done((bf16[288,512]{1,0:T(8,128)(2,1)S(1)}, bf16[288,512]{1,0:T(8,128)(2,1)S(1)}, u32[]{:S(2)}, u32[]{:S(2)}) %collective-permute-start) | collective-permute-done | bytes 294944 | tf_op jit(solution)/shard_map/ppermute | solution.py:17
  21.6 3.5 %collective-permute-start.1 = (bf16[2,2,128,512]{3,2,1,0:T(8,128)(2,1)S(1)}, bf16[2,2,128,512]{3,2,1,0:T(8,128)(2,1)S(1)}, u32[]{:S(2)}, u32[]{:S(2)}) collective-permute-start(bf16[2,2,128,512]{3,2,1,0:T(8,128)(2,1)S(1)} %get-tuple-element.26), channel_id=1, source_target_pairs={{0,4},{2,6},{4,8},{6,10},{8,12},{10,14},{1,5},{3,7},{5,9},{7,11},{... | collective-permute-start | bytes 1572872 | tf_op jit(solution)/shard_map/ppermute | solution.py:17
  25.3 1.3 collective-permute-start.3
  26.6 9.8 %collective-permute-done.1 = bf16[2,2,128,512]{3,2,1,0:T(8,128)(2,1)S(1)} collective-permute-done((bf16[2,2,128,512]{3,2,1,0:T(8,128)(2,1)S(1)}, bf16[2,2,128,512]{3,2,1,0:T(8,128)(2,1)S(1)}, u32[]{:S(2)}, u32[]{:S(2)}) %collective-permute-start.1) | collective-permute-done | bytes 524320 | tf_op jit(solution)/shard_map/ppermute | solution.py:17
  36.6 4.2 %collective-permute-done.3 = bf16[2,2,128,512]{3,2,1,0:T(8,128)(2,1)S(1)} collective-permute-done((bf16[2,2,128,512]{3,2,1,0:T(8,128)(2,1)S(1)}, bf16[2,2,128,512]{3,2,1,0:T(8,128)(2,1)S(1)}, u32[]{:S(2)}, u32[]{:S(2)}) %collective-permute-start.3) | collective-permute-done | bytes 524320 | tf_op jit(solution)/shard_map/ppermute | solution.py:17
  41.0 1.4 fusion
  42.4 0.9 exponential_reduce_fusion
  44.1 1.2 select_reduce_fusion.1
  45.7 1.9 %collective-permute-start.5 = (bf16[30,1024]{1,0:T(8,128)(2,1)S(1)}, bf16[30,1024]{1,0:T(8,128)(2,1)S(1)}, u32[]{:S(2)}, u32[]{:S(2)}) collective-permute-start(bf16[30,1024]{1,0:T(8,128)(2,1)S(1)} %get-tuple-element.24), channel_id=1, source_target_pairs={{2,0},{4,2},{6,4},{8,6},{10,8},{12,10},{14,12},{3,1},{5,3},{7,5},{... | collective-permute-start | bytes 184328 | tf_op jit(solution)/shard_map/ppermute | solution.py:30
  47.7 5.0 %collective-permute-start.4 = (bf16[30,1024]{1,0:T(8,128)(2,1)S(1)}, bf16[30,1024]{1,0:T(8,128)(2,1)S(1)}, u32[]{:S(2)}, u32[]{:S(2)}) collective-permute-start(bf16[30,1024]{1,0:T(8,128)(2,1)S(1)} %get-tuple-element.23), channel_id=1, source_target_pairs={{0,2},{2,4},{4,6},{6,8},{8,10},{10,12},{12,14},{1,3},{3,5},{5,7},{... | collective-permute-start | bytes 184328 | tf_op jit(solution)/shard_map/ppermute | solution.py:28
  52.8 1.6 collective-permute-done.4
  54.6 3.0 %multiply_convert_fusion.1 = bf16[158,1024]{1,0:T(8,128)(2,1)S(1)} fusion(bf16[188,1024]{1,0:T(8,128)(2,1)S(1)} %pad_maximum_fusion.3, bf16[15,1024]{1,0:T(8,128)(2,1)S(1)} %slice.422, bf16[128,1024]{1,0:T(8,128)(2,1)S(1)} %bitcast.150, bf16[15,1024]{1,0:T(8,128)(2,1)S(1)} %slice.420, bf16[128,1024]{1,0:T(8,128)(2,1)S(1)} %fusion.1, ...), kind=kLoop, calls=%fused_computation.19 | loop fusion | flops 18282496 | bytes 10543104 | tf_op jit(solution)/shard_map/convert_element_type | solution.py:170
  57.6 2.2 %add_convert_fusion = bf16[128,1024]{1,0:T(8,128)(2,1)S(1)} fusion(bf16[158,1024]{1,0:T(8,128)(2,1)S(1)} %multiply_convert_fusion.1, f32[1024]{0:T(1024)S(1)} %bitcast.223, f32[1024]{0:T(1024)S(1)} %bitcast.225, f32[1024]{0:T(1024)S(1)} %bitcast.167, f32[1024]{0:T(1024)S(1)} %bitcast.169, f32[1024]{0:T(1024)S(1)} %bitcast.171, f32[1024]{0:T(1024)S(1)} %bitcast.173, ...), kind=kLoop, calls=%fused_computation.39 | loop fusion | flops 12582912 | bytes 8777856 | tf_op jit(solution)/shard_map/convert_element_type | solution.py:188
  60.4 1.2 copy_dynamic-update-slice_fusion
  61.6 2.4 %fusion.3 = f32[1,31,1024]{2,0,1:T(1,128)S(1)} fusion(bf16[1,158,1024]{2,1,0:T(8,128)(2,1)S(1)} %slice_bitcast_fusion, bf16[128,1,1024]{2,0,1:T(8,128)(2,1)S(1)} %slice_bitcast_fusion.1), kind=kOutput, calls=%fused_computation.20 | convolution fusion | flops 8126464 | bytes 712704 | tf_op jit(solution)/shard_map/conv_general_dilated | solution.py:177
  64.7 1.6 %reshape.161 = f32[2,8,2,1024]{3,2,1,0:T(2,128)} reshape(f32[32,1024]{1,0:T(8,128)} %pad.13) | data formatting | bytes 262144 | tf_op jit(solution)/shard_map/reshape | solution.py:201
  66.3 0.9 copy_dynamic-update-slice_fusion.1
  67.3 0.9 dynamic-slice_convert_fusion
  68.2 2.2 %convert_multiply_fusion = (f32[128,512]{1,0:T(8,128)}, bf16[128,512]{1,0:T(8,128)(2,1)}) fusion(bf16[128,512]{1,0:T(8,128)(2,1)} %copy-done.4, bf16[128,1024]{1,0:T(8,128)(2,1)S(1)} %add_convert_fusion, bf16[512,1024]{1,0:T(8,128)(2,1)S(1)} %copy-done), kind=kOutput, calls=%fused_computation.63 | convolution fusion | flops 134479872 | bytes 1835008 | tf_op jit(solution)/shard_map/dot_general | solution.py:206
  70.4 1.1 copy.55
  71.5 1.3 convert_add_fusion
  73.1 8.9 %collective-permute-done.13 = bf16[4,34,1024]{2,0,1:T(4,128)(2,1)S(1)} collective-permute-done((bf16[4,34,1024]{2,0,1:T(4,128)(2,1)S(1)}, bf16[4,34,1024]{2,0,1:T(4,128)(2,1)S(1)}, u32[]{:S(2)}, u32[]{:S(2)}) %collective-permute-start.13) | collective-permute-done | bytes 278560 | tf_op jit(solution)/shard_map/ppermute | solution.py:62
  82.4 2.1 %collective-permute-start.14 = (bf16[2,34,1024]{2,0,1:T(2,128)(2,1)S(1)}, bf16[2,34,1024]{2,0,1:T(2,128)(2,1)S(1)}, u32[]{:S(2)}, u32[]{:S(2)}) collective-permute-start(bf16[2,34,1024]{2,0,1:T(2,128)(2,1)S(1)} %dynamic-slice_convert_fusion.2), channel_id=1, source_target_pairs={{0,4},{2,6},{4,0},{6,2},{8,12},{10,14},{12,8},{14,10},{1,5},{3,7},... | collective-permute-start | bytes 417800 | tf_op jit(solution)/shard_map/ppermute | solution.py:62
  84.5 1.3 multiply_convert_fusion
  85.8 2.5 %collective-permute-done.14 = bf16[2,34,1024]{2,0,1:T(2,128)(2,1)S(1)} collective-permute-done((bf16[2,34,1024]{2,0,1:T(2,128)(2,1)S(1)}, bf16[2,34,1024]{2,0,1:T(2,128)(2,1)S(1)}, u32[]{:S(2)}, u32[]{:S(2)}) %collective-permute-start.14) | collective-permute-done | bytes 139296 | tf_op jit(solution)/shard_map/ppermute | solution.py:62
  88.6 2.8 %collective-permute-start.15 = (bf16[1,34,1024]{2,0,1:T(2,128)(2,1)S(1)}, bf16[1,34,1024]{2,0,1:T(2,128)(2,1)S(1)}, u32[]{:S(2)}, u32[]{:S(2)}) collective-permute-start(bf16[1,34,1024]{2,0,1:T(2,128)(2,1)S(1)} %dynamic-slice_convert_fusion.3), channel_id=1, source_target_pairs={{0,8},{2,10},{4,12},{6,14},{8,0},{10,2},{12,4},{14,6},{1,9},{3,11}... | collective-permute-start | bytes 208904 | tf_op jit(solution)/shard_map/ppermute | solution.py:62
  91.4 1.1 fusion.31
  92.6 5.0 %collective-permute-done.15 = bf16[1,34,1024]{2,0,1:T(2,128)(2,1)S(1)} collective-permute-done((bf16[1,34,1024]{2,0,1:T(2,128)(2,1)S(1)}, bf16[1,34,1024]{2,0,1:T(2,128)(2,1)S(1)}, u32[]{:S(2)}, u32[]{:S(2)}) %collective-permute-start.15) | collective-permute-done | bytes 69664 | tf_op jit(solution)/shard_map/ppermute | solution.py:62
  97.8 1.2 fusion.32
  99.0 6.7 %collective-permute-done.16 = bf16[1,34,1024]{2,0,1:T(2,128)(2,1)S(1)} collective-permute-done((bf16[1,34,1024]{2,0,1:T(2,128)(2,1)S(1)}, bf16[1,34,1024]{2,0,1:T(2,128)(2,1)S(1)}, u32[]{:S(2)}, u32[]{:S(2)}) %collective-permute-start.16) | collective-permute-done | bytes 69664 | tf_op jit(solution)/shard_map/ppermute | solution.py:62
  106.5 4.4 %collective-permute-start.11 = (bf16[2,128,512]{2,1,0:T(8,128)(2,1)S(1)}, bf16[2,128,512]{2,1,0:T(8,128)(2,1)S(1)}, u32[]{:S(2)}, u32[]{:S(2)}) collective-permute-start(bf16[2,128,512]{2,1,0:T(8,128)(2,1)S(1)} %get-tuple-element.10), channel_id=1, source_target_pairs={{0,6},{2,8},{4,10},{6,12},{8,14},{1,7},{3,9},{5,11},{7,13},{9,15},... | collective-permute-start | bytes 786440 | tf_op jit(solution)/shard_map/ppermute | solution.py:17
  110.8 1.9 %collective-permute-start.10 = (bf16[2,128,512]{2,1,0:T(8,128)(2,1)S(1)}, bf16[2,128,512]{2,1,0:T(8,128)(2,1)S(1)}, u32[]{:S(2)}, u32[]{:S(2)}) collective-permute-start(bf16[2,128,512]{2,1,0:T(8,128)(2,1)S(1)} %get-tuple-element.6), channel_id=1, source_target_pairs={{0,4},{2,6},{4,8},{6,10},{8,12},{10,14},{1,5},{3,7},{5,9},{7,11},{... | collective-permute-start | bytes 786440 | tf_op jit(solution)/shard_map/ppermute | solution.py:17
  112.8 3.5 %collective-permute-start.9 = (bf16[2,128,512]{2,1,0:T(8,128)(2,1)S(1)}, bf16[2,128,512]{2,1,0:T(8,128)(2,1)S(1)}, u32[]{:S(2)}, u32[]{:S(2)}) collective-permute-start(bf16[2,128,512]{2,1,0:T(8,128)(2,1)S(1)} %get-tuple-element.7), channel_id=1, source_target_pairs={{0,2},{2,4},{4,6},{6,8},{8,10},{10,12},{12,14},{1,3},{3,5},{5,7},{... | collective-permute-start | bytes 786440 | tf_op jit(solution)/shard_map/ppermute | solution.py:17
  116.3 2.6 %collective-permute-start.8 = (bf16[2,128,512]{2,1,0:T(8,128)(2,1)S(1)}, bf16[2,128,512]{2,1,0:T(8,128)(2,1)S(1)}, u32[]{:S(2)}, u32[]{:S(2)}) collective-permute-start(bf16[2,128,512]{2,1,0:T(8,128)(2,1)S(1)} %get-tuple-element.8), channel_id=1, source_target_pairs={{2,0},{4,2},{6,4},{8,6},{10,8},{12,10},{14,12},{3,1},{5,3},{7,5},{... | collective-permute-start | bytes 786440 | tf_op jit(solution)/shard_map/ppermute | solution.py:17
  119.7 1.2 select_reduce_fusion
  121.0 12.5 %collective-permute-done.18 = bf16[4,34,1024]{2,0,1:T(4,128)(2,1)S(1)} collective-permute-done((bf16[4,34,1024]{2,0,1:T(4,128)(2,1)S(1)}, bf16[4,34,1024]{2,0,1:T(4,128)(2,1)S(1)}, u32[]{:S(2)}, u32[]{:S(2)}) %collective-permute-start.18) | collective-permute-done | bytes 278560 | tf_op jit(solution)/shard_map/ppermute | solution.py:62
  133.5 1.3 collective-permute-start.7
  135.2 1.3 collective-permute-start.6
  137.7 7.7 %collective-permute-done.7 = bf16[2,128,512]{2,1,0:T(8,128)(2,1)S(1)} collective-permute-done((bf16[2,128,512]{2,1,0:T(8,128)(2,1)S(1)}, bf16[2,128,512]{2,1,0:T(8,128)(2,1)S(1)}, u32[]{:S(2)}, u32[]{:S(2)}) %collective-permute-start.7) | collective-permute-done | bytes 262176 | tf_op jit(solution)/shard_map/ppermute | solution.py:17
  145.4 11.8 %collective-permute-done.6 = bf16[2,128,512]{2,1,0:T(8,128)(2,1)S(1)} collective-permute-done((bf16[2,128,512]{2,1,0:T(8,128)(2,1)S(1)}, bf16[2,128,512]{2,1,0:T(8,128)(2,1)S(1)}, u32[]{:S(2)}, u32[]{:S(2)}) %collective-permute-start.6) | collective-permute-done | bytes 262176 | tf_op jit(solution)/shard_map/ppermute | solution.py:17
  157.5 0.7 fusion.27
  158.7 1.5 copy.64
  (102 shorter events, 9.2 us)
Async XLA Ops:
  0.6 44.7 %copy-start = (bf16[512,1024]{1,0:T(8,128)(2,1)S(1)}, bf16[512,1024]{1,0:T(8,128)(2,1)}, u32[]{:S(2)}) copy-start(bf16[512,1024]{1,0:T(8,128)(2,1)} %param.11) | copy-start | bytes 3145732
  3.4 21.7 %copy-start.13 = (f32[31,1024]{1,0:T(8,128)S(1)}, f32[31,1024]{1,0:T(8,128)}, u32[]{:S(2)}) copy-start(f32[31,1024]{1,0:T(8,128)} %param.12) | copy-start | bytes 380932
  3.5 21.8 %copy-start.12 = (bf16[1,128,512]{2,1,0:T(8,128)(2,1)S(1)}, bf16[1,128,512]{2,1,0:T(8,128)(2,1)}, u32[]{:S(2)}) copy-start(bf16[1,128,512]{2,1,0:T(8,128)(2,1)} %param.7) | copy-start | bytes 393220
  3.5 11.8 %collective-permute-start.2 = (bf16[288,512]{1,0:T(8,128)(2,1)S(1)}, bf16[288,512]{1,0:T(8,128)(2,1)S(1)}, u32[]{:S(2)}, u32[]{:S(2)}) collective-permute-start(bf16[288,512]{1,0:T(8,128)(2,1)S(1)} %get-tuple-element.27), channel_id=1, source_target_pairs={{2,0},{4,2},{6,4},{8,6},{10,8},{12,10},{14,12},{3,1},{5,3},{7,5},{... | collective-permute-start | bytes 884744 | tf_op jit(solution)/shard_map/ppermute | solution.py:17
  5.6 15.9 %collective-permute-start = (bf16[288,512]{1,0:T(8,128)(2,1)S(1)}, bf16[288,512]{1,0:T(8,128)(2,1)S(1)}, u32[]{:S(2)}, u32[]{:S(2)}) collective-permute-start(bf16[288,512]{1,0:T(8,128)(2,1)S(1)} %get-tuple-element.28), channel_id=1, source_target_pairs={{0,2},{2,4},{4,6},{6,8},{8,10},{10,12},{12,14},{1,3},{3,5},{5,7},{... | collective-permute-start | bytes 884744 | tf_op jit(solution)/shard_map/ppermute | solution.py:17
  21.6 14.8 %collective-permute-start.1 = (bf16[2,2,128,512]{3,2,1,0:T(8,128)(2,1)S(1)}, bf16[2,2,128,512]{3,2,1,0:T(8,128)(2,1)S(1)}, u32[]{:S(2)}, u32[]{:S(2)}) collective-permute-start(bf16[2,2,128,512]{3,2,1,0:T(8,128)(2,1)S(1)} %get-tuple-element.26), channel_id=1, source_target_pairs={{0,4},{2,6},{4,8},{6,10},{8,12},{10,14},{1,5},{3,7},{5,9},{7,11},{... | collective-permute-start | bytes 1572872 | tf_op jit(solution)/shard_map/ppermute | solution.py:17
  25.3 15.7 %copy-start.5 = (bf16[8,128,512]{2,1,0:T(8,128)(2,1)}, bf16[8,128,512]{2,1,0:T(8,128)(2,1)S(1)}, u32[]{:S(2)}) copy-start(bf16[8,128,512]{2,1,0:T(8,128)(2,1)S(1)} %broadcast_select_fusion.1) | copy-start | bytes 3145732
  25.3 15.5 %collective-permute-start.3 = (bf16[2,2,128,512]{3,2,1,0:T(8,128)(2,1)S(1)}, bf16[2,2,128,512]{3,2,1,0:T(8,128)(2,1)S(1)}, u32[]{:S(2)}, u32[]{:S(2)}) collective-permute-start(bf16[2,2,128,512]{3,2,1,0:T(8,128)(2,1)S(1)} %get-tuple-element.25), channel_id=1, source_target_pairs={{4,0},{6,2},{8,4},{10,6},{12,8},{14,10},{5,1},{7,3},{9,5},{11,7},{... | collective-permute-start | bytes 1572872 | tf_op jit(solution)/shard_map/ppermute | solution.py:17
  41.0 1.4 copy-start.7
  41.0 3.1 %copy-start.9 = (bf16[7,1,128,512]{3,2,1,0:T(8,128)(2,1)}, bf16[7,1,128,512]{3,2,1,0:T(8,128)(2,1)S(1)}, u32[]{:S(2)}) copy-start(bf16[7,1,128,512]{3,2,1,0:T(8,128)(2,1)S(1)} %get-tuple-element.11) | copy-start | bytes 2752516
  44.1 1.3 copy-start.1
  45.4 14.6 %copy-start.4 = (bf16[128,512]{1,0:T(8,128)(2,1)}, bf16[128,512]{1,0:T(8,128)(2,1)S(1)}, u32[]{:S(2)}) copy-start(bf16[128,512]{1,0:T(8,128)(2,1)S(1)} %select_reduce_fusion.1) | copy-start | bytes 393220
  45.4 9.2 %copy-start.3 = (bf16[1,128,1024]{2,1,0:T(8,128)(2,1)S(1)}, bf16[1,128,1024]{2,1,0:T(8,128)(2,1)}, u32[]{:S(2)}) copy-start(bf16[1,128,1024]{2,1,0:T(8,128)(2,1)} %param.10) | copy-start | bytes 786436
  45.7 7.1 %collective-permute-start.5 = (bf16[30,1024]{1,0:T(8,128)(2,1)S(1)}, bf16[30,1024]{1,0:T(8,128)(2,1)S(1)}, u32[]{:S(2)}, u32[]{:S(2)}) collective-permute-start(bf16[30,1024]{1,0:T(8,128)(2,1)S(1)} %get-tuple-element.24), channel_id=1, source_target_pairs={{2,0},{4,2},{6,4},{8,6},{10,8},{12,10},{14,12},{3,1},{5,3},{7,5},{... | collective-permute-start | bytes 184328 | tf_op jit(solution)/shard_map/ppermute | solution.py:30
  47.7 6.7 %collective-permute-start.4 = (bf16[30,1024]{1,0:T(8,128)(2,1)S(1)}, bf16[30,1024]{1,0:T(8,128)(2,1)S(1)}, u32[]{:S(2)}, u32[]{:S(2)}) collective-permute-start(bf16[30,1024]{1,0:T(8,128)(2,1)S(1)} %get-tuple-element.23), channel_id=1, source_target_pairs={{0,2},{2,4},{4,6},{6,8},{8,10},{10,12},{12,14},{1,3},{3,5},{5,7},{... | collective-permute-start | bytes 184328 | tf_op jit(solution)/shard_map/ppermute | solution.py:28
  68.2 3.3 %collective-permute-start.12 = (bf16[1,8,34,1024]{3,1,2,0:T(8,128)(2,1)}, bf16[1,8,34,1024]{3,1,2,0:T(8,128)(2,1)}, u32[]{:S(2)}, u32[]{:S(2)}) collective-permute-start(bf16[1,8,34,1024]{3,1,2,0:T(8,128)(2,1)} %dynamic-slice_convert_fusion), channel_id=1, source_target_pairs={{0,1},{1,0},{2,3},{3,2},{4,5},{5,4},{6,7},{7,6},{8,9},{9,8},{10,11... | collective-permute-start | bytes 1671176 | tf_op jit(solution)/shard_map/ppermute | solution.py:62
  71.4 1.6 copy-start.11
  72.8 11.8 %copy-start.2 = (bf16[1024,896]{1,0:T(8,128)(2,1)S(1)}, bf16[1024,896]{1,0:T(8,128)(2,1)}, u32[]{:S(2)}) copy-start(bf16[1024,896]{1,0:T(8,128)(2,1)} %copy-done.1) | copy-start | bytes 5505028
  72.8 11.8 %copy-start.10 = (bf16[7,1,128,512]{3,2,1,0:T(8,128)(2,1)S(1)}, bf16[7,1,128,512]{3,2,1,0:T(8,128)(2,1)}, u32[]{:S(2)}) copy-start(bf16[7,1,128,512]{3,2,1,0:T(8,128)(2,1)} %copy-done.9) | copy-start | bytes 2752516
  72.9 9.1 %collective-permute-start.13 = (bf16[4,34,1024]{2,0,1:T(4,128)(2,1)S(1)}, bf16[4,34,1024]{2,0,1:T(4,128)(2,1)S(1)}, u32[]{:S(2)}, u32[]{:S(2)}) collective-permute-start(bf16[4,34,1024]{2,0,1:T(4,128)(2,1)S(1)} %fusion.14), channel_id=1, source_target_pairs={{0,2},{2,0},{4,6},{6,4},{8,10},{10,8},{12,14},{14,12},{1,3},{3,1},... | collective-permute-start | bytes 835592 | tf_op jit(solution)/shard_map/ppermute | solution.py:62
  82.4 5.9 %collective-permute-start.14 = (bf16[2,34,1024]{2,0,1:T(2,128)(2,1)S(1)}, bf16[2,34,1024]{2,0,1:T(2,128)(2,1)S(1)}, u32[]{:S(2)}, u32[]{:S(2)}) collective-permute-start(bf16[2,34,1024]{2,0,1:T(2,128)(2,1)S(1)} %dynamic-slice_convert_fusion.2), channel_id=1, source_target_pairs={{0,4},{2,6},{4,0},{6,2},{8,12},{10,14},{12,8},{14,10},{1,5},{3,7},... | collective-permute-start | bytes 417800 | tf_op jit(solution)/shard_map/ppermute | solution.py:62
  88.6 9.2 %copy-start.6 = (bf16[8,128,512]{2,1,0:T(8,128)(2,1)S(1)}, bf16[8,128,512]{2,1,0:T(8,128)(2,1)}, u32[]{:S(2)}) copy-start(bf16[8,128,512]{2,1,0:T(8,128)(2,1)} %copy-done.5) | copy-start | bytes 3145732
  88.6 8.9 %collective-permute-start.15 = (bf16[1,34,1024]{2,0,1:T(2,128)(2,1)S(1)}, bf16[1,34,1024]{2,0,1:T(2,128)(2,1)S(1)}, u32[]{:S(2)}, u32[]{:S(2)}) collective-permute-start(bf16[1,34,1024]{2,0,1:T(2,128)(2,1)S(1)} %dynamic-slice_convert_fusion.3), channel_id=1, source_target_pairs={{0,8},{2,10},{4,12},{6,14},{8,0},{10,2},{12,4},{14,6},{1,9},{3,11}... | collective-permute-start | bytes 208904 | tf_op jit(solution)/shard_map/ppermute | solution.py:62
  97.7 7.9 %collective-permute-start.16 = (bf16[1,34,1024]{2,0,1:T(2,128)(2,1)S(1)}, bf16[1,34,1024]{2,0,1:T(2,128)(2,1)S(1)}, u32[]{:S(2)}, u32[]{:S(2)}) collective-permute-start(bf16[1,34,1024]{2,0,1:T(2,128)(2,1)S(1)} %add_convert_fusion.1), channel_id=1, source_target_pairs={{0,8},{2,10},{4,12},{6,14},{8,0},{10,2},{12,4},{14,6},{1,9},{3,11}... | collective-permute-start | bytes 208904 | tf_op jit(solution)/shard_map/ppermute | solution.py:62
  106.3 12.6 %collective-permute-start.17 = (bf16[2,34,1024]{2,0,1:T(2,128)(2,1)S(1)}, bf16[2,34,1024]{2,0,1:T(2,128)(2,1)S(1)}, u32[]{:S(2)}, u32[]{:S(2)}) collective-permute-start(bf16[2,34,1024]{2,0,1:T(2,128)(2,1)S(1)} %pad_maximum_fusion.8), channel_id=1, source_target_pairs={{0,4},{2,6},{4,0},{6,2},{8,12},{10,14},{12,8},{14,10},{1,5},{3,7},... | collective-permute-start | bytes 417800 | tf_op jit(solution)/shard_map/ppermute | solution.py:62
  106.3 13.4 %copy-start.8 = (bf16[7,1,128,512]{3,2,1,0:T(8,128)(2,1)S(1)}, bf16[7,1,128,512]{3,2,1,0:T(8,128)(2,1)}, u32[]{:S(2)}) copy-start(bf16[7,1,128,512]{3,2,1,0:T(8,128)(2,1)} %copy-done.7) | copy-start | bytes 2752516
  106.5 28.7 %collective-permute-start.11 = (bf16[2,128,512]{2,1,0:T(8,128)(2,1)S(1)}, bf16[2,128,512]{2,1,0:T(8,128)(2,1)S(1)}, u32[]{:S(2)}, u32[]{:S(2)}) collective-permute-start(bf16[2,128,512]{2,1,0:T(8,128)(2,1)S(1)} %get-tuple-element.10), channel_id=1, source_target_pairs={{0,6},{2,8},{4,10},{6,12},{8,14},{1,7},{3,9},{5,11},{7,13},{9,15},... | collective-permute-start | bytes 786440 | tf_op jit(solution)/shard_map/ppermute | solution.py:17
  110.8 25.9 %collective-permute-start.10 = (bf16[2,128,512]{2,1,0:T(8,128)(2,1)S(1)}, bf16[2,128,512]{2,1,0:T(8,128)(2,1)S(1)}, u32[]{:S(2)}, u32[]{:S(2)}) collective-permute-start(bf16[2,128,512]{2,1,0:T(8,128)(2,1)S(1)} %get-tuple-element.6), channel_id=1, source_target_pairs={{0,4},{2,6},{4,8},{6,10},{8,12},{10,14},{1,5},{3,7},{5,9},{7,11},{... | collective-permute-start | bytes 786440 | tf_op jit(solution)/shard_map/ppermute | solution.py:17
  112.8 24.9 %collective-permute-start.9 = (bf16[2,128,512]{2,1,0:T(8,128)(2,1)S(1)}, bf16[2,128,512]{2,1,0:T(8,128)(2,1)S(1)}, u32[]{:S(2)}, u32[]{:S(2)}) collective-permute-start(bf16[2,128,512]{2,1,0:T(8,128)(2,1)S(1)} %get-tuple-element.7), channel_id=1, source_target_pairs={{0,2},{2,4},{4,6},{6,8},{8,10},{10,12},{12,14},{1,3},{3,5},{5,7},{... | collective-permute-start | bytes 786440 | tf_op jit(solution)/shard_map/ppermute | solution.py:17
  116.3 21.4 %collective-permute-start.8 = (bf16[2,128,512]{2,1,0:T(8,128)(2,1)S(1)}, bf16[2,128,512]{2,1,0:T(8,128)(2,1)S(1)}, u32[]{:S(2)}, u32[]{:S(2)}) collective-permute-start(bf16[2,128,512]{2,1,0:T(8,128)(2,1)S(1)} %get-tuple-element.8), channel_id=1, source_target_pairs={{2,0},{4,2},{6,4},{8,6},{10,8},{12,10},{14,12},{3,1},{5,3},{7,5},{... | collective-permute-start | bytes 786440 | tf_op jit(solution)/shard_map/ppermute | solution.py:17
  119.6 13.8 %collective-permute-start.18 = (bf16[4,34,1024]{2,0,1:T(4,128)(2,1)S(1)}, bf16[4,34,1024]{2,0,1:T(4,128)(2,1)S(1)}, u32[]{:S(2)}, u32[]{:S(2)}) collective-permute-start(bf16[4,34,1024]{2,0,1:T(4,128)(2,1)S(1)} %pad_maximum_fusion.6), channel_id=1, source_target_pairs={{0,2},{2,0},{4,6},{6,4},{8,10},{10,8},{12,14},{14,12},{1,3},{3,1},... | collective-permute-start | bytes 835592 | tf_op jit(solution)/shard_map/ppermute | solution.py:62
  133.5 11.9 %collective-permute-start.7 = (bf16[2,128,512]{2,1,0:T(8,128)(2,1)S(1)}, bf16[2,128,512]{2,1,0:T(8,128)(2,1)S(1)}, u32[]{:S(2)}, u32[]{:S(2)}) collective-permute-start(bf16[2,128,512]{2,1,0:T(8,128)(2,1)S(1)} %get-tuple-element.9), channel_id=1, source_target_pairs={{4,0},{6,2},{8,4},{10,6},{12,8},{14,10},{5,1},{7,3},{9,5},{11,7},{... | collective-permute-start | bytes 786440 | tf_op jit(solution)/shard_map/ppermute | solution.py:17
  135.2 22.0 %collective-permute-start.6 = (bf16[2,128,512]{2,1,0:T(8,128)(2,1)S(1)}, bf16[2,128,512]{2,1,0:T(8,128)(2,1)S(1)}, u32[]{:S(2)}, u32[]{:S(2)}) collective-permute-start(bf16[2,128,512]{2,1,0:T(8,128)(2,1)S(1)} %get-tuple-element.5), channel_id=1, source_target_pairs={{6,0},{8,2},{10,4},{12,6},{14,8},{7,1},{9,3},{11,5},{13,7},{15,9},... | collective-permute-start | bytes 786440 | tf_op jit(solution)/shard_map/ppermute | solution.py:17
  136.8 21.4 %collective-permute-start.19 = (bf16[1,8,34,1024]{3,1,2,0:T(8,128)(2,1)S(1)}, bf16[1,8,34,1024]{3,1,2,0:T(8,128)(2,1)S(1)}, u32[]{:S(2)}, u32[]{:S(2)}) collective-permute-start(bf16[1,8,34,1024]{3,1,2,0:T(8,128)(2,1)S(1)} %maximum_bitcast_fusion), channel_id=1, source_target_pairs={{0,1},{1,0},{2,3},{3,2},{4,5},{5,4},{6,7},{7,6},{8,9},{9,8},{10,11... | collective-permute-start | bytes 1671176 | tf_op jit(solution)/shard_map/ppermute | solution.py:62

commit v15 on v12

--- a/solution.py
+++ b/solution.py
@@ -51,13 +51,13 @@
 
 def give_back(near, narrow, shifter):
     from_below = shifter(narrow[REACH + 2 :], 2).astype(jnp.float32)
-    from_above = shifter(narrow[REACH - 2 :: -1], -2).astype(jnp.float32)
+    from_above = shifter(narrow[: REACH - 1], -2).astype(jnp.float32)
     upward = (near[2] + from_below[1]).astype(jnp.bfloat16)
-    downward = (near[0] + from_above[1]).astype(jnp.bfloat16)
+    downward = (near[0] + from_above[0]).astype(jnp.bfloat16)
     return (
         near[1]
         + from_below[0]
-        + from_above[0]
+        + from_above[1]
         + shifter(upward, 1).astype(jnp.float32)
         + shifter(downward, -1).astype(jnp.float32)
     )

time: 151 us -> 148 us (0.980)
  waiting for transfers between devices: 55.3 us -> 60 us
  matrix products: 18.4 us -> 14.3 us
  local copies, waits for them, and re-layouts: 17.5 us -> 15.2 us
    dot_general x6, matrix products: 13.1 us -> 9.02 us  [contract(): lax.dot_general(lhs, rhs, (((lhs_dim,), (rhs_dim,)), ((), ())), preferred...]
    ppermute x8, waiting for transfers between devices: 35.4 us -> 38.8 us  [passed_along(): return lax.ppermute(block, axis, route)]
    unnamed x39 -> x37, local copies, waits for them, and re-layouts: 3.33 us -> 3.33 us
  transfers between devices with their start and end apart: 18 -> 18, of which waited for: 13 -> 13; matrix products, arithmetic and copies ran while one was open for 16% -> 11% of each run, Pallas kernels for 0% -> 0%
where the time goes in v15:
time: 148 us; the launch traced here: 147 us
  waiting for transfers between devices  60 us (41%)
  starting transfers between devices  38.9 us (26%)
  other arithmetic  16.7 us (11%)
  local copies, waits for them, and re-layouts  15.2 us (10%)
  matrix products  14.3 us (10%)
  between operations  2.18 us (1%)
    ppermute x8, waiting for transfers between devices, passed_along(): return lax.ppermute(block, axis, route)  38.8 us
    ppermute x8, starting transfers between devices, passed_along(): return lax.ppermute(block, axis, route)  25.2 us
    ppermute x8, waiting for transfers between devices, exchange(): return lax.ppermute(block, axis, [(i, i ^ bit) for i in range(count)])  19.6 us
    dot_general x6, matrix products, contract(): lax.dot_general(lhs, rhs, (((lhs_dim,), (rhs_dim,)), ((), ())), preferred...  9.02 us
    ppermute x8, starting transfers between devices, exchange(): return lax.ppermute(block, axis, [(i, i ^ bit) for i in range(count)])  6.7 us
    ppermute x1, starting transfers between devices, padded(): lax.ppermute(tail, axis, [(i, (i + 1) % count) for i in range(ends)])  5 us
    unnamed x37, local copies, waits for them, and re-layouts  3.33 us
    convert_element_type x1, other arithmetic, on_device(): grad_conv = (cot_wide.astype(jnp.float32) * (sigmoid_c + conv_out * sigmo...  3.04 us
  transfers between devices with their start and end apart: 18, of which 13 were waited for; matrix products, arithmetic and copies ran while one was open for 11% of the time, Pallas kernels for 0%

profile of v15, /device:TPU:2, one launch (start us, length us, event | category | flops | bytes accessed | tf_op | source)
XLA Modules:
  0.0 147.2 jit_solution(9696811315850782933)
XLA Ops:
  1.6 0.9 constant_dynamic-update-slice_fusion.1
  3.5 2.1 %collective-permute-start.2 = (bf16[288,512]{1,0:T(8,128)(2,1)S(1)}, bf16[288,512]{1,0:T(8,128)(2,1)S(1)}, u32[]{:S(2)}, u32[]{:S(2)}) collective-permute-start(bf16[288,512]{1,0:T(8,128)(2,1)S(1)} %get-tuple-element.25), channel_id=1, source_target_pairs={{2,0},{4,2},{6,4},{8,6},{10,8},{12,10},{14,12},{3,1},{5,3},{7,5},{... | collective-permute-start | bytes 884744 | tf_op jit(solution)/shard_map/ppermute | solution.py:17
  5.6 4.8 %collective-permute-start = (bf16[288,512]{1,0:T(8,128)(2,1)S(1)}, bf16[288,512]{1,0:T(8,128)(2,1)S(1)}, u32[]{:S(2)}, u32[]{:S(2)}) collective-permute-start(bf16[288,512]{1,0:T(8,128)(2,1)S(1)} %get-tuple-element.26), channel_id=1, source_target_pairs={{0,2},{2,4},{4,6},{6,8},{8,10},{10,12},{12,14},{1,3},{3,5},{5,7},{... | collective-permute-start | bytes 884744 | tf_op jit(solution)/shard_map/ppermute | solution.py:17
  11.1 4.2 %collective-permute-done.2 = bf16[288,512]{1,0:T(8,128)(2,1)S(1)} collective-permute-done((bf16[288,512]{1,0:T(8,128)(2,1)S(1)}, bf16[288,512]{1,0:T(8,128)(2,1)S(1)}, u32[]{:S(2)}, u32[]{:S(2)}) %collective-permute-start.2) | collective-permute-done | bytes 294944 | tf_op jit(solution)/shard_map/ppermute | solution.py:17
  15.3 6.2 %collective-permute-done = bf16[288,512]{1,0:T(8,128)(2,1)S(1)} collective-permute-done((bf16[288,512]{1,0:T(8,128)(2,1)S(1)}, bf16[288,512]{1,0:T(8,128)(2,1)S(1)}, u32[]{:S(2)}, u32[]{:S(2)}) %collective-permute-start) | collective-permute-done | bytes 294944 | tf_op jit(solution)/shard_map/ppermute | solution.py:17
  21.6 3.5 %collective-permute-start.1 = (bf16[2,2,128,512]{3,2,1,0:T(8,128)(2,1)S(1)}, bf16[2,2,128,512]{3,2,1,0:T(8,128)(2,1)S(1)}, u32[]{:S(2)}, u32[]{:S(2)}) collective-permute-start(bf16[2,2,128,512]{3,2,1,0:T(8,128)(2,1)S(1)} %get-tuple-element.24), channel_id=1, source_target_pairs={{0,4},{2,6},{4,8},{6,10},{8,12},{10,14},{1,5},{3,7},{5,9},{7,11},{... | collective-permute-start | bytes 1572872 | tf_op jit(solution)/shard_map/ppermute | solution.py:17
  25.3 1.3 collective-permute-start.3
  26.6 9.8 %collective-permute-done.1 = bf16[2,2,128,512]{3,2,1,0:T(8,128)(2,1)S(1)} collective-permute-done((bf16[2,2,128,512]{3,2,1,0:T(8,128)(2,1)S(1)}, bf16[2,2,128,512]{3,2,1,0:T(8,128)(2,1)S(1)}, u32[]{:S(2)}, u32[]{:S(2)}) %collective-permute-start.1) | collective-permute-done | bytes 524320 | tf_op jit(solution)/shard_map/ppermute | solution.py:17
  36.6 4.2 %collective-permute-done.3 = bf16[2,2,128,512]{3,2,1,0:T(8,128)(2,1)S(1)} collective-permute-done((bf16[2,2,128,512]{3,2,1,0:T(8,128)(2,1)S(1)}, bf16[2,2,128,512]{3,2,1,0:T(8,128)(2,1)S(1)}, u32[]{:S(2)}, u32[]{:S(2)}) %collective-permute-start.3) | collective-permute-done | bytes 524320 | tf_op jit(solution)/shard_map/ppermute | solution.py:17
  41.0 1.4 fusion
  42.4 0.9 exponential_reduce_fusion
  44.1 1.2 select_reduce_fusion.1
  45.7 1.9 %collective-permute-start.5 = (bf16[30,1024]{1,0:T(8,128)(2,1)S(1)}, bf16[30,1024]{1,0:T(8,128)(2,1)S(1)}, u32[]{:S(2)}, u32[]{:S(2)}) collective-permute-start(bf16[30,1024]{1,0:T(8,128)(2,1)S(1)} %get-tuple-element.22), channel_id=1, source_target_pairs={{2,0},{4,2},{6,4},{8,6},{10,8},{12,10},{14,12},{3,1},{5,3},{7,5},{... | collective-permute-start | bytes 184328 | tf_op jit(solution)/shard_map/ppermute | solution.py:30
  47.7 5.0 %collective-permute-start.4 = (bf16[30,1024]{1,0:T(8,128)(2,1)S(1)}, bf16[30,1024]{1,0:T(8,128)(2,1)S(1)}, u32[]{:S(2)}, u32[]{:S(2)}) collective-permute-start(bf16[30,1024]{1,0:T(8,128)(2,1)S(1)} %get-tuple-element.21), channel_id=1, source_target_pairs={{0,2},{2,4},{4,6},{6,8},{8,10},{10,12},{12,14},{1,3},{3,5},{5,7},{... | collective-permute-start | bytes 184328 | tf_op jit(solution)/shard_map/ppermute | solution.py:28
  52.8 1.6 %collective-permute-done.4 = bf16[30,1024]{1,0:T(8,128)(2,1)S(1)} collective-permute-done((bf16[30,1024]{1,0:T(8,128)(2,1)S(1)}, bf16[30,1024]{1,0:T(8,128)(2,1)S(1)}, u32[]{:S(2)}, u32[]{:S(2)}) %collective-permute-start.4) | collective-permute-done | bytes 61472 | tf_op jit(solution)/shard_map/ppermute | solution.py:28
  54.6 3.0 %multiply_convert_fusion.1 = bf16[158,1024]{1,0:T(8,128)(2,1)S(1)} fusion(bf16[188,1024]{1,0:T(8,128)(2,1)S(1)} %pad_maximum_fusion.5, bf16[15,1024]{1,0:T(8,128)(2,1)S(1)} %slice.428, bf16[128,1024]{1,0:T(8,128)(2,1)S(1)} %bitcast.136, bf16[15,1024]{1,0:T(8,128)(2,1)S(1)} %slice.426, bf16[128,1024]{1,0:T(8,128)(2,1)S(1)} %fusion.1, ...), kind=kLoop, calls=%fused_computation.23 | loop fusion | flops 18282496 | bytes 10543104 | tf_op jit(solution)/shard_map/convert_element_type | solution.py:176
  57.6 2.2 %add_convert_fusion = bf16[128,1024]{1,0:T(8,128)(2,1)S(1)} fusion(bf16[158,1024]{1,0:T(8,128)(2,1)S(1)} %multiply_convert_fusion.1, f32[1024]{0:T(1024)S(1)} %bitcast.209, f32[1024]{0:T(1024)S(1)} %bitcast.211, f32[1024]{0:T(1024)S(1)} %bitcast.153, f32[1024]{0:T(1024)S(1)} %bitcast.155, f32[1024]{0:T(1024)S(1)} %bitcast.157, f32[1024]{0:T(1024)S(1)} %bitcast.159, ...), kind=kLoop, calls=%fused_computation.49 | loop fusion | flops 12582912 | bytes 8777856 | tf_op jit(solution)/shard_map/convert_element_type | solution.py:194
  60.4 1.2 copy_dynamic-update-slice_fusion
  61.6 2.4 %fusion.3 = f32[1,31,1024]{2,0,1:T(1,128)S(1)} fusion(bf16[1,158,1024]{2,1,0:T(8,128)(2,1)S(1)} %slice_bitcast_fusion, bf16[128,1,1024]{2,0,1:T(8,128)(2,1)S(1)} %slice_bitcast_fusion.1), kind=kOutput, calls=%fused_computation.24 | convolution fusion | flops 8126464 | bytes 712704 | tf_op jit(solution)/shard_map/conv_general_dilated | solution.py:183
  64.7 1.6 %reshape.167 = f32[2,8,2,1024]{3,2,1,0:T(2,128)} reshape(f32[32,1024]{1,0:T(8,128)} %pad.13) | data formatting | bytes 262144 | tf_op jit(solution)/shard_map/reshape | solution.py:207
  66.3 0.9 copy_dynamic-update-slice_fusion.1
  68.2 2.3 %collective-permute-done.10 = bf16[1,8,34,1024]{3,1,2,0:T(8,128)(2,1)} collective-permute-done((bf16[1,8,34,1024]{3,1,2,0:T(8,128)(2,1)}, bf16[1,8,34,1024]{3,1,2,0:T(8,128)(2,1)}, u32[]{:S(2)}, u32[]{:S(2)}) %collective-permute-start.10) | collective-permute-done | bytes 557088 | tf_op jit(solution)/shard_map/ppermute | solution.py:68
  70.5 1.2 convert_add_fusion
  71.8 1.0 copy-done.1
  73.0 2.2 %convert_multiply_fusion = (f32[128,512]{1,0:T(8,128)}, bf16[128,512]{1,0:T(8,128)(2,1)S(1)}) fusion(bf16[128,512]{1,0:T(8,128)(2,1)} %copy-done.6, bf16[128,1024]{1,0:T(8,128)(2,1)S(1)} %add_convert_fusion, bf16[512,1024]{1,0:T(8,128)(2,1)S(1)} %copy-done), kind=kOutput, calls=%fused_computation.67 | convolution fusion | flops 134479872 | bytes 1835008 | tf_op jit(solution)/shard_map/dot_general | solution.py:212
  75.2 6.5 %collective-permute-done.11 = bf16[4,34,1024]{2,0,1:T(4,128)(2,1)S(1)} collective-permute-done((bf16[4,34,1024]{2,0,1:T(4,128)(2,1)S(1)}, bf16[4,34,1024]{2,0,1:T(4,128)(2,1)S(1)}, u32[]{:S(2)}, u32[]{:S(2)}) %collective-permute-start.11) | collective-permute-done | bytes 278560 | tf_op jit(solution)/shard_map/ppermute | solution.py:68
  82.7 2.1 %collective-permute-start.12 = (bf16[2,34,1024]{2,0,1:T(2,128)(2,1)}, bf16[2,34,1024]{2,0,1:T(2,128)(2,1)}, u32[]{:S(2)}, u32[]{:S(2)}) collective-permute-start(bf16[2,34,1024]{2,0,1:T(2,128)(2,1)} %dynamic-slice_convert_fusion.2), channel_id=1, source_target_pairs={{0,4},{2,6},{4,0},{6,2},{8,12},{10,14},{12,8},{14,10},{1,5},{3,7},... | collective-permute-start | bytes 417800 | tf_op jit(solution)/shard_map/ppermute | solution.py:68
  84.7 1.0 broadcast_select_fusion
  85.8 1.8 %copy.55 = f32[128,512]{0,1:T(8,128)} copy(f32[128,512]{1,0:T(8,128)} %get-tuple-element.62) | data formatting | bytes 524288 | tf_op jit(solution)/shard_map/mul | solution.py:216
  87.6 1.0 bitcast_reduce_fusion
  88.5 1.1 convert_add_fusion.1
  89.8 2.7 %collective-permute-start.13 = (bf16[1,34,1024]{2,0,1:T(2,128)(2,1)S(1)}, bf16[1,34,1024]{2,0,1:T(2,128)(2,1)S(1)}, u32[]{:S(2)}, u32[]{:S(2)}) collective-permute-start(bf16[1,34,1024]{2,0,1:T(2,128)(2,1)S(1)} %dynamic-slice_convert_fusion.3), channel_id=1, source_target_pairs={{0,8},{2,10},{4,12},{6,14},{8,0},{10,2},{12,4},{14,6},{1,9},{3,11}... | collective-permute-start | bytes 208904 | tf_op jit(solution)/shard_map/ppermute | solution.py:68
  92.5 2.9 %multiply_convert_fusion = bf16[1024,896]{1,0:T(8,128)(2,1)S(1)} fusion(bf16[1024,896]{1,0:T(8,128)(2,1)S(1)} %copy-done.4, bf16[1024,512]{1,0:T(8,128)(2,1)} %bitcast.139, bf16[896,512]{1,0:T(8,128)(2,1)} %bitcast.145, f32[1024]{0:T(1024)S(1)} %bitcast.212), kind=kOutput, calls=%fused_computation | convolution fusion | flops 943194112 | bytes 5640192 | tf_op jit(solution)/shard_map/dot_general | solution.py:153
  95.3 3.2 %collective-permute-done.13 = bf16[1,34,1024]{2,0,1:T(2,128)(2,1)S(1)} collective-permute-done((bf16[1,34,1024]{2,0,1:T(2,128)(2,1)S(1)}, bf16[1,34,1024]{2,0,1:T(2,128)(2,1)S(1)}, u32[]{:S(2)}, u32[]{:S(2)}) %collective-permute-start.13) | collective-permute-done | bytes 69664 | tf_op jit(solution)/shard_map/ppermute | solution.py:68
  98.9 1.1 fusion.35
  100.0 7.6 %collective-permute-done.14 = bf16[1,34,1024]{2,0,1:T(2,128)(2,1)S(1)} collective-permute-done((bf16[1,34,1024]{2,0,1:T(2,128)(2,1)S(1)}, bf16[1,34,1024]{2,0,1:T(2,128)(2,1)S(1)}, u32[]{:S(2)}, u32[]{:S(2)}) %collective-permute-start.14) | collective-permute-done | bytes 69664 | tf_op jit(solution)/shard_map/ppermute | solution.py:68
  108.4 1.2 fusion.36
  109.6 1.4 collective-permute-start.7
  111.1 4.8 %collective-permute-start.6 = (bf16[2,2,128,512]{3,2,1,0:T(8,128)(2,1)S(1)}, bf16[2,2,128,512]{3,2,1,0:T(8,128)(2,1)S(1)}, u32[]{:S(2)}, u32[]{:S(2)}) collective-permute-start(bf16[2,2,128,512]{3,2,1,0:T(8,128)(2,1)S(1)} %get-tuple-element.5), channel_id=1, source_target_pairs={{0,4},{2,6},{4,8},{6,10},{8,12},{10,14},{1,5},{3,7},{5,9},{7,11},{... | collective-permute-start | bytes 1572872 | tf_op jit(solution)/shard_map/ppermute | solution.py:17
  116.6 1.6 %collective-permute-start.16 = (bf16[4,34,1024]{2,0,1:T(4,128)(2,1)S(1)}, bf16[4,34,1024]{2,0,1:T(4,128)(2,1)S(1)}, u32[]{:S(2)}, u32[]{:S(2)}) collective-permute-start(bf16[4,34,1024]{2,0,1:T(4,128)(2,1)S(1)} %pad_maximum_fusion.8), channel_id=1, source_target_pairs={{0,2},{2,0},{4,6},{6,4},{8,10},{10,8},{12,14},{14,12},{1,3},{3,1},... | collective-permute-start | bytes 835592 | tf_op jit(solution)/shard_map/ppermute | solution.py:68
  118.3 1.2 select_reduce_fusion
  119.7 5.8 %collective-permute-done.7 = bf16[2,2,128,512]{3,2,1,0:T(8,128)(2,1)S(1)} collective-permute-done((bf16[2,2,128,512]{3,2,1,0:T(8,128)(2,1)S(1)}, bf16[2,2,128,512]{3,2,1,0:T(8,128)(2,1)S(1)}, u32[]{:S(2)}, u32[]{:S(2)}) %collective-permute-start.7) | collective-permute-done | bytes 524320 | tf_op jit(solution)/shard_map/ppermute | solution.py:17
  125.6 1.1 collective-permute-done.6
  127.1 3.5 %collective-permute-start.9 = (bf16[2,128,512]{2,1,0:T(8,128)(2,1)S(1)}, bf16[2,128,512]{2,1,0:T(8,128)(2,1)S(1)}, u32[]{:S(2)}, u32[]{:S(2)}) collective-permute-start(bf16[2,128,512]{2,1,0:T(8,128)(2,1)S(1)} %get-tuple-element.10), channel_id=1, source_target_pairs={{2,0},{4,2},{6,4},{8,6},{10,8},{12,10},{14,12},{3,1},{5,3},{7,5},{... | collective-permute-start | bytes 786440 | tf_op jit(solution)/shard_map/ppermute | solution.py:17
  130.6 3.8 %collective-permute-start.8 = (bf16[2,128,512]{2,1,0:T(8,128)(2,1)S(1)}, bf16[2,128,512]{2,1,0:T(8,128)(2,1)S(1)}, u32[]{:S(2)}, u32[]{:S(2)}) collective-permute-start(bf16[2,128,512]{2,1,0:T(8,128)(2,1)S(1)} %get-tuple-element.9), channel_id=1, source_target_pairs={{0,2},{2,4},{4,6},{6,8},{8,10},{10,12},{12,14},{1,3},{3,5},{5,7},{... | collective-permute-start | bytes 786440 | tf_op jit(solution)/shard_map/ppermute | solution.py:17
  135.9 2.0 %collective-permute-done.9 = bf16[2,128,512]{2,1,0:T(8,128)(2,1)S(1)} collective-permute-done((bf16[2,128,512]{2,1,0:T(8,128)(2,1)S(1)}, bf16[2,128,512]{2,1,0:T(8,128)(2,1)S(1)}, u32[]{:S(2)}, u32[]{:S(2)}) %collective-permute-start.9) | collective-permute-done | bytes 262176 | tf_op jit(solution)/shard_map/ppermute | solution.py:17
  137.9 5.5 %collective-permute-done.8 = bf16[2,128,512]{2,1,0:T(8,128)(2,1)S(1)} collective-permute-done((bf16[2,128,512]{2,1,0:T(8,128)(2,1)S(1)}, bf16[2,128,512]{2,1,0:T(8,128)(2,1)S(1)}, u32[]{:S(2)}, u32[]{:S(2)}) %collective-permute-start.8) | collective-permute-done | bytes 262176 | tf_op jit(solution)/shard_map/ppermute | solution.py:17
  144.9 1.5 %copy.64 = bf16[2,8,32,1024]{3,2,1,0:T(8,128)(2,1)} copy(bf16[2,8,32,1024]{3,1,2,0:T(8,128)(2,1)S(1)} %fusion.2) | data formatting | bytes 2097152 | tf_op jit(solution)/shard_map/slice | solution.py:242
  (103 shorter events, 13.3 us)
Async XLA Ops:
  0.6 44.7 %copy-start = (bf16[512,1024]{1,0:T(8,128)(2,1)S(1)}, bf16[512,1024]{1,0:T(8,128)(2,1)}, u32[]{:S(2)}) copy-start(bf16[512,1024]{1,0:T(8,128)(2,1)} %param.11) | copy-start | bytes 3145732
  3.4 21.7 %copy-start.14 = (f32[31,1024]{1,0:T(8,128)S(1)}, f32[31,1024]{1,0:T(8,128)}, u32[]{:S(2)}) copy-start(f32[31,1024]{1,0:T(8,128)} %param.12) | copy-start | bytes 380932
  3.5 21.8 %copy-start.13 = (bf16[1,128,512]{2,1,0:T(8,128)(2,1)S(1)}, bf16[1,128,512]{2,1,0:T(8,128)(2,1)}, u32[]{:S(2)}) copy-start(bf16[1,128,512]{2,1,0:T(8,128)(2,1)} %param.7) | copy-start | bytes 393220
  3.5 11.8 %collective-permute-start.2 = (bf16[288,512]{1,0:T(8,128)(2,1)S(1)}, bf16[288,512]{1,0:T(8,128)(2,1)S(1)}, u32[]{:S(2)}, u32[]{:S(2)}) collective-permute-start(bf16[288,512]{1,0:T(8,128)(2,1)S(1)} %get-tuple-element.25), channel_id=1, source_target_pairs={{2,0},{4,2},{6,4},{8,6},{10,8},{12,10},{14,12},{3,1},{5,3},{7,5},{... | collective-permute-start | bytes 884744 | tf_op jit(solution)/shard_map/ppermute | solution.py:17
  5.6 15.9 %collective-permute-start = (bf16[288,512]{1,0:T(8,128)(2,1)S(1)}, bf16[288,512]{1,0:T(8,128)(2,1)S(1)}, u32[]{:S(2)}, u32[]{:S(2)}) collective-permute-start(bf16[288,512]{1,0:T(8,128)(2,1)S(1)} %get-tuple-element.26), channel_id=1, source_target_pairs={{0,2},{2,4},{4,6},{6,8},{8,10},{10,12},{12,14},{1,3},{3,5},{5,7},{... | collective-permute-start | bytes 884744 | tf_op jit(solution)/shard_map/ppermute | solution.py:17
  21.6 14.8 %collective-permute-start.1 = (bf16[2,2,128,512]{3,2,1,0:T(8,128)(2,1)S(1)}, bf16[2,2,128,512]{3,2,1,0:T(8,128)(2,1)S(1)}, u32[]{:S(2)}, u32[]{:S(2)}) collective-permute-start(bf16[2,2,128,512]{3,2,1,0:T(8,128)(2,1)S(1)} %get-tuple-element.24), channel_id=1, source_target_pairs={{0,4},{2,6},{4,8},{6,10},{8,12},{10,14},{1,5},{3,7},{5,9},{7,11},{... | collective-permute-start | bytes 1572872 | tf_op jit(solution)/shard_map/ppermute | solution.py:17
  25.3 15.7 %copy-start.7 = (bf16[8,128,512]{2,1,0:T(8,128)(2,1)}, bf16[8,128,512]{2,1,0:T(8,128)(2,1)S(1)}, u32[]{:S(2)}) copy-start(bf16[8,128,512]{2,1,0:T(8,128)(2,1)S(1)} %broadcast_select_fusion.1) | copy-start | bytes 3145732
  25.3 15.5 %collective-permute-start.3 = (bf16[2,2,128,512]{3,2,1,0:T(8,128)(2,1)S(1)}, bf16[2,2,128,512]{3,2,1,0:T(8,128)(2,1)S(1)}, u32[]{:S(2)}, u32[]{:S(2)}) collective-permute-start(bf16[2,2,128,512]{3,2,1,0:T(8,128)(2,1)S(1)} %get-tuple-element.23), channel_id=1, source_target_pairs={{4,0},{6,2},{8,4},{10,6},{12,8},{14,10},{5,1},{7,3},{9,5},{11,7},{... | collective-permute-start | bytes 1572872 | tf_op jit(solution)/shard_map/ppermute | solution.py:17
  41.0 1.4 copy-start.10
  41.0 3.1 %copy-start.12 = (bf16[7,1,128,512]{3,2,1,0:T(8,128)(2,1)}, bf16[7,1,128,512]{3,2,1,0:T(8,128)(2,1)S(1)}, u32[]{:S(2)}) copy-start(bf16[7,1,128,512]{3,2,1,0:T(8,128)(2,1)S(1)} %get-tuple-element.7) | copy-start | bytes 2752516
  44.1 1.3 copy-start.3
  45.4 14.6 %copy-start.6 = (bf16[128,512]{1,0:T(8,128)(2,1)}, bf16[128,512]{1,0:T(8,128)(2,1)S(1)}, u32[]{:S(2)}) copy-start(bf16[128,512]{1,0:T(8,128)(2,1)S(1)} %select_reduce_fusion.1) | copy-start | bytes 393220
  45.4 9.2 %copy-start.5 = (bf16[1,128,1024]{2,1,0:T(8,128)(2,1)S(1)}, bf16[1,128,1024]{2,1,0:T(8,128)(2,1)}, u32[]{:S(2)}) copy-start(bf16[1,128,1024]{2,1,0:T(8,128)(2,1)} %param.10) | copy-start | bytes 786436
  45.7 7.1 %collective-permute-start.5 = (bf16[30,1024]{1,0:T(8,128)(2,1)S(1)}, bf16[30,1024]{1,0:T(8,128)(2,1)S(1)}, u32[]{:S(2)}, u32[]{:S(2)}) collective-permute-start(bf16[30,1024]{1,0:T(8,128)(2,1)S(1)} %get-tuple-element.22), channel_id=1, source_target_pairs={{2,0},{4,2},{6,4},{8,6},{10,8},{12,10},{14,12},{3,1},{5,3},{7,5},{... | collective-permute-start | bytes 184328 | tf_op jit(solution)/shard_map/ppermute | solution.py:30
  47.7 6.7 %collective-permute-start.4 = (bf16[30,1024]{1,0:T(8,128)(2,1)S(1)}, bf16[30,1024]{1,0:T(8,128)(2,1)S(1)}, u32[]{:S(2)}, u32[]{:S(2)}) collective-permute-start(bf16[30,1024]{1,0:T(8,128)(2,1)S(1)} %get-tuple-element.21), channel_id=1, source_target_pairs={{0,2},{2,4},{4,6},{6,8},{8,10},{10,12},{12,14},{1,3},{3,5},{5,7},{... | collective-permute-start | bytes 184328 | tf_op jit(solution)/shard_map/ppermute | solution.py:28
  68.2 2.3 %collective-permute-start.10 = (bf16[1,8,34,1024]{3,1,2,0:T(8,128)(2,1)}, bf16[1,8,34,1024]{3,1,2,0:T(8,128)(2,1)}, u32[]{:S(2)}, u32[]{:S(2)}) collective-permute-start(bf16[1,8,34,1024]{3,1,2,0:T(8,128)(2,1)} %dynamic-slice_convert_fusion), channel_id=1, source_target_pairs={{0,1},{1,0},{2,3},{3,2},{4,5},{5,4},{6,7},{7,6},{8,9},{9,8},{10,11... | collective-permute-start | bytes 1671176 | tf_op jit(solution)/shard_map/ppermute | solution.py:68
  71.7 1.0 copy-start.1
  72.9 8.8 %copy-start.2 = (f32[1,8,34,1024]{3,1,2,0:T(8,128)S(1)}, f32[1,8,34,1024]{3,1,2,0:T(8,128)}, u32[]{:S(2)}) copy-start(f32[1,8,34,1024]{3,1,2,0:T(8,128)} %copy-done.1) | copy-start | bytes 3342340
  72.9 8.8 %collective-permute-start.11 = (bf16[4,34,1024]{2,0,1:T(4,128)(2,1)S(1)}, bf16[4,34,1024]{2,0,1:T(4,128)(2,1)S(1)}, u32[]{:S(2)}, u32[]{:S(2)}) collective-permute-start(bf16[4,34,1024]{2,0,1:T(4,128)(2,1)S(1)} %fusion.17), channel_id=1, source_target_pairs={{0,2},{2,0},{4,6},{6,4},{8,10},{10,8},{12,14},{14,12},{1,3},{3,1},... | collective-permute-start | bytes 835592 | tf_op jit(solution)/shard_map/ppermute | solution.py:68
  81.8 10.6 %copy-start.4 = (bf16[1024,896]{1,0:T(8,128)(2,1)S(1)}, bf16[1024,896]{1,0:T(8,128)(2,1)}, u32[]{:S(2)}) copy-start(bf16[1024,896]{1,0:T(8,128)(2,1)} %copy-done.3) | copy-start | bytes 5505028
  82.7 5.9 %collective-permute-start.12 = (bf16[2,34,1024]{2,0,1:T(2,128)(2,1)}, bf16[2,34,1024]{2,0,1:T(2,128)(2,1)}, u32[]{:S(2)}, u32[]{:S(2)}) collective-permute-start(bf16[2,34,1024]{2,0,1:T(2,128)(2,1)} %dynamic-slice_convert_fusion.2), channel_id=1, source_target_pairs={{0,4},{2,6},{4,0},{6,2},{8,12},{10,14},{12,8},{14,10},{1,5},{3,7},... | collective-permute-start | bytes 417800 | tf_op jit(solution)/shard_map/ppermute | solution.py:68
  89.8 8.8 %collective-permute-start.13 = (bf16[1,34,1024]{2,0,1:T(2,128)(2,1)S(1)}, bf16[1,34,1024]{2,0,1:T(2,128)(2,1)S(1)}, u32[]{:S(2)}, u32[]{:S(2)}) collective-permute-start(bf16[1,34,1024]{2,0,1:T(2,128)(2,1)S(1)} %dynamic-slice_convert_fusion.3), channel_id=1, source_target_pairs={{0,8},{2,10},{4,12},{6,14},{8,0},{10,2},{12,4},{14,6},{1,9},{3,11}... | collective-permute-start | bytes 208904 | tf_op jit(solution)/shard_map/ppermute | solution.py:68
  92.5 6.4 %copy-start.9 = (bf16[8,128,512]{2,1,0:T(8,128)(2,1)S(1)}, bf16[8,128,512]{2,1,0:T(8,128)(2,1)}, u32[]{:S(2)}) copy-start(bf16[8,128,512]{2,1,0:T(8,128)(2,1)} %broadcast_select_fusion) | copy-start | bytes 3145732
  98.8 9.6 %copy-start.8 = (bf16[8,128,512]{2,1,0:T(8,128)(2,1)S(1)}, bf16[8,128,512]{2,1,0:T(8,128)(2,1)}, u32[]{:S(2)}) copy-start(bf16[8,128,512]{2,1,0:T(8,128)(2,1)} %copy-done.7) | copy-start | bytes 3145732
  98.8 8.8 %collective-permute-start.14 = (bf16[1,34,1024]{2,0,1:T(2,128)(2,1)S(1)}, bf16[1,34,1024]{2,0,1:T(2,128)(2,1)S(1)}, u32[]{:S(2)}, u32[]{:S(2)}) collective-permute-start(bf16[1,34,1024]{2,0,1:T(2,128)(2,1)S(1)} %add_convert_fusion.1), channel_id=1, source_target_pairs={{0,8},{2,10},{4,12},{6,14},{8,0},{10,2},{12,4},{14,6},{1,9},{3,11}... | collective-permute-start | bytes 208904 | tf_op jit(solution)/shard_map/ppermute | solution.py:68
  108.3 7.6 %collective-permute-start.15 = (bf16[2,34,1024]{2,0,1:T(2,128)(2,1)S(1)}, bf16[2,34,1024]{2,0,1:T(2,128)(2,1)S(1)}, u32[]{:S(2)}, u32[]{:S(2)}) collective-permute-start(bf16[2,34,1024]{2,0,1:T(2,128)(2,1)S(1)} %pad_maximum_fusion.9), channel_id=1, source_target_pairs={{0,4},{2,6},{4,0},{6,2},{8,12},{10,14},{12,8},{14,10},{1,5},{3,7},... | collective-permute-start | bytes 417800 | tf_op jit(solution)/shard_map/ppermute | solution.py:68
  109.5 8.8 %copy-start.11 = (bf16[7,1,128,512]{3,2,1,0:T(8,128)(2,1)S(1)}, bf16[7,1,128,512]{3,2,1,0:T(8,128)(2,1)}, u32[]{:S(2)}) copy-start(bf16[7,1,128,512]{3,2,1,0:T(8,128)(2,1)} %copy-done.10) | copy-start | bytes 2752516
  109.6 15.9 %collective-permute-start.7 = (bf16[2,2,128,512]{3,2,1,0:T(8,128)(2,1)S(1)}, bf16[2,2,128,512]{3,2,1,0:T(8,128)(2,1)S(1)}, u32[]{:S(2)}, u32[]{:S(2)}) collective-permute-start(bf16[2,2,128,512]{3,2,1,0:T(8,128)(2,1)S(1)} %get-tuple-element.6), channel_id=1, source_target_pairs={{4,0},{6,2},{8,4},{10,6},{12,8},{14,10},{5,1},{7,3},{9,5},{11,7},{... | collective-permute-start | bytes 1572872 | tf_op jit(solution)/shard_map/ppermute | solution.py:17
  111.1 15.6 %collective-permute-start.6 = (bf16[2,2,128,512]{3,2,1,0:T(8,128)(2,1)S(1)}, bf16[2,2,128,512]{3,2,1,0:T(8,128)(2,1)S(1)}, u32[]{:S(2)}, u32[]{:S(2)}) collective-permute-start(bf16[2,2,128,512]{3,2,1,0:T(8,128)(2,1)S(1)} %get-tuple-element.5), channel_id=1, source_target_pairs={{0,4},{2,6},{4,8},{6,10},{8,12},{10,14},{1,5},{3,7},{5,9},{7,11},{... | collective-permute-start | bytes 1572872 | tf_op jit(solution)/shard_map/ppermute | solution.py:17
  116.6 17.8 %collective-permute-start.16 = (bf16[4,34,1024]{2,0,1:T(4,128)(2,1)S(1)}, bf16[4,34,1024]{2,0,1:T(4,128)(2,1)S(1)}, u32[]{:S(2)}, u32[]{:S(2)}) collective-permute-start(bf16[4,34,1024]{2,0,1:T(4,128)(2,1)S(1)} %pad_maximum_fusion.8), channel_id=1, source_target_pairs={{0,2},{2,0},{4,6},{6,4},{8,10},{10,8},{12,14},{14,12},{1,3},{3,1},... | collective-permute-start | bytes 835592 | tf_op jit(solution)/shard_map/ppermute | solution.py:68
  127.1 10.9 %collective-permute-start.9 = (bf16[2,128,512]{2,1,0:T(8,128)(2,1)S(1)}, bf16[2,128,512]{2,1,0:T(8,128)(2,1)S(1)}, u32[]{:S(2)}, u32[]{:S(2)}) collective-permute-start(bf16[2,128,512]{2,1,0:T(8,128)(2,1)S(1)} %get-tuple-element.10), channel_id=1, source_target_pairs={{2,0},{4,2},{6,4},{8,6},{10,8},{12,10},{14,12},{3,1},{5,3},{7,5},{... | collective-permute-start | bytes 786440 | tf_op jit(solution)/shard_map/ppermute | solution.py:17
  130.6 12.9 %collective-permute-start.8 = (bf16[2,128,512]{2,1,0:T(8,128)(2,1)S(1)}, bf16[2,128,512]{2,1,0:T(8,128)(2,1)S(1)}, u32[]{:S(2)}, u32[]{:S(2)}) collective-permute-start(bf16[2,128,512]{2,1,0:T(8,128)(2,1)S(1)} %get-tuple-element.9), channel_id=1, source_target_pairs={{0,2},{2,4},{4,6},{6,8},{8,10},{10,12},{12,14},{1,3},{3,5},{5,7},{... | collective-permute-start | bytes 786440 | tf_op jit(solution)/shard_map/ppermute | solution.py:17
  135.2 9.2 %collective-permute-start.17 = (bf16[1,8,34,1024]{3,1,2,0:T(8,128)(2,1)S(1)}, bf16[1,8,34,1024]{3,1,2,0:T(8,128)(2,1)S(1)}, u32[]{:S(2)}, u32[]{:S(2)}) collective-permute-start(bf16[1,8,34,1024]{3,1,2,0:T(8,128)(2,1)S(1)} %maximum_bitcast_fusion), channel_id=1, source_target_pairs={{0,1},{1,0},{2,3},{3,2},{4,5},{5,4},{6,7},{7,6},{8,9},{9,8},{10,11... | collective-permute-start | bytes 1671176 | tf_op jit(solution)/shard_map/ppermute | solution.py:68

commit v16 on v15

--- a/solution.py
+++ b/solution.py
@@ -88,10 +88,11 @@
     acc = acc[None]
     for level in range(levels - 1, -1, -1):
         theirs = exchange(acc, axis, 1 << level)
-        first = (here >> level) % 2 == 0
-        acc = jnp.concatenate(
-            [jnp.where(first, acc, theirs), jnp.where(first, theirs, acc)], axis=0
-        )
+        mine = (here >> level) % 2
+        width = acc.shape[0]
+        joined = jnp.zeros((2 * width,) + acc.shape[1:], acc.dtype)
+        joined = lax.dynamic_update_slice_in_dim(joined, acc, mine * width, 0)
+        acc = lax.dynamic_update_slice_in_dim(joined, theirs, (1 - mine) * width, 0)
     return acc
 
 

time: 148 us -> 152 us (1.027)
  local copies, waits for them, and re-layouts: 15.2 us -> 21.1 us
  waiting for transfers between devices: 60 us -> 57.1 us
  matrix products: 14.3 us -> 17 us
    ppermute x8, waiting for transfers between devices: 38.8 us -> 27.8 us  [passed_along(): return lax.ppermute(block, axis, route)]
    ppermute x8, waiting for transfers between devices: 19.6 us -> 27.7 us  [exchange(): return lax.ppermute(block, axis, [(i, i ^ bit) for i in range(count)])]
    dynamic_update_slice x0 -> x8, local copies, waits for them, and re-layouts: none -> 6.11 us  [the longest x4 3.76 us: doubling(): acc = lax.dynamic_update_slice_in_dim(joined, theirs, (1 - mine) * width, 0)]
    dot_general x6, matrix products: 9.02 us -> 12.7 us  [contract(): lax.dot_general(lhs, rhs, (((lhs_dim,), (rhs_dim,)), ((), ())), preferred...]
    select_n x4 -> x0, other arithmetic: 1.58 us -> none  [the longest x3 1.18 us: doubling(): jnp.where(first, acc, theirs)]
    unnamed x37 -> x31, local copies, waits for them, and re-layouts: 3.33 us -> 2.65 us
  transfers between devices with their start and end apart: 18 -> 18, of which waited for: 13 -> 12; matrix products, arithmetic and copies ran while one was open for 11% -> 17% of each run, Pallas kernels for 0% -> 0%
where the time goes in v16:
time: 152 us; the launch traced here: 150 us
  waiting for transfers between devices  57.1 us (38%)
  starting transfers between devices  37.9 us (25%)
  local copies, waits for them, and re-layouts  21.1 us (14%)
  matrix products  17 us (11%)
  other arithmetic  15.2 us (10%)
  between operations  2.16 us (1%)
    ppermute x8, waiting for transfers between devices, passed_along(): return lax.ppermute(block, axis, route)  27.8 us
    ppermute x8, waiting for transfers between devices, exchange(): return lax.ppermute(block, axis, [(i, i ^ bit) for i in range(count)])  27.7 us
    ppermute x8, starting transfers between devices, passed_along(): return lax.ppermute(block, axis, route)  24.5 us
    dot_general x6, matrix products, contract(): lax.dot_general(lhs, rhs, (((lhs_dim,), (rhs_dim,)), ((), ())), preferred...  12.7 us
    ppermute x8, starting transfers between devices, exchange(): return lax.ppermute(block, axis, [(i, i ^ bit) for i in range(count)])  6.47 us
    ppermute x1, starting transfers between devices, padded(): lax.ppermute(tail, axis, [(i, (i + 1) % count) for i in range(ends)])  5 us
    dynamic_update_slice x4, local copies, waits for them, and re-layouts, doubling(): acc = lax.dynamic_update_slice_in_dim(joined, theirs, (1 - mine) * width, 0)  3.76 us
    convert_element_type x1, other arithmetic, on_device(): grad_conv = (cot_wide.astype(jnp.float32) * (sigmoid_c + conv_out * sigmo...  3.04 us
  transfers between devices with their start and end apart: 18, of which 12 were waited for; matrix products, arithmetic and copies ran while one was open for 17% of the time, Pallas kernels for 0%

profile of v16, /device:TPU:2, one launch (start us, length us, event | category | flops | bytes accessed | tf_op | source)
XLA Modules:
  0.0 150.4 jit_solution(515782403784302429)
XLA Ops:
  1.6 0.9 constant_dynamic-update-slice_fusion.1
  2.5 0.9 constant_dynamic-update-slice_fusion
  3.5 2.1 %collective-permute-start.2 = (bf16[288,512]{1,0:T(8,128)(2,1)S(1)}, bf16[288,512]{1,0:T(8,128)(2,1)S(1)}, u32[]{:S(2)}, u32[]{:S(2)}) collective-permute-start(bf16[288,512]{1,0:T(8,128)(2,1)S(1)} %get-tuple-element.17), channel_id=1, source_target_pairs={{2,0},{4,2},{6,4},{8,6},{10,8},{12,10},{14,12},{3,1},{5,3},{7,5},{... | collective-permute-start | bytes 884744 | tf_op jit(solution)/shard_map/ppermute | solution.py:17
  5.6 4.8 %collective-permute-start = (bf16[288,512]{1,0:T(8,128)(2,1)S(1)}, bf16[288,512]{1,0:T(8,128)(2,1)S(1)}, u32[]{:S(2)}, u32[]{:S(2)}) collective-permute-start(bf16[288,512]{1,0:T(8,128)(2,1)S(1)} %get-tuple-element.18), channel_id=1, source_target_pairs={{0,2},{2,4},{4,6},{6,8},{8,10},{10,12},{12,14},{1,3},{3,5},{5,7},{... | collective-permute-start | bytes 884744 | tf_op jit(solution)/shard_map/ppermute | solution.py:17
  11.1 4.2 %collective-permute-done.2 = bf16[288,512]{1,0:T(8,128)(2,1)S(1)} collective-permute-done((bf16[288,512]{1,0:T(8,128)(2,1)S(1)}, bf16[288,512]{1,0:T(8,128)(2,1)S(1)}, u32[]{:S(2)}, u32[]{:S(2)}) %collective-permute-start.2) | collective-permute-done | bytes 294944 | tf_op jit(solution)/shard_map/ppermute | solution.py:17
  15.3 6.2 %collective-permute-done = bf16[288,512]{1,0:T(8,128)(2,1)S(1)} collective-permute-done((bf16[288,512]{1,0:T(8,128)(2,1)S(1)}, bf16[288,512]{1,0:T(8,128)(2,1)S(1)}, u32[]{:S(2)}, u32[]{:S(2)}) %collective-permute-start) | collective-permute-done | bytes 294944 | tf_op jit(solution)/shard_map/ppermute | solution.py:17
  21.6 3.5 %collective-permute-start.1 = (bf16[2,2,128,512]{3,2,1,0:T(8,128)(2,1)S(1)}, bf16[2,2,128,512]{3,2,1,0:T(8,128)(2,1)S(1)}, u32[]{:S(2)}, u32[]{:S(2)}) collective-permute-start(bf16[2,2,128,512]{3,2,1,0:T(8,128)(2,1)S(1)} %get-tuple-element.16), channel_id=1, source_target_pairs={{0,4},{2,6},{4,8},{6,10},{8,12},{10,14},{1,5},{3,7},{5,9},{7,11},{... | collective-permute-start | bytes 1572872 | tf_op jit(solution)/shard_map/ppermute | solution.py:17
  25.3 1.3 collective-permute-start.3
  26.6 9.8 %collective-permute-done.1 = bf16[2,2,128,512]{3,2,1,0:T(8,128)(2,1)S(1)} collective-permute-done((bf16[2,2,128,512]{3,2,1,0:T(8,128)(2,1)S(1)}, bf16[2,2,128,512]{3,2,1,0:T(8,128)(2,1)S(1)}, u32[]{:S(2)}, u32[]{:S(2)}) %collective-permute-start.1) | collective-permute-done | bytes 524320 | tf_op jit(solution)/shard_map/ppermute | solution.py:17
  36.6 4.2 %collective-permute-done.3 = bf16[2,2,128,512]{3,2,1,0:T(8,128)(2,1)S(1)} collective-permute-done((bf16[2,2,128,512]{3,2,1,0:T(8,128)(2,1)S(1)}, bf16[2,2,128,512]{3,2,1,0:T(8,128)(2,1)S(1)}, u32[]{:S(2)}, u32[]{:S(2)}) %collective-permute-start.3) | collective-permute-done | bytes 524320 | tf_op jit(solution)/shard_map/ppermute | solution.py:17
  41.0 1.4 fusion
  42.4 0.9 exponential_reduce_fusion
  44.1 1.2 select_reduce_fusion.1
  45.7 1.9 %collective-permute-start.5 = (bf16[30,1024]{1,0:T(8,128)(2,1)S(1)}, bf16[30,1024]{1,0:T(8,128)(2,1)S(1)}, u32[]{:S(2)}, u32[]{:S(2)}) collective-permute-start(bf16[30,1024]{1,0:T(8,128)(2,1)S(1)} %get-tuple-element.14), channel_id=1, source_target_pairs={{2,0},{4,2},{6,4},{8,6},{10,8},{12,10},{14,12},{3,1},{5,3},{7,5},{... | collective-permute-start | bytes 184328 | tf_op jit(solution)/shard_map/ppermute | solution.py:30
  47.7 5.0 %collective-permute-start.4 = (bf16[30,1024]{1,0:T(8,128)(2,1)S(1)}, bf16[30,1024]{1,0:T(8,128)(2,1)S(1)}, u32[]{:S(2)}, u32[]{:S(2)}) collective-permute-start(bf16[30,1024]{1,0:T(8,128)(2,1)S(1)} %get-tuple-element.13), channel_id=1, source_target_pairs={{0,2},{2,4},{4,6},{6,8},{8,10},{10,12},{12,14},{1,3},{3,5},{5,7},{... | collective-permute-start | bytes 184328 | tf_op jit(solution)/shard_map/ppermute | solution.py:28
  52.9 1.5 collective-permute-done.4
  54.5 3.0 %multiply_convert_fusion.1 = bf16[158,1024]{1,0:T(8,128)(2,1)S(1)} fusion(bf16[188,1024]{1,0:T(8,128)(2,1)S(1)} %pad_maximum_fusion.5, bf16[15,1024]{1,0:T(8,128)(2,1)S(1)} %slice.428, bf16[128,1024]{1,0:T(8,128)(2,1)S(1)} %bitcast.134, bf16[15,1024]{1,0:T(8,128)(2,1)S(1)} %slice.426, bf16[128,1024]{1,0:T(8,128)(2,1)S(1)} %fusion.1, ...), kind=kLoop, calls=%fused_computation.22 | loop fusion | flops 18282496 | bytes 10543104 | tf_op jit(solution)/shard_map/convert_element_type | solution.py:177
  57.5 2.2 %add_convert_fusion = bf16[128,1024]{1,0:T(8,128)(2,1)S(1)} fusion(bf16[158,1024]{1,0:T(8,128)(2,1)S(1)} %multiply_convert_fusion.1, f32[1024]{0:T(1024)S(1)} %bitcast.207, f32[1024]{0:T(1024)S(1)} %bitcast.209, f32[1024]{0:T(1024)S(1)} %bitcast.151, f32[1024]{0:T(1024)S(1)} %bitcast.153, f32[1024]{0:T(1024)S(1)} %bitcast.155, f32[1024]{0:T(1024)S(1)} %bitcast.157, ...), kind=kLoop, calls=%fused_computation.45 | loop fusion | flops 12582912 | bytes 8777856 | tf_op jit(solution)/shard_map/convert_element_type | solution.py:195
  59.8 1.1 convert_multiply_fusion
  61.5 1.2 copy_dynamic-update-slice_fusion
  62.8 2.4 %fusion.2 = f32[1,31,1024]{2,0,1:T(1,128)S(1)} fusion(bf16[1,158,1024]{2,1,0:T(8,128)(2,1)S(1)} %slice_bitcast_fusion, bf16[128,1,1024]{2,0,1:T(8,128)(2,1)S(1)} %slice_bitcast_fusion.1), kind=kOutput, calls=%fused_computation.23 | convolution fusion | flops 8126464 | bytes 712704 | tf_op jit(solution)/shard_map/conv_general_dilated | solution.py:184
  65.8 1.6 %reshape.171 = f32[2,8,2,1024]{3,2,1,0:T(2,128)} reshape(f32[32,1024]{1,0:T(8,128)} %pad.13) | data formatting | bytes 262144 | tf_op jit(solution)/shard_map/reshape | solution.py:208
  67.5 0.9 copy_dynamic-update-slice_fusion.3
  69.3 1.9 %broadcast_select_fusion = bf16[8,128,512]{2,1,0:T(8,128)(2,1)} fusion(pred[8,512]{1,0:T(8,128)(4,1)S(1)} %iota_compare_fusion, bf16[128,512]{1,0:T(8,128)(2,1)} %get-tuple-element.55), kind=kLoop, calls=%fused_computation.18 | loop fusion | flops 524288 | bytes 1183744 | tf_op jit(solution)/shard_map/jit(_where)/select_n | solution.py:145
  72.1 1.0 bitcast_reduce_fusion
  73.1 3.4 %multiply_convert_fusion = bf16[1024,896]{1,0:T(8,128)(2,1)S(1)} fusion(bf16[1024,896]{1,0:T(8,128)(2,1)} %copy-done.1, bf16[1024,512]{1,0:T(8,128)(2,1)} %bitcast.137, bf16[896,512]{1,0:T(8,128)(2,1)} %bitcast.143, f32[1024]{0:T(1024)S(1)} %bitcast.210), kind=kOutput, calls=%fused_computation | convolution fusion | flops 943194112 | bytes 5640192 | tf_op jit(solution)/shard_map/dot_general | solution.py:154
  76.5 1.3 convert_add_fusion
  78.4 2.4 %fusion.34 = (bf16[896,512]{1,0:T(8,128)(2,1)S(1)}, f32[896,512]{1,0:T(8,128)}) fusion(bf16[1024,896]{1,0:T(8,128)(2,1)S(1)} %copy-done.2, bf16[1024,512]{1,0:T(8,128)(2,1)S(1)} %bitcast.138), kind=kOutput, calls=%fused_computation.100 | convolution fusion | flops 939982848 | bytes 5636096 | tf_op jit(solution)/shard_map/dot_general | solution.py:154
  80.8 6.4 %collective-permute-done.11 = bf16[4,34,1024]{2,0,1:T(4,128)(2,1)S(1)} collective-permute-done((bf16[4,34,1024]{2,0,1:T(4,128)(2,1)S(1)}, bf16[4,34,1024]{2,0,1:T(4,128)(2,1)S(1)}, u32[]{:S(2)}, u32[]{:S(2)}) %collective-permute-start.11) | collective-permute-done | bytes 278560 | tf_op jit(solution)/shard_map/ppermute | solution.py:68
  87.5 2.1 %collective-permute-start.12 = (bf16[2,34,1024]{2,0,1:T(2,128)(2,1)S(1)}, bf16[2,34,1024]{2,0,1:T(2,128)(2,1)S(1)}, u32[]{:S(2)}, u32[]{:S(2)}) collective-permute-start(bf16[2,34,1024]{2,0,1:T(2,128)(2,1)S(1)} %dynamic-slice_convert_fusion.2), channel_id=1, source_target_pairs={{0,4},{2,6},{4,0},{6,2},{8,12},{10,14},{12,8},{14,10},{1,5},{3,7},... | collective-permute-start | bytes 417800 | tf_op jit(solution)/shard_map/ppermute | solution.py:68
  89.6 2.4 %fusion.35 = (bf16[896,512]{1,0:T(8,128)(2,1)S(1)}, f32[896,512]{1,0:T(8,128)}) fusion(bf16[1024,896]{1,0:T(8,128)(2,1)S(1)} %multiply_convert_fusion, bf16[1024,512]{1,0:T(8,128)(2,1)S(1)} %bitcast.136), kind=kOutput, calls=%fused_computation.101 | convolution fusion | flops 940441600 | bytes 5636096 | tf_op jit(solution)/shard_map/dot_general | solution.py:154
  92.1 1.3 collective-permute-done.12
  93.7 2.8 %collective-permute-start.13 = (bf16[1,34,1024]{2,0,1:T(2,128)(2,1)S(1)}, bf16[1,34,1024]{2,0,1:T(2,128)(2,1)S(1)}, u32[]{:S(2)}, u32[]{:S(2)}) collective-permute-start(bf16[1,34,1024]{2,0,1:T(2,128)(2,1)S(1)} %dynamic-slice_convert_fusion.3), channel_id=1, source_target_pairs={{0,8},{2,10},{4,12},{6,14},{8,0},{10,2},{12,4},{14,6},{1,9},{3,11}... | collective-permute-start | bytes 208904 | tf_op jit(solution)/shard_map/ppermute | solution.py:68
  96.6 1.3 collective-permute-start.7
  97.9 4.8 %collective-permute-start.6 = (bf16[2,2,128,512]{3,2,1,0:T(8,128)(2,1)S(1)}, bf16[2,2,128,512]{3,2,1,0:T(8,128)(2,1)S(1)}, u32[]{:S(2)}, u32[]{:S(2)}) collective-permute-start(bf16[2,2,128,512]{3,2,1,0:T(8,128)(2,1)S(1)} %get-tuple-element.5), channel_id=1, source_target_pairs={{0,4},{2,6},{4,8},{6,10},{8,12},{10,14},{1,5},{3,7},{5,9},{7,11},{... | collective-permute-start | bytes 1572872 | tf_op jit(solution)/shard_map/ppermute | solution.py:17
  103.9 2.0 %select_reduce_fusion = f32[128,512]{1,0:T(8,128)} fusion(bf16[8,128,896]{2,1,0:T(8,128)(2,1)S(1)} %bitcast.211, bf16[896,512,1]{1,0,2:T(8,128)(2,1)S(1)} %bitcast.141, pred[8,512]{1,0:T(8,128)(4,1)S(1)} %iota_compare_fusion), kind=kOutput, calls=%fused_computation.6 | convolution fusion | flops 940507136 | bytes 3018752 | tf_op jit(solution)/shard_map/dot_general | solution.py:154
  105.9 1.6 %dynamic_update_slice.26 = bf16[2,34,1024]{2,0,1:T(2,128)(2,1)S(1)} dynamic-update-slice(bf16[2,34,1024]{2,0,1:T(2,128)(2,1)S(1)} %broadcast_in_dim.127, bf16[1,34,1024]{2,0,1:T(2,128)(2,1)S(1)} %add_convert_fusion.1, s32[]{:T(128)S(6)} %select_n.141, s32[]{:T(128)} %constant.80.clone.1, s32[]{:T(128)} %constant.80.clone.1) | dynamic-update-slice | bytes 139268 | tf_op jit(solution)/shard_map/dynamic_update_slice | solution.py:94
  107.6 12.4 %collective-permute-done.14 = bf16[1,34,1024]{2,0,1:T(2,128)(2,1)} collective-permute-done((bf16[1,34,1024]{2,0,1:T(2,128)(2,1)S(1)}, bf16[1,34,1024]{2,0,1:T(2,128)(2,1)}, u32[]{:S(2)}, u32[]{:S(2)}) %collective-permute-start.14) | collective-permute-done | bytes 69664 | tf_op jit(solution)/shard_map/ppermute | solution.py:68
  119.9 3.0 %dynamic_update_slice.27 = bf16[2,34,1024]{2,0,1:T(2,128)(2,1)S(1)} dynamic-update-slice(bf16[2,34,1024]{2,0,1:T(2,128)(2,1)S(1)} %dynamic_update_slice.26, bf16[1,34,1024]{2,0,1:T(2,128)(2,1)} %collective-permute-done.14, s32[]{:T(128)S(6)} %select_n.142, s32[]{:T(128)} %constant.80.clone.1, s32[]{:T(128)} %constant.80.clone.1) | dynamic-update-slice | bytes 139268 | tf_op jit(solution)/shard_map/dynamic_update_slice | solution.py:95
  123.0 1.6 %fusion.19 = bf16[1,128,512]{2,1,0:T(8,128)(2,1)} fusion(f32[128,512]{1,0:T(8,128)} %select_reduce_fusion), kind=kLoop, calls=%fused_computation.63 | loop fusion | flops 131072 | bytes 393216 | tf_op jit(solution)/shard_map/convert_element_type | solution.py:227
  124.7 1.2 slice.607
  125.9 1.2 slice.608
  128.3 1.2 collective-permute-start.16
  129.8 2.8 %collective-permute-start.9 = (bf16[2,128,512]{2,1,0:T(8,128)(2,1)S(1)}, bf16[2,128,512]{2,1,0:T(8,128)(2,1)S(1)}, u32[]{:S(2)}, u32[]{:S(2)}) collective-permute-start(bf16[2,128,512]{2,1,0:T(8,128)(2,1)S(1)} %get-tuple-element.10), channel_id=1, source_target_pairs={{2,0},{4,2},{6,4},{8,6},{10,8},{12,10},{14,12},{3,1},{5,3},{7,5},{... | collective-permute-start | bytes 786440 | tf_op jit(solution)/shard_map/ppermute | solution.py:17
  132.5 4.0 %collective-permute-start.8 = (bf16[2,128,512]{2,1,0:T(8,128)(2,1)S(1)}, bf16[2,128,512]{2,1,0:T(8,128)(2,1)S(1)}, u32[]{:S(2)}, u32[]{:S(2)}) collective-permute-start(bf16[2,128,512]{2,1,0:T(8,128)(2,1)S(1)} %get-tuple-element.9), channel_id=1, source_target_pairs={{0,2},{2,4},{4,6},{6,8},{8,10},{10,12},{12,14},{1,3},{3,5},{5,7},{... | collective-permute-start | bytes 786440 | tf_op jit(solution)/shard_map/ppermute | solution.py:17
  136.8 6.3 %collective-permute-done.16 = bf16[4,34,1024]{2,0,1:T(4,128)(2,1)S(1)} collective-permute-done((bf16[4,34,1024]{2,0,1:T(4,128)(2,1)S(1)}, bf16[4,34,1024]{2,0,1:T(4,128)(2,1)S(1)}, u32[]{:S(2)}, u32[]{:S(2)}) %collective-permute-start.16) | collective-permute-done | bytes 278560 | tf_op jit(solution)/shard_map/ppermute | solution.py:68
  143.4 3.4 %collective-permute-done.8 = bf16[2,128,512]{2,1,0:T(8,128)(2,1)S(1)} collective-permute-done((bf16[2,128,512]{2,1,0:T(8,128)(2,1)S(1)}, bf16[2,128,512]{2,1,0:T(8,128)(2,1)S(1)}, u32[]{:S(2)}, u32[]{:S(2)}) %collective-permute-start.8) | collective-permute-done | bytes 262176 | tf_op jit(solution)/shard_map/ppermute | solution.py:17
  148.6 1.1 slice.619
  (100 shorter events, 12.9 us)
Async XLA Ops:
  0.6 44.7 %copy-start = (bf16[512,1024]{1,0:T(8,128)(2,1)S(1)}, bf16[512,1024]{1,0:T(8,128)(2,1)}, u32[]{:S(2)}) copy-start(bf16[512,1024]{1,0:T(8,128)(2,1)} %param.11) | copy-start | bytes 3145732
  3.4 21.7 %copy-start.11 = (f32[31,1024]{1,0:T(8,128)S(1)}, f32[31,1024]{1,0:T(8,128)}, u32[]{:S(2)}) copy-start(f32[31,1024]{1,0:T(8,128)} %param.12) | copy-start | bytes 380932
  3.5 21.8 %copy-start.10 = (bf16[1,128,512]{2,1,0:T(8,128)(2,1)S(1)}, bf16[1,128,512]{2,1,0:T(8,128)(2,1)}, u32[]{:S(2)}) copy-start(bf16[1,128,512]{2,1,0:T(8,128)(2,1)} %param.7) | copy-start | bytes 393220
  3.5 11.8 %collective-permute-start.2 = (bf16[288,512]{1,0:T(8,128)(2,1)S(1)}, bf16[288,512]{1,0:T(8,128)(2,1)S(1)}, u32[]{:S(2)}, u32[]{:S(2)}) collective-permute-start(bf16[288,512]{1,0:T(8,128)(2,1)S(1)} %get-tuple-element.17), channel_id=1, source_target_pairs={{2,0},{4,2},{6,4},{8,6},{10,8},{12,10},{14,12},{3,1},{5,3},{7,5},{... | collective-permute-start | bytes 884744 | tf_op jit(solution)/shard_map/ppermute | solution.py:17
  5.6 15.9 %collective-permute-start = (bf16[288,512]{1,0:T(8,128)(2,1)S(1)}, bf16[288,512]{1,0:T(8,128)(2,1)S(1)}, u32[]{:S(2)}, u32[]{:S(2)}) collective-permute-start(bf16[288,512]{1,0:T(8,128)(2,1)S(1)} %get-tuple-element.18), channel_id=1, source_target_pairs={{0,2},{2,4},{4,6},{6,8},{8,10},{10,12},{12,14},{1,3},{3,5},{5,7},{... | collective-permute-start | bytes 884744 | tf_op jit(solution)/shard_map/ppermute | solution.py:17
  21.6 14.8 %collective-permute-start.1 = (bf16[2,2,128,512]{3,2,1,0:T(8,128)(2,1)S(1)}, bf16[2,2,128,512]{3,2,1,0:T(8,128)(2,1)S(1)}, u32[]{:S(2)}, u32[]{:S(2)}) collective-permute-start(bf16[2,2,128,512]{3,2,1,0:T(8,128)(2,1)S(1)} %get-tuple-element.16), channel_id=1, source_target_pairs={{0,4},{2,6},{4,8},{6,10},{8,12},{10,14},{1,5},{3,7},{5,9},{7,11},{... | collective-permute-start | bytes 1572872 | tf_op jit(solution)/shard_map/ppermute | solution.py:17
  25.3 15.7 %copy-start.4 = (bf16[8,128,512]{2,1,0:T(8,128)(2,1)}, bf16[8,128,512]{2,1,0:T(8,128)(2,1)S(1)}, u32[]{:S(2)}) copy-start(bf16[8,128,512]{2,1,0:T(8,128)(2,1)S(1)} %broadcast_select_fusion.1) | copy-start | bytes 3145732
  25.3 15.5 %collective-permute-start.3 = (bf16[2,2,128,512]{3,2,1,0:T(8,128)(2,1)S(1)}, bf16[2,2,128,512]{3,2,1,0:T(8,128)(2,1)S(1)}, u32[]{:S(2)}, u32[]{:S(2)}) collective-permute-start(bf16[2,2,128,512]{3,2,1,0:T(8,128)(2,1)S(1)} %get-tuple-element.15), channel_id=1, source_target_pairs={{4,0},{6,2},{8,4},{10,6},{12,8},{14,10},{5,1},{7,3},{9,5},{11,7},{... | collective-permute-start | bytes 1572872 | tf_op jit(solution)/shard_map/ppermute | solution.py:17
  41.0 1.4 copy-start.7
  41.0 3.1 %copy-start.9 = (bf16[7,1,128,512]{3,2,1,0:T(8,128)(2,1)}, bf16[7,1,128,512]{3,2,1,0:T(8,128)(2,1)S(1)}, u32[]{:S(2)}) copy-start(bf16[7,1,128,512]{3,2,1,0:T(8,128)(2,1)S(1)} %get-tuple-element.7) | copy-start | bytes 2752516
  44.1 1.3 copy-start.1
  45.4 9.1 %copy-start.3 = (bf16[1,128,1024]{2,1,0:T(8,128)(2,1)S(1)}, bf16[1,128,1024]{2,1,0:T(8,128)(2,1)}, u32[]{:S(2)}) copy-start(bf16[1,128,1024]{2,1,0:T(8,128)(2,1)} %param.10) | copy-start | bytes 786436
  45.7 7.1 %collective-permute-start.5 = (bf16[30,1024]{1,0:T(8,128)(2,1)S(1)}, bf16[30,1024]{1,0:T(8,128)(2,1)S(1)}, u32[]{:S(2)}, u32[]{:S(2)}) collective-permute-start(bf16[30,1024]{1,0:T(8,128)(2,1)S(1)} %get-tuple-element.14), channel_id=1, source_target_pairs={{2,0},{4,2},{6,4},{8,6},{10,8},{12,10},{14,12},{3,1},{5,3},{7,5},{... | collective-permute-start | bytes 184328 | tf_op jit(solution)/shard_map/ppermute | solution.py:30
  47.7 6.7 %collective-permute-start.4 = (bf16[30,1024]{1,0:T(8,128)(2,1)S(1)}, bf16[30,1024]{1,0:T(8,128)(2,1)S(1)}, u32[]{:S(2)}, u32[]{:S(2)}) collective-permute-start(bf16[30,1024]{1,0:T(8,128)(2,1)S(1)} %get-tuple-element.13), channel_id=1, source_target_pairs={{0,2},{2,4},{4,6},{6,8},{8,10},{10,12},{12,14},{1,3},{3,5},{5,7},{... | collective-permute-start | bytes 184328 | tf_op jit(solution)/shard_map/ppermute | solution.py:28
  69.3 7.2 %collective-permute-start.10 = (bf16[1,8,34,1024]{3,1,2,0:T(8,128)(2,1)}, bf16[1,8,34,1024]{3,1,2,0:T(8,128)(2,1)}, u32[]{:S(2)}, u32[]{:S(2)}) collective-permute-start(bf16[1,8,34,1024]{3,1,2,0:T(8,128)(2,1)} %dynamic-slice_convert_fusion), channel_id=1, source_target_pairs={{0,1},{1,0},{2,3},{3,2},{4,5},{5,4},{6,7},{7,6},{8,9},{9,8},{10,11... | collective-permute-start | bytes 1671176 | tf_op jit(solution)/shard_map/ppermute | solution.py:68
  76.5 1.7 %copy-start.2 = (bf16[1024,896]{1,0:T(8,128)(2,1)S(1)}, bf16[1024,896]{1,0:T(8,128)(2,1)}, u32[]{:S(2)}) copy-start(bf16[1024,896]{1,0:T(8,128)(2,1)} %copy-done.1) | copy-start | bytes 5505028
  76.5 1.9 %copy-start.6 = (bf16[8,128,512]{2,1,0:T(8,128)(2,1)S(1)}, bf16[8,128,512]{2,1,0:T(8,128)(2,1)}, u32[]{:S(2)}) copy-start(bf16[8,128,512]{2,1,0:T(8,128)(2,1)} %broadcast_select_fusion) | copy-start | bytes 3145732
  78.0 11.6 %copy-start.5 = (bf16[8,128,512]{2,1,0:T(8,128)(2,1)S(1)}, bf16[8,128,512]{2,1,0:T(8,128)(2,1)}, u32[]{:S(2)}) copy-start(bf16[8,128,512]{2,1,0:T(8,128)(2,1)} %copy-done.4) | copy-start | bytes 3145732
  78.0 9.1 %collective-permute-start.11 = (bf16[4,34,1024]{2,0,1:T(4,128)(2,1)S(1)}, bf16[4,34,1024]{2,0,1:T(4,128)(2,1)S(1)}, u32[]{:S(2)}, u32[]{:S(2)}) collective-permute-start(bf16[4,34,1024]{2,0,1:T(4,128)(2,1)S(1)} %fusion.16), channel_id=1, source_target_pairs={{0,2},{2,0},{4,6},{6,4},{8,10},{10,8},{12,14},{14,12},{1,3},{3,1},... | collective-permute-start | bytes 835592 | tf_op jit(solution)/shard_map/ppermute | solution.py:68
  87.5 5.9 %collective-permute-start.12 = (bf16[2,34,1024]{2,0,1:T(2,128)(2,1)S(1)}, bf16[2,34,1024]{2,0,1:T(2,128)(2,1)S(1)}, u32[]{:S(2)}, u32[]{:S(2)}) collective-permute-start(bf16[2,34,1024]{2,0,1:T(2,128)(2,1)S(1)} %dynamic-slice_convert_fusion.2), channel_id=1, source_target_pairs={{0,4},{2,6},{4,0},{6,2},{8,12},{10,14},{12,8},{14,10},{1,5},{3,7},... | collective-permute-start | bytes 417800 | tf_op jit(solution)/shard_map/ppermute | solution.py:68
  93.6 10.3 %copy-start.8 = (bf16[7,1,128,512]{3,2,1,0:T(8,128)(2,1)S(1)}, bf16[7,1,128,512]{3,2,1,0:T(8,128)(2,1)}, u32[]{:S(2)}) copy-start(bf16[7,1,128,512]{3,2,1,0:T(8,128)(2,1)} %copy-done.7) | copy-start | bytes 2752516
  93.7 9.9 %collective-permute-start.13 = (bf16[1,34,1024]{2,0,1:T(2,128)(2,1)S(1)}, bf16[1,34,1024]{2,0,1:T(2,128)(2,1)S(1)}, u32[]{:S(2)}, u32[]{:S(2)}) collective-permute-start(bf16[1,34,1024]{2,0,1:T(2,128)(2,1)S(1)} %dynamic-slice_convert_fusion.3), channel_id=1, source_target_pairs={{0,8},{2,10},{4,12},{6,14},{8,0},{10,2},{12,4},{14,6},{1,9},{3,11}... | collective-permute-start | bytes 208904 | tf_op jit(solution)/shard_map/ppermute | solution.py:68
  96.6 30.4 %collective-permute-start.7 = (bf16[2,2,128,512]{3,2,1,0:T(8,128)(2,1)S(1)}, bf16[2,2,128,512]{3,2,1,0:T(8,128)(2,1)S(1)}, u32[]{:S(2)}, u32[]{:S(2)}) collective-permute-start(bf16[2,2,128,512]{3,2,1,0:T(8,128)(2,1)S(1)} %get-tuple-element.6), channel_id=1, source_target_pairs={{4,0},{6,2},{8,4},{10,6},{12,8},{14,10},{5,1},{7,3},{9,5},{11,7},{... | collective-permute-start | bytes 1572872 | tf_op jit(solution)/shard_map/ppermute | solution.py:17
  97.9 29.3 %collective-permute-start.6 = (bf16[2,2,128,512]{3,2,1,0:T(8,128)(2,1)S(1)}, bf16[2,2,128,512]{3,2,1,0:T(8,128)(2,1)S(1)}, u32[]{:S(2)}, u32[]{:S(2)}) collective-permute-start(bf16[2,2,128,512]{3,2,1,0:T(8,128)(2,1)S(1)} %get-tuple-element.5), channel_id=1, source_target_pairs={{0,4},{2,6},{4,8},{6,10},{8,12},{10,14},{1,5},{3,7},{5,9},{7,11},{... | collective-permute-start | bytes 1572872 | tf_op jit(solution)/shard_map/ppermute | solution.py:17
  103.8 16.1 %collective-permute-start.14 = (bf16[1,34,1024]{2,0,1:T(2,128)(2,1)S(1)}, bf16[1,34,1024]{2,0,1:T(2,128)(2,1)}, u32[]{:S(2)}, u32[]{:S(2)}) collective-permute-start(bf16[1,34,1024]{2,0,1:T(2,128)(2,1)S(1)} %add_convert_fusion.1), channel_id=1, source_target_pairs={{0,8},{2,10},{4,12},{6,14},{8,0},{10,2},{12,4},{14,6},{1,9},{3,11}... | collective-permute-start | bytes 208904 | tf_op jit(solution)/shard_map/ppermute | solution.py:68
  123.0 5.1 %collective-permute-start.15 = (bf16[2,34,1024]{2,0,1:T(2,128)(2,1)S(1)}, bf16[2,34,1024]{2,0,1:T(2,128)(2,1)S(1)}, u32[]{:S(2)}, u32[]{:S(2)}) collective-permute-start(bf16[2,34,1024]{2,0,1:T(2,128)(2,1)S(1)} %dynamic_update_slice.27), channel_id=1, source_target_pairs={{0,4},{2,6},{4,0},{6,2},{8,12},{10,14},{12,8},{14,10},{1,5},{3,7},... | collective-permute-start | bytes 417800 | tf_op jit(solution)/shard_map/ppermute | solution.py:68
  128.3 14.8 %collective-permute-start.16 = (bf16[4,34,1024]{2,0,1:T(4,128)(2,1)S(1)}, bf16[4,34,1024]{2,0,1:T(4,128)(2,1)S(1)}, u32[]{:S(2)}, u32[]{:S(2)}) collective-permute-start(bf16[4,34,1024]{2,0,1:T(4,128)(2,1)S(1)} %constant_dynamic-update-slice_fusion.7), channel_id=1, source_target_pairs={{0,2},{2,0},{4,6},{6,4},{8,10},{10,8},{12,14},{14,12},{1,3},{3,1},... | collective-permute-start | bytes 835592 | tf_op jit(solution)/shard_map/ppermute | solution.py:68
  129.8 13.6 %collective-permute-start.9 = (bf16[2,128,512]{2,1,0:T(8,128)(2,1)S(1)}, bf16[2,128,512]{2,1,0:T(8,128)(2,1)S(1)}, u32[]{:S(2)}, u32[]{:S(2)}) collective-permute-start(bf16[2,128,512]{2,1,0:T(8,128)(2,1)S(1)} %get-tuple-element.10), channel_id=1, source_target_pairs={{2,0},{4,2},{6,4},{8,6},{10,8},{12,10},{14,12},{3,1},{5,3},{7,5},{... | collective-permute-start | bytes 786440 | tf_op jit(solution)/shard_map/ppermute | solution.py:17
  132.5 14.3 %collective-permute-start.8 = (bf16[2,128,512]{2,1,0:T(8,128)(2,1)S(1)}, bf16[2,128,512]{2,1,0:T(8,128)(2,1)S(1)}, u32[]{:S(2)}, u32[]{:S(2)}) collective-permute-start(bf16[2,128,512]{2,1,0:T(8,128)(2,1)S(1)} %get-tuple-element.9), channel_id=1, source_target_pairs={{0,2},{2,4},{4,6},{6,8},{8,10},{10,12},{12,14},{1,3},{3,5},{5,7},{... | collective-permute-start | bytes 786440 | tf_op jit(solution)/shard_map/ppermute | solution.py:17
  143.3 5.0 %collective-permute-start.17 = (bf16[1,8,34,1024]{3,1,2,0:T(8,128)(2,1)S(1)}, bf16[1,8,34,1024]{3,1,2,0:T(8,128)(2,1)S(1)}, u32[]{:S(2)}, u32[]{:S(2)}) collective-permute-start(bf16[1,8,34,1024]{3,1,2,0:T(8,128)(2,1)S(1)} %bitcast_dynamic-update-slice_fusion), channel_id=1, source_target_pairs={{0,1},{1,0},{2,3},{3,2},{4,5},{5,4},{6,7},{7,6},{8,9},{9,8},{10,11... | collective-permute-start | bytes 1671176 | tf_op jit(solution)/shard_map/ppermute | solution.py:68

commit v17 on v15

--- a/solution.py
+++ b/solution.py
@@ -43,9 +43,7 @@
     above_one = got_above[:rows].reshape(piece_own.shape)
     below = shifter(jnp.stack([below_one, piece_own], axis=0), 2)
     above = shifter(jnp.stack([piece_own, above_one], axis=0), -2)
-    window = jnp.stack(
-        [below[0], below[1], below_one, piece_own, above_one, above[0], above[1]], axis=0
-    )
+    window = [below[0], below[1], below_one, piece_own, above_one, above[0], above[1]]
     return window, got_below[rows:], got_above[rows:]
 
 
@@ -133,8 +131,8 @@
     )
     cot_wide = jnp.concatenate([edge_back(cot_low), cot_here, edge_back(cot_high)], axis=0)
     kv_rows = span_blocks * tokens
-    key_all = gathered[:, 0].reshape(kv_rows, width_heads)
-    value_all = gathered[:, 1].reshape(kv_rows, width_heads)
+    key_all = jnp.concatenate([block[0] for block in gathered], axis=0)
+    value_all = jnp.concatenate([block[1] for block in gathered], axis=0)
     head_mask = (
         jnp.arange(HEADS, dtype=jnp.int32)[:, None, None]
         == (jnp.arange(width_heads, dtype=jnp.int32) // HDIM)[None, None, :]

time: 148 us -> 145 us (0.980)
  waiting for transfers between devices: 60 us -> 64.9 us
  local copies, waits for them, and re-layouts: 15.2 us -> 12.7 us
  other arithmetic: 16.7 us -> 14.5 us
  matrix products: 14.3 us -> 12.4 us
  starting transfers between devices: 38.9 us -> 37 us
    ppermute x8, waiting for transfers between devices: 19.6 us -> 23.2 us  [exchange(): return lax.ppermute(block, axis, [(i, i ^ bit) for i in range(count)])]
    dot_general x6, matrix products: 9.02 us -> 7.12 us  [contract(): lax.dot_general(lhs, rhs, (((lhs_dim,), (rhs_dim,)), ((), ())), preferred...]
    unnamed x37 -> x41, local copies, waits for them, and re-layouts: 3.33 us -> 2.37 us
  transfers between devices with their start and end apart: 18 -> 18, of which waited for: 13 -> 13; matrix products, arithmetic and copies ran while one was open for 11% -> 9% of each run, Pallas kernels for 0% -> 0%
where the time goes in v17:
time: 145 us; the launch traced here: 144 us
  waiting for transfers between devices  64.9 us (45%)
  starting transfers between devices  37 us (26%)
  other arithmetic  14.5 us (10%)
  local copies, waits for them, and re-layouts  12.7 us (9%)
  matrix products  12.4 us (9%)
  between operations  2.19 us (2%)
    ppermute x8, waiting for transfers between devices, passed_along(): return lax.ppermute(block, axis, route)  40.1 us
    ppermute x8, starting transfers between devices, passed_along(): return lax.ppermute(block, axis, route)  24.4 us
    ppermute x8, waiting for transfers between devices, exchange(): return lax.ppermute(block, axis, [(i, i ^ bit) for i in range(count)])  23.2 us
    dot_general x6, matrix products, contract(): lax.dot_general(lhs, rhs, (((lhs_dim,), (rhs_dim,)), ((), ())), preferred...  7.12 us
    ppermute x8, starting transfers between devices, exchange(): return lax.ppermute(block, axis, [(i, i ^ bit) for i in range(count)])  5.72 us
    ppermute x1, starting transfers between devices, padded(): lax.ppermute(tail, axis, [(i, (i + 1) % count) for i in range(ends)])  5 us
    convert_element_type x1, other arithmetic, on_device(): grad_conv = (cot_wide.astype(jnp.float32) * (sigmoid_c + conv_out * sigmo...  3.04 us
  transfers between devices with their start and end apart: 18, of which 13 were waited for; matrix products, arithmetic and copies ran while one was open for 9% of the time, Pallas kernels for 0%

profile of v17, /device:TPU:2, one launch (start us, length us, event | category | flops | bytes accessed | tf_op | source)
XLA Modules:
  0.0 143.6 jit_solution(11750040761702883307)
XLA Ops:
  0.6 0.9 slice_bitcast_fusion.10
  1.6 0.9 constant_dynamic-update-slice_fusion.1
  2.5 1.0 constant_dynamic-update-slice_fusion
  3.6 1.9 %collective-permute-start.2 = (bf16[288,512]{1,0:T(8,128)(2,1)S(1)}, bf16[288,512]{1,0:T(8,128)(2,1)S(1)}, u32[]{:S(2)}, u32[]{:S(2)}) collective-permute-start(bf16[288,512]{1,0:T(8,128)(2,1)S(1)} %get-tuple-element.35), channel_id=1, source_target_pairs={{2,0},{4,2},{6,4},{8,6},{10,8},{12,10},{14,12},{3,1},{5,3},{7,5},{... | collective-permute-start | bytes 884744 | tf_op jit(solution)/shard_map/ppermute | solution.py:17
  5.5 4.8 %collective-permute-start = (bf16[288,512]{1,0:T(8,128)(2,1)S(1)}, bf16[288,512]{1,0:T(8,128)(2,1)S(1)}, u32[]{:S(2)}, u32[]{:S(2)}) collective-permute-start(bf16[288,512]{1,0:T(8,128)(2,1)S(1)} %get-tuple-element.36), channel_id=1, source_target_pairs={{0,2},{2,4},{4,6},{6,8},{8,10},{10,12},{12,14},{1,3},{3,5},{5,7},{... | collective-permute-start | bytes 884744 | tf_op jit(solution)/shard_map/ppermute | solution.py:17
  11.0 4.2 %collective-permute-done.2 = bf16[288,512]{1,0:T(8,128)(2,1)S(1)} collective-permute-done((bf16[288,512]{1,0:T(8,128)(2,1)S(1)}, bf16[288,512]{1,0:T(8,128)(2,1)S(1)}, u32[]{:S(2)}, u32[]{:S(2)}) %collective-permute-start.2) | collective-permute-done | bytes 294944 | tf_op jit(solution)/shard_map/ppermute | solution.py:17
  15.2 6.2 %collective-permute-done = bf16[288,512]{1,0:T(8,128)(2,1)S(1)} collective-permute-done((bf16[288,512]{1,0:T(8,128)(2,1)S(1)}, bf16[288,512]{1,0:T(8,128)(2,1)S(1)}, u32[]{:S(2)}, u32[]{:S(2)}) %collective-permute-start) | collective-permute-done | bytes 294944 | tf_op jit(solution)/shard_map/ppermute | solution.py:17
  21.6 3.5 %collective-permute-start.1 = (bf16[2,2,128,512]{3,2,1,0:T(8,128)(2,1)S(1)}, bf16[2,2,128,512]{3,2,1,0:T(8,128)(2,1)S(1)}, u32[]{:S(2)}, u32[]{:S(2)}) collective-permute-start(bf16[2,2,128,512]{3,2,1,0:T(8,128)(2,1)S(1)} %get-tuple-element.34), channel_id=1, source_target_pairs={{0,4},{2,6},{4,8},{6,10},{8,12},{10,14},{1,5},{3,7},{5,9},{7,11},{... | collective-permute-start | bytes 1572872 | tf_op jit(solution)/shard_map/ppermute | solution.py:17
  25.3 1.3 collective-permute-start.3
  26.6 9.8 %collective-permute-done.1 = bf16[2,2,128,512]{3,2,1,0:T(8,128)(2,1)S(1)} collective-permute-done((bf16[2,2,128,512]{3,2,1,0:T(8,128)(2,1)S(1)}, bf16[2,2,128,512]{3,2,1,0:T(8,128)(2,1)S(1)}, u32[]{:S(2)}, u32[]{:S(2)}) %collective-permute-start.1) | collective-permute-done | bytes 524320 | tf_op jit(solution)/shard_map/ppermute | solution.py:17
  36.5 4.2 %collective-permute-done.3 = bf16[2,2,128,512]{3,2,1,0:T(8,128)(2,1)S(1)} collective-permute-done((bf16[2,2,128,512]{3,2,1,0:T(8,128)(2,1)S(1)}, bf16[2,2,128,512]{3,2,1,0:T(8,128)(2,1)S(1)}, u32[]{:S(2)}, u32[]{:S(2)}) %collective-permute-start.3) | collective-permute-done | bytes 524320 | tf_op jit(solution)/shard_map/ppermute | solution.py:17
  40.8 1.2 fusion
  42.0 0.8 exponential_reduce_fusion
  42.8 0.7 exponential_convert_fusion
  43.6 1.3 fusion.44
  45.5 1.9 %collective-permute-start.5 = (bf16[30,1024]{1,0:T(8,128)(2,1)S(1)}, bf16[30,1024]{1,0:T(8,128)(2,1)S(1)}, u32[]{:S(2)}, u32[]{:S(2)}) collective-permute-start(bf16[30,1024]{1,0:T(8,128)(2,1)S(1)} %get-tuple-element.32), channel_id=1, source_target_pairs={{2,0},{4,2},{6,4},{8,6},{10,8},{12,10},{14,12},{3,1},{5,3},{7,5},{... | collective-permute-start | bytes 184328 | tf_op jit(solution)/shard_map/ppermute | solution.py:30
  47.5 5.0 %collective-permute-start.4 = (bf16[30,1024]{1,0:T(8,128)(2,1)S(1)}, bf16[30,1024]{1,0:T(8,128)(2,1)S(1)}, u32[]{:S(2)}, u32[]{:S(2)}) collective-permute-start(bf16[30,1024]{1,0:T(8,128)(2,1)S(1)} %get-tuple-element.31), channel_id=1, source_target_pairs={{0,2},{2,4},{4,6},{6,8},{8,10},{10,12},{12,14},{1,3},{3,5},{5,7},{... | collective-permute-start | bytes 184328 | tf_op jit(solution)/shard_map/ppermute | solution.py:28
  52.6 1.6 %collective-permute-done.4 = bf16[30,1024]{1,0:T(8,128)(2,1)S(1)} collective-permute-done((bf16[30,1024]{1,0:T(8,128)(2,1)S(1)}, bf16[30,1024]{1,0:T(8,128)(2,1)S(1)}, u32[]{:S(2)}, u32[]{:S(2)}) %collective-permute-start.4) | collective-permute-done | bytes 61472 | tf_op jit(solution)/shard_map/ppermute | solution.py:28
  54.4 3.0 %multiply_convert_fusion.1 = bf16[158,1024]{1,0:T(8,128)(2,1)S(1)} fusion(bf16[188,1024]{1,0:T(8,128)(2,1)S(1)} %pad_maximum_fusion.5, bf16[15,1024]{1,0:T(8,128)(2,1)S(1)} %slice.485, bf16[128,1024]{1,0:T(8,128)(2,1)S(1)} %bitcast.162, bf16[15,1024]{1,0:T(8,128)(2,1)S(1)} %slice.483, bf16[128,1024]{1,0:T(8,128)(2,1)S(1)} %fusion.1, ...), kind=kLoop, calls=%fused_computation.23 | loop fusion | flops 18282496 | bytes 10543104 | tf_op jit(solution)/shard_map/convert_element_type | solution.py:174
  57.4 2.2 %add_convert_fusion = bf16[128,1024]{1,0:T(8,128)(2,1)S(1)} fusion(bf16[158,1024]{1,0:T(8,128)(2,1)S(1)} %multiply_convert_fusion.1, f32[1024]{0:T(1024)S(1)} %bitcast.233, f32[1024]{0:T(1024)S(1)} %bitcast.235, f32[1024]{0:T(1024)S(1)} %bitcast.177, f32[1024]{0:T(1024)S(1)} %bitcast.179, f32[1024]{0:T(1024)S(1)} %bitcast.181, f32[1024]{0:T(1024)S(1)} %bitcast.183, ...), kind=kLoop, calls=%fused_computation.49 | loop fusion | flops 12582912 | bytes 8777856 | tf_op jit(solution)/shard_map/convert_element_type | solution.py:192
  60.2 1.2 copy_dynamic-update-slice_fusion
  61.4 2.4 %fusion.3 = f32[1,31,1024]{2,0,1:T(1,128)S(1)} fusion(bf16[1,158,1024]{2,1,0:T(8,128)(2,1)S(1)} %slice_bitcast_fusion, bf16[128,1,1024]{2,0,1:T(8,128)(2,1)S(1)} %slice_bitcast_fusion.1), kind=kOutput, calls=%fused_computation.24 | convolution fusion | flops 8126464 | bytes 712704 | tf_op jit(solution)/shard_map/conv_general_dilated | solution.py:181
  64.5 1.6 %reshape.177 = f32[2,8,2,1024]{3,2,1,0:T(2,128)} reshape(f32[32,1024]{1,0:T(8,128)} %pad.13) | data formatting | bytes 262144 | tf_op jit(solution)/shard_map/reshape | solution.py:205
  66.1 0.9 copy_dynamic-update-slice_fusion.1
  67.1 0.9 dynamic-slice_convert_fusion
  68.0 2.2 %convert_multiply_fusion = (f32[128,512]{1,0:T(8,128)}, bf16[128,512]{1,0:T(8,128)(2,1)}) fusion(bf16[128,512]{1,0:T(8,128)(2,1)} %copy-done.1, bf16[128,1024]{1,0:T(8,128)(2,1)S(1)} %add_convert_fusion, bf16[512,1024]{1,0:T(8,128)(2,1)S(1)} %copy-done), kind=kOutput, calls=%fused_computation.67 | convolution fusion | flops 134479872 | bytes 1835008 | tf_op jit(solution)/shard_map/dot_general | solution.py:210
  70.1 1.1 copy.60
  71.2 1.3 convert_add_fusion
  72.9 8.9 %collective-permute-done.11 = bf16[4,34,1024]{2,0,1:T(4,128)(2,1)S(1)} collective-permute-done((bf16[4,34,1024]{2,0,1:T(4,128)(2,1)S(1)}, bf16[4,34,1024]{2,0,1:T(4,128)(2,1)S(1)}, u32[]{:S(2)}, u32[]{:S(2)}) %collective-permute-start.11) | collective-permute-done | bytes 278560 | tf_op jit(solution)/shard_map/ppermute | solution.py:66
  82.2 2.1 %collective-permute-start.12 = (bf16[2,34,1024]{2,0,1:T(2,128)(2,1)S(1)}, bf16[2,34,1024]{2,0,1:T(2,128)(2,1)S(1)}, u32[]{:S(2)}, u32[]{:S(2)}) collective-permute-start(bf16[2,34,1024]{2,0,1:T(2,128)(2,1)S(1)} %dynamic-slice_convert_fusion.2), channel_id=1, source_target_pairs={{0,4},{2,6},{4,0},{6,2},{8,12},{10,14},{12,8},{14,10},{1,5},{3,7},... | collective-permute-start | bytes 417800 | tf_op jit(solution)/shard_map/ppermute | solution.py:66
  84.3 1.1 multiply_convert_fusion
  85.5 2.6 %collective-permute-done.12 = bf16[2,34,1024]{2,0,1:T(2,128)(2,1)S(1)} collective-permute-done((bf16[2,34,1024]{2,0,1:T(2,128)(2,1)S(1)}, bf16[2,34,1024]{2,0,1:T(2,128)(2,1)S(1)}, u32[]{:S(2)}, u32[]{:S(2)}) %collective-permute-start.12) | collective-permute-done | bytes 139296 | tf_op jit(solution)/shard_map/ppermute | solution.py:66
  88.4 2.8 %collective-permute-start.13 = (bf16[1,34,1024]{2,0,1:T(2,128)(2,1)S(1)}, bf16[1,34,1024]{2,0,1:T(2,128)(2,1)S(1)}, u32[]{:S(2)}, u32[]{:S(2)}) collective-permute-start(bf16[1,34,1024]{2,0,1:T(2,128)(2,1)S(1)} %dynamic-slice_convert_fusion.3), channel_id=1, source_target_pairs={{0,8},{2,10},{4,12},{6,14},{8,0},{10,2},{12,4},{14,6},{1,9},{3,11}... | collective-permute-start | bytes 208904 | tf_op jit(solution)/shard_map/ppermute | solution.py:66
  91.2 1.1 fusion.42
  92.3 5.0 %collective-permute-done.13 = bf16[1,34,1024]{2,0,1:T(2,128)(2,1)S(1)} collective-permute-done((bf16[1,34,1024]{2,0,1:T(2,128)(2,1)S(1)}, bf16[1,34,1024]{2,0,1:T(2,128)(2,1)S(1)}, u32[]{:S(2)}, u32[]{:S(2)}) %collective-permute-start.13) | collective-permute-done | bytes 69664 | tf_op jit(solution)/shard_map/ppermute | solution.py:66
  97.6 1.1 fusion.43
  98.7 6.7 %collective-permute-done.14 = bf16[1,34,1024]{2,0,1:T(2,128)(2,1)S(1)} collective-permute-done((bf16[1,34,1024]{2,0,1:T(2,128)(2,1)S(1)}, bf16[1,34,1024]{2,0,1:T(2,128)(2,1)S(1)}, u32[]{:S(2)}, u32[]{:S(2)}) %collective-permute-start.14) | collective-permute-done | bytes 69664 | tf_op jit(solution)/shard_map/ppermute | solution.py:66
  106.1 1.3 fusion.45
  107.5 1.3 collective-permute-start.7
  108.8 4.8 %collective-permute-start.6 = (bf16[2,2,128,512]{3,2,1,0:T(8,128)(2,1)S(1)}, bf16[2,2,128,512]{3,2,1,0:T(8,128)(2,1)S(1)}, u32[]{:S(2)}, u32[]{:S(2)}) collective-permute-start(bf16[2,2,128,512]{3,2,1,0:T(8,128)(2,1)S(1)} %get-tuple-element.5), channel_id=1, source_target_pairs={{0,4},{2,6},{4,8},{6,10},{8,12},{10,14},{1,5},{3,7},{5,9},{7,11},{... | collective-permute-start | bytes 1572872 | tf_op jit(solution)/shard_map/ppermute | solution.py:17
  115.3 7.7 %collective-permute-done.7 = bf16[2,2,128,512]{3,2,1,0:T(8,128)(2,1)S(1)} collective-permute-done((bf16[2,2,128,512]{3,2,1,0:T(8,128)(2,1)S(1)}, bf16[2,2,128,512]{3,2,1,0:T(8,128)(2,1)S(1)}, u32[]{:S(2)}, u32[]{:S(2)}) %collective-permute-start.7) | collective-permute-done | bytes 524320 | tf_op jit(solution)/shard_map/ppermute | solution.py:17
  123.1 1.1 collective-permute-done.6
  124.5 1.9 %collective-permute-start.9 = (bf16[2,128,512]{2,1,0:T(8,128)(2,1)S(1)}, bf16[2,128,512]{2,1,0:T(8,128)(2,1)S(1)}, u32[]{:S(2)}, u32[]{:S(2)}) collective-permute-start(bf16[2,128,512]{2,1,0:T(8,128)(2,1)S(1)} %get-tuple-element.8), channel_id=1, source_target_pairs={{2,0},{4,2},{6,4},{8,6},{10,8},{12,10},{14,12},{3,1},{5,3},{7,5},{... | collective-permute-start | bytes 786440 | tf_op jit(solution)/shard_map/ppermute | solution.py:17
  126.5 4.8 %collective-permute-start.8 = (bf16[2,128,512]{2,1,0:T(8,128)(2,1)S(1)}, bf16[2,128,512]{2,1,0:T(8,128)(2,1)S(1)}, u32[]{:S(2)}, u32[]{:S(2)}) collective-permute-start(bf16[2,128,512]{2,1,0:T(8,128)(2,1)S(1)} %get-tuple-element.7), channel_id=1, source_target_pairs={{0,2},{2,4},{4,6},{6,8},{8,10},{10,12},{12,14},{1,3},{3,5},{5,7},{... | collective-permute-start | bytes 786440 | tf_op jit(solution)/shard_map/ppermute | solution.py:17
  132.8 1.5 %collective-permute-done.9 = bf16[2,128,512]{2,1,0:T(8,128)(2,1)S(1)} collective-permute-done((bf16[2,128,512]{2,1,0:T(8,128)(2,1)S(1)}, bf16[2,128,512]{2,1,0:T(8,128)(2,1)S(1)}, u32[]{:S(2)}, u32[]{:S(2)}) %collective-permute-start.9) | collective-permute-done | bytes 262176 | tf_op jit(solution)/shard_map/ppermute | solution.py:17
  134.3 5.5 %collective-permute-done.8 = bf16[2,128,512]{2,1,0:T(8,128)(2,1)S(1)} collective-permute-done((bf16[2,128,512]{2,1,0:T(8,128)(2,1)S(1)}, bf16[2,128,512]{2,1,0:T(8,128)(2,1)S(1)}, u32[]{:S(2)}, u32[]{:S(2)}) %collective-permute-start.8) | collective-permute-done | bytes 262176 | tf_op jit(solution)/shard_map/ppermute | solution.py:17
  140.0 0.7 fusion.38
  141.3 1.5 %copy.70 = bf16[2,8,32,1024]{3,2,1,0:T(8,128)(2,1)} copy(bf16[2,8,32,1024]{3,1,2,0:T(8,128)(2,1)S(1)} %fusion.2) | data formatting | bytes 2097152 | tf_op jit(solution)/shard_map/slice | solution.py:240
  (108 shorter events, 9.8 us)
Async XLA Ops:
  0.6 44.5 %copy-start = (bf16[512,1024]{1,0:T(8,128)(2,1)S(1)}, bf16[512,1024]{1,0:T(8,128)(2,1)}, u32[]{:S(2)}) copy-start(bf16[512,1024]{1,0:T(8,128)(2,1)} %param.11) | copy-start | bytes 3145732
  2.5 22.6 %copy-start.11 = (f32[31,1024]{1,0:T(8,128)S(1)}, f32[31,1024]{1,0:T(8,128)}, u32[]{:S(2)}) copy-start(f32[31,1024]{1,0:T(8,128)} %param.12) | copy-start | bytes 380932
  2.5 22.6 %copy-start.10 = (bf16[1,128,512]{2,1,0:T(8,128)(2,1)S(1)}, bf16[1,128,512]{2,1,0:T(8,128)(2,1)}, u32[]{:S(2)}) copy-start(bf16[1,128,512]{2,1,0:T(8,128)(2,1)} %param.7) | copy-start | bytes 393220
  3.6 11.6 %collective-permute-start.2 = (bf16[288,512]{1,0:T(8,128)(2,1)S(1)}, bf16[288,512]{1,0:T(8,128)(2,1)S(1)}, u32[]{:S(2)}, u32[]{:S(2)}) collective-permute-start(bf16[288,512]{1,0:T(8,128)(2,1)S(1)} %get-tuple-element.35), channel_id=1, source_target_pairs={{2,0},{4,2},{6,4},{8,6},{10,8},{12,10},{14,12},{3,1},{5,3},{7,5},{... | collective-permute-start | bytes 884744 | tf_op jit(solution)/shard_map/ppermute | solution.py:17
  5.5 15.9 %collective-permute-start = (bf16[288,512]{1,0:T(8,128)(2,1)S(1)}, bf16[288,512]{1,0:T(8,128)(2,1)S(1)}, u32[]{:S(2)}, u32[]{:S(2)}) collective-permute-start(bf16[288,512]{1,0:T(8,128)(2,1)S(1)} %get-tuple-element.36), channel_id=1, source_target_pairs={{0,2},{2,4},{4,6},{6,8},{8,10},{10,12},{12,14},{1,3},{3,5},{5,7},{... | collective-permute-start | bytes 884744 | tf_op jit(solution)/shard_map/ppermute | solution.py:17
  21.4 15.0 %copy-start.8 = (bf16[1,128,512]{2,1,0:T(8,128)(2,1)S(1)}, bf16[1,128,512]{2,1,0:T(8,128)(2,1)}, u32[]{:S(2)}) copy-start(bf16[1,128,512]{2,1,0:T(8,128)(2,1)} %param.8) | copy-start | bytes 393220
  21.5 15.0 %copy-start.9 = (bf16[1,128,512]{2,1,0:T(8,128)(2,1)S(1)}, bf16[1,128,512]{2,1,0:T(8,128)(2,1)}, u32[]{:S(2)}) copy-start(bf16[1,128,512]{2,1,0:T(8,128)(2,1)} %param.9) | copy-start | bytes 393220
  21.6 14.8 %collective-permute-start.1 = (bf16[2,2,128,512]{3,2,1,0:T(8,128)(2,1)S(1)}, bf16[2,2,128,512]{3,2,1,0:T(8,128)(2,1)S(1)}, u32[]{:S(2)}, u32[]{:S(2)}) collective-permute-start(bf16[2,2,128,512]{3,2,1,0:T(8,128)(2,1)S(1)} %get-tuple-element.34), channel_id=1, source_target_pairs={{0,4},{2,6},{4,8},{6,10},{8,12},{10,14},{1,5},{3,7},{5,9},{7,11},{... | collective-permute-start | bytes 1572872 | tf_op jit(solution)/shard_map/ppermute | solution.py:17
  25.3 16.7 %copy-start.5 = (bf16[8,128,512]{2,1,0:T(8,128)(2,1)}, bf16[8,128,512]{2,1,0:T(8,128)(2,1)S(1)}, u32[]{:S(2)}) copy-start(bf16[8,128,512]{2,1,0:T(8,128)(2,1)S(1)} %broadcast_select_fusion.1) | copy-start | bytes 3145732
  25.3 15.5 %collective-permute-start.3 = (bf16[2,2,128,512]{3,2,1,0:T(8,128)(2,1)S(1)}, bf16[2,2,128,512]{3,2,1,0:T(8,128)(2,1)S(1)}, u32[]{:S(2)}, u32[]{:S(2)}) collective-permute-start(bf16[2,2,128,512]{3,2,1,0:T(8,128)(2,1)S(1)} %get-tuple-element.33), channel_id=1, source_target_pairs={{4,0},{6,2},{8,4},{10,6},{12,8},{14,10},{5,1},{7,3},{9,5},{11,7},{... | collective-permute-start | bytes 1572872 | tf_op jit(solution)/shard_map/ppermute | solution.py:17
  40.8 1.2 copy-start.14
  40.8 2.8 %copy-start.12 = (bf16[896,512]{1,0:T(8,128)(2,1)}, bf16[896,512]{1,0:T(8,128)(2,1)S(1)}, u32[]{:S(2)}) copy-start(bf16[896,512]{1,0:T(8,128)(2,1)S(1)} %get-tuple-element.13) | copy-start | bytes 2752516
  43.6 1.3 copy-start.2
  45.2 14.6 %copy-start.1 = (bf16[128,512]{1,0:T(8,128)(2,1)}, bf16[128,512]{1,0:T(8,128)(2,1)S(1)}, u32[]{:S(2)}) copy-start(bf16[128,512]{1,0:T(8,128)(2,1)S(1)} %select_reduce_fusion.1) | copy-start | bytes 393220
  45.2 9.2 %copy-start.4 = (bf16[1,128,1024]{2,1,0:T(8,128)(2,1)S(1)}, bf16[1,128,1024]{2,1,0:T(8,128)(2,1)}, u32[]{:S(2)}) copy-start(bf16[1,128,1024]{2,1,0:T(8,128)(2,1)} %param.10) | copy-start | bytes 786436
  45.5 7.1 %collective-permute-start.5 = (bf16[30,1024]{1,0:T(8,128)(2,1)S(1)}, bf16[30,1024]{1,0:T(8,128)(2,1)S(1)}, u32[]{:S(2)}, u32[]{:S(2)}) collective-permute-start(bf16[30,1024]{1,0:T(8,128)(2,1)S(1)} %get-tuple-element.32), channel_id=1, source_target_pairs={{2,0},{4,2},{6,4},{8,6},{10,8},{12,10},{14,12},{3,1},{5,3},{7,5},{... | collective-permute-start | bytes 184328 | tf_op jit(solution)/shard_map/ppermute | solution.py:30
  47.5 6.7 %collective-permute-start.4 = (bf16[30,1024]{1,0:T(8,128)(2,1)S(1)}, bf16[30,1024]{1,0:T(8,128)(2,1)S(1)}, u32[]{:S(2)}, u32[]{:S(2)}) collective-permute-start(bf16[30,1024]{1,0:T(8,128)(2,1)S(1)} %get-tuple-element.31), channel_id=1, source_target_pairs={{0,2},{2,4},{4,6},{6,8},{8,10},{10,12},{12,14},{1,3},{3,5},{5,7},{... | collective-permute-start | bytes 184328 | tf_op jit(solution)/shard_map/ppermute | solution.py:28
  68.0 3.3 %collective-permute-start.10 = (bf16[1,8,34,1024]{3,1,2,0:T(8,128)(2,1)}, bf16[1,8,34,1024]{3,1,2,0:T(8,128)(2,1)}, u32[]{:S(2)}, u32[]{:S(2)}) collective-permute-start(bf16[1,8,34,1024]{3,1,2,0:T(8,128)(2,1)} %dynamic-slice_convert_fusion), channel_id=1, source_target_pairs={{0,1},{1,0},{2,3},{3,2},{4,5},{5,4},{6,7},{7,6},{8,9},{9,8},{10,11... | collective-permute-start | bytes 1671176 | tf_op jit(solution)/shard_map/ppermute | solution.py:66
  71.2 1.6 %copy-start.7 = (bf16[128,512]{1,0:T(8,128)(2,1)S(1)}, bf16[128,512]{1,0:T(8,128)(2,1)}, u32[]{:S(2)}) copy-start(bf16[128,512]{1,0:T(8,128)(2,1)} %get-tuple-element.73) | copy-start | bytes 393220
  72.5 11.8 %copy-start.3 = (bf16[1024,896]{0,1:T(8,128)(2,1)S(1)}, bf16[1024,896]{0,1:T(8,128)(2,1)}, u32[]{:S(2)}) copy-start(bf16[1024,896]{0,1:T(8,128)(2,1)} %copy-done.2) | copy-start | bytes 5505028
  72.5 11.8 %copy-start.13 = (bf16[896,512]{1,0:T(8,128)(2,1)S(1)}, bf16[896,512]{1,0:T(8,128)(2,1)}, u32[]{:S(2)}) copy-start(bf16[896,512]{1,0:T(8,128)(2,1)} %copy-done.12) | copy-start | bytes 2752516
  72.7 9.1 %collective-permute-start.11 = (bf16[4,34,1024]{2,0,1:T(4,128)(2,1)S(1)}, bf16[4,34,1024]{2,0,1:T(4,128)(2,1)S(1)}, u32[]{:S(2)}, u32[]{:S(2)}) collective-permute-start(bf16[4,34,1024]{2,0,1:T(4,128)(2,1)S(1)} %fusion.17), channel_id=1, source_target_pairs={{0,2},{2,0},{4,6},{6,4},{8,10},{10,8},{12,14},{14,12},{1,3},{3,1},... | collective-permute-start | bytes 835592 | tf_op jit(solution)/shard_map/ppermute | solution.py:66
  82.2 5.9 %collective-permute-start.12 = (bf16[2,34,1024]{2,0,1:T(2,128)(2,1)S(1)}, bf16[2,34,1024]{2,0,1:T(2,128)(2,1)S(1)}, u32[]{:S(2)}, u32[]{:S(2)}) collective-permute-start(bf16[2,34,1024]{2,0,1:T(2,128)(2,1)S(1)} %dynamic-slice_convert_fusion.2), channel_id=1, source_target_pairs={{0,4},{2,6},{4,0},{6,2},{8,12},{10,14},{12,8},{14,10},{1,5},{3,7},... | collective-permute-start | bytes 417800 | tf_op jit(solution)/shard_map/ppermute | solution.py:66
  88.4 9.2 %copy-start.6 = (bf16[8,128,512]{2,1,0:T(8,128)(2,1)S(1)}, bf16[8,128,512]{2,1,0:T(8,128)(2,1)}, u32[]{:S(2)}) copy-start(bf16[8,128,512]{2,1,0:T(8,128)(2,1)} %copy-done.5) | copy-start | bytes 3145732
  88.4 8.9 %collective-permute-start.13 = (bf16[1,34,1024]{2,0,1:T(2,128)(2,1)S(1)}, bf16[1,34,1024]{2,0,1:T(2,128)(2,1)S(1)}, u32[]{:S(2)}, u32[]{:S(2)}) collective-permute-start(bf16[1,34,1024]{2,0,1:T(2,128)(2,1)S(1)} %dynamic-slice_convert_fusion.3), channel_id=1, source_target_pairs={{0,8},{2,10},{4,12},{6,14},{8,0},{10,2},{12,4},{14,6},{1,9},{3,11}... | collective-permute-start | bytes 208904 | tf_op jit(solution)/shard_map/ppermute | solution.py:66
  97.5 8.6 %copy-start.15 = (bf16[896,512]{1,0:T(8,128)(2,1)S(1)}, bf16[896,512]{1,0:T(8,128)(2,1)}, u32[]{:S(2)}) copy-start(bf16[896,512]{1,0:T(8,128)(2,1)} %copy-done.14) | copy-start | bytes 2752516
  97.5 7.9 %collective-permute-start.14 = (bf16[1,34,1024]{2,0,1:T(2,128)(2,1)S(1)}, bf16[1,34,1024]{2,0,1:T(2,128)(2,1)S(1)}, u32[]{:S(2)}, u32[]{:S(2)}) collective-permute-start(bf16[1,34,1024]{2,0,1:T(2,128)(2,1)S(1)} %add_convert_fusion.1), channel_id=1, source_target_pairs={{0,8},{2,10},{4,12},{6,14},{8,0},{10,2},{12,4},{14,6},{1,9},{3,11}... | collective-permute-start | bytes 208904 | tf_op jit(solution)/shard_map/ppermute | solution.py:66
  106.0 7.6 %collective-permute-start.15 = (bf16[2,34,1024]{2,0,1:T(2,128)(2,1)S(1)}, bf16[2,34,1024]{2,0,1:T(2,128)(2,1)S(1)}, u32[]{:S(2)}, u32[]{:S(2)}) collective-permute-start(bf16[2,34,1024]{2,0,1:T(2,128)(2,1)S(1)} %pad_maximum_fusion.9), channel_id=1, source_target_pairs={{0,4},{2,6},{4,0},{6,2},{8,12},{10,14},{12,8},{14,10},{1,5},{3,7},... | collective-permute-start | bytes 417800 | tf_op jit(solution)/shard_map/ppermute | solution.py:66
  107.5 15.5 %collective-permute-start.7 = (bf16[2,2,128,512]{3,2,1,0:T(8,128)(2,1)S(1)}, bf16[2,2,128,512]{3,2,1,0:T(8,128)(2,1)S(1)}, u32[]{:S(2)}, u32[]{:S(2)}) collective-permute-start(bf16[2,2,128,512]{3,2,1,0:T(8,128)(2,1)S(1)} %get-tuple-element.6), channel_id=1, source_target_pairs={{4,0},{6,2},{8,4},{10,6},{12,8},{14,10},{5,1},{7,3},{9,5},{11,7},{... | collective-permute-start | bytes 1572872 | tf_op jit(solution)/shard_map/ppermute | solution.py:17
  108.8 15.4 %collective-permute-start.6 = (bf16[2,2,128,512]{3,2,1,0:T(8,128)(2,1)S(1)}, bf16[2,2,128,512]{3,2,1,0:T(8,128)(2,1)S(1)}, u32[]{:S(2)}, u32[]{:S(2)}) collective-permute-start(bf16[2,2,128,512]{3,2,1,0:T(8,128)(2,1)S(1)} %get-tuple-element.5), channel_id=1, source_target_pairs={{0,4},{2,6},{4,8},{6,10},{8,12},{10,14},{1,5},{3,7},{5,9},{7,11},{... | collective-permute-start | bytes 1572872 | tf_op jit(solution)/shard_map/ppermute | solution.py:17
  114.4 16.9 %collective-permute-start.16 = (bf16[4,34,1024]{2,0,1:T(4,128)(2,1)S(1)}, bf16[4,34,1024]{2,0,1:T(4,128)(2,1)S(1)}, u32[]{:S(2)}, u32[]{:S(2)}) collective-permute-start(bf16[4,34,1024]{2,0,1:T(4,128)(2,1)S(1)} %pad_maximum_fusion.8), channel_id=1, source_target_pairs={{0,2},{2,0},{4,6},{6,4},{8,10},{10,8},{12,14},{14,12},{1,3},{3,1},... | collective-permute-start | bytes 835592 | tf_op jit(solution)/shard_map/ppermute | solution.py:66
  124.5 9.7 %collective-permute-start.9 = (bf16[2,128,512]{2,1,0:T(8,128)(2,1)S(1)}, bf16[2,128,512]{2,1,0:T(8,128)(2,1)S(1)}, u32[]{:S(2)}, u32[]{:S(2)}) collective-permute-start(bf16[2,128,512]{2,1,0:T(8,128)(2,1)S(1)} %get-tuple-element.8), channel_id=1, source_target_pairs={{2,0},{4,2},{6,4},{8,6},{10,8},{12,10},{14,12},{3,1},{5,3},{7,5},{... | collective-permute-start | bytes 786440 | tf_op jit(solution)/shard_map/ppermute | solution.py:17
  126.5 13.3 %collective-permute-start.8 = (bf16[2,128,512]{2,1,0:T(8,128)(2,1)S(1)}, bf16[2,128,512]{2,1,0:T(8,128)(2,1)S(1)}, u32[]{:S(2)}, u32[]{:S(2)}) collective-permute-start(bf16[2,128,512]{2,1,0:T(8,128)(2,1)S(1)} %get-tuple-element.7), channel_id=1, source_target_pairs={{0,2},{2,4},{4,6},{6,8},{8,10},{10,12},{12,14},{1,3},{3,5},{5,7},{... | collective-permute-start | bytes 786440 | tf_op jit(solution)/shard_map/ppermute | solution.py:17
  132.0 8.7 %collective-permute-start.17 = (bf16[1,8,34,1024]{3,1,2,0:T(8,128)(2,1)S(1)}, bf16[1,8,34,1024]{3,1,2,0:T(8,128)(2,1)S(1)}, u32[]{:S(2)}, u32[]{:S(2)}) collective-permute-start(bf16[1,8,34,1024]{3,1,2,0:T(8,128)(2,1)S(1)} %maximum_bitcast_fusion), channel_id=1, source_target_pairs={{0,1},{1,0},{2,3},{3,2},{4,5},{5,4},{6,7},{7,6},{8,9},{9,8},{10,11... | collective-permute-start | bytes 1671176 | tf_op jit(solution)/shard_map/ppermute | solution.py:66

commit v18 on v17

--- a/solution.py
+++ b/solution.py
@@ -47,9 +47,9 @@
     return window, got_below[rows:], got_above[rows:]
 
 
-def give_back(near, narrow, shifter):
-    from_below = shifter(narrow[REACH + 2 :], 2).astype(jnp.float32)
-    from_above = shifter(narrow[: REACH - 1], -2).astype(jnp.float32)
+def give_back(near, far_down, far_up, shifter):
+    from_below = shifter(far_up, 2).astype(jnp.float32)
+    from_above = shifter(far_down, -2).astype(jnp.float32)
     upward = (near[2] + from_below[1]).astype(jnp.bfloat16)
     downward = (near[0] + from_above[0]).astype(jnp.bfloat16)
     return (
@@ -228,10 +228,12 @@
     grad_value_all = contract(weights, grad_spread, 0, 0)
     key_blocks = grad_key_all.reshape(span_blocks, tokens, width_heads)
     value_blocks = grad_value_all.reshape(span_blocks, tokens, width_heads)
-    narrow = jnp.stack([key_blocks, value_blocks], axis=1).astype(jnp.bfloat16)
-    near = jnp.stack(
-        [key_blocks[REACH - 1 : REACH + 2], value_blocks[REACH - 1 : REACH + 2]], axis=1
-    )
+    def pair_rows(first, last):
+        return jnp.stack([key_blocks[first:last], value_blocks[first:last]], axis=1)
+
+    far_down = pair_rows(0, REACH - 1).astype(jnp.bfloat16)
+    far_up = pair_rows(REACH + 2, span_blocks).astype(jnp.bfloat16)
+    near = pair_rows(REACH - 1, REACH + 2)
 
     def grad_shift(piece_rows, offset_by):
         return passed_along(piece_rows, "ctx", offset_by)
@@ -241,7 +243,7 @@
     kernel_sum = (
         gathered[:, :, proj_rows:].astype(jnp.float32).reshape(members * kernel_rows, channels)[:KW]
     )
-    own_grads = give_back(near, narrow, grad_shift)
+    own_grads = give_back(near, far_down, far_up, grad_shift)
     grad_key = own_grads[0].astype(jnp.bfloat16)
     grad_value = own_grads[1].astype(jnp.bfloat16)
     return (

time: 145 us -> 152 us (1.048)
  matrix products: 12.4 us -> 16.1 us
  other arithmetic: 14.5 us -> 16.3 us
    dot_general x6, matrix products: 7.12 us -> 12.5 us  [contract(): lax.dot_general(lhs, rhs, (((lhs_dim,), (rhs_dim,)), ((), ())), preferred...]
    dot_general x1, matrix products: 2.15 us -> 0.49 us  [on_device(): lax.dot_general(grad_hidden, out_proj, (((1,), (1,)), ((), ())), preferre...]
  transfers between devices with their start and end apart: 18 -> 18, of which waited for: 13 -> 14; matrix products, arithmetic and copies ran while one was open for 9% -> 12% of each run, Pallas kernels for 0% -> 0%
where the time goes in v18:
time: 152 us; the launch traced here: 150 us
  waiting for transfers between devices  64.9 us (43%)
  starting transfers between devices  37.2 us (24%)
  other arithmetic  16.3 us (11%)
  matrix products  16.1 us (11%)
  local copies, waits for them, and re-layouts  13.7 us (9%)
  between operations  2.21 us (1%)
    ppermute x8, waiting for transfers between devices, passed_along(): return lax.ppermute(block, axis, route)  39.1 us
    ppermute x8, starting transfers between devices, passed_along(): return lax.ppermute(block, axis, route)  24.4 us
    ppermute x8, waiting for transfers between devices, exchange(): return lax.ppermute(block, axis, [(i, i ^ bit) for i in range(count)])  24.3 us
    dot_general x6, matrix products, contract(): lax.dot_general(lhs, rhs, (((lhs_dim,), (rhs_dim,)), ((), ())), preferred...  12.5 us
    ppermute x8, starting transfers between devices, exchange(): return lax.ppermute(block, axis, [(i, i ^ bit) for i in range(count)])  5.91 us
    ppermute x1, starting transfers between devices, padded(): lax.ppermute(tail, axis, [(i, (i + 1) % count) for i in range(ends)])  5 us
  transfers between devices with their start and end apart: 18, of which 14 were waited for; matrix products, arithmetic and copies ran while one was open for 12% of the time, Pallas kernels for 0%

profile of v18, /device:TPU:2, one launch (start us, length us, event | category | flops | bytes accessed | tf_op | source)
XLA Modules:
  0.0 150.5 jit_solution(13569550432769261846)
XLA Ops:
  0.6 0.9 slice_bitcast_fusion.10
  1.6 0.9 constant_dynamic-update-slice_fusion.1
  2.5 1.0 constant_dynamic-update-slice_fusion
  3.6 1.9 %collective-permute-start.2 = (bf16[288,512]{1,0:T(8,128)(2,1)S(1)}, bf16[288,512]{1,0:T(8,128)(2,1)S(1)}, u32[]{:S(2)}, u32[]{:S(2)}) collective-permute-start(bf16[288,512]{1,0:T(8,128)(2,1)S(1)} %get-tuple-element.37), channel_id=1, source_target_pairs={{2,0},{4,2},{6,4},{8,6},{10,8},{12,10},{14,12},{3,1},{5,3},{7,5},{... | collective-permute-start | bytes 884744 | tf_op jit(solution)/shard_map/ppermute | solution.py:17
  5.5 4.8 %collective-permute-start = (bf16[288,512]{1,0:T(8,128)(2,1)S(1)}, bf16[288,512]{1,0:T(8,128)(2,1)S(1)}, u32[]{:S(2)}, u32[]{:S(2)}) collective-permute-start(bf16[288,512]{1,0:T(8,128)(2,1)S(1)} %get-tuple-element.38), channel_id=1, source_target_pairs={{0,2},{2,4},{4,6},{6,8},{8,10},{10,12},{12,14},{1,3},{3,5},{5,7},{... | collective-permute-start | bytes 884744 | tf_op jit(solution)/shard_map/ppermute | solution.py:17
  11.0 4.2 %collective-permute-done.2 = bf16[288,512]{1,0:T(8,128)(2,1)S(1)} collective-permute-done((bf16[288,512]{1,0:T(8,128)(2,1)S(1)}, bf16[288,512]{1,0:T(8,128)(2,1)S(1)}, u32[]{:S(2)}, u32[]{:S(2)}) %collective-permute-start.2) | collective-permute-done | bytes 294944 | tf_op jit(solution)/shard_map/ppermute | solution.py:17
  15.2 6.2 %collective-permute-done = bf16[288,512]{1,0:T(8,128)(2,1)S(1)} collective-permute-done((bf16[288,512]{1,0:T(8,128)(2,1)S(1)}, bf16[288,512]{1,0:T(8,128)(2,1)S(1)}, u32[]{:S(2)}, u32[]{:S(2)}) %collective-permute-start) | collective-permute-done | bytes 294944 | tf_op jit(solution)/shard_map/ppermute | solution.py:17
  21.6 3.5 %collective-permute-start.1 = (bf16[2,2,128,512]{3,2,1,0:T(8,128)(2,1)S(1)}, bf16[2,2,128,512]{3,2,1,0:T(8,128)(2,1)S(1)}, u32[]{:S(2)}, u32[]{:S(2)}) collective-permute-start(bf16[2,2,128,512]{3,2,1,0:T(8,128)(2,1)S(1)} %get-tuple-element.36), channel_id=1, source_target_pairs={{0,4},{2,6},{4,8},{6,10},{8,12},{10,14},{1,5},{3,7},{5,9},{7,11},{... | collective-permute-start | bytes 1572872 | tf_op jit(solution)/shard_map/ppermute | solution.py:17
  25.3 1.3 collective-permute-start.3
  26.6 9.8 %collective-permute-done.1 = bf16[2,2,128,512]{3,2,1,0:T(8,128)(2,1)S(1)} collective-permute-done((bf16[2,2,128,512]{3,2,1,0:T(8,128)(2,1)S(1)}, bf16[2,2,128,512]{3,2,1,0:T(8,128)(2,1)S(1)}, u32[]{:S(2)}, u32[]{:S(2)}) %collective-permute-start.1) | collective-permute-done | bytes 524320 | tf_op jit(solution)/shard_map/ppermute | solution.py:17
  36.5 4.2 %collective-permute-done.3 = bf16[2,2,128,512]{3,2,1,0:T(8,128)(2,1)S(1)} collective-permute-done((bf16[2,2,128,512]{3,2,1,0:T(8,128)(2,1)S(1)}, bf16[2,2,128,512]{3,2,1,0:T(8,128)(2,1)S(1)}, u32[]{:S(2)}, u32[]{:S(2)}) %collective-permute-start.3) | collective-permute-done | bytes 524320 | tf_op jit(solution)/shard_map/ppermute | solution.py:17
  40.8 1.2 fusion
  42.0 0.8 exponential_reduce_fusion
  42.8 0.7 exponential_convert_fusion
  43.6 1.3 fusion.46
  45.5 1.9 %collective-permute-start.5 = (bf16[30,1024]{1,0:T(8,128)(2,1)S(1)}, bf16[30,1024]{1,0:T(8,128)(2,1)S(1)}, u32[]{:S(2)}, u32[]{:S(2)}) collective-permute-start(bf16[30,1024]{1,0:T(8,128)(2,1)S(1)} %get-tuple-element.34), channel_id=1, source_target_pairs={{2,0},{4,2},{6,4},{8,6},{10,8},{12,10},{14,12},{3,1},{5,3},{7,5},{... | collective-permute-start | bytes 184328 | tf_op jit(solution)/shard_map/ppermute | solution.py:30
  47.4 5.0 %collective-permute-start.4 = (bf16[30,1024]{1,0:T(8,128)(2,1)S(1)}, bf16[30,1024]{1,0:T(8,128)(2,1)S(1)}, u32[]{:S(2)}, u32[]{:S(2)}) collective-permute-start(bf16[30,1024]{1,0:T(8,128)(2,1)S(1)} %get-tuple-element.33), channel_id=1, source_target_pairs={{0,2},{2,4},{4,6},{6,8},{8,10},{10,12},{12,14},{1,3},{3,5},{5,7},{... | collective-permute-start | bytes 184328 | tf_op jit(solution)/shard_map/ppermute | solution.py:28
  52.7 1.5 collective-permute-done.4
  54.3 3.0 %multiply_convert_fusion.1 = bf16[158,1024]{1,0:T(8,128)(2,1)S(1)} fusion(bf16[188,1024]{1,0:T(8,128)(2,1)S(1)} %pad_maximum_fusion.5, bf16[15,1024]{1,0:T(8,128)(2,1)S(1)} %slice.499, bf16[128,1024]{1,0:T(8,128)(2,1)S(1)} %bitcast.168, bf16[15,1024]{1,0:T(8,128)(2,1)S(1)} %slice.497, bf16[128,1024]{1,0:T(8,128)(2,1)S(1)} %fusion.1, ...), kind=kLoop, calls=%fused_computation.23 | loop fusion | flops 18282496 | bytes 10543104 | tf_op jit(solution)/shard_map/convert_element_type | solution.py:174
  57.3 2.2 %add_convert_fusion = bf16[128,1024]{1,0:T(8,128)(2,1)S(1)} fusion(bf16[158,1024]{1,0:T(8,128)(2,1)S(1)} %multiply_convert_fusion.1, f32[1024]{0:T(1024)S(1)} %bitcast.241, f32[1024]{0:T(1024)S(1)} %bitcast.243, f32[1024]{0:T(1024)S(1)} %bitcast.185, f32[1024]{0:T(1024)S(1)} %bitcast.187, f32[1024]{0:T(1024)S(1)} %bitcast.189, f32[1024]{0:T(1024)S(1)} %bitcast.191, ...), kind=kLoop, calls=%fused_computation.49 | loop fusion | flops 12582912 | bytes 8777856 | tf_op jit(solution)/shard_map/convert_element_type | solution.py:192
  60.7 1.0 broadcast_select_fusion
  61.7 1.2 copy_dynamic-update-slice_fusion
  62.9 2.4 %fusion.3 = f32[1,31,1024]{2,0,1:T(1,128)S(1)} fusion(bf16[1,158,1024]{2,1,0:T(8,128)(2,1)S(1)} %slice_bitcast_fusion, bf16[128,1,1024]{2,0,1:T(8,128)(2,1)S(1)} %slice_bitcast_fusion.1), kind=kOutput, calls=%fused_computation.24 | convolution fusion | flops 8126464 | bytes 712704 | tf_op jit(solution)/shard_map/conv_general_dilated | solution.py:181
  66.0 1.6 %reshape.185 = f32[2,8,2,1024]{3,2,1,0:T(2,128)} reshape(f32[32,1024]{1,0:T(8,128)} %pad.13) | data formatting | bytes 262144 | tf_op jit(solution)/shard_map/reshape | solution.py:205
  67.6 0.9 copy_dynamic-update-slice_fusion.1
  68.6 0.9 dynamic-slice_convert_fusion
  69.5 4.4 %fusion.44 = (bf16[896,512]{1,0:T(8,128)(2,1)}, f32[896,512]{1,0:T(8,128)}) fusion(bf16[1024,896]{0,1:T(8,128)(2,1)} %copy-done.1, bf16[1024,512]{1,0:T(8,128)(2,1)} %bitcast.173), kind=kOutput, calls=%fused_computation.127 | convolution fusion | flops 939982848 | bytes 5636096 | tf_op jit(solution)/shard_map/dot_general | solution.py:151
  73.9 0.9 copy.70
  74.8 1.0 bitcast_reduce_fusion
  75.8 3.3 %multiply_convert_fusion = bf16[1024,896]{0,1:T(8,128)(2,1)S(1)} fusion(bf16[1024,896]{0,1:T(8,128)(2,1)} %copy-done.1, bf16[1024,512]{1,0:T(8,128)(2,1)} %bitcast.174, bf16[896,512]{1,0:T(8,128)(2,1)} %copy-done.10, f32[1024]{0:T(1024)S(1)} %bitcast.244), kind=kOutput, calls=%fused_computation | convolution fusion | flops 943194112 | bytes 5640192 | tf_op jit(solution)/shard_map/dot_general | solution.py:151
  79.1 1.3 convert_add_fusion
  80.6 1.1 fusion.45
  81.7 7.9 %collective-permute-done.11 = bf16[4,34,1024]{2,0,1:T(4,128)(2,1)S(1)} collective-permute-done((bf16[4,34,1024]{2,0,1:T(4,128)(2,1)S(1)}, bf16[4,34,1024]{2,0,1:T(4,128)(2,1)S(1)}, u32[]{:S(2)}, u32[]{:S(2)}) %collective-permute-start.11) | collective-permute-done | bytes 278560 | tf_op jit(solution)/shard_map/ppermute | solution.py:66
  90.0 2.1 %collective-permute-start.12 = (bf16[2,34,1024]{2,0,1:T(2,128)(2,1)S(1)}, bf16[2,34,1024]{2,0,1:T(2,128)(2,1)S(1)}, u32[]{:S(2)}, u32[]{:S(2)}) collective-permute-start(bf16[2,34,1024]{2,0,1:T(2,128)(2,1)S(1)} %dynamic-slice_convert_fusion.2), channel_id=1, source_target_pairs={{0,4},{2,6},{4,0},{6,2},{8,12},{10,14},{12,8},{14,10},{1,5},{3,7},... | collective-permute-start | bytes 417800 | tf_op jit(solution)/shard_map/ppermute | solution.py:66
  92.1 1.3 fusion.47
  93.4 2.5 %collective-permute-done.12 = bf16[2,34,1024]{2,0,1:T(2,128)(2,1)S(1)} collective-permute-done((bf16[2,34,1024]{2,0,1:T(2,128)(2,1)S(1)}, bf16[2,34,1024]{2,0,1:T(2,128)(2,1)S(1)}, u32[]{:S(2)}, u32[]{:S(2)}) %collective-permute-start.12) | collective-permute-done | bytes 139296 | tf_op jit(solution)/shard_map/ppermute | solution.py:66
  96.2 2.8 %collective-permute-start.13 = (bf16[1,34,1024]{2,0,1:T(2,128)(2,1)S(1)}, bf16[1,34,1024]{2,0,1:T(2,128)(2,1)S(1)}, u32[]{:S(2)}, u32[]{:S(2)}) collective-permute-start(bf16[1,34,1024]{2,0,1:T(2,128)(2,1)S(1)} %dynamic-slice_convert_fusion.3), channel_id=1, source_target_pairs={{0,8},{2,10},{4,12},{6,14},{8,0},{10,2},{12,4},{14,6},{1,9},{3,11}... | collective-permute-start | bytes 208904 | tf_op jit(solution)/shard_map/ppermute | solution.py:66
  99.0 6.0 %collective-permute-done.13 = bf16[1,34,1024]{2,0,1:T(2,128)(2,1)S(1)} collective-permute-done((bf16[1,34,1024]{2,0,1:T(2,128)(2,1)S(1)}, bf16[1,34,1024]{2,0,1:T(2,128)(2,1)S(1)}, u32[]{:S(2)}, u32[]{:S(2)}) %collective-permute-start.13) | collective-permute-done | bytes 69664 | tf_op jit(solution)/shard_map/ppermute | solution.py:66
  105.4 7.8 %collective-permute-done.14 = bf16[1,34,1024]{2,0,1:T(2,128)(2,1)S(1)} collective-permute-done((bf16[1,34,1024]{2,0,1:T(2,128)(2,1)S(1)}, bf16[1,34,1024]{2,0,1:T(2,128)(2,1)S(1)}, u32[]{:S(2)}, u32[]{:S(2)}) %collective-permute-start.14) | collective-permute-done | bytes 69664 | tf_op jit(solution)/shard_map/ppermute | solution.py:66
  113.9 1.3 collective-permute-start.7
  115.3 4.8 %collective-permute-start.6 = (bf16[2,2,128,512]{3,2,1,0:T(8,128)(2,1)S(1)}, bf16[2,2,128,512]{3,2,1,0:T(8,128)(2,1)S(1)}, u32[]{:S(2)}, u32[]{:S(2)}) collective-permute-start(bf16[2,2,128,512]{3,2,1,0:T(8,128)(2,1)S(1)} %pad_maximum_fusion.3), channel_id=1, source_target_pairs={{0,4},{2,6},{4,8},{6,10},{8,12},{10,14},{1,5},{3,7},{5,9},{7,11},{... | collective-permute-start | bytes 1572872 | tf_op jit(solution)/shard_map/ppermute | solution.py:17
  122.0 1.2 slice.696
  123.2 7.2 %collective-permute-done.7 = bf16[2,2,128,512]{3,2,1,0:T(8,128)(2,1)S(1)} collective-permute-done((bf16[2,2,128,512]{3,2,1,0:T(8,128)(2,1)S(1)}, bf16[2,2,128,512]{3,2,1,0:T(8,128)(2,1)S(1)}, u32[]{:S(2)}, u32[]{:S(2)}) %collective-permute-start.7) | collective-permute-done | bytes 524320 | tf_op jit(solution)/shard_map/ppermute | solution.py:17
  131.1 1.9 %collective-permute-start.9 = (bf16[2,128,512]{2,1,0:T(8,128)(2,1)S(1)}, bf16[2,128,512]{2,1,0:T(8,128)(2,1)S(1)}, u32[]{:S(2)}, u32[]{:S(2)}) collective-permute-start(bf16[2,128,512]{2,1,0:T(8,128)(2,1)S(1)} %get-tuple-element.6), channel_id=1, source_target_pairs={{2,0},{4,2},{6,4},{8,6},{10,8},{12,10},{14,12},{3,1},{5,3},{7,5},{... | collective-permute-start | bytes 786440 | tf_op jit(solution)/shard_map/ppermute | solution.py:17
  133.0 4.8 %collective-permute-start.8 = (bf16[2,128,512]{2,1,0:T(8,128)(2,1)S(1)}, bf16[2,128,512]{2,1,0:T(8,128)(2,1)S(1)}, u32[]{:S(2)}, u32[]{:S(2)}) collective-permute-start(bf16[2,128,512]{2,1,0:T(8,128)(2,1)S(1)} %get-tuple-element.5), channel_id=1, source_target_pairs={{0,2},{2,4},{4,6},{6,8},{8,10},{10,12},{12,14},{1,3},{3,5},{5,7},{... | collective-permute-start | bytes 786440 | tf_op jit(solution)/shard_map/ppermute | solution.py:17
  139.3 1.9 %collective-permute-done.9 = bf16[2,128,512]{2,1,0:T(8,128)(2,1)S(1)} collective-permute-done((bf16[2,128,512]{2,1,0:T(8,128)(2,1)S(1)}, bf16[2,128,512]{2,1,0:T(8,128)(2,1)S(1)}, u32[]{:S(2)}, u32[]{:S(2)}) %collective-permute-start.9) | collective-permute-done | bytes 262176 | tf_op jit(solution)/shard_map/ppermute | solution.py:17
  141.2 5.5 %collective-permute-done.8 = bf16[2,128,512]{2,1,0:T(8,128)(2,1)S(1)} collective-permute-done((bf16[2,128,512]{2,1,0:T(8,128)(2,1)S(1)}, bf16[2,128,512]{2,1,0:T(8,128)(2,1)S(1)}, u32[]{:S(2)}, u32[]{:S(2)}) %collective-permute-start.8) | collective-permute-done | bytes 262176 | tf_op jit(solution)/shard_map/ppermute | solution.py:17
  148.2 1.5 %copy.82 = bf16[2,8,32,1024]{3,2,1,0:T(8,128)(2,1)} copy(bf16[2,8,32,1024]{3,1,2,0:T(8,128)(2,1)S(1)} %fusion.2) | data formatting | bytes 2097152 | tf_op jit(solution)/shard_map/slice | solution.py:242
  (105 shorter events, 11.3 us)
Async XLA Ops:
  0.6 44.5 %copy-start = (bf16[512,1024]{1,0:T(8,128)(2,1)S(1)}, bf16[512,1024]{1,0:T(8,128)(2,1)}, u32[]{:S(2)}) copy-start(bf16[512,1024]{1,0:T(8,128)(2,1)} %param.11) | copy-start | bytes 3145732
  2.5 22.6 %copy-start.9 = (f32[31,1024]{1,0:T(8,128)S(1)}, f32[31,1024]{1,0:T(8,128)}, u32[]{:S(2)}) copy-start(f32[31,1024]{1,0:T(8,128)} %param.12) | copy-start | bytes 380932
  2.5 22.6 %copy-start.8 = (bf16[1,128,512]{2,1,0:T(8,128)(2,1)S(1)}, bf16[1,128,512]{2,1,0:T(8,128)(2,1)}, u32[]{:S(2)}) copy-start(bf16[1,128,512]{2,1,0:T(8,128)(2,1)} %param.7) | copy-start | bytes 393220
  3.6 11.6 %collective-permute-start.2 = (bf16[288,512]{1,0:T(8,128)(2,1)S(1)}, bf16[288,512]{1,0:T(8,128)(2,1)S(1)}, u32[]{:S(2)}, u32[]{:S(2)}) collective-permute-start(bf16[288,512]{1,0:T(8,128)(2,1)S(1)} %get-tuple-element.37), channel_id=1, source_target_pairs={{2,0},{4,2},{6,4},{8,6},{10,8},{12,10},{14,12},{3,1},{5,3},{7,5},{... | collective-permute-start | bytes 884744 | tf_op jit(solution)/shard_map/ppermute | solution.py:17
  5.5 15.9 %collective-permute-start = (bf16[288,512]{1,0:T(8,128)(2,1)S(1)}, bf16[288,512]{1,0:T(8,128)(2,1)S(1)}, u32[]{:S(2)}, u32[]{:S(2)}) collective-permute-start(bf16[288,512]{1,0:T(8,128)(2,1)S(1)} %get-tuple-element.38), channel_id=1, source_target_pairs={{0,2},{2,4},{4,6},{6,8},{8,10},{10,12},{12,14},{1,3},{3,5},{5,7},{... | collective-permute-start | bytes 884744 | tf_op jit(solution)/shard_map/ppermute | solution.py:17
  21.4 15.0 %copy-start.5 = (bf16[1,128,512]{2,1,0:T(8,128)(2,1)S(1)}, bf16[1,128,512]{2,1,0:T(8,128)(2,1)}, u32[]{:S(2)}) copy-start(bf16[1,128,512]{2,1,0:T(8,128)(2,1)} %param.8) | copy-start | bytes 393220
  21.5 15.0 %copy-start.6 = (bf16[1,128,512]{2,1,0:T(8,128)(2,1)S(1)}, bf16[1,128,512]{2,1,0:T(8,128)(2,1)}, u32[]{:S(2)}) copy-start(bf16[1,128,512]{2,1,0:T(8,128)(2,1)} %param.9) | copy-start | bytes 393220
  21.6 14.8 %collective-permute-start.1 = (bf16[2,2,128,512]{3,2,1,0:T(8,128)(2,1)S(1)}, bf16[2,2,128,512]{3,2,1,0:T(8,128)(2,1)S(1)}, u32[]{:S(2)}, u32[]{:S(2)}) collective-permute-start(bf16[2,2,128,512]{3,2,1,0:T(8,128)(2,1)S(1)} %get-tuple-element.36), channel_id=1, source_target_pairs={{0,4},{2,6},{4,8},{6,10},{8,12},{10,14},{1,5},{3,7},{5,9},{7,11},{... | collective-permute-start | bytes 1572872 | tf_op jit(solution)/shard_map/ppermute | solution.py:17
  25.3 16.7 %copy-start.3 = (bf16[8,128,512]{2,1,0:T(8,128)(2,1)}, bf16[8,128,512]{2,1,0:T(8,128)(2,1)S(1)}, u32[]{:S(2)}) copy-start(bf16[8,128,512]{2,1,0:T(8,128)(2,1)S(1)} %broadcast_select_fusion.1) | copy-start | bytes 3145732
  25.3 15.5 %collective-permute-start.3 = (bf16[2,2,128,512]{3,2,1,0:T(8,128)(2,1)S(1)}, bf16[2,2,128,512]{3,2,1,0:T(8,128)(2,1)S(1)}, u32[]{:S(2)}, u32[]{:S(2)}) collective-permute-start(bf16[2,2,128,512]{3,2,1,0:T(8,128)(2,1)S(1)} %get-tuple-element.35), channel_id=1, source_target_pairs={{4,0},{6,2},{8,4},{10,6},{12,8},{14,10},{5,1},{7,3},{9,5},{11,7},{... | collective-permute-start | bytes 1572872 | tf_op jit(solution)/shard_map/ppermute | solution.py:17
  40.8 1.2 copy-start.11
  40.8 2.8 %copy-start.10 = (bf16[896,512]{1,0:T(8,128)(2,1)}, bf16[896,512]{1,0:T(8,128)(2,1)S(1)}, u32[]{:S(2)}) copy-start(bf16[896,512]{1,0:T(8,128)(2,1)S(1)} %get-tuple-element.15) | copy-start | bytes 2752516
  43.6 1.3 copy-start.1
  45.2 9.1 %copy-start.2 = (bf16[1,128,1024]{2,1,0:T(8,128)(2,1)S(1)}, bf16[1,128,1024]{2,1,0:T(8,128)(2,1)}, u32[]{:S(2)}) copy-start(bf16[1,128,1024]{2,1,0:T(8,128)(2,1)} %param.10) | copy-start | bytes 786436
  45.5 7.1 %collective-permute-start.5 = (bf16[30,1024]{1,0:T(8,128)(2,1)S(1)}, bf16[30,1024]{1,0:T(8,128)(2,1)S(1)}, u32[]{:S(2)}, u32[]{:S(2)}) collective-permute-start(bf16[30,1024]{1,0:T(8,128)(2,1)S(1)} %get-tuple-element.34), channel_id=1, source_target_pairs={{2,0},{4,2},{6,4},{8,6},{10,8},{12,10},{14,12},{3,1},{5,3},{7,5},{... | collective-permute-start | bytes 184328 | tf_op jit(solution)/shard_map/ppermute | solution.py:30
  47.4 6.7 %collective-permute-start.4 = (bf16[30,1024]{1,0:T(8,128)(2,1)S(1)}, bf16[30,1024]{1,0:T(8,128)(2,1)S(1)}, u32[]{:S(2)}, u32[]{:S(2)}) collective-permute-start(bf16[30,1024]{1,0:T(8,128)(2,1)S(1)} %get-tuple-element.33), channel_id=1, source_target_pairs={{0,2},{2,4},{4,6},{6,8},{8,10},{10,12},{12,14},{1,3},{3,5},{5,7},{... | collective-permute-start | bytes 184328 | tf_op jit(solution)/shard_map/ppermute | solution.py:28
  69.5 9.5 %collective-permute-start.10 = (bf16[1,8,34,1024]{3,1,2,0:T(8,128)(2,1)}, bf16[1,8,34,1024]{3,1,2,0:T(8,128)(2,1)}, u32[]{:S(2)}, u32[]{:S(2)}) collective-permute-start(bf16[1,8,34,1024]{3,1,2,0:T(8,128)(2,1)} %dynamic-slice_convert_fusion), channel_id=1, source_target_pairs={{0,1},{1,0},{2,3},{3,2},{4,5},{5,4},{6,7},{7,6},{8,9},{9,8},{10,11... | collective-permute-start | bytes 1671176 | tf_op jit(solution)/shard_map/ppermute | solution.py:66
  79.0 1.5 %copy-start.4 = (bf16[8,128,512]{2,1,0:T(8,128)(2,1)S(1)}, bf16[8,128,512]{2,1,0:T(8,128)(2,1)}, u32[]{:S(2)}) copy-start(bf16[8,128,512]{2,1,0:T(8,128)(2,1)} %copy-done.3) | copy-start | bytes 3145732
  80.5 11.6 %copy-start.12 = (bf16[896,512]{1,0:T(8,128)(2,1)S(1)}, bf16[896,512]{1,0:T(8,128)(2,1)}, u32[]{:S(2)}) copy-start(bf16[896,512]{1,0:T(8,128)(2,1)} %copy-done.11) | copy-start | bytes 2752516
  80.5 9.1 %collective-permute-start.11 = (bf16[4,34,1024]{2,0,1:T(4,128)(2,1)S(1)}, bf16[4,34,1024]{2,0,1:T(4,128)(2,1)S(1)}, u32[]{:S(2)}, u32[]{:S(2)}) collective-permute-start(bf16[4,34,1024]{2,0,1:T(4,128)(2,1)S(1)} %fusion.17), channel_id=1, source_target_pairs={{0,2},{2,0},{4,6},{6,4},{8,10},{10,8},{12,14},{14,12},{1,3},{3,1},... | collective-permute-start | bytes 835592 | tf_op jit(solution)/shard_map/ppermute | solution.py:66
  90.0 9.0 %copy-start.7 = (bf16[896,512]{1,0:T(8,128)(2,1)S(1)}, bf16[896,512]{1,0:T(8,128)(2,1)}, u32[]{:S(2)}) copy-start(bf16[896,512]{1,0:T(8,128)(2,1)} %get-tuple-element.76) | copy-start | bytes 2752516
  90.0 5.9 %collective-permute-start.12 = (bf16[2,34,1024]{2,0,1:T(2,128)(2,1)S(1)}, bf16[2,34,1024]{2,0,1:T(2,128)(2,1)S(1)}, u32[]{:S(2)}, u32[]{:S(2)}) collective-permute-start(bf16[2,34,1024]{2,0,1:T(2,128)(2,1)S(1)} %dynamic-slice_convert_fusion.2), channel_id=1, source_target_pairs={{0,4},{2,6},{4,0},{6,2},{8,12},{10,14},{12,8},{14,10},{1,5},{3,7},... | collective-permute-start | bytes 417800 | tf_op jit(solution)/shard_map/ppermute | solution.py:66
  96.2 8.9 %collective-permute-start.13 = (bf16[1,34,1024]{2,0,1:T(2,128)(2,1)S(1)}, bf16[1,34,1024]{2,0,1:T(2,128)(2,1)S(1)}, u32[]{:S(2)}, u32[]{:S(2)}) collective-permute-start(bf16[1,34,1024]{2,0,1:T(2,128)(2,1)S(1)} %dynamic-slice_convert_fusion.3), channel_id=1, source_target_pairs={{0,8},{2,10},{4,12},{6,14},{8,0},{10,2},{12,4},{14,6},{1,9},{3,11}... | collective-permute-start | bytes 208904 | tf_op jit(solution)/shard_map/ppermute | solution.py:66
  105.3 7.9 %collective-permute-start.14 = (bf16[1,34,1024]{2,0,1:T(2,128)(2,1)S(1)}, bf16[1,34,1024]{2,0,1:T(2,128)(2,1)S(1)}, u32[]{:S(2)}, u32[]{:S(2)}) collective-permute-start(bf16[1,34,1024]{2,0,1:T(2,128)(2,1)S(1)} %add_convert_fusion.1), channel_id=1, source_target_pairs={{0,8},{2,10},{4,12},{6,14},{8,0},{10,2},{12,4},{14,6},{1,9},{3,11}... | collective-permute-start | bytes 208904 | tf_op jit(solution)/shard_map/ppermute | solution.py:66
  113.8 6.4 %collective-permute-start.15 = (bf16[2,34,1024]{2,0,1:T(2,128)(2,1)S(1)}, bf16[2,34,1024]{2,0,1:T(2,128)(2,1)S(1)}, u32[]{:S(2)}, u32[]{:S(2)}) collective-permute-start(bf16[2,34,1024]{2,0,1:T(2,128)(2,1)S(1)} %pad_maximum_fusion.9), channel_id=1, source_target_pairs={{0,4},{2,6},{4,0},{6,2},{8,12},{10,14},{12,8},{14,10},{1,5},{3,7},... | collective-permute-start | bytes 417800 | tf_op jit(solution)/shard_map/ppermute | solution.py:66
  113.9 16.5 %collective-permute-start.7 = (bf16[2,2,128,512]{3,2,1,0:T(8,128)(2,1)S(1)}, bf16[2,2,128,512]{3,2,1,0:T(8,128)(2,1)S(1)}, u32[]{:S(2)}, u32[]{:S(2)}) collective-permute-start(bf16[2,2,128,512]{3,2,1,0:T(8,128)(2,1)S(1)} %pad_maximum_fusion.4), channel_id=1, source_target_pairs={{4,0},{6,2},{8,4},{10,6},{12,8},{14,10},{5,1},{7,3},{9,5},{11,7},{... | collective-permute-start | bytes 1572872 | tf_op jit(solution)/shard_map/ppermute | solution.py:17
  115.3 15.4 %collective-permute-start.6 = (bf16[2,2,128,512]{3,2,1,0:T(8,128)(2,1)S(1)}, bf16[2,2,128,512]{3,2,1,0:T(8,128)(2,1)S(1)}, u32[]{:S(2)}, u32[]{:S(2)}) collective-permute-start(bf16[2,2,128,512]{3,2,1,0:T(8,128)(2,1)S(1)} %pad_maximum_fusion.3), channel_id=1, source_target_pairs={{0,4},{2,6},{4,8},{6,10},{8,12},{10,14},{1,5},{3,7},{5,9},{7,11},{... | collective-permute-start | bytes 1572872 | tf_op jit(solution)/shard_map/ppermute | solution.py:17
  121.0 16.8 %collective-permute-start.16 = (bf16[4,34,1024]{2,0,1:T(4,128)(2,1)S(1)}, bf16[4,34,1024]{2,0,1:T(4,128)(2,1)S(1)}, u32[]{:S(2)}, u32[]{:S(2)}) collective-permute-start(bf16[4,34,1024]{2,0,1:T(4,128)(2,1)S(1)} %pad_maximum_fusion.8), channel_id=1, source_target_pairs={{0,2},{2,0},{4,6},{6,4},{8,10},{10,8},{12,14},{14,12},{1,3},{3,1},... | collective-permute-start | bytes 835592 | tf_op jit(solution)/shard_map/ppermute | solution.py:66
  131.1 10.1 %collective-permute-start.9 = (bf16[2,128,512]{2,1,0:T(8,128)(2,1)S(1)}, bf16[2,128,512]{2,1,0:T(8,128)(2,1)S(1)}, u32[]{:S(2)}, u32[]{:S(2)}) collective-permute-start(bf16[2,128,512]{2,1,0:T(8,128)(2,1)S(1)} %get-tuple-element.6), channel_id=1, source_target_pairs={{2,0},{4,2},{6,4},{8,6},{10,8},{12,10},{14,12},{3,1},{5,3},{7,5},{... | collective-permute-start | bytes 786440 | tf_op jit(solution)/shard_map/ppermute | solution.py:17
  133.0 13.7 %collective-permute-start.8 = (bf16[2,128,512]{2,1,0:T(8,128)(2,1)S(1)}, bf16[2,128,512]{2,1,0:T(8,128)(2,1)S(1)}, u32[]{:S(2)}, u32[]{:S(2)}) collective-permute-start(bf16[2,128,512]{2,1,0:T(8,128)(2,1)S(1)} %get-tuple-element.5), channel_id=1, source_target_pairs={{0,2},{2,4},{4,6},{6,8},{8,10},{10,12},{12,14},{1,3},{3,5},{5,7},{... | collective-permute-start | bytes 786440 | tf_op jit(solution)/shard_map/ppermute | solution.py:17
  138.6 9.1 %collective-permute-start.17 = (bf16[1,8,34,1024]{3,1,2,0:T(8,128)(2,1)S(1)}, bf16[1,8,34,1024]{3,1,2,0:T(8,128)(2,1)S(1)}, u32[]{:S(2)}, u32[]{:S(2)}) collective-permute-start(bf16[1,8,34,1024]{3,1,2,0:T(8,128)(2,1)S(1)} %maximum_bitcast_fusion), channel_id=1, source_target_pairs={{0,1},{1,0},{2,3},{3,2},{4,5},{5,4},{6,7},{7,6},{8,9},{9,8},{10,11... | collective-permute-start | bytes 1671176 | tf_op jit(solution)/shard_map/ppermute | solution.py:66

commit v19 on v17

--- a/solution.py
+++ b/solution.py
@@ -197,7 +197,7 @@
     dp_count = lax.axis_size("dp")
     members = ctx_count * dp_count
     proj_rows = proj_local.shape[0] // members
-    kernel_rows = -(-KW // members)
+    kernel_rows = -(-KW // (members * 8)) * 8
     kernel_padded = jnp.pad(kernel_local, ((0, kernel_rows * members - KW), (0, 0)))
     stacked = jnp.concatenate(
         [

time: 145 us -> 130 us (0.90)
  waiting for transfers between devices: 64.9 us -> 53.8 us
  local copies, waits for them, and re-layouts: 12.7 us -> 6.21 us
  starting transfers between devices: 37 us -> 42.1 us
    ppermute x8, waiting for transfers between devices: 23.2 us -> 16.3 us  [exchange(): return lax.ppermute(block, axis, [(i, i ^ bit) for i in range(count)])]
    ppermute x8, starting transfers between devices: 5.72 us -> 11 us  [exchange(): return lax.ppermute(block, axis, [(i, i ^ bit) for i in range(count)])]
    ppermute x8, waiting for transfers between devices: 40.1 us -> 36 us  [passed_along(): return lax.ppermute(block, axis, route)]
    reshape x2 -> x0, local copies, waits for them, and re-layouts: 1.66 us -> none  [the longest x1 1.63 us: on_device(): kernel_padded.reshape(dp_count, ctx_count, kernel_rows, channels)]
    slice x2 -> x0, local copies, waits for them, and re-layouts: 1.62 us -> none  [the longest x1 1.55 us: on_device(): proj_sum = gathered[:, :, :proj_rows].reshape(members * proj_rows, channels)]
  transfers between devices with their start and end apart: 18 -> 18, of which waited for: 13 -> 13; matrix products, arithmetic and copies ran while one was open for 9% -> 8% of each run, Pallas kernels for 0% -> 0%
where the time goes in v19:
time: 130 us; the launch traced here: 129 us
  waiting for transfers between devices  53.8 us (41%)
  starting transfers between devices  42.1 us (32%)
  other arithmetic  13.8 us (11%)
  matrix products  11.5 us (9%)
  local copies, waits for them, and re-layouts  6.21 us (5%)
  between operations  2.15 us (2%)
    ppermute x8, waiting for transfers between devices, passed_along(): return lax.ppermute(block, axis, route)  36 us
    ppermute x8, starting transfers between devices, passed_along(): return lax.ppermute(block, axis, route)  24.2 us
    ppermute x8, waiting for transfers between devices, exchange(): return lax.ppermute(block, axis, [(i, i ^ bit) for i in range(count)])  16.3 us
    ppermute x8, starting transfers between devices, exchange(): return lax.ppermute(block, axis, [(i, i ^ bit) for i in range(count)])  11 us
    dot_general x6, matrix products, contract(): lax.dot_general(lhs, rhs, (((lhs_dim,), (rhs_dim,)), ((), ())), preferred...  7.13 us
    ppermute x1, starting transfers between devices, padded(): lax.ppermute(tail, axis, [(i, (i + 1) % count) for i in range(ends)])  5 us
    convert_element_type x1, other arithmetic, on_device(): grad_conv = (cot_wide.astype(jnp.float32) * (sigmoid_c + conv_out * sigmo...  3.04 us
  transfers between devices with their start and end apart: 18, of which 13 were waited for; matrix products, arithmetic and copies ran while one was open for 8% of the time, Pallas kernels for 0%

profile of v19, /device:TPU:2, one launch (start us, length us, event | category | flops | bytes accessed | tf_op | source)
XLA Modules:
  0.0 129.5 jit_solution(3080006892770721597)
XLA Ops:
  0.6 0.9 slice_bitcast_fusion.10
  1.6 0.9 constant_dynamic-update-slice_fusion.1
  2.5 1.0 constant_dynamic-update-slice_fusion
  3.6 1.9 %collective-permute-start.2 = (bf16[288,512]{1,0:T(8,128)(2,1)S(1)}, bf16[288,512]{1,0:T(8,128)(2,1)S(1)}, u32[]{:S(2)}, u32[]{:S(2)}) collective-permute-start(bf16[288,512]{1,0:T(8,128)(2,1)S(1)} %get-tuple-element.33), channel_id=1, source_target_pairs={{2,0},{4,2},{6,4},{8,6},{10,8},{12,10},{14,12},{3,1},{5,3},{7,5},{... | collective-permute-start | bytes 884744 | tf_op jit(solution)/shard_map/ppermute | solution.py:17
  5.5 4.8 %collective-permute-start = (bf16[288,512]{1,0:T(8,128)(2,1)S(1)}, bf16[288,512]{1,0:T(8,128)(2,1)S(1)}, u32[]{:S(2)}, u32[]{:S(2)}) collective-permute-start(bf16[288,512]{1,0:T(8,128)(2,1)S(1)} %get-tuple-element.34), channel_id=1, source_target_pairs={{0,2},{2,4},{4,6},{6,8},{8,10},{10,12},{12,14},{1,3},{3,5},{5,7},{... | collective-permute-start | bytes 884744 | tf_op jit(solution)/shard_map/ppermute | solution.py:17
  11.0 4.2 %collective-permute-done.2 = bf16[288,512]{1,0:T(8,128)(2,1)S(1)} collective-permute-done((bf16[288,512]{1,0:T(8,128)(2,1)S(1)}, bf16[288,512]{1,0:T(8,128)(2,1)S(1)}, u32[]{:S(2)}, u32[]{:S(2)}) %collective-permute-start.2) | collective-permute-done | bytes 294944 | tf_op jit(solution)/shard_map/ppermute | solution.py:17
  15.2 6.2 %collective-permute-done = bf16[288,512]{1,0:T(8,128)(2,1)S(1)} collective-permute-done((bf16[288,512]{1,0:T(8,128)(2,1)S(1)}, bf16[288,512]{1,0:T(8,128)(2,1)S(1)}, u32[]{:S(2)}, u32[]{:S(2)}) %collective-permute-start) | collective-permute-done | bytes 294944 | tf_op jit(solution)/shard_map/ppermute | solution.py:17
  21.6 3.5 %collective-permute-start.1 = (bf16[2,2,128,512]{3,2,1,0:T(8,128)(2,1)S(1)}, bf16[2,2,128,512]{3,2,1,0:T(8,128)(2,1)S(1)}, u32[]{:S(2)}, u32[]{:S(2)}) collective-permute-start(bf16[2,2,128,512]{3,2,1,0:T(8,128)(2,1)S(1)} %get-tuple-element.32), channel_id=1, source_target_pairs={{0,4},{2,6},{4,8},{6,10},{8,12},{10,14},{1,5},{3,7},{5,9},{7,11},{... | collective-permute-start | bytes 1572872 | tf_op jit(solution)/shard_map/ppermute | solution.py:17
  25.3 1.3 collective-permute-start.3
  26.6 9.8 %collective-permute-done.1 = bf16[2,2,128,512]{3,2,1,0:T(8,128)(2,1)S(1)} collective-permute-done((bf16[2,2,128,512]{3,2,1,0:T(8,128)(2,1)S(1)}, bf16[2,2,128,512]{3,2,1,0:T(8,128)(2,1)S(1)}, u32[]{:S(2)}, u32[]{:S(2)}) %collective-permute-start.1) | collective-permute-done | bytes 524320 | tf_op jit(solution)/shard_map/ppermute | solution.py:17
  36.5 4.2 %collective-permute-done.3 = bf16[2,2,128,512]{3,2,1,0:T(8,128)(2,1)S(1)} collective-permute-done((bf16[2,2,128,512]{3,2,1,0:T(8,128)(2,1)S(1)}, bf16[2,2,128,512]{3,2,1,0:T(8,128)(2,1)S(1)}, u32[]{:S(2)}, u32[]{:S(2)}) %collective-permute-start.3) | collective-permute-done | bytes 524320 | tf_op jit(solution)/shard_map/ppermute | solution.py:17
  40.8 1.2 fusion
  42.0 0.8 exponential_reduce_fusion
  42.8 0.7 exponential_convert_fusion
  43.6 1.3 fusion.48
  45.5 1.9 %collective-permute-start.5 = (bf16[30,1024]{1,0:T(8,128)(2,1)S(1)}, bf16[30,1024]{1,0:T(8,128)(2,1)S(1)}, u32[]{:S(2)}, u32[]{:S(2)}) collective-permute-start(bf16[30,1024]{1,0:T(8,128)(2,1)S(1)} %get-tuple-element.30), channel_id=1, source_target_pairs={{2,0},{4,2},{6,4},{8,6},{10,8},{12,10},{14,12},{3,1},{5,3},{7,5},{... | collective-permute-start | bytes 184328 | tf_op jit(solution)/shard_map/ppermute | solution.py:30
  47.4 5.0 %collective-permute-start.4 = (bf16[30,1024]{1,0:T(8,128)(2,1)S(1)}, bf16[30,1024]{1,0:T(8,128)(2,1)S(1)}, u32[]{:S(2)}, u32[]{:S(2)}) collective-permute-start(bf16[30,1024]{1,0:T(8,128)(2,1)S(1)} %get-tuple-element.29), channel_id=1, source_target_pairs={{0,2},{2,4},{4,6},{6,8},{8,10},{10,12},{12,14},{1,3},{3,5},{5,7},{... | collective-permute-start | bytes 184328 | tf_op jit(solution)/shard_map/ppermute | solution.py:28
  52.6 1.6 %collective-permute-done.4 = bf16[30,1024]{1,0:T(8,128)(2,1)S(1)} collective-permute-done((bf16[30,1024]{1,0:T(8,128)(2,1)S(1)}, bf16[30,1024]{1,0:T(8,128)(2,1)S(1)}, u32[]{:S(2)}, u32[]{:S(2)}) %collective-permute-start.4) | collective-permute-done | bytes 61472 | tf_op jit(solution)/shard_map/ppermute | solution.py:28
  54.4 3.0 %multiply_convert_fusion.1 = bf16[158,1024]{1,0:T(8,128)(2,1)S(1)} fusion(bf16[188,1024]{1,0:T(8,128)(2,1)S(1)} %pad_maximum_fusion.5, bf16[15,1024]{1,0:T(8,128)(2,1)S(1)} %slice.485, bf16[128,1024]{1,0:T(8,128)(2,1)S(1)} %bitcast.167, bf16[15,1024]{1,0:T(8,128)(2,1)S(1)} %slice.483, bf16[128,1024]{1,0:T(8,128)(2,1)S(1)} %fusion.5, ...), kind=kLoop, calls=%fused_computation.31 | loop fusion | flops 18282496 | bytes 10543104 | tf_op jit(solution)/shard_map/convert_element_type | solution.py:174
  57.4 2.2 %add_convert_fusion = bf16[128,1024]{1,0:T(8,128)(2,1)S(1)} fusion(bf16[158,1024]{1,0:T(8,128)(2,1)S(1)} %multiply_convert_fusion.1, f32[1024]{0:T(1024)S(1)} %bitcast.239, f32[1024]{0:T(1024)S(1)} %bitcast.241, f32[1024]{0:T(1024)S(1)} %bitcast.183, f32[1024]{0:T(1024)S(1)} %bitcast.185, f32[1024]{0:T(1024)S(1)} %bitcast.187, f32[1024]{0:T(1024)S(1)} %bitcast.189, ...), kind=kLoop, calls=%fused_computation.54 | loop fusion | flops 12582912 | bytes 8777856 | tf_op jit(solution)/shard_map/convert_element_type | solution.py:192
  60.2 2.4 %fusion.7 = f32[1,31,1024]{2,0,1:T(1,128)S(1)} fusion(bf16[1,158,1024]{2,1,0:T(8,128)(2,1)S(1)} %slice_bitcast_fusion, bf16[128,1,1024]{2,0,1:T(8,128)(2,1)S(1)} %slice_bitcast_fusion.1), kind=kOutput, calls=%fused_computation.34 | convolution fusion | flops 8126464 | bytes 712704 | tf_op jit(solution)/shard_map/conv_general_dilated | solution.py:181
  62.6 0.8 copy-done.1
  63.4 0.9 fusion.2
  64.4 1.2 convert_multiply_fusion
  65.6 1.1 copy.19
  66.8 1.3 %fusion.4 = f32[1,8,40,1024]{3,2,1,0:T(8,128)S(1)} fusion(s32[]{:T(128)S(6)} %select_n.165, f32[2,8,32,1024]{3,2,1,0:T(8,128)S(1)} %bitcast.156, f32[2,8,8,1024]{3,2,1,0:T(8,128)} %bitcast.162, bf16[1,8,40,1024]{3,2,1,0:T(8,128)(2,1)} %collective-permute-done.10), kind=kLoop, calls=%fused_computation.19 | loop fusion | flops 983040 | bytes 4587524 | tf_op jit(solution)/shard_map/add | solution.py:78
  68.5 9.9 %collective-permute-done.11 = bf16[4,40,1024]{2,1,0:T(8,128)(2,1)S(1)} collective-permute-done((bf16[4,40,1024]{2,1,0:T(8,128)(2,1)S(1)}, bf16[4,40,1024]{2,1,0:T(8,128)(2,1)S(1)}, u32[]{:S(2)}, u32[]{:S(2)}) %collective-permute-start.11) | collective-permute-done | bytes 327712 | tf_op jit(solution)/shard_map/ppermute | solution.py:66
  78.5 2.1 %collective-permute-start.12 = (bf16[2,40,1024]{2,1,0:T(8,128)(2,1)S(1)}, bf16[2,40,1024]{2,1,0:T(8,128)(2,1)S(1)}, u32[]{:S(2)}, u32[]{:S(2)}) collective-permute-start(bf16[2,40,1024]{2,1,0:T(8,128)(2,1)S(1)} %dynamic-slice_convert_fusion.1), channel_id=1, source_target_pairs={{0,4},{2,6},{4,0},{6,2},{8,12},{10,14},{12,8},{14,10},{1,5},{3,7},... | collective-permute-start | bytes 491528 | tf_op jit(solution)/shard_map/ppermute | solution.py:66
  80.6 1.1 multiply_convert_fusion
  81.8 3.1 %collective-permute-done.12 = bf16[2,40,1024]{2,1,0:T(8,128)(2,1)S(1)} collective-permute-done((bf16[2,40,1024]{2,1,0:T(8,128)(2,1)S(1)}, bf16[2,40,1024]{2,1,0:T(8,128)(2,1)S(1)}, u32[]{:S(2)}, u32[]{:S(2)}) %collective-permute-start.12) | collective-permute-done | bytes 163872 | tf_op jit(solution)/shard_map/ppermute | solution.py:66
  84.9 2.8 %collective-permute-start.13 = (bf16[1,40,1024]{2,1,0:T(8,128)(2,1)S(1)}, bf16[1,40,1024]{2,1,0:T(8,128)(2,1)S(1)}, u32[]{:S(2)}, u32[]{:S(2)}) collective-permute-start(bf16[1,40,1024]{2,1,0:T(8,128)(2,1)S(1)} %dynamic-slice_convert_fusion.2), channel_id=1, source_target_pairs={{0,8},{2,10},{4,12},{6,14},{8,0},{10,2},{12,4},{14,6},{1,9},{3,11}... | collective-permute-start | bytes 245768 | tf_op jit(solution)/shard_map/ppermute | solution.py:66
  87.7 1.1 fusion.46
  88.8 1.6 %collective-permute-done.13 = bf16[1,40,1024]{2,1,0:T(8,128)(2,1)S(1)} collective-permute-done((bf16[1,40,1024]{2,1,0:T(8,128)(2,1)S(1)}, bf16[1,40,1024]{2,1,0:T(8,128)(2,1)S(1)}, u32[]{:S(2)}, u32[]{:S(2)}) %collective-permute-start.13) | collective-permute-done | bytes 81952 | tf_op jit(solution)/shard_map/ppermute | solution.py:66
  90.5 2.7 %collective-permute-start.14 = (bf16[1,40,1024]{2,1,0:T(8,128)(2,1)S(1)}, bf16[1,40,1024]{2,1,0:T(8,128)(2,1)S(1)}, u32[]{:S(2)}, u32[]{:S(2)}) collective-permute-start(bf16[1,40,1024]{2,1,0:T(8,128)(2,1)S(1)} %add_convert_fusion.1), channel_id=1, source_target_pairs={{0,8},{2,10},{4,12},{6,14},{8,0},{10,2},{12,4},{14,6},{1,9},{3,11}... | collective-permute-start | bytes 245768 | tf_op jit(solution)/shard_map/ppermute | solution.py:66
  93.2 1.1 fusion.47
  94.3 1.6 %collective-permute-done.14 = bf16[1,40,1024]{2,1,0:T(8,128)(2,1)S(1)} collective-permute-done((bf16[1,40,1024]{2,1,0:T(8,128)(2,1)S(1)}, bf16[1,40,1024]{2,1,0:T(8,128)(2,1)S(1)}, u32[]{:S(2)}, u32[]{:S(2)}) %collective-permute-start.14) | collective-permute-done | bytes 81952 | tf_op jit(solution)/shard_map/ppermute | solution.py:66
  95.9 1.7 %collective-permute-start.15 = (bf16[2,40,1024]{2,1,0:T(8,128)(2,1)S(1)}, bf16[2,40,1024]{2,1,0:T(8,128)(2,1)S(1)}, u32[]{:S(2)}, u32[]{:S(2)}) collective-permute-start(bf16[2,40,1024]{2,1,0:T(8,128)(2,1)S(1)} %pad_maximum_fusion.10), channel_id=1, source_target_pairs={{0,4},{2,6},{4,0},{6,2},{8,12},{10,14},{12,8},{14,10},{1,5},{3,7},... | collective-permute-start | bytes 491528 | tf_op jit(solution)/shard_map/ppermute | solution.py:66
  97.6 1.3 %fusion.49 = f32[1024,512]{1,0:T(8,128)S(1)} fusion(bf16[1024,896]{0,1:T(8,128)(2,1)S(1)} %multiply_convert_fusion, bf16[896,512]{1,0:T(8,128)(2,1)S(1)} %copy-done.15), kind=kOutput, calls=%fused_computation.132 | convolution fusion | flops 939524096 | bytes 4849664 | tf_op jit(solution)/shard_map/dot_general | solution.py:151
  99.0 1.3 collective-permute-start.7
  100.3 4.6 %collective-permute-start.6 = (bf16[2,2,128,512]{3,2,1,0:T(8,128)(2,1)S(1)}, bf16[2,2,128,512]{3,2,1,0:T(8,128)(2,1)S(1)}, u32[]{:S(2)}, u32[]{:S(2)}) collective-permute-start(bf16[2,2,128,512]{3,2,1,0:T(8,128)(2,1)S(1)} %get-tuple-element.5), channel_id=1, source_target_pairs={{0,4},{2,6},{4,8},{6,10},{8,12},{10,14},{1,5},{3,7},{5,9},{7,11},{... | collective-permute-start | bytes 1572872 | tf_op jit(solution)/shard_map/ppermute | solution.py:17
  105.0 1.5 %collective-permute-start.16 = (bf16[4,40,1024]{2,1,0:T(8,128)(2,1)S(1)}, bf16[4,40,1024]{2,1,0:T(8,128)(2,1)S(1)}, u32[]{:S(2)}, u32[]{:S(2)}) collective-permute-start(bf16[4,40,1024]{2,1,0:T(8,128)(2,1)S(1)} %pad_maximum_fusion.6), channel_id=1, source_target_pairs={{0,2},{2,0},{4,6},{6,4},{8,10},{10,8},{12,14},{14,12},{1,3},{3,1},... | collective-permute-start | bytes 983048 | tf_op jit(solution)/shard_map/ppermute | solution.py:66
  106.9 5.6 %collective-permute-done.7 = bf16[2,2,128,512]{3,2,1,0:T(8,128)(2,1)S(1)} collective-permute-done((bf16[2,2,128,512]{3,2,1,0:T(8,128)(2,1)S(1)}, bf16[2,2,128,512]{3,2,1,0:T(8,128)(2,1)S(1)}, u32[]{:S(2)}, u32[]{:S(2)}) %collective-permute-start.7) | collective-permute-done | bytes 524320 | tf_op jit(solution)/shard_map/ppermute | solution.py:17
  113.1 3.5 %collective-permute-start.9 = (bf16[2,128,512]{2,1,0:T(8,128)(2,1)S(1)}, bf16[2,128,512]{2,1,0:T(8,128)(2,1)S(1)}, u32[]{:S(2)}, u32[]{:S(2)}) collective-permute-start(bf16[2,128,512]{2,1,0:T(8,128)(2,1)S(1)} %get-tuple-element.8), channel_id=1, source_target_pairs={{2,0},{4,2},{6,4},{8,6},{10,8},{12,10},{14,12},{3,1},{5,3},{7,5},{... | collective-permute-start | bytes 786440 | tf_op jit(solution)/shard_map/ppermute | solution.py:17
  116.6 3.3 %collective-permute-start.8 = (bf16[2,128,512]{2,1,0:T(8,128)(2,1)S(1)}, bf16[2,128,512]{2,1,0:T(8,128)(2,1)S(1)}, u32[]{:S(2)}, u32[]{:S(2)}) collective-permute-start(bf16[2,128,512]{2,1,0:T(8,128)(2,1)S(1)} %get-tuple-element.7), channel_id=1, source_target_pairs={{0,2},{2,4},{4,6},{6,8},{8,10},{10,12},{12,14},{1,3},{3,5},{5,7},{... | collective-permute-start | bytes 786440 | tf_op jit(solution)/shard_map/ppermute | solution.py:17
  120.7 1.6 %collective-permute-done.9 = bf16[2,128,512]{2,1,0:T(8,128)(2,1)S(1)} collective-permute-done((bf16[2,128,512]{2,1,0:T(8,128)(2,1)S(1)}, bf16[2,128,512]{2,1,0:T(8,128)(2,1)S(1)}, u32[]{:S(2)}, u32[]{:S(2)}) %collective-permute-start.9) | collective-permute-done | bytes 262176 | tf_op jit(solution)/shard_map/ppermute | solution.py:17
  122.4 4.3 %collective-permute-done.8 = bf16[2,128,512]{2,1,0:T(8,128)(2,1)S(1)} collective-permute-done((bf16[2,128,512]{2,1,0:T(8,128)(2,1)S(1)}, bf16[2,128,512]{2,1,0:T(8,128)(2,1)S(1)}, u32[]{:S(2)}, u32[]{:S(2)}) %collective-permute-start.8) | collective-permute-done | bytes 262176 | tf_op jit(solution)/shard_map/ppermute | solution.py:17
  126.9 0.7 fusion.42
  127.7 1.1 fusion.6
  (102 shorter events, 5.5 us)
Async XLA Ops:
  0.6 44.5 %copy-start = (bf16[512,1024]{1,0:T(8,128)(2,1)S(1)}, bf16[512,1024]{1,0:T(8,128)(2,1)}, u32[]{:S(2)}) copy-start(bf16[512,1024]{1,0:T(8,128)(2,1)} %param.11) | copy-start | bytes 3145732
  2.5 22.6 %copy-start.11 = (f32[31,1024]{1,0:T(8,128)S(1)}, f32[31,1024]{1,0:T(8,128)}, u32[]{:S(2)}) copy-start(f32[31,1024]{1,0:T(8,128)} %param.12) | copy-start | bytes 380932
  2.5 22.6 %copy-start.10 = (bf16[1,128,512]{2,1,0:T(8,128)(2,1)S(1)}, bf16[1,128,512]{2,1,0:T(8,128)(2,1)}, u32[]{:S(2)}) copy-start(bf16[1,128,512]{2,1,0:T(8,128)(2,1)} %param.7) | copy-start | bytes 393220
  3.6 11.6 %collective-permute-start.2 = (bf16[288,512]{1,0:T(8,128)(2,1)S(1)}, bf16[288,512]{1,0:T(8,128)(2,1)S(1)}, u32[]{:S(2)}, u32[]{:S(2)}) collective-permute-start(bf16[288,512]{1,0:T(8,128)(2,1)S(1)} %get-tuple-element.33), channel_id=1, source_target_pairs={{2,0},{4,2},{6,4},{8,6},{10,8},{12,10},{14,12},{3,1},{5,3},{7,5},{... | collective-permute-start | bytes 884744 | tf_op jit(solution)/shard_map/ppermute | solution.py:17
  5.5 15.9 %collective-permute-start = (bf16[288,512]{1,0:T(8,128)(2,1)S(1)}, bf16[288,512]{1,0:T(8,128)(2,1)S(1)}, u32[]{:S(2)}, u32[]{:S(2)}) collective-permute-start(bf16[288,512]{1,0:T(8,128)(2,1)S(1)} %get-tuple-element.34), channel_id=1, source_target_pairs={{0,2},{2,4},{4,6},{6,8},{8,10},{10,12},{12,14},{1,3},{3,5},{5,7},{... | collective-permute-start | bytes 884744 | tf_op jit(solution)/shard_map/ppermute | solution.py:17
  21.4 15.0 %copy-start.8 = (bf16[1,128,512]{2,1,0:T(8,128)(2,1)S(1)}, bf16[1,128,512]{2,1,0:T(8,128)(2,1)}, u32[]{:S(2)}) copy-start(bf16[1,128,512]{2,1,0:T(8,128)(2,1)} %param.8) | copy-start | bytes 393220
  21.5 15.0 %copy-start.9 = (bf16[1,128,512]{2,1,0:T(8,128)(2,1)S(1)}, bf16[1,128,512]{2,1,0:T(8,128)(2,1)}, u32[]{:S(2)}) copy-start(bf16[1,128,512]{2,1,0:T(8,128)(2,1)} %param.9) | copy-start | bytes 393220
  21.6 14.8 %collective-permute-start.1 = (bf16[2,2,128,512]{3,2,1,0:T(8,128)(2,1)S(1)}, bf16[2,2,128,512]{3,2,1,0:T(8,128)(2,1)S(1)}, u32[]{:S(2)}, u32[]{:S(2)}) collective-permute-start(bf16[2,2,128,512]{3,2,1,0:T(8,128)(2,1)S(1)} %get-tuple-element.32), channel_id=1, source_target_pairs={{0,4},{2,6},{4,8},{6,10},{8,12},{10,14},{1,5},{3,7},{5,9},{7,11},{... | collective-permute-start | bytes 1572872 | tf_op jit(solution)/shard_map/ppermute | solution.py:17
  25.3 16.7 %copy-start.5 = (bf16[8,128,512]{2,1,0:T(8,128)(2,1)}, bf16[8,128,512]{2,1,0:T(8,128)(2,1)S(1)}, u32[]{:S(2)}) copy-start(bf16[8,128,512]{2,1,0:T(8,128)(2,1)S(1)} %broadcast_select_fusion.1) | copy-start | bytes 3145732
  25.3 15.5 %collective-permute-start.3 = (bf16[2,2,128,512]{3,2,1,0:T(8,128)(2,1)S(1)}, bf16[2,2,128,512]{3,2,1,0:T(8,128)(2,1)S(1)}, u32[]{:S(2)}, u32[]{:S(2)}) collective-permute-start(bf16[2,2,128,512]{3,2,1,0:T(8,128)(2,1)S(1)} %get-tuple-element.31), channel_id=1, source_target_pairs={{4,0},{6,2},{8,4},{10,6},{12,8},{14,10},{5,1},{7,3},{9,5},{11,7},{... | collective-permute-start | bytes 1572872 | tf_op jit(solution)/shard_map/ppermute | solution.py:17
  40.8 1.2 copy-start.14
  40.8 2.8 %copy-start.12 = (bf16[896,512]{1,0:T(8,128)(2,1)}, bf16[896,512]{1,0:T(8,128)(2,1)S(1)}, u32[]{:S(2)}) copy-start(bf16[896,512]{1,0:T(8,128)(2,1)S(1)} %get-tuple-element.13) | copy-start | bytes 2752516
  43.6 1.3 %copy-start.2 = (bf16[1024,896]{0,1:T(8,128)(2,1)}, bf16[1024,896]{0,1:T(8,128)(2,1)S(1)}, u32[]{:S(2)}) copy-start(bf16[1024,896]{0,1:T(8,128)(2,1)S(1)} %exponential_convert_fusion) | copy-start | bytes 5505028
  45.2 9.2 %copy-start.4 = (bf16[1,128,1024]{2,1,0:T(8,128)(2,1)S(1)}, bf16[1,128,1024]{2,1,0:T(8,128)(2,1)}, u32[]{:S(2)}) copy-start(bf16[1,128,1024]{2,1,0:T(8,128)(2,1)} %param.10) | copy-start | bytes 786436
  45.5 7.1 %collective-permute-start.5 = (bf16[30,1024]{1,0:T(8,128)(2,1)S(1)}, bf16[30,1024]{1,0:T(8,128)(2,1)S(1)}, u32[]{:S(2)}, u32[]{:S(2)}) collective-permute-start(bf16[30,1024]{1,0:T(8,128)(2,1)S(1)} %get-tuple-element.30), channel_id=1, source_target_pairs={{2,0},{4,2},{6,4},{8,6},{10,8},{12,10},{14,12},{3,1},{5,3},{7,5},{... | collective-permute-start | bytes 184328 | tf_op jit(solution)/shard_map/ppermute | solution.py:30
  47.4 6.7 %collective-permute-start.4 = (bf16[30,1024]{1,0:T(8,128)(2,1)S(1)}, bf16[30,1024]{1,0:T(8,128)(2,1)S(1)}, u32[]{:S(2)}, u32[]{:S(2)}) collective-permute-start(bf16[30,1024]{1,0:T(8,128)(2,1)S(1)} %get-tuple-element.29), channel_id=1, source_target_pairs={{0,2},{2,4},{4,6},{6,8},{8,10},{10,12},{12,14},{1,3},{3,5},{5,7},{... | collective-permute-start | bytes 184328 | tf_op jit(solution)/shard_map/ppermute | solution.py:28
  62.6 0.8 copy-start.1
  64.4 2.4 %collective-permute-start.10 = (bf16[1,8,40,1024]{3,2,1,0:T(8,128)(2,1)}, bf16[1,8,40,1024]{3,2,1,0:T(8,128)(2,1)}, u32[]{:S(2)}, u32[]{:S(2)}) collective-permute-start(bf16[1,8,40,1024]{3,2,1,0:T(8,128)(2,1)} %fusion.2), channel_id=1, source_target_pairs={{0,1},{1,0},{2,3},{3,2},{4,5},{5,4},{6,7},{7,6},{8,9},{9,8},{10,11... | collective-permute-start | bytes 1966088 | tf_op jit(solution)/shard_map/ppermute | solution.py:66
  66.7 1.7 %copy-start.7 = (bf16[128,512]{1,0:T(8,128)(2,1)S(1)}, bf16[128,512]{1,0:T(8,128)(2,1)}, u32[]{:S(2)}) copy-start(bf16[128,512]{1,0:T(8,128)(2,1)} %get-tuple-element.73) | copy-start | bytes 393220
  68.2 12.5 %copy-start.3 = (bf16[1024,896]{0,1:T(8,128)(2,1)S(1)}, bf16[1024,896]{0,1:T(8,128)(2,1)}, u32[]{:S(2)}) copy-start(bf16[1024,896]{0,1:T(8,128)(2,1)} %copy-done.2) | copy-start | bytes 5505028
  68.2 12.4 %copy-start.13 = (bf16[896,512]{1,0:T(8,128)(2,1)S(1)}, bf16[896,512]{1,0:T(8,128)(2,1)}, u32[]{:S(2)}) copy-start(bf16[896,512]{1,0:T(8,128)(2,1)} %copy-done.12) | copy-start | bytes 2752516
  68.2 10.1 %collective-permute-start.11 = (bf16[4,40,1024]{2,1,0:T(8,128)(2,1)S(1)}, bf16[4,40,1024]{2,1,0:T(8,128)(2,1)S(1)}, u32[]{:S(2)}, u32[]{:S(2)}) collective-permute-start(bf16[4,40,1024]{2,1,0:T(8,128)(2,1)S(1)} %fusion.21), channel_id=1, source_target_pairs={{0,2},{2,0},{4,6},{6,4},{8,10},{10,8},{12,14},{14,12},{1,3},{3,1},... | collective-permute-start | bytes 983048 | tf_op jit(solution)/shard_map/ppermute | solution.py:66
  78.5 6.4 %collective-permute-start.12 = (bf16[2,40,1024]{2,1,0:T(8,128)(2,1)S(1)}, bf16[2,40,1024]{2,1,0:T(8,128)(2,1)S(1)}, u32[]{:S(2)}, u32[]{:S(2)}) collective-permute-start(bf16[2,40,1024]{2,1,0:T(8,128)(2,1)S(1)} %dynamic-slice_convert_fusion.1), channel_id=1, source_target_pairs={{0,4},{2,6},{4,0},{6,2},{8,12},{10,14},{12,8},{14,10},{1,5},{3,7},... | collective-permute-start | bytes 491528 | tf_op jit(solution)/shard_map/ppermute | solution.py:66
  84.9 8.2 %copy-start.6 = (bf16[8,128,512]{2,1,0:T(8,128)(2,1)S(1)}, bf16[8,128,512]{2,1,0:T(8,128)(2,1)}, u32[]{:S(2)}) copy-start(bf16[8,128,512]{2,1,0:T(8,128)(2,1)} %copy-done.5) | copy-start | bytes 3145732
  84.9 5.5 %collective-permute-start.13 = (bf16[1,40,1024]{2,1,0:T(8,128)(2,1)S(1)}, bf16[1,40,1024]{2,1,0:T(8,128)(2,1)S(1)}, u32[]{:S(2)}, u32[]{:S(2)}) collective-permute-start(bf16[1,40,1024]{2,1,0:T(8,128)(2,1)S(1)} %dynamic-slice_convert_fusion.2), channel_id=1, source_target_pairs={{0,8},{2,10},{4,12},{6,14},{8,0},{10,2},{12,4},{14,6},{1,9},{3,11}... | collective-permute-start | bytes 245768 | tf_op jit(solution)/shard_map/ppermute | solution.py:66
  90.4 7.2 %copy-start.15 = (bf16[896,512]{1,0:T(8,128)(2,1)S(1)}, bf16[896,512]{1,0:T(8,128)(2,1)}, u32[]{:S(2)}) copy-start(bf16[896,512]{1,0:T(8,128)(2,1)} %copy-done.14) | copy-start | bytes 2752516
  90.5 5.4 %collective-permute-start.14 = (bf16[1,40,1024]{2,1,0:T(8,128)(2,1)S(1)}, bf16[1,40,1024]{2,1,0:T(8,128)(2,1)S(1)}, u32[]{:S(2)}, u32[]{:S(2)}) collective-permute-start(bf16[1,40,1024]{2,1,0:T(8,128)(2,1)S(1)} %add_convert_fusion.1), channel_id=1, source_target_pairs={{0,8},{2,10},{4,12},{6,14},{8,0},{10,2},{12,4},{14,6},{1,9},{3,11}... | collective-permute-start | bytes 245768 | tf_op jit(solution)/shard_map/ppermute | solution.py:66
  95.9 9.0 %collective-permute-start.15 = (bf16[2,40,1024]{2,1,0:T(8,128)(2,1)S(1)}, bf16[2,40,1024]{2,1,0:T(8,128)(2,1)S(1)}, u32[]{:S(2)}, u32[]{:S(2)}) collective-permute-start(bf16[2,40,1024]{2,1,0:T(8,128)(2,1)S(1)} %pad_maximum_fusion.10), channel_id=1, source_target_pairs={{0,4},{2,6},{4,0},{6,2},{8,12},{10,14},{12,8},{14,10},{1,5},{3,7},... | collective-permute-start | bytes 491528 | tf_op jit(solution)/shard_map/ppermute | solution.py:66
  99.0 13.5 %collective-permute-start.7 = (bf16[2,2,128,512]{3,2,1,0:T(8,128)(2,1)S(1)}, bf16[2,2,128,512]{3,2,1,0:T(8,128)(2,1)S(1)}, u32[]{:S(2)}, u32[]{:S(2)}) collective-permute-start(bf16[2,2,128,512]{3,2,1,0:T(8,128)(2,1)S(1)} %get-tuple-element.6), channel_id=1, source_target_pairs={{4,0},{6,2},{8,4},{10,6},{12,8},{14,10},{5,1},{7,3},{9,5},{11,7},{... | collective-permute-start | bytes 1572872 | tf_op jit(solution)/shard_map/ppermute | solution.py:17
  100.3 12.4 %collective-permute-start.6 = (bf16[2,2,128,512]{3,2,1,0:T(8,128)(2,1)S(1)}, bf16[2,2,128,512]{3,2,1,0:T(8,128)(2,1)S(1)}, u32[]{:S(2)}, u32[]{:S(2)}) collective-permute-start(bf16[2,2,128,512]{3,2,1,0:T(8,128)(2,1)S(1)} %get-tuple-element.5), channel_id=1, source_target_pairs={{0,4},{2,6},{4,8},{6,10},{8,12},{10,14},{1,5},{3,7},{5,9},{7,11},{... | collective-permute-start | bytes 1572872 | tf_op jit(solution)/shard_map/ppermute | solution.py:17
  105.0 14.9 %collective-permute-start.16 = (bf16[4,40,1024]{2,1,0:T(8,128)(2,1)S(1)}, bf16[4,40,1024]{2,1,0:T(8,128)(2,1)S(1)}, u32[]{:S(2)}, u32[]{:S(2)}) collective-permute-start(bf16[4,40,1024]{2,1,0:T(8,128)(2,1)S(1)} %pad_maximum_fusion.6), channel_id=1, source_target_pairs={{0,2},{2,0},{4,6},{6,4},{8,10},{10,8},{12,14},{14,12},{1,3},{3,1},... | collective-permute-start | bytes 983048 | tf_op jit(solution)/shard_map/ppermute | solution.py:66
  113.1 9.3 %collective-permute-start.9 = (bf16[2,128,512]{2,1,0:T(8,128)(2,1)S(1)}, bf16[2,128,512]{2,1,0:T(8,128)(2,1)S(1)}, u32[]{:S(2)}, u32[]{:S(2)}) collective-permute-start(bf16[2,128,512]{2,1,0:T(8,128)(2,1)S(1)} %get-tuple-element.8), channel_id=1, source_target_pairs={{2,0},{4,2},{6,4},{8,6},{10,8},{12,10},{14,12},{3,1},{5,3},{7,5},{... | collective-permute-start | bytes 786440 | tf_op jit(solution)/shard_map/ppermute | solution.py:17
  116.6 10.1 %collective-permute-start.8 = (bf16[2,128,512]{2,1,0:T(8,128)(2,1)S(1)}, bf16[2,128,512]{2,1,0:T(8,128)(2,1)S(1)}, u32[]{:S(2)}, u32[]{:S(2)}) collective-permute-start(bf16[2,128,512]{2,1,0:T(8,128)(2,1)S(1)} %get-tuple-element.7), channel_id=1, source_target_pairs={{0,2},{2,4},{4,6},{6,8},{8,10},{10,12},{12,14},{1,3},{3,5},{5,7},{... | collective-permute-start | bytes 786440 | tf_op jit(solution)/shard_map/ppermute | solution.py:17
  120.0 7.6 %collective-permute-start.17 = (bf16[1,8,40,1024]{3,2,1,0:T(8,128)(2,1)S(1)}, bf16[1,8,40,1024]{3,2,1,0:T(8,128)(2,1)S(1)}, u32[]{:S(2)}, u32[]{:S(2)}) collective-permute-start(bf16[1,8,40,1024]{3,2,1,0:T(8,128)(2,1)S(1)} %maximum_bitcast_fusion), channel_id=1, source_target_pairs={{0,1},{1,0},{2,3},{3,2},{4,5},{5,4},{6,7},{7,6},{8,9},{9,8},{10,11... | collective-permute-start | bytes 1966088 | tf_op jit(solution)/shard_map/ppermute | solution.py:66

commit v20 on v19

--- a/solution.py
+++ b/solution.py
@@ -164,10 +164,12 @@
     masked = jnp.where(valid_rows[:, None], hidden, 0.0).astype(jnp.bfloat16)
 
     wide_rows = tokens + 2 * halo_width
-    padded_m = padded(masked, (("ctx", 0),), 2 * halo_width)
+    edge = -(-2 * halo_width // 8) * 8
+    lead = edge - 2 * halo_width
+    padded_m = padded(masked, (("ctx", 0),), edge)
     conv_out = jnp.zeros((wide_rows, channels), jnp.float32)
     for tap_index in range(KW):
-        conv_out = conv_out + conv_kernel[tap_index] * padded_m[tap_index : tap_index + wide_rows]
+        conv_out = conv_out + conv_kernel[tap_index] * padded_m[lead + tap_index : lead + tap_index + wide_rows]
     sigmoid_c = jax.nn.sigmoid(conv_out)
     grad_conv = (
         cot_wide.astype(jnp.float32) * (sigmoid_c + conv_out * sigmoid_c * (1.0 - sigmoid_c))
@@ -179,7 +181,7 @@
             grad_masked + conv_kernel[tap_index] * grad_conv[start_row : start_row + tokens]
         )
     kernel_local = lax.conv_general_dilated(
-        padded_m[None, halo_width : halo_width + wide_rows],
+        padded_m[None, lead + halo_width : lead + halo_width + wide_rows],
         grad_conv[halo_width : halo_width + tokens, None, :],
         window_strides=(1,),
         padding="VALID",

time: 130 us -> 130 us (level)
  no operation moved by 1% of the time
where the time goes in v20:
time: 130 us; the launch traced here: 129 us
  waiting for transfers between devices  53.8 us (41%)
  starting transfers between devices  42 us (32%)
  other arithmetic  13.7 us (11%)
  matrix products  11.5 us (9%)
  local copies, waits for them, and re-layouts  6.21 us (5%)
  between operations  2.15 us (2%)
    ppermute x8, waiting for transfers between devices, passed_along(): return lax.ppermute(block, axis, route)  36 us
    ppermute x8, starting transfers between devices, passed_along(): return lax.ppermute(block, axis, route)  24.2 us
    ppermute x8, waiting for transfers between devices, exchange(): return lax.ppermute(block, axis, [(i, i ^ bit) for i in range(count)])  16.3 us
    ppermute x8, starting transfers between devices, exchange(): return lax.ppermute(block, axis, [(i, i ^ bit) for i in range(count)])  11 us
    dot_general x6, matrix products, contract(): lax.dot_general(lhs, rhs, (((lhs_dim,), (rhs_dim,)), ((), ())), preferred...  7.13 us
    ppermute x1, starting transfers between devices, padded(): lax.ppermute(tail, axis, [(i, (i + 1) % count) for i in range(ends)])  5 us
    convert_element_type x1, other arithmetic, on_device(): grad_conv = (cot_wide.astype(jnp.float32) * (sigmoid_c + conv_out * sigmo...  3.06 us
  transfers between devices with their start and end apart: 18, of which 13 were waited for; matrix products, arithmetic and copies ran while one was open for 8% of the time, Pallas kernels for 0%

profile of v20, /device:TPU:2, one launch (start us, length us, event | category | flops | bytes accessed | tf_op | source)
XLA Modules:
  0.0 129.4 jit_solution(7682475924765134624)
XLA Ops:
  0.6 0.9 slice_bitcast_fusion.10
  1.6 0.9 constant_dynamic-update-slice_fusion.1
  2.5 1.0 constant_dynamic-update-slice_fusion
  3.6 1.9 %collective-permute-start.2 = (bf16[288,512]{1,0:T(8,128)(2,1)S(1)}, bf16[288,512]{1,0:T(8,128)(2,1)S(1)}, u32[]{:S(2)}, u32[]{:S(2)}) collective-permute-start(bf16[288,512]{1,0:T(8,128)(2,1)S(1)} %get-tuple-element.33), channel_id=1, source_target_pairs={{2,0},{4,2},{6,4},{8,6},{10,8},{12,10},{14,12},{3,1},{5,3},{7,5},{... | collective-permute-start | bytes 884744 | tf_op jit(solution)/shard_map/ppermute | solution.py:17
  5.5 4.8 %collective-permute-start = (bf16[288,512]{1,0:T(8,128)(2,1)S(1)}, bf16[288,512]{1,0:T(8,128)(2,1)S(1)}, u32[]{:S(2)}, u32[]{:S(2)}) collective-permute-start(bf16[288,512]{1,0:T(8,128)(2,1)S(1)} %get-tuple-element.34), channel_id=1, source_target_pairs={{0,2},{2,4},{4,6},{6,8},{8,10},{10,12},{12,14},{1,3},{3,5},{5,7},{... | collective-permute-start | bytes 884744 | tf_op jit(solution)/shard_map/ppermute | solution.py:17
  11.0 4.2 %collective-permute-done.2 = bf16[288,512]{1,0:T(8,128)(2,1)S(1)} collective-permute-done((bf16[288,512]{1,0:T(8,128)(2,1)S(1)}, bf16[288,512]{1,0:T(8,128)(2,1)S(1)}, u32[]{:S(2)}, u32[]{:S(2)}) %collective-permute-start.2) | collective-permute-done | bytes 294944 | tf_op jit(solution)/shard_map/ppermute | solution.py:17
  15.2 6.2 %collective-permute-done = bf16[288,512]{1,0:T(8,128)(2,1)S(1)} collective-permute-done((bf16[288,512]{1,0:T(8,128)(2,1)S(1)}, bf16[288,512]{1,0:T(8,128)(2,1)S(1)}, u32[]{:S(2)}, u32[]{:S(2)}) %collective-permute-start) | collective-permute-done | bytes 294944 | tf_op jit(solution)/shard_map/ppermute | solution.py:17
  21.6 3.5 %collective-permute-start.1 = (bf16[2,2,128,512]{3,2,1,0:T(8,128)(2,1)S(1)}, bf16[2,2,128,512]{3,2,1,0:T(8,128)(2,1)S(1)}, u32[]{:S(2)}, u32[]{:S(2)}) collective-permute-start(bf16[2,2,128,512]{3,2,1,0:T(8,128)(2,1)S(1)} %get-tuple-element.32), channel_id=1, source_target_pairs={{0,4},{2,6},{4,8},{6,10},{8,12},{10,14},{1,5},{3,7},{5,9},{7,11},{... | collective-permute-start | bytes 1572872 | tf_op jit(solution)/shard_map/ppermute | solution.py:17
  25.3 1.3 collective-permute-start.3
  26.6 9.8 %collective-permute-done.1 = bf16[2,2,128,512]{3,2,1,0:T(8,128)(2,1)S(1)} collective-permute-done((bf16[2,2,128,512]{3,2,1,0:T(8,128)(2,1)S(1)}, bf16[2,2,128,512]{3,2,1,0:T(8,128)(2,1)S(1)}, u32[]{:S(2)}, u32[]{:S(2)}) %collective-permute-start.1) | collective-permute-done | bytes 524320 | tf_op jit(solution)/shard_map/ppermute | solution.py:17
  36.5 4.2 %collective-permute-done.3 = bf16[2,2,128,512]{3,2,1,0:T(8,128)(2,1)S(1)} collective-permute-done((bf16[2,2,128,512]{3,2,1,0:T(8,128)(2,1)S(1)}, bf16[2,2,128,512]{3,2,1,0:T(8,128)(2,1)S(1)}, u32[]{:S(2)}, u32[]{:S(2)}) %collective-permute-start.3) | collective-permute-done | bytes 524320 | tf_op jit(solution)/shard_map/ppermute | solution.py:17
  40.8 1.2 fusion
  42.0 0.8 exponential_reduce_fusion
  42.8 0.7 exponential_convert_fusion
  43.6 1.3 fusion.48
  45.5 1.9 %collective-permute-start.5 = (bf16[32,1024]{1,0:T(8,128)(2,1)S(1)}, bf16[32,1024]{1,0:T(8,128)(2,1)S(1)}, u32[]{:S(2)}, u32[]{:S(2)}) collective-permute-start(bf16[32,1024]{1,0:T(8,128)(2,1)S(1)} %get-tuple-element.30), channel_id=1, source_target_pairs={{2,0},{4,2},{6,4},{8,6},{10,8},{12,10},{14,12},{3,1},{5,3},{7,5},{... | collective-permute-start | bytes 196616 | tf_op jit(solution)/shard_map/ppermute | solution.py:30
  47.4 5.0 %collective-permute-start.4 = (bf16[32,1024]{1,0:T(8,128)(2,1)S(1)}, bf16[32,1024]{1,0:T(8,128)(2,1)S(1)}, u32[]{:S(2)}, u32[]{:S(2)}) collective-permute-start(bf16[32,1024]{1,0:T(8,128)(2,1)S(1)} %get-tuple-element.29), channel_id=1, source_target_pairs={{0,2},{2,4},{4,6},{6,8},{8,10},{10,12},{12,14},{1,3},{3,5},{5,7},{... | collective-permute-start | bytes 196616 | tf_op jit(solution)/shard_map/ppermute | solution.py:28
  52.6 1.6 %collective-permute-done.4 = bf16[32,1024]{1,0:T(8,128)(2,1)S(1)} collective-permute-done((bf16[32,1024]{1,0:T(8,128)(2,1)S(1)}, bf16[32,1024]{1,0:T(8,128)(2,1)S(1)}, u32[]{:S(2)}, u32[]{:S(2)}) %collective-permute-start.4) | collective-permute-done | bytes 65568 | tf_op jit(solution)/shard_map/ppermute | solution.py:28
  54.3 3.1 %multiply_convert_fusion.1 = bf16[158,1024]{1,0:T(8,128)(2,1)S(1)} fusion(bf16[32,1024]{1,0:T(8,128)(2,1)S(1)} %collective-permute-done.5, bf16[128,1024]{1,0:T(8,128)(2,1)S(1)} %fusion.5, bf16[192,1024]{1,0:T(8,128)(2,1)S(1)} %pad_maximum_fusion.5, bf16[32,1024]{1,0:T(8,128)(2,1)S(1)} %collective-permute-done.4, bf16[15,1024]{1,0:T(8,128)(2,1)S(1)} %slice.489, ...), kind=kLoop, calls=%fused_computation.31 | loop fusion | flops 18282496 | bytes 10551296 | tf_op jit(solution)/shard_map/convert_element_type | solution.py:176
  57.3 2.2 %add_convert_fusion = bf16[128,1024]{1,0:T(8,128)(2,1)S(1)} fusion(bf16[158,1024]{1,0:T(8,128)(2,1)S(1)} %multiply_convert_fusion.1, f32[1024]{0:T(1024)S(1)} %bitcast.239, f32[1024]{0:T(1024)S(1)} %bitcast.241, f32[1024]{0:T(1024)S(1)} %bitcast.183, f32[1024]{0:T(1024)S(1)} %bitcast.185, f32[1024]{0:T(1024)S(1)} %bitcast.187, f32[1024]{0:T(1024)S(1)} %bitcast.189, ...), kind=kLoop, calls=%fused_computation.54 | loop fusion | flops 12582912 | bytes 8777856 | tf_op jit(solution)/shard_map/convert_element_type | solution.py:194
  60.1 2.4 %fusion.7 = f32[1,31,1024]{2,0,1:T(1,128)S(1)} fusion(bf16[1,158,1024]{2,1,0:T(8,128)(2,1)S(1)} %slice_bitcast_fusion, bf16[128,1,1024]{2,0,1:T(8,128)(2,1)S(1)} %slice_bitcast_fusion.1), kind=kOutput, calls=%fused_computation.34 | convolution fusion | flops 8126464 | bytes 712704 | tf_op jit(solution)/shard_map/conv_general_dilated | solution.py:183
  62.6 0.8 copy-done.1
  63.4 0.9 fusion.2
  64.3 1.2 convert_multiply_fusion
  65.6 1.1 copy.19
  66.8 1.3 %fusion.4 = f32[1,8,40,1024]{3,2,1,0:T(8,128)S(1)} fusion(s32[]{:T(128)S(6)} %select_n.165, f32[2,8,32,1024]{3,2,1,0:T(8,128)S(1)} %bitcast.156, f32[2,8,8,1024]{3,2,1,0:T(8,128)} %bitcast.162, bf16[1,8,40,1024]{3,2,1,0:T(8,128)(2,1)} %collective-permute-done.10), kind=kLoop, calls=%fused_computation.19 | loop fusion | flops 983040 | bytes 4587524 | tf_op jit(solution)/shard_map/add | solution.py:78
  68.4 9.9 %collective-permute-done.11 = bf16[4,40,1024]{2,1,0:T(8,128)(2,1)S(1)} collective-permute-done((bf16[4,40,1024]{2,1,0:T(8,128)(2,1)S(1)}, bf16[4,40,1024]{2,1,0:T(8,128)(2,1)S(1)}, u32[]{:S(2)}, u32[]{:S(2)}) %collective-permute-start.11) | collective-permute-done | bytes 327712 | tf_op jit(solution)/shard_map/ppermute | solution.py:66
  78.4 2.1 %collective-permute-start.12 = (bf16[2,40,1024]{2,1,0:T(8,128)(2,1)S(1)}, bf16[2,40,1024]{2,1,0:T(8,128)(2,1)S(1)}, u32[]{:S(2)}, u32[]{:S(2)}) collective-permute-start(bf16[2,40,1024]{2,1,0:T(8,128)(2,1)S(1)} %dynamic-slice_convert_fusion.1), channel_id=1, source_target_pairs={{0,4},{2,6},{4,0},{6,2},{8,12},{10,14},{12,8},{14,10},{1,5},{3,7},... | collective-permute-start | bytes 491528 | tf_op jit(solution)/shard_map/ppermute | solution.py:66
  80.6 1.1 multiply_convert_fusion
  81.7 3.1 %collective-permute-done.12 = bf16[2,40,1024]{2,1,0:T(8,128)(2,1)S(1)} collective-permute-done((bf16[2,40,1024]{2,1,0:T(8,128)(2,1)S(1)}, bf16[2,40,1024]{2,1,0:T(8,128)(2,1)S(1)}, u32[]{:S(2)}, u32[]{:S(2)}) %collective-permute-start.12) | collective-permute-done | bytes 163872 | tf_op jit(solution)/shard_map/ppermute | solution.py:66
  84.9 2.8 %collective-permute-start.13 = (bf16[1,40,1024]{2,1,0:T(8,128)(2,1)S(1)}, bf16[1,40,1024]{2,1,0:T(8,128)(2,1)S(1)}, u32[]{:S(2)}, u32[]{:S(2)}) collective-permute-start(bf16[1,40,1024]{2,1,0:T(8,128)(2,1)S(1)} %dynamic-slice_convert_fusion.2), channel_id=1, source_target_pairs={{0,8},{2,10},{4,12},{6,14},{8,0},{10,2},{12,4},{14,6},{1,9},{3,11}... | collective-permute-start | bytes 245768 | tf_op jit(solution)/shard_map/ppermute | solution.py:66
  87.7 1.1 fusion.46
  88.8 1.6 %collective-permute-done.13 = bf16[1,40,1024]{2,1,0:T(8,128)(2,1)S(1)} collective-permute-done((bf16[1,40,1024]{2,1,0:T(8,128)(2,1)S(1)}, bf16[1,40,1024]{2,1,0:T(8,128)(2,1)S(1)}, u32[]{:S(2)}, u32[]{:S(2)}) %collective-permute-start.13) | collective-permute-done | bytes 81952 | tf_op jit(solution)/shard_map/ppermute | solution.py:66
  90.4 2.7 %collective-permute-start.14 = (bf16[1,40,1024]{2,1,0:T(8,128)(2,1)S(1)}, bf16[1,40,1024]{2,1,0:T(8,128)(2,1)S(1)}, u32[]{:S(2)}, u32[]{:S(2)}) collective-permute-start(bf16[1,40,1024]{2,1,0:T(8,128)(2,1)S(1)} %add_convert_fusion.1), channel_id=1, source_target_pairs={{0,8},{2,10},{4,12},{6,14},{8,0},{10,2},{12,4},{14,6},{1,9},{3,11}... | collective-permute-start | bytes 245768 | tf_op jit(solution)/shard_map/ppermute | solution.py:66
  93.1 1.1 fusion.47
  94.2 1.6 %collective-permute-done.14 = bf16[1,40,1024]{2,1,0:T(8,128)(2,1)S(1)} collective-permute-done((bf16[1,40,1024]{2,1,0:T(8,128)(2,1)S(1)}, bf16[1,40,1024]{2,1,0:T(8,128)(2,1)S(1)}, u32[]{:S(2)}, u32[]{:S(2)}) %collective-permute-start.14) | collective-permute-done | bytes 81952 | tf_op jit(solution)/shard_map/ppermute | solution.py:66
  95.9 1.7 %collective-permute-start.15 = (bf16[2,40,1024]{2,1,0:T(8,128)(2,1)S(1)}, bf16[2,40,1024]{2,1,0:T(8,128)(2,1)S(1)}, u32[]{:S(2)}, u32[]{:S(2)}) collective-permute-start(bf16[2,40,1024]{2,1,0:T(8,128)(2,1)S(1)} %pad_maximum_fusion.12), channel_id=1, source_target_pairs={{0,4},{2,6},{4,0},{6,2},{8,12},{10,14},{12,8},{14,10},{1,5},{3,7},... | collective-permute-start | bytes 491528 | tf_op jit(solution)/shard_map/ppermute | solution.py:66
  97.6 1.3 %fusion.49 = f32[1024,512]{1,0:T(8,128)S(1)} fusion(bf16[1024,896]{0,1:T(8,128)(2,1)S(1)} %multiply_convert_fusion, bf16[896,512]{1,0:T(8,128)(2,1)S(1)} %copy-done.15), kind=kOutput, calls=%fused_computation.134 | convolution fusion | flops 939524096 | bytes 4849664 | tf_op jit(solution)/shard_map/dot_general | solution.py:151
  99.0 1.3 collective-permute-start.7
  100.3 4.6 %collective-permute-start.6 = (bf16[2,2,128,512]{3,2,1,0:T(8,128)(2,1)S(1)}, bf16[2,2,128,512]{3,2,1,0:T(8,128)(2,1)S(1)}, u32[]{:S(2)}, u32[]{:S(2)}) collective-permute-start(bf16[2,2,128,512]{3,2,1,0:T(8,128)(2,1)S(1)} %get-tuple-element.5), channel_id=1, source_target_pairs={{0,4},{2,6},{4,8},{6,10},{8,12},{10,14},{1,5},{3,7},{5,9},{7,11},{... | collective-permute-start | bytes 1572872 | tf_op jit(solution)/shard_map/ppermute | solution.py:17
  104.9 1.5 %collective-permute-start.16 = (bf16[4,40,1024]{2,1,0:T(8,128)(2,1)S(1)}, bf16[4,40,1024]{2,1,0:T(8,128)(2,1)S(1)}, u32[]{:S(2)}, u32[]{:S(2)}) collective-permute-start(bf16[4,40,1024]{2,1,0:T(8,128)(2,1)S(1)} %pad_maximum_fusion.8), channel_id=1, source_target_pairs={{0,2},{2,0},{4,6},{6,4},{8,10},{10,8},{12,14},{14,12},{1,3},{3,1},... | collective-permute-start | bytes 983048 | tf_op jit(solution)/shard_map/ppermute | solution.py:66
  106.9 5.6 %collective-permute-done.7 = bf16[2,2,128,512]{3,2,1,0:T(8,128)(2,1)S(1)} collective-permute-done((bf16[2,2,128,512]{3,2,1,0:T(8,128)(2,1)S(1)}, bf16[2,2,128,512]{3,2,1,0:T(8,128)(2,1)S(1)}, u32[]{:S(2)}, u32[]{:S(2)}) %collective-permute-start.7) | collective-permute-done | bytes 524320 | tf_op jit(solution)/shard_map/ppermute | solution.py:17
  113.0 3.5 %collective-permute-start.9 = (bf16[2,128,512]{2,1,0:T(8,128)(2,1)S(1)}, bf16[2,128,512]{2,1,0:T(8,128)(2,1)S(1)}, u32[]{:S(2)}, u32[]{:S(2)}) collective-permute-start(bf16[2,128,512]{2,1,0:T(8,128)(2,1)S(1)} %get-tuple-element.8), channel_id=1, source_target_pairs={{2,0},{4,2},{6,4},{8,6},{10,8},{12,10},{14,12},{3,1},{5,3},{7,5},{... | collective-permute-start | bytes 786440 | tf_op jit(solution)/shard_map/ppermute | solution.py:17
  116.5 3.3 %collective-permute-start.8 = (bf16[2,128,512]{2,1,0:T(8,128)(2,1)S(1)}, bf16[2,128,512]{2,1,0:T(8,128)(2,1)S(1)}, u32[]{:S(2)}, u32[]{:S(2)}) collective-permute-start(bf16[2,128,512]{2,1,0:T(8,128)(2,1)S(1)} %get-tuple-element.7), channel_id=1, source_target_pairs={{0,2},{2,4},{4,6},{6,8},{8,10},{10,12},{12,14},{1,3},{3,5},{5,7},{... | collective-permute-start | bytes 786440 | tf_op jit(solution)/shard_map/ppermute | solution.py:17
  120.7 1.6 %collective-permute-done.9 = bf16[2,128,512]{2,1,0:T(8,128)(2,1)S(1)} collective-permute-done((bf16[2,128,512]{2,1,0:T(8,128)(2,1)S(1)}, bf16[2,128,512]{2,1,0:T(8,128)(2,1)S(1)}, u32[]{:S(2)}, u32[]{:S(2)}) %collective-permute-start.9) | collective-permute-done | bytes 262176 | tf_op jit(solution)/shard_map/ppermute | solution.py:17
  122.3 4.3 %collective-permute-done.8 = bf16[2,128,512]{2,1,0:T(8,128)(2,1)S(1)} collective-permute-done((bf16[2,128,512]{2,1,0:T(8,128)(2,1)S(1)}, bf16[2,128,512]{2,1,0:T(8,128)(2,1)S(1)}, u32[]{:S(2)}, u32[]{:S(2)}) %collective-permute-start.8) | collective-permute-done | bytes 262176 | tf_op jit(solution)/shard_map/ppermute | solution.py:17
  126.9 0.7 fusion.42
  127.7 1.1 fusion.6
  (102 shorter events, 5.4 us)
Async XLA Ops:
  0.6 44.5 %copy-start = (bf16[512,1024]{1,0:T(8,128)(2,1)S(1)}, bf16[512,1024]{1,0:T(8,128)(2,1)}, u32[]{:S(2)}) copy-start(bf16[512,1024]{1,0:T(8,128)(2,1)} %param.11) | copy-start | bytes 3145732
  2.5 22.6 %copy-start.11 = (f32[31,1024]{1,0:T(8,128)S(1)}, f32[31,1024]{1,0:T(8,128)}, u32[]{:S(2)}) copy-start(f32[31,1024]{1,0:T(8,128)} %param.12) | copy-start | bytes 380932
  2.5 22.6 %copy-start.10 = (bf16[1,128,512]{2,1,0:T(8,128)(2,1)S(1)}, bf16[1,128,512]{2,1,0:T(8,128)(2,1)}, u32[]{:S(2)}) copy-start(bf16[1,128,512]{2,1,0:T(8,128)(2,1)} %param.7) | copy-start | bytes 393220
  3.6 11.6 %collective-permute-start.2 = (bf16[288,512]{1,0:T(8,128)(2,1)S(1)}, bf16[288,512]{1,0:T(8,128)(2,1)S(1)}, u32[]{:S(2)}, u32[]{:S(2)}) collective-permute-start(bf16[288,512]{1,0:T(8,128)(2,1)S(1)} %get-tuple-element.33), channel_id=1, source_target_pairs={{2,0},{4,2},{6,4},{8,6},{10,8},{12,10},{14,12},{3,1},{5,3},{7,5},{... | collective-permute-start | bytes 884744 | tf_op jit(solution)/shard_map/ppermute | solution.py:17
  5.5 15.9 %collective-permute-start = (bf16[288,512]{1,0:T(8,128)(2,1)S(1)}, bf16[288,512]{1,0:T(8,128)(2,1)S(1)}, u32[]{:S(2)}, u32[]{:S(2)}) collective-permute-start(bf16[288,512]{1,0:T(8,128)(2,1)S(1)} %get-tuple-element.34), channel_id=1, source_target_pairs={{0,2},{2,4},{4,6},{6,8},{8,10},{10,12},{12,14},{1,3},{3,5},{5,7},{... | collective-permute-start | bytes 884744 | tf_op jit(solution)/shard_map/ppermute | solution.py:17
  21.4 15.0 %copy-start.8 = (bf16[1,128,512]{2,1,0:T(8,128)(2,1)S(1)}, bf16[1,128,512]{2,1,0:T(8,128)(2,1)}, u32[]{:S(2)}) copy-start(bf16[1,128,512]{2,1,0:T(8,128)(2,1)} %param.8) | copy-start | bytes 393220
  21.5 15.0 %copy-start.9 = (bf16[1,128,512]{2,1,0:T(8,128)(2,1)S(1)}, bf16[1,128,512]{2,1,0:T(8,128)(2,1)}, u32[]{:S(2)}) copy-start(bf16[1,128,512]{2,1,0:T(8,128)(2,1)} %param.9) | copy-start | bytes 393220
  21.6 14.8 %collective-permute-start.1 = (bf16[2,2,128,512]{3,2,1,0:T(8,128)(2,1)S(1)}, bf16[2,2,128,512]{3,2,1,0:T(8,128)(2,1)S(1)}, u32[]{:S(2)}, u32[]{:S(2)}) collective-permute-start(bf16[2,2,128,512]{3,2,1,0:T(8,128)(2,1)S(1)} %get-tuple-element.32), channel_id=1, source_target_pairs={{0,4},{2,6},{4,8},{6,10},{8,12},{10,14},{1,5},{3,7},{5,9},{7,11},{... | collective-permute-start | bytes 1572872 | tf_op jit(solution)/shard_map/ppermute | solution.py:17
  25.3 16.7 %copy-start.5 = (bf16[8,128,512]{2,1,0:T(8,128)(2,1)}, bf16[8,128,512]{2,1,0:T(8,128)(2,1)S(1)}, u32[]{:S(2)}) copy-start(bf16[8,128,512]{2,1,0:T(8,128)(2,1)S(1)} %broadcast_select_fusion.1) | copy-start | bytes 3145732
  25.3 15.5 %collective-permute-start.3 = (bf16[2,2,128,512]{3,2,1,0:T(8,128)(2,1)S(1)}, bf16[2,2,128,512]{3,2,1,0:T(8,128)(2,1)S(1)}, u32[]{:S(2)}, u32[]{:S(2)}) collective-permute-start(bf16[2,2,128,512]{3,2,1,0:T(8,128)(2,1)S(1)} %get-tuple-element.31), channel_id=1, source_target_pairs={{4,0},{6,2},{8,4},{10,6},{12,8},{14,10},{5,1},{7,3},{9,5},{11,7},{... | collective-permute-start | bytes 1572872 | tf_op jit(solution)/shard_map/ppermute | solution.py:17
  40.8 1.2 copy-start.14
  40.8 2.8 %copy-start.12 = (bf16[896,512]{1,0:T(8,128)(2,1)}, bf16[896,512]{1,0:T(8,128)(2,1)S(1)}, u32[]{:S(2)}) copy-start(bf16[896,512]{1,0:T(8,128)(2,1)S(1)} %get-tuple-element.13) | copy-start | bytes 2752516
  43.6 1.3 %copy-start.2 = (bf16[1024,896]{0,1:T(8,128)(2,1)}, bf16[1024,896]{0,1:T(8,128)(2,1)S(1)}, u32[]{:S(2)}) copy-start(bf16[1024,896]{0,1:T(8,128)(2,1)S(1)} %exponential_convert_fusion) | copy-start | bytes 5505028
  45.2 9.1 %copy-start.4 = (bf16[1,128,1024]{2,1,0:T(8,128)(2,1)S(1)}, bf16[1,128,1024]{2,1,0:T(8,128)(2,1)}, u32[]{:S(2)}) copy-start(bf16[1,128,1024]{2,1,0:T(8,128)(2,1)} %param.10) | copy-start | bytes 786436
  45.5 7.1 %collective-permute-start.5 = (bf16[32,1024]{1,0:T(8,128)(2,1)S(1)}, bf16[32,1024]{1,0:T(8,128)(2,1)S(1)}, u32[]{:S(2)}, u32[]{:S(2)}) collective-permute-start(bf16[32,1024]{1,0:T(8,128)(2,1)S(1)} %get-tuple-element.30), channel_id=1, source_target_pairs={{2,0},{4,2},{6,4},{8,6},{10,8},{12,10},{14,12},{3,1},{5,3},{7,5},{... | collective-permute-start | bytes 196616 | tf_op jit(solution)/shard_map/ppermute | solution.py:30
  47.4 6.7 %collective-permute-start.4 = (bf16[32,1024]{1,0:T(8,128)(2,1)S(1)}, bf16[32,1024]{1,0:T(8,128)(2,1)S(1)}, u32[]{:S(2)}, u32[]{:S(2)}) collective-permute-start(bf16[32,1024]{1,0:T(8,128)(2,1)S(1)} %get-tuple-element.29), channel_id=1, source_target_pairs={{0,2},{2,4},{4,6},{6,8},{8,10},{10,12},{12,14},{1,3},{3,5},{5,7},{... | collective-permute-start | bytes 196616 | tf_op jit(solution)/shard_map/ppermute | solution.py:28
  62.6 0.8 copy-start.1
  64.3 2.4 %collective-permute-start.10 = (bf16[1,8,40,1024]{3,2,1,0:T(8,128)(2,1)}, bf16[1,8,40,1024]{3,2,1,0:T(8,128)(2,1)}, u32[]{:S(2)}, u32[]{:S(2)}) collective-permute-start(bf16[1,8,40,1024]{3,2,1,0:T(8,128)(2,1)} %fusion.2), channel_id=1, source_target_pairs={{0,1},{1,0},{2,3},{3,2},{4,5},{5,4},{6,7},{7,6},{8,9},{9,8},{10,11... | collective-permute-start | bytes 1966088 | tf_op jit(solution)/shard_map/ppermute | solution.py:66
  66.6 1.7 %copy-start.7 = (bf16[128,512]{1,0:T(8,128)(2,1)S(1)}, bf16[128,512]{1,0:T(8,128)(2,1)}, u32[]{:S(2)}) copy-start(bf16[128,512]{1,0:T(8,128)(2,1)} %get-tuple-element.73) | copy-start | bytes 393220
  68.1 12.5 %copy-start.3 = (bf16[1024,896]{0,1:T(8,128)(2,1)S(1)}, bf16[1024,896]{0,1:T(8,128)(2,1)}, u32[]{:S(2)}) copy-start(bf16[1024,896]{0,1:T(8,128)(2,1)} %copy-done.2) | copy-start | bytes 5505028
  68.1 12.5 %copy-start.13 = (bf16[896,512]{1,0:T(8,128)(2,1)S(1)}, bf16[896,512]{1,0:T(8,128)(2,1)}, u32[]{:S(2)}) copy-start(bf16[896,512]{1,0:T(8,128)(2,1)} %copy-done.12) | copy-start | bytes 2752516
  68.2 10.1 %collective-permute-start.11 = (bf16[4,40,1024]{2,1,0:T(8,128)(2,1)S(1)}, bf16[4,40,1024]{2,1,0:T(8,128)(2,1)S(1)}, u32[]{:S(2)}, u32[]{:S(2)}) collective-permute-start(bf16[4,40,1024]{2,1,0:T(8,128)(2,1)S(1)} %fusion.21), channel_id=1, source_target_pairs={{0,2},{2,0},{4,6},{6,4},{8,10},{10,8},{12,14},{14,12},{1,3},{3,1},... | collective-permute-start | bytes 983048 | tf_op jit(solution)/shard_map/ppermute | solution.py:66
  78.4 6.4 %collective-permute-start.12 = (bf16[2,40,1024]{2,1,0:T(8,128)(2,1)S(1)}, bf16[2,40,1024]{2,1,0:T(8,128)(2,1)S(1)}, u32[]{:S(2)}, u32[]{:S(2)}) collective-permute-start(bf16[2,40,1024]{2,1,0:T(8,128)(2,1)S(1)} %dynamic-slice_convert_fusion.1), channel_id=1, source_target_pairs={{0,4},{2,6},{4,0},{6,2},{8,12},{10,14},{12,8},{14,10},{1,5},{3,7},... | collective-permute-start | bytes 491528 | tf_op jit(solution)/shard_map/ppermute | solution.py:66
  84.9 8.2 %copy-start.6 = (bf16[8,128,512]{2,1,0:T(8,128)(2,1)S(1)}, bf16[8,128,512]{2,1,0:T(8,128)(2,1)}, u32[]{:S(2)}) copy-start(bf16[8,128,512]{2,1,0:T(8,128)(2,1)} %copy-done.5) | copy-start | bytes 3145732
  84.9 5.5 %collective-permute-start.13 = (bf16[1,40,1024]{2,1,0:T(8,128)(2,1)S(1)}, bf16[1,40,1024]{2,1,0:T(8,128)(2,1)S(1)}, u32[]{:S(2)}, u32[]{:S(2)}) collective-permute-start(bf16[1,40,1024]{2,1,0:T(8,128)(2,1)S(1)} %dynamic-slice_convert_fusion.2), channel_id=1, source_target_pairs={{0,8},{2,10},{4,12},{6,14},{8,0},{10,2},{12,4},{14,6},{1,9},{3,11}... | collective-permute-start | bytes 245768 | tf_op jit(solution)/shard_map/ppermute | solution.py:66
  90.4 7.2 %copy-start.15 = (bf16[896,512]{1,0:T(8,128)(2,1)S(1)}, bf16[896,512]{1,0:T(8,128)(2,1)}, u32[]{:S(2)}) copy-start(bf16[896,512]{1,0:T(8,128)(2,1)} %copy-done.14) | copy-start | bytes 2752516
  90.4 5.4 %collective-permute-start.14 = (bf16[1,40,1024]{2,1,0:T(8,128)(2,1)S(1)}, bf16[1,40,1024]{2,1,0:T(8,128)(2,1)S(1)}, u32[]{:S(2)}, u32[]{:S(2)}) collective-permute-start(bf16[1,40,1024]{2,1,0:T(8,128)(2,1)S(1)} %add_convert_fusion.1), channel_id=1, source_target_pairs={{0,8},{2,10},{4,12},{6,14},{8,0},{10,2},{12,4},{14,6},{1,9},{3,11}... | collective-permute-start | bytes 245768 | tf_op jit(solution)/shard_map/ppermute | solution.py:66
  95.9 9.0 %collective-permute-start.15 = (bf16[2,40,1024]{2,1,0:T(8,128)(2,1)S(1)}, bf16[2,40,1024]{2,1,0:T(8,128)(2,1)S(1)}, u32[]{:S(2)}, u32[]{:S(2)}) collective-permute-start(bf16[2,40,1024]{2,1,0:T(8,128)(2,1)S(1)} %pad_maximum_fusion.12), channel_id=1, source_target_pairs={{0,4},{2,6},{4,0},{6,2},{8,12},{10,14},{12,8},{14,10},{1,5},{3,7},... | collective-permute-start | bytes 491528 | tf_op jit(solution)/shard_map/ppermute | solution.py:66
  99.0 13.5 %collective-permute-start.7 = (bf16[2,2,128,512]{3,2,1,0:T(8,128)(2,1)S(1)}, bf16[2,2,128,512]{3,2,1,0:T(8,128)(2,1)S(1)}, u32[]{:S(2)}, u32[]{:S(2)}) collective-permute-start(bf16[2,2,128,512]{3,2,1,0:T(8,128)(2,1)S(1)} %get-tuple-element.6), channel_id=1, source_target_pairs={{4,0},{6,2},{8,4},{10,6},{12,8},{14,10},{5,1},{7,3},{9,5},{11,7},{... | collective-permute-start | bytes 1572872 | tf_op jit(solution)/shard_map/ppermute | solution.py:17
  100.3 12.4 %collective-permute-start.6 = (bf16[2,2,128,512]{3,2,1,0:T(8,128)(2,1)S(1)}, bf16[2,2,128,512]{3,2,1,0:T(8,128)(2,1)S(1)}, u32[]{:S(2)}, u32[]{:S(2)}) collective-permute-start(bf16[2,2,128,512]{3,2,1,0:T(8,128)(2,1)S(1)} %get-tuple-element.5), channel_id=1, source_target_pairs={{0,4},{2,6},{4,8},{6,10},{8,12},{10,14},{1,5},{3,7},{5,9},{7,11},{... | collective-permute-start | bytes 1572872 | tf_op jit(solution)/shard_map/ppermute | solution.py:17
  104.9 14.9 %collective-permute-start.16 = (bf16[4,40,1024]{2,1,0:T(8,128)(2,1)S(1)}, bf16[4,40,1024]{2,1,0:T(8,128)(2,1)S(1)}, u32[]{:S(2)}, u32[]{:S(2)}) collective-permute-start(bf16[4,40,1024]{2,1,0:T(8,128)(2,1)S(1)} %pad_maximum_fusion.8), channel_id=1, source_target_pairs={{0,2},{2,0},{4,6},{6,4},{8,10},{10,8},{12,14},{14,12},{1,3},{3,1},... | collective-permute-start | bytes 983048 | tf_op jit(solution)/shard_map/ppermute | solution.py:66
  113.0 9.3 %collective-permute-start.9 = (bf16[2,128,512]{2,1,0:T(8,128)(2,1)S(1)}, bf16[2,128,512]{2,1,0:T(8,128)(2,1)S(1)}, u32[]{:S(2)}, u32[]{:S(2)}) collective-permute-start(bf16[2,128,512]{2,1,0:T(8,128)(2,1)S(1)} %get-tuple-element.8), channel_id=1, source_target_pairs={{2,0},{4,2},{6,4},{8,6},{10,8},{12,10},{14,12},{3,1},{5,3},{7,5},{... | collective-permute-start | bytes 786440 | tf_op jit(solution)/shard_map/ppermute | solution.py:17
  116.5 10.1 %collective-permute-start.8 = (bf16[2,128,512]{2,1,0:T(8,128)(2,1)S(1)}, bf16[2,128,512]{2,1,0:T(8,128)(2,1)S(1)}, u32[]{:S(2)}, u32[]{:S(2)}) collective-permute-start(bf16[2,128,512]{2,1,0:T(8,128)(2,1)S(1)} %get-tuple-element.7), channel_id=1, source_target_pairs={{0,2},{2,4},{4,6},{6,8},{8,10},{10,12},{12,14},{1,3},{3,5},{5,7},{... | collective-permute-start | bytes 786440 | tf_op jit(solution)/shard_map/ppermute | solution.py:17
  119.9 7.6 %collective-permute-start.17 = (bf16[1,8,40,1024]{3,2,1,0:T(8,128)(2,1)S(1)}, bf16[1,8,40,1024]{3,2,1,0:T(8,128)(2,1)S(1)}, u32[]{:S(2)}, u32[]{:S(2)}) collective-permute-start(bf16[1,8,40,1024]{3,2,1,0:T(8,128)(2,1)S(1)} %maximum_bitcast_fusion), channel_id=1, source_target_pairs={{0,1},{1,0},{2,3},{3,2},{4,5},{5,4},{6,7},{7,6},{8,9},{9,8},{10,11... | collective-permute-start | bytes 1966088 | tf_op jit(solution)/shard_map/ppermute | solution.py:66

commit v21 on v20

--- a/solution.py
+++ b/solution.py
@@ -117,17 +117,16 @@
     halo_rows = -(-halo_width // 8) * 8
 
     def edge_rows(rows_here):
-        padded_rows = jnp.pad(rows_here, ((0, halo_rows - halo_width), (0, 0)))
-        return padded_rows.reshape(-1, width_heads)
+        return rows_here.reshape(-1, width_heads)
 
     def edge_back(packed):
-        return packed.reshape(halo_rows, channels)[:halo_width]
+        return packed.reshape(halo_rows, channels)
 
     gathered, cot_low, cot_high = collect(
         jnp.stack([key_here, value_here], axis=0),
         kv_shift,
-        edge_rows(cot_here[tokens - halo_width :]),
-        edge_rows(cot_here[:halo_width]),
+        edge_rows(cot_here[tokens - halo_rows :]),
+        edge_rows(cot_here[:halo_rows]),
     )
     cot_wide = jnp.concatenate([edge_back(cot_low), cot_here, edge_back(cot_high)], axis=0)
     kv_rows = span_blocks * tokens
@@ -163,9 +162,9 @@
     hidden = jnp.dot(attended, out_proj, preferred_element_type=jnp.float32)
     masked = jnp.where(valid_rows[:, None], hidden, 0.0).astype(jnp.bfloat16)
 
-    wide_rows = tokens + 2 * halo_width
+    wide_rows = tokens + 2 * halo_rows
     edge = -(-2 * halo_width // 8) * 8
-    lead = edge - 2 * halo_width
+    lead = edge - halo_rows - halo_width
     padded_m = padded(masked, (("ctx", 0),), edge)
     conv_out = jnp.zeros((wide_rows, channels), jnp.float32)
     for tap_index in range(KW):
@@ -176,13 +175,13 @@
     ).astype(jnp.bfloat16)
     grad_masked = jnp.zeros((tokens, channels), jnp.float32)
     for tap_index in range(KW):
-        start_row = 2 * halo_width - tap_index
+        start_row = halo_rows + halo_width - tap_index
         grad_masked = (
             grad_masked + conv_kernel[tap_index] * grad_conv[start_row : start_row + tokens]
         )
     kernel_local = lax.conv_general_dilated(
-        padded_m[None, lead + halo_width : lead + halo_width + wide_rows],
-        grad_conv[halo_width : halo_width + tokens, None, :],
+        padded_m[None, edge - halo_width : edge + tokens + halo_width],
+        grad_conv[halo_rows : halo_rows + tokens, None, :],
         window_strides=(1,),
         padding="VALID",
         dimension_numbers=("NWC", "WIO", "NWC"),

time: 130 us -> 130 us (level)
  no operation moved by 1% of the time
where the time goes in v21:
time: 130 us; the launch traced here: 129 us
  waiting for transfers between devices  53.8 us (41%)
  starting transfers between devices  42.1 us (32%)
  other arithmetic  13.7 us (11%)
  matrix products  11.5 us (9%)
  local copies, waits for them, and re-layouts  6.13 us (5%)
  between operations  2.13 us (2%)
    ppermute x8, waiting for transfers between devices, passed_along(): return lax.ppermute(block, axis, route)  36 us
    ppermute x8, starting transfers between devices, passed_along(): return lax.ppermute(block, axis, route)  24.2 us
    ppermute x8, waiting for transfers between devices, exchange(): return lax.ppermute(block, axis, [(i, i ^ bit) for i in range(count)])  16.3 us
    ppermute x8, starting transfers between devices, exchange(): return lax.ppermute(block, axis, [(i, i ^ bit) for i in range(count)])  11 us
    dot_general x6, matrix products, contract(): lax.dot_general(lhs, rhs, (((lhs_dim,), (rhs_dim,)), ((), ())), preferred...  7.13 us
    ppermute x1, starting transfers between devices, padded(): lax.ppermute(tail, axis, [(i, (i + 1) % count) for i in range(ends)])  5 us
    convert_element_type x1, other arithmetic, on_device(): grad_conv = (cot_wide.astype(jnp.float32) * (sigmoid_c + conv_out * sigmo...  2.96 us
  transfers between devices with their start and end apart: 18, of which 13 were waited for; matrix products, arithmetic and copies ran while one was open for 8% of the time, Pallas kernels for 0%

profile of v21, /device:TPU:2, one launch (start us, length us, event | category | flops | bytes accessed | tf_op | source)
XLA Modules:
  0.0 129.3 jit_solution(4003825200428418171)
XLA Ops:
  0.6 0.9 fusion.44
  1.5 0.9 constant_dynamic-update-slice_fusion.1
  2.5 1.0 constant_dynamic-update-slice_fusion
  3.5 1.9 %collective-permute-start.2 = (bf16[288,512]{1,0:T(8,128)(2,1)S(1)}, bf16[288,512]{1,0:T(8,128)(2,1)S(1)}, u32[]{:S(2)}, u32[]{:S(2)}) collective-permute-start(bf16[288,512]{1,0:T(8,128)(2,1)S(1)} %get-tuple-element.33), channel_id=1, source_target_pairs={{2,0},{4,2},{6,4},{8,6},{10,8},{12,10},{14,12},{3,1},{5,3},{7,5},{... | collective-permute-start | bytes 884744 | tf_op jit(solution)/shard_map/ppermute | solution.py:17
  5.4 4.8 %collective-permute-start = (bf16[288,512]{1,0:T(8,128)(2,1)S(1)}, bf16[288,512]{1,0:T(8,128)(2,1)S(1)}, u32[]{:S(2)}, u32[]{:S(2)}) collective-permute-start(bf16[288,512]{1,0:T(8,128)(2,1)S(1)} %get-tuple-element.34), channel_id=1, source_target_pairs={{0,2},{2,4},{4,6},{6,8},{8,10},{10,12},{12,14},{1,3},{3,5},{5,7},{... | collective-permute-start | bytes 884744 | tf_op jit(solution)/shard_map/ppermute | solution.py:17
  11.0 4.2 %collective-permute-done.2 = bf16[288,512]{1,0:T(8,128)(2,1)S(1)} collective-permute-done((bf16[288,512]{1,0:T(8,128)(2,1)S(1)}, bf16[288,512]{1,0:T(8,128)(2,1)S(1)}, u32[]{:S(2)}, u32[]{:S(2)}) %collective-permute-start.2) | collective-permute-done | bytes 294944 | tf_op jit(solution)/shard_map/ppermute | solution.py:17
  15.2 6.2 %collective-permute-done = bf16[288,512]{1,0:T(8,128)(2,1)S(1)} collective-permute-done((bf16[288,512]{1,0:T(8,128)(2,1)S(1)}, bf16[288,512]{1,0:T(8,128)(2,1)S(1)}, u32[]{:S(2)}, u32[]{:S(2)}) %collective-permute-start) | collective-permute-done | bytes 294944 | tf_op jit(solution)/shard_map/ppermute | solution.py:17
  21.5 3.5 %collective-permute-start.1 = (bf16[2,2,128,512]{3,2,1,0:T(8,128)(2,1)S(1)}, bf16[2,2,128,512]{3,2,1,0:T(8,128)(2,1)S(1)}, u32[]{:S(2)}, u32[]{:S(2)}) collective-permute-start(bf16[2,2,128,512]{3,2,1,0:T(8,128)(2,1)S(1)} %get-tuple-element.32), channel_id=1, source_target_pairs={{0,4},{2,6},{4,8},{6,10},{8,12},{10,14},{1,5},{3,7},{5,9},{7,11},{... | collective-permute-start | bytes 1572872 | tf_op jit(solution)/shard_map/ppermute | solution.py:17
  25.2 1.3 collective-permute-start.3
  26.5 9.8 %collective-permute-done.1 = bf16[2,2,128,512]{3,2,1,0:T(8,128)(2,1)S(1)} collective-permute-done((bf16[2,2,128,512]{3,2,1,0:T(8,128)(2,1)S(1)}, bf16[2,2,128,512]{3,2,1,0:T(8,128)(2,1)S(1)}, u32[]{:S(2)}, u32[]{:S(2)}) %collective-permute-start.1) | collective-permute-done | bytes 524320 | tf_op jit(solution)/shard_map/ppermute | solution.py:17
  36.5 4.2 %collective-permute-done.3 = bf16[2,2,128,512]{3,2,1,0:T(8,128)(2,1)S(1)} collective-permute-done((bf16[2,2,128,512]{3,2,1,0:T(8,128)(2,1)S(1)}, bf16[2,2,128,512]{3,2,1,0:T(8,128)(2,1)S(1)}, u32[]{:S(2)}, u32[]{:S(2)}) %collective-permute-start.3) | collective-permute-done | bytes 524320 | tf_op jit(solution)/shard_map/ppermute | solution.py:17
  40.8 1.2 fusion
  42.0 0.8 exponential_reduce_fusion
  42.8 0.7 exponential_convert_fusion
  43.5 1.3 fusion.49
  45.5 1.9 %collective-permute-start.5 = (bf16[32,1024]{1,0:T(8,128)(2,1)S(1)}, bf16[32,1024]{1,0:T(8,128)(2,1)S(1)}, u32[]{:S(2)}, u32[]{:S(2)}) collective-permute-start(bf16[32,1024]{1,0:T(8,128)(2,1)S(1)} %get-tuple-element.30), channel_id=1, source_target_pairs={{2,0},{4,2},{6,4},{8,6},{10,8},{12,10},{14,12},{3,1},{5,3},{7,5},{... | collective-permute-start | bytes 196616 | tf_op jit(solution)/shard_map/ppermute | solution.py:30
  47.4 5.0 %collective-permute-start.4 = (bf16[32,1024]{1,0:T(8,128)(2,1)S(1)}, bf16[32,1024]{1,0:T(8,128)(2,1)S(1)}, u32[]{:S(2)}, u32[]{:S(2)}) collective-permute-start(bf16[32,1024]{1,0:T(8,128)(2,1)S(1)} %get-tuple-element.29), channel_id=1, source_target_pairs={{0,2},{2,4},{4,6},{6,8},{8,10},{10,12},{12,14},{1,3},{3,5},{5,7},{... | collective-permute-start | bytes 196616 | tf_op jit(solution)/shard_map/ppermute | solution.py:28
  52.5 1.6 %collective-permute-done.4 = bf16[32,1024]{1,0:T(8,128)(2,1)S(1)} collective-permute-done((bf16[32,1024]{1,0:T(8,128)(2,1)S(1)}, bf16[32,1024]{1,0:T(8,128)(2,1)S(1)}, u32[]{:S(2)}, u32[]{:S(2)}) %collective-permute-start.4) | collective-permute-done | bytes 65568 | tf_op jit(solution)/shard_map/ppermute | solution.py:28
  54.2 3.0 %multiply_convert_fusion.1 = bf16[160,1024]{1,0:T(8,128)(2,1)S(1)} fusion(bf16[192,1024]{1,0:T(8,128)(2,1)S(1)} %pad_maximum_fusion.5, bf16[16,1024]{1,0:T(8,128)(2,1)S(1)} %reshape.178, bf16[128,1024]{1,0:T(8,128)(2,1)S(1)} %bitcast.163, bf16[16,1024]{1,0:T(8,128)(2,1)S(1)} %reshape.177, f32[1024]{0:T(1024)S(1)} %bitcast.234, f32[1024]{0:T(1024)S(1)} %bitcast.236, ...), kind=kLoop, calls=%fused_computation.31 | loop fusion | flops 17530880 | bytes 10940416 | tf_op jit(solution)/shard_map/convert_element_type | solution.py:175
  57.2 2.3 %add_convert_fusion = bf16[128,1024]{1,0:T(8,128)(2,1)S(1)} fusion(bf16[160,1024]{1,0:T(8,128)(2,1)S(1)} %multiply_convert_fusion.1, f32[1024]{0:T(1024)S(1)} %bitcast.235, f32[1024]{0:T(1024)S(1)} %bitcast.237, f32[1024]{0:T(1024)S(1)} %bitcast.179, f32[1024]{0:T(1024)S(1)} %bitcast.181, f32[1024]{0:T(1024)S(1)} %bitcast.183, f32[1024]{0:T(1024)S(1)} %bitcast.185, ...), kind=kLoop, calls=%fused_computation.54 | loop fusion | flops 12582912 | bytes 8777856 | tf_op jit(solution)/shard_map/convert_element_type | solution.py:193
  60.0 2.4 %fusion.7 = f32[1,31,1024]{2,0,1:T(1,128)S(1)} fusion(bf16[1,158,1024]{2,1,0:T(8,128)(2,1)S(1)} %slice_bitcast_fusion, bf16[128,1,1024]{2,0,1:T(8,128)(2,1)S(1)} %slice_bitcast_fusion.1), kind=kOutput, calls=%fused_computation.34 | convolution fusion | flops 8126464 | bytes 712704 | tf_op jit(solution)/shard_map/conv_general_dilated | solution.py:182
  62.4 0.8 copy-done.1
  63.2 0.9 fusion.2
  64.2 1.2 convert_multiply_fusion
  65.4 1.1 copy.19
  66.6 1.3 %fusion.4 = f32[1,8,40,1024]{3,2,1,0:T(8,128)S(1)} fusion(s32[]{:T(128)S(6)} %select_n.165, f32[2,8,32,1024]{3,2,1,0:T(8,128)S(1)} %bitcast.152, f32[2,8,8,1024]{3,2,1,0:T(8,128)} %bitcast.158, bf16[1,8,40,1024]{3,2,1,0:T(8,128)(2,1)} %collective-permute-done.10), kind=kLoop, calls=%fused_computation.19 | loop fusion | flops 983040 | bytes 4587524 | tf_op jit(solution)/shard_map/add | solution.py:78
  68.2 9.9 %collective-permute-done.11 = bf16[4,40,1024]{2,1,0:T(8,128)(2,1)S(1)} collective-permute-done((bf16[4,40,1024]{2,1,0:T(8,128)(2,1)S(1)}, bf16[4,40,1024]{2,1,0:T(8,128)(2,1)S(1)}, u32[]{:S(2)}, u32[]{:S(2)}) %collective-permute-start.11) | collective-permute-done | bytes 327712 | tf_op jit(solution)/shard_map/ppermute | solution.py:66
  78.3 2.1 %collective-permute-start.12 = (bf16[2,40,1024]{2,1,0:T(8,128)(2,1)S(1)}, bf16[2,40,1024]{2,1,0:T(8,128)(2,1)S(1)}, u32[]{:S(2)}, u32[]{:S(2)}) collective-permute-start(bf16[2,40,1024]{2,1,0:T(8,128)(2,1)S(1)} %dynamic-slice_convert_fusion.1), channel_id=1, source_target_pairs={{0,4},{2,6},{4,0},{6,2},{8,12},{10,14},{12,8},{14,10},{1,5},{3,7},... | collective-permute-start | bytes 491528 | tf_op jit(solution)/shard_map/ppermute | solution.py:66
  80.4 1.2 multiply_convert_fusion
  81.6 3.1 %collective-permute-done.12 = bf16[2,40,1024]{2,1,0:T(8,128)(2,1)S(1)} collective-permute-done((bf16[2,40,1024]{2,1,0:T(8,128)(2,1)S(1)}, bf16[2,40,1024]{2,1,0:T(8,128)(2,1)S(1)}, u32[]{:S(2)}, u32[]{:S(2)}) %collective-permute-start.12) | collective-permute-done | bytes 163872 | tf_op jit(solution)/shard_map/ppermute | solution.py:66
  84.7 2.8 %collective-permute-start.13 = (bf16[1,40,1024]{2,1,0:T(8,128)(2,1)S(1)}, bf16[1,40,1024]{2,1,0:T(8,128)(2,1)S(1)}, u32[]{:S(2)}, u32[]{:S(2)}) collective-permute-start(bf16[1,40,1024]{2,1,0:T(8,128)(2,1)S(1)} %dynamic-slice_convert_fusion.2), channel_id=1, source_target_pairs={{0,8},{2,10},{4,12},{6,14},{8,0},{10,2},{12,4},{14,6},{1,9},{3,11}... | collective-permute-start | bytes 245768 | tf_op jit(solution)/shard_map/ppermute | solution.py:66
  87.5 1.1 fusion.47
  88.6 1.6 %collective-permute-done.13 = bf16[1,40,1024]{2,1,0:T(8,128)(2,1)S(1)} collective-permute-done((bf16[1,40,1024]{2,1,0:T(8,128)(2,1)S(1)}, bf16[1,40,1024]{2,1,0:T(8,128)(2,1)S(1)}, u32[]{:S(2)}, u32[]{:S(2)}) %collective-permute-start.13) | collective-permute-done | bytes 81952 | tf_op jit(solution)/shard_map/ppermute | solution.py:66
  90.2 2.7 %collective-permute-start.14 = (bf16[1,40,1024]{2,1,0:T(8,128)(2,1)S(1)}, bf16[1,40,1024]{2,1,0:T(8,128)(2,1)S(1)}, u32[]{:S(2)}, u32[]{:S(2)}) collective-permute-start(bf16[1,40,1024]{2,1,0:T(8,128)(2,1)S(1)} %add_convert_fusion.1), channel_id=1, source_target_pairs={{0,8},{2,10},{4,12},{6,14},{8,0},{10,2},{12,4},{14,6},{1,9},{3,11}... | collective-permute-start | bytes 245768 | tf_op jit(solution)/shard_map/ppermute | solution.py:66
  93.0 1.1 fusion.48
  94.1 1.6 %collective-permute-done.14 = bf16[1,40,1024]{2,1,0:T(8,128)(2,1)S(1)} collective-permute-done((bf16[1,40,1024]{2,1,0:T(8,128)(2,1)S(1)}, bf16[1,40,1024]{2,1,0:T(8,128)(2,1)S(1)}, u32[]{:S(2)}, u32[]{:S(2)}) %collective-permute-start.14) | collective-permute-done | bytes 81952 | tf_op jit(solution)/shard_map/ppermute | solution.py:66
  95.7 1.7 %collective-permute-start.15 = (bf16[2,40,1024]{2,1,0:T(8,128)(2,1)S(1)}, bf16[2,40,1024]{2,1,0:T(8,128)(2,1)S(1)}, u32[]{:S(2)}, u32[]{:S(2)}) collective-permute-start(bf16[2,40,1024]{2,1,0:T(8,128)(2,1)S(1)} %pad_maximum_fusion.10), channel_id=1, source_target_pairs={{0,4},{2,6},{4,0},{6,2},{8,12},{10,14},{12,8},{14,10},{1,5},{3,7},... | collective-permute-start | bytes 491528 | tf_op jit(solution)/shard_map/ppermute | solution.py:66
  97.4 1.3 %fusion.50 = f32[1024,512]{1,0:T(8,128)S(1)} fusion(bf16[1024,896]{0,1:T(8,128)(2,1)S(1)} %multiply_convert_fusion, bf16[896,512]{1,0:T(8,128)(2,1)S(1)} %copy-done.15), kind=kOutput, calls=%fused_computation.131 | convolution fusion | flops 939524096 | bytes 4849664 | tf_op jit(solution)/shard_map/dot_general | solution.py:150
  98.8 1.3 collective-permute-start.7
  100.1 4.6 %collective-permute-start.6 = (bf16[2,2,128,512]{3,2,1,0:T(8,128)(2,1)S(1)}, bf16[2,2,128,512]{3,2,1,0:T(8,128)(2,1)S(1)}, u32[]{:S(2)}, u32[]{:S(2)}) collective-permute-start(bf16[2,2,128,512]{3,2,1,0:T(8,128)(2,1)S(1)} %get-tuple-element.5), channel_id=1, source_target_pairs={{0,4},{2,6},{4,8},{6,10},{8,12},{10,14},{1,5},{3,7},{5,9},{7,11},{... | collective-permute-start | bytes 1572872 | tf_op jit(solution)/shard_map/ppermute | solution.py:17
  104.8 1.5 %collective-permute-start.16 = (bf16[4,40,1024]{2,1,0:T(8,128)(2,1)S(1)}, bf16[4,40,1024]{2,1,0:T(8,128)(2,1)S(1)}, u32[]{:S(2)}, u32[]{:S(2)}) collective-permute-start(bf16[4,40,1024]{2,1,0:T(8,128)(2,1)S(1)} %pad_maximum_fusion.6), channel_id=1, source_target_pairs={{0,2},{2,0},{4,6},{6,4},{8,10},{10,8},{12,14},{14,12},{1,3},{3,1},... | collective-permute-start | bytes 983048 | tf_op jit(solution)/shard_map/ppermute | solution.py:66
  106.7 5.6 %collective-permute-done.7 = bf16[2,2,128,512]{3,2,1,0:T(8,128)(2,1)S(1)} collective-permute-done((bf16[2,2,128,512]{3,2,1,0:T(8,128)(2,1)S(1)}, bf16[2,2,128,512]{3,2,1,0:T(8,128)(2,1)S(1)}, u32[]{:S(2)}, u32[]{:S(2)}) %collective-permute-start.7) | collective-permute-done | bytes 524320 | tf_op jit(solution)/shard_map/ppermute | solution.py:17
  112.9 3.5 %collective-permute-start.9 = (bf16[2,128,512]{2,1,0:T(8,128)(2,1)S(1)}, bf16[2,128,512]{2,1,0:T(8,128)(2,1)S(1)}, u32[]{:S(2)}, u32[]{:S(2)}) collective-permute-start(bf16[2,128,512]{2,1,0:T(8,128)(2,1)S(1)} %get-tuple-element.8), channel_id=1, source_target_pairs={{2,0},{4,2},{6,4},{8,6},{10,8},{12,10},{14,12},{3,1},{5,3},{7,5},{... | collective-permute-start | bytes 786440 | tf_op jit(solution)/shard_map/ppermute | solution.py:17
  116.3 3.3 %collective-permute-start.8 = (bf16[2,128,512]{2,1,0:T(8,128)(2,1)S(1)}, bf16[2,128,512]{2,1,0:T(8,128)(2,1)S(1)}, u32[]{:S(2)}, u32[]{:S(2)}) collective-permute-start(bf16[2,128,512]{2,1,0:T(8,128)(2,1)S(1)} %get-tuple-element.7), channel_id=1, source_target_pairs={{0,2},{2,4},{4,6},{6,8},{8,10},{10,12},{12,14},{1,3},{3,5},{5,7},{... | collective-permute-start | bytes 786440 | tf_op jit(solution)/shard_map/ppermute | solution.py:17
  120.5 1.6 %collective-permute-done.9 = bf16[2,128,512]{2,1,0:T(8,128)(2,1)S(1)} collective-permute-done((bf16[2,128,512]{2,1,0:T(8,128)(2,1)S(1)}, bf16[2,128,512]{2,1,0:T(8,128)(2,1)S(1)}, u32[]{:S(2)}, u32[]{:S(2)}) %collective-permute-start.9) | collective-permute-done | bytes 262176 | tf_op jit(solution)/shard_map/ppermute | solution.py:17
  122.1 4.3 %collective-permute-done.8 = bf16[2,128,512]{2,1,0:T(8,128)(2,1)S(1)} collective-permute-done((bf16[2,128,512]{2,1,0:T(8,128)(2,1)S(1)}, bf16[2,128,512]{2,1,0:T(8,128)(2,1)S(1)}, u32[]{:S(2)}, u32[]{:S(2)}) %collective-permute-start.8) | collective-permute-done | bytes 262176 | tf_op jit(solution)/shard_map/ppermute | solution.py:17
  126.7 0.7 fusion.42
  127.5 1.1 fusion.6
  (100 shorter events, 5.4 us)
Async XLA Ops:
  0.6 44.5 %copy-start = (bf16[512,1024]{1,0:T(8,128)(2,1)S(1)}, bf16[512,1024]{1,0:T(8,128)(2,1)}, u32[]{:S(2)}) copy-start(bf16[512,1024]{1,0:T(8,128)(2,1)} %param.11) | copy-start | bytes 3145732
  2.5 22.6 %copy-start.11 = (f32[31,1024]{1,0:T(8,128)S(1)}, f32[31,1024]{1,0:T(8,128)}, u32[]{:S(2)}) copy-start(f32[31,1024]{1,0:T(8,128)} %param.12) | copy-start | bytes 380932
  2.5 22.6 %copy-start.10 = (bf16[1,128,512]{2,1,0:T(8,128)(2,1)S(1)}, bf16[1,128,512]{2,1,0:T(8,128)(2,1)}, u32[]{:S(2)}) copy-start(bf16[1,128,512]{2,1,0:T(8,128)(2,1)} %param.7) | copy-start | bytes 393220
  3.5 11.6 %collective-permute-start.2 = (bf16[288,512]{1,0:T(8,128)(2,1)S(1)}, bf16[288,512]{1,0:T(8,128)(2,1)S(1)}, u32[]{:S(2)}, u32[]{:S(2)}) collective-permute-start(bf16[288,512]{1,0:T(8,128)(2,1)S(1)} %get-tuple-element.33), channel_id=1, source_target_pairs={{2,0},{4,2},{6,4},{8,6},{10,8},{12,10},{14,12},{3,1},{5,3},{7,5},{... | collective-permute-start | bytes 884744 | tf_op jit(solution)/shard_map/ppermute | solution.py:17
  5.4 15.9 %collective-permute-start = (bf16[288,512]{1,0:T(8,128)(2,1)S(1)}, bf16[288,512]{1,0:T(8,128)(2,1)S(1)}, u32[]{:S(2)}, u32[]{:S(2)}) collective-permute-start(bf16[288,512]{1,0:T(8,128)(2,1)S(1)} %get-tuple-element.34), channel_id=1, source_target_pairs={{0,2},{2,4},{4,6},{6,8},{8,10},{10,12},{12,14},{1,3},{3,5},{5,7},{... | collective-permute-start | bytes 884744 | tf_op jit(solution)/shard_map/ppermute | solution.py:17
  21.4 15.0 %copy-start.8 = (bf16[1,128,512]{2,1,0:T(8,128)(2,1)S(1)}, bf16[1,128,512]{2,1,0:T(8,128)(2,1)}, u32[]{:S(2)}) copy-start(bf16[1,128,512]{2,1,0:T(8,128)(2,1)} %param.8) | copy-start | bytes 393220
  21.4 15.0 %copy-start.9 = (bf16[1,128,512]{2,1,0:T(8,128)(2,1)S(1)}, bf16[1,128,512]{2,1,0:T(8,128)(2,1)}, u32[]{:S(2)}) copy-start(bf16[1,128,512]{2,1,0:T(8,128)(2,1)} %param.9) | copy-start | bytes 393220
  21.5 14.8 %collective-permute-start.1 = (bf16[2,2,128,512]{3,2,1,0:T(8,128)(2,1)S(1)}, bf16[2,2,128,512]{3,2,1,0:T(8,128)(2,1)S(1)}, u32[]{:S(2)}, u32[]{:S(2)}) collective-permute-start(bf16[2,2,128,512]{3,2,1,0:T(8,128)(2,1)S(1)} %get-tuple-element.32), channel_id=1, source_target_pairs={{0,4},{2,6},{4,8},{6,10},{8,12},{10,14},{1,5},{3,7},{5,9},{7,11},{... | collective-permute-start | bytes 1572872 | tf_op jit(solution)/shard_map/ppermute | solution.py:17
  25.2 16.7 %copy-start.5 = (bf16[8,128,512]{2,1,0:T(8,128)(2,1)}, bf16[8,128,512]{2,1,0:T(8,128)(2,1)S(1)}, u32[]{:S(2)}) copy-start(bf16[8,128,512]{2,1,0:T(8,128)(2,1)S(1)} %broadcast_select_fusion.1) | copy-start | bytes 3145732
  25.2 15.5 %collective-permute-start.3 = (bf16[2,2,128,512]{3,2,1,0:T(8,128)(2,1)S(1)}, bf16[2,2,128,512]{3,2,1,0:T(8,128)(2,1)S(1)}, u32[]{:S(2)}, u32[]{:S(2)}) collective-permute-start(bf16[2,2,128,512]{3,2,1,0:T(8,128)(2,1)S(1)} %get-tuple-element.31), channel_id=1, source_target_pairs={{4,0},{6,2},{8,4},{10,6},{12,8},{14,10},{5,1},{7,3},{9,5},{11,7},{... | collective-permute-start | bytes 1572872 | tf_op jit(solution)/shard_map/ppermute | solution.py:17
  40.7 1.2 copy-start.14
  40.8 2.8 %copy-start.12 = (bf16[896,512]{1,0:T(8,128)(2,1)}, bf16[896,512]{1,0:T(8,128)(2,1)S(1)}, u32[]{:S(2)}) copy-start(bf16[896,512]{1,0:T(8,128)(2,1)S(1)} %get-tuple-element.13) | copy-start | bytes 2752516
  43.5 1.3 %copy-start.2 = (bf16[1024,896]{0,1:T(8,128)(2,1)}, bf16[1024,896]{0,1:T(8,128)(2,1)S(1)}, u32[]{:S(2)}) copy-start(bf16[1024,896]{0,1:T(8,128)(2,1)S(1)} %exponential_convert_fusion) | copy-start | bytes 5505028
  45.1 9.1 %copy-start.4 = (bf16[1,128,1024]{2,1,0:T(8,128)(2,1)S(1)}, bf16[1,128,1024]{2,1,0:T(8,128)(2,1)}, u32[]{:S(2)}) copy-start(bf16[1,128,1024]{2,1,0:T(8,128)(2,1)} %param.10) | copy-start | bytes 786436
  45.5 7.1 %collective-permute-start.5 = (bf16[32,1024]{1,0:T(8,128)(2,1)S(1)}, bf16[32,1024]{1,0:T(8,128)(2,1)S(1)}, u32[]{:S(2)}, u32[]{:S(2)}) collective-permute-start(bf16[32,1024]{1,0:T(8,128)(2,1)S(1)} %get-tuple-element.30), channel_id=1, source_target_pairs={{2,0},{4,2},{6,4},{8,6},{10,8},{12,10},{14,12},{3,1},{5,3},{7,5},{... | collective-permute-start | bytes 196616 | tf_op jit(solution)/shard_map/ppermute | solution.py:30
  47.4 6.7 %collective-permute-start.4 = (bf16[32,1024]{1,0:T(8,128)(2,1)S(1)}, bf16[32,1024]{1,0:T(8,128)(2,1)S(1)}, u32[]{:S(2)}, u32[]{:S(2)}) collective-permute-start(bf16[32,1024]{1,0:T(8,128)(2,1)S(1)} %get-tuple-element.29), channel_id=1, source_target_pairs={{0,2},{2,4},{4,6},{6,8},{8,10},{10,12},{12,14},{1,3},{3,5},{5,7},{... | collective-permute-start | bytes 196616 | tf_op jit(solution)/shard_map/ppermute | solution.py:28
  62.4 0.8 copy-start.1
  64.2 2.4 %collective-permute-start.10 = (bf16[1,8,40,1024]{3,2,1,0:T(8,128)(2,1)}, bf16[1,8,40,1024]{3,2,1,0:T(8,128)(2,1)}, u32[]{:S(2)}, u32[]{:S(2)}) collective-permute-start(bf16[1,8,40,1024]{3,2,1,0:T(8,128)(2,1)} %fusion.2), channel_id=1, source_target_pairs={{0,1},{1,0},{2,3},{3,2},{4,5},{5,4},{6,7},{7,6},{8,9},{9,8},{10,11... | collective-permute-start | bytes 1966088 | tf_op jit(solution)/shard_map/ppermute | solution.py:66
  66.5 1.7 %copy-start.7 = (bf16[128,512]{1,0:T(8,128)(2,1)S(1)}, bf16[128,512]{1,0:T(8,128)(2,1)}, u32[]{:S(2)}) copy-start(bf16[128,512]{1,0:T(8,128)(2,1)} %get-tuple-element.73) | copy-start | bytes 393220
  68.0 12.5 %copy-start.3 = (bf16[1024,896]{0,1:T(8,128)(2,1)S(1)}, bf16[1024,896]{0,1:T(8,128)(2,1)}, u32[]{:S(2)}) copy-start(bf16[1024,896]{0,1:T(8,128)(2,1)} %copy-done.2) | copy-start | bytes 5505028
  68.0 12.5 %copy-start.13 = (bf16[896,512]{1,0:T(8,128)(2,1)S(1)}, bf16[896,512]{1,0:T(8,128)(2,1)}, u32[]{:S(2)}) copy-start(bf16[896,512]{1,0:T(8,128)(2,1)} %copy-done.12) | copy-start | bytes 2752516
  68.0 10.1 %collective-permute-start.11 = (bf16[4,40,1024]{2,1,0:T(8,128)(2,1)S(1)}, bf16[4,40,1024]{2,1,0:T(8,128)(2,1)S(1)}, u32[]{:S(2)}, u32[]{:S(2)}) collective-permute-start(bf16[4,40,1024]{2,1,0:T(8,128)(2,1)S(1)} %fusion.21), channel_id=1, source_target_pairs={{0,2},{2,0},{4,6},{6,4},{8,10},{10,8},{12,14},{14,12},{1,3},{3,1},... | collective-permute-start | bytes 983048 | tf_op jit(solution)/shard_map/ppermute | solution.py:66
  78.3 6.4 %collective-permute-start.12 = (bf16[2,40,1024]{2,1,0:T(8,128)(2,1)S(1)}, bf16[2,40,1024]{2,1,0:T(8,128)(2,1)S(1)}, u32[]{:S(2)}, u32[]{:S(2)}) collective-permute-start(bf16[2,40,1024]{2,1,0:T(8,128)(2,1)S(1)} %dynamic-slice_convert_fusion.1), channel_id=1, source_target_pairs={{0,4},{2,6},{4,0},{6,2},{8,12},{10,14},{12,8},{14,10},{1,5},{3,7},... | collective-permute-start | bytes 491528 | tf_op jit(solution)/shard_map/ppermute | solution.py:66
  84.7 8.2 %copy-start.6 = (bf16[8,128,512]{2,1,0:T(8,128)(2,1)S(1)}, bf16[8,128,512]{2,1,0:T(8,128)(2,1)}, u32[]{:S(2)}) copy-start(bf16[8,128,512]{2,1,0:T(8,128)(2,1)} %copy-done.5) | copy-start | bytes 3145732
  84.7 5.5 %collective-permute-start.13 = (bf16[1,40,1024]{2,1,0:T(8,128)(2,1)S(1)}, bf16[1,40,1024]{2,1,0:T(8,128)(2,1)S(1)}, u32[]{:S(2)}, u32[]{:S(2)}) collective-permute-start(bf16[1,40,1024]{2,1,0:T(8,128)(2,1)S(1)} %dynamic-slice_convert_fusion.2), channel_id=1, source_target_pairs={{0,8},{2,10},{4,12},{6,14},{8,0},{10,2},{12,4},{14,6},{1,9},{3,11}... | collective-permute-start | bytes 245768 | tf_op jit(solution)/shard_map/ppermute | solution.py:66
  90.2 7.2 %copy-start.15 = (bf16[896,512]{1,0:T(8,128)(2,1)S(1)}, bf16[896,512]{1,0:T(8,128)(2,1)}, u32[]{:S(2)}) copy-start(bf16[896,512]{1,0:T(8,128)(2,1)} %copy-done.14) | copy-start | bytes 2752516
  90.2 5.4 %collective-permute-start.14 = (bf16[1,40,1024]{2,1,0:T(8,128)(2,1)S(1)}, bf16[1,40,1024]{2,1,0:T(8,128)(2,1)S(1)}, u32[]{:S(2)}, u32[]{:S(2)}) collective-permute-start(bf16[1,40,1024]{2,1,0:T(8,128)(2,1)S(1)} %add_convert_fusion.1), channel_id=1, source_target_pairs={{0,8},{2,10},{4,12},{6,14},{8,0},{10,2},{12,4},{14,6},{1,9},{3,11}... | collective-permute-start | bytes 245768 | tf_op jit(solution)/shard_map/ppermute | solution.py:66
  95.7 9.0 %collective-permute-start.15 = (bf16[2,40,1024]{2,1,0:T(8,128)(2,1)S(1)}, bf16[2,40,1024]{2,1,0:T(8,128)(2,1)S(1)}, u32[]{:S(2)}, u32[]{:S(2)}) collective-permute-start(bf16[2,40,1024]{2,1,0:T(8,128)(2,1)S(1)} %pad_maximum_fusion.10), channel_id=1, source_target_pairs={{0,4},{2,6},{4,0},{6,2},{8,12},{10,14},{12,8},{14,10},{1,5},{3,7},... | collective-permute-start | bytes 491528 | tf_op jit(solution)/shard_map/ppermute | solution.py:66
  98.8 13.5 %collective-permute-start.7 = (bf16[2,2,128,512]{3,2,1,0:T(8,128)(2,1)S(1)}, bf16[2,2,128,512]{3,2,1,0:T(8,128)(2,1)S(1)}, u32[]{:S(2)}, u32[]{:S(2)}) collective-permute-start(bf16[2,2,128,512]{3,2,1,0:T(8,128)(2,1)S(1)} %get-tuple-element.6), channel_id=1, source_target_pairs={{4,0},{6,2},{8,4},{10,6},{12,8},{14,10},{5,1},{7,3},{9,5},{11,7},{... | collective-permute-start | bytes 1572872 | tf_op jit(solution)/shard_map/ppermute | solution.py:17
  100.1 12.4 %collective-permute-start.6 = (bf16[2,2,128,512]{3,2,1,0:T(8,128)(2,1)S(1)}, bf16[2,2,128,512]{3,2,1,0:T(8,128)(2,1)S(1)}, u32[]{:S(2)}, u32[]{:S(2)}) collective-permute-start(bf16[2,2,128,512]{3,2,1,0:T(8,128)(2,1)S(1)} %get-tuple-element.5), channel_id=1, source_target_pairs={{0,4},{2,6},{4,8},{6,10},{8,12},{10,14},{1,5},{3,7},{5,9},{7,11},{... | collective-permute-start | bytes 1572872 | tf_op jit(solution)/shard_map/ppermute | solution.py:17
  104.8 14.8 %collective-permute-start.16 = (bf16[4,40,1024]{2,1,0:T(8,128)(2,1)S(1)}, bf16[4,40,1024]{2,1,0:T(8,128)(2,1)S(1)}, u32[]{:S(2)}, u32[]{:S(2)}) collective-permute-start(bf16[4,40,1024]{2,1,0:T(8,128)(2,1)S(1)} %pad_maximum_fusion.6), channel_id=1, source_target_pairs={{0,2},{2,0},{4,6},{6,4},{8,10},{10,8},{12,14},{14,12},{1,3},{3,1},... | collective-permute-start | bytes 983048 | tf_op jit(solution)/shard_map/ppermute | solution.py:66
  112.9 9.3 %collective-permute-start.9 = (bf16[2,128,512]{2,1,0:T(8,128)(2,1)S(1)}, bf16[2,128,512]{2,1,0:T(8,128)(2,1)S(1)}, u32[]{:S(2)}, u32[]{:S(2)}) collective-permute-start(bf16[2,128,512]{2,1,0:T(8,128)(2,1)S(1)} %get-tuple-element.8), channel_id=1, source_target_pairs={{2,0},{4,2},{6,4},{8,6},{10,8},{12,10},{14,12},{3,1},{5,3},{7,5},{... | collective-permute-start | bytes 786440 | tf_op jit(solution)/shard_map/ppermute | solution.py:17
  116.3 10.1 %collective-permute-start.8 = (bf16[2,128,512]{2,1,0:T(8,128)(2,1)S(1)}, bf16[2,128,512]{2,1,0:T(8,128)(2,1)S(1)}, u32[]{:S(2)}, u32[]{:S(2)}) collective-permute-start(bf16[2,128,512]{2,1,0:T(8,128)(2,1)S(1)} %get-tuple-element.7), channel_id=1, source_target_pairs={{0,2},{2,4},{4,6},{6,8},{8,10},{10,12},{12,14},{1,3},{3,5},{5,7},{... | collective-permute-start | bytes 786440 | tf_op jit(solution)/shard_map/ppermute | solution.py:17
  119.8 7.7 %collective-permute-start.17 = (bf16[1,8,40,1024]{3,2,1,0:T(8,128)(2,1)S(1)}, bf16[1,8,40,1024]{3,2,1,0:T(8,128)(2,1)S(1)}, u32[]{:S(2)}, u32[]{:S(2)}) collective-permute-start(bf16[1,8,40,1024]{3,2,1,0:T(8,128)(2,1)S(1)} %maximum_bitcast_fusion), channel_id=1, source_target_pairs={{0,1},{1,0},{2,3},{3,2},{4,5},{5,4},{6,7},{7,6},{8,9},{9,8},{10,11... | collective-permute-start | bytes 1966088 | tf_op jit(solution)/shard_map/ppermute | solution.py:66

commit v22 on v21

--- a/solution.py
+++ b/solution.py
@@ -230,9 +230,7 @@
     key_blocks = grad_key_all.reshape(span_blocks, tokens, width_heads)
     value_blocks = grad_value_all.reshape(span_blocks, tokens, width_heads)
     narrow = jnp.stack([key_blocks, value_blocks], axis=1).astype(jnp.bfloat16)
-    near = jnp.stack(
-        [key_blocks[REACH - 1 : REACH + 2], value_blocks[REACH - 1 : REACH + 2]], axis=1
-    )
+    near = [jnp.stack([key_blocks[row], value_blocks[row]], axis=0) for row in range(REACH - 1, REACH + 2)]
 
     def grad_shift(piece_rows, offset_by):
         return passed_along(piece_rows, "ctx", offset_by)

time: 130 us -> 135 us (1.038)
  local copies, waits for them, and re-layouts: 6.13 us -> 8.95 us
  starting transfers between devices: 42.1 us -> 44 us
    ppermute x8, waiting for transfers between devices: 36 us -> 26.3 us  [passed_along(): return lax.ppermute(block, axis, route)]
    ppermute x8, waiting for transfers between devices: 16.3 us -> 25.6 us  [exchange(): return lax.ppermute(block, axis, [(i, i ^ bit) for i in range(count)])]
    ppermute x8, starting transfers between devices: 11 us -> 13 us  [exchange(): return lax.ppermute(block, axis, [(i, i ^ bit) for i in range(count)])]
    unnamed x40 -> x38, local copies, waits for them, and re-layouts: 1.94 us -> 3.53 us
  transfers between devices with their start and end apart: 18 -> 18, of which waited for: 13 -> 11; matrix products, arithmetic and copies ran while one was open for 8% -> 6% of each run, Pallas kernels for 0% -> 0%
where the time goes in v22:
time: 135 us; the launch traced here: 134 us
  waiting for transfers between devices  53.4 us (40%)
  starting transfers between devices  44 us (33%)
  other arithmetic  13.5 us (10%)
  matrix products  11.8 us (9%)
  local copies, waits for them, and re-layouts  8.95 us (7%)
  between operations  2.16 us (2%)
    ppermute x8, waiting for transfers between devices, passed_along(): return lax.ppermute(block, axis, route)  26.3 us
    ppermute x8, waiting for transfers between devices, exchange(): return lax.ppermute(block, axis, [(i, i ^ bit) for i in range(count)])  25.6 us
    ppermute x8, starting transfers between devices, passed_along(): return lax.ppermute(block, axis, route)  24.2 us
    ppermute x8, starting transfers between devices, exchange(): return lax.ppermute(block, axis, [(i, i ^ bit) for i in range(count)])  13 us
    dot_general x6, matrix products, contract(): lax.dot_general(lhs, rhs, (((lhs_dim,), (rhs_dim,)), ((), ())), preferred...  7.13 us
    ppermute x1, starting transfers between devices, padded(): lax.ppermute(tail, axis, [(i, (i + 1) % count) for i in range(ends)])  5 us
    unnamed x38, local copies, waits for them, and re-layouts  3.53 us
    conv_general_dilated x1, matrix products, on_device(): lax.conv_general_dilated(padded_m[None, edge - halo_width:edge + tokens +...  3.45 us
  transfers between devices with their start and end apart: 18, of which 11 were waited for; matrix products, arithmetic and copies ran while one was open for 6% of the time, Pallas kernels for 0%

profile of v22, /device:TPU:2, one launch (start us, length us, event | category | flops | bytes accessed | tf_op | source)
XLA Modules:
  0.0 133.9 jit_solution(17802872858843052545)
XLA Ops:
  0.6 0.9 fusion.40
  1.5 0.9 constant_dynamic-update-slice_fusion.1
  2.5 1.0 constant_dynamic-update-slice_fusion
  3.5 1.9 %collective-permute-start.2 = (bf16[288,512]{1,0:T(8,128)(2,1)S(1)}, bf16[288,512]{1,0:T(8,128)(2,1)S(1)}, u32[]{:S(2)}, u32[]{:S(2)}) collective-permute-start(bf16[288,512]{1,0:T(8,128)(2,1)S(1)} %get-tuple-element.37), channel_id=1, source_target_pairs={{2,0},{4,2},{6,4},{8,6},{10,8},{12,10},{14,12},{3,1},{5,3},{7,5},{... | collective-permute-start | bytes 884744 | tf_op jit(solution)/shard_map/ppermute | solution.py:17
  5.4 4.8 %collective-permute-start = (bf16[288,512]{1,0:T(8,128)(2,1)S(1)}, bf16[288,512]{1,0:T(8,128)(2,1)S(1)}, u32[]{:S(2)}, u32[]{:S(2)}) collective-permute-start(bf16[288,512]{1,0:T(8,128)(2,1)S(1)} %get-tuple-element.38), channel_id=1, source_target_pairs={{0,2},{2,4},{4,6},{6,8},{8,10},{10,12},{12,14},{1,3},{3,5},{5,7},{... | collective-permute-start | bytes 884744 | tf_op jit(solution)/shard_map/ppermute | solution.py:17
  11.0 4.2 %collective-permute-done.2 = bf16[288,512]{1,0:T(8,128)(2,1)S(1)} collective-permute-done((bf16[288,512]{1,0:T(8,128)(2,1)S(1)}, bf16[288,512]{1,0:T(8,128)(2,1)S(1)}, u32[]{:S(2)}, u32[]{:S(2)}) %collective-permute-start.2) | collective-permute-done | bytes 294944 | tf_op jit(solution)/shard_map/ppermute | solution.py:17
  15.2 6.2 %collective-permute-done = bf16[288,512]{1,0:T(8,128)(2,1)S(1)} collective-permute-done((bf16[288,512]{1,0:T(8,128)(2,1)S(1)}, bf16[288,512]{1,0:T(8,128)(2,1)S(1)}, u32[]{:S(2)}, u32[]{:S(2)}) %collective-permute-start) | collective-permute-done | bytes 294944 | tf_op jit(solution)/shard_map/ppermute | solution.py:17
  21.5 3.5 %collective-permute-start.1 = (bf16[2,2,128,512]{3,2,1,0:T(8,128)(2,1)S(1)}, bf16[2,2,128,512]{3,2,1,0:T(8,128)(2,1)S(1)}, u32[]{:S(2)}, u32[]{:S(2)}) collective-permute-start(bf16[2,2,128,512]{3,2,1,0:T(8,128)(2,1)S(1)} %get-tuple-element.36), channel_id=1, source_target_pairs={{0,4},{2,6},{4,8},{6,10},{8,12},{10,14},{1,5},{3,7},{5,9},{7,11},{... | collective-permute-start | bytes 1572872 | tf_op jit(solution)/shard_map/ppermute | solution.py:17
  25.2 1.3 collective-permute-start.3
  26.5 9.8 %collective-permute-done.1 = bf16[2,2,128,512]{3,2,1,0:T(8,128)(2,1)S(1)} collective-permute-done((bf16[2,2,128,512]{3,2,1,0:T(8,128)(2,1)S(1)}, bf16[2,2,128,512]{3,2,1,0:T(8,128)(2,1)S(1)}, u32[]{:S(2)}, u32[]{:S(2)}) %collective-permute-start.1) | collective-permute-done | bytes 524320 | tf_op jit(solution)/shard_map/ppermute | solution.py:17
  36.5 4.2 %collective-permute-done.3 = bf16[2,2,128,512]{3,2,1,0:T(8,128)(2,1)S(1)} collective-permute-done((bf16[2,2,128,512]{3,2,1,0:T(8,128)(2,1)S(1)}, bf16[2,2,128,512]{3,2,1,0:T(8,128)(2,1)S(1)}, u32[]{:S(2)}, u32[]{:S(2)}) %collective-permute-start.3) | collective-permute-done | bytes 524320 | tf_op jit(solution)/shard_map/ppermute | solution.py:17
  40.8 1.2 fusion
  42.0 0.8 exponential_reduce_fusion
  42.8 0.7 exponential_convert_fusion
  43.5 1.3 fusion.45
  45.5 1.9 %collective-permute-start.5 = (bf16[32,1024]{1,0:T(8,128)(2,1)S(1)}, bf16[32,1024]{1,0:T(8,128)(2,1)S(1)}, u32[]{:S(2)}, u32[]{:S(2)}) collective-permute-start(bf16[32,1024]{1,0:T(8,128)(2,1)S(1)} %get-tuple-element.34), channel_id=1, source_target_pairs={{2,0},{4,2},{6,4},{8,6},{10,8},{12,10},{14,12},{3,1},{5,3},{7,5},{... | collective-permute-start | bytes 196616 | tf_op jit(solution)/shard_map/ppermute | solution.py:30
  47.4 5.0 %collective-permute-start.4 = (bf16[32,1024]{1,0:T(8,128)(2,1)S(1)}, bf16[32,1024]{1,0:T(8,128)(2,1)S(1)}, u32[]{:S(2)}, u32[]{:S(2)}) collective-permute-start(bf16[32,1024]{1,0:T(8,128)(2,1)S(1)} %get-tuple-element.33), channel_id=1, source_target_pairs={{0,2},{2,4},{4,6},{6,8},{8,10},{10,12},{12,14},{1,3},{3,5},{5,7},{... | collective-permute-start | bytes 196616 | tf_op jit(solution)/shard_map/ppermute | solution.py:28
  52.6 1.5 %collective-permute-done.4 = bf16[32,1024]{1,0:T(8,128)(2,1)S(1)} collective-permute-done((bf16[32,1024]{1,0:T(8,128)(2,1)S(1)}, bf16[32,1024]{1,0:T(8,128)(2,1)S(1)}, u32[]{:S(2)}, u32[]{:S(2)}) %collective-permute-start.4) | collective-permute-done | bytes 65568 | tf_op jit(solution)/shard_map/ppermute | solution.py:28
  54.1 3.0 %multiply_convert_fusion.1 = bf16[160,1024]{1,0:T(8,128)(2,1)S(1)} fusion(bf16[192,1024]{1,0:T(8,128)(2,1)S(1)} %pad_maximum_fusion.4, bf16[16,1024]{1,0:T(8,128)(2,1)S(1)} %reshape.174, bf16[128,1024]{1,0:T(8,128)(2,1)S(1)} %bitcast.177, bf16[16,1024]{1,0:T(8,128)(2,1)S(1)} %reshape.173, f32[1024]{0:T(1024)S(1)} %bitcast.248, f32[1024]{0:T(1024)S(1)} %bitcast.250, ...), kind=kLoop, calls=%fused_computation.27 | loop fusion | flops 17530880 | bytes 10940416 | tf_op jit(solution)/shard_map/convert_element_type | solution.py:175
  57.1 2.3 %add_convert_fusion = bf16[128,1024]{1,0:T(8,128)(2,1)S(1)} fusion(bf16[160,1024]{1,0:T(8,128)(2,1)S(1)} %multiply_convert_fusion.1, f32[1024]{0:T(1024)S(1)} %bitcast.249, f32[1024]{0:T(1024)S(1)} %bitcast.251, f32[1024]{0:T(1024)S(1)} %bitcast.193, f32[1024]{0:T(1024)S(1)} %bitcast.195, f32[1024]{0:T(1024)S(1)} %bitcast.197, f32[1024]{0:T(1024)S(1)} %bitcast.199, ...), kind=kLoop, calls=%fused_computation.50 | loop fusion | flops 12582912 | bytes 8777856 | tf_op jit(solution)/shard_map/convert_element_type | solution.py:193
  60.3 0.8 slice_bitcast_fusion.4
  61.2 0.7 slice_bitcast_fusion.11
  61.9 1.0 broadcast_select_fusion
  62.9 0.8 copy.15
  63.8 1.0 bitcast_reduce_fusion
  64.8 3.5 %fusion.7 = f32[1,31,1024]{2,0,1:T(1,128)S(1)} fusion(bf16[1,158,1024]{2,1,0:T(8,128)(2,1)} %slice_bitcast_fusion.4, bf16[128,1,1024]{2,0,1:T(8,128)(2,1)} %slice_bitcast_fusion.11), kind=kOutput, calls=%fused_computation.30 | convolution fusion | flops 8126464 | bytes 712704 | tf_op jit(solution)/shard_map/conv_general_dilated | solution.py:182
  68.5 1.2 copy-done.2
  70.0 1.1 fusion.43
  71.2 1.1 multiply_convert_fusion
  72.7 0.9 copy-done.5
  73.6 1.1 fusion.44
  74.7 6.6 %collective-permute-done.11 = bf16[4,40,1024]{2,1,0:T(8,128)(2,1)S(1)} collective-permute-done((bf16[4,40,1024]{2,1,0:T(8,128)(2,1)S(1)}, bf16[4,40,1024]{2,1,0:T(8,128)(2,1)S(1)}, u32[]{:S(2)}, u32[]{:S(2)}) %collective-permute-start.11) | collective-permute-done | bytes 327712 | tf_op jit(solution)/shard_map/ppermute | solution.py:66
  81.5 2.1 %collective-permute-start.12 = (bf16[2,40,1024]{2,1,0:T(8,128)(2,1)S(1)}, bf16[2,40,1024]{2,1,0:T(8,128)(2,1)S(1)}, u32[]{:S(2)}, u32[]{:S(2)}) collective-permute-start(bf16[2,40,1024]{2,1,0:T(8,128)(2,1)S(1)} %dynamic-slice_convert_fusion.1), channel_id=1, source_target_pairs={{0,4},{2,6},{4,0},{6,2},{8,12},{10,14},{12,8},{14,10},{1,5},{3,7},... | collective-permute-start | bytes 491528 | tf_op jit(solution)/shard_map/ppermute | solution.py:66
  83.6 1.3 fusion.46
  85.0 1.3 collective-permute-start.7
  86.3 4.6 %collective-permute-start.6 = (bf16[2,2,128,512]{3,2,1,0:T(8,128)(2,1)S(1)}, bf16[2,2,128,512]{3,2,1,0:T(8,128)(2,1)S(1)}, u32[]{:S(2)}, u32[]{:S(2)}) collective-permute-start(bf16[2,2,128,512]{3,2,1,0:T(8,128)(2,1)S(1)} %get-tuple-element.11), channel_id=1, source_target_pairs={{0,4},{2,6},{4,8},{6,10},{8,12},{10,14},{1,5},{3,7},{5,9},{7,11},{... | collective-permute-start | bytes 1572872 | tf_op jit(solution)/shard_map/ppermute | solution.py:17
  91.0 1.3 collective-permute-start.13
  92.4 9.5 %collective-permute-done.13 = bf16[1,40,1024]{2,1,0:T(8,128)(2,1)S(1)} collective-permute-done((bf16[1,40,1024]{2,1,0:T(8,128)(2,1)S(1)}, bf16[1,40,1024]{2,1,0:T(8,128)(2,1)S(1)}, u32[]{:S(2)}, u32[]{:S(2)}) %collective-permute-start.13) | collective-permute-done | bytes 81952 | tf_op jit(solution)/shard_map/ppermute | solution.py:66
  101.8 3.5 %collective-permute-start.14 = (bf16[1,40,1024]{2,1,0:T(8,128)(2,1)S(1)}, bf16[1,40,1024]{2,1,0:T(8,128)(2,1)S(1)}, u32[]{:S(2)}, u32[]{:S(2)}) collective-permute-start(bf16[1,40,1024]{2,1,0:T(8,128)(2,1)S(1)} %add_convert_fusion.1), channel_id=1, source_target_pairs={{0,8},{2,10},{4,12},{6,14},{8,0},{10,2},{12,4},{14,6},{1,9},{3,11}... | collective-permute-start | bytes 245768 | tf_op jit(solution)/shard_map/ppermute | solution.py:66
  105.5 2.8 %collective-permute-done.14 = bf16[1,40,1024]{2,1,0:T(8,128)(2,1)S(1)} collective-permute-done((bf16[1,40,1024]{2,1,0:T(8,128)(2,1)S(1)}, bf16[1,40,1024]{2,1,0:T(8,128)(2,1)S(1)}, u32[]{:S(2)}, u32[]{:S(2)}) %collective-permute-start.14) | collective-permute-done | bytes 81952 | tf_op jit(solution)/shard_map/ppermute | solution.py:66
  108.3 3.6 %collective-permute-start.15 = (bf16[2,40,1024]{2,1,0:T(8,128)(2,1)S(1)}, bf16[2,40,1024]{2,1,0:T(8,128)(2,1)S(1)}, u32[]{:S(2)}, u32[]{:S(2)}) collective-permute-start(bf16[2,40,1024]{2,1,0:T(8,128)(2,1)S(1)} %pad_maximum_fusion.9), channel_id=1, source_target_pairs={{0,4},{2,6},{4,0},{6,2},{8,12},{10,14},{12,8},{14,10},{1,5},{3,7},... | collective-permute-start | bytes 491528 | tf_op jit(solution)/shard_map/ppermute | solution.py:66
  112.3 2.9 %collective-permute-done.15 = bf16[2,40,1024]{2,1,0:T(8,128)(2,1)S(1)} collective-permute-done((bf16[2,40,1024]{2,1,0:T(8,128)(2,1)S(1)}, bf16[2,40,1024]{2,1,0:T(8,128)(2,1)S(1)}, u32[]{:S(2)}, u32[]{:S(2)}) %collective-permute-start.15) | collective-permute-done | bytes 163872 | tf_op jit(solution)/shard_map/ppermute | solution.py:66
  115.3 2.1 %collective-permute-start.16 = (bf16[4,40,1024]{2,1,0:T(8,128)(2,1)S(1)}, bf16[4,40,1024]{2,1,0:T(8,128)(2,1)S(1)}, u32[]{:S(2)}, u32[]{:S(2)}) collective-permute-start(bf16[4,40,1024]{2,1,0:T(8,128)(2,1)S(1)} %pad_maximum_fusion.5), channel_id=1, source_target_pairs={{0,2},{2,0},{4,6},{6,4},{8,10},{10,8},{12,14},{14,12},{1,3},{3,1},... | collective-permute-start | bytes 983048 | tf_op jit(solution)/shard_map/ppermute | solution.py:66
  117.5 1.9 %collective-permute-start.9 = (bf16[2,128,512]{2,1,0:T(8,128)(2,1)S(1)}, bf16[2,128,512]{2,1,0:T(8,128)(2,1)S(1)}, u32[]{:S(2)}, u32[]{:S(2)}) collective-permute-start(bf16[2,128,512]{2,1,0:T(8,128)(2,1)S(1)} %fusion.10), channel_id=1, source_target_pairs={{2,0},{4,2},{6,4},{8,6},{10,8},{12,10},{14,12},{3,1},{5,3},{7,5},{... | collective-permute-start | bytes 786440 | tf_op jit(solution)/shard_map/ppermute | solution.py:17
  119.7 4.8 %collective-permute-start.8 = (bf16[2,128,512]{2,1,0:T(8,128)(2,1)S(1)}, bf16[2,128,512]{2,1,0:T(8,128)(2,1)S(1)}, u32[]{:S(2)}, u32[]{:S(2)}) collective-permute-start(bf16[2,128,512]{2,1,0:T(8,128)(2,1)S(1)} %fusion.12), channel_id=1, source_target_pairs={{0,2},{2,4},{4,6},{6,8},{8,10},{10,12},{12,14},{1,3},{3,5},{5,7},{... | collective-permute-start | bytes 786440 | tf_op jit(solution)/shard_map/ppermute | solution.py:17
  124.5 3.8 %collective-permute-done.16 = bf16[4,40,1024]{2,1,0:T(8,128)(2,1)S(1)} collective-permute-done((bf16[4,40,1024]{2,1,0:T(8,128)(2,1)S(1)}, bf16[4,40,1024]{2,1,0:T(8,128)(2,1)S(1)}, u32[]{:S(2)}, u32[]{:S(2)}) %collective-permute-start.16) | collective-permute-done | bytes 327712 | tf_op jit(solution)/shard_map/ppermute | solution.py:66
  129.1 1.9 %collective-permute-done.8 = bf16[2,128,512]{2,1,0:T(8,128)(2,1)S(1)} collective-permute-done((bf16[2,128,512]{2,1,0:T(8,128)(2,1)S(1)}, bf16[2,128,512]{2,1,0:T(8,128)(2,1)S(1)}, u32[]{:S(2)}, u32[]{:S(2)}) %collective-permute-start.8) | collective-permute-done | bytes 262176 | tf_op jit(solution)/shard_map/ppermute | solution.py:17
  132.1 1.1 fusion.6
  (99 shorter events, 6.9 us)
Async XLA Ops:
  0.6 44.5 %copy-start = (bf16[512,1024]{1,0:T(8,128)(2,1)S(1)}, bf16[512,1024]{1,0:T(8,128)(2,1)}, u32[]{:S(2)}) copy-start(bf16[512,1024]{1,0:T(8,128)(2,1)} %param.11) | copy-start | bytes 3145732
  2.5 22.6 %copy-start.10 = (f32[31,1024]{1,0:T(8,128)S(1)}, f32[31,1024]{1,0:T(8,128)}, u32[]{:S(2)}) copy-start(f32[31,1024]{1,0:T(8,128)} %param.12) | copy-start | bytes 380932
  2.5 22.6 %copy-start.9 = (bf16[1,128,512]{2,1,0:T(8,128)(2,1)S(1)}, bf16[1,128,512]{2,1,0:T(8,128)(2,1)}, u32[]{:S(2)}) copy-start(bf16[1,128,512]{2,1,0:T(8,128)(2,1)} %param.7) | copy-start | bytes 393220
  3.5 11.6 %collective-permute-start.2 = (bf16[288,512]{1,0:T(8,128)(2,1)S(1)}, bf16[288,512]{1,0:T(8,128)(2,1)S(1)}, u32[]{:S(2)}, u32[]{:S(2)}) collective-permute-start(bf16[288,512]{1,0:T(8,128)(2,1)S(1)} %get-tuple-element.37), channel_id=1, source_target_pairs={{2,0},{4,2},{6,4},{8,6},{10,8},{12,10},{14,12},{3,1},{5,3},{7,5},{... | collective-permute-start | bytes 884744 | tf_op jit(solution)/shard_map/ppermute | solution.py:17
  5.4 15.9 %collective-permute-start = (bf16[288,512]{1,0:T(8,128)(2,1)S(1)}, bf16[288,512]{1,0:T(8,128)(2,1)S(1)}, u32[]{:S(2)}, u32[]{:S(2)}) collective-permute-start(bf16[288,512]{1,0:T(8,128)(2,1)S(1)} %get-tuple-element.38), channel_id=1, source_target_pairs={{0,2},{2,4},{4,6},{6,8},{8,10},{10,12},{12,14},{1,3},{3,5},{5,7},{... | collective-permute-start | bytes 884744 | tf_op jit(solution)/shard_map/ppermute | solution.py:17
  21.4 15.0 %copy-start.7 = (bf16[1,128,512]{2,1,0:T(8,128)(2,1)S(1)}, bf16[1,128,512]{2,1,0:T(8,128)(2,1)}, u32[]{:S(2)}) copy-start(bf16[1,128,512]{2,1,0:T(8,128)(2,1)} %param.8) | copy-start | bytes 393220
  21.4 15.0 %copy-start.8 = (bf16[1,128,512]{2,1,0:T(8,128)(2,1)S(1)}, bf16[1,128,512]{2,1,0:T(8,128)(2,1)}, u32[]{:S(2)}) copy-start(bf16[1,128,512]{2,1,0:T(8,128)(2,1)} %param.9) | copy-start | bytes 393220
  21.5 14.8 %collective-permute-start.1 = (bf16[2,2,128,512]{3,2,1,0:T(8,128)(2,1)S(1)}, bf16[2,2,128,512]{3,2,1,0:T(8,128)(2,1)S(1)}, u32[]{:S(2)}, u32[]{:S(2)}) collective-permute-start(bf16[2,2,128,512]{3,2,1,0:T(8,128)(2,1)S(1)} %get-tuple-element.36), channel_id=1, source_target_pairs={{0,4},{2,6},{4,8},{6,10},{8,12},{10,14},{1,5},{3,7},{5,9},{7,11},{... | collective-permute-start | bytes 1572872 | tf_op jit(solution)/shard_map/ppermute | solution.py:17
  25.2 16.7 %copy-start.4 = (bf16[8,128,512]{2,1,0:T(8,128)(2,1)}, bf16[8,128,512]{2,1,0:T(8,128)(2,1)S(1)}, u32[]{:S(2)}) copy-start(bf16[8,128,512]{2,1,0:T(8,128)(2,1)S(1)} %broadcast_select_fusion.1) | copy-start | bytes 3145732
  25.2 15.5 %collective-permute-start.3 = (bf16[2,2,128,512]{3,2,1,0:T(8,128)(2,1)S(1)}, bf16[2,2,128,512]{3,2,1,0:T(8,128)(2,1)S(1)}, u32[]{:S(2)}, u32[]{:S(2)}) collective-permute-start(bf16[2,2,128,512]{3,2,1,0:T(8,128)(2,1)S(1)} %get-tuple-element.35), channel_id=1, source_target_pairs={{4,0},{6,2},{8,4},{10,6},{12,8},{14,10},{5,1},{7,3},{9,5},{11,7},{... | collective-permute-start | bytes 1572872 | tf_op jit(solution)/shard_map/ppermute | solution.py:17
  40.7 1.2 copy-start.13
  40.8 2.8 %copy-start.11 = (bf16[896,512]{1,0:T(8,128)(2,1)}, bf16[896,512]{1,0:T(8,128)(2,1)S(1)}, u32[]{:S(2)}) copy-start(bf16[896,512]{1,0:T(8,128)(2,1)S(1)} %get-tuple-element.17) | copy-start | bytes 2752516
  43.5 1.3 copy-start.1
  45.1 9.0 %copy-start.3 = (bf16[1,128,1024]{2,1,0:T(8,128)(2,1)S(1)}, bf16[1,128,1024]{2,1,0:T(8,128)(2,1)}, u32[]{:S(2)}) copy-start(bf16[1,128,1024]{2,1,0:T(8,128)(2,1)} %param.10) | copy-start | bytes 786436
  45.5 7.1 %collective-permute-start.5 = (bf16[32,1024]{1,0:T(8,128)(2,1)S(1)}, bf16[32,1024]{1,0:T(8,128)(2,1)S(1)}, u32[]{:S(2)}, u32[]{:S(2)}) collective-permute-start(bf16[32,1024]{1,0:T(8,128)(2,1)S(1)} %get-tuple-element.34), channel_id=1, source_target_pairs={{2,0},{4,2},{6,4},{8,6},{10,8},{12,10},{14,12},{3,1},{5,3},{7,5},{... | collective-permute-start | bytes 196616 | tf_op jit(solution)/shard_map/ppermute | solution.py:30
  47.4 6.7 %collective-permute-start.4 = (bf16[32,1024]{1,0:T(8,128)(2,1)S(1)}, bf16[32,1024]{1,0:T(8,128)(2,1)S(1)}, u32[]{:S(2)}, u32[]{:S(2)}) collective-permute-start(bf16[32,1024]{1,0:T(8,128)(2,1)S(1)} %get-tuple-element.33), channel_id=1, source_target_pairs={{0,2},{2,4},{4,6},{6,8},{8,10},{10,12},{12,14},{1,3},{3,5},{5,7},{... | collective-permute-start | bytes 196616 | tf_op jit(solution)/shard_map/ppermute | solution.py:28
  68.2 1.5 %copy-start.2 = (bf16[1024,896]{0,1:T(8,128)(2,1)S(1)}, bf16[1024,896]{0,1:T(8,128)(2,1)}, u32[]{:S(2)}) copy-start(bf16[1024,896]{0,1:T(8,128)(2,1)} %copy-done.1) | copy-start | bytes 5505028
  68.2 1.8 %copy-start.6 = (bf16[8,128,512]{2,1,0:T(8,128)(2,1)S(1)}, bf16[8,128,512]{2,1,0:T(8,128)(2,1)}, u32[]{:S(2)}) copy-start(bf16[8,128,512]{2,1,0:T(8,128)(2,1)} %broadcast_select_fusion) | copy-start | bytes 3145732
  68.4 3.9 %collective-permute-start.10 = (bf16[1,8,40,1024]{3,2,1,0:T(8,128)(2,1)S(1)}, bf16[1,8,40,1024]{3,2,1,0:T(8,128)(2,1)S(1)}, u32[]{:S(2)}, u32[]{:S(2)}) collective-permute-start(bf16[1,8,40,1024]{3,2,1,0:T(8,128)(2,1)S(1)} %fusion.2), channel_id=1, source_target_pairs={{0,1},{1,0},{2,3},{3,2},{4,5},{5,4},{6,7},{7,6},{8,9},{9,8},{10,11... | collective-permute-start | bytes 1966088 | tf_op jit(solution)/shard_map/ppermute | solution.py:66
  70.0 1.2 copy-start.12
  72.3 1.2 copy-start.5
  72.6 11.0 %copy-start.14 = (bf16[896,512]{1,0:T(8,128)(2,1)S(1)}, bf16[896,512]{1,0:T(8,128)(2,1)}, u32[]{:S(2)}) copy-start(bf16[896,512]{1,0:T(8,128)(2,1)} %copy-done.13) | copy-start | bytes 2752516
  72.6 8.7 %collective-permute-start.11 = (bf16[4,40,1024]{2,1,0:T(8,128)(2,1)S(1)}, bf16[4,40,1024]{2,1,0:T(8,128)(2,1)S(1)}, u32[]{:S(2)}, u32[]{:S(2)}) collective-permute-start(bf16[4,40,1024]{2,1,0:T(8,128)(2,1)S(1)} %fusion.19), channel_id=1, source_target_pairs={{0,2},{2,0},{4,6},{6,4},{8,10},{10,8},{12,14},{14,12},{1,3},{3,1},... | collective-permute-start | bytes 983048 | tf_op jit(solution)/shard_map/ppermute | solution.py:66
  81.5 9.4 %collective-permute-start.12 = (bf16[2,40,1024]{2,1,0:T(8,128)(2,1)S(1)}, bf16[2,40,1024]{2,1,0:T(8,128)(2,1)S(1)}, u32[]{:S(2)}, u32[]{:S(2)}) collective-permute-start(bf16[2,40,1024]{2,1,0:T(8,128)(2,1)S(1)} %dynamic-slice_convert_fusion.1), channel_id=1, source_target_pairs={{0,4},{2,6},{4,0},{6,2},{8,12},{10,14},{12,8},{14,10},{1,5},{3,7},... | collective-permute-start | bytes 491528 | tf_op jit(solution)/shard_map/ppermute | solution.py:66
  85.0 27.2 %collective-permute-start.7 = (bf16[2,2,128,512]{3,2,1,0:T(8,128)(2,1)S(1)}, bf16[2,2,128,512]{3,2,1,0:T(8,128)(2,1)S(1)}, u32[]{:S(2)}, u32[]{:S(2)}) collective-permute-start(bf16[2,2,128,512]{3,2,1,0:T(8,128)(2,1)S(1)} %get-tuple-element.12), channel_id=1, source_target_pairs={{4,0},{6,2},{8,4},{10,6},{12,8},{14,10},{5,1},{7,3},{9,5},{11,7},{... | collective-permute-start | bytes 1572872 | tf_op jit(solution)/shard_map/ppermute | solution.py:17
  86.3 33.1 %collective-permute-start.6 = (bf16[2,2,128,512]{3,2,1,0:T(8,128)(2,1)S(1)}, bf16[2,2,128,512]{3,2,1,0:T(8,128)(2,1)S(1)}, u32[]{:S(2)}, u32[]{:S(2)}) collective-permute-start(bf16[2,2,128,512]{3,2,1,0:T(8,128)(2,1)S(1)} %get-tuple-element.11), channel_id=1, source_target_pairs={{0,4},{2,6},{4,8},{6,10},{8,12},{10,14},{1,5},{3,7},{5,9},{7,11},{... | collective-permute-start | bytes 1572872 | tf_op jit(solution)/shard_map/ppermute | solution.py:17
  91.0 10.9 %collective-permute-start.13 = (bf16[1,40,1024]{2,1,0:T(8,128)(2,1)S(1)}, bf16[1,40,1024]{2,1,0:T(8,128)(2,1)S(1)}, u32[]{:S(2)}, u32[]{:S(2)}) collective-permute-start(bf16[1,40,1024]{2,1,0:T(8,128)(2,1)S(1)} %dynamic-slice_convert_fusion.2), channel_id=1, source_target_pairs={{0,8},{2,10},{4,12},{6,14},{8,0},{10,2},{12,4},{14,6},{1,9},{3,11}... | collective-permute-start | bytes 245768 | tf_op jit(solution)/shard_map/ppermute | solution.py:66
  101.8 6.4 %collective-permute-start.14 = (bf16[1,40,1024]{2,1,0:T(8,128)(2,1)S(1)}, bf16[1,40,1024]{2,1,0:T(8,128)(2,1)S(1)}, u32[]{:S(2)}, u32[]{:S(2)}) collective-permute-start(bf16[1,40,1024]{2,1,0:T(8,128)(2,1)S(1)} %add_convert_fusion.1), channel_id=1, source_target_pairs={{0,8},{2,10},{4,12},{6,14},{8,0},{10,2},{12,4},{14,6},{1,9},{3,11}... | collective-permute-start | bytes 245768 | tf_op jit(solution)/shard_map/ppermute | solution.py:66
  108.3 6.9 %collective-permute-start.15 = (bf16[2,40,1024]{2,1,0:T(8,128)(2,1)S(1)}, bf16[2,40,1024]{2,1,0:T(8,128)(2,1)S(1)}, u32[]{:S(2)}, u32[]{:S(2)}) collective-permute-start(bf16[2,40,1024]{2,1,0:T(8,128)(2,1)S(1)} %pad_maximum_fusion.9), channel_id=1, source_target_pairs={{0,4},{2,6},{4,0},{6,2},{8,12},{10,14},{12,8},{14,10},{1,5},{3,7},... | collective-permute-start | bytes 491528 | tf_op jit(solution)/shard_map/ppermute | solution.py:66
  115.3 13.0 %collective-permute-start.16 = (bf16[4,40,1024]{2,1,0:T(8,128)(2,1)S(1)}, bf16[4,40,1024]{2,1,0:T(8,128)(2,1)S(1)}, u32[]{:S(2)}, u32[]{:S(2)}) collective-permute-start(bf16[4,40,1024]{2,1,0:T(8,128)(2,1)S(1)} %pad_maximum_fusion.5), channel_id=1, source_target_pairs={{0,2},{2,0},{4,6},{6,4},{8,10},{10,8},{12,14},{14,12},{1,3},{3,1},... | collective-permute-start | bytes 983048 | tf_op jit(solution)/shard_map/ppermute | solution.py:66
  117.5 11.7 %collective-permute-start.9 = (bf16[2,128,512]{2,1,0:T(8,128)(2,1)S(1)}, bf16[2,128,512]{2,1,0:T(8,128)(2,1)S(1)}, u32[]{:S(2)}, u32[]{:S(2)}) collective-permute-start(bf16[2,128,512]{2,1,0:T(8,128)(2,1)S(1)} %fusion.10), channel_id=1, source_target_pairs={{2,0},{4,2},{6,4},{8,6},{10,8},{12,10},{14,12},{3,1},{5,3},{7,5},{... | collective-permute-start | bytes 786440 | tf_op jit(solution)/shard_map/ppermute | solution.py:17
  119.7 11.4 %collective-permute-start.8 = (bf16[2,128,512]{2,1,0:T(8,128)(2,1)S(1)}, bf16[2,128,512]{2,1,0:T(8,128)(2,1)S(1)}, u32[]{:S(2)}, u32[]{:S(2)}) collective-permute-start(bf16[2,128,512]{2,1,0:T(8,128)(2,1)S(1)} %fusion.12), channel_id=1, source_target_pairs={{0,2},{2,4},{4,6},{6,8},{8,10},{10,12},{12,14},{1,3},{3,5},{5,7},{... | collective-permute-start | bytes 786440 | tf_op jit(solution)/shard_map/ppermute | solution.py:17
  128.4 3.7 %collective-permute-start.17 = (bf16[1,8,40,1024]{3,2,1,0:T(8,128)(2,1)S(1)}, bf16[1,8,40,1024]{3,2,1,0:T(8,128)(2,1)S(1)}, u32[]{:S(2)}, u32[]{:S(2)}) collective-permute-start(bf16[1,8,40,1024]{3,2,1,0:T(8,128)(2,1)S(1)} %maximum_bitcast_fusion), channel_id=1, source_target_pairs={{0,1},{1,0},{2,3},{3,2},{4,5},{5,4},{6,7},{7,6},{8,9},{9,8},{10,11... | collective-permute-start | bytes 1966088 | tf_op jit(solution)/shard_map/ppermute | solution.py:66

commit v23 on v21

--- a/solution.py
+++ b/solution.py
@@ -198,7 +198,7 @@
     dp_count = lax.axis_size("dp")
     members = ctx_count * dp_count
     proj_rows = proj_local.shape[0] // members
-    kernel_rows = -(-KW // (members * 8)) * 8
+    kernel_rows = -(-KW // (members * 16)) * 16
     kernel_padded = jnp.pad(kernel_local, ((0, kernel_rows * members - KW), (0, 0)))
     stacked = jnp.concatenate(
         [

time: 130 us -> 137 us (1.054)
  waiting for transfers between devices: 53.8 us -> 57.7 us
    ppermute x8, waiting for transfers between devices: 16.3 us -> 20.9 us  [exchange(): return lax.ppermute(block, axis, [(i, i ^ bit) for i in range(count)])]
    unnamed x40 -> x44, local copies, waits for them, and re-layouts: 1.94 us -> 3.27 us
  transfers between devices with their start and end apart: 18 -> 18, of which waited for: 13 -> 13; matrix products, arithmetic and copies ran while one was open for 8% -> 7% of each run, Pallas kernels for 0% -> 0%
where the time goes in v23:
time: 137 us; the launch traced here: 136 us
  waiting for transfers between devices  57.7 us (42%)
  starting transfers between devices  42.2 us (31%)
  other arithmetic  15 us (11%)
  matrix products  11.4 us (8%)
  local copies, waits for them, and re-layouts  7.33 us (5%)
  between operations  2.11 us (2%)
    ppermute x8, waiting for transfers between devices, passed_along(): return lax.ppermute(block, axis, route)  35.3 us
    ppermute x8, starting transfers between devices, passed_along(): return lax.ppermute(block, axis, route)  24.3 us
    ppermute x8, waiting for transfers between devices, exchange(): return lax.ppermute(block, axis, [(i, i ^ bit) for i in range(count)])  20.9 us
    ppermute x8, starting transfers between devices, exchange(): return lax.ppermute(block, axis, [(i, i ^ bit) for i in range(count)])  11 us
    dot_general x6, matrix products, contract(): lax.dot_general(lhs, rhs, (((lhs_dim,), (rhs_dim,)), ((), ())), preferred...  7.12 us
    ppermute x1, starting transfers between devices, padded(): lax.ppermute(tail, axis, [(i, (i + 1) % count) for i in range(ends)])  5 us
    unnamed x44, local copies, waits for them, and re-layouts  3.27 us
    convert_element_type x1, other arithmetic, on_device(): grad_conv = (cot_wide.astype(jnp.float32) * (sigmoid_c + conv_out * sigmo...  2.96 us
  transfers between devices with their start and end apart: 18, of which 13 were waited for; matrix products, arithmetic and copies ran while one was open for 7% of the time, Pallas kernels for 0%

profile of v23, /device:TPU:2, one launch (start us, length us, event | category | flops | bytes accessed | tf_op | source)
XLA Modules:
  0.0 135.7 jit_solution(6839436788583637812)
XLA Ops:
  0.6 0.9 fusion.44
  1.5 0.9 constant_dynamic-update-slice_fusion.1
  2.5 1.0 constant_dynamic-update-slice_fusion
  3.5 1.9 %collective-permute-start.2 = (bf16[288,512]{1,0:T(8,128)(2,1)S(1)}, bf16[288,512]{1,0:T(8,128)(2,1)S(1)}, u32[]{:S(2)}, u32[]{:S(2)}) collective-permute-start(bf16[288,512]{1,0:T(8,128)(2,1)S(1)} %get-tuple-element.33), channel_id=1, source_target_pairs={{2,0},{4,2},{6,4},{8,6},{10,8},{12,10},{14,12},{3,1},{5,3},{7,5},{... | collective-permute-start | bytes 884744 | tf_op jit(solution)/shard_map/ppermute | solution.py:17
  5.4 4.8 %collective-permute-start = (bf16[288,512]{1,0:T(8,128)(2,1)S(1)}, bf16[288,512]{1,0:T(8,128)(2,1)S(1)}, u32[]{:S(2)}, u32[]{:S(2)}) collective-permute-start(bf16[288,512]{1,0:T(8,128)(2,1)S(1)} %get-tuple-element.34), channel_id=1, source_target_pairs={{0,2},{2,4},{4,6},{6,8},{8,10},{10,12},{12,14},{1,3},{3,5},{5,7},{... | collective-permute-start | bytes 884744 | tf_op jit(solution)/shard_map/ppermute | solution.py:17
  11.0 4.2 %collective-permute-done.2 = bf16[288,512]{1,0:T(8,128)(2,1)S(1)} collective-permute-done((bf16[288,512]{1,0:T(8,128)(2,1)S(1)}, bf16[288,512]{1,0:T(8,128)(2,1)S(1)}, u32[]{:S(2)}, u32[]{:S(2)}) %collective-permute-start.2) | collective-permute-done | bytes 294944 | tf_op jit(solution)/shard_map/ppermute | solution.py:17
  15.2 6.2 %collective-permute-done = bf16[288,512]{1,0:T(8,128)(2,1)S(1)} collective-permute-done((bf16[288,512]{1,0:T(8,128)(2,1)S(1)}, bf16[288,512]{1,0:T(8,128)(2,1)S(1)}, u32[]{:S(2)}, u32[]{:S(2)}) %collective-permute-start) | collective-permute-done | bytes 294944 | tf_op jit(solution)/shard_map/ppermute | solution.py:17
  21.5 3.5 %collective-permute-start.1 = (bf16[2,2,128,512]{3,2,1,0:T(8,128)(2,1)S(1)}, bf16[2,2,128,512]{3,2,1,0:T(8,128)(2,1)S(1)}, u32[]{:S(2)}, u32[]{:S(2)}) collective-permute-start(bf16[2,2,128,512]{3,2,1,0:T(8,128)(2,1)S(1)} %get-tuple-element.32), channel_id=1, source_target_pairs={{0,4},{2,6},{4,8},{6,10},{8,12},{10,14},{1,5},{3,7},{5,9},{7,11},{... | collective-permute-start | bytes 1572872 | tf_op jit(solution)/shard_map/ppermute | solution.py:17
  25.2 1.3 collective-permute-start.3
  26.5 9.8 %collective-permute-done.1 = bf16[2,2,128,512]{3,2,1,0:T(8,128)(2,1)S(1)} collective-permute-done((bf16[2,2,128,512]{3,2,1,0:T(8,128)(2,1)S(1)}, bf16[2,2,128,512]{3,2,1,0:T(8,128)(2,1)S(1)}, u32[]{:S(2)}, u32[]{:S(2)}) %collective-permute-start.1) | collective-permute-done | bytes 524320 | tf_op jit(solution)/shard_map/ppermute | solution.py:17
  36.5 4.2 %collective-permute-done.3 = bf16[2,2,128,512]{3,2,1,0:T(8,128)(2,1)S(1)} collective-permute-done((bf16[2,2,128,512]{3,2,1,0:T(8,128)(2,1)S(1)}, bf16[2,2,128,512]{3,2,1,0:T(8,128)(2,1)S(1)}, u32[]{:S(2)}, u32[]{:S(2)}) %collective-permute-start.3) | collective-permute-done | bytes 524320 | tf_op jit(solution)/shard_map/ppermute | solution.py:17
  40.8 1.2 fusion
  42.0 0.8 exponential_reduce_fusion
  43.5 1.3 fusion.49
  45.5 1.9 %collective-permute-start.5 = (bf16[32,1024]{1,0:T(8,128)(2,1)S(1)}, bf16[32,1024]{1,0:T(8,128)(2,1)S(1)}, u32[]{:S(2)}, u32[]{:S(2)}) collective-permute-start(bf16[32,1024]{1,0:T(8,128)(2,1)S(1)} %get-tuple-element.30), channel_id=1, source_target_pairs={{2,0},{4,2},{6,4},{8,6},{10,8},{12,10},{14,12},{3,1},{5,3},{7,5},{... | collective-permute-start | bytes 196616 | tf_op jit(solution)/shard_map/ppermute | solution.py:30
  47.4 5.0 %collective-permute-start.4 = (bf16[32,1024]{1,0:T(8,128)(2,1)S(1)}, bf16[32,1024]{1,0:T(8,128)(2,1)S(1)}, u32[]{:S(2)}, u32[]{:S(2)}) collective-permute-start(bf16[32,1024]{1,0:T(8,128)(2,1)S(1)} %get-tuple-element.29), channel_id=1, source_target_pairs={{0,2},{2,4},{4,6},{6,8},{8,10},{10,12},{12,14},{1,3},{3,5},{5,7},{... | collective-permute-start | bytes 196616 | tf_op jit(solution)/shard_map/ppermute | solution.py:28
  52.5 1.6 %collective-permute-done.4 = bf16[32,1024]{1,0:T(8,128)(2,1)S(1)} collective-permute-done((bf16[32,1024]{1,0:T(8,128)(2,1)S(1)}, bf16[32,1024]{1,0:T(8,128)(2,1)S(1)}, u32[]{:S(2)}, u32[]{:S(2)}) %collective-permute-start.4) | collective-permute-done | bytes 65568 | tf_op jit(solution)/shard_map/ppermute | solution.py:28
  54.2 3.0 %multiply_convert_fusion.1 = bf16[160,1024]{1,0:T(8,128)(2,1)S(1)} fusion(bf16[192,1024]{1,0:T(8,128)(2,1)S(1)} %pad_maximum_fusion.6, bf16[16,1024]{1,0:T(8,128)(2,1)S(1)} %reshape.178, bf16[128,1024]{1,0:T(8,128)(2,1)S(1)} %bitcast.163, bf16[16,1024]{1,0:T(8,128)(2,1)S(1)} %reshape.177, f32[1024]{0:T(1024)S(1)} %bitcast.234, f32[1024]{0:T(1024)S(1)} %bitcast.236, ...), kind=kLoop, calls=%fused_computation.33 | loop fusion | flops 17530880 | bytes 10940416 | tf_op jit(solution)/shard_map/convert_element_type | solution.py:175
  57.2 2.3 %add_convert_fusion = bf16[128,1024]{1,0:T(8,128)(2,1)S(1)} fusion(bf16[160,1024]{1,0:T(8,128)(2,1)S(1)} %multiply_convert_fusion.1, f32[1024]{0:T(1024)S(1)} %bitcast.235, f32[1024]{0:T(1024)S(1)} %bitcast.237, f32[1024]{0:T(1024)S(1)} %bitcast.179, f32[1024]{0:T(1024)S(1)} %bitcast.181, f32[1024]{0:T(1024)S(1)} %bitcast.183, f32[1024]{0:T(1024)S(1)} %bitcast.185, ...), kind=kLoop, calls=%fused_computation.55 | loop fusion | flops 12582912 | bytes 8777856 | tf_op jit(solution)/shard_map/convert_element_type | solution.py:193
  60.0 2.4 %fusion.7 = f32[1,31,1024]{2,0,1:T(1,128)S(1)} fusion(bf16[1,158,1024]{2,1,0:T(8,128)(2,1)S(1)} %slice_bitcast_fusion, bf16[128,1,1024]{2,0,1:T(8,128)(2,1)S(1)} %slice_bitcast_fusion.1), kind=kOutput, calls=%fused_computation.34 | convolution fusion | flops 8126464 | bytes 712704 | tf_op jit(solution)/shard_map/conv_general_dilated | solution.py:182
  62.5 1.0 copy-done.1
  63.5 1.0 fusion.2
  64.5 2.6 %collective-permute-done.10 = bf16[1,8,48,1024]{3,2,1,0:T(8,128)(2,1)} collective-permute-done((bf16[1,8,48,1024]{3,2,1,0:T(8,128)(2,1)}, bf16[1,8,48,1024]{3,2,1,0:T(8,128)(2,1)}, u32[]{:S(2)}, u32[]{:S(2)}) %collective-permute-start.10) | collective-permute-done | bytes 786464 | tf_op jit(solution)/shard_map/ppermute | solution.py:66
  67.1 1.5 %fusion.4 = f32[1,8,48,1024]{3,2,1,0:T(8,128)S(1)} fusion(s32[]{:T(128)S(6)} %select_n.165, f32[2,8,32,1024]{3,2,1,0:T(8,128)S(1)} %bitcast.152, f32[2,8,16,1024]{3,2,1,0:T(8,128)} %bitcast.154, bf16[1,8,48,1024]{3,2,1,0:T(8,128)(2,1)} %collective-permute-done.10), kind=kLoop, calls=%fused_computation.18 | loop fusion | flops 1179648 | bytes 5505028 | tf_op jit(solution)/shard_map/add | solution.py:78
  68.6 1.2 copy-done.2
  70.6 1.1 convert_multiply_fusion
  71.9 10.1 %collective-permute-done.11 = bf16[4,48,1024]{2,1,0:T(8,128)(2,1)} collective-permute-done((bf16[4,48,1024]{2,1,0:T(8,128)(2,1)}, bf16[4,48,1024]{2,1,0:T(8,128)(2,1)}, u32[]{:S(2)}, u32[]{:S(2)}) %collective-permute-start.11) | collective-permute-done | bytes 393248 | tf_op jit(solution)/shard_map/ppermute | solution.py:66
  82.1 1.1 bitcast_add_fusion
  83.2 2.1 %collective-permute-start.12 = (bf16[2,48,1024]{2,1,0:T(8,128)(2,1)S(1)}, bf16[2,48,1024]{2,1,0:T(8,128)(2,1)S(1)}, u32[]{:S(2)}, u32[]{:S(2)}) collective-permute-start(bf16[2,48,1024]{2,1,0:T(8,128)(2,1)S(1)} %dynamic-slice_convert_fusion.1), channel_id=1, source_target_pairs={{0,4},{2,6},{4,0},{6,2},{8,12},{10,14},{12,8},{14,10},{1,5},{3,7},... | collective-permute-start | bytes 589832 | tf_op jit(solution)/shard_map/ppermute | solution.py:66
  85.4 4.5 %collective-permute-done.12 = bf16[2,48,1024]{2,1,0:T(8,128)(2,1)S(1)} collective-permute-done((bf16[2,48,1024]{2,1,0:T(8,128)(2,1)S(1)}, bf16[2,48,1024]{2,1,0:T(8,128)(2,1)S(1)}, u32[]{:S(2)}, u32[]{:S(2)}) %collective-permute-start.12) | collective-permute-done | bytes 196640 | tf_op jit(solution)/shard_map/ppermute | solution.py:66
  90.1 2.8 %collective-permute-start.13 = (bf16[1,48,1024]{2,1,0:T(8,128)(2,1)S(1)}, bf16[1,48,1024]{2,1,0:T(8,128)(2,1)S(1)}, u32[]{:S(2)}, u32[]{:S(2)}) collective-permute-start(bf16[1,48,1024]{2,1,0:T(8,128)(2,1)S(1)} %dynamic-slice_convert_fusion.2), channel_id=1, source_target_pairs={{0,8},{2,10},{4,12},{6,14},{8,0},{10,2},{12,4},{14,6},{1,9},{3,11}... | collective-permute-start | bytes 294920 | tf_op jit(solution)/shard_map/ppermute | solution.py:66
  92.8 1.1 multiply_convert_fusion
  94.0 1.8 %collective-permute-done.13 = bf16[1,48,1024]{2,1,0:T(8,128)(2,1)S(1)} collective-permute-done((bf16[1,48,1024]{2,1,0:T(8,128)(2,1)S(1)}, bf16[1,48,1024]{2,1,0:T(8,128)(2,1)S(1)}, u32[]{:S(2)}, u32[]{:S(2)}) %collective-permute-start.13) | collective-permute-done | bytes 98336 | tf_op jit(solution)/shard_map/ppermute | solution.py:66
  95.8 2.7 %collective-permute-start.14 = (bf16[1,48,1024]{2,1,0:T(8,128)(2,1)S(1)}, bf16[1,48,1024]{2,1,0:T(8,128)(2,1)S(1)}, u32[]{:S(2)}, u32[]{:S(2)}) collective-permute-start(bf16[1,48,1024]{2,1,0:T(8,128)(2,1)S(1)} %add_convert_fusion.1), channel_id=1, source_target_pairs={{0,8},{2,10},{4,12},{6,14},{8,0},{10,2},{12,4},{14,6},{1,9},{3,11}... | collective-permute-start | bytes 294920 | tf_op jit(solution)/shard_map/ppermute | solution.py:66
  98.5 1.1 fusion.47
  99.6 1.8 %collective-permute-done.14 = bf16[1,48,1024]{2,1,0:T(8,128)(2,1)S(1)} collective-permute-done((bf16[1,48,1024]{2,1,0:T(8,128)(2,1)S(1)}, bf16[1,48,1024]{2,1,0:T(8,128)(2,1)S(1)}, u32[]{:S(2)}, u32[]{:S(2)}) %collective-permute-start.14) | collective-permute-done | bytes 98336 | tf_op jit(solution)/shard_map/ppermute | solution.py:66
  101.4 1.7 %collective-permute-start.15 = (bf16[2,48,1024]{2,1,0:T(8,128)(2,1)S(1)}, bf16[2,48,1024]{2,1,0:T(8,128)(2,1)S(1)}, u32[]{:S(2)}, u32[]{:S(2)}) collective-permute-start(bf16[2,48,1024]{2,1,0:T(8,128)(2,1)S(1)} %pad_maximum_fusion.10), channel_id=1, source_target_pairs={{0,4},{2,6},{4,0},{6,2},{8,12},{10,14},{12,8},{14,10},{1,5},{3,7},... | collective-permute-start | bytes 589832 | tf_op jit(solution)/shard_map/ppermute | solution.py:66
  103.1 1.1 fusion.48
  104.3 1.4 %collective-permute-start.7 = (bf16[2,2,128,512]{3,2,1,0:T(8,128)(2,1)S(1)}, bf16[2,2,128,512]{3,2,1,0:T(8,128)(2,1)S(1)}, u32[]{:S(2)}, u32[]{:S(2)}) collective-permute-start(bf16[2,2,128,512]{3,2,1,0:T(8,128)(2,1)S(1)} %get-tuple-element.6), channel_id=1, source_target_pairs={{4,0},{6,2},{8,4},{10,6},{12,8},{14,10},{5,1},{7,3},{9,5},{11,7},{... | collective-permute-start | bytes 1572872 | tf_op jit(solution)/shard_map/ppermute | solution.py:17
  105.8 4.6 %collective-permute-start.6 = (bf16[2,2,128,512]{3,2,1,0:T(8,128)(2,1)S(1)}, bf16[2,2,128,512]{3,2,1,0:T(8,128)(2,1)S(1)}, u32[]{:S(2)}, u32[]{:S(2)}) collective-permute-start(bf16[2,2,128,512]{3,2,1,0:T(8,128)(2,1)S(1)} %get-tuple-element.5), channel_id=1, source_target_pairs={{0,4},{2,6},{4,8},{6,10},{8,12},{10,14},{1,5},{3,7},{5,9},{7,11},{... | collective-permute-start | bytes 1572872 | tf_op jit(solution)/shard_map/ppermute | solution.py:17
  110.5 1.6 %collective-permute-start.16 = (bf16[4,48,1024]{2,1,0:T(8,128)(2,1)S(1)}, bf16[4,48,1024]{2,1,0:T(8,128)(2,1)S(1)}, u32[]{:S(2)}, u32[]{:S(2)}) collective-permute-start(bf16[4,48,1024]{2,1,0:T(8,128)(2,1)S(1)} %pad_maximum_fusion.7), channel_id=1, source_target_pairs={{0,2},{2,0},{4,6},{6,4},{8,10},{10,8},{12,14},{14,12},{1,3},{3,1},... | collective-permute-start | bytes 1179656 | tf_op jit(solution)/shard_map/ppermute | solution.py:66
  112.1 1.3 fusion.50
  113.5 4.9 %collective-permute-done.7 = bf16[2,2,128,512]{3,2,1,0:T(8,128)(2,1)S(1)} collective-permute-done((bf16[2,2,128,512]{3,2,1,0:T(8,128)(2,1)S(1)}, bf16[2,2,128,512]{3,2,1,0:T(8,128)(2,1)S(1)}, u32[]{:S(2)}, u32[]{:S(2)}) %collective-permute-start.7) | collective-permute-done | bytes 524320 | tf_op jit(solution)/shard_map/ppermute | solution.py:17
  118.9 3.3 %collective-permute-start.9 = (bf16[2,128,512]{2,1,0:T(8,128)(2,1)S(1)}, bf16[2,128,512]{2,1,0:T(8,128)(2,1)S(1)}, u32[]{:S(2)}, u32[]{:S(2)}) collective-permute-start(bf16[2,128,512]{2,1,0:T(8,128)(2,1)S(1)} %get-tuple-element.10), channel_id=1, source_target_pairs={{2,0},{4,2},{6,4},{8,6},{10,8},{12,10},{14,12},{3,1},{5,3},{7,5},{... | collective-permute-start | bytes 786440 | tf_op jit(solution)/shard_map/ppermute | solution.py:17
  122.2 3.5 %collective-permute-start.8 = (bf16[2,128,512]{2,1,0:T(8,128)(2,1)S(1)}, bf16[2,128,512]{2,1,0:T(8,128)(2,1)S(1)}, u32[]{:S(2)}, u32[]{:S(2)}) collective-permute-start(bf16[2,128,512]{2,1,0:T(8,128)(2,1)S(1)} %get-tuple-element.9), channel_id=1, source_target_pairs={{0,2},{2,4},{4,6},{6,8},{8,10},{10,12},{12,14},{1,3},{3,5},{5,7},{... | collective-permute-start | bytes 786440 | tf_op jit(solution)/shard_map/ppermute | solution.py:17
  126.9 1.3 collective-permute-done.9
  128.3 4.6 %collective-permute-done.8 = bf16[2,128,512]{2,1,0:T(8,128)(2,1)S(1)} collective-permute-done((bf16[2,128,512]{2,1,0:T(8,128)(2,1)S(1)}, bf16[2,128,512]{2,1,0:T(8,128)(2,1)S(1)}, u32[]{:S(2)}, u32[]{:S(2)}) %collective-permute-start.8) | collective-permute-done | bytes 262176 | tf_op jit(solution)/shard_map/ppermute | solution.py:17
  133.9 1.1 fusion.6
  (104 shorter events, 7.6 us)
Async XLA Ops:
  0.6 44.5 %copy-start = (bf16[512,1024]{1,0:T(8,128)(2,1)S(1)}, bf16[512,1024]{1,0:T(8,128)(2,1)}, u32[]{:S(2)}) copy-start(bf16[512,1024]{1,0:T(8,128)(2,1)} %param.11) | copy-start | bytes 3145732
  2.5 22.6 %copy-start.13 = (f32[31,1024]{1,0:T(8,128)S(1)}, f32[31,1024]{1,0:T(8,128)}, u32[]{:S(2)}) copy-start(f32[31,1024]{1,0:T(8,128)} %param.12) | copy-start | bytes 380932
  2.5 22.6 %copy-start.12 = (bf16[1,128,512]{2,1,0:T(8,128)(2,1)S(1)}, bf16[1,128,512]{2,1,0:T(8,128)(2,1)}, u32[]{:S(2)}) copy-start(bf16[1,128,512]{2,1,0:T(8,128)(2,1)} %param.7) | copy-start | bytes 393220
  3.5 11.6 %collective-permute-start.2 = (bf16[288,512]{1,0:T(8,128)(2,1)S(1)}, bf16[288,512]{1,0:T(8,128)(2,1)S(1)}, u32[]{:S(2)}, u32[]{:S(2)}) collective-permute-start(bf16[288,512]{1,0:T(8,128)(2,1)S(1)} %get-tuple-element.33), channel_id=1, source_target_pairs={{2,0},{4,2},{6,4},{8,6},{10,8},{12,10},{14,12},{3,1},{5,3},{7,5},{... | collective-permute-start | bytes 884744 | tf_op jit(solution)/shard_map/ppermute | solution.py:17
  5.4 15.9 %collective-permute-start = (bf16[288,512]{1,0:T(8,128)(2,1)S(1)}, bf16[288,512]{1,0:T(8,128)(2,1)S(1)}, u32[]{:S(2)}, u32[]{:S(2)}) collective-permute-start(bf16[288,512]{1,0:T(8,128)(2,1)S(1)} %get-tuple-element.34), channel_id=1, source_target_pairs={{0,2},{2,4},{4,6},{6,8},{8,10},{10,12},{12,14},{1,3},{3,5},{5,7},{... | collective-permute-start | bytes 884744 | tf_op jit(solution)/shard_map/ppermute | solution.py:17
  21.4 15.0 %copy-start.10 = (bf16[1,128,512]{2,1,0:T(8,128)(2,1)S(1)}, bf16[1,128,512]{2,1,0:T(8,128)(2,1)}, u32[]{:S(2)}) copy-start(bf16[1,128,512]{2,1,0:T(8,128)(2,1)} %param.8) | copy-start | bytes 393220
  21.4 15.0 %copy-start.11 = (bf16[1,128,512]{2,1,0:T(8,128)(2,1)S(1)}, bf16[1,128,512]{2,1,0:T(8,128)(2,1)}, u32[]{:S(2)}) copy-start(bf16[1,128,512]{2,1,0:T(8,128)(2,1)} %param.9) | copy-start | bytes 393220
  21.5 14.8 %collective-permute-start.1 = (bf16[2,2,128,512]{3,2,1,0:T(8,128)(2,1)S(1)}, bf16[2,2,128,512]{3,2,1,0:T(8,128)(2,1)S(1)}, u32[]{:S(2)}, u32[]{:S(2)}) collective-permute-start(bf16[2,2,128,512]{3,2,1,0:T(8,128)(2,1)S(1)} %get-tuple-element.32), channel_id=1, source_target_pairs={{0,4},{2,6},{4,8},{6,10},{8,12},{10,14},{1,5},{3,7},{5,9},{7,11},{... | collective-permute-start | bytes 1572872 | tf_op jit(solution)/shard_map/ppermute | solution.py:17
  25.2 16.7 %copy-start.7 = (bf16[8,128,512]{2,1,0:T(8,128)(2,1)}, bf16[8,128,512]{2,1,0:T(8,128)(2,1)S(1)}, u32[]{:S(2)}) copy-start(bf16[8,128,512]{2,1,0:T(8,128)(2,1)S(1)} %broadcast_select_fusion.1) | copy-start | bytes 3145732
  25.2 15.5 %collective-permute-start.3 = (bf16[2,2,128,512]{3,2,1,0:T(8,128)(2,1)S(1)}, bf16[2,2,128,512]{3,2,1,0:T(8,128)(2,1)S(1)}, u32[]{:S(2)}, u32[]{:S(2)}) collective-permute-start(bf16[2,2,128,512]{3,2,1,0:T(8,128)(2,1)S(1)} %get-tuple-element.31), channel_id=1, source_target_pairs={{4,0},{6,2},{8,4},{10,6},{12,8},{14,10},{5,1},{7,3},{9,5},{11,7},{... | collective-permute-start | bytes 1572872 | tf_op jit(solution)/shard_map/ppermute | solution.py:17
  40.7 1.2 copy-start.16
  40.8 2.8 %copy-start.14 = (bf16[896,512]{1,0:T(8,128)(2,1)}, bf16[896,512]{1,0:T(8,128)(2,1)S(1)}, u32[]{:S(2)}) copy-start(bf16[896,512]{1,0:T(8,128)(2,1)S(1)} %get-tuple-element.13) | copy-start | bytes 2752516
  43.5 1.3 copy-start.4
  45.1 9.1 %copy-start.6 = (bf16[1,128,1024]{2,1,0:T(8,128)(2,1)S(1)}, bf16[1,128,1024]{2,1,0:T(8,128)(2,1)}, u32[]{:S(2)}) copy-start(bf16[1,128,1024]{2,1,0:T(8,128)(2,1)} %param.10) | copy-start | bytes 786436
  45.5 7.1 %collective-permute-start.5 = (bf16[32,1024]{1,0:T(8,128)(2,1)S(1)}, bf16[32,1024]{1,0:T(8,128)(2,1)S(1)}, u32[]{:S(2)}, u32[]{:S(2)}) collective-permute-start(bf16[32,1024]{1,0:T(8,128)(2,1)S(1)} %get-tuple-element.30), channel_id=1, source_target_pairs={{2,0},{4,2},{6,4},{8,6},{10,8},{12,10},{14,12},{3,1},{5,3},{7,5},{... | collective-permute-start | bytes 196616 | tf_op jit(solution)/shard_map/ppermute | solution.py:30
  47.4 6.7 %collective-permute-start.4 = (bf16[32,1024]{1,0:T(8,128)(2,1)S(1)}, bf16[32,1024]{1,0:T(8,128)(2,1)S(1)}, u32[]{:S(2)}, u32[]{:S(2)}) collective-permute-start(bf16[32,1024]{1,0:T(8,128)(2,1)S(1)} %get-tuple-element.29), channel_id=1, source_target_pairs={{0,2},{2,4},{4,6},{6,8},{8,10},{10,12},{12,14},{1,3},{3,5},{5,7},{... | collective-permute-start | bytes 196616 | tf_op jit(solution)/shard_map/ppermute | solution.py:28
  62.5 1.0 copy-start.1
  64.5 2.6 %collective-permute-start.10 = (bf16[1,8,48,1024]{3,2,1,0:T(8,128)(2,1)}, bf16[1,8,48,1024]{3,2,1,0:T(8,128)(2,1)}, u32[]{:S(2)}, u32[]{:S(2)}) collective-permute-start(bf16[1,8,48,1024]{3,2,1,0:T(8,128)(2,1)} %fusion.2), channel_id=1, source_target_pairs={{0,1},{1,0},{2,3},{3,2},{4,5},{5,4},{6,7},{7,6},{8,9},{9,8},{10,11... | collective-permute-start | bytes 2359304 | tf_op jit(solution)/shard_map/ppermute | solution.py:66
  68.6 1.2 copy-start.2
  70.6 11.5 %copy-start.3 = (f32[1,8,48,1024]{3,2,1,0:T(8,128)S(1)}, f32[1,8,48,1024]{3,2,1,0:T(8,128)}, u32[]{:S(2)}) copy-start(f32[1,8,48,1024]{3,2,1,0:T(8,128)} %copy-done.2) | copy-start | bytes 4718596
  70.6 11.5 %collective-permute-start.11 = (bf16[4,48,1024]{2,1,0:T(8,128)(2,1)}, bf16[4,48,1024]{2,1,0:T(8,128)(2,1)}, u32[]{:S(2)}, u32[]{:S(2)}) collective-permute-start(bf16[4,48,1024]{2,1,0:T(8,128)(2,1)} %fusion.21), channel_id=1, source_target_pairs={{0,2},{2,0},{4,6},{6,4},{8,10},{10,8},{12,14},{14,12},{1,3},{3,1},... | collective-permute-start | bytes 1179656 | tf_op jit(solution)/shard_map/ppermute | solution.py:66
  71.7 13.6 %copy-start.9 = (bf16[128,512]{1,0:T(8,128)(2,1)S(1)}, bf16[128,512]{1,0:T(8,128)(2,1)}, u32[]{:S(2)}) copy-start(bf16[128,512]{1,0:T(8,128)(2,1)} %get-tuple-element.73) | copy-start | bytes 393220
  71.9 21.0 %copy-start.5 = (bf16[1024,896]{0,1:T(8,128)(2,1)S(1)}, bf16[1024,896]{0,1:T(8,128)(2,1)}, u32[]{:S(2)}) copy-start(bf16[1024,896]{0,1:T(8,128)(2,1)} %copy-done.4) | copy-start | bytes 5505028
  71.9 20.9 %copy-start.15 = (bf16[896,512]{1,0:T(8,128)(2,1)S(1)}, bf16[896,512]{1,0:T(8,128)(2,1)}, u32[]{:S(2)}) copy-start(bf16[896,512]{1,0:T(8,128)(2,1)} %copy-done.14) | copy-start | bytes 2752516
  83.2 6.8 %collective-permute-start.12 = (bf16[2,48,1024]{2,1,0:T(8,128)(2,1)S(1)}, bf16[2,48,1024]{2,1,0:T(8,128)(2,1)S(1)}, u32[]{:S(2)}, u32[]{:S(2)}) collective-permute-start(bf16[2,48,1024]{2,1,0:T(8,128)(2,1)S(1)} %dynamic-slice_convert_fusion.1), channel_id=1, source_target_pairs={{0,4},{2,6},{4,0},{6,2},{8,12},{10,14},{12,8},{14,10},{1,5},{3,7},... | collective-permute-start | bytes 589832 | tf_op jit(solution)/shard_map/ppermute | solution.py:66
  90.1 5.7 %collective-permute-start.13 = (bf16[1,48,1024]{2,1,0:T(8,128)(2,1)S(1)}, bf16[1,48,1024]{2,1,0:T(8,128)(2,1)S(1)}, u32[]{:S(2)}, u32[]{:S(2)}) collective-permute-start(bf16[1,48,1024]{2,1,0:T(8,128)(2,1)S(1)} %dynamic-slice_convert_fusion.2), channel_id=1, source_target_pairs={{0,8},{2,10},{4,12},{6,14},{8,0},{10,2},{12,4},{14,6},{1,9},{3,11}... | collective-permute-start | bytes 294920 | tf_op jit(solution)/shard_map/ppermute | solution.py:66
  95.8 7.3 %copy-start.8 = (bf16[8,128,512]{2,1,0:T(8,128)(2,1)S(1)}, bf16[8,128,512]{2,1,0:T(8,128)(2,1)}, u32[]{:S(2)}) copy-start(bf16[8,128,512]{2,1,0:T(8,128)(2,1)} %copy-done.7) | copy-start | bytes 3145732
  95.8 5.6 %collective-permute-start.14 = (bf16[1,48,1024]{2,1,0:T(8,128)(2,1)S(1)}, bf16[1,48,1024]{2,1,0:T(8,128)(2,1)S(1)}, u32[]{:S(2)}, u32[]{:S(2)}) collective-permute-start(bf16[1,48,1024]{2,1,0:T(8,128)(2,1)S(1)} %add_convert_fusion.1), channel_id=1, source_target_pairs={{0,8},{2,10},{4,12},{6,14},{8,0},{10,2},{12,4},{14,6},{1,9},{3,11}... | collective-permute-start | bytes 294920 | tf_op jit(solution)/shard_map/ppermute | solution.py:66
  101.4 8.9 %collective-permute-start.15 = (bf16[2,48,1024]{2,1,0:T(8,128)(2,1)S(1)}, bf16[2,48,1024]{2,1,0:T(8,128)(2,1)S(1)}, u32[]{:S(2)}, u32[]{:S(2)}) collective-permute-start(bf16[2,48,1024]{2,1,0:T(8,128)(2,1)S(1)} %pad_maximum_fusion.10), channel_id=1, source_target_pairs={{0,4},{2,6},{4,0},{6,2},{8,12},{10,14},{12,8},{14,10},{1,5},{3,7},... | collective-permute-start | bytes 589832 | tf_op jit(solution)/shard_map/ppermute | solution.py:66
  104.2 7.8 %copy-start.17 = (bf16[896,512]{1,0:T(8,128)(2,1)S(1)}, bf16[896,512]{1,0:T(8,128)(2,1)}, u32[]{:S(2)}) copy-start(bf16[896,512]{1,0:T(8,128)(2,1)} %copy-done.16) | copy-start | bytes 2752516
  104.3 14.1 %collective-permute-start.7 = (bf16[2,2,128,512]{3,2,1,0:T(8,128)(2,1)S(1)}, bf16[2,2,128,512]{3,2,1,0:T(8,128)(2,1)S(1)}, u32[]{:S(2)}, u32[]{:S(2)}) collective-permute-start(bf16[2,2,128,512]{3,2,1,0:T(8,128)(2,1)S(1)} %get-tuple-element.6), channel_id=1, source_target_pairs={{4,0},{6,2},{8,4},{10,6},{12,8},{14,10},{5,1},{7,3},{9,5},{11,7},{... | collective-permute-start | bytes 1572872 | tf_op jit(solution)/shard_map/ppermute | solution.py:17
  105.8 12.8 %collective-permute-start.6 = (bf16[2,2,128,512]{3,2,1,0:T(8,128)(2,1)S(1)}, bf16[2,2,128,512]{3,2,1,0:T(8,128)(2,1)S(1)}, u32[]{:S(2)}, u32[]{:S(2)}) collective-permute-start(bf16[2,2,128,512]{3,2,1,0:T(8,128)(2,1)S(1)} %get-tuple-element.5), channel_id=1, source_target_pairs={{0,4},{2,6},{4,8},{6,10},{8,12},{10,14},{1,5},{3,7},{5,9},{7,11},{... | collective-permute-start | bytes 1572872 | tf_op jit(solution)/shard_map/ppermute | solution.py:17
  110.5 15.3 %collective-permute-start.16 = (bf16[4,48,1024]{2,1,0:T(8,128)(2,1)S(1)}, bf16[4,48,1024]{2,1,0:T(8,128)(2,1)S(1)}, u32[]{:S(2)}, u32[]{:S(2)}) collective-permute-start(bf16[4,48,1024]{2,1,0:T(8,128)(2,1)S(1)} %pad_maximum_fusion.7), channel_id=1, source_target_pairs={{0,2},{2,0},{4,6},{6,4},{8,10},{10,8},{12,14},{14,12},{1,3},{3,1},... | collective-permute-start | bytes 1179656 | tf_op jit(solution)/shard_map/ppermute | solution.py:66
  118.9 9.3 %collective-permute-start.9 = (bf16[2,128,512]{2,1,0:T(8,128)(2,1)S(1)}, bf16[2,128,512]{2,1,0:T(8,128)(2,1)S(1)}, u32[]{:S(2)}, u32[]{:S(2)}) collective-permute-start(bf16[2,128,512]{2,1,0:T(8,128)(2,1)S(1)} %get-tuple-element.10), channel_id=1, source_target_pairs={{2,0},{4,2},{6,4},{8,6},{10,8},{12,10},{14,12},{3,1},{5,3},{7,5},{... | collective-permute-start | bytes 786440 | tf_op jit(solution)/shard_map/ppermute | solution.py:17
  122.2 10.7 %collective-permute-start.8 = (bf16[2,128,512]{2,1,0:T(8,128)(2,1)S(1)}, bf16[2,128,512]{2,1,0:T(8,128)(2,1)S(1)}, u32[]{:S(2)}, u32[]{:S(2)}) collective-permute-start(bf16[2,128,512]{2,1,0:T(8,128)(2,1)S(1)} %get-tuple-element.9), channel_id=1, source_target_pairs={{0,2},{2,4},{4,6},{6,8},{8,10},{10,12},{12,14},{1,3},{3,5},{5,7},{... | collective-permute-start | bytes 786440 | tf_op jit(solution)/shard_map/ppermute | solution.py:17
  125.9 7.9 %collective-permute-start.17 = (bf16[1,8,48,1024]{3,2,1,0:T(8,128)(2,1)S(1)}, bf16[1,8,48,1024]{3,2,1,0:T(8,128)(2,1)S(1)}, u32[]{:S(2)}, u32[]{:S(2)}) collective-permute-start(bf16[1,8,48,1024]{3,2,1,0:T(8,128)(2,1)S(1)} %maximum_bitcast_fusion), channel_id=1, source_target_pairs={{0,1},{1,0},{2,3},{3,2},{4,5},{5,4},{6,7},{7,6},{8,9},{9,8},{10,11... | collective-permute-start | bytes 2359304 | tf_op jit(solution)/shard_map/ppermute | solution.py:66

commit v24 on v21

--- a/solution.py
+++ b/solution.py
@@ -180,14 +180,14 @@
             grad_masked + conv_kernel[tap_index] * grad_conv[start_row : start_row + tokens]
         )
     kernel_local = lax.conv_general_dilated(
-        padded_m[None, edge - halo_width : edge + tokens + halo_width],
+        padded_m[None, edge - halo_rows : edge + tokens + halo_rows],
         grad_conv[halo_rows : halo_rows + tokens, None, :],
         window_strides=(1,),
         padding="VALID",
         dimension_numbers=("NWC", "WIO", "NWC"),
         feature_group_count=channels,
         preferred_element_type=jnp.float32,
-    )[0]
+    )[0, halo_rows - halo_width : halo_rows - halo_width + KW]
     grad_hidden = (
         cot_here.astype(jnp.float32) + jnp.where(valid_rows[:, None], grad_masked, 0.0)
     ).astype(jnp.bfloat16)

time: 130 us -> 130 us (level)
    slice x0 -> x1, matrix products: none -> 2.48 us  [on_device(): lax.conv_general_dilated(padded_m[None, edge - halo_rows:edge + tokens +...]
    conv_general_dilated x1 -> x0, matrix products: 2.36 us -> none  [on_device(): lax.conv_general_dilated(padded_m[None, edge - halo_width:edge + tokens +...]
where the time goes in v24:
time: 130 us; the launch traced here: 129 us
  waiting for transfers between devices  53.8 us (41%)
  starting transfers between devices  42.1 us (32%)
  other arithmetic  13.7 us (11%)
  matrix products  11.6 us (9%)
  local copies, waits for them, and re-layouts  6.07 us (5%)
  between operations  2.14 us (2%)
    ppermute x8, waiting for transfers between devices, passed_along(): return lax.ppermute(block, axis, route)  36 us
    ppermute x8, starting transfers between devices, passed_along(): return lax.ppermute(block, axis, route)  24.2 us
    ppermute x8, waiting for transfers between devices, exchange(): return lax.ppermute(block, axis, [(i, i ^ bit) for i in range(count)])  16.3 us
    ppermute x8, starting transfers between devices, exchange(): return lax.ppermute(block, axis, [(i, i ^ bit) for i in range(count)])  11 us
    dot_general x6, matrix products, contract(): lax.dot_general(lhs, rhs, (((lhs_dim,), (rhs_dim,)), ((), ())), preferred...  7.13 us
    ppermute x1, starting transfers between devices, padded(): lax.ppermute(tail, axis, [(i, (i + 1) % count) for i in range(ends)])  5 us
    convert_element_type x1, other arithmetic, on_device(): grad_conv = (cot_wide.astype(jnp.float32) * (sigmoid_c + conv_out * sigmo...  2.96 us
  transfers between devices with their start and end apart: 18, of which 13 were waited for; matrix products, arithmetic and copies ran while one was open for 8% of the time, Pallas kernels for 0%

profile of v24, /device:TPU:2, one launch (start us, length us, event | category | flops | bytes accessed | tf_op | source)
XLA Modules:
  0.0 129.3 jit_solution(4030256006847715621)
XLA Ops:
  0.6 0.9 fusion.44
  1.5 0.9 constant_dynamic-update-slice_fusion.1
  2.5 1.0 constant_dynamic-update-slice_fusion
  3.5 1.9 %collective-permute-start.2 = (bf16[288,512]{1,0:T(8,128)(2,1)S(1)}, bf16[288,512]{1,0:T(8,128)(2,1)S(1)}, u32[]{:S(2)}, u32[]{:S(2)}) collective-permute-start(bf16[288,512]{1,0:T(8,128)(2,1)S(1)} %get-tuple-element.33), channel_id=1, source_target_pairs={{2,0},{4,2},{6,4},{8,6},{10,8},{12,10},{14,12},{3,1},{5,3},{7,5},{... | collective-permute-start | bytes 884744 | tf_op jit(solution)/shard_map/ppermute | solution.py:17
  5.4 4.8 %collective-permute-start = (bf16[288,512]{1,0:T(8,128)(2,1)S(1)}, bf16[288,512]{1,0:T(8,128)(2,1)S(1)}, u32[]{:S(2)}, u32[]{:S(2)}) collective-permute-start(bf16[288,512]{1,0:T(8,128)(2,1)S(1)} %get-tuple-element.34), channel_id=1, source_target_pairs={{0,2},{2,4},{4,6},{6,8},{8,10},{10,12},{12,14},{1,3},{3,5},{5,7},{... | collective-permute-start | bytes 884744 | tf_op jit(solution)/shard_map/ppermute | solution.py:17
  11.0 4.2 %collective-permute-done.2 = bf16[288,512]{1,0:T(8,128)(2,1)S(1)} collective-permute-done((bf16[288,512]{1,0:T(8,128)(2,1)S(1)}, bf16[288,512]{1,0:T(8,128)(2,1)S(1)}, u32[]{:S(2)}, u32[]{:S(2)}) %collective-permute-start.2) | collective-permute-done | bytes 294944 | tf_op jit(solution)/shard_map/ppermute | solution.py:17
  15.2 6.2 %collective-permute-done = bf16[288,512]{1,0:T(8,128)(2,1)S(1)} collective-permute-done((bf16[288,512]{1,0:T(8,128)(2,1)S(1)}, bf16[288,512]{1,0:T(8,128)(2,1)S(1)}, u32[]{:S(2)}, u32[]{:S(2)}) %collective-permute-start) | collective-permute-done | bytes 294944 | tf_op jit(solution)/shard_map/ppermute | solution.py:17
  21.5 3.5 %collective-permute-start.1 = (bf16[2,2,128,512]{3,2,1,0:T(8,128)(2,1)S(1)}, bf16[2,2,128,512]{3,2,1,0:T(8,128)(2,1)S(1)}, u32[]{:S(2)}, u32[]{:S(2)}) collective-permute-start(bf16[2,2,128,512]{3,2,1,0:T(8,128)(2,1)S(1)} %get-tuple-element.32), channel_id=1, source_target_pairs={{0,4},{2,6},{4,8},{6,10},{8,12},{10,14},{1,5},{3,7},{5,9},{7,11},{... | collective-permute-start | bytes 1572872 | tf_op jit(solution)/shard_map/ppermute | solution.py:17
  25.2 1.3 collective-permute-start.3
  26.5 9.8 %collective-permute-done.1 = bf16[2,2,128,512]{3,2,1,0:T(8,128)(2,1)S(1)} collective-permute-done((bf16[2,2,128,512]{3,2,1,0:T(8,128)(2,1)S(1)}, bf16[2,2,128,512]{3,2,1,0:T(8,128)(2,1)S(1)}, u32[]{:S(2)}, u32[]{:S(2)}) %collective-permute-start.1) | collective-permute-done | bytes 524320 | tf_op jit(solution)/shard_map/ppermute | solution.py:17
  36.5 4.2 %collective-permute-done.3 = bf16[2,2,128,512]{3,2,1,0:T(8,128)(2,1)S(1)} collective-permute-done((bf16[2,2,128,512]{3,2,1,0:T(8,128)(2,1)S(1)}, bf16[2,2,128,512]{3,2,1,0:T(8,128)(2,1)S(1)}, u32[]{:S(2)}, u32[]{:S(2)}) %collective-permute-start.3) | collective-permute-done | bytes 524320 | tf_op jit(solution)/shard_map/ppermute | solution.py:17
  40.8 1.2 fusion
  42.0 0.8 exponential_reduce_fusion
  42.8 0.7 exponential_convert_fusion
  43.5 1.3 fusion.49
  45.5 1.9 %collective-permute-start.5 = (bf16[32,1024]{1,0:T(8,128)(2,1)S(1)}, bf16[32,1024]{1,0:T(8,128)(2,1)S(1)}, u32[]{:S(2)}, u32[]{:S(2)}) collective-permute-start(bf16[32,1024]{1,0:T(8,128)(2,1)S(1)} %get-tuple-element.30), channel_id=1, source_target_pairs={{2,0},{4,2},{6,4},{8,6},{10,8},{12,10},{14,12},{3,1},{5,3},{7,5},{... | collective-permute-start | bytes 196616 | tf_op jit(solution)/shard_map/ppermute | solution.py:30
  47.4 5.0 %collective-permute-start.4 = (bf16[32,1024]{1,0:T(8,128)(2,1)S(1)}, bf16[32,1024]{1,0:T(8,128)(2,1)S(1)}, u32[]{:S(2)}, u32[]{:S(2)}) collective-permute-start(bf16[32,1024]{1,0:T(8,128)(2,1)S(1)} %get-tuple-element.29), channel_id=1, source_target_pairs={{0,2},{2,4},{4,6},{6,8},{8,10},{10,12},{12,14},{1,3},{3,5},{5,7},{... | collective-permute-start | bytes 196616 | tf_op jit(solution)/shard_map/ppermute | solution.py:28
  52.5 1.6 %collective-permute-done.4 = bf16[32,1024]{1,0:T(8,128)(2,1)S(1)} collective-permute-done((bf16[32,1024]{1,0:T(8,128)(2,1)S(1)}, bf16[32,1024]{1,0:T(8,128)(2,1)S(1)}, u32[]{:S(2)}, u32[]{:S(2)}) %collective-permute-start.4) | collective-permute-done | bytes 65568 | tf_op jit(solution)/shard_map/ppermute | solution.py:28
  54.2 3.0 %multiply_convert_fusion.1 = bf16[160,1024]{1,0:T(8,128)(2,1)S(1)} fusion(bf16[192,1024]{1,0:T(8,128)(2,1)S(1)} %pad_maximum_fusion.5, bf16[16,1024]{1,0:T(8,128)(2,1)S(1)} %reshape.178, bf16[128,1024]{1,0:T(8,128)(2,1)S(1)} %bitcast.163, bf16[16,1024]{1,0:T(8,128)(2,1)S(1)} %reshape.177, f32[1024]{0:T(1024)S(1)} %bitcast.234, f32[1024]{0:T(1024)S(1)} %bitcast.236, ...), kind=kLoop, calls=%fused_computation.33 | loop fusion | flops 17530880 | bytes 10940416 | tf_op jit(solution)/shard_map/convert_element_type | solution.py:175
  57.1 2.3 %add_convert_fusion = bf16[128,1024]{1,0:T(8,128)(2,1)S(1)} fusion(bf16[160,1024]{1,0:T(8,128)(2,1)S(1)} %multiply_convert_fusion.1, f32[1024]{0:T(1024)S(1)} %bitcast.235, f32[1024]{0:T(1024)S(1)} %bitcast.237, f32[1024]{0:T(1024)S(1)} %bitcast.179, f32[1024]{0:T(1024)S(1)} %bitcast.181, f32[1024]{0:T(1024)S(1)} %bitcast.183, f32[1024]{0:T(1024)S(1)} %bitcast.185, ...), kind=kLoop, calls=%fused_computation.54 | loop fusion | flops 12582912 | bytes 8777856 | tf_op jit(solution)/shard_map/convert_element_type | solution.py:193
  59.9 2.5 %fusion.7 = f32[1,31,1024]{2,0,1:T(1,128)S(1)} fusion(bf16[1,160,1024]{2,1,0:T(8,128)(2,1)S(1)} %slice_bitcast_fusion, bf16[128,1,1024]{2,0,1:T(8,128)(2,1)S(1)} %slice_bitcast_fusion.1), kind=kOutput, calls=%fused_computation.30 | convolution fusion | flops 8126464 | bytes 716800 | tf_op jit(solution)/shard_map/slice | solution.py:182
  62.5 0.8 copy-done.1
  63.3 0.9 fusion.2
  64.2 1.2 convert_multiply_fusion
  65.5 1.1 copy.19
  66.7 1.3 %fusion.4 = f32[1,8,40,1024]{3,2,1,0:T(8,128)S(1)} fusion(s32[]{:T(128)S(6)} %select_n.165, f32[2,8,32,1024]{3,2,1,0:T(8,128)S(1)} %bitcast.152, f32[2,8,8,1024]{3,2,1,0:T(8,128)} %bitcast.158, bf16[1,8,40,1024]{3,2,1,0:T(8,128)(2,1)} %collective-permute-done.10), kind=kLoop, calls=%fused_computation.19 | loop fusion | flops 983040 | bytes 4587524 | tf_op jit(solution)/shard_map/add | solution.py:78
  68.3 9.9 %collective-permute-done.11 = bf16[4,40,1024]{2,1,0:T(8,128)(2,1)S(1)} collective-permute-done((bf16[4,40,1024]{2,1,0:T(8,128)(2,1)S(1)}, bf16[4,40,1024]{2,1,0:T(8,128)(2,1)S(1)}, u32[]{:S(2)}, u32[]{:S(2)}) %collective-permute-start.11) | collective-permute-done | bytes 327712 | tf_op jit(solution)/shard_map/ppermute | solution.py:66
  78.3 2.1 %collective-permute-start.12 = (bf16[2,40,1024]{2,1,0:T(8,128)(2,1)S(1)}, bf16[2,40,1024]{2,1,0:T(8,128)(2,1)S(1)}, u32[]{:S(2)}, u32[]{:S(2)}) collective-permute-start(bf16[2,40,1024]{2,1,0:T(8,128)(2,1)S(1)} %dynamic-slice_convert_fusion.1), channel_id=1, source_target_pairs={{0,4},{2,6},{4,0},{6,2},{8,12},{10,14},{12,8},{14,10},{1,5},{3,7},... | collective-permute-start | bytes 491528 | tf_op jit(solution)/shard_map/ppermute | solution.py:66
  80.5 1.1 multiply_convert_fusion
  81.7 3.1 %collective-permute-done.12 = bf16[2,40,1024]{2,1,0:T(8,128)(2,1)S(1)} collective-permute-done((bf16[2,40,1024]{2,1,0:T(8,128)(2,1)S(1)}, bf16[2,40,1024]{2,1,0:T(8,128)(2,1)S(1)}, u32[]{:S(2)}, u32[]{:S(2)}) %collective-permute-start.12) | collective-permute-done | bytes 163872 | tf_op jit(solution)/shard_map/ppermute | solution.py:66
  84.8 2.8 %collective-permute-start.13 = (bf16[1,40,1024]{2,1,0:T(8,128)(2,1)S(1)}, bf16[1,40,1024]{2,1,0:T(8,128)(2,1)S(1)}, u32[]{:S(2)}, u32[]{:S(2)}) collective-permute-start(bf16[1,40,1024]{2,1,0:T(8,128)(2,1)S(1)} %dynamic-slice_convert_fusion.2), channel_id=1, source_target_pairs={{0,8},{2,10},{4,12},{6,14},{8,0},{10,2},{12,4},{14,6},{1,9},{3,11}... | collective-permute-start | bytes 245768 | tf_op jit(solution)/shard_map/ppermute | solution.py:66
  87.6 1.1 fusion.47
  88.7 1.6 %collective-permute-done.13 = bf16[1,40,1024]{2,1,0:T(8,128)(2,1)S(1)} collective-permute-done((bf16[1,40,1024]{2,1,0:T(8,128)(2,1)S(1)}, bf16[1,40,1024]{2,1,0:T(8,128)(2,1)S(1)}, u32[]{:S(2)}, u32[]{:S(2)}) %collective-permute-start.13) | collective-permute-done | bytes 81952 | tf_op jit(solution)/shard_map/ppermute | solution.py:66
  90.3 2.7 %collective-permute-start.14 = (bf16[1,40,1024]{2,1,0:T(8,128)(2,1)S(1)}, bf16[1,40,1024]{2,1,0:T(8,128)(2,1)S(1)}, u32[]{:S(2)}, u32[]{:S(2)}) collective-permute-start(bf16[1,40,1024]{2,1,0:T(8,128)(2,1)S(1)} %add_convert_fusion.1), channel_id=1, source_target_pairs={{0,8},{2,10},{4,12},{6,14},{8,0},{10,2},{12,4},{14,6},{1,9},{3,11}... | collective-permute-start | bytes 245768 | tf_op jit(solution)/shard_map/ppermute | solution.py:66
  93.0 1.1 fusion.48
  94.2 1.6 %collective-permute-done.14 = bf16[1,40,1024]{2,1,0:T(8,128)(2,1)S(1)} collective-permute-done((bf16[1,40,1024]{2,1,0:T(8,128)(2,1)S(1)}, bf16[1,40,1024]{2,1,0:T(8,128)(2,1)S(1)}, u32[]{:S(2)}, u32[]{:S(2)}) %collective-permute-start.14) | collective-permute-done | bytes 81952 | tf_op jit(solution)/shard_map/ppermute | solution.py:66
  95.8 1.7 %collective-permute-start.15 = (bf16[2,40,1024]{2,1,0:T(8,128)(2,1)S(1)}, bf16[2,40,1024]{2,1,0:T(8,128)(2,1)S(1)}, u32[]{:S(2)}, u32[]{:S(2)}) collective-permute-start(bf16[2,40,1024]{2,1,0:T(8,128)(2,1)S(1)} %pad_maximum_fusion.10), channel_id=1, source_target_pairs={{0,4},{2,6},{4,0},{6,2},{8,12},{10,14},{12,8},{14,10},{1,5},{3,7},... | collective-permute-start | bytes 491528 | tf_op jit(solution)/shard_map/ppermute | solution.py:66
  97.5 1.3 %fusion.50 = f32[1024,512]{1,0:T(8,128)S(1)} fusion(bf16[1024,896]{0,1:T(8,128)(2,1)S(1)} %multiply_convert_fusion, bf16[896,512]{1,0:T(8,128)(2,1)S(1)} %copy-done.15), kind=kOutput, calls=%fused_computation.131 | convolution fusion | flops 939524096 | bytes 4849664 | tf_op jit(solution)/shard_map/dot_general | solution.py:150
  98.9 1.3 collective-permute-start.7
  100.2 4.6 %collective-permute-start.6 = (bf16[2,2,128,512]{3,2,1,0:T(8,128)(2,1)S(1)}, bf16[2,2,128,512]{3,2,1,0:T(8,128)(2,1)S(1)}, u32[]{:S(2)}, u32[]{:S(2)}) collective-permute-start(bf16[2,2,128,512]{3,2,1,0:T(8,128)(2,1)S(1)} %get-tuple-element.5), channel_id=1, source_target_pairs={{0,4},{2,6},{4,8},{6,10},{8,12},{10,14},{1,5},{3,7},{5,9},{7,11},{... | collective-permute-start | bytes 1572872 | tf_op jit(solution)/shard_map/ppermute | solution.py:17
  104.9 1.5 %collective-permute-start.16 = (bf16[4,40,1024]{2,1,0:T(8,128)(2,1)S(1)}, bf16[4,40,1024]{2,1,0:T(8,128)(2,1)S(1)}, u32[]{:S(2)}, u32[]{:S(2)}) collective-permute-start(bf16[4,40,1024]{2,1,0:T(8,128)(2,1)S(1)} %pad_maximum_fusion.6), channel_id=1, source_target_pairs={{0,2},{2,0},{4,6},{6,4},{8,10},{10,8},{12,14},{14,12},{1,3},{3,1},... | collective-permute-start | bytes 983048 | tf_op jit(solution)/shard_map/ppermute | solution.py:66
  106.8 5.6 %collective-permute-done.7 = bf16[2,2,128,512]{3,2,1,0:T(8,128)(2,1)S(1)} collective-permute-done((bf16[2,2,128,512]{3,2,1,0:T(8,128)(2,1)S(1)}, bf16[2,2,128,512]{3,2,1,0:T(8,128)(2,1)S(1)}, u32[]{:S(2)}, u32[]{:S(2)}) %collective-permute-start.7) | collective-permute-done | bytes 524320 | tf_op jit(solution)/shard_map/ppermute | solution.py:17
  112.9 3.5 %collective-permute-start.9 = (bf16[2,128,512]{2,1,0:T(8,128)(2,1)S(1)}, bf16[2,128,512]{2,1,0:T(8,128)(2,1)S(1)}, u32[]{:S(2)}, u32[]{:S(2)}) collective-permute-start(bf16[2,128,512]{2,1,0:T(8,128)(2,1)S(1)} %get-tuple-element.8), channel_id=1, source_target_pairs={{2,0},{4,2},{6,4},{8,6},{10,8},{12,10},{14,12},{3,1},{5,3},{7,5},{... | collective-permute-start | bytes 786440 | tf_op jit(solution)/shard_map/ppermute | solution.py:17
  116.4 3.3 %collective-permute-start.8 = (bf16[2,128,512]{2,1,0:T(8,128)(2,1)S(1)}, bf16[2,128,512]{2,1,0:T(8,128)(2,1)S(1)}, u32[]{:S(2)}, u32[]{:S(2)}) collective-permute-start(bf16[2,128,512]{2,1,0:T(8,128)(2,1)S(1)} %get-tuple-element.7), channel_id=1, source_target_pairs={{0,2},{2,4},{4,6},{6,8},{8,10},{10,12},{12,14},{1,3},{3,5},{5,7},{... | collective-permute-start | bytes 786440 | tf_op jit(solution)/shard_map/ppermute | solution.py:17
  120.6 1.6 %collective-permute-done.9 = bf16[2,128,512]{2,1,0:T(8,128)(2,1)S(1)} collective-permute-done((bf16[2,128,512]{2,1,0:T(8,128)(2,1)S(1)}, bf16[2,128,512]{2,1,0:T(8,128)(2,1)S(1)}, u32[]{:S(2)}, u32[]{:S(2)}) %collective-permute-start.9) | collective-permute-done | bytes 262176 | tf_op jit(solution)/shard_map/ppermute | solution.py:17
  122.2 4.3 %collective-permute-done.8 = bf16[2,128,512]{2,1,0:T(8,128)(2,1)S(1)} collective-permute-done((bf16[2,128,512]{2,1,0:T(8,128)(2,1)S(1)}, bf16[2,128,512]{2,1,0:T(8,128)(2,1)S(1)}, u32[]{:S(2)}, u32[]{:S(2)}) %collective-permute-start.8) | collective-permute-done | bytes 262176 | tf_op jit(solution)/shard_map/ppermute | solution.py:17
  126.8 0.7 fusion.42
  127.6 1.1 fusion.6
  (100 shorter events, 5.3 us)
Async XLA Ops:
  0.6 44.5 %copy-start = (bf16[512,1024]{1,0:T(8,128)(2,1)S(1)}, bf16[512,1024]{1,0:T(8,128)(2,1)}, u32[]{:S(2)}) copy-start(bf16[512,1024]{1,0:T(8,128)(2,1)} %param.11) | copy-start | bytes 3145732
  2.5 22.6 %copy-start.11 = (f32[31,1024]{1,0:T(8,128)S(1)}, f32[31,1024]{1,0:T(8,128)}, u32[]{:S(2)}) copy-start(f32[31,1024]{1,0:T(8,128)} %param.12) | copy-start | bytes 380932
  2.5 22.6 %copy-start.10 = (bf16[1,128,512]{2,1,0:T(8,128)(2,1)S(1)}, bf16[1,128,512]{2,1,0:T(8,128)(2,1)}, u32[]{:S(2)}) copy-start(bf16[1,128,512]{2,1,0:T(8,128)(2,1)} %param.7) | copy-start | bytes 393220
  3.5 11.6 %collective-permute-start.2 = (bf16[288,512]{1,0:T(8,128)(2,1)S(1)}, bf16[288,512]{1,0:T(8,128)(2,1)S(1)}, u32[]{:S(2)}, u32[]{:S(2)}) collective-permute-start(bf16[288,512]{1,0:T(8,128)(2,1)S(1)} %get-tuple-element.33), channel_id=1, source_target_pairs={{2,0},{4,2},{6,4},{8,6},{10,8},{12,10},{14,12},{3,1},{5,3},{7,5},{... | collective-permute-start | bytes 884744 | tf_op jit(solution)/shard_map/ppermute | solution.py:17
  5.4 15.9 %collective-permute-start = (bf16[288,512]{1,0:T(8,128)(2,1)S(1)}, bf16[288,512]{1,0:T(8,128)(2,1)S(1)}, u32[]{:S(2)}, u32[]{:S(2)}) collective-permute-start(bf16[288,512]{1,0:T(8,128)(2,1)S(1)} %get-tuple-element.34), channel_id=1, source_target_pairs={{0,2},{2,4},{4,6},{6,8},{8,10},{10,12},{12,14},{1,3},{3,5},{5,7},{... | collective-permute-start | bytes 884744 | tf_op jit(solution)/shard_map/ppermute | solution.py:17
  21.4 15.0 %copy-start.8 = (bf16[1,128,512]{2,1,0:T(8,128)(2,1)S(1)}, bf16[1,128,512]{2,1,0:T(8,128)(2,1)}, u32[]{:S(2)}) copy-start(bf16[1,128,512]{2,1,0:T(8,128)(2,1)} %param.8) | copy-start | bytes 393220
  21.4 15.0 %copy-start.9 = (bf16[1,128,512]{2,1,0:T(8,128)(2,1)S(1)}, bf16[1,128,512]{2,1,0:T(8,128)(2,1)}, u32[]{:S(2)}) copy-start(bf16[1,128,512]{2,1,0:T(8,128)(2,1)} %param.9) | copy-start | bytes 393220
  21.5 14.8 %collective-permute-start.1 = (bf16[2,2,128,512]{3,2,1,0:T(8,128)(2,1)S(1)}, bf16[2,2,128,512]{3,2,1,0:T(8,128)(2,1)S(1)}, u32[]{:S(2)}, u32[]{:S(2)}) collective-permute-start(bf16[2,2,128,512]{3,2,1,0:T(8,128)(2,1)S(1)} %get-tuple-element.32), channel_id=1, source_target_pairs={{0,4},{2,6},{4,8},{6,10},{8,12},{10,14},{1,5},{3,7},{5,9},{7,11},{... | collective-permute-start | bytes 1572872 | tf_op jit(solution)/shard_map/ppermute | solution.py:17
  25.2 16.7 %copy-start.5 = (bf16[8,128,512]{2,1,0:T(8,128)(2,1)}, bf16[8,128,512]{2,1,0:T(8,128)(2,1)S(1)}, u32[]{:S(2)}) copy-start(bf16[8,128,512]{2,1,0:T(8,128)(2,1)S(1)} %broadcast_select_fusion.1) | copy-start | bytes 3145732
  25.2 15.5 %collective-permute-start.3 = (bf16[2,2,128,512]{3,2,1,0:T(8,128)(2,1)S(1)}, bf16[2,2,128,512]{3,2,1,0:T(8,128)(2,1)S(1)}, u32[]{:S(2)}, u32[]{:S(2)}) collective-permute-start(bf16[2,2,128,512]{3,2,1,0:T(8,128)(2,1)S(1)} %get-tuple-element.31), channel_id=1, source_target_pairs={{4,0},{6,2},{8,4},{10,6},{12,8},{14,10},{5,1},{7,3},{9,5},{11,7},{... | collective-permute-start | bytes 1572872 | tf_op jit(solution)/shard_map/ppermute | solution.py:17
  40.7 1.2 copy-start.14
  40.8 2.8 %copy-start.12 = (bf16[896,512]{1,0:T(8,128)(2,1)}, bf16[896,512]{1,0:T(8,128)(2,1)S(1)}, u32[]{:S(2)}) copy-start(bf16[896,512]{1,0:T(8,128)(2,1)S(1)} %get-tuple-element.13) | copy-start | bytes 2752516
  43.5 1.3 %copy-start.2 = (bf16[1024,896]{0,1:T(8,128)(2,1)}, bf16[1024,896]{0,1:T(8,128)(2,1)S(1)}, u32[]{:S(2)}) copy-start(bf16[1024,896]{0,1:T(8,128)(2,1)S(1)} %exponential_convert_fusion) | copy-start | bytes 5505028
  45.1 9.1 %copy-start.4 = (bf16[1,128,1024]{2,1,0:T(8,128)(2,1)S(1)}, bf16[1,128,1024]{2,1,0:T(8,128)(2,1)}, u32[]{:S(2)}) copy-start(bf16[1,128,1024]{2,1,0:T(8,128)(2,1)} %param.10) | copy-start | bytes 786436
  45.5 7.1 %collective-permute-start.5 = (bf16[32,1024]{1,0:T(8,128)(2,1)S(1)}, bf16[32,1024]{1,0:T(8,128)(2,1)S(1)}, u32[]{:S(2)}, u32[]{:S(2)}) collective-permute-start(bf16[32,1024]{1,0:T(8,128)(2,1)S(1)} %get-tuple-element.30), channel_id=1, source_target_pairs={{2,0},{4,2},{6,4},{8,6},{10,8},{12,10},{14,12},{3,1},{5,3},{7,5},{... | collective-permute-start | bytes 196616 | tf_op jit(solution)/shard_map/ppermute | solution.py:30
  47.4 6.7 %collective-permute-start.4 = (bf16[32,1024]{1,0:T(8,128)(2,1)S(1)}, bf16[32,1024]{1,0:T(8,128)(2,1)S(1)}, u32[]{:S(2)}, u32[]{:S(2)}) collective-permute-start(bf16[32,1024]{1,0:T(8,128)(2,1)S(1)} %get-tuple-element.29), channel_id=1, source_target_pairs={{0,2},{2,4},{4,6},{6,8},{8,10},{10,12},{12,14},{1,3},{3,5},{5,7},{... | collective-permute-start | bytes 196616 | tf_op jit(solution)/shard_map/ppermute | solution.py:28
  62.5 0.8 copy-start.1
  64.2 2.4 %collective-permute-start.10 = (bf16[1,8,40,1024]{3,2,1,0:T(8,128)(2,1)}, bf16[1,8,40,1024]{3,2,1,0:T(8,128)(2,1)}, u32[]{:S(2)}, u32[]{:S(2)}) collective-permute-start(bf16[1,8,40,1024]{3,2,1,0:T(8,128)(2,1)} %fusion.2), channel_id=1, source_target_pairs={{0,1},{1,0},{2,3},{3,2},{4,5},{5,4},{6,7},{7,6},{8,9},{9,8},{10,11... | collective-permute-start | bytes 1966088 | tf_op jit(solution)/shard_map/ppermute | solution.py:66
  66.5 1.7 %copy-start.7 = (bf16[128,512]{1,0:T(8,128)(2,1)S(1)}, bf16[128,512]{1,0:T(8,128)(2,1)}, u32[]{:S(2)}) copy-start(bf16[128,512]{1,0:T(8,128)(2,1)} %get-tuple-element.73) | copy-start | bytes 393220
  68.0 12.5 %copy-start.3 = (bf16[1024,896]{0,1:T(8,128)(2,1)S(1)}, bf16[1024,896]{0,1:T(8,128)(2,1)}, u32[]{:S(2)}) copy-start(bf16[1024,896]{0,1:T(8,128)(2,1)} %copy-done.2) | copy-start | bytes 5505028
  68.0 12.5 %copy-start.13 = (bf16[896,512]{1,0:T(8,128)(2,1)S(1)}, bf16[896,512]{1,0:T(8,128)(2,1)}, u32[]{:S(2)}) copy-start(bf16[896,512]{1,0:T(8,128)(2,1)} %copy-done.12) | copy-start | bytes 2752516
  68.1 10.1 %collective-permute-start.11 = (bf16[4,40,1024]{2,1,0:T(8,128)(2,1)S(1)}, bf16[4,40,1024]{2,1,0:T(8,128)(2,1)S(1)}, u32[]{:S(2)}, u32[]{:S(2)}) collective-permute-start(bf16[4,40,1024]{2,1,0:T(8,128)(2,1)S(1)} %fusion.21), channel_id=1, source_target_pairs={{0,2},{2,0},{4,6},{6,4},{8,10},{10,8},{12,14},{14,12},{1,3},{3,1},... | collective-permute-start | bytes 983048 | tf_op jit(solution)/shard_map/ppermute | solution.py:66
  78.3 6.4 %collective-permute-start.12 = (bf16[2,40,1024]{2,1,0:T(8,128)(2,1)S(1)}, bf16[2,40,1024]{2,1,0:T(8,128)(2,1)S(1)}, u32[]{:S(2)}, u32[]{:S(2)}) collective-permute-start(bf16[2,40,1024]{2,1,0:T(8,128)(2,1)S(1)} %dynamic-slice_convert_fusion.1), channel_id=1, source_target_pairs={{0,4},{2,6},{4,0},{6,2},{8,12},{10,14},{12,8},{14,10},{1,5},{3,7},... | collective-permute-start | bytes 491528 | tf_op jit(solution)/shard_map/ppermute | solution.py:66
  84.8 8.2 %copy-start.6 = (bf16[8,128,512]{2,1,0:T(8,128)(2,1)S(1)}, bf16[8,128,512]{2,1,0:T(8,128)(2,1)}, u32[]{:S(2)}) copy-start(bf16[8,128,512]{2,1,0:T(8,128)(2,1)} %copy-done.5) | copy-start | bytes 3145732
  84.8 5.5 %collective-permute-start.13 = (bf16[1,40,1024]{2,1,0:T(8,128)(2,1)S(1)}, bf16[1,40,1024]{2,1,0:T(8,128)(2,1)S(1)}, u32[]{:S(2)}, u32[]{:S(2)}) collective-permute-start(bf16[1,40,1024]{2,1,0:T(8,128)(2,1)S(1)} %dynamic-slice_convert_fusion.2), channel_id=1, source_target_pairs={{0,8},{2,10},{4,12},{6,14},{8,0},{10,2},{12,4},{14,6},{1,9},{3,11}... | collective-permute-start | bytes 245768 | tf_op jit(solution)/shard_map/ppermute | solution.py:66
  90.3 7.2 %copy-start.15 = (bf16[896,512]{1,0:T(8,128)(2,1)S(1)}, bf16[896,512]{1,0:T(8,128)(2,1)}, u32[]{:S(2)}) copy-start(bf16[896,512]{1,0:T(8,128)(2,1)} %copy-done.14) | copy-start | bytes 2752516
  90.3 5.4 %collective-permute-start.14 = (bf16[1,40,1024]{2,1,0:T(8,128)(2,1)S(1)}, bf16[1,40,1024]{2,1,0:T(8,128)(2,1)S(1)}, u32[]{:S(2)}, u32[]{:S(2)}) collective-permute-start(bf16[1,40,1024]{2,1,0:T(8,128)(2,1)S(1)} %add_convert_fusion.1), channel_id=1, source_target_pairs={{0,8},{2,10},{4,12},{6,14},{8,0},{10,2},{12,4},{14,6},{1,9},{3,11}... | collective-permute-start | bytes 245768 | tf_op jit(solution)/shard_map/ppermute | solution.py:66
  95.8 9.0 %collective-permute-start.15 = (bf16[2,40,1024]{2,1,0:T(8,128)(2,1)S(1)}, bf16[2,40,1024]{2,1,0:T(8,128)(2,1)S(1)}, u32[]{:S(2)}, u32[]{:S(2)}) collective-permute-start(bf16[2,40,1024]{2,1,0:T(8,128)(2,1)S(1)} %pad_maximum_fusion.10), channel_id=1, source_target_pairs={{0,4},{2,6},{4,0},{6,2},{8,12},{10,14},{12,8},{14,10},{1,5},{3,7},... | collective-permute-start | bytes 491528 | tf_op jit(solution)/shard_map/ppermute | solution.py:66
  98.9 13.5 %collective-permute-start.7 = (bf16[2,2,128,512]{3,2,1,0:T(8,128)(2,1)S(1)}, bf16[2,2,128,512]{3,2,1,0:T(8,128)(2,1)S(1)}, u32[]{:S(2)}, u32[]{:S(2)}) collective-permute-start(bf16[2,2,128,512]{3,2,1,0:T(8,128)(2,1)S(1)} %get-tuple-element.6), channel_id=1, source_target_pairs={{4,0},{6,2},{8,4},{10,6},{12,8},{14,10},{5,1},{7,3},{9,5},{11,7},{... | collective-permute-start | bytes 1572872 | tf_op jit(solution)/shard_map/ppermute | solution.py:17
  100.2 12.4 %collective-permute-start.6 = (bf16[2,2,128,512]{3,2,1,0:T(8,128)(2,1)S(1)}, bf16[2,2,128,512]{3,2,1,0:T(8,128)(2,1)S(1)}, u32[]{:S(2)}, u32[]{:S(2)}) collective-permute-start(bf16[2,2,128,512]{3,2,1,0:T(8,128)(2,1)S(1)} %get-tuple-element.5), channel_id=1, source_target_pairs={{0,4},{2,6},{4,8},{6,10},{8,12},{10,14},{1,5},{3,7},{5,9},{7,11},{... | collective-permute-start | bytes 1572872 | tf_op jit(solution)/shard_map/ppermute | solution.py:17
  104.9 14.8 %collective-permute-start.16 = (bf16[4,40,1024]{2,1,0:T(8,128)(2,1)S(1)}, bf16[4,40,1024]{2,1,0:T(8,128)(2,1)S(1)}, u32[]{:S(2)}, u32[]{:S(2)}) collective-permute-start(bf16[4,40,1024]{2,1,0:T(8,128)(2,1)S(1)} %pad_maximum_fusion.6), channel_id=1, source_target_pairs={{0,2},{2,0},{4,6},{6,4},{8,10},{10,8},{12,14},{14,12},{1,3},{3,1},... | collective-permute-start | bytes 983048 | tf_op jit(solution)/shard_map/ppermute | solution.py:66
  112.9 9.3 %collective-permute-start.9 = (bf16[2,128,512]{2,1,0:T(8,128)(2,1)S(1)}, bf16[2,128,512]{2,1,0:T(8,128)(2,1)S(1)}, u32[]{:S(2)}, u32[]{:S(2)}) collective-permute-start(bf16[2,128,512]{2,1,0:T(8,128)(2,1)S(1)} %get-tuple-element.8), channel_id=1, source_target_pairs={{2,0},{4,2},{6,4},{8,6},{10,8},{12,10},{14,12},{3,1},{5,3},{7,5},{... | collective-permute-start | bytes 786440 | tf_op jit(solution)/shard_map/ppermute | solution.py:17
  116.4 10.1 %collective-permute-start.8 = (bf16[2,128,512]{2,1,0:T(8,128)(2,1)S(1)}, bf16[2,128,512]{2,1,0:T(8,128)(2,1)S(1)}, u32[]{:S(2)}, u32[]{:S(2)}) collective-permute-start(bf16[2,128,512]{2,1,0:T(8,128)(2,1)S(1)} %get-tuple-element.7), channel_id=1, source_target_pairs={{0,2},{2,4},{4,6},{6,8},{8,10},{10,12},{12,14},{1,3},{3,5},{5,7},{... | collective-permute-start | bytes 786440 | tf_op jit(solution)/shard_map/ppermute | solution.py:17
  119.8 7.7 %collective-permute-start.17 = (bf16[1,8,40,1024]{3,2,1,0:T(8,128)(2,1)S(1)}, bf16[1,8,40,1024]{3,2,1,0:T(8,128)(2,1)S(1)}, u32[]{:S(2)}, u32[]{:S(2)}) collective-permute-start(bf16[1,8,40,1024]{3,2,1,0:T(8,128)(2,1)S(1)} %maximum_bitcast_fusion), channel_id=1, source_target_pairs={{0,1},{1,0},{2,3},{3,2},{4,5},{5,4},{6,7},{7,6},{8,9},{9,8},{10,11... | collective-permute-start | bytes 1966088 | tf_op jit(solution)/shard_map/ppermute | solution.py:66
